TPU v7x, 32 devices: a whole 2x2x4 slice. The times are simulated.
32 devices in a mesh: group: 2 (over y), seq: 16 (over z, x, core).
Axes of the slice: x: 2, y: 2, z: 4, core: 2. Of those that a mesh axis runs over, the one named last changes fastest.
Arguments:
- node_feats: bfloat16 [16384, 1024], P(('group', 'seq')), parts along dimension 0, may hold values from -6 to 6
- struct_feats: float32 [16384, 128], P(('group', 'seq')), parts along dimension 0, may hold values from -6 to 6
- op_blocks: float32 [256, 3, 64, 64], P(('group', 'seq')), parts along dimension 0, may hold values from -0.07 to 0.07
- laplace_index: int32 [256, 3], P(('group', 'seq')), parts along dimension 0, may hold values from 0 to 127, as said below
- graph_links: int32 [256, 3], P(('group', 'seq')), parts along dimension 0, may hold values from 0 to 127, as said below
- expander_slot: int32 [256, 4], P(('group', 'seq')), parts along dimension 0, may hold values from 0 to 7
- series_coef: float32 [9], replicated, may hold values from 0.3 to 1
- encode_weight: bfloat16 [128, 1024], replicated, may hold values from -0.5 to 0.5
- qkv_weight: bfloat16 [1024, 3072], replicated, may hold values from -0.1875 to 0.1875
- out_weight: bfloat16 [1024, 1024], replicated, may hold values from -0.1875 to 0.1875
Outputs:
- mixed: bfloat16 [16384, 1024], P(('group', 'seq')), parts along dimension 0
There are 2 independent parts, one for each index of `group`. A program takes and returns all parts, laid end to end along the dimension named above; an argument that names none is the same for every part. Nothing has to cross between parts.
Inputs may be any that keep to these rules, and one draw needn't show every extreme that they name: `laplace_index`: each entry lies within 2 blocks of its row's block. `graph_links`: each entry lies within 2 blocks of its row's block.
All inputs are finite; a program needn't handle non-finite values.
Results may differ from a plain program's by a relative error of at most 0.012.
The roundings to bfloat16 on the way count: a program that leaves them out, or rounds other values in their place, can miss the bound.
Values may be sent and summed in bfloat16 or wider, within the bound.
No kernel may reach another device: no remote copies, remote signals or barrier semaphores. Data moves between devices by JAX's collectives and lax.ppermute only.
A program may use at most 192 MiB of HBM per device.

v0:
```python
import jax
import jax.numpy as jnp
from jax import lax
from jax.sharding import PartitionSpec as P

D = 1024
HEADS = 16
HD = 64
BS = 64
DEG = 8
NEXP = 4
REACH = 2


def extended(x, sides, width):
    for axis, dim in sides:
        peers, length = (lax.axis_size(axis), x.shape[dim])
        up = [(i, (i + 1) % peers) for i in range(peers - 1)]
        down = [(j, i) for i, j in up]
        last = lax.slice_in_dim(x, length - width, length, axis=dim)
        first = lax.slice_in_dim(x, 0, width, axis=dim)
        before = lax.ppermute(last, axis, up)
        after = lax.ppermute(first, axis, down)
        x = jnp.concatenate([before, x, after], axis=dim)
    return x


def partner(value, axis, distance):
    mask = 2**distance
    pairs = [(source, source ^ mask) for source in range(lax.axis_size(axis))]
    return lax.ppermute(value, axis, pairs)


def apply_operator(field, op_blocks, laplace_index, first_block):
    count = op_blocks.shape[0]
    padded = extended(field, (("seq", 0),), REACH * BS)
    pooled = padded.reshape(count + 2 * REACH, BS, field.shape[1])
    position = laplace_index - first_block + REACH
    picked = pooled[position]
    result = jnp.einsum("bjst,bjtc->bsc", op_blocks, picked, precision=lax.Precision.HIGHEST)
    return result.reshape(field.shape)


def on_device(
    node_feats,
    struct_feats,
    op_blocks,
    laplace_index,
    graph_links,
    expander_slot,
    series_coef,
    encode_weight,
    qkv_weight,
    out_weight,
):
    count = op_blocks.shape[0]
    first_block = lax.axis_index("seq") * count
    previous = struct_feats
    current = apply_operator(previous, op_blocks, laplace_index, first_block)
    encoding = series_coef[0] * previous + series_coef[1] * current
    for degree in range(2, DEG + 1):
        following = 2.0 * apply_operator(current, op_blocks, laplace_index, first_block) - previous
        encoding = encoding + series_coef[degree] * following
        previous, current = (current, following)
    encoded = jnp.dot(
        encoding.astype(jnp.bfloat16), encode_weight, preferred_element_type=jnp.float32
    )
    blended = (node_feats.astype(jnp.float32) + encoded).astype(jnp.bfloat16)
    projected = jnp.dot(blended, qkv_weight, preferred_element_type=jnp.float32)
    queries = projected[:, :D].astype(jnp.bfloat16)
    keyvals = projected[:, D:].astype(jnp.bfloat16)
    rim_rows = REACH * BS
    near_pool = extended(keyvals, (("seq", 0),), rim_rows)
    levels = lax.axis_size("seq").bit_length() - 1
    far_parts = []
    for link in range(NEXP):
        bit_number = link * (levels - 1) // (NEXP - 1)
        far_rows = partner(keyvals, "seq", bit_number)
        far_parts.append(far_rows)
    pool_rows = jnp.concatenate([near_pool] + far_parts, axis=0)
    pool_blocks = pool_rows.reshape(-1, BS, 2 * D)
    own_slot = jnp.arange(count, dtype=jnp.int32)[:, None] + REACH
    graph_slot = graph_links - first_block + REACH
    far_base = count + 2 * REACH + jnp.arange(NEXP, dtype=jnp.int32) * count
    far_slot = far_base[None, :] + expander_slot
    key_slots = jnp.concatenate([own_slot, graph_slot, far_slot], axis=1)
    picked = pool_blocks[key_slots].reshape(count, -1, 2 * D)
    keys = picked[:, :, :D].reshape(count, -1, HEADS, HD)
    values = picked[:, :, D:].reshape(count, -1, HEADS, HD)
    qheads = queries.reshape(count, BS, HEADS, HD)
    scale = 1.0 / HD**0.5
    scores = jnp.einsum("bqhd,bkhd->bhqk", qheads, keys, preferred_element_type=jnp.float32) * scale
    weights = jax.nn.softmax(scores, axis=-1).astype(jnp.bfloat16)
    attended = jnp.einsum("bhqk,bkhd->bqhd", weights, values, preferred_element_type=jnp.float32)
    attended = attended.reshape(count * BS, D).astype(jnp.bfloat16)
    return jnp.dot(attended, out_weight, preferred_element_type=jnp.float32).astype(jnp.bfloat16)


def solution(mesh):
    placed = (
        P(("group", "seq"), None),
        P(("group", "seq"), None),
        P(("group", "seq"), None, None, None),
        P(("group", "seq"), None),
        P(("group", "seq"), None),
        P(("group", "seq"), None),
        P(),
        P(),
        P(),
        P(),
    )
    return jax.shard_map(
        on_device, mesh=mesh, in_specs=placed, out_specs=P(("group", "seq"), None), check_vma=False
    )
```

profile of v0, /device:TPU:15, one launch (start us, length us, event | category | flops | bytes accessed | tf_op | source)
XLA Modules:
  0.0 343.2 jit_solution(6311281531585466854)
XLA Ops:
  1.0 3.7 %collective-permute-start = (f32[128,128]{1,0:T(8,128)S(1)}, f32[128,128]{1,0:T(8,128)S(1)}, u32[]{:S(2)}, u32[]{:S(2)}) collective-permute-start(f32[128,128]{1,0:T(8,128)S(1)} %get-tuple-element.25), channel_id=1, source_target_pairs={{0,1},{1,2},{2,3},{3,4},{4,5},{5,6},{6,7},{7,8},{8,9},{9,10},{10,1... | collective-permute-start | bytes 196616 | tf_op jit(solution)/shard_map/ppermute | solution.py:22
  7.6 3.7 %collective-permute-done.1 = f32[128,128]{1,0:T(8,128)S(1)} collective-permute-done((f32[128,128]{1,0:T(8,128)S(1)}, f32[128,128]{1,0:T(8,128)S(1)}, u32[]{:S(2)}, u32[]{:S(2)}) %collective-permute-start.1) | collective-permute-done | bytes 65568 | tf_op jit(solution)/shard_map/ppermute | solution.py:23
  13.7 2.4 fusion.43
  18.0 4.5 %collective-permute-start.2 = (f32[128,128]{1,0:T(8,128)S(1)}, f32[128,128]{1,0:T(8,128)S(1)}, u32[]{:S(2)}, u32[]{:S(2)}) collective-permute-start(f32[128,128]{1,0:T(8,128)S(1)} %bitcast.167), channel_id=1, source_target_pairs={{0,1},{1,2},{2,3},{3,4},{4,5},{5,6},{6,7},{7,8},{8,9},{9,10},{10,1... | collective-permute-start | bytes 196616 | tf_op jit(solution)/shard_map/ppermute | solution.py:22
  25.4 2.4 fusion.15
  28.8 5.2 %collective-permute-start.4 = (f32[128,128]{1,0:T(8,128)S(1)}, f32[128,128]{1,0:T(8,128)S(1)}, u32[]{:S(2)}, u32[]{:S(2)}) collective-permute-start(f32[128,128]{1,0:T(8,128)S(1)} %get-tuple-element.21), channel_id=1, source_target_pairs={{0,1},{1,2},{2,3},{3,4},{4,5},{5,6},{6,7},{7,8},{8,9},{9,10},{10,1... | collective-permute-start | bytes 196616 | tf_op jit(solution)/shard_map/ppermute | solution.py:22
  35.9 4.5 %collective-permute-done.5 = f32[128,128]{1,0:T(8,128)S(1)} collective-permute-done((f32[128,128]{1,0:T(8,128)S(1)}, f32[128,128]{1,0:T(8,128)S(1)}, u32[]{:S(2)}, u32[]{:S(2)}) %collective-permute-start.5) | collective-permute-done | bytes 65568 | tf_op jit(solution)/shard_map/ppermute | solution.py:23
  41.2 2.5 gather_fusion.2
  43.7 2.1 fusion.16
  47.8 2.4 collective-permute-start.7
  50.3 4.1 %collective-permute-done.7 = f32[128,128]{1,0:T(8,128)S(1)} collective-permute-done((f32[128,128]{1,0:T(8,128)S(1)}, f32[128,128]{1,0:T(8,128)S(1)}, u32[]{:S(2)}, u32[]{:S(2)}) %collective-permute-start.7) | collective-permute-done | bytes 65568 | tf_op jit(solution)/shard_map/ppermute | solution.py:23
  55.1 2.5 gather_fusion.3
  57.6 2.1 fusion.17
  61.7 2.4 collective-permute-start.9
  64.2 4.1 %collective-permute-done.9 = f32[128,128]{1,0:T(8,128)S(1)} collective-permute-done((f32[128,128]{1,0:T(8,128)S(1)}, f32[128,128]{1,0:T(8,128)S(1)}, u32[]{:S(2)}, u32[]{:S(2)}) %collective-permute-start.9) | collective-permute-done | bytes 65568 | tf_op jit(solution)/shard_map/ppermute | solution.py:23
  69.0 2.5 gather_fusion.4
  76.6 2.4 collective-permute-start.11
  79.0 4.1 %collective-permute-done.11 = f32[128,128]{1,0:T(8,128)S(1)} collective-permute-done((f32[128,128]{1,0:T(8,128)S(1)}, f32[128,128]{1,0:T(8,128)S(1)}, u32[]{:S(2)}, u32[]{:S(2)}) %collective-permute-start.11) | collective-permute-done | bytes 65568 | tf_op jit(solution)/shard_map/ppermute | solution.py:23
  83.8 2.5 gather_fusion.5
  91.4 2.4 collective-permute-start.13
  93.8 4.1 %collective-permute-done.13 = f32[128,128]{1,0:T(8,128)S(1)} collective-permute-done((f32[128,128]{1,0:T(8,128)S(1)}, f32[128,128]{1,0:T(8,128)S(1)}, u32[]{:S(2)}, u32[]{:S(2)}) %collective-permute-start.13) | collective-permute-done | bytes 65568 | tf_op jit(solution)/shard_map/ppermute | solution.py:23
  98.6 2.5 gather_fusion.6
  101.1 2.1 fusion.20
  106.2 2.6 collective-permute-start.15
  109.5 3.2 collective-permute-done.15
  113.5 2.5 gather_fusion.7
  118.1 7.1 %fusion.24 = bf16[512,128]{1,0:T(8,128)(2,1)S(1)} fusion(f32[512,128]{1,0:T(8,128)} %copy-done.5, f32[8,128,64]{1,2,0:T(8,128)S(1)} %fusion.21, f32[512,128]{1,0:T(8,128)} %copy-done.6, f32[512,128]{1,0:T(8,128)} %copy-done.4, f32[512,128]{1,0:T(8,128)} %copy-done.3, f32[512,128]{1,0:T(8,128)} %copy-done.2, f32[512,128]{1,0:T(8,128)S(1)} %bitcast_subtract_fusion.6, ...), kind=kLoop, calls=%fused_computation.49 | loop fusion | flops 1245184 | bytes 2490404 | tf_op jit(solution)/shard_map/convert_element_type | solution.py:66
  125.1 8.5 %convolution_convert_fusion = bf16[512,3072]{1,0:T(8,128)(2,1)} fusion(bf16[1024,3072]{1,0:T(8,128)(2,1)} %param.18, bf16[512,1024]{1,0:T(8,128)(2,1)} %param.10, bf16[512,128]{1,0:T(8,128)(2,1)S(1)} %fusion.24, bf16[128,1024]{1,0:T(8,128)(2,1)} %param.17), kind=kOutput, calls=%fused_computation.16 | convolution fusion | flops 3358588928 | bytes 10878976 | tf_op jit(solution)/shard_map/dot_general | solution.py:69
  136.9 6.1 %collective-permute-done.16 = bf16[128,2048]{1,0:T(8,128)(2,1)S(1)} collective-permute-done((bf16[128,2048]{1,0:T(8,128)(2,1)S(1)}, bf16[128,2048]{1,0:T(8,128)(2,1)S(1)}, u32[]{:S(2)}, u32[]{:S(2)}) %collective-permute-start.16) | collective-permute-done | bytes 524320 | tf_op jit(solution)/shard_map/ppermute | solution.py:22
  143.8 4.1 %fusion.27 = (bf16[512,2048]{1,0:T(8,128)(2,1)}, bf16[2816,2048]{1,0:T(8,128)(2,1)}) fusion(bf16[512,3072]{1,0:T(8,128)(2,1)} %convolution_convert_fusion, bf16[2816,2048]{1,0:T(8,128)(2,1)} %constant_dynamic-update-slice_fusion.6), kind=kLoop, calls=%fused_computation.73 | loop fusion | bytes 6291456 | tf_op jit(solution)/shard_map/slice | solution.py:71
  150.4 2.5 collective-permute-start.21
  152.9 2.8 collective-permute-start.17
  155.9 2.3 slice.172
  158.2 4.0 %reshape.199 = bf16[8,64,16,64]{3,2,1,0:T(8,128)(2,1)} reshape(bf16[512,1024]{1,0:T(8,128)(2,1)} %slice.172) | data formatting | bytes 2097152 | tf_op jit(solution)/shard_map/reshape | solution.py:90
  162.2 87.3 %collective-permute-done.17 = bf16[128,2048]{1,0:T(8,128)(2,1)S(1)} collective-permute-done((bf16[128,2048]{1,0:T(8,128)(2,1)S(1)}, bf16[128,2048]{1,0:T(8,128)(2,1)S(1)}, u32[]{:S(2)}, u32[]{:S(2)}) %collective-permute-start.17) | collective-permute-done | bytes 524320 | tf_op jit(solution)/shard_map/ppermute | solution.py:23
  250.3 3.2 constant_dynamic-update-slice_fusion.3
  253.5 3.1 constant_dynamic-update-slice_fusion.2
  256.7 3.2 constant_dynamic-update-slice_fusion.1
  259.9 3.1 constant_dynamic-update-slice_fusion
  263.0 11.9 %gather_fusion.8 = bf16[64,64,2048]{2,1,0:T(8,128)(2,1)} fusion(bf16[44,64,2048]{2,1,0:T(8,128)(2,1)} %bitcast.61, s32[1024]{0:T(1024)S(1)} %pad_clamp_fusion), kind=kCustom, calls=%fused_computation.8 | custom fusion | bytes 33554688 | tf_op jit(solution)/shard_map/gather | solution.py:87
  274.9 11.7 %fusion.26 = (bf16[8,512,1024]{2,1,0:T(8,128)(2,1)}, bf16[8,512,1024]{2,1,0:T(8,128)(2,1)}) fusion(bf16[8,512,2048]{2,1,0:T(8,128)(2,1)} %bitcast.146), kind=kLoop, calls=%fused_computation.72 | loop fusion | bytes 33554432 | tf_op jit(solution)/shard_map/slice | solution.py:88
  286.6 11.4 %copy.33 = bf16[8,512,1024]{1,2,0:T(8,128)(2,1)} copy(bf16[8,512,1024]{2,1,0:T(8,128)(2,1)} %get-tuple-element.5) | data formatting | bytes 16777216
  298.0 11.4 %copy.32 = bf16[8,512,1024]{1,2,0:T(8,128)(2,1)} copy(bf16[8,512,1024]{2,1,0:T(8,128)(2,1)} %get-tuple-element.6) | data formatting | bytes 16777216
  309.4 10.9 %fusion.38 = (f32[8,16,64]{2,1,0:T(8,128)S(1)}, f32[8,16,64,512]{3,2,1,0:T(8,128)}) fusion(bf16[8,512,16,64]{1,3,2,0:T(8,128)(2,1)} %bitcast.147, bf16[8,64,16,64]{3,2,1,0:T(8,128)(2,1)} %reshape.199), kind=kOutput, calls=%fused_computation.84 | convolution fusion | flops 549454336 | bytes 26247168 | tf_op jit(solution)/shard_map/sub | solution.py:93
  320.3 11.0 %convert_bitcast_fusion = bf16[8,64,16,64]{1,3,2,0:T(8,128)(2,1)} fusion(bf16[8,512,16,64]{1,3,2,0:T(8,128)(2,1)} %bitcast.148, f32[8,16,64,512]{3,2,1,0:T(8,128)} %get-tuple-element.37, f32[8,16,64]{2,1,0:T(8,128)S(1)} %get-tuple-element.36), kind=kOutput, calls=%fused_computation.18 | convolution fusion | flops 545783808 | bytes 26247168 | tf_op jit(solution)/shard_map/bhqk,bkhd->bqhd/dot_general | solution.py:94
  331.3 4.4 %copy.23 = bf16[8,64,16,64]{3,2,1,0:T(8,128)(2,1)} copy(bf16[8,64,16,64]{1,3,2,0:T(8,128)(2,1)} %convert_bitcast_fusion) | data formatting | bytes 2097152 | tf_op jit(solution)/shard_map/convert_element_type | solution.py:95
  335.7 4.1 %convert_element_type.32 = bf16[512,1024]{1,0:T(8,128)(2,1)} reshape(bf16[8,64,16,64]{3,2,1,0:T(8,128)(2,1)} %copy.23) | data formatting | bytes 2097152 | tf_op jit(solution)/shard_map/convert_element_type | solution.py:95
  339.8 3.4 %convolution_convert_fusion.1 = bf16[512,1024]{1,0:T(8,128)(2,1)} fusion(bf16[512,1024]{1,0:T(8,128)(2,1)} %convert_element_type.32, bf16[1024,1024]{1,0:T(8,128)(2,1)S(1)} %copy-done), kind=kOutput, calls=%fused_computation.23 | convolution fusion | flops 1074266112 | bytes 4194304 | tf_op jit(solution)/shard_map/dot_general | solution.py:96
  (88 shorter events, 46.1 us)
Async XLA Ops:
  0.0 339.8 %copy-start = (bf16[1024,1024]{1,0:T(8,128)(2,1)S(1)}, bf16[1024,1024]{1,0:T(8,128)(2,1)}, u32[]{:S(2)}) copy-start(bf16[1024,1024]{1,0:T(8,128)(2,1)} %param.19) | copy-start | bytes 6291460
  0.0 43.7 %copy-start.1 = (f32[8,3,64,64]{3,2,1,0:T(8,128)S(1)}, f32[8,3,64,64]{3,2,1,0:T(8,128)}, u32[]{:S(2)}) copy-start(f32[8,3,64,64]{3,2,1,0:T(8,128)} %param.12) | copy-start | bytes 1179652
  1.0 6.5 %collective-permute-start = (f32[128,128]{1,0:T(8,128)S(1)}, f32[128,128]{1,0:T(8,128)S(1)}, u32[]{:S(2)}, u32[]{:S(2)}) collective-permute-start(f32[128,128]{1,0:T(8,128)S(1)} %get-tuple-element.25), channel_id=1, source_target_pairs={{0,1},{1,2},{2,3},{3,4},{4,5},{5,6},{6,7},{7,8},{8,9},{9,10},{10,1... | collective-permute-start | bytes 196616 | tf_op jit(solution)/shard_map/ppermute | solution.py:22
  4.8 6.5 %collective-permute-start.1 = (f32[128,128]{1,0:T(8,128)S(1)}, f32[128,128]{1,0:T(8,128)S(1)}, u32[]{:S(2)}, u32[]{:S(2)}) collective-permute-start(f32[128,128]{1,0:T(8,128)S(1)} %get-tuple-element.26), channel_id=1, source_target_pairs={{1,0},{2,1},{3,2},{4,3},{5,4},{6,5},{7,6},{8,7},{9,8},{10,9},{11,1... | collective-permute-start | bytes 196616 | tf_op jit(solution)/shard_map/ppermute | solution.py:23
  16.1 6.6 %collective-permute-start.3 = (f32[128,128]{1,0:T(8,128)S(1)}, f32[128,128]{1,0:T(8,128)S(1)}, u32[]{:S(2)}, u32[]{:S(2)}) collective-permute-start(f32[128,128]{1,0:T(8,128)S(1)} %bitcast.168), channel_id=1, source_target_pairs={{1,0},{2,1},{3,2},{4,3},{5,4},{6,5},{7,6},{8,7},{9,8},{10,9},{11,1... | collective-permute-start | bytes 196616 | tf_op jit(solution)/shard_map/ppermute | solution.py:23
  18.0 5.9 %collective-permute-start.2 = (f32[128,128]{1,0:T(8,128)S(1)}, f32[128,128]{1,0:T(8,128)S(1)}, u32[]{:S(2)}, u32[]{:S(2)}) collective-permute-start(f32[128,128]{1,0:T(8,128)S(1)} %bitcast.167), channel_id=1, source_target_pairs={{0,1},{1,2},{2,3},{3,4},{4,5},{5,6},{6,7},{7,8},{8,9},{9,10},{10,1... | collective-permute-start | bytes 196616 | tf_op jit(solution)/shard_map/ppermute | solution.py:22
  28.8 7.1 %collective-permute-start.4 = (f32[128,128]{1,0:T(8,128)S(1)}, f32[128,128]{1,0:T(8,128)S(1)}, u32[]{:S(2)}, u32[]{:S(2)}) collective-permute-start(f32[128,128]{1,0:T(8,128)S(1)} %get-tuple-element.21), channel_id=1, source_target_pairs={{0,1},{1,2},{2,3},{3,4},{4,5},{5,6},{6,7},{7,8},{8,9},{9,10},{10,1... | collective-permute-start | bytes 196616 | tf_op jit(solution)/shard_map/ppermute | solution.py:22
  34.0 6.5 %collective-permute-start.5 = (f32[128,128]{1,0:T(8,128)S(1)}, f32[128,128]{1,0:T(8,128)S(1)}, u32[]{:S(2)}, u32[]{:S(2)}) collective-permute-start(f32[128,128]{1,0:T(8,128)S(1)} %get-tuple-element.22), channel_id=1, source_target_pairs={{1,0},{2,1},{3,2},{4,3},{5,4},{6,5},{7,6},{8,7},{9,8},{10,9},{11,1... | collective-permute-start | bytes 196616 | tf_op jit(solution)/shard_map/ppermute | solution.py:23
  45.9 8.4 %copy-start.2 = (f32[512,128]{1,0:T(8,128)}, f32[512,128]{1,0:T(8,128)S(1)}, u32[]{:S(2)}) copy-start(f32[512,128]{1,0:T(8,128)S(1)} %bitcast_subtract_fusion.5) | copy-start | bytes 786436
  45.9 4.3 %collective-permute-start.6 = (f32[128,128]{1,0:T(8,128)S(1)}, f32[128,128]{1,0:T(8,128)S(1)}, u32[]{:S(2)}, u32[]{:S(2)}) collective-permute-start(f32[128,128]{1,0:T(8,128)S(1)} %get-tuple-element.19), channel_id=1, source_target_pairs={{0,1},{1,2},{2,3},{3,4},{4,5},{5,6},{6,7},{7,8},{8,9},{9,10},{10,1... | collective-permute-start | bytes 196616 | tf_op jit(solution)/shard_map/ppermute | solution.py:22
  47.8 6.5 %collective-permute-start.7 = (f32[128,128]{1,0:T(8,128)S(1)}, f32[128,128]{1,0:T(8,128)S(1)}, u32[]{:S(2)}, u32[]{:S(2)}) collective-permute-start(f32[128,128]{1,0:T(8,128)S(1)} %get-tuple-element.20), channel_id=1, source_target_pairs={{1,0},{2,1},{3,2},{4,3},{5,4},{6,5},{7,6},{8,7},{9,8},{10,9},{11,1... | collective-permute-start | bytes 196616 | tf_op jit(solution)/shard_map/ppermute | solution.py:23
  59.7 49.1 %copy-start.7 = (f32[9]{0:T(128)S(1)}, f32[9]{0:T(128)}, u32[]{:S(2)}) copy-start(f32[9]{0:T(128)} %param.16) | copy-start | bytes 112
  59.8 8.4 %copy-start.3 = (f32[512,128]{1,0:T(8,128)}, f32[512,128]{1,0:T(8,128)S(1)}, u32[]{:S(2)}) copy-start(f32[512,128]{1,0:T(8,128)S(1)} %bitcast_subtract_fusion.4) | copy-start | bytes 786436
  59.8 4.3 %collective-permute-start.8 = (f32[128,128]{1,0:T(8,128)S(1)}, f32[128,128]{1,0:T(8,128)S(1)}, u32[]{:S(2)}, u32[]{:S(2)}) collective-permute-start(f32[128,128]{1,0:T(8,128)S(1)} %get-tuple-element.17), channel_id=1, source_target_pairs={{0,1},{1,2},{2,3},{3,4},{4,5},{5,6},{6,7},{7,8},{8,9},{9,10},{10,1... | collective-permute-start | bytes 196616 | tf_op jit(solution)/shard_map/ppermute | solution.py:22
  61.7 6.5 %collective-permute-start.9 = (f32[128,128]{1,0:T(8,128)S(1)}, f32[128,128]{1,0:T(8,128)S(1)}, u32[]{:S(2)}, u32[]{:S(2)}) collective-permute-start(f32[128,128]{1,0:T(8,128)S(1)} %get-tuple-element.18), channel_id=1, source_target_pairs={{1,0},{2,1},{3,2},{4,3},{5,4},{6,5},{7,6},{8,7},{9,8},{10,9},{11,1... | collective-permute-start | bytes 196616 | tf_op jit(solution)/shard_map/ppermute | solution.py:23
  74.6 8.4 %copy-start.4 = (f32[512,128]{1,0:T(8,128)}, f32[512,128]{1,0:T(8,128)S(1)}, u32[]{:S(2)}) copy-start(f32[512,128]{1,0:T(8,128)S(1)} %bitcast_subtract_fusion.3) | copy-start | bytes 786436
  74.6 4.3 %collective-permute-start.10 = (f32[128,128]{1,0:T(8,128)S(1)}, f32[128,128]{1,0:T(8,128)S(1)}, u32[]{:S(2)}, u32[]{:S(2)}) collective-permute-start(f32[128,128]{1,0:T(8,128)S(1)} %get-tuple-element.15), channel_id=1, source_target_pairs={{0,1},{1,2},{2,3},{3,4},{4,5},{5,6},{6,7},{7,8},{8,9},{9,10},{10,1... | collective-permute-start | bytes 196616 | tf_op jit(solution)/shard_map/ppermute | solution.py:22
  76.6 6.5 %collective-permute-start.11 = (f32[128,128]{1,0:T(8,128)S(1)}, f32[128,128]{1,0:T(8,128)S(1)}, u32[]{:S(2)}, u32[]{:S(2)}) collective-permute-start(f32[128,128]{1,0:T(8,128)S(1)} %get-tuple-element.16), channel_id=1, source_target_pairs={{1,0},{2,1},{3,2},{4,3},{5,4},{6,5},{7,6},{8,7},{9,8},{10,9},{11,1... | collective-permute-start | bytes 196616 | tf_op jit(solution)/shard_map/ppermute | solution.py:23
  89.4 8.4 %copy-start.5 = (f32[512,128]{1,0:T(8,128)}, f32[512,128]{1,0:T(8,128)S(1)}, u32[]{:S(2)}) copy-start(f32[512,128]{1,0:T(8,128)S(1)} %bitcast_subtract_fusion.2) | copy-start | bytes 786436
  89.5 4.3 %collective-permute-start.12 = (f32[128,128]{1,0:T(8,128)S(1)}, f32[128,128]{1,0:T(8,128)S(1)}, u32[]{:S(2)}, u32[]{:S(2)}) collective-permute-start(f32[128,128]{1,0:T(8,128)S(1)} %get-tuple-element.13), channel_id=1, source_target_pairs={{0,1},{1,2},{2,3},{3,4},{4,5},{5,6},{6,7},{7,8},{8,9},{9,10},{10,1... | collective-permute-start | bytes 196616 | tf_op jit(solution)/shard_map/ppermute | solution.py:22
  91.4 6.5 %collective-permute-start.13 = (f32[128,128]{1,0:T(8,128)S(1)}, f32[128,128]{1,0:T(8,128)S(1)}, u32[]{:S(2)}, u32[]{:S(2)}) collective-permute-start(f32[128,128]{1,0:T(8,128)S(1)} %get-tuple-element.14), channel_id=1, source_target_pairs={{1,0},{2,1},{3,2},{4,3},{5,4},{6,5},{7,6},{8,7},{9,8},{10,9},{11,1... | collective-permute-start | bytes 196616 | tf_op jit(solution)/shard_map/ppermute | solution.py:23
  104.2 8.4 %copy-start.6 = (f32[512,128]{1,0:T(8,128)}, f32[512,128]{1,0:T(8,128)S(1)}, u32[]{:S(2)}) copy-start(f32[512,128]{1,0:T(8,128)S(1)} %bitcast_subtract_fusion.1) | copy-start | bytes 786436
  104.3 5.2 %collective-permute-start.14 = (f32[128,128]{1,0:T(8,128)S(1)}, f32[128,128]{1,0:T(8,128)S(1)}, u32[]{:S(2)}, u32[]{:S(2)}) collective-permute-start(f32[128,128]{1,0:T(8,128)S(1)} %get-tuple-element.11), channel_id=1, source_target_pairs={{0,1},{1,2},{2,3},{3,4},{4,5},{5,6},{6,7},{7,8},{8,9},{9,10},{10,1... | collective-permute-start | bytes 196616 | tf_op jit(solution)/shard_map/ppermute | solution.py:22
  106.2 6.5 %collective-permute-start.15 = (f32[128,128]{1,0:T(8,128)S(1)}, f32[128,128]{1,0:T(8,128)S(1)}, u32[]{:S(2)}, u32[]{:S(2)}) collective-permute-start(f32[128,128]{1,0:T(8,128)S(1)} %get-tuple-element.12), channel_id=1, source_target_pairs={{1,0},{2,1},{3,2},{4,3},{5,4},{6,5},{7,6},{8,7},{9,8},{10,9},{11,1... | collective-permute-start | bytes 196616 | tf_op jit(solution)/shard_map/ppermute | solution.py:23
  133.7 19.2 %copy-start.8 = (s32[8,3]{0,1:T(4,128)S(1)}, s32[8,3]{0,1:T(4,128)}, u32[]{:S(2)}) copy-start(s32[8,3]{0,1:T(4,128)} %param.14) | copy-start | bytes 292
  133.7 22.0 %copy-start.9 = (s32[8,4]{0,1:T(4,128)S(1)}, s32[8,4]{0,1:T(4,128)}, u32[]{:S(2)}) copy-start(s32[8,4]{0,1:T(4,128)} %param.15) | copy-start | bytes 388
  135.0 8.0 %collective-permute-start.16 = (bf16[128,2048]{1,0:T(8,128)(2,1)S(1)}, bf16[128,2048]{1,0:T(8,128)(2,1)S(1)}, u32[]{:S(2)}, u32[]{:S(2)}) collective-permute-start(bf16[128,2048]{1,0:T(8,128)(2,1)S(1)} %get-tuple-element.10), channel_id=1, source_target_pairs={{0,1},{1,2},{2,3},{3,4},{4,5},{5,6},{6,7},{7,8},{8,9},{9,10},{10,1... | collective-permute-start | bytes 1572872 | tf_op jit(solution)/shard_map/ppermute | solution.py:22
  147.9 102.4 %collective-permute-start.18 = (bf16[512,2048]{1,0:T(8,128)(2,1)}, bf16[512,2048]{1,0:T(8,128)(2,1)}, u32[]{:S(2)}, u32[]{:S(2)}) collective-permute-start(bf16[512,2048]{1,0:T(8,128)(2,1)} %get-tuple-element.7), channel_id=1, source_target_pairs={{0,1},{1,0},{2,3},{3,2},{4,5},{5,4},{6,7},{7,6},{8,9},{9,8},{10,11... | collective-permute-start | bytes 6291464 | tf_op jit(solution)/shard_map/ppermute | solution.py:31
  148.3 105.2 %collective-permute-start.19 = (bf16[512,2048]{1,0:T(8,128)(2,1)}, bf16[512,2048]{1,0:T(8,128)(2,1)}, u32[]{:S(2)}, u32[]{:S(2)}) collective-permute-start(bf16[512,2048]{1,0:T(8,128)(2,1)} %get-tuple-element.7), channel_id=1, source_target_pairs={{0,2},{1,3},{2,0},{3,1},{4,6},{5,7},{6,4},{7,5},{8,10},{9,11},{10,... | collective-permute-start | bytes 6291464 | tf_op jit(solution)/shard_map/ppermute | solution.py:31
  150.4 106.2 %collective-permute-start.20 = (bf16[512,2048]{1,0:T(8,128)(2,1)}, bf16[512,2048]{1,0:T(8,128)(2,1)}, u32[]{:S(2)}, u32[]{:S(2)}) collective-permute-start(bf16[512,2048]{1,0:T(8,128)(2,1)} %get-tuple-element.7), channel_id=1, source_target_pairs={{0,4},{1,5},{2,6},{3,7},{4,0},{5,1},{6,2},{7,3},{8,12},{9,13},{10,... | collective-permute-start | bytes 6291464 | tf_op jit(solution)/shard_map/ppermute | solution.py:31
  150.4 109.5 %collective-permute-start.21 = (bf16[512,2048]{1,0:T(8,128)(2,1)}, bf16[512,2048]{1,0:T(8,128)(2,1)}, u32[]{:S(2)}, u32[]{:S(2)}) collective-permute-start(bf16[512,2048]{1,0:T(8,128)(2,1)} %get-tuple-element.7), channel_id=1, source_target_pairs={{0,8},{1,9},{2,10},{3,11},{4,12},{5,13},{6,14},{7,15},{8,0},{9,1},... | collective-permute-start | bytes 6291464 | tf_op jit(solution)/shard_map/ppermute | solution.py:31
  152.9 96.6 %collective-permute-start.17 = (bf16[128,2048]{1,0:T(8,128)(2,1)S(1)}, bf16[128,2048]{1,0:T(8,128)(2,1)S(1)}, u32[]{:S(2)}, u32[]{:S(2)}) collective-permute-start(bf16[128,2048]{1,0:T(8,128)(2,1)S(1)} %get-tuple-element.9), channel_id=1, source_target_pairs={{1,0},{2,1},{3,2},{4,3},{5,4},{6,5},{7,6},{8,7},{9,8},{10,9},{11,1... | collective-permute-start | bytes 1572872 | tf_op jit(solution)/shard_map/ppermute | solution.py:23
where the time goes:
time: 346 us; the launch traced here: 343 us
  waiting for transfers between devices  122 us (35%)
  local copies, waits for them, and re-layouts  101 us (29%)
  matrix products  51.4 us (15%)
  starting transfers between devices  50.7 us (15%)
  other arithmetic  17.5 us (5%)
    ppermute x9, waiting for transfers between devices, extended(): after = lax.ppermute(first, axis, down)  115 us
    unnamed x27, local copies, waits for them, and re-layouts  34.1 us
    ppermute x9, starting transfers between devices, extended(): before = lax.ppermute(last, axis, up)  25 us
    ppermute x9, starting transfers between devices, extended(): after = lax.ppermute(first, axis, down)  20.7 us
    gather x8, local copies, waits for them, and re-layouts, apply_operator(): picked = pooled[position]  17.8 us
    dot_general x8, matrix products, apply_operator(): jnp.einsum('bjst,bjtc->bsc', op_blocks, picked, precision=lax.Precision.H...  17.6 us
    gather x1, local copies, waits for them, and re-layouts, on_device(): picked = pool_blocks[key_slots].reshape(count, -1, 2 * D)  11.9 us
    slice x1, local copies, waits for them, and re-layouts, on_device(): keys = picked[:, :, :D].reshape(count, -1, HEADS, HD)  11.7 us
  transfers between devices with their start and end apart: 22, of which 11 were waited for; matrix products, arithmetic and copies ran while one was open for 5% of the time, Pallas kernels for 0%

commit v1 on v0

v1 whole, which is shorter than its diff:
```python
import functools

import jax
import jax.numpy as jnp
from jax import lax
from jax.experimental import pallas as pl
from jax.experimental.pallas import tpu as pltpu
from jax.sharding import PartitionSpec as P

D = 1024
HEADS = 16
HD = 64
BS = 64
DEG = 8
NEXP = 4
REACH = 2
NKEY = 1 + 3 + NEXP


def shift_rows(x, axis, step):
    peers = lax.axis_size(axis)
    if step > 0:
        pairs = [(i, i + step) for i in range(peers - step)]
    else:
        pairs = [(i, i + step) for i in range(-step, peers)]
    return lax.ppermute(x, axis, pairs)


def extended(x, axis, width):
    length = x.shape[0]
    before = shift_rows(x[length - width:], axis, 1)
    after = shift_rows(x[:width], axis, -1)
    return jnp.concatenate([before, x, after], axis=0)


def partner(value, axis, distance):
    mask = 2**distance
    pairs = [(source, source ^ mask) for source in range(lax.axis_size(axis))]
    return lax.ppermute(value, axis, pairs)


def apply_operator(field, op_blocks, laplace_index, first_block):
    count = op_blocks.shape[0]
    padded = extended(field, "seq", REACH * BS)
    pooled = padded.reshape(count + 2 * REACH, BS, field.shape[1])
    position = laplace_index - first_block + REACH
    picked = pooled[position]
    result = jnp.einsum("bjst,bjtc->bsc", op_blocks, picked, precision=lax.Precision.HIGHEST)
    return result.reshape(field.shape)


def attention_kernel(table_ref, q_ref, *refs):
    kv_refs = refs[:NKEY]
    out_ref = refs[NKEY]
    scale = 1.0 / HD**0.5
    lane = lax.broadcasted_iota(jnp.int32, (1, 2 * HD), 1)
    low = lane < HD
    for pair in range(HEADS // 2):
        cols = slice(pair * 2 * HD, (pair + 1) * 2 * HD)
        vcols = slice(D + pair * 2 * HD, D + (pair + 1) * 2 * HD)
        qs = q_ref[:, cols]
        ks = jnp.concatenate([r[:, cols] for r in kv_refs], axis=0)
        vs = jnp.concatenate([r[:, vcols] for r in kv_refs], axis=0)
        merged = None
        for half in range(2):
            keep = low if half == 0 else jnp.logical_not(low)
            qm = jnp.where(keep, qs, jnp.zeros_like(qs))
            scores = lax.dot_general(
                qm, ks, (((1,), (1,)), ((), ())), preferred_element_type=jnp.float32
            ) * scale
            top = jnp.max(scores, axis=-1, keepdims=True)
            expd = jnp.exp(scores - top)
            total = jnp.sum(expd, axis=-1, keepdims=True)
            weights = (expd / total).astype(jnp.bfloat16)
            part = jnp.dot(weights, vs, preferred_element_type=jnp.float32)
            merged = part if half == 0 else jnp.where(low, merged, part)
        out_ref[:, cols] = merged.astype(jnp.bfloat16)


def attend(queries, kv_sources, table):
    count = table.shape[0]
    in_specs = [pl.BlockSpec((BS, D), lambda b, t: (b, 0))]
    operands = [queries]
    for j, src in enumerate(kv_sources):
        in_specs.append(pl.BlockSpec((BS, 2 * D), lambda b, t, j=j: (t[b, j], 0)))
        operands.append(src)
    grid_spec = pltpu.PrefetchScalarGridSpec(
        num_scalar_prefetch=1,
        grid=(count,),
        in_specs=in_specs,
        out_specs=pl.BlockSpec((BS, D), lambda b, t: (b, 0)),
    )
    return pl.pallas_call(
        attention_kernel,
        grid_spec=grid_spec,
        out_shape=jax.ShapeDtypeStruct((count * BS, D), jnp.bfloat16),
    )(table, *operands)


def on_device(
    node_feats,
    struct_feats,
    op_blocks,
    laplace_index,
    graph_links,
    expander_slot,
    series_coef,
    encode_weight,
    qkv_weight,
    out_weight,
):
    count = op_blocks.shape[0]
    rows = count * BS
    rim = REACH * BS
    first_block = lax.axis_index("seq") * count
    levels = lax.axis_size("seq").bit_length() - 1
    bits = [link * (levels - 1) // (NEXP - 1) for link in range(NEXP)]

    feats_before = shift_rows(node_feats[rows - rim:], "seq", 1)
    feats_after = shift_rows(node_feats[:rim], "seq", -1)
    feats_far = [partner(node_feats, "seq", bit) for bit in bits]

    previous = struct_feats
    current = apply_operator(previous, op_blocks, laplace_index, first_block)
    encoding = series_coef[0] * previous + series_coef[1] * current
    for degree in range(2, DEG + 1):
        following = 2.0 * apply_operator(current, op_blocks, laplace_index, first_block) - previous
        encoding = encoding + series_coef[degree] * following
        previous, current = (current, following)
    encoding_b = encoding.astype(jnp.bfloat16)

    enc_before = shift_rows(encoding_b[rows - rim:], "seq", 1)
    enc_after = shift_rows(encoding_b[:rim], "seq", -1)
    enc_far = [partner(encoding_b, "seq", bit) for bit in bits]

    def blend(feats, enc):
        encoded = jnp.dot(enc, encode_weight, preferred_element_type=jnp.float32)
        return (feats.astype(jnp.float32) + encoded).astype(jnp.bfloat16)

    kv_weight = qkv_weight[:, D:]
    blended = blend(node_feats, encoding_b)
    queries = jnp.dot(blended, qkv_weight[:, :D], preferred_element_type=jnp.float32).astype(
        jnp.bfloat16
    )
    near_blended = jnp.concatenate(
        [blend(feats_before, enc_before), blended, blend(feats_after, enc_after)], axis=0
    )
    kv_near = jnp.dot(near_blended, kv_weight, preferred_element_type=jnp.float32).astype(
        jnp.bfloat16
    )
    kv_far = [
        jnp.dot(blend(f, e), kv_weight, preferred_element_type=jnp.float32).astype(jnp.bfloat16)
        for f, e in zip(feats_far, enc_far)
    ]

    near_blocks = count + 2 * REACH
    own_slot = jnp.arange(count, dtype=jnp.int32)[:, None] + REACH
    graph_slot = jnp.clip(graph_links - first_block + REACH, 0, near_blocks - 1)
    far_slot = jnp.clip(expander_slot, 0, count - 1)
    table = jnp.concatenate([own_slot, graph_slot, far_slot], axis=1).astype(jnp.int32)
    sources = [kv_near] * 4 + kv_far
    attended = attend(queries, sources, table)
    return jnp.dot(attended, out_weight, preferred_element_type=jnp.float32).astype(jnp.bfloat16)


def solution(mesh):
    placed = (
        P(("group", "seq"), None),
        P(("group", "seq"), None),
        P(("group", "seq"), None, None, None),
        P(("group", "seq"), None),
        P(("group", "seq"), None),
        P(("group", "seq"), None),
        P(),
        P(),
        P(),
        P(),
    )
    return jax.shard_map(
        on_device, mesh=mesh, in_specs=placed, out_specs=P(("group", "seq"), None), check_vma=False
    )
```

time: 346 us -> 281 us (0.81)
  the two profiles are of different devices: /device:TPU:15 before, /device:TPU:0 now
where the time goes in v1:
time: 281 us; the launch traced here: 280 us
  starting transfers between devices  115 us (41%)
  matrix products  59.4 us (21%)
  Pallas kernels  48.3 us (17%)
  local copies, waits for them, and re-layouts  25.8 us (9%)
  other arithmetic  18.9 us (7%)
  waiting for transfers between devices  11.5 us (4%)
    ppermute x20, starting transfers between devices, shift_rows(): return lax.ppermute(x, axis, pairs)  83 us
    pallas_call x1, Pallas kernels, attend(): pl.pallas_call(attention_kernel, grid_spec=grid_spec, out_shape=jax.Shape...  48.3 us
    ppermute x8, starting transfers between devices, partner(): return lax.ppermute(value, axis, pairs)  32.1 us
    dot_general x4, matrix products, on_device(): jnp.dot(blend(f, e), kv_weight, preferred_element_type=jnp.float32)  25.8 us
    gather x8, local copies, waits for them, and re-layouts, apply_operator(): picked = pooled[position]  18.8 us
    dot_general x8, matrix products, apply_operator(): jnp.einsum('bjst,bjtc->bsc', op_blocks, picked, precision=lax.Precision.H...  17.2 us
    ppermute x20, waiting for transfers between devices, shift_rows(): return lax.ppermute(x, axis, pairs)  11.4 us
    concatenate x8, other arithmetic, extended(): return jnp.concatenate([before, x, after], axis=0)  7.37 us
  transfers between devices with their start and end apart: 28, of which 6 were waited for; matrix products, arithmetic and copies ran while one was open for 31% of the time, Pallas kernels for 0%

profile of v1, /device:TPU:0, one launch (start us, length us, event | category | flops | bytes accessed | tf_op | source)
XLA Modules:
  0.0 279.6 jit_solution(11324100321038896226)
XLA Ops:
  1.0 2.4 collective-permute-start
  5.6 3.1 %collective-permute-done.1 = f32[128,128]{1,0:T(8,128)S(1)} collective-permute-done((f32[128,128]{1,0:T(8,128)S(1)}, f32[128,128]{1,0:T(8,128)S(1)}, u32[]{:S(2)}, u32[]{:S(2)}) %collective-permute-start.1) | collective-permute-done | bytes 65568 | tf_op jit(solution)/shard_map/ppermute | solution.py:26
  9.6 1.5 gather_fusion
  11.1 2.1 fusion.45
  13.3 4.8 %collective-permute-start.2 = (f32[128,128]{1,0:T(8,128)S(1)}, f32[128,128]{1,0:T(8,128)S(1)}, u32[]{:S(2)}, u32[]{:S(2)}) collective-permute-start(f32[128,128]{1,0:T(8,128)S(1)} %bitcast.156), channel_id=1, source_target_pairs={{0,1},{1,2},{2,3},{3,4},{4,5},{5,6},{6,7},{7,8},{8,9},{9,10},{10,1... | collective-permute-start | bytes 196616 | tf_op jit(solution)/shard_map/ppermute | solution.py:26
  18.1 1.3 collective-permute-start.3
  19.4 5.2 %collective-permute-start.26 = (bf16[512,1024]{1,0:T(8,128)(2,1)}, bf16[512,1024]{1,0:T(8,128)(2,1)}, u32[]{:S(2)}, u32[]{:S(2)}) collective-permute-start(bf16[512,1024]{1,0:T(8,128)(2,1)} %param.10), channel_id=1, source_target_pairs={{0,8},{1,9},{2,10},{3,11},{4,12},{5,13},{6,14},{7,15},{8,0},{9,1},... | collective-permute-start | bytes 3145736 | tf_op jit(solution)/shard_map/ppermute | solution.py:39
  24.7 1.6 collective-permute-start.24
  27.0 2.5 gather_fusion.1
  29.5 2.2 fusion.15
  35.9 1.8 fusion.34
  37.7 3.7 %collective-permute-start.16 = (bf16[128,1024]{1,0:T(8,128)(2,1)}, bf16[128,1024]{1,0:T(8,128)(2,1)}, u32[]{:S(2)}, u32[]{:S(2)}) collective-permute-start(bf16[128,1024]{1,0:T(8,128)(2,1)} %get-tuple-element.5), channel_id=1, source_target_pairs={{0,1},{1,2},{2,3},{3,4},{4,5},{5,6},{6,7},{7,8},{8,9},{9,10},{10,1... | collective-permute-start | bytes 786440 | tf_op jit(solution)/shard_map/ppermute | solution.py:26
  42.4 2.5 gather_fusion.2
  44.8 2.1 fusion.16
  48.4 3.4 %collective-permute-start.6 = (f32[128,128]{1,0:T(8,128)}, f32[128,128]{1,0:T(8,128)S(1)}, u32[]{:S(2)}, u32[]{:S(2)}) collective-permute-start(f32[128,128]{1,0:T(8,128)} %get-tuple-element.15), channel_id=1, source_target_pairs={{0,1},{1,2},{2,3},{3,4},{4,5},{5,6},{6,7},{7,8},{8,9},{9,10},{10,1... | collective-permute-start | bytes 196616 | tf_op jit(solution)/shard_map/ppermute | solution.py:26
  53.2 1.9 collective-permute-done.7
  55.1 1.7 pad_maximum_fusion.3
  56.9 2.5 gather_fusion.3
  59.3 2.1 fusion.17
  61.6 31.6 %collective-permute-start.8 = (f32[128,128]{1,0:T(8,128)S(1)}, f32[128,128]{1,0:T(8,128)S(1)}, u32[]{:S(2)}, u32[]{:S(2)}) collective-permute-start(f32[128,128]{1,0:T(8,128)S(1)} %get-tuple-element.13), channel_id=1, source_target_pairs={{0,1},{1,2},{2,3},{3,4},{4,5},{5,6},{6,7},{7,8},{8,9},{9,10},{10,1... | collective-permute-start | bytes 196616 | tf_op jit(solution)/shard_map/ppermute | solution.py:26
  94.5 3.3 %collective-permute-done.9 = f32[128,128]{1,0:T(8,128)S(1)} collective-permute-done((f32[128,128]{1,0:T(8,128)S(1)}, f32[128,128]{1,0:T(8,128)S(1)}, u32[]{:S(2)}, u32[]{:S(2)}) %collective-permute-start.9) | collective-permute-done | bytes 65568 | tf_op jit(solution)/shard_map/ppermute | solution.py:26
  98.6 2.5 gather_fusion.4
  101.1 2.1 fusion.18
  104.3 6.9 %collective-permute-start.10 = (f32[128,128]{1,0:T(8,128)S(1)}, f32[128,128]{1,0:T(8,128)S(1)}, u32[]{:S(2)}, u32[]{:S(2)}) collective-permute-start(f32[128,128]{1,0:T(8,128)S(1)} %get-tuple-element.11), channel_id=1, source_target_pairs={{0,1},{1,2},{2,3},{3,4},{4,5},{5,6},{6,7},{7,8},{8,9},{9,10},{10,1... | collective-permute-start | bytes 196616 | tf_op jit(solution)/shard_map/ppermute | solution.py:26
  115.1 2.5 gather_fusion.5
  117.6 2.1 fusion.19
  120.8 5.3 %collective-permute-start.12 = (f32[128,128]{1,0:T(8,128)S(1)}, f32[128,128]{1,0:T(8,128)S(1)}, u32[]{:S(2)}, u32[]{:S(2)}) collective-permute-start(f32[128,128]{1,0:T(8,128)S(1)} %get-tuple-element.9), channel_id=1, source_target_pairs={{0,1},{1,2},{2,3},{3,4},{4,5},{5,6},{6,7},{7,8},{8,9},{9,10},{10,1... | collective-permute-start | bytes 196616 | tf_op jit(solution)/shard_map/ppermute | solution.py:26
  127.4 1.8 collective-permute-done.13
  130.0 2.5 gather_fusion.6
  132.5 2.1 fusion.20
  135.6 5.3 %collective-permute-start.14 = (f32[128,128]{1,0:T(8,128)S(1)}, f32[128,128]{1,0:T(8,128)S(1)}, u32[]{:S(2)}, u32[]{:S(2)}) collective-permute-start(f32[128,128]{1,0:T(8,128)S(1)} %get-tuple-element.7), channel_id=1, source_target_pairs={{0,1},{1,2},{2,3},{3,4},{4,5},{5,6},{6,7},{7,8},{8,9},{9,10},{10,1... | collective-permute-start | bytes 196616 | tf_op jit(solution)/shard_map/ppermute | solution.py:26
  145.0 2.5 gather_fusion.7
  147.4 2.2 fusion.21
  149.6 6.9 %fusion.32 = bf16[512,128]{1,0:T(8,128)(2,1)S(1)} fusion(f32[512,128]{1,0:T(8,128)} %copy-done.5, f32[8,128,64]{1,2,0:T(8,128)S(1)} %fusion.21, f32[512,128]{1,0:T(8,128)} %copy-done.6, f32[512,128]{1,0:T(8,128)} %copy-done.4, f32[512,128]{1,0:T(8,128)} %copy-done.3, f32[512,128]{1,0:T(8,128)} %copy-done.2, f32[512,128]{1,0:T(8,128)S(1)} %bitcast_subtract_fusion.6, ...), kind=kLoop, calls=%fused_computation.63 | loop fusion | flops 1245184 | bytes 2490404 | tf_op jit(solution)/shard_map/convert_element_type | solution.py:130
  156.5 5.1 %collective-permute-start.17 = (bf16[128,128]{1,0:T(8,128)(2,1)S(1)}, bf16[128,128]{1,0:T(8,128)(2,1)S(1)}, u32[]{:S(2)}, u32[]{:S(2)}) collective-permute-start(bf16[128,128]{1,0:T(8,128)(2,1)S(1)} %get-tuple-element.23), channel_id=1, source_target_pairs={{0,1},{1,2},{2,3},{3,4},{4,5},{5,6},{6,7},{7,8},{8,9},{9,10},{10,1... | collective-permute-start | bytes 98312 | tf_op jit(solution)/shard_map/ppermute | solution.py:26
  161.7 1.8 add_convert_fusion.4
  163.5 4.0 %fusion.12.q_ref = bf16[512,1024]{1,0:T(8,128)(2,1)} fusion(bf16[512,1024]{1,0:T(8,128)(2,1)S(1)} %add_convert_fusion.4, bf16[1024,3072]{1,0:T(8,128)(2,1)} %param.18), kind=kOutput, calls=%fused_computation.30 | convolution fusion | flops 1074266112 | bytes 4194304 | tf_op jit(solution)/shard_map/dot_general | solution.py:142
  167.5 2.5 collective-permute-start.22
  170.0 1.5 collective-permute-start.19
  172.6 1.6 collective-permute-start.20
  176.5 4.9 %convolution_convert_fusion.refs_0_.refs_1_.refs_2_.refs_3_ = bf16[768,2048]{1,0:T(8,128)(2,1)} fusion(bf16[1024,3072]{1,0:T(8,128)(2,1)S(1)} %bitcast.158, bf16[128,1024]{1,0:T(8,128)(2,1)S(1)} %add_convert_fusion.9, bf16[512,1024]{1,0:T(8,128)(2,1)S(1)} %add_convert_fusion.4, bf16[128,1024]{1,0:T(8,128)(2,1)S(1)} %add_convert_fusion.10), kind=kOutput, calls=%fused_computation.8 | convolution fusion | flops 3227516928 | bytes 8912896 | tf_op jit(solution)/shard_map/dot_general | solution.py:148
  182.2 19.8 %collective-permute-start.23 = (bf16[512,128]{1,0:T(8,128)(2,1)S(1)}, bf16[512,128]{1,0:T(8,128)(2,1)S(1)}, u32[]{:S(2)}, u32[]{:S(2)}) collective-permute-start(bf16[512,128]{1,0:T(8,128)(2,1)S(1)} %fusion.32), channel_id=1, source_target_pairs={{0,2},{1,3},{2,0},{3,1},{4,6},{5,7},{6,4},{7,5},{8,10},{9,11},{10,... | collective-permute-start | bytes 393224 | tf_op jit(solution)/shard_map/ppermute | solution.py:39
  202.0 6.5 %convolution_convert_fusion.1.refs_7_ = bf16[512,2048]{1,0:T(8,128)(2,1)} fusion(bf16[1024,3072]{1,0:T(8,128)(2,1)} %param.18, bf16[512,1024]{1,0:T(8,128)(2,1)} %collective-permute-done.26, bf16[512,128]{1,0:T(8,128)(2,1)} %copy-done.12, bf16[128,1024]{1,0:T(8,128)(2,1)S(1)} %copy-done.8), kind=kOutput, calls=%fused_computation.9 | convolution fusion | flops 2284322816 | bytes 7733248 | tf_op jit(solution)/shard_map/dot_general | solution.py:152
  208.5 6.4 %convolution_convert_fusion.2.refs_6_ = bf16[512,2048]{1,0:T(8,128)(2,1)} fusion(bf16[1024,3072]{1,0:T(8,128)(2,1)} %param.18, bf16[512,1024]{1,0:T(8,128)(2,1)} %collective-permute-done.24, bf16[512,128]{1,0:T(8,128)(2,1)S(1)} %collective-permute-done.25, bf16[128,1024]{1,0:T(8,128)(2,1)S(1)} %copy-done.8), kind=kOutput, calls=%fused_computation.10 | convolution fusion | flops 2284322816 | bytes 7733248 | tf_op jit(solution)/shard_map/dot_general | solution.py:152
  214.9 6.5 %convolution_convert_fusion.3.refs_5_ = bf16[512,2048]{1,0:T(8,128)(2,1)} fusion(bf16[1024,3072]{1,0:T(8,128)(2,1)} %param.18, bf16[512,1024]{1,0:T(8,128)(2,1)} %collective-permute-done.22, bf16[512,128]{1,0:T(8,128)(2,1)S(1)} %collective-permute-done.23, bf16[128,1024]{1,0:T(8,128)(2,1)S(1)} %copy-done.8), kind=kOutput, calls=%fused_computation.11 | convolution fusion | flops 2284322816 | bytes 7733248 | tf_op jit(solution)/shard_map/dot_general | solution.py:152
  221.4 6.4 %convolution_convert_fusion.4.refs_4_ = bf16[512,2048]{1,0:T(8,128)(2,1)} fusion(bf16[1024,3072]{1,0:T(8,128)(2,1)} %param.18, bf16[512,1024]{1,0:T(8,128)(2,1)} %collective-permute-done.20, bf16[512,128]{1,0:T(8,128)(2,1)S(1)} %collective-permute-done.21, bf16[128,1024]{1,0:T(8,128)(2,1)S(1)} %copy-done.8), kind=kOutput, calls=%fused_computation.12 | convolution fusion | flops 2284322816 | bytes 7733248 | tf_op jit(solution)/shard_map/dot_general | solution.py:152
  227.8 48.3 %shard_map.100 = bf16[512,1024]{1,0:T(8,128)(2,1)} custom-call(s32[8,8]{1,0:T(8,128)} %pad_add_fusion.table_ref, bf16[512,1024]{1,0:T(8,128)(2,1)} %fusion.12.q_ref, bf16[768,2048]{1,0:T(8,128)(2,1)} %convolution_convert_fusion.refs_0_.refs_1_.refs_2_.refs_3_, bf16[768,2048]{1,0:T(8,128)(2,1)} %convolution_convert_fusion.refs_0_.refs_1_.refs_2_.refs_3_, ...), custom_call_target="tpu_custom_call" | custom-call | tf_op jit(solution)/shard_map/pallas_call | solution.py:93
  276.2 3.4 %convolution_convert_fusion.5 = bf16[512,1024]{1,0:T(8,128)(2,1)} fusion(bf16[512,1024]{1,0:T(8,128)(2,1)} %shard_map.100, bf16[1024,1024]{1,0:T(8,128)(2,1)S(1)} %copy-done), kind=kOutput, calls=%fused_computation.31 | convolution fusion | flops 1074266112 | bytes 4194304 | tf_op jit(solution)/shard_map/dot_general | solution.py:163
  (102 shorter events, 32.1 us)
Async XLA Ops:
  0.0 276.2 %copy-start = (bf16[1024,1024]{1,0:T(8,128)(2,1)S(1)}, bf16[1024,1024]{1,0:T(8,128)(2,1)}, u32[]{:S(2)}) copy-start(bf16[1024,1024]{1,0:T(8,128)(2,1)} %param.19) | copy-start | bytes 6291460
  0.0 11.1 %copy-start.1 = (f32[8,3,64,64]{3,2,1,0:T(8,128)S(1)}, f32[8,3,64,64]{3,2,1,0:T(8,128)}, u32[]{:S(2)}) copy-start(f32[8,3,64,64]{3,2,1,0:T(8,128)} %param.12) | copy-start | bytes 1179652
  1.0 4.5 %collective-permute-start = (f32[128,128]{1,0:T(8,128)S(1)}, f32[128,128]{1,0:T(8,128)S(1)}, u32[]{:S(2)}, u32[]{:S(2)}) collective-permute-start(f32[128,128]{1,0:T(8,128)S(1)} %get-tuple-element.21), channel_id=1, source_target_pairs={{0,1},{1,2},{2,3},{3,4},{4,5},{5,6},{6,7},{7,8},{8,9},{9,10},{10,1... | collective-permute-start | bytes 196616 | tf_op jit(solution)/shard_map/ppermute | solution.py:26
  3.4 5.3 %collective-permute-start.1 = (f32[128,128]{1,0:T(8,128)S(1)}, f32[128,128]{1,0:T(8,128)S(1)}, u32[]{:S(2)}, u32[]{:S(2)}) collective-permute-start(f32[128,128]{1,0:T(8,128)S(1)} %get-tuple-element.22), channel_id=1, source_target_pairs={{1,0},{2,1},{3,2},{4,3},{5,4},{6,5},{7,6},{8,7},{9,8},{10,9},{11,1... | collective-permute-start | bytes 196616 | tf_op jit(solution)/shard_map/ppermute | solution.py:26
  13.3 12.9 %collective-permute-start.2 = (f32[128,128]{1,0:T(8,128)S(1)}, f32[128,128]{1,0:T(8,128)S(1)}, u32[]{:S(2)}, u32[]{:S(2)}) collective-permute-start(f32[128,128]{1,0:T(8,128)S(1)} %bitcast.156), channel_id=1, source_target_pairs={{0,1},{1,2},{2,3},{3,4},{4,5},{5,6},{6,7},{7,8},{8,9},{9,10},{10,1... | collective-permute-start | bytes 196616 | tf_op jit(solution)/shard_map/ppermute | solution.py:26
  18.1 8.1 %collective-permute-start.3 = (f32[128,128]{1,0:T(8,128)S(1)}, f32[128,128]{1,0:T(8,128)S(1)}, u32[]{:S(2)}, u32[]{:S(2)}) collective-permute-start(f32[128,128]{1,0:T(8,128)S(1)} %bitcast.155), channel_id=1, source_target_pairs={{1,0},{2,1},{3,2},{4,3},{5,4},{6,5},{7,6},{8,7},{9,8},{10,9},{11,1... | collective-permute-start | bytes 196616 | tf_op jit(solution)/shard_map/ppermute | solution.py:26
  19.4 162.7 %collective-permute-start.26 = (bf16[512,1024]{1,0:T(8,128)(2,1)}, bf16[512,1024]{1,0:T(8,128)(2,1)}, u32[]{:S(2)}, u32[]{:S(2)}) collective-permute-start(bf16[512,1024]{1,0:T(8,128)(2,1)} %param.10), channel_id=1, source_target_pairs={{0,8},{1,9},{2,10},{3,11},{4,12},{5,13},{6,14},{7,15},{8,0},{9,1},... | collective-permute-start | bytes 3145736 | tf_op jit(solution)/shard_map/ppermute | solution.py:39
  24.7 183.8 %collective-permute-start.24 = (bf16[512,1024]{1,0:T(8,128)(2,1)}, bf16[512,1024]{1,0:T(8,128)(2,1)}, u32[]{:S(2)}, u32[]{:S(2)}) collective-permute-start(bf16[512,1024]{1,0:T(8,128)(2,1)} %param.10), channel_id=1, source_target_pairs={{0,4},{1,5},{2,6},{3,7},{4,0},{5,1},{6,2},{7,3},{8,12},{9,13},{10,... | collective-permute-start | bytes 3145736 | tf_op jit(solution)/shard_map/ppermute | solution.py:39
  29.5 12.0 %copy-start.10 = (s32[8,3]{0,1:T(4,128)S(1)}, s32[8,3]{0,1:T(4,128)}, u32[]{:S(2)}) copy-start(s32[8,3]{0,1:T(4,128)} %param.14) | copy-start | bytes 292
  33.3 8.3 %collective-permute-start.4 = (f32[128,128]{1,0:T(8,128)}, f32[128,128]{1,0:T(8,128)S(1)}, u32[]{:S(2)}, u32[]{:S(2)}) collective-permute-start(f32[128,128]{1,0:T(8,128)} %get-tuple-element.17), channel_id=1, source_target_pairs={{0,1},{1,2},{2,3},{3,4},{4,5},{5,6},{6,7},{7,8},{8,9},{9,10},{10,1... | collective-permute-start | bytes 196616 | tf_op jit(solution)/shard_map/ppermute | solution.py:26
  34.6 7.0 %collective-permute-start.5 = (f32[128,128]{1,0:T(8,128)}, f32[128,128]{1,0:T(8,128)S(1)}, u32[]{:S(2)}, u32[]{:S(2)}) collective-permute-start(f32[128,128]{1,0:T(8,128)} %get-tuple-element.18), channel_id=1, source_target_pairs={{1,0},{2,1},{3,2},{4,3},{5,4},{6,5},{7,6},{8,7},{9,8},{10,9},{11,1... | collective-permute-start | bytes 196616 | tf_op jit(solution)/shard_map/ppermute | solution.py:26
  37.7 129.7 %collective-permute-start.16 = (bf16[128,1024]{1,0:T(8,128)(2,1)}, bf16[128,1024]{1,0:T(8,128)(2,1)}, u32[]{:S(2)}, u32[]{:S(2)}) collective-permute-start(bf16[128,1024]{1,0:T(8,128)(2,1)} %get-tuple-element.5), channel_id=1, source_target_pairs={{0,1},{1,2},{2,3},{3,4},{4,5},{5,6},{6,7},{7,8},{8,9},{9,10},{10,1... | collective-permute-start | bytes 786440 | tf_op jit(solution)/shard_map/ppermute | solution.py:26
  42.3 10.8 %copy-start.11 = (s32[8,4]{0,1:T(4,128)S(1)}, s32[8,4]{0,1:T(4,128)}, u32[]{:S(2)}) copy-start(s32[8,4]{0,1:T(4,128)} %param.15) | copy-start | bytes 388
  47.0 0.7 copy-start.2
  48.4 4.8 %collective-permute-start.6 = (f32[128,128]{1,0:T(8,128)}, f32[128,128]{1,0:T(8,128)S(1)}, u32[]{:S(2)}, u32[]{:S(2)}) collective-permute-start(f32[128,128]{1,0:T(8,128)} %get-tuple-element.15), channel_id=1, source_target_pairs={{0,1},{1,2},{2,3},{3,4},{4,5},{5,6},{6,7},{7,8},{8,9},{9,10},{10,1... | collective-permute-start | bytes 196616 | tf_op jit(solution)/shard_map/ppermute | solution.py:26
  51.8 3.4 %collective-permute-start.7 = (f32[128,128]{1,0:T(8,128)}, f32[128,128]{1,0:T(8,128)S(1)}, u32[]{:S(2)}, u32[]{:S(2)}) collective-permute-start(f32[128,128]{1,0:T(8,128)} %get-tuple-element.16), channel_id=1, source_target_pairs={{1,0},{2,1},{3,2},{4,3},{5,4},{6,5},{7,6},{8,7},{9,8},{10,9},{11,1... | collective-permute-start | bytes 196616 | tf_op jit(solution)/shard_map/ppermute | solution.py:26
  61.5 36.3 %copy-start.3 = (f32[512,128]{1,0:T(8,128)}, f32[512,128]{1,0:T(8,128)S(1)}, u32[]{:S(2)}) copy-start(f32[512,128]{1,0:T(8,128)S(1)} %bitcast_subtract_fusion.4) | copy-start | bytes 786436
  61.6 33.0 %collective-permute-start.8 = (f32[128,128]{1,0:T(8,128)S(1)}, f32[128,128]{1,0:T(8,128)S(1)}, u32[]{:S(2)}, u32[]{:S(2)}) collective-permute-start(f32[128,128]{1,0:T(8,128)S(1)} %get-tuple-element.13), channel_id=1, source_target_pairs={{0,1},{1,2},{2,3},{3,4},{4,5},{5,6},{6,7},{7,8},{8,9},{9,10},{10,1... | collective-permute-start | bytes 196616 | tf_op jit(solution)/shard_map/ppermute | solution.py:26
  93.2 4.6 %collective-permute-start.9 = (f32[128,128]{1,0:T(8,128)S(1)}, f32[128,128]{1,0:T(8,128)S(1)}, u32[]{:S(2)}, u32[]{:S(2)}) collective-permute-start(f32[128,128]{1,0:T(8,128)S(1)} %get-tuple-element.14), channel_id=1, source_target_pairs={{1,0},{2,1},{3,2},{4,3},{5,4},{6,5},{7,6},{8,7},{9,8},{10,9},{11,1... | collective-permute-start | bytes 196616 | tf_op jit(solution)/shard_map/ppermute | solution.py:26
  98.6 13.9 %copy-start.9 = (f32[9]{0:T(128)S(1)}, f32[9]{0:T(128)}, u32[]{:S(2)}) copy-start(f32[9]{0:T(128)} %param.16) | copy-start | bytes 112
  104.2 10.1 %copy-start.4 = (f32[512,128]{1,0:T(8,128)}, f32[512,128]{1,0:T(8,128)S(1)}, u32[]{:S(2)}) copy-start(f32[512,128]{1,0:T(8,128)S(1)} %bitcast_subtract_fusion.3) | copy-start | bytes 786436
  104.3 8.9 %collective-permute-start.10 = (f32[128,128]{1,0:T(8,128)S(1)}, f32[128,128]{1,0:T(8,128)S(1)}, u32[]{:S(2)}, u32[]{:S(2)}) collective-permute-start(f32[128,128]{1,0:T(8,128)S(1)} %get-tuple-element.11), channel_id=1, source_target_pairs={{0,1},{1,2},{2,3},{3,4},{4,5},{5,6},{6,7},{7,8},{8,9},{9,10},{10,1... | collective-permute-start | bytes 196616 | tf_op jit(solution)/shard_map/ppermute | solution.py:26
  111.2 3.1 %collective-permute-start.11 = (f32[128,128]{1,0:T(8,128)S(1)}, f32[128,128]{1,0:T(8,128)S(1)}, u32[]{:S(2)}, u32[]{:S(2)}) collective-permute-start(f32[128,128]{1,0:T(8,128)S(1)} %get-tuple-element.12), channel_id=1, source_target_pairs={{1,0},{2,1},{3,2},{4,3},{5,4},{6,5},{7,6},{8,7},{9,8},{10,9},{11,1... | collective-permute-start | bytes 196616 | tf_op jit(solution)/shard_map/ppermute | solution.py:26
  120.7 8.5 %copy-start.5 = (f32[512,128]{1,0:T(8,128)}, f32[512,128]{1,0:T(8,128)S(1)}, u32[]{:S(2)}) copy-start(f32[512,128]{1,0:T(8,128)S(1)} %bitcast_subtract_fusion.2) | copy-start | bytes 786436
  120.8 6.6 %collective-permute-start.12 = (f32[128,128]{1,0:T(8,128)S(1)}, f32[128,128]{1,0:T(8,128)S(1)}, u32[]{:S(2)}, u32[]{:S(2)}) collective-permute-start(f32[128,128]{1,0:T(8,128)S(1)} %get-tuple-element.9), channel_id=1, source_target_pairs={{0,1},{1,2},{2,3},{3,4},{4,5},{5,6},{6,7},{7,8},{8,9},{9,10},{10,1... | collective-permute-start | bytes 196616 | tf_op jit(solution)/shard_map/ppermute | solution.py:26
  126.1 3.1 %collective-permute-start.13 = (f32[128,128]{1,0:T(8,128)S(1)}, f32[128,128]{1,0:T(8,128)S(1)}, u32[]{:S(2)}, u32[]{:S(2)}) collective-permute-start(f32[128,128]{1,0:T(8,128)S(1)} %get-tuple-element.10), channel_id=1, source_target_pairs={{1,0},{2,1},{3,2},{4,3},{5,4},{6,5},{7,6},{8,7},{9,8},{10,9},{11,1... | collective-permute-start | bytes 196616 | tf_op jit(solution)/shard_map/ppermute | solution.py:26
  135.6 8.6 %copy-start.6 = (f32[512,128]{1,0:T(8,128)}, f32[512,128]{1,0:T(8,128)S(1)}, u32[]{:S(2)}) copy-start(f32[512,128]{1,0:T(8,128)S(1)} %bitcast_subtract_fusion.1) | copy-start | bytes 786436
  135.6 7.2 %collective-permute-start.14 = (f32[128,128]{1,0:T(8,128)S(1)}, f32[128,128]{1,0:T(8,128)S(1)}, u32[]{:S(2)}, u32[]{:S(2)}) collective-permute-start(f32[128,128]{1,0:T(8,128)S(1)} %get-tuple-element.7), channel_id=1, source_target_pairs={{0,1},{1,2},{2,3},{3,4},{4,5},{5,6},{6,7},{7,8},{8,9},{9,10},{10,1... | collective-permute-start | bytes 196616 | tf_op jit(solution)/shard_map/ppermute | solution.py:26
  140.9 3.3 %collective-permute-start.15 = (f32[128,128]{1,0:T(8,128)S(1)}, f32[128,128]{1,0:T(8,128)S(1)}, u32[]{:S(2)}, u32[]{:S(2)}) collective-permute-start(f32[128,128]{1,0:T(8,128)S(1)} %get-tuple-element.8), channel_id=1, source_target_pairs={{1,0},{2,1},{3,2},{4,3},{5,4},{6,5},{7,6},{8,7},{9,8},{10,9},{11,1... | collective-permute-start | bytes 196616 | tf_op jit(solution)/shard_map/ppermute | solution.py:26
  142.9 29.8 %collective-permute-start.18 = (bf16[128,1024]{1,0:T(8,128)(2,1)}, bf16[128,1024]{1,0:T(8,128)(2,1)}, u32[]{:S(2)}, u32[]{:S(2)}) collective-permute-start(bf16[128,1024]{1,0:T(8,128)(2,1)} %get-tuple-element.6), channel_id=1, source_target_pairs={{1,0},{2,1},{3,2},{4,3},{5,4},{6,5},{7,6},{8,7},{9,8},{10,9},{11,1... | collective-permute-start | bytes 786440 | tf_op jit(solution)/shard_map/ppermute | solution.py:26
  147.4 14.2 %copy-start.7 = (bf16[128,1024]{1,0:T(8,128)(2,1)S(1)}, bf16[128,1024]{1,0:T(8,128)(2,1)}, u32[]{:S(2)}) copy-start(bf16[128,1024]{1,0:T(8,128)(2,1)} %param.17) | copy-start | bytes 786436
  156.5 13.5 %collective-permute-start.17 = (bf16[128,128]{1,0:T(8,128)(2,1)S(1)}, bf16[128,128]{1,0:T(8,128)(2,1)S(1)}, u32[]{:S(2)}, u32[]{:S(2)}) collective-permute-start(bf16[128,128]{1,0:T(8,128)(2,1)S(1)} %get-tuple-element.23), channel_id=1, source_target_pairs={{0,1},{1,2},{2,3},{3,4},{4,5},{5,6},{6,7},{7,8},{8,9},{9,10},{10,1... | collective-permute-start | bytes 98312 | tf_op jit(solution)/shard_map/ppermute | solution.py:26
  161.7 14.9 %slice-start = ((s8[6291456]{0:T(1024)(128)(4,1)}), s8[4194304]{0:T(1024)(128)(4,1)S(1)}, s32[]{:S(2)}) async-start(s8[6291456]{0:T(1024)(128)(4,1)} %bitcast.157), calls=%async_computation | async-start | bytes 8388608
  163.5 13.0 %slice-start.1 = ((s8[6291456]{0:T(1024)(128)(4,1)}), s8[2097152]{0:T(1024)(128)(4,1)S(1)}, s32[]{:S(2)}) async-start(s8[6291456]{0:T(1024)(128)(4,1)} %bitcast.157), calls=%async_computation.1 | async-start | bytes 4194304
  167.5 47.5 %collective-permute-start.22 = (bf16[512,1024]{1,0:T(8,128)(2,1)}, bf16[512,1024]{1,0:T(8,128)(2,1)}, u32[]{:S(2)}, u32[]{:S(2)}) collective-permute-start(bf16[512,1024]{1,0:T(8,128)(2,1)} %param.10), channel_id=1, source_target_pairs={{0,2},{1,3},{2,0},{3,1},{4,6},{5,7},{6,4},{7,5},{8,10},{9,11},{10,... | collective-permute-start | bytes 3145736 | tf_op jit(solution)/shard_map/ppermute | solution.py:39
  170.0 4.2 %collective-permute-start.19 = (bf16[128,128]{1,0:T(8,128)(2,1)S(1)}, bf16[128,128]{1,0:T(8,128)(2,1)S(1)}, u32[]{:S(2)}, u32[]{:S(2)}) collective-permute-start(bf16[128,128]{1,0:T(8,128)(2,1)S(1)} %get-tuple-element.24), channel_id=1, source_target_pairs={{1,0},{2,1},{3,2},{4,3},{5,4},{6,5},{7,6},{8,7},{9,8},{10,9},{11,1... | collective-permute-start | bytes 98312 | tf_op jit(solution)/shard_map/ppermute | solution.py:26
  172.6 48.8 %collective-permute-start.20 = (bf16[512,1024]{1,0:T(8,128)(2,1)}, bf16[512,1024]{1,0:T(8,128)(2,1)}, u32[]{:S(2)}, u32[]{:S(2)}) collective-permute-start(bf16[512,1024]{1,0:T(8,128)(2,1)} %param.10), channel_id=1, source_target_pairs={{0,1},{1,0},{2,3},{3,2},{4,5},{5,4},{6,7},{7,6},{8,9},{9,8},{10,11... | collective-permute-start | bytes 3145736 | tf_op jit(solution)/shard_map/ppermute | solution.py:39
  174.2 7.3 %collective-permute-start.27 = (bf16[512,128]{1,0:T(8,128)(2,1)S(1)}, bf16[512,128]{1,0:T(8,128)(2,1)S(1)}, u32[]{:S(2)}, u32[]{:S(2)}) collective-permute-start(bf16[512,128]{1,0:T(8,128)(2,1)S(1)} %fusion.32), channel_id=1, source_target_pairs={{0,8},{1,9},{2,10},{3,11},{4,12},{5,13},{6,14},{7,15},{8,0},{9,1},... | collective-permute-start | bytes 393224 | tf_op jit(solution)/shard_map/ppermute | solution.py:39
  176.5 25.5 %copy-start.8 = (bf16[128,1024]{1,0:T(8,128)(2,1)S(1)}, bf16[128,1024]{1,0:T(8,128)(2,1)}, u32[]{:S(2)}) copy-start(bf16[128,1024]{1,0:T(8,128)(2,1)} %param.17) | copy-start | bytes 786436
  181.5 0.7 copy-start.12
  181.5 27.0 %collective-permute-start.25 = (bf16[512,128]{1,0:T(8,128)(2,1)S(1)}, bf16[512,128]{1,0:T(8,128)(2,1)S(1)}, u32[]{:S(2)}, u32[]{:S(2)}) collective-permute-start(bf16[512,128]{1,0:T(8,128)(2,1)S(1)} %fusion.32), channel_id=1, source_target_pairs={{0,4},{1,5},{2,6},{3,7},{4,0},{5,1},{6,2},{7,3},{8,12},{9,13},{10,... | collective-permute-start | bytes 393224 | tf_op jit(solution)/shard_map/ppermute | solution.py:39
  182.2 32.8 %collective-permute-start.23 = (bf16[512,128]{1,0:T(8,128)(2,1)S(1)}, bf16[512,128]{1,0:T(8,128)(2,1)S(1)}, u32[]{:S(2)}, u32[]{:S(2)}) collective-permute-start(bf16[512,128]{1,0:T(8,128)(2,1)S(1)} %fusion.32), channel_id=1, source_target_pairs={{0,2},{1,3},{2,0},{3,1},{4,6},{5,7},{6,4},{7,5},{8,10},{9,11},{10,... | collective-permute-start | bytes 393224 | tf_op jit(solution)/shard_map/ppermute | solution.py:39
  208.5 13.0 %collective-permute-start.21 = (bf16[512,128]{1,0:T(8,128)(2,1)S(1)}, bf16[512,128]{1,0:T(8,128)(2,1)S(1)}, u32[]{:S(2)}, u32[]{:S(2)}) collective-permute-start(bf16[512,128]{1,0:T(8,128)(2,1)S(1)} %fusion.32), channel_id=1, source_target_pairs={{0,1},{1,0},{2,3},{3,2},{4,5},{5,4},{6,7},{7,6},{8,9},{9,8},{10,11... | collective-permute-start | bytes 393224 | tf_op jit(solution)/shard_map/ppermute | solution.py:39

commit v2 on v1

--- a/solution.py
+++ b/solution.py
@@ -47,6 +47,66 @@
     picked = pooled[position]
     result = jnp.einsum("bjst,bjtc->bsc", op_blocks, picked, precision=lax.Precision.HIGHEST)
     return result.reshape(field.shape)
+
+
+def chebyshev(struct_feats, op_blocks, laplace_index, series_coef, first_block):
+    count = op_blocks.shape[0]
+    chans = struct_feats.shape[1]
+    lap_rows = jnp.zeros((count, chans), jnp.float32).at[:, : laplace_index.shape[1]].set(
+        laplace_index.astype(jnp.float32)
+    )
+    payload = jnp.concatenate(
+        [struct_feats, op_blocks.reshape(-1, chans), lap_rows], axis=0
+    )
+    reach_dev = -(-DEG * REACH // count)
+    parts = {0: payload}
+    for off in range(1, reach_dev + 1):
+        parts[-off] = shift_rows(payload, "seq", off)
+        parts[off] = shift_rows(payload, "seq", -off)
+    order = list(range(-reach_dev, reach_dev + 1))
+    rows = count * BS
+    n_op = op_blocks.size // chans
+    field = jnp.concatenate([parts[o][:rows] for o in order], axis=0)
+    field = field.reshape(-1, BS, chans)
+    ops = jnp.concatenate(
+        [parts[o][rows : rows + n_op].reshape(op_blocks.shape) for o in order], axis=0
+    )
+    lap = jnp.concatenate(
+        [parts[o][rows + n_op : rows + n_op + count, : laplace_index.shape[1]] for o in order],
+        axis=0,
+    ).astype(jnp.int32)
+    width = field.shape[0]
+    centre = reach_dev * count
+    block_ids = first_block - centre + jnp.arange(width, dtype=jnp.int32)
+    offsets = lap - block_ids[:, None] + REACH
+    diag = jnp.arange(2 * REACH + 1, dtype=jnp.int32)
+    hit = offsets[:, :, None] == diag[None, None, :]
+    bands = jnp.sum(
+        jnp.where(hit[:, :, :, None, None], ops[:, :, None, :, :], 0.0), axis=1
+    )
+
+    def step(values, lo, hi, base):
+        stacked = jnp.stack(
+            [values[lo - REACH + o - base : hi - REACH + o - base] for o in range(2 * REACH + 1)],
+            axis=1,
+        )
+        return jnp.einsum(
+            "wosu,wouc->wsc", bands[lo:hi], stacked, precision=lax.Precision.HIGHEST
+        )
+
+    own = slice(centre, centre + count)
+    prev, prev_base = field, 0
+    lo, hi = REACH, width - REACH
+    cur = step(field, lo, hi, 0)
+    cur_base = lo
+    encoding = series_coef[0] * field[own] + series_coef[1] * cur[centre - cur_base : centre - cur_base + count]
+    for degree in range(2, DEG + 1):
+        lo, hi = lo + REACH, hi - REACH
+        nxt = 2.0 * step(cur, lo, hi, cur_base) - prev[lo - prev_base : hi - prev_base]
+        encoding = encoding + series_coef[degree] * nxt[centre - lo : centre - lo + count]
+        prev, prev_base = cur, cur_base
+        cur, cur_base = nxt, lo
+    return encoding.reshape(rows, chans)
 
 
 def attention_kernel(table_ref, q_ref, *refs):
@@ -120,13 +180,7 @@
     feats_after = shift_rows(node_feats[:rim], "seq", -1)
     feats_far = [partner(node_feats, "seq", bit) for bit in bits]
 
-    previous = struct_feats
-    current = apply_operator(previous, op_blocks, laplace_index, first_block)
-    encoding = series_coef[0] * previous + series_coef[1] * current
-    for degree in range(2, DEG + 1):
-        following = 2.0 * apply_operator(current, op_blocks, laplace_index, first_block) - previous
-        encoding = encoding + series_coef[degree] * following
-        previous, current = (current, following)
+    encoding = chebyshev(struct_feats, op_blocks, laplace_index, series_coef, first_block)
     encoding_b = encoding.astype(jnp.bfloat16)
 
     enc_before = shift_rows(encoding_b[rows - rim:], "seq", 1)

time: 281 us -> 272 us (0.968); the launches traced: 280 us -> 267 us
  starting transfers between devices: 115 us -> 63.3 us
  local copies, waits for them, and re-layouts: 25.8 us -> 49.2 us
  matrix products: 59.4 us -> 76.6 us
  other arithmetic: 18.9 us -> 9.28 us
  waiting for transfers between devices: 11.5 us -> 19.4 us
    ppermute x20 -> x8, starting transfers between devices: 83 us -> 25.1 us  [shift_rows(): return lax.ppermute(x, axis, pairs)]
    unnamed x33 -> x74, local copies, waits for them, and re-layouts: 2.03 us -> 21.1 us
    dot_general x8, matrix products: 17.2 us -> 36.1 us  [step(): jnp.einsum('wosu,wouc->wsc', bands[lo:hi], stacked, precision=lax.Precisi...]
    gather x8 -> x0, local copies, waits for them, and re-layouts: 18.8 us -> none  [apply_operator(): picked = pooled[position]]
    slice x9 -> x16, local copies, waits for them, and re-layouts: 3.07 us -> 13.8 us  [the longest x4 6.1 us: chebyshev(): parts[o][rows:rows + n_op].reshape(op_blocks.shape)]
    reshape x0 -> x5, local copies, waits for them, and re-layouts: none -> 9.63 us  [the longest x4 8.33 us: chebyshev(): parts[o][rows:rows + n_op].reshape(op_blocks.shape)]
    ppermute x20 -> x8, waiting for transfers between devices: 11.4 us -> 19.3 us  [shift_rows(): return lax.ppermute(x, axis, pairs)]
    convert_element_type x1 -> x0, other arithmetic: 6.86 us -> none  [on_device(): encoding_b = encoding.astype(jnp.bfloat16)]
  transfers between devices with their start and end apart: 28 -> 16, of which waited for: 6 -> 1; matrix products, arithmetic and copies ran while one was open for 31% -> 44% of each run, Pallas kernels for 0% -> 0%
where the time goes in v2:
time: 272 us; the launch traced here: 267 us
  matrix products  76.6 us (28%)
  starting transfers between devices  63.3 us (23%)
  local copies, waits for them, and re-layouts  49.2 us (18%)
  Pallas kernels  48 us (18%)
  waiting for transfers between devices  19.4 us (7%)
  other arithmetic  9.28 us (3%)
    pallas_call x1, Pallas kernels, attend(): pl.pallas_call(attention_kernel, grid_spec=grid_spec, out_shape=jax.Shape...  48 us
    ppermute x8, starting transfers between devices, partner(): return lax.ppermute(value, axis, pairs)  38.2 us
    dot_general x8, matrix products, step(): jnp.einsum('wosu,wouc->wsc', bands[lo:hi], stacked, precision=lax.Precisi...  36.1 us
    dot_general x4, matrix products, on_device(): jnp.dot(blend(f, e), kv_weight, preferred_element_type=jnp.float32)  25.7 us
    ppermute x8, starting transfers between devices, shift_rows(): return lax.ppermute(x, axis, pairs)  25.1 us
    unnamed x74, local copies, waits for them, and re-layouts  21.1 us
    ppermute x8, waiting for transfers between devices, shift_rows(): return lax.ppermute(x, axis, pairs)  19.3 us
    reshape x4, local copies, waits for them, and re-layouts, chebyshev(): parts[o][rows:rows + n_op].reshape(op_blocks.shape)  8.33 us
  transfers between devices with their start and end apart: 16, of which 1 were waited for; matrix products, arithmetic and copies ran while one was open for 44% of the time, Pallas kernels for 0%

profile of v2, /device:TPU:0, one launch (start us, length us, event | category | flops | bytes accessed | tf_op | source)
XLA Modules:
  0.0 266.7 jit_solution(4906518929301343223)
XLA Ops:
  1.5 1.3 reshape.128
  3.4 1.8 select_maximum_fusion
  5.3 5.7 %collective-permute-start = (f32[1288,128]{1,0:T(8,128)}, f32[1288,128]{1,0:T(8,128)}, u32[]{:S(2)}, u32[]{:S(2)}) collective-permute-start(f32[1288,128]{1,0:T(8,128)} %select_maximum_fusion), channel_id=1, source_target_pairs={{0,2},{1,3},{2,4},{3,5},{4,6},{5,7},{6,8},{7,9},{8,10},{9,11},{10,... | collective-permute-start | bytes 1978376 | tf_op jit(solution)/shard_map/ppermute | solution.py:26
  11.0 2.3 collective-permute-start.1
  14.5 1.3 collective-permute-start.3
  15.8 5.8 %collective-permute-start.14 = (bf16[512,1024]{1,0:T(8,128)(2,1)}, bf16[512,1024]{1,0:T(8,128)(2,1)}, u32[]{:S(2)}, u32[]{:S(2)}) collective-permute-start(bf16[512,1024]{1,0:T(8,128)(2,1)} %param.12), channel_id=1, source_target_pairs={{0,8},{1,9},{2,10},{3,11},{4,12},{5,13},{6,14},{7,15},{8,0},{9,1},... | collective-permute-start | bytes 3145736 | tf_op jit(solution)/shard_map/ppermute | solution.py:39
  24.0 1.7 fusion.154
  25.6 1.9 fusion.152
  27.5 19.3 %collective-permute-done = f32[1288,128]{1,0:T(8,128)} collective-permute-done((f32[1288,128]{1,0:T(8,128)}, f32[1288,128]{1,0:T(8,128)}, u32[]{:S(2)}, u32[]{:S(2)}) %collective-permute-start) | collective-permute-done | bytes 659488 | tf_op jit(solution)/shard_map/ppermute | solution.py:26
  47.8 7.7 %collective-permute-start.4 = (bf16[128,1024]{1,0:T(8,128)(2,1)}, bf16[128,1024]{1,0:T(8,128)(2,1)}, u32[]{:S(2)}, u32[]{:S(2)}) collective-permute-start(bf16[128,1024]{1,0:T(8,128)(2,1)} %get-tuple-element.22), channel_id=1, source_target_pairs={{0,1},{1,2},{2,3},{3,4},{4,5},{5,6},{6,7},{7,8},{8,9},{9,10},{10,1... | collective-permute-start | bytes 786440 | tf_op jit(solution)/shard_map/ppermute | solution.py:26
  56.5 1.4 broadcast_multiply_fusion
  57.9 1.3 collective-permute-start.6
  60.2 1.9 fusion.151
  67.6 1.8 slice.393
  69.4 2.1 reshape.129
  71.5 2.1 constant_dynamic-update-slice_fusion.4
  73.6 1.8 slice.394
  75.4 2.1 reshape.130
  77.4 2.2 constant_dynamic-update-slice_fusion.3
  79.6 2.2 constant_dynamic-update-slice_fusion.2
  82.5 2.1 reshape.131
  84.6 1.8 slice.396
  86.4 2.1 reshape.132
  88.5 2.5 constant_dynamic-update-slice_fusion.9
  91.0 2.6 constant_dynamic-update-slice_fusion.8
  96.0 3.9 %select_reduce_fusion = f32[40,5,64,64]{3,2,1,0:T(8,128)S(1)} fusion(f32[40,3,64,64]{3,2,1,0:T(8,128)S(1)} %constant_dynamic-update-slice_fusion, pred[40,3,5]{2,1,0:T(4,128)(4,1)S(1)} %iota_compare_fusion.1), kind=kLoop, calls=%fused_computation | loop fusion | flops 4096000 | bytes 5243480 | tf_op jit(solution)/shard_map/reduce_sum | solution.py:84
  100.0 6.2 %convolution_bitcast_fusion = f32[36,64,128]{2,1,0:T(8,128)S(1)} fusion(f32[40,5,64,64]{3,2,1,0:T(8,128)S(1)} %select_reduce_fusion, f32[36,5,64,128]{3,2,1,0:T(8,128)S(1)} %bitcast.244), kind=kOutput, calls=%fused_computation.37 | convolution fusion | flops 1132462080 | bytes 10354688 | tf_op jit(solution)/shard_map/wosu,wouc->wsc/dot_general | solution.py:93
  107.6 5.7 %fusion.33 = f32[32,64,128]{2,1,0:T(8,128)S(1)} fusion(f32[32,64,128]{2,1,0:T(8,128)S(1)} %bitcast.250, f32[40,5,64,64]{3,2,1,0:T(8,128)S(1)} %select_reduce_fusion, f32[32,5,64,128]{3,2,0,1:T(8,128)S(1)} %fusion.109), kind=kOutput, calls=%fused_computation.40 | convolution fusion | flops 1007157248 | bytes 10616832 | tf_op jit(solution)/shard_map/wosu,wouc->wsc/dot_general | solution.py:93
  113.7 4.8 %fusion.42 = f32[28,64,128]{2,1,0:T(8,128)S(1)} fusion(f32[40,5,64,64]{3,2,1,0:T(8,128)S(1)} %select_reduce_fusion, f32[28,5,64,128]{3,2,0,1:T(8,128)S(1)} %fusion.114, f32[36,64,128]{2,1,0:T(8,128)S(1)} %convolution_bitcast_fusion), kind=kOutput, calls=%fused_computation.43 | convolution fusion | flops 881262592 | bytes 9699328 | tf_op jit(solution)/shard_map/wosu,wouc->wsc/dot_general | solution.py:93
  118.8 4.2 %fusion.53 = f32[24,64,128]{2,1,0:T(8,128)S(1)} fusion(f32[40,5,64,64]{3,2,1,0:T(8,128)S(1)} %select_reduce_fusion, f32[24,5,64,128]{3,2,0,1:T(8,128)S(1)} %fusion.119, f32[32,64,128]{2,1,0:T(8,128)S(1)} %fusion.33), kind=kOutput, calls=%fused_computation.48 | convolution fusion | flops 755367936 | bytes 8781824 | tf_op jit(solution)/shard_map/wosu,wouc->wsc/dot_general | solution.py:93
  123.3 3.7 %fusion.62 = f32[20,64,128]{2,1,0:T(8,128)S(1)} fusion(f32[40,5,64,64]{3,2,1,0:T(8,128)S(1)} %select_reduce_fusion, f32[20,5,64,128]{3,2,0,1:T(8,128)S(1)} %fusion.124, f32[28,64,128]{2,1,0:T(8,128)S(1)} %fusion.42), kind=kOutput, calls=%fused_computation.51 | convolution fusion | flops 629473280 | bytes 7864320 | tf_op jit(solution)/shard_map/wosu,wouc->wsc/dot_general | solution.py:93
  127.3 2.8 %fusion.71 = f32[16,64,128]{2,1,0:T(8,128)S(1)} fusion(f32[40,5,64,64]{3,2,1,0:T(8,128)S(1)} %select_reduce_fusion, f32[16,5,64,128]{3,2,0,1:T(8,128)S(1)} %fusion.129, f32[24,64,128]{2,1,0:T(8,128)S(1)} %fusion.53), kind=kOutput, calls=%fused_computation.54 | convolution fusion | flops 503578624 | bytes 6946816 | tf_op jit(solution)/shard_map/wosu,wouc->wsc/dot_general | solution.py:93
  130.3 2.2 fusion.98
  132.7 6.5 %fusion.95 = bf16[8,64,128]{2,1,0:T(8,128)(2,1)S(1)} fusion(f32[40,5,64,64]{3,2,1,0:T(8,128)S(1)} %select_reduce_fusion, f32[8,5,64,128]{3,2,0,1:T(8,128)S(1)} %fusion.139, f32[20,64,128]{2,1,0:T(8,128)S(1)} %fusion.62, f32[24,64,128]{2,1,0:T(8,128)S(1)} %fusion.53, f32[28,64,128]{2,1,0:T(8,128)S(1)} %fusion.42, f32[32,64,128]{2,1,0:T(8,128)S(1)} %fusion.33, ...), kind=kOutput, calls=%fused_computation.62 | convolution fusion | flops 252903424 | bytes 6815776 | tf_op jit(solution)/shard_map/wosu,wouc->wsc/dot_general | solution.py:93
  139.2 4.3 %collective-permute-start.5 = (bf16[128,128]{1,0:T(8,128)(2,1)S(1)}, bf16[128,128]{1,0:T(8,128)(2,1)S(1)}, u32[]{:S(2)}, u32[]{:S(2)}) collective-permute-start(bf16[128,128]{1,0:T(8,128)(2,1)S(1)} %bitcast.258), channel_id=1, source_target_pairs={{0,1},{1,2},{2,3},{3,4},{4,5},{5,6},{6,7},{7,8},{8,9},{9,10},{10,1... | collective-permute-start | bytes 98312 | tf_op jit(solution)/shard_map/ppermute | solution.py:26
  143.5 1.6 add_convert_fusion.4
  145.2 2.2 fusion.24.q_ref
  147.4 1.6 collective-permute-start.10
  149.1 1.3 collective-permute-start.7
  152.8 12.6 %collective-permute-start.15 = (bf16[512,128]{1,0:T(8,128)(2,1)S(1)}, bf16[512,128]{1,0:T(8,128)(2,1)S(1)}, u32[]{:S(2)}, u32[]{:S(2)}) collective-permute-start(bf16[512,128]{1,0:T(8,128)(2,1)S(1)} %bitcast.253), channel_id=1, source_target_pairs={{0,8},{1,9},{2,10},{3,11},{4,12},{5,13},{6,14},{7,15},{8,0},{9,1},... | collective-permute-start | bytes 393224 | tf_op jit(solution)/shard_map/ppermute | solution.py:39
  166.5 5.1 %convolution_convert_fusion.refs_0_.refs_1_.refs_2_.refs_3_ = bf16[768,2048]{1,0:T(8,128)(2,1)} fusion(bf16[1024,3072]{1,0:T(8,128)(2,1)S(1)} %bitcast.260, bf16[128,1024]{1,0:T(8,128)(2,1)S(1)} %add_convert_fusion.9, bf16[512,1024]{1,0:T(8,128)(2,1)S(1)} %add_convert_fusion.4, bf16[128,1024]{1,0:T(8,128)(2,1)S(1)} %add_convert_fusion.10), kind=kOutput, calls=%fused_computation.7 | convolution fusion | flops 3227516928 | bytes 8912896 | tf_op jit(solution)/shard_map/dot_general | solution.py:202
  172.3 16.9 %collective-permute-start.11 = (bf16[512,128]{1,0:T(8,128)(2,1)S(1)}, bf16[512,128]{1,0:T(8,128)(2,1)}, u32[]{:S(2)}, u32[]{:S(2)}) collective-permute-start(bf16[512,128]{1,0:T(8,128)(2,1)S(1)} %bitcast.255), channel_id=1, source_target_pairs={{0,2},{1,3},{2,0},{3,1},{4,6},{5,7},{6,4},{7,5},{8,10},{9,11},{10,... | collective-permute-start | bytes 393224 | tf_op jit(solution)/shard_map/ppermute | solution.py:39
  189.2 6.5 %convolution_convert_fusion.1.refs_7_ = bf16[512,2048]{1,0:T(8,128)(2,1)} fusion(bf16[1024,3072]{1,0:T(8,128)(2,1)} %param.20, bf16[512,1024]{1,0:T(8,128)(2,1)} %collective-permute-done.14, bf16[512,128]{1,0:T(8,128)(2,1)} %copy-done.11, bf16[128,1024]{1,0:T(8,128)(2,1)S(1)} %copy-done.6), kind=kOutput, calls=%fused_computation.10 | convolution fusion | flops 2284322816 | bytes 7733248 | tf_op jit(solution)/shard_map/dot_general | solution.py:206
  195.7 6.5 %convolution_convert_fusion.2.refs_6_ = bf16[512,2048]{1,0:T(8,128)(2,1)} fusion(bf16[1024,3072]{1,0:T(8,128)(2,1)} %param.20, bf16[512,1024]{1,0:T(8,128)(2,1)} %collective-permute-done.12, bf16[512,128]{1,0:T(8,128)(2,1)} %collective-permute-done.13, bf16[128,1024]{1,0:T(8,128)(2,1)S(1)} %copy-done.6), kind=kOutput, calls=%fused_computation.11 | convolution fusion | flops 2284322816 | bytes 7733248 | tf_op jit(solution)/shard_map/dot_general | solution.py:206
  202.1 6.3 %convolution_convert_fusion.3.refs_5_ = bf16[512,2048]{1,0:T(8,128)(2,1)} fusion(bf16[1024,3072]{1,0:T(8,128)(2,1)} %param.20, bf16[512,1024]{1,0:T(8,128)(2,1)S(1)} %collective-permute-done.10, bf16[512,128]{1,0:T(8,128)(2,1)} %collective-permute-done.11, bf16[128,1024]{1,0:T(8,128)(2,1)S(1)} %copy-done.6), kind=kOutput, calls=%fused_computation.12 | convolution fusion | flops 2284322816 | bytes 7733248 | tf_op jit(solution)/shard_map/dot_general | solution.py:206
  208.4 6.5 %convolution_convert_fusion.4.refs_4_ = bf16[512,2048]{1,0:T(8,128)(2,1)} fusion(bf16[1024,3072]{1,0:T(8,128)(2,1)} %param.20, bf16[512,1024]{1,0:T(8,128)(2,1)} %collective-permute-done.8, bf16[512,128]{1,0:T(8,128)(2,1)} %collective-permute-done.9, bf16[128,1024]{1,0:T(8,128)(2,1)S(1)} %copy-done.6), kind=kOutput, calls=%fused_computation.13 | convolution fusion | flops 2284322816 | bytes 7733248 | tf_op jit(solution)/shard_map/dot_general | solution.py:206
  214.9 48.0 %shard_map.100 = bf16[512,1024]{1,0:T(8,128)(2,1)} custom-call(s32[8,8]{1,0:T(8,128)} %pad_add_fusion.table_ref, bf16[512,1024]{1,0:T(8,128)(2,1)} %fusion.24.q_ref, bf16[768,2048]{1,0:T(8,128)(2,1)} %convolution_convert_fusion.refs_0_.refs_1_.refs_2_.refs_3_, bf16[768,2048]{1,0:T(8,128)(2,1)} %convolution_convert_fusion.refs_0_.refs_1_.refs_2_.refs_3_, ...), custom_call_target="tpu_custom_call" | custom-call | tf_op jit(solution)/shard_map/pallas_call | solution.py:153
  262.8 3.4 %convolution_convert_fusion.5 = bf16[512,1024]{1,0:T(8,128)(2,1)} fusion(bf16[512,1024]{1,0:T(8,128)(2,1)} %shard_map.100, bf16[1024,1024]{1,0:T(8,128)(2,1)S(1)} %copy-done), kind=kOutput, calls=%fused_computation.36 | convolution fusion | flops 1074266112 | bytes 4194304 | tf_op jit(solution)/shard_map/dot_general | solution.py:217
  (126 shorter events, 24.2 us)
Async XLA Ops:
  0.0 262.8 %copy-start = (bf16[1024,1024]{1,0:T(8,128)(2,1)S(1)}, bf16[1024,1024]{1,0:T(8,128)(2,1)}, u32[]{:S(2)}) copy-start(bf16[1024,1024]{1,0:T(8,128)(2,1)} %param.21) | copy-start | bytes 6291460
  0.0 56.4 %copy-start.7 = (f32[512,128]{1,0:T(8,128)S(1)}, f32[512,128]{1,0:T(8,128)}, u32[]{:S(2)}) copy-start(f32[512,128]{1,0:T(8,128)} %param.13) | copy-start | bytes 786436
  5.3 41.6 %collective-permute-start = (f32[1288,128]{1,0:T(8,128)}, f32[1288,128]{1,0:T(8,128)}, u32[]{:S(2)}, u32[]{:S(2)}) collective-permute-start(f32[1288,128]{1,0:T(8,128)} %select_maximum_fusion), channel_id=1, source_target_pairs={{0,2},{1,3},{2,4},{3,5},{4,6},{5,7},{6,8},{7,9},{8,10},{9,11},{10,... | collective-permute-start | bytes 1978376 | tf_op jit(solution)/shard_map/ppermute | solution.py:26
  11.0 36.8 %collective-permute-start.1 = (f32[1288,128]{1,0:T(8,128)}, f32[1288,128]{1,0:T(8,128)}, u32[]{:S(2)}, u32[]{:S(2)}) collective-permute-start(f32[1288,128]{1,0:T(8,128)} %select_maximum_fusion), channel_id=1, source_target_pairs={{0,1},{1,2},{2,3},{3,4},{4,5},{5,6},{6,7},{7,8},{8,9},{9,10},{10,1... | collective-permute-start | bytes 1978376 | tf_op jit(solution)/shard_map/ppermute | solution.py:26
  13.2 44.6 %collective-permute-start.2 = (f32[1288,128]{1,0:T(8,128)}, f32[1288,128]{1,0:T(8,128)S(1)}, u32[]{:S(2)}, u32[]{:S(2)}) collective-permute-start(f32[1288,128]{1,0:T(8,128)} %select_maximum_fusion), channel_id=1, source_target_pairs={{1,0},{2,1},{3,2},{4,3},{5,4},{6,5},{7,6},{8,7},{9,8},{10,9},{11,1... | collective-permute-start | bytes 1978376 | tf_op jit(solution)/shard_map/ppermute | solution.py:26
  14.5 44.7 %collective-permute-start.3 = (f32[1288,128]{1,0:T(8,128)}, f32[1288,128]{1,0:T(8,128)}, u32[]{:S(2)}, u32[]{:S(2)}) collective-permute-start(f32[1288,128]{1,0:T(8,128)} %select_maximum_fusion), channel_id=1, source_target_pairs={{2,0},{3,1},{4,2},{5,3},{6,4},{7,5},{8,6},{9,7},{10,8},{11,9},{12,... | collective-permute-start | bytes 1978376 | tf_op jit(solution)/shard_map/ppermute | solution.py:26
  15.8 156.4 %collective-permute-start.14 = (bf16[512,1024]{1,0:T(8,128)(2,1)}, bf16[512,1024]{1,0:T(8,128)(2,1)}, u32[]{:S(2)}, u32[]{:S(2)}) collective-permute-start(bf16[512,1024]{1,0:T(8,128)(2,1)} %param.12), channel_id=1, source_target_pairs={{0,8},{1,9},{2,10},{3,11},{4,12},{5,13},{6,14},{7,15},{8,0},{9,1},... | collective-permute-start | bytes 3145736 | tf_op jit(solution)/shard_map/ppermute | solution.py:39
  46.8 148.9 %collective-permute-start.12 = (bf16[512,1024]{1,0:T(8,128)(2,1)}, bf16[512,1024]{1,0:T(8,128)(2,1)}, u32[]{:S(2)}, u32[]{:S(2)}) collective-permute-start(bf16[512,1024]{1,0:T(8,128)(2,1)} %param.12), channel_id=1, source_target_pairs={{0,4},{1,5},{2,6},{3,7},{4,0},{5,1},{6,2},{7,3},{8,12},{9,13},{10,... | collective-permute-start | bytes 3145736 | tf_op jit(solution)/shard_map/ppermute | solution.py:39
  47.8 99.6 %collective-permute-start.4 = (bf16[128,1024]{1,0:T(8,128)(2,1)}, bf16[128,1024]{1,0:T(8,128)(2,1)}, u32[]{:S(2)}, u32[]{:S(2)}) collective-permute-start(bf16[128,1024]{1,0:T(8,128)(2,1)} %get-tuple-element.22), channel_id=1, source_target_pairs={{0,1},{1,2},{2,3},{3,4},{4,5},{5,6},{6,7},{7,8},{8,9},{9,10},{10,1... | collective-permute-start | bytes 786440 | tf_op jit(solution)/shard_map/ppermute | solution.py:26
  57.9 1.3 copy-start.9
  57.9 93.7 %collective-permute-start.6 = (bf16[128,1024]{1,0:T(8,128)(2,1)}, bf16[128,1024]{1,0:T(8,128)(2,1)}, u32[]{:S(2)}, u32[]{:S(2)}) collective-permute-start(bf16[128,1024]{1,0:T(8,128)(2,1)} %get-tuple-element.23), channel_id=1, source_target_pairs={{1,0},{2,1},{3,2},{4,3},{5,4},{6,5},{7,6},{8,7},{9,8},{10,9},{11,1... | collective-permute-start | bytes 786440 | tf_op jit(solution)/shard_map/ppermute | solution.py:26
  77.4 4.3 %copy-start.10 = (f32[1288,128]{1,0:T(8,128)S(1)}, f32[1288,128]{1,0:T(8,128)}, u32[]{:S(2)}) copy-start(f32[1288,128]{1,0:T(8,128)} %copy-done.9) | copy-start | bytes 1978372
  88.5 5.1 %copy-start.2 = (f32[2304,128]{1,0:T(8,128)S(1)}, f32[2304,128]{1,0:T(8,128)}, u32[]{:S(2)}) copy-start(f32[2304,128]{1,0:T(8,128)} %get-tuple-element.18) | copy-start | bytes 3538948
  91.0 4.8 %copy-start.1 = (f32[40,3,64,64]{3,2,1,0:T(8,128)S(1)}, f32[40,3,64,64]{3,2,1,0:T(8,128)}, u32[]{:S(2)}) copy-start(f32[40,3,64,64]{3,2,1,0:T(8,128)} %constant_dynamic-update-slice_fusion.2) | copy-start | bytes 5898244
  91.0 4.8 %copy-start.4 = (f32[8,3,64,64]{3,2,1,0:T(8,128)S(1)}, f32[8,3,64,64]{3,2,1,0:T(8,128)}, u32[]{:S(2)}) copy-start(f32[8,3,64,64]{3,2,1,0:T(8,128)} %reshape.131) | copy-start | bytes 1179652
  93.6 2.3 copy-start.5
  95.9 4.0 %slice-start = ((s8[5898240]{0:T(1024)(128)(4,1)}), s8[4194304]{0:T(1024)(128)(4,1)S(1)}, s32[]{:S(2)}) async-start(s8[5898240]{0:T(1024)(128)(4,1)} %bitcast.243), calls=%async_computation | async-start | bytes 8388608
  96.0 4.0 %slice-start.1 = ((s8[5898240]{0:T(1024)(128)(4,1)}), s8[1703936]{0:T(1024)(128)(4,1)S(1)}, s32[]{:S(2)}) async-start(s8[5898240]{0:T(1024)(128)(4,1)} %bitcast.243), calls=%async_computation.1 | async-start | bytes 3407872
  106.4 1.2 copy-start.3
  127.3 17.9 %slice-start.2 = ((s8[6291456]{0:T(1024)(128)(4,1)}), s8[4194304]{0:T(1024)(128)(4,1)S(1)}, s32[]{:S(2)}) async-start(s8[6291456]{0:T(1024)(128)(4,1)} %bitcast.259), calls=%async_computation.2 | async-start | bytes 8388608
  130.2 15.0 %slice-start.3 = ((s8[6291456]{0:T(1024)(128)(4,1)}), s8[2097152]{0:T(1024)(128)(4,1)S(1)}, s32[]{:S(2)}) async-start(s8[6291456]{0:T(1024)(128)(4,1)} %bitcast.259), calls=%async_computation.3 | async-start | bytes 4194304
  130.3 2.4 copy-start.8
  132.7 10.8 %copy-start.6 = (bf16[128,1024]{1,0:T(8,128)(2,1)S(1)}, bf16[128,1024]{1,0:T(8,128)(2,1)}, u32[]{:S(2)}) copy-start(bf16[128,1024]{1,0:T(8,128)(2,1)} %param.19) | copy-start | bytes 786436
  139.2 9.9 %collective-permute-start.5 = (bf16[128,128]{1,0:T(8,128)(2,1)S(1)}, bf16[128,128]{1,0:T(8,128)(2,1)S(1)}, u32[]{:S(2)}, u32[]{:S(2)}) collective-permute-start(bf16[128,128]{1,0:T(8,128)(2,1)S(1)} %bitcast.258), channel_id=1, source_target_pairs={{0,1},{1,2},{2,3},{3,4},{4,5},{5,6},{6,7},{7,8},{8,9},{9,10},{10,1... | collective-permute-start | bytes 98312 | tf_op jit(solution)/shard_map/ppermute | solution.py:26
  147.4 54.7 %collective-permute-start.10 = (bf16[512,1024]{1,0:T(8,128)(2,1)}, bf16[512,1024]{1,0:T(8,128)(2,1)S(1)}, u32[]{:S(2)}, u32[]{:S(2)}) collective-permute-start(bf16[512,1024]{1,0:T(8,128)(2,1)} %param.12), channel_id=1, source_target_pairs={{0,2},{1,3},{2,0},{3,1},{4,6},{5,7},{6,4},{7,5},{8,10},{9,11},{10,... | collective-permute-start | bytes 3145736 | tf_op jit(solution)/shard_map/ppermute | solution.py:39
  149.1 3.7 %collective-permute-start.7 = (bf16[128,128]{1,0:T(8,128)(2,1)S(1)}, bf16[128,128]{1,0:T(8,128)(2,1)S(1)}, u32[]{:S(2)}, u32[]{:S(2)}) collective-permute-start(bf16[128,128]{1,0:T(8,128)(2,1)S(1)} %bitcast.257), channel_id=1, source_target_pairs={{1,0},{2,1},{3,2},{4,3},{5,4},{6,5},{7,6},{8,7},{9,8},{10,9},{11,1... | collective-permute-start | bytes 98312 | tf_op jit(solution)/shard_map/ppermute | solution.py:26
  151.6 56.9 %collective-permute-start.8 = (bf16[512,1024]{1,0:T(8,128)(2,1)}, bf16[512,1024]{1,0:T(8,128)(2,1)}, u32[]{:S(2)}, u32[]{:S(2)}) collective-permute-start(bf16[512,1024]{1,0:T(8,128)(2,1)} %param.12), channel_id=1, source_target_pairs={{0,1},{1,0},{2,3},{3,2},{4,5},{5,4},{6,7},{7,6},{8,9},{9,8},{10,11... | collective-permute-start | bytes 3145736 | tf_op jit(solution)/shard_map/ppermute | solution.py:39
  152.8 18.9 %collective-permute-start.15 = (bf16[512,128]{1,0:T(8,128)(2,1)S(1)}, bf16[512,128]{1,0:T(8,128)(2,1)S(1)}, u32[]{:S(2)}, u32[]{:S(2)}) collective-permute-start(bf16[512,128]{1,0:T(8,128)(2,1)S(1)} %bitcast.253), channel_id=1, source_target_pairs={{0,8},{1,9},{2,10},{3,11},{4,12},{5,13},{6,14},{7,15},{8,0},{9,1},... | collective-permute-start | bytes 393224 | tf_op jit(solution)/shard_map/ppermute | solution.py:39
  171.6 0.6 copy-start.11
  171.6 24.1 %collective-permute-start.13 = (bf16[512,128]{1,0:T(8,128)(2,1)S(1)}, bf16[512,128]{1,0:T(8,128)(2,1)}, u32[]{:S(2)}, u32[]{:S(2)}) collective-permute-start(bf16[512,128]{1,0:T(8,128)(2,1)S(1)} %bitcast.254), channel_id=1, source_target_pairs={{0,4},{1,5},{2,6},{3,7},{4,0},{5,1},{6,2},{7,3},{8,12},{9,13},{10,... | collective-permute-start | bytes 393224 | tf_op jit(solution)/shard_map/ppermute | solution.py:39
  172.3 29.9 %collective-permute-start.11 = (bf16[512,128]{1,0:T(8,128)(2,1)S(1)}, bf16[512,128]{1,0:T(8,128)(2,1)}, u32[]{:S(2)}, u32[]{:S(2)}) collective-permute-start(bf16[512,128]{1,0:T(8,128)(2,1)S(1)} %bitcast.255), channel_id=1, source_target_pairs={{0,2},{1,3},{2,0},{3,1},{4,6},{5,7},{6,4},{7,5},{8,10},{9,11},{10,... | collective-permute-start | bytes 393224 | tf_op jit(solution)/shard_map/ppermute | solution.py:39
  195.7 12.8 %collective-permute-start.9 = (bf16[512,128]{1,0:T(8,128)(2,1)S(1)}, bf16[512,128]{1,0:T(8,128)(2,1)}, u32[]{:S(2)}, u32[]{:S(2)}) collective-permute-start(bf16[512,128]{1,0:T(8,128)(2,1)S(1)} %bitcast.256), channel_id=1, source_target_pairs={{0,1},{1,0},{2,3},{3,2},{4,5},{5,4},{6,7},{7,6},{8,9},{9,8},{10,11... | collective-permute-start | bytes 393224 | tf_op jit(solution)/shard_map/ppermute | solution.py:39

commit v3 on v2

--- a/solution.py
+++ b/solution.py
@@ -52,29 +52,17 @@
 def chebyshev(struct_feats, op_blocks, laplace_index, series_coef, first_block):
     count = op_blocks.shape[0]
     chans = struct_feats.shape[1]
-    lap_rows = jnp.zeros((count, chans), jnp.float32).at[:, : laplace_index.shape[1]].set(
-        laplace_index.astype(jnp.float32)
-    )
-    payload = jnp.concatenate(
-        [struct_feats, op_blocks.reshape(-1, chans), lap_rows], axis=0
-    )
     reach_dev = -(-DEG * REACH // count)
+    payload = (struct_feats, op_blocks, laplace_index)
     parts = {0: payload}
     for off in range(1, reach_dev + 1):
         parts[-off] = shift_rows(payload, "seq", off)
         parts[off] = shift_rows(payload, "seq", -off)
     order = list(range(-reach_dev, reach_dev + 1))
     rows = count * BS
-    n_op = op_blocks.size // chans
-    field = jnp.concatenate([parts[o][:rows] for o in order], axis=0)
-    field = field.reshape(-1, BS, chans)
-    ops = jnp.concatenate(
-        [parts[o][rows : rows + n_op].reshape(op_blocks.shape) for o in order], axis=0
-    )
-    lap = jnp.concatenate(
-        [parts[o][rows + n_op : rows + n_op + count, : laplace_index.shape[1]] for o in order],
-        axis=0,
-    ).astype(jnp.int32)
+    field = jnp.concatenate([parts[o][0] for o in order], axis=0).reshape(-1, BS, chans)
+    ops = jnp.concatenate([parts[o][1] for o in order], axis=0)
+    lap = jnp.concatenate([parts[o][2] for o in order], axis=0)
     width = field.shape[0]
     centre = reach_dev * count
     block_ids = first_block - centre + jnp.arange(width, dtype=jnp.int32)
@@ -106,7 +94,7 @@
         encoding = encoding + series_coef[degree] * nxt[centre - lo : centre - lo + count]
         prev, prev_base = cur, cur_base
         cur, cur_base = nxt, lo
-    return encoding.reshape(rows, chans)
+    return encoding.reshape(rows, chans), parts
 
 
 def attention_kernel(table_ref, q_ref, *refs):
@@ -176,16 +164,19 @@
     levels = lax.axis_size("seq").bit_length() - 1
     bits = [link * (levels - 1) // (NEXP - 1) for link in range(NEXP)]
 
-    feats_before = shift_rows(node_feats[rows - rim:], "seq", 1)
-    feats_after = shift_rows(node_feats[:rim], "seq", -1)
-    feats_far = [partner(node_feats, "seq", bit) for bit in bits]
-
-    encoding = chebyshev(struct_feats, op_blocks, laplace_index, series_coef, first_block)
+    encoding, parts = chebyshev(struct_feats, op_blocks, laplace_index, series_coef, first_block)
+    held = lax.optimization_barrier((node_feats, [p[0] for p in parts.values()]))[0]
+    feats_before = shift_rows(held[rows - rim:], "seq", 1)
+    feats_after = shift_rows(held[:rim], "seq", -1)
+    feats_far = [partner(held, "seq", bit) for bit in bits[1:]]
+    encoding, feats_before, feats_after, feats_far = lax.optimization_barrier(
+        (encoding, feats_before, feats_after, feats_far)
+    )
     encoding_b = encoding.astype(jnp.bfloat16)
 
     enc_before = shift_rows(encoding_b[rows - rim:], "seq", 1)
     enc_after = shift_rows(encoding_b[:rim], "seq", -1)
-    enc_far = [partner(encoding_b, "seq", bit) for bit in bits]
+    enc_far = [partner(encoding_b, "seq", bit) for bit in bits[1:]]
 
     def blend(feats, enc):
         encoded = jnp.dot(enc, encode_weight, preferred_element_type=jnp.float32)
@@ -202,7 +193,8 @@
     kv_near = jnp.dot(near_blended, kv_weight, preferred_element_type=jnp.float32).astype(
         jnp.bfloat16
     )
-    kv_far = [
+    kv_own = kv_near[rim : rim + rows]
+    kv_far = [partner(kv_own, "seq", bits[0])] + [
         jnp.dot(blend(f, e), kv_weight, preferred_element_type=jnp.float32).astype(jnp.bfloat16)
         for f, e in zip(feats_far, enc_far)
     ]

time: 272 us -> 245 us (0.901)
  local copies, waits for them, and re-layouts: 49.2 us -> 12.8 us
  waiting for transfers between devices: 19.4 us -> 35.2 us
  matrix products: 76.6 us -> 69.8 us
    ppermute x8 -> x16, starting transfers between devices: 25.1 us -> 51 us  [shift_rows(): return lax.ppermute(x, axis, pairs)]
    ppermute x8 -> x7, starting transfers between devices: 38.2 us -> 15.1 us  [partner(): return lax.ppermute(value, axis, pairs)]
    unnamed x74 -> x55, local copies, waits for them, and re-layouts: 21.1 us -> 4.67 us
    ppermute x8 -> x16, waiting for transfers between devices: 19.3 us -> 35.2 us  [shift_rows(): return lax.ppermute(x, axis, pairs)]
    reshape x5 -> x0, local copies, waits for them, and re-layouts: 9.63 us -> none  [the longest x4 8.33 us: chebyshev(): parts[o][rows:rows + n_op].reshape(op_blocks.shape)]
    slice x14 -> x2, local copies, waits for them, and re-layouts: 11.1 us -> 3.62 us  [the longest x1 1.94 us: on_device(): feats_after = shift_rows(held[:rim], 'seq', -1)]
    dot_general x4 -> x3, matrix products: 25.7 us -> 19.4 us  [on_device(): jnp.dot(blend(f, e), kv_weight, preferred_element_type=jnp.float32)]
  transfers between devices with their start and end apart: 16 -> 23, of which waited for: 1 -> 3; matrix products, arithmetic and copies ran while one was open for 44% -> 36% of each run, Pallas kernels for 0% -> 0%
where the time goes in v3:
time: 245 us; the launch traced here: 241 us
  matrix products  69.8 us (28%)
  starting transfers between devices  66 us (27%)
  Pallas kernels  48.4 us (20%)
  waiting for transfers between devices  35.2 us (14%)
  local copies, waits for them, and re-layouts  12.8 us (5%)
  other arithmetic  7.05 us (3%)
    ppermute x16, starting transfers between devices, shift_rows(): return lax.ppermute(x, axis, pairs)  51 us
    pallas_call x1, Pallas kernels, attend(): pl.pallas_call(attention_kernel, grid_spec=grid_spec, out_shape=jax.Shape...  48.4 us
    dot_general x8, matrix products, step(): jnp.einsum('wosu,wouc->wsc', bands[lo:hi], stacked, precision=lax.Precisi...  36.9 us
    ppermute x16, waiting for transfers between devices, shift_rows(): return lax.ppermute(x, axis, pairs)  35.2 us
    dot_general x3, matrix products, on_device(): jnp.dot(blend(f, e), kv_weight, preferred_element_type=jnp.float32)  19.4 us
    ppermute x7, starting transfers between devices, partner(): return lax.ppermute(value, axis, pairs)  15.1 us
  transfers between devices with their start and end apart: 23, of which 3 were waited for; matrix products, arithmetic and copies ran while one was open for 36% of the time, Pallas kernels for 0%

profile of v3, /device:TPU:0, one launch (start us, length us, event | category | flops | bytes accessed | tf_op | source)
XLA Modules:
  0.0 240.6 jit_solution(15838074819069463042)
XLA Ops:
  0.0 5.7 %collective-permute-start.8 = (f32[512,128]{1,0:T(8,128)}, f32[512,128]{1,0:T(8,128)}, u32[]{:S(2)}, u32[]{:S(2)}) collective-permute-start(f32[512,128]{1,0:T(8,128)} %param.11), channel_id=1, source_target_pairs={{0,2},{1,3},{2,4},{3,5},{4,6},{5,7},{6,8},{7,9},{8,10},{9,11},{10,... | collective-permute-start | bytes 786440 | tf_op jit(solution)/shard_map/ppermute | solution.py:26
  5.7 1.5 collective-permute-start.9
  7.1 1.3 collective-permute-start.10
  8.4 5.6 %collective-permute-start = (s32[8,3]{0,1:T(4,128)}, s32[8,3]{0,1:T(4,128)S(1)}, u32[]{:S(2)}, u32[]{:S(2)}) collective-permute-start(s32[8,3]{0,1:T(4,128)} %param.13), channel_id=1, source_target_pairs={{0,2},{1,3},{2,4},{3,5},{4,6},{5,7},{6,8},{7,9},{8,10},{9,11},{10,... | collective-permute-start | bytes 296 | tf_op jit(solution)/shard_map/ppermute | solution.py:26
  14.0 1.5 collective-permute-start.1
  15.5 1.7 fusion.148
  19.4 1.3 collective-permute-start.2
  20.7 1.3 collective-permute-start.3
  22.0 3.1 %collective-permute-done.2 = s32[8,3]{0,1:T(4,128)S(1)} collective-permute-done((s32[8,3]{0,1:T(4,128)}, s32[8,3]{0,1:T(4,128)S(1)}, u32[]{:S(2)}, u32[]{:S(2)}) %collective-permute-start.2) | collective-permute-done | bytes 128 | tf_op jit(solution)/shard_map/ppermute | solution.py:26
  25.1 1.3 collective-permute-start.11
  26.4 3.2 %collective-permute-done.3 = s32[8,3]{0,1:T(4,128)S(1)} collective-permute-done((s32[8,3]{0,1:T(4,128)}, s32[8,3]{0,1:T(4,128)S(1)}, u32[]{:S(2)}, u32[]{:S(2)}) %collective-permute-start.3) | collective-permute-done | bytes 128 | tf_op jit(solution)/shard_map/ppermute | solution.py:26
  29.6 4.9 %collective-permute-start.4 = (f32[8,3,64,64]{3,2,1,0:T(8,128)}, f32[8,3,64,64]{3,2,1,0:T(8,128)S(1)}, u32[]{:S(2)}, u32[]{:S(2)}) collective-permute-start(f32[8,3,64,64]{3,2,1,0:T(8,128)} %param.12), channel_id=1, source_target_pairs={{0,2},{1,3},{2,4},{3,5},{4,6},{5,7},{6,8},{7,9},{8,10},{9,11},{10,... | collective-permute-start | bytes 1179656 | tf_op jit(solution)/shard_map/ppermute | solution.py:26
  35.4 1.3 collective-permute-start.5
  37.8 1.3 collective-permute-start.6
  39.1 2.3 broadcast_multiply_fusion
  41.4 1.3 collective-permute-start.7
  42.7 1.0 constant_dynamic-update-slice_fusion.5
  44.3 4.2 %collective-permute-start.14 = (bf16[512,1024]{1,0:T(8,128)(2,1)}, bf16[512,1024]{1,0:T(8,128)(2,1)}, u32[]{:S(2)}, u32[]{:S(2)}) collective-permute-start(bf16[512,1024]{1,0:T(8,128)(2,1)} %param.10), channel_id=1, source_target_pairs={{0,2},{1,3},{2,0},{3,1},{4,6},{5,7},{6,4},{7,5},{8,10},{9,11},{10,... | collective-permute-start | bytes 3145736 | tf_op jit(solution)/shard_map/ppermute | solution.py:39
  49.0 1.9 fusion.146
  51.0 28.9 %collective-permute-done.4 = f32[8,3,64,64]{3,2,1,0:T(8,128)S(1)} collective-permute-done((f32[8,3,64,64]{3,2,1,0:T(8,128)}, f32[8,3,64,64]{3,2,1,0:T(8,128)S(1)}, u32[]{:S(2)}, u32[]{:S(2)}) %collective-permute-start.4) | collective-permute-done | bytes 393248 | tf_op jit(solution)/shard_map/ppermute | solution.py:26
  79.9 1.8 collective-permute-start.15
  82.3 19.0 %collective-permute-start.12 = (bf16[128,1024]{1,0:T(8,128)(2,1)}, bf16[128,1024]{1,0:T(8,128)(2,1)}, u32[]{:S(2)}, u32[]{:S(2)}) collective-permute-start(bf16[128,1024]{1,0:T(8,128)(2,1)} %get-tuple-element.25), channel_id=1, source_target_pairs={{0,1},{1,2},{2,3},{3,4},{4,5},{5,6},{6,7},{7,8},{8,9},{9,10},{10,1... | collective-permute-start | bytes 786440 | tf_op jit(solution)/shard_map/ppermute | solution.py:26
  101.4 1.3 collective-permute-start.13
  102.7 3.9 %select_reduce_fusion = f32[40,5,64,64]{3,2,1,0:T(8,128)S(1)} fusion(f32[40,3,64,64]{3,2,1,0:T(8,128)S(1)} %constant_dynamic-update-slice_fusion, pred[40,3,5]{2,1,0:T(4,128)(4,1)S(1)} %iota_compare_fusion), kind=kLoop, calls=%fused_computation | loop fusion | flops 4096000 | bytes 5243480 | tf_op jit(solution)/shard_map/reduce_sum | solution.py:72
  106.7 6.2 %convolution_bitcast_fusion = f32[36,64,128]{2,1,0:T(8,128)S(1)} fusion(f32[40,5,64,64]{3,2,1,0:T(8,128)S(1)} %select_reduce_fusion, f32[36,5,64,128]{3,2,1,0:T(8,128)S(1)} %constant_dynamic-update-slice_fusion.10), kind=kOutput, calls=%fused_computation.34 | convolution fusion | flops 1132462080 | bytes 10354688 | tf_op jit(solution)/shard_map/wosu,wouc->wsc/dot_general | solution.py:81
  113.4 5.6 %fusion.32 = f32[32,64,128]{2,1,0:T(8,128)S(1)} fusion(f32[32,64,128]{2,1,0:T(8,128)S(1)} %bitcast.240, f32[40,5,64,64]{3,2,1,0:T(8,128)S(1)} %select_reduce_fusion, f32[32,5,64,128]{3,2,0,1:T(8,128)S(1)} %fusion.103), kind=kOutput, calls=%fused_computation.37 | convolution fusion | flops 1007157248 | bytes 10616832 | tf_op jit(solution)/shard_map/wosu,wouc->wsc/dot_general | solution.py:81
  119.4 4.8 %fusion.41 = f32[28,64,128]{2,1,0:T(8,128)S(1)} fusion(f32[40,5,64,64]{3,2,1,0:T(8,128)S(1)} %select_reduce_fusion, f32[28,5,64,128]{3,2,0,1:T(8,128)S(1)} %fusion.108, f32[36,64,128]{2,1,0:T(8,128)S(1)} %convolution_bitcast_fusion), kind=kOutput, calls=%fused_computation.40 | convolution fusion | flops 881262592 | bytes 9699328 | tf_op jit(solution)/shard_map/wosu,wouc->wsc/dot_general | solution.py:81
  124.6 4.2 %fusion.52 = f32[24,64,128]{2,1,0:T(8,128)S(1)} fusion(f32[40,5,64,64]{3,2,1,0:T(8,128)S(1)} %select_reduce_fusion, f32[24,5,64,128]{3,2,0,1:T(8,128)S(1)} %fusion.113, f32[32,64,128]{2,1,0:T(8,128)S(1)} %fusion.32), kind=kOutput, calls=%fused_computation.45 | convolution fusion | flops 755367936 | bytes 8781824 | tf_op jit(solution)/shard_map/wosu,wouc->wsc/dot_general | solution.py:81
  129.0 3.7 %fusion.61 = f32[20,64,128]{2,1,0:T(8,128)S(1)} fusion(f32[40,5,64,64]{3,2,1,0:T(8,128)S(1)} %select_reduce_fusion, f32[20,5,64,128]{3,2,0,1:T(8,128)S(1)} %fusion.118, f32[28,64,128]{2,1,0:T(8,128)S(1)} %fusion.41), kind=kOutput, calls=%fused_computation.48 | convolution fusion | flops 629473280 | bytes 7864320 | tf_op jit(solution)/shard_map/wosu,wouc->wsc/dot_general | solution.py:81
  133.0 2.8 %fusion.70 = f32[16,64,128]{2,1,0:T(8,128)S(1)} fusion(f32[40,5,64,64]{3,2,1,0:T(8,128)S(1)} %select_reduce_fusion, f32[16,5,64,128]{3,2,0,1:T(8,128)S(1)} %fusion.123, f32[24,64,128]{2,1,0:T(8,128)S(1)} %fusion.52), kind=kOutput, calls=%fused_computation.51 | convolution fusion | flops 503578624 | bytes 6946816 | tf_op jit(solution)/shard_map/wosu,wouc->wsc/dot_general | solution.py:81
  136.0 2.2 fusion.94
  138.4 7.3 %fusion.91 = bf16[8,64,128]{2,1,0:T(8,128)(2,1)S(1)} fusion(f32[40,5,64,64]{3,2,1,0:T(8,128)S(1)} %select_reduce_fusion, f32[8,5,64,128]{3,2,0,1:T(8,128)S(1)} %fusion.133, f32[20,64,128]{2,1,0:T(8,128)S(1)} %fusion.61, f32[24,64,128]{2,1,0:T(8,128)S(1)} %fusion.52, f32[28,64,128]{2,1,0:T(8,128)S(1)} %fusion.41, f32[32,64,128]{2,1,0:T(8,128)S(1)} %fusion.32, ...), kind=kOutput, calls=%fused_computation.58 | convolution fusion | flops 252903424 | bytes 6815776 | tf_op jit(solution)/shard_map/wosu,wouc->wsc/dot_general | solution.py:81
  145.8 2.7 %collective-permute-start.22 = (bf16[512,128]{1,0:T(8,128)(2,1)S(1)}, bf16[512,128]{1,0:T(8,128)(2,1)S(1)}, u32[]{:S(2)}, u32[]{:S(2)}) collective-permute-start(bf16[512,128]{1,0:T(8,128)(2,1)S(1)} %bitcast.242), channel_id=1, source_target_pairs={{0,8},{1,9},{2,10},{3,11},{4,12},{5,13},{6,14},{7,15},{8,0},{9,1},... | collective-permute-start | bytes 393224 | tf_op jit(solution)/shard_map/ppermute | solution.py:39
  148.5 4.1 %collective-permute-start.20 = (bf16[512,128]{1,0:T(8,128)(2,1)S(1)}, bf16[512,128]{1,0:T(8,128)(2,1)S(1)}, u32[]{:S(2)}, u32[]{:S(2)}) collective-permute-start(bf16[512,128]{1,0:T(8,128)(2,1)S(1)} %bitcast.244), channel_id=1, source_target_pairs={{0,2},{1,3},{2,0},{3,1},{4,6},{5,7},{6,4},{7,5},{8,10},{9,11},{10,... | collective-permute-start | bytes 393224 | tf_op jit(solution)/shard_map/ppermute | solution.py:39
  152.6 1.3 collective-permute-start.17
  153.9 1.3 collective-permute-start.18
  155.2 1.6 add_convert_fusion.3
  156.8 1.2 add_convert_fusion.8
  158.0 1.2 add_convert_fusion.7
  159.2 3.9 %convolution_convert_fusion.refs_0_.refs_1_.refs_2_.refs_3_ = bf16[768,2048]{1,0:T(8,128)(2,1)S(1)} fusion(bf16[1024,3072]{1,0:T(8,128)(2,1)S(1)} %bitcast.248, bf16[128,1024]{1,0:T(8,128)(2,1)S(1)} %add_convert_fusion.7, bf16[512,1024]{1,0:T(8,128)(2,1)S(1)} %add_convert_fusion.3, bf16[128,1024]{1,0:T(8,128)(2,1)S(1)} %add_convert_fusion.8), kind=kOutput, calls=%fused_computation.7 | convolution fusion | flops 3227516928 | bytes 8912896 | tf_op jit(solution)/shard_map/dot_general | solution.py:193
  163.1 1.7 slice.371
  164.8 1.8 collective-permute-start.19
  166.6 2.2 fusion.23.q_ref
  168.9 6.4 %convolution_convert_fusion.1.refs_7_ = bf16[512,2048]{1,0:T(8,128)(2,1)} fusion(bf16[1024,3072]{1,0:T(8,128)(2,1)} %param.18, bf16[512,1024]{1,0:T(8,128)(2,1)} %collective-permute-done.16, bf16[512,128]{1,0:T(8,128)(2,1)S(1)} %collective-permute-done.22, bf16[128,1024]{1,0:T(8,128)(2,1)S(1)} %copy-done.2), kind=kOutput, calls=%fused_computation.10 | convolution fusion | flops 2284322816 | bytes 7733248 | tf_op jit(solution)/shard_map/dot_general | solution.py:198
  175.3 6.5 %convolution_convert_fusion.2.refs_6_ = bf16[512,2048]{1,0:T(8,128)(2,1)} fusion(bf16[1024,3072]{1,0:T(8,128)(2,1)} %param.18, bf16[512,1024]{1,0:T(8,128)(2,1)} %collective-permute-done.15, bf16[512,128]{1,0:T(8,128)(2,1)S(1)} %collective-permute-done.21, bf16[128,1024]{1,0:T(8,128)(2,1)S(1)} %copy-done.2), kind=kOutput, calls=%fused_computation.11 | convolution fusion | flops 2284322816 | bytes 7733248 | tf_op jit(solution)/shard_map/dot_general | solution.py:198
  181.8 6.4 %convolution_convert_fusion.3.refs_5_ = bf16[512,2048]{1,0:T(8,128)(2,1)} fusion(bf16[1024,3072]{1,0:T(8,128)(2,1)} %param.18, bf16[512,1024]{1,0:T(8,128)(2,1)} %collective-permute-done.14, bf16[512,128]{1,0:T(8,128)(2,1)S(1)} %collective-permute-done.20, bf16[128,1024]{1,0:T(8,128)(2,1)S(1)} %copy-done.2), kind=kOutput, calls=%fused_computation.12 | convolution fusion | flops 2284322816 | bytes 7733248 | tf_op jit(solution)/shard_map/dot_general | solution.py:198
  188.3 48.4 %shard_map.100 = bf16[512,1024]{1,0:T(8,128)(2,1)} custom-call(s32[8,8]{1,0:T(8,128)} %pad_add_fusion.table_ref, bf16[512,1024]{1,0:T(8,128)(2,1)} %fusion.23.q_ref, bf16[768,2048]{1,0:T(8,128)(2,1)} %copy-done.1, bf16[768,2048]{1,0:T(8,128)(2,1)} %copy-done.1, bf16[768,2048]{1,0:T(8,128)(2,1)} %copy-done.1, bf16[768,2048]{1,0:T(8,128)(2,1)} %copy-done.1, ...), custom_call_target="tpu_custom_call" | custom-call | tf_op jit(solution)/shard_map/pallas_call | solution.py:141
  236.7 3.4 %convolution_convert_fusion.4 = bf16[512,1024]{1,0:T(8,128)(2,1)} fusion(bf16[512,1024]{1,0:T(8,128)(2,1)} %shard_map.100, bf16[1024,1024]{1,0:T(8,128)(2,1)S(1)} %copy-done), kind=kOutput, calls=%fused_computation.33 | convolution fusion | flops 1074266112 | bytes 4194304 | tf_op jit(solution)/shard_map/dot_general | solution.py:209
  (99 shorter events, 7.8 us)
Async XLA Ops:
  0.0 236.7 %copy-start = (bf16[1024,1024]{1,0:T(8,128)(2,1)S(1)}, bf16[1024,1024]{1,0:T(8,128)(2,1)}, u32[]{:S(2)}) copy-start(bf16[1024,1024]{1,0:T(8,128)(2,1)} %param.19) | copy-start | bytes 6291460
  0.0 35.4 %collective-permute-start.8 = (f32[512,128]{1,0:T(8,128)}, f32[512,128]{1,0:T(8,128)}, u32[]{:S(2)}, u32[]{:S(2)}) collective-permute-start(f32[512,128]{1,0:T(8,128)} %param.11), channel_id=1, source_target_pairs={{0,2},{1,3},{2,4},{3,5},{4,6},{5,7},{6,8},{7,9},{8,10},{9,11},{10,... | collective-permute-start | bytes 786440 | tf_op jit(solution)/shard_map/ppermute | solution.py:26
  5.7 32.1 %collective-permute-start.9 = (f32[512,128]{1,0:T(8,128)}, f32[512,128]{1,0:T(8,128)S(1)}, u32[]{:S(2)}, u32[]{:S(2)}) collective-permute-start(f32[512,128]{1,0:T(8,128)} %param.11), channel_id=1, source_target_pairs={{0,1},{1,2},{2,3},{3,4},{4,5},{5,6},{6,7},{7,8},{8,9},{9,10},{10,1... | collective-permute-start | bytes 786440 | tf_op jit(solution)/shard_map/ppermute | solution.py:26
  7.1 34.3 %collective-permute-start.10 = (f32[512,128]{1,0:T(8,128)}, f32[512,128]{1,0:T(8,128)S(1)}, u32[]{:S(2)}, u32[]{:S(2)}) collective-permute-start(f32[512,128]{1,0:T(8,128)} %param.11), channel_id=1, source_target_pairs={{1,0},{2,1},{3,2},{4,3},{5,4},{6,5},{7,6},{8,7},{9,8},{10,9},{11,1... | collective-permute-start | bytes 786440 | tf_op jit(solution)/shard_map/ppermute | solution.py:26
  8.4 11.0 %collective-permute-start = (s32[8,3]{0,1:T(4,128)}, s32[8,3]{0,1:T(4,128)S(1)}, u32[]{:S(2)}, u32[]{:S(2)}) collective-permute-start(s32[8,3]{0,1:T(4,128)} %param.13), channel_id=1, source_target_pairs={{0,2},{1,3},{2,4},{3,5},{4,6},{5,7},{6,8},{7,9},{8,10},{9,11},{10,... | collective-permute-start | bytes 296 | tf_op jit(solution)/shard_map/ppermute | solution.py:26
  14.0 6.7 %collective-permute-start.1 = (s32[8,3]{0,1:T(4,128)}, s32[8,3]{0,1:T(4,128)S(1)}, u32[]{:S(2)}, u32[]{:S(2)}) collective-permute-start(s32[8,3]{0,1:T(4,128)} %param.13), channel_id=1, source_target_pairs={{0,1},{1,2},{2,3},{3,4},{4,5},{5,6},{6,7},{7,8},{8,9},{9,10},{10,1... | collective-permute-start | bytes 296 | tf_op jit(solution)/shard_map/ppermute | solution.py:26
  19.4 5.7 %collective-permute-start.2 = (s32[8,3]{0,1:T(4,128)}, s32[8,3]{0,1:T(4,128)S(1)}, u32[]{:S(2)}, u32[]{:S(2)}) collective-permute-start(s32[8,3]{0,1:T(4,128)} %param.13), channel_id=1, source_target_pairs={{1,0},{2,1},{3,2},{4,3},{5,4},{6,5},{7,6},{8,7},{9,8},{10,9},{11,1... | collective-permute-start | bytes 296 | tf_op jit(solution)/shard_map/ppermute | solution.py:26
  20.7 8.8 %collective-permute-start.3 = (s32[8,3]{0,1:T(4,128)}, s32[8,3]{0,1:T(4,128)S(1)}, u32[]{:S(2)}, u32[]{:S(2)}) collective-permute-start(s32[8,3]{0,1:T(4,128)} %param.13), channel_id=1, source_target_pairs={{2,0},{3,1},{4,2},{5,3},{6,4},{7,5},{8,6},{9,7},{10,8},{11,9},{12,... | collective-permute-start | bytes 296 | tf_op jit(solution)/shard_map/ppermute | solution.py:26
  25.1 17.6 %collective-permute-start.11 = (f32[512,128]{1,0:T(8,128)}, f32[512,128]{1,0:T(8,128)}, u32[]{:S(2)}, u32[]{:S(2)}) collective-permute-start(f32[512,128]{1,0:T(8,128)} %param.11), channel_id=1, source_target_pairs={{2,0},{3,1},{4,2},{5,3},{6,4},{7,5},{8,6},{9,7},{10,8},{11,9},{12,... | collective-permute-start | bytes 786440 | tf_op jit(solution)/shard_map/ppermute | solution.py:26
  29.6 50.3 %collective-permute-start.4 = (f32[8,3,64,64]{3,2,1,0:T(8,128)}, f32[8,3,64,64]{3,2,1,0:T(8,128)S(1)}, u32[]{:S(2)}, u32[]{:S(2)}) collective-permute-start(f32[8,3,64,64]{3,2,1,0:T(8,128)} %param.12), channel_id=1, source_target_pairs={{0,2},{1,3},{2,4},{3,5},{4,6},{5,7},{6,8},{7,9},{8,10},{9,11},{10,... | collective-permute-start | bytes 1179656 | tf_op jit(solution)/shard_map/ppermute | solution.py:26
  35.4 46.3 %collective-permute-start.5 = (f32[8,3,64,64]{3,2,1,0:T(8,128)}, f32[8,3,64,64]{3,2,1,0:T(8,128)S(1)}, u32[]{:S(2)}, u32[]{:S(2)}) collective-permute-start(f32[8,3,64,64]{3,2,1,0:T(8,128)} %param.12), channel_id=1, source_target_pairs={{0,1},{1,2},{2,3},{3,4},{4,5},{5,6},{6,7},{7,8},{8,9},{9,10},{10,1... | collective-permute-start | bytes 1179656 | tf_op jit(solution)/shard_map/ppermute | solution.py:26
  37.8 44.5 %collective-permute-start.6 = (f32[8,3,64,64]{3,2,1,0:T(8,128)}, f32[8,3,64,64]{3,2,1,0:T(8,128)S(1)}, u32[]{:S(2)}, u32[]{:S(2)}) collective-permute-start(f32[8,3,64,64]{3,2,1,0:T(8,128)} %param.12), channel_id=1, source_target_pairs={{1,0},{2,1},{3,2},{4,3},{5,4},{6,5},{7,6},{8,7},{9,8},{10,9},{11,1... | collective-permute-start | bytes 1179656 | tf_op jit(solution)/shard_map/ppermute | solution.py:26
  41.4 60.0 %collective-permute-start.7 = (f32[8,3,64,64]{3,2,1,0:T(8,128)}, f32[8,3,64,64]{3,2,1,0:T(8,128)S(1)}, u32[]{:S(2)}, u32[]{:S(2)}) collective-permute-start(f32[8,3,64,64]{3,2,1,0:T(8,128)} %param.12), channel_id=1, source_target_pairs={{2,0},{3,1},{4,2},{5,3},{6,4},{7,5},{8,6},{9,7},{10,8},{11,9},{12,... | collective-permute-start | bytes 1179656 | tf_op jit(solution)/shard_map/ppermute | solution.py:26
  44.3 101.4 %collective-permute-start.14 = (bf16[512,1024]{1,0:T(8,128)(2,1)}, bf16[512,1024]{1,0:T(8,128)(2,1)}, u32[]{:S(2)}, u32[]{:S(2)}) collective-permute-start(bf16[512,1024]{1,0:T(8,128)(2,1)} %param.10), channel_id=1, source_target_pairs={{0,2},{1,3},{2,0},{3,1},{4,6},{5,7},{6,4},{7,5},{8,10},{9,11},{10,... | collective-permute-start | bytes 3145736 | tf_op jit(solution)/shard_map/ppermute | solution.py:39
  48.9 33.3 %copy-start.4 = (f32[8,3,64,64]{3,2,1,0:T(8,128)S(1)}, f32[8,3,64,64]{3,2,1,0:T(8,128)}, u32[]{:S(2)}) copy-start(f32[8,3,64,64]{3,2,1,0:T(8,128)} %param.12) | copy-start | bytes 1179652
  79.9 65.9 %collective-permute-start.15 = (bf16[512,1024]{1,0:T(8,128)(2,1)}, bf16[512,1024]{1,0:T(8,128)(2,1)}, u32[]{:S(2)}, u32[]{:S(2)}) collective-permute-start(bf16[512,1024]{1,0:T(8,128)(2,1)} %param.10), channel_id=1, source_target_pairs={{0,4},{1,5},{2,6},{3,7},{4,0},{5,1},{6,2},{7,3},{8,12},{9,13},{10,... | collective-permute-start | bytes 3145736 | tf_op jit(solution)/shard_map/ppermute | solution.py:39
  81.7 64.0 %collective-permute-start.16 = (bf16[512,1024]{1,0:T(8,128)(2,1)}, bf16[512,1024]{1,0:T(8,128)(2,1)}, u32[]{:S(2)}, u32[]{:S(2)}) collective-permute-start(bf16[512,1024]{1,0:T(8,128)(2,1)} %param.10), channel_id=1, source_target_pairs={{0,8},{1,9},{2,10},{3,11},{4,12},{5,13},{6,14},{7,15},{8,0},{9,1},... | collective-permute-start | bytes 3145736 | tf_op jit(solution)/shard_map/ppermute | solution.py:39
  82.3 63.4 %collective-permute-start.12 = (bf16[128,1024]{1,0:T(8,128)(2,1)}, bf16[128,1024]{1,0:T(8,128)(2,1)}, u32[]{:S(2)}, u32[]{:S(2)}) collective-permute-start(bf16[128,1024]{1,0:T(8,128)(2,1)} %get-tuple-element.25), channel_id=1, source_target_pairs={{0,1},{1,2},{2,3},{3,4},{4,5},{5,6},{6,7},{7,8},{8,9},{9,10},{10,1... | collective-permute-start | bytes 786440 | tf_op jit(solution)/shard_map/ppermute | solution.py:26
  101.4 44.3 %collective-permute-start.13 = (bf16[128,1024]{1,0:T(8,128)(2,1)}, bf16[128,1024]{1,0:T(8,128)(2,1)}, u32[]{:S(2)}, u32[]{:S(2)}) collective-permute-start(bf16[128,1024]{1,0:T(8,128)(2,1)} %get-tuple-element.24), channel_id=1, source_target_pairs={{1,0},{2,1},{3,2},{4,3},{5,4},{6,5},{7,6},{8,7},{9,8},{10,9},{11,1... | collective-permute-start | bytes 786440 | tf_op jit(solution)/shard_map/ppermute | solution.py:26
  136.0 2.4 copy-start.3
  138.4 20.8 %slice-start = ((s8[6291456]{0:T(1024)(128)(4,1)}), s8[4194304]{0:T(1024)(128)(4,1)S(1)}, s32[]{:S(2)}) async-start(s8[6291456]{0:T(1024)(128)(4,1)} %bitcast.247), calls=%async_computation | async-start | bytes 8388608
  138.4 16.7 %copy-start.2 = (bf16[128,1024]{1,0:T(8,128)(2,1)S(1)}, bf16[128,1024]{1,0:T(8,128)(2,1)}, u32[]{:S(2)}) copy-start(bf16[128,1024]{1,0:T(8,128)(2,1)} %param.17) | copy-start | bytes 786436
  138.4 20.8 %slice-start.1 = ((s8[6291456]{0:T(1024)(128)(4,1)}), s8[2097152]{0:T(1024)(128)(4,1)S(1)}, s32[]{:S(2)}) async-start(s8[6291456]{0:T(1024)(128)(4,1)} %bitcast.247), calls=%async_computation.1 | async-start | bytes 4194304
  145.8 23.1 %collective-permute-start.22 = (bf16[512,128]{1,0:T(8,128)(2,1)S(1)}, bf16[512,128]{1,0:T(8,128)(2,1)S(1)}, u32[]{:S(2)}, u32[]{:S(2)}) collective-permute-start(bf16[512,128]{1,0:T(8,128)(2,1)S(1)} %bitcast.242), channel_id=1, source_target_pairs={{0,8},{1,9},{2,10},{3,11},{4,12},{5,13},{6,14},{7,15},{8,0},{9,1},... | collective-permute-start | bytes 393224 | tf_op jit(solution)/shard_map/ppermute | solution.py:39
  148.5 26.8 %collective-permute-start.21 = (bf16[512,128]{1,0:T(8,128)(2,1)S(1)}, bf16[512,128]{1,0:T(8,128)(2,1)S(1)}, u32[]{:S(2)}, u32[]{:S(2)}) collective-permute-start(bf16[512,128]{1,0:T(8,128)(2,1)S(1)} %bitcast.243), channel_id=1, source_target_pairs={{0,4},{1,5},{2,6},{3,7},{4,0},{5,1},{6,2},{7,3},{8,12},{9,13},{10,... | collective-permute-start | bytes 393224 | tf_op jit(solution)/shard_map/ppermute | solution.py:39
  148.5 33.4 %collective-permute-start.20 = (bf16[512,128]{1,0:T(8,128)(2,1)S(1)}, bf16[512,128]{1,0:T(8,128)(2,1)S(1)}, u32[]{:S(2)}, u32[]{:S(2)}) collective-permute-start(bf16[512,128]{1,0:T(8,128)(2,1)S(1)} %bitcast.244), channel_id=1, source_target_pairs={{0,2},{1,3},{2,0},{3,1},{4,6},{5,7},{6,4},{7,5},{8,10},{9,11},{10,... | collective-permute-start | bytes 393224 | tf_op jit(solution)/shard_map/ppermute | solution.py:39
  152.6 4.3 %collective-permute-start.17 = (bf16[128,128]{1,0:T(8,128)(2,1)S(1)}, bf16[128,128]{1,0:T(8,128)(2,1)S(1)}, u32[]{:S(2)}, u32[]{:S(2)}) collective-permute-start(bf16[128,128]{1,0:T(8,128)(2,1)S(1)} %get-tuple-element.28), channel_id=1, source_target_pairs={{0,1},{1,2},{2,3},{3,4},{4,5},{5,6},{6,7},{7,8},{8,9},{9,10},{10,1... | collective-permute-start | bytes 98312 | tf_op jit(solution)/shard_map/ppermute | solution.py:26
  153.9 4.2 %collective-permute-start.18 = (bf16[128,128]{1,0:T(8,128)(2,1)S(1)}, bf16[128,128]{1,0:T(8,128)(2,1)S(1)}, u32[]{:S(2)}, u32[]{:S(2)}) collective-permute-start(bf16[128,128]{1,0:T(8,128)(2,1)S(1)} %get-tuple-element.29), channel_id=1, source_target_pairs={{1,0},{2,1},{3,2},{4,3},{5,4},{6,5},{7,6},{8,7},{9,8},{10,9},{11,1... | collective-permute-start | bytes 98312 | tf_op jit(solution)/shard_map/ppermute | solution.py:26
  163.1 5.8 %copy-start.1 = (bf16[768,2048]{1,0:T(8,128)(2,1)}, bf16[768,2048]{1,0:T(8,128)(2,1)S(1)}, u32[]{:S(2)}) copy-start(bf16[768,2048]{1,0:T(8,128)(2,1)S(1)} %convolution_convert_fusion.refs_0_.refs_1_.refs_2_.refs_3_) | copy-start | bytes 9437188
  164.8 23.4 %collective-permute-start.19 = (bf16[512,2048]{1,0:T(8,128)(2,1)}, bf16[512,2048]{1,0:T(8,128)(2,1)}, u32[]{:S(2)}, u32[]{:S(2)}) collective-permute-start(bf16[512,2048]{1,0:T(8,128)(2,1)} %slice.371), channel_id=1, source_target_pairs={{0,1},{1,0},{2,3},{3,2},{4,5},{5,4},{6,7},{7,6},{8,9},{9,8},{10,11... | collective-permute-start | bytes 6291464 | tf_op jit(solution)/shard_map/ppermute | solution.py:39

commit v4 on v3

--- a/solution.py
+++ b/solution.py
@@ -52,34 +52,31 @@
 def chebyshev(struct_feats, op_blocks, laplace_index, series_coef, first_block):
     count = op_blocks.shape[0]
     chans = struct_feats.shape[1]
+    taps = 2 * REACH + 1
     reach_dev = -(-DEG * REACH // count)
-    payload = (struct_feats, op_blocks, laplace_index)
+    block_ids = first_block + jnp.arange(count, dtype=jnp.int32)
+    offsets = laplace_index - block_ids[:, None] + REACH
+    hit = offsets[:, :, None] == jnp.arange(taps, dtype=jnp.int32)[None, None, :]
+    bands = jnp.sum(jnp.where(hit[:, :, :, None, None], op_blocks[:, :, None], 0.0), axis=1)
+    bands = bands.transpose(0, 2, 1, 3).reshape(count, BS, taps * BS)
+    payload = jnp.concatenate([struct_feats.reshape(count, BS, chans), bands], axis=2)
     parts = {0: payload}
     for off in range(1, reach_dev + 1):
         parts[-off] = shift_rows(payload, "seq", off)
         parts[off] = shift_rows(payload, "seq", -off)
-    order = list(range(-reach_dev, reach_dev + 1))
-    rows = count * BS
-    field = jnp.concatenate([parts[o][0] for o in order], axis=0).reshape(-1, BS, chans)
-    ops = jnp.concatenate([parts[o][1] for o in order], axis=0)
-    lap = jnp.concatenate([parts[o][2] for o in order], axis=0)
-    width = field.shape[0]
+    window = jnp.concatenate([parts[o] for o in range(-reach_dev, reach_dev + 1)], axis=0)
+    field = window[:, :, :chans]
+    bands = window[:, :, chans:]
+    width = window.shape[0]
     centre = reach_dev * count
-    block_ids = first_block - centre + jnp.arange(width, dtype=jnp.int32)
-    offsets = lap - block_ids[:, None] + REACH
-    diag = jnp.arange(2 * REACH + 1, dtype=jnp.int32)
-    hit = offsets[:, :, None] == diag[None, None, :]
-    bands = jnp.sum(
-        jnp.where(hit[:, :, :, None, None], ops[:, :, None, :, :], 0.0), axis=1
-    )
 
     def step(values, lo, hi, base):
         stacked = jnp.stack(
-            [values[lo - REACH + o - base : hi - REACH + o - base] for o in range(2 * REACH + 1)],
-            axis=1,
-        )
+            [values[lo - REACH + o - base : hi - REACH + o - base] for o in range(taps)], axis=1
+        ).reshape(hi - lo, taps * BS, chans)
         return jnp.einsum(
-            "wosu,wouc->wsc", bands[lo:hi], stacked, precision=lax.Precision.HIGHEST
+            "wsk,wkc->wsc", bands[lo:hi], stacked, precision=lax.Precision.HIGH,
+            preferred_element_type=jnp.float32,
         )
 
     own = slice(centre, centre + count)
@@ -94,7 +91,7 @@
         encoding = encoding + series_coef[degree] * nxt[centre - lo : centre - lo + count]
         prev, prev_base = cur, cur_base
         cur, cur_base = nxt, lo
-    return encoding.reshape(rows, chans), parts
+    return encoding.reshape(count * BS, chans), parts
 
 
 def attention_kernel(table_ref, q_ref, *refs):
@@ -165,7 +162,7 @@
     bits = [link * (levels - 1) // (NEXP - 1) for link in range(NEXP)]
 
     encoding, parts = chebyshev(struct_feats, op_blocks, laplace_index, series_coef, first_block)
-    held = lax.optimization_barrier((node_feats, [p[0] for p in parts.values()]))[0]
+    held = lax.optimization_barrier((node_feats, list(parts.values())))[0]
     feats_before = shift_rows(held[rows - rim:], "seq", 1)
     feats_after = shift_rows(held[:rim], "seq", -1)
     feats_far = [partner(held, "seq", bit) for bit in bits[1:]]

time: 245 us -> 229 us (0.935); the launches traced: 241 us -> 228 us
  waiting for transfers between devices: 35.2 us -> 57.6 us
  matrix products: 69.8 us -> 49.3 us
  starting transfers between devices: 66 us -> 46.1 us
  local copies, waits for them, and re-layouts: 12.8 us -> 19.4 us
    ppermute x16 -> x8, starting transfers between devices: 51 us -> 17.1 us  [shift_rows(): return lax.ppermute(x, axis, pairs)]
    ppermute x16 -> x8, waiting for transfers between devices: 35.2 us -> 54.1 us  [shift_rows(): return lax.ppermute(x, axis, pairs)]
    dot_general x8, matrix products: 36.9 us -> 20 us  [step(): jnp.einsum('wsk,wkc->wsc', bands[lo:hi], stacked, precision=lax.Precision...]
    ppermute x7, starting transfers between devices: 15.1 us -> 29 us  [partner(): return lax.ppermute(value, axis, pairs)]
    another operation x8 -> x16, local copies, waits for them, and re-layouts: 0.47 us -> 4.55 us  [step(): jnp.stack([values[lo - REACH + o - base:hi - REACH + o - base] for o in r...]
    concatenate x0 -> x2, other arithmetic: none -> 3.98 us  [the longest x1 2.12 us: chebyshev(): jnp.concatenate([struct_feats.reshape(count, BS, chans), bands], axis=2)]
    ppermute x7, waiting for transfers between devices: 0.02 us -> 3.57 us  [partner(): return lax.ppermute(value, axis, pairs)]
    unnamed x55 -> x70, local copies, waits for them, and re-layouts: 4.67 us -> 8 us
  transfers between devices with their start and end apart: 23 -> 15, of which waited for: 3 -> 3; matrix products, arithmetic and copies ran while one was open for 36% -> 28% of each run, Pallas kernels for 0% -> 0%
where the time goes in v4:
time: 229 us; the launch traced here: 228 us
  waiting for transfers between devices  57.6 us (25%)
  matrix products  49.3 us (22%)
  Pallas kernels  48.2 us (21%)
  starting transfers between devices  46.1 us (20%)
  local copies, waits for them, and re-layouts  19.4 us (8%)
  other arithmetic  6.7 us (3%)
    ppermute x8, waiting for transfers between devices, shift_rows(): return lax.ppermute(x, axis, pairs)  54.1 us
    pallas_call x1, Pallas kernels, attend(): pl.pallas_call(attention_kernel, grid_spec=grid_spec, out_shape=jax.Shape...  48.2 us
    ppermute x7, starting transfers between devices, partner(): return lax.ppermute(value, axis, pairs)  29 us
    dot_general x8, matrix products, step(): jnp.einsum('wsk,wkc->wsc', bands[lo:hi], stacked, precision=lax.Precision...  20 us
    dot_general x3, matrix products, on_device(): jnp.dot(blend(f, e), kv_weight, preferred_element_type=jnp.float32)  19.1 us
    ppermute x8, starting transfers between devices, shift_rows(): return lax.ppermute(x, axis, pairs)  17.1 us
    unnamed x70, local copies, waits for them, and re-layouts  8 us
  transfers between devices with their start and end apart: 15, of which 3 were waited for; matrix products, arithmetic and copies ran while one was open for 28% of the time, Pallas kernels for 0%

profile of v4, /device:TPU:0, one launch (start us, length us, event | category | flops | bytes accessed | tf_op | source)
XLA Modules:
  0.0 228.1 jit_solution(1108526727866002589)
XLA Ops:
  0.0 0.9 copy.30
  1.1 1.8 select_reduce_fusion
  2.9 1.5 copy.31
  4.3 1.8 copy.32
  6.1 2.1 pad_maximum_fusion.1
  8.3 3.4 %collective-permute-start.1 = (f32[8,64,448]{2,1,0:T(8,128)}, f32[8,64,448]{2,1,0:T(8,128)}, u32[]{:S(2)}, u32[]{:S(2)}) collective-permute-start(f32[8,64,448]{2,1,0:T(8,128)} %pad_maximum_fusion.1), channel_id=1, source_target_pairs={{0,1},{1,2},{2,3},{3,4},{4,5},{5,6},{6,7},{7,8},{8,9},{9,10},{10,1... | collective-permute-start | bytes 2752520 | tf_op jit(solution)/shard_map/ppermute | solution.py:26
  11.6 4.4 %collective-permute-start = (f32[8,64,448]{2,1,0:T(8,128)}, f32[8,64,448]{2,1,0:T(8,128)}, u32[]{:S(2)}, u32[]{:S(2)}) collective-permute-start(f32[8,64,448]{2,1,0:T(8,128)} %pad_maximum_fusion.1), channel_id=1, source_target_pairs={{0,2},{1,3},{2,4},{3,5},{4,6},{5,7},{6,8},{7,9},{8,10},{9,11},{10,... | collective-permute-start | bytes 2752520 | tf_op jit(solution)/shard_map/ppermute | solution.py:26
  16.0 1.3 collective-permute-start.2
  17.3 1.3 collective-permute-start.3
  18.8 0.7 pad_add_fusion.table_ref
  19.4 0.7 fusion.116
  20.1 52.5 %collective-permute-done = f32[8,64,448]{2,1,0:T(8,128)} collective-permute-done((f32[8,64,448]{2,1,0:T(8,128)}, f32[8,64,448]{2,1,0:T(8,128)}, u32[]{:S(2)}, u32[]{:S(2)}) %collective-permute-start) | collective-permute-done | bytes 917536 | tf_op jit(solution)/shard_map/ppermute | solution.py:26
  72.7 2.5 %collective-permute-start.6 = (bf16[512,1024]{1,0:T(8,128)(2,1)}, bf16[512,1024]{1,0:T(8,128)(2,1)S(1)}, u32[]{:S(2)}, u32[]{:S(2)}) collective-permute-start(bf16[512,1024]{1,0:T(8,128)(2,1)} %param.10), channel_id=1, source_target_pairs={{0,2},{1,3},{2,0},{3,1},{4,6},{5,7},{6,4},{7,5},{8,10},{9,11},{10,... | collective-permute-start | bytes 3145736 | tf_op jit(solution)/shard_map/ppermute | solution.py:39
  75.1 9.6 %collective-permute-start.7 = (bf16[512,1024]{1,0:T(8,128)(2,1)}, bf16[512,1024]{1,0:T(8,128)(2,1)S(1)}, u32[]{:S(2)}, u32[]{:S(2)}) collective-permute-start(bf16[512,1024]{1,0:T(8,128)(2,1)} %param.10), channel_id=1, source_target_pairs={{0,4},{1,5},{2,6},{3,7},{4,0},{5,1},{6,2},{7,3},{8,12},{9,13},{10,... | collective-permute-start | bytes 3145736 | tf_op jit(solution)/shard_map/ppermute | solution.py:39
  84.8 10.6 %collective-permute-start.8 = (bf16[512,1024]{1,0:T(8,128)(2,1)}, bf16[512,1024]{1,0:T(8,128)(2,1)S(1)}, u32[]{:S(2)}, u32[]{:S(2)}) collective-permute-start(bf16[512,1024]{1,0:T(8,128)(2,1)} %param.10), channel_id=1, source_target_pairs={{0,8},{1,9},{2,10},{3,11},{4,12},{5,13},{6,14},{7,15},{8,0},{9,1},... | collective-permute-start | bytes 3145736 | tf_op jit(solution)/shard_map/ppermute | solution.py:39
  95.4 1.3 constant_dynamic-update-slice_fusion.4
  96.7 1.3 constant_dynamic-update-slice_fusion.3
  98.2 1.3 constant_dynamic-update-slice_fusion.1
  99.5 1.3 constant_dynamic-update-slice_fusion
  101.6 1.0 copy.33
  102.6 2.7 %fusion = f32[36,64,128]{2,1,0:T(8,128)S(1)} fusion(f32[36,320,128]{2,1,0:T(8,128)S(1)} %bitcast.203, f32[40,64,448]{2,1,0:T(8,128)S(1)} %constant_dynamic-update-slice_fusion), kind=kOutput, calls=%fused_computation.1 | convolution fusion | flops 566231040 | bytes 10616832 | tf_op jit(solution)/shard_map/wsk,wkc->wsc/dot_general | solution.py:77
  105.9 0.8 copy.34
  106.8 2.5 %fusion.29 = f32[32,64,128]{2,1,0:T(8,128)S(1)} fusion(f32[32,320,128]{2,1,0:T(8,128)S(1)} %bitcast.204, f32[40,64,448]{2,1,0:T(8,128)S(1)} %constant_dynamic-update-slice_fusion), kind=kOutput, calls=%fused_computation.36 | convolution fusion | flops 503840768 | bytes 10485760 | tf_op jit(solution)/shard_map/wsk,wkc->wsc/dot_general | solution.py:77
  109.6 0.7 copy.35
  110.3 2.2 fusion.35
  113.3 1.9 pad_maximum_fusion
  115.2 2.0 fusion.41
  117.9 1.6 fusion.47
  120.0 1.2 fusion.53
  121.6 0.9 fusion.56
  122.8 0.9 copy-done.5
  123.7 1.4 collective-permute-start.4
  125.2 1.3 collective-permute-start.5
  126.5 6.9 %fusion.108 = bf16[8,64,128]{2,1,0:T(8,128)(2,1)S(1)} fusion(f32[20,64,128]{2,1,0:T(8,128)S(1)} %fusion.47, f32[24,64,128]{2,1,0:T(8,128)S(1)} %fusion.41, f32[28,64,128]{2,1,0:T(8,128)S(1)} %fusion.35, f32[32,64,128]{2,1,0:T(8,128)S(1)} %fusion.29, f32[36,64,128]{2,1,0:T(8,128)S(1)} %fusion, f32[8,64,128]{2,1,0:T(8,128)S(1)} %bitcast.217, ...), kind=kOutput, calls=%fused_computation.139 | convolution fusion | flops 127139840 | bytes 4194340 | tf_op jit(solution)/shard_map/wsk,wkc->wsc/dot_general | solution.py:77
  133.5 3.6 %collective-permute-done.8 = bf16[512,1024]{1,0:T(8,128)(2,1)S(1)} collective-permute-done((bf16[512,1024]{1,0:T(8,128)(2,1)}, bf16[512,1024]{1,0:T(8,128)(2,1)S(1)}, u32[]{:S(2)}, u32[]{:S(2)}) %collective-permute-start.8) | collective-permute-done | bytes 1048608 | tf_op jit(solution)/shard_map/ppermute | solution.py:39
  137.0 3.2 %collective-permute-start.14 = (bf16[512,128]{1,0:T(8,128)(2,1)S(1)}, bf16[512,128]{1,0:T(8,128)(2,1)}, u32[]{:S(2)}, u32[]{:S(2)}) collective-permute-start(bf16[512,128]{1,0:T(8,128)(2,1)S(1)} %bitcast.218), channel_id=1, source_target_pairs={{0,8},{1,9},{2,10},{3,11},{4,12},{5,13},{6,14},{7,15},{8,0},{9,1},... | collective-permute-start | bytes 393224 | tf_op jit(solution)/shard_map/ppermute | solution.py:39
  140.7 2.5 %collective-permute-start.9 = (bf16[128,128]{1,0:T(8,128)(2,1)S(1)}, bf16[128,128]{1,0:T(8,128)(2,1)S(1)}, u32[]{:S(2)}, u32[]{:S(2)}) collective-permute-start(bf16[128,128]{1,0:T(8,128)(2,1)S(1)} %get-tuple-element.21), channel_id=1, source_target_pairs={{0,1},{1,2},{2,3},{3,4},{4,5},{5,6},{6,7},{7,8},{8,9},{9,10},{10,1... | collective-permute-start | bytes 98312 | tf_op jit(solution)/shard_map/ppermute | solution.py:26
  143.2 1.5 collective-permute-start.10
  145.4 1.5 collective-permute-done.10
  147.2 3.6 %convolution_convert_fusion.refs_0_.refs_1_.refs_2_.refs_3_ = bf16[768,2048]{1,0:T(8,128)(2,1)S(1)} fusion(bf16[1024,3072]{1,0:T(8,128)(2,1)S(1)} %bitcast.224, bf16[128,1024]{1,0:T(8,128)(2,1)S(1)} %add_convert_fusion.7, bf16[512,1024]{1,0:T(8,128)(2,1)S(1)} %add_convert_fusion.3, bf16[128,1024]{1,0:T(8,128)(2,1)S(1)} %add_convert_fusion.8), kind=kOutput, calls=%fused_computation.3 | convolution fusion | flops 3227516928 | bytes 8912896 | tf_op jit(solution)/shard_map/dot_general | solution.py:190
  150.9 1.6 slice.388
  152.5 2.6 %collective-permute-start.11 = (bf16[512,2048]{1,0:T(8,128)(2,1)}, bf16[512,2048]{1,0:T(8,128)(2,1)}, u32[]{:S(2)}, u32[]{:S(2)}) collective-permute-start(bf16[512,2048]{1,0:T(8,128)(2,1)} %slice.388), channel_id=1, source_target_pairs={{0,1},{1,0},{2,3},{3,2},{4,5},{5,4},{6,7},{7,6},{8,9},{9,8},{10,11... | collective-permute-start | bytes 6291464 | tf_op jit(solution)/shard_map/ppermute | solution.py:39
  155.1 2.2 fusion.23.q_ref
  157.4 6.2 %convolution_convert_fusion.1.refs_7_ = bf16[512,2048]{1,0:T(8,128)(2,1)} fusion(bf16[1024,3072]{1,0:T(8,128)(2,1)} %param.18, bf16[512,1024]{1,0:T(8,128)(2,1)S(1)} %copy-done.13, bf16[512,128]{1,0:T(8,128)(2,1)} %collective-permute-done.14, bf16[128,1024]{1,0:T(8,128)(2,1)S(1)} %copy-done.4), kind=kOutput, calls=%fused_computation.7 | convolution fusion | flops 2284322816 | bytes 7733248 | tf_op jit(solution)/shard_map/dot_general | solution.py:195
  163.6 6.6 %convolution_convert_fusion.2.refs_6_ = bf16[512,2048]{1,0:T(8,128)(2,1)} fusion(bf16[1024,3072]{1,0:T(8,128)(2,1)} %param.18, bf16[512,1024]{1,0:T(8,128)(2,1)} %copy-done.11, bf16[512,128]{1,0:T(8,128)(2,1)} %collective-permute-done.13, bf16[128,1024]{1,0:T(8,128)(2,1)S(1)} %copy-done.4), kind=kOutput, calls=%fused_computation.8 | convolution fusion | flops 2284322816 | bytes 7733248 | tf_op jit(solution)/shard_map/dot_general | solution.py:195
  170.2 6.3 %convolution_convert_fusion.3.refs_5_ = bf16[512,2048]{1,0:T(8,128)(2,1)} fusion(bf16[1024,3072]{1,0:T(8,128)(2,1)} %param.18, bf16[512,1024]{1,0:T(8,128)(2,1)S(1)} %copy-done.10, bf16[512,128]{1,0:T(8,128)(2,1)} %collective-permute-done.12, bf16[128,1024]{1,0:T(8,128)(2,1)S(1)} %copy-done.4), kind=kOutput, calls=%fused_computation.9 | convolution fusion | flops 2284322816 | bytes 7733248 | tf_op jit(solution)/shard_map/dot_general | solution.py:195
  176.4 48.2 %shard_map.100 = bf16[512,1024]{1,0:T(8,128)(2,1)} custom-call(s32[8,8]{1,0:T(8,128)} %pad_add_fusion.table_ref, bf16[512,1024]{1,0:T(8,128)(2,1)} %fusion.23.q_ref, bf16[768,2048]{1,0:T(8,128)(2,1)} %copy-done.1, bf16[768,2048]{1,0:T(8,128)(2,1)} %copy-done.1, bf16[768,2048]{1,0:T(8,128)(2,1)} %copy-done.1, bf16[768,2048]{1,0:T(8,128)(2,1)} %copy-done.1, ...), custom_call_target="tpu_custom_call" | custom-call | tf_op jit(solution)/shard_map/pallas_call | solution.py:138
  224.7 3.4 %convolution_convert_fusion.4 = bf16[512,1024]{1,0:T(8,128)(2,1)} fusion(bf16[512,1024]{1,0:T(8,128)(2,1)} %shard_map.100, bf16[1024,1024]{1,0:T(8,128)(2,1)S(1)} %copy-done), kind=kOutput, calls=%fused_computation.34 | convolution fusion | flops 1074266112 | bytes 4194304 | tf_op jit(solution)/shard_map/dot_general | solution.py:206
  (105 shorter events, 5.9 us)
Async XLA Ops:
  0.0 224.7 %copy-start = (bf16[1024,1024]{1,0:T(8,128)(2,1)S(1)}, bf16[1024,1024]{1,0:T(8,128)(2,1)}, u32[]{:S(2)}) copy-start(bf16[1024,1024]{1,0:T(8,128)(2,1)} %param.19) | copy-start | bytes 6291460
  2.8 15.8 %copy-start.7 = (s32[8,3]{0,1:T(4,128)S(1)}, s32[8,3]{0,1:T(4,128)}, u32[]{:S(2)}) copy-start(s32[8,3]{0,1:T(4,128)} %param.14) | copy-start | bytes 292
  2.8 15.8 %copy-start.8 = (s32[8,4]{0,1:T(4,128)S(1)}, s32[8,4]{0,1:T(4,128)}, u32[]{:S(2)}) copy-start(s32[8,4]{0,1:T(4,128)} %param.15) | copy-start | bytes 388
  2.9 16.6 %copy-start.6 = (f32[9]{0:T(128)S(1)}, f32[9]{0:T(128)}, u32[]{:S(2)}) copy-start(f32[9]{0:T(128)} %param.16) | copy-start | bytes 112
  6.1 91.9 %copy-start.3 = (f32[512,128]{1,0:T(8,128)S(1)}, f32[512,128]{1,0:T(8,128)}, u32[]{:S(2)}) copy-start(f32[512,128]{1,0:T(8,128)} %param.11) | copy-start | bytes 786436
  8.3 11.9 %collective-permute-start.1 = (f32[8,64,448]{2,1,0:T(8,128)}, f32[8,64,448]{2,1,0:T(8,128)}, u32[]{:S(2)}, u32[]{:S(2)}) collective-permute-start(f32[8,64,448]{2,1,0:T(8,128)} %pad_maximum_fusion.1), channel_id=1, source_target_pairs={{0,1},{1,2},{2,3},{3,4},{4,5},{5,6},{6,7},{7,8},{8,9},{9,10},{10,1... | collective-permute-start | bytes 2752520 | tf_op jit(solution)/shard_map/ppermute | solution.py:26
  11.6 61.0 %collective-permute-start = (f32[8,64,448]{2,1,0:T(8,128)}, f32[8,64,448]{2,1,0:T(8,128)}, u32[]{:S(2)}, u32[]{:S(2)}) collective-permute-start(f32[8,64,448]{2,1,0:T(8,128)} %pad_maximum_fusion.1), channel_id=1, source_target_pairs={{0,2},{1,3},{2,4},{3,5},{4,6},{5,7},{6,8},{7,9},{8,10},{9,11},{10,... | collective-permute-start | bytes 2752520 | tf_op jit(solution)/shard_map/ppermute | solution.py:26
  16.0 56.7 %collective-permute-start.2 = (f32[8,64,448]{2,1,0:T(8,128)}, f32[8,64,448]{2,1,0:T(8,128)}, u32[]{:S(2)}, u32[]{:S(2)}) collective-permute-start(f32[8,64,448]{2,1,0:T(8,128)} %pad_maximum_fusion.1), channel_id=1, source_target_pairs={{1,0},{2,1},{3,2},{4,3},{5,4},{6,5},{7,6},{8,7},{9,8},{10,9},{11,1... | collective-permute-start | bytes 2752520 | tf_op jit(solution)/shard_map/ppermute | solution.py:26
  17.3 55.4 %collective-permute-start.3 = (f32[8,64,448]{2,1,0:T(8,128)}, f32[8,64,448]{2,1,0:T(8,128)}, u32[]{:S(2)}, u32[]{:S(2)}) collective-permute-start(f32[8,64,448]{2,1,0:T(8,128)} %pad_maximum_fusion.1), channel_id=1, source_target_pairs={{2,0},{3,1},{4,2},{5,3},{6,4},{7,5},{8,6},{9,7},{10,8},{11,9},{12,... | collective-permute-start | bytes 2752520 | tf_op jit(solution)/shard_map/ppermute | solution.py:26
  72.7 60.8 %collective-permute-start.6 = (bf16[512,1024]{1,0:T(8,128)(2,1)}, bf16[512,1024]{1,0:T(8,128)(2,1)S(1)}, u32[]{:S(2)}, u32[]{:S(2)}) collective-permute-start(bf16[512,1024]{1,0:T(8,128)(2,1)} %param.10), channel_id=1, source_target_pairs={{0,2},{1,3},{2,0},{3,1},{4,6},{5,7},{6,4},{7,5},{8,10},{9,11},{10,... | collective-permute-start | bytes 3145736 | tf_op jit(solution)/shard_map/ppermute | solution.py:39
  75.1 58.3 %collective-permute-start.7 = (bf16[512,1024]{1,0:T(8,128)(2,1)}, bf16[512,1024]{1,0:T(8,128)(2,1)S(1)}, u32[]{:S(2)}, u32[]{:S(2)}) collective-permute-start(bf16[512,1024]{1,0:T(8,128)(2,1)} %param.10), channel_id=1, source_target_pairs={{0,4},{1,5},{2,6},{3,7},{4,0},{5,1},{6,2},{7,3},{8,12},{9,13},{10,... | collective-permute-start | bytes 3145736 | tf_op jit(solution)/shard_map/ppermute | solution.py:39
  84.8 52.3 %collective-permute-start.8 = (bf16[512,1024]{1,0:T(8,128)(2,1)}, bf16[512,1024]{1,0:T(8,128)(2,1)S(1)}, u32[]{:S(2)}, u32[]{:S(2)}) collective-permute-start(bf16[512,1024]{1,0:T(8,128)(2,1)} %param.10), channel_id=1, source_target_pairs={{0,8},{1,9},{2,10},{3,11},{4,12},{5,13},{6,14},{7,15},{8,0},{9,1},... | collective-permute-start | bytes 3145736 | tf_op jit(solution)/shard_map/ppermute | solution.py:39
  122.5 1.2 copy-start.5
  122.5 4.0 %copy-start.2 = (f32[8,64,5,64]{1,3,2,0:T(8,128)S(1)}, f32[8,64,5,64]{1,3,2,0:T(8,128)}, u32[]{:S(2)}) copy-start(f32[8,64,5,64]{1,3,2,0:T(8,128)} %copy.31) | copy-start | bytes 1966084
  122.6 24.5 %slice-start = ((s8[6291456]{0:T(1024)(128)(4,1)}), s8[4194304]{0:T(1024)(128)(4,1)S(1)}, s32[]{:S(2)}) async-start(s8[6291456]{0:T(1024)(128)(4,1)} %bitcast.223), calls=%async_computation | async-start | bytes 8388608
  123.7 21.0 %copy-start.4 = (bf16[128,1024]{1,0:T(8,128)(2,1)S(1)}, bf16[128,1024]{1,0:T(8,128)(2,1)}, u32[]{:S(2)}) copy-start(bf16[128,1024]{1,0:T(8,128)(2,1)} %param.17) | copy-start | bytes 786436
  123.7 9.7 %collective-permute-start.4 = (bf16[128,1024]{1,0:T(8,128)(2,1)S(1)}, bf16[128,1024]{1,0:T(8,128)(2,1)S(1)}, u32[]{:S(2)}, u32[]{:S(2)}) collective-permute-start(bf16[128,1024]{1,0:T(8,128)(2,1)S(1)} %get-tuple-element.20), channel_id=1, source_target_pairs={{0,1},{1,2},{2,3},{3,4},{4,5},{5,6},{6,7},{7,8},{8,9},{9,10},{10,1... | collective-permute-start | bytes 786440 | tf_op jit(solution)/shard_map/ppermute | solution.py:26
  125.2 8.3 %collective-permute-start.5 = (bf16[128,1024]{1,0:T(8,128)(2,1)S(1)}, bf16[128,1024]{1,0:T(8,128)(2,1)S(1)}, u32[]{:S(2)}, u32[]{:S(2)}) collective-permute-start(bf16[128,1024]{1,0:T(8,128)(2,1)S(1)} %get-tuple-element.19), channel_id=1, source_target_pairs={{1,0},{2,1},{3,2},{4,3},{5,4},{6,5},{7,6},{8,7},{9,8},{10,9},{11,1... | collective-permute-start | bytes 786440 | tf_op jit(solution)/shard_map/ppermute | solution.py:26
  126.5 20.7 %slice-start.1 = ((s8[6291456]{0:T(1024)(128)(4,1)}), s8[2097152]{0:T(1024)(128)(4,1)S(1)}, s32[]{:S(2)}) async-start(s8[6291456]{0:T(1024)(128)(4,1)} %bitcast.223), calls=%async_computation.1 | async-start | bytes 4194304
  133.5 17.4 %copy-start.9 = (bf16[512,1024]{1,0:T(8,128)(2,1)}, bf16[512,1024]{1,0:T(8,128)(2,1)S(1)}, u32[]{:S(2)}) copy-start(bf16[512,1024]{1,0:T(8,128)(2,1)S(1)} %collective-permute-done.6) | copy-start | bytes 3145732
  133.5 17.4 %copy-start.11 = (bf16[512,1024]{1,0:T(8,128)(2,1)}, bf16[512,1024]{1,0:T(8,128)(2,1)S(1)}, u32[]{:S(2)}) copy-start(bf16[512,1024]{1,0:T(8,128)(2,1)S(1)} %collective-permute-done.7) | copy-start | bytes 3145732
  137.0 13.8 %copy-start.12 = (bf16[512,1024]{1,0:T(8,128)(2,1)}, bf16[512,1024]{1,0:T(8,128)(2,1)S(1)}, u32[]{:S(2)}) copy-start(bf16[512,1024]{1,0:T(8,128)(2,1)S(1)} %collective-permute-done.8) | copy-start | bytes 3145732
  137.0 20.3 %collective-permute-start.14 = (bf16[512,128]{1,0:T(8,128)(2,1)S(1)}, bf16[512,128]{1,0:T(8,128)(2,1)}, u32[]{:S(2)}, u32[]{:S(2)}) collective-permute-start(bf16[512,128]{1,0:T(8,128)(2,1)S(1)} %bitcast.218), channel_id=1, source_target_pairs={{0,8},{1,9},{2,10},{3,11},{4,12},{5,13},{6,14},{7,15},{8,0},{9,1},... | collective-permute-start | bytes 393224 | tf_op jit(solution)/shard_map/ppermute | solution.py:39
  140.3 23.3 %collective-permute-start.13 = (bf16[512,128]{1,0:T(8,128)(2,1)S(1)}, bf16[512,128]{1,0:T(8,128)(2,1)}, u32[]{:S(2)}, u32[]{:S(2)}) collective-permute-start(bf16[512,128]{1,0:T(8,128)(2,1)S(1)} %bitcast.219), channel_id=1, source_target_pairs={{0,4},{1,5},{2,6},{3,7},{4,0},{5,1},{6,2},{7,3},{8,12},{9,13},{10,... | collective-permute-start | bytes 393224 | tf_op jit(solution)/shard_map/ppermute | solution.py:39
  140.3 29.9 %collective-permute-start.12 = (bf16[512,128]{1,0:T(8,128)(2,1)S(1)}, bf16[512,128]{1,0:T(8,128)(2,1)}, u32[]{:S(2)}, u32[]{:S(2)}) collective-permute-start(bf16[512,128]{1,0:T(8,128)(2,1)S(1)} %bitcast.220), channel_id=1, source_target_pairs={{0,2},{1,3},{2,0},{3,1},{4,6},{5,7},{6,4},{7,5},{8,10},{9,11},{10,... | collective-permute-start | bytes 393224 | tf_op jit(solution)/shard_map/ppermute | solution.py:39
  140.7 4.5 %collective-permute-start.9 = (bf16[128,128]{1,0:T(8,128)(2,1)S(1)}, bf16[128,128]{1,0:T(8,128)(2,1)S(1)}, u32[]{:S(2)}, u32[]{:S(2)}) collective-permute-start(bf16[128,128]{1,0:T(8,128)(2,1)S(1)} %get-tuple-element.21), channel_id=1, source_target_pairs={{0,1},{1,2},{2,3},{3,4},{4,5},{5,6},{6,7},{7,8},{8,9},{9,10},{10,1... | collective-permute-start | bytes 98312 | tf_op jit(solution)/shard_map/ppermute | solution.py:26
  143.2 3.7 %collective-permute-start.10 = (bf16[128,128]{1,0:T(8,128)(2,1)S(1)}, bf16[128,128]{1,0:T(8,128)(2,1)S(1)}, u32[]{:S(2)}, u32[]{:S(2)}) collective-permute-start(bf16[128,128]{1,0:T(8,128)(2,1)S(1)} %get-tuple-element.22), channel_id=1, source_target_pairs={{1,0},{2,1},{3,2},{4,3},{5,4},{6,5},{7,6},{8,7},{9,8},{10,9},{11,1... | collective-permute-start | bytes 98312 | tf_op jit(solution)/shard_map/ppermute | solution.py:26
  150.8 6.5 %copy-start.1 = (bf16[768,2048]{1,0:T(8,128)(2,1)}, bf16[768,2048]{1,0:T(8,128)(2,1)S(1)}, u32[]{:S(2)}) copy-start(bf16[768,2048]{1,0:T(8,128)(2,1)S(1)} %convolution_convert_fusion.refs_0_.refs_1_.refs_2_.refs_3_) | copy-start | bytes 9437188
  152.5 4.9 %copy-start.13 = (bf16[512,1024]{1,0:T(8,128)(2,1)S(1)}, bf16[512,1024]{1,0:T(8,128)(2,1)}, u32[]{:S(2)}) copy-start(bf16[512,1024]{1,0:T(8,128)(2,1)} %copy-done.12) | copy-start | bytes 3145732
  152.5 24.0 %collective-permute-start.11 = (bf16[512,2048]{1,0:T(8,128)(2,1)}, bf16[512,2048]{1,0:T(8,128)(2,1)}, u32[]{:S(2)}, u32[]{:S(2)}) collective-permute-start(bf16[512,2048]{1,0:T(8,128)(2,1)} %slice.388), channel_id=1, source_target_pairs={{0,1},{1,0},{2,3},{3,2},{4,5},{5,4},{6,7},{7,6},{8,9},{9,8},{10,11... | collective-permute-start | bytes 6291464 | tf_op jit(solution)/shard_map/ppermute | solution.py:39
  163.6 6.6 %copy-start.10 = (bf16[512,1024]{1,0:T(8,128)(2,1)S(1)}, bf16[512,1024]{1,0:T(8,128)(2,1)}, u32[]{:S(2)}) copy-start(bf16[512,1024]{1,0:T(8,128)(2,1)} %copy-done.9) | copy-start | bytes 3145732

commit v5 on v4

--- a/solution.py
+++ b/solution.py
@@ -15,6 +15,7 @@
 NEXP = 4
 REACH = 2
 NKEY = 1 + 3 + NEXP
+PER_EXCHANGE = 4
 
 
 def shift_rows(x, axis, step):
@@ -53,45 +54,66 @@
     count = op_blocks.shape[0]
     chans = struct_feats.shape[1]
     taps = 2 * REACH + 1
-    reach_dev = -(-DEG * REACH // count)
+    halo = PER_EXCHANGE * REACH
     block_ids = first_block + jnp.arange(count, dtype=jnp.int32)
     offsets = laplace_index - block_ids[:, None] + REACH
     hit = offsets[:, :, None] == jnp.arange(taps, dtype=jnp.int32)[None, None, :]
     bands = jnp.sum(jnp.where(hit[:, :, :, None, None], op_blocks[:, :, None], 0.0), axis=1)
     bands = bands.transpose(0, 2, 1, 3).reshape(count, BS, taps * BS)
-    payload = jnp.concatenate([struct_feats.reshape(count, BS, chans), bands], axis=2)
-    parts = {0: payload}
-    for off in range(1, reach_dev + 1):
-        parts[-off] = shift_rows(payload, "seq", off)
-        parts[off] = shift_rows(payload, "seq", -off)
-    window = jnp.concatenate([parts[o] for o in range(-reach_dev, reach_dev + 1)], axis=0)
-    field = window[:, :, :chans]
-    bands = window[:, :, chans:]
-    width = window.shape[0]
-    centre = reach_dev * count
+    own_field = struct_feats.reshape(count, BS, chans)
+    payload = jnp.concatenate([own_field, bands], axis=2)
+    left = shift_rows(payload, "seq", 1)
+    right = shift_rows(payload, "seq", -1)
+    edge = halo - REACH
+    bands = jnp.concatenate(
+        [left[count - edge :, :, chans:], bands, right[:edge, :, chans:]], axis=0
+    )
+    field = jnp.concatenate(
+        [left[count - halo :, :, :chans], own_field, right[:halo, :, :chans]], axis=0
+    )
+    width = field.shape[0]
 
     def step(values, lo, hi, base):
         stacked = jnp.stack(
             [values[lo - REACH + o - base : hi - REACH + o - base] for o in range(taps)], axis=1
         ).reshape(hi - lo, taps * BS, chans)
         return jnp.einsum(
-            "wsk,wkc->wsc", bands[lo:hi], stacked, precision=lax.Precision.HIGH,
-            preferred_element_type=jnp.float32,
+            "wsk,wkc->wsc", bands[lo - REACH : hi - REACH], stacked,
+            precision=lax.Precision.HIGH, preferred_element_type=jnp.float32,
         )
 
-    own = slice(centre, centre + count)
-    prev, prev_base = field, 0
-    lo, hi = REACH, width - REACH
-    cur = step(field, lo, hi, 0)
-    cur_base = lo
-    encoding = series_coef[0] * field[own] + series_coef[1] * cur[centre - cur_base : centre - cur_base + count]
-    for degree in range(2, DEG + 1):
-        lo, hi = lo + REACH, hi - REACH
-        nxt = 2.0 * step(cur, lo, hi, cur_base) - prev[lo - prev_base : hi - prev_base]
-        encoding = encoding + series_coef[degree] * nxt[centre - lo : centre - lo + count]
+    own = slice(halo, halo + count)
+    cur, cur_base = field, 0
+    prev, prev_base = None, 0
+    encoding = series_coef[0] * field[own]
+    for degree in range(1, DEG + 1):
+        if degree > 1 and (degree - 1) % PER_EXCHANGE == 0:
+            packed = jnp.concatenate([prev[own.start - prev_base : own.stop - prev_base], cur], axis=2)
+            left = shift_rows(packed, "seq", 1)
+            right = shift_rows(packed, "seq", -1)
+            older = prev[own.start - prev_base : own.stop - prev_base]
+            prev = jnp.concatenate(
+                [left[count - edge :, :, :chans], older, right[:edge, :, :chans]], axis=0
+            )
+            prev_base = REACH
+            cur = jnp.concatenate(
+                [left[count - halo :, :, chans:], cur, right[:halo, :, chans:]], axis=0
+            )
+            cur_base = 0
+            lo, hi = 0, width
+        if degree == 1 or (degree - 1) % PER_EXCHANGE == 0:
+            lo, hi = REACH, width - REACH
+        else:
+            lo, hi = lo + REACH, hi - REACH
+        applied = step(cur, lo, hi, cur_base)
+        if degree == 1:
+            nxt = applied
+        else:
+            nxt = 2.0 * applied - prev[lo - prev_base : hi - prev_base]
+        encoding = encoding + series_coef[degree] * nxt[own.start - lo : own.stop - lo]
         prev, prev_base = cur, cur_base
         cur, cur_base = nxt, lo
-    return encoding.reshape(count * BS, chans), parts
+    return encoding.reshape(count * BS, chans), {0: payload, 1: left, -1: right}
 
 
 def attention_kernel(table_ref, q_ref, *refs):

time: 229 us -> 210 us (0.917)
  waiting for transfers between devices: 57.6 us -> 31.3 us
  starting transfers between devices: 46.1 us -> 63.4 us
  local copies, waits for them, and re-layouts: 19.4 us -> 14.4 us
  matrix products: 49.3 us -> 44.5 us
    ppermute x8, waiting for transfers between devices: 54.1 us -> 0.9 us  [shift_rows(): return lax.ppermute(x, axis, pairs)]
    ppermute x7, waiting for transfers between devices: 3.57 us -> 30.4 us  [partner(): return lax.ppermute(value, axis, pairs)]
    ppermute x8, starting transfers between devices: 17.1 us -> 40.2 us  [shift_rows(): return lax.ppermute(x, axis, pairs)]
    ppermute x7, starting transfers between devices: 29 us -> 23.2 us  [partner(): return lax.ppermute(value, axis, pairs)]
    unnamed x70 -> x69, local copies, waits for them, and re-layouts: 8 us -> 2.88 us
    dot_general x8, matrix products: 20 us -> 15.3 us  [step(): jnp.einsum('wsk,wkc->wsc', bands[lo - REACH:hi - REACH], stacked, precisi...]
    slice x1 -> x10, local copies, waits for them, and re-layouts: 0.69 us -> 4.97 us  [the longest x1 1.18 us: chebyshev(): right[:edge, :, chans:]]
    another operation x16, local copies, waits for them, and re-layouts: 4.55 us -> 1.82 us  [step(): jnp.stack([values[lo - REACH + o - base:hi - REACH + o - base] for o in r...]
  transfers between devices with their start and end apart: 15 -> 15, of which waited for: 3 -> 5; matrix products, arithmetic and copies ran while one was open for 28% -> 20% of each run, Pallas kernels for 0% -> 0%
where the time goes in v5:
time: 210 us
  starting transfers between devices  63.4 us (30%)
  Pallas kernels  48.4 us (23%)
  matrix products  44.5 us (21%)
  waiting for transfers between devices  31.3 us (15%)
  local copies, waits for them, and re-layouts  14.4 us (7%)
  other arithmetic  7.07 us (3%)
    pallas_call x1, Pallas kernels, attend(): pl.pallas_call(attention_kernel, grid_spec=grid_spec, out_shape=jax.Shape...  48.4 us
    ppermute x8, starting transfers between devices, shift_rows(): return lax.ppermute(x, axis, pairs)  40.2 us
    ppermute x7, waiting for transfers between devices, partner(): return lax.ppermute(value, axis, pairs)  30.4 us
    ppermute x7, starting transfers between devices, partner(): return lax.ppermute(value, axis, pairs)  23.2 us
    dot_general x3, matrix products, on_device(): jnp.dot(blend(f, e), kv_weight, preferred_element_type=jnp.float32)  19.1 us
    dot_general x8, matrix products, step(): jnp.einsum('wsk,wkc->wsc', bands[lo - REACH:hi - REACH], stacked, precisi...  15.3 us
  transfers between devices with their start and end apart: 15, of which 5 were waited for; matrix products, arithmetic and copies ran while one was open for 20% of the time, Pallas kernels for 0%

profile of v5, /device:TPU:0, one launch (start us, length us, event | category | flops | bytes accessed | tf_op | source)
XLA Modules:
  0.0 209.9 jit_solution(15146432117797222884)
XLA Ops:
  0.0 0.9 copy.32
  1.1 2.8 %select_reduce_fusion = f32[8,5,64,64]{3,2,1,0:T(8,128)} fusion(f32[8,3,64,64]{3,2,1,0:T(8,128)} %param.12, pred[8,3,5]{2,1,0:T(4,128)(4,1)S(1)} %iota_compare_fusion), kind=kLoop, calls=%fused_computation | loop fusion | flops 819200 | bytes 1048696 | tf_op jit(solution)/shard_map/reduce_sum | solution.py:61
  3.9 1.7 copy.33
  5.7 1.3 copy.34
  7.0 2.3 %pad_maximum_fusion.1 = f32[8,64,448]{2,1,0:T(8,128)} fusion(f32[8,64,320]{2,1,0:T(8,128)} %copy.34, f32[8,64,128]{2,1,0:T(8,128)} %bitcast.212), kind=kLoop, calls=%fused_computation.42 | loop fusion | flops 229376 | bytes 1835008 | tf_op jit(solution)/shard_map/concatenate | solution.py:64
  9.3 1.3 collective-permute-start.1
  10.6 4.0 %collective-permute-start = (f32[8,64,448]{2,1,0:T(8,128)}, f32[8,64,448]{2,1,0:T(8,128)}, u32[]{:S(2)}, u32[]{:S(2)}) collective-permute-start(f32[8,64,448]{2,1,0:T(8,128)} %pad_maximum_fusion.1), channel_id=1, source_target_pairs={{0,1},{1,2},{2,3},{3,4},{4,5},{5,6},{6,7},{7,8},{8,9},{9,10},{10,1... | collective-permute-start | bytes 2752520 | tf_op jit(solution)/shard_map/ppermute | solution.py:27
  14.7 1.0 slice.307
  15.7 0.5 collective-permute-done
  16.2 1.0 slice.306
  17.2 1.0 pad_maximum_fusion.2
  18.4 0.4 copy.36
  18.9 1.2 slice.305
  20.1 1.1 slice.304
  21.2 1.3 fusion.75
  23.0 1.2 fusion.21
  24.5 1.0 fusion.15
  25.8 1.2 fusion.18
  27.1 1.3 collective-permute-start.3
  28.4 25.0 %collective-permute-start.2 = (f32[8,64,256]{2,1,0:T(8,128)S(1)}, f32[8,64,256]{2,1,0:T(8,128)S(1)}, u32[]{:S(2)}, u32[]{:S(2)}) collective-permute-start(f32[8,64,256]{2,1,0:T(8,128)S(1)} %pad_maximum_fusion.4), channel_id=1, source_target_pairs={{0,1},{1,2},{2,3},{3,4},{4,5},{5,6},{6,7},{7,8},{8,9},{9,10},{10,1... | collective-permute-start | bytes 1572872 | tf_op jit(solution)/shard_map/ppermute | solution.py:27
  53.4 0.7 pad_add_fusion.table_ref
  54.1 0.7 fusion.78
  54.7 9.3 %collective-permute-start.6 = (bf16[512,1024]{1,0:T(8,128)(2,1)S(1)}, bf16[512,1024]{1,0:T(8,128)(2,1)S(1)}, u32[]{:S(2)}, u32[]{:S(2)}) collective-permute-start(bf16[512,1024]{1,0:T(8,128)(2,1)S(1)} %copy-done.5), channel_id=1, source_target_pairs={{0,2},{1,3},{2,0},{3,1},{4,6},{5,7},{6,4},{7,5},{8,10},{9,11},{10,... | collective-permute-start | bytes 3145736 | tf_op jit(solution)/shard_map/ppermute | solution.py:40
  64.1 3.5 %collective-permute-start.7 = (bf16[512,1024]{1,0:T(8,128)(2,1)S(1)}, bf16[512,1024]{1,0:T(8,128)(2,1)S(1)}, u32[]{:S(2)}, u32[]{:S(2)}) collective-permute-start(bf16[512,1024]{1,0:T(8,128)(2,1)S(1)} %copy-done.5), channel_id=1, source_target_pairs={{0,4},{1,5},{2,6},{3,7},{4,0},{5,1},{6,2},{7,3},{8,12},{9,13},{10,... | collective-permute-start | bytes 3145736 | tf_op jit(solution)/shard_map/ppermute | solution.py:40
  67.5 2.6 %collective-permute-start.8 = (bf16[512,1024]{1,0:T(8,128)(2,1)S(1)}, bf16[512,1024]{1,0:T(8,128)(2,1)S(1)}, u32[]{:S(2)}, u32[]{:S(2)}) collective-permute-start(bf16[512,1024]{1,0:T(8,128)(2,1)S(1)} %copy-done.5), channel_id=1, source_target_pairs={{0,8},{1,9},{2,10},{3,11},{4,12},{5,13},{6,14},{7,15},{8,0},{9,1},... | collective-permute-start | bytes 3145736 | tf_op jit(solution)/shard_map/ppermute | solution.py:40
  70.8 1.3 fusion.14
  72.6 1.2 fusion.22
  74.2 1.0 fusion.16
  75.5 2.0 collective-permute-start.4
  77.5 1.3 collective-permute-start.5
  78.8 7.0 %fusion.20 = bf16[8,64,128]{2,1,0:T(8,128)(2,1)S(1)} fusion(f32[8,64,320]{1,2,0:T(8,128)S(1)} %bitcast.204, f32[8,320,128]{2,1,0:T(8,128)S(1)} %bitcast.209, f32[20,64,128]{2,1,0:T(8,128)S(1)} %fusion.14, f32[20,64,128]{2,1,0:T(8,128)S(1)} %fusion.75, f32[16,64,128]{2,1,0:T(8,128)S(1)} %fusion.22, f32[8,64,128]{2,1,0:T(8,128)S(1)} %fusion.18, ...), kind=kOutput, calls=%fused_computation.36 | convolution fusion | flops 127139840 | bytes 4194340 | tf_op jit(solution)/shard_map/wsk,wkc->wsc/dot_general | solution.py:80
  85.8 1.8 collective-permute-done.6
  87.6 26.0 %collective-permute-done.7 = bf16[512,1024]{1,0:T(8,128)(2,1)S(1)} collective-permute-done((bf16[512,1024]{1,0:T(8,128)(2,1)S(1)}, bf16[512,1024]{1,0:T(8,128)(2,1)S(1)}, u32[]{:S(2)}, u32[]{:S(2)}) %collective-permute-start.7) | collective-permute-done | bytes 1048608 | tf_op jit(solution)/shard_map/ppermute | solution.py:40
  113.6 2.6 %collective-permute-done.8 = bf16[512,1024]{1,0:T(8,128)(2,1)S(1)} collective-permute-done((bf16[512,1024]{1,0:T(8,128)(2,1)S(1)}, bf16[512,1024]{1,0:T(8,128)(2,1)S(1)}, u32[]{:S(2)}, u32[]{:S(2)}) %collective-permute-start.8) | collective-permute-done | bytes 1048608 | tf_op jit(solution)/shard_map/ppermute | solution.py:40
  116.3 1.3 collective-permute-start.10
  118.0 4.1 %collective-permute-start.9 = (bf16[128,128]{1,0:T(8,128)(2,1)S(1)}, bf16[128,128]{1,0:T(8,128)(2,1)S(1)}, u32[]{:S(2)}, u32[]{:S(2)}) collective-permute-start(bf16[128,128]{1,0:T(8,128)(2,1)S(1)} %get-tuple-element.21), channel_id=1, source_target_pairs={{0,1},{1,2},{2,3},{3,4},{4,5},{5,6},{6,7},{7,8},{8,9},{9,10},{10,1... | collective-permute-start | bytes 98312 | tf_op jit(solution)/shard_map/ppermute | solution.py:27
  123.0 3.6 %convolution_convert_fusion.refs_0_.refs_1_.refs_2_.refs_3_ = bf16[768,2048]{1,0:T(8,128)(2,1)S(1)} fusion(bf16[1024,3072]{1,0:T(8,128)(2,1)S(1)} %bitcast.223, bf16[128,1024]{1,0:T(8,128)(2,1)S(1)} %add_convert_fusion.7, bf16[512,1024]{1,0:T(8,128)(2,1)S(1)} %add_convert_fusion.3, bf16[128,1024]{1,0:T(8,128)(2,1)S(1)} %add_convert_fusion.8), kind=kOutput, calls=%fused_computation.1 | convolution fusion | flops 3227516928 | bytes 8912896 | tf_op jit(solution)/shard_map/dot_general | solution.py:212
  126.7 1.6 slice.362
  128.3 0.6 copy-done.1
  128.9 1.9 collective-permute-start.11
  130.8 2.2 %fusion.11.q_ref = bf16[512,1024]{1,0:T(8,128)(2,1)} fusion(bf16[512,1024]{1,0:T(8,128)(2,1)S(1)} %add_convert_fusion.3, bf16[1024,3072]{1,0:T(8,128)(2,1)S(1)} %bitcast.223), kind=kOutput, calls=%fused_computation.21 | convolution fusion | flops 1074266112 | bytes 4194304 | tf_op jit(solution)/shard_map/dot_general | solution.py:206
  133.0 3.0 %collective-permute-start.13 = (bf16[512,128]{1,0:T(8,128)(2,1)S(1)}, bf16[512,128]{1,0:T(8,128)(2,1)}, u32[]{:S(2)}, u32[]{:S(2)}) collective-permute-start(bf16[512,128]{1,0:T(8,128)(2,1)S(1)} %bitcast.220), channel_id=1, source_target_pairs={{0,4},{1,5},{2,6},{3,7},{4,0},{5,1},{6,2},{7,3},{8,12},{9,13},{10,... | collective-permute-start | bytes 393224 | tf_op jit(solution)/shard_map/ppermute | solution.py:40
  136.0 2.9 %collective-permute-start.14 = (bf16[512,128]{1,0:T(8,128)(2,1)S(1)}, bf16[512,128]{1,0:T(8,128)(2,1)}, u32[]{:S(2)}, u32[]{:S(2)}) collective-permute-start(bf16[512,128]{1,0:T(8,128)(2,1)S(1)} %bitcast.221), channel_id=1, source_target_pairs={{0,8},{1,9},{2,10},{3,11},{4,12},{5,13},{6,14},{7,15},{8,0},{9,1},... | collective-permute-start | bytes 393224 | tf_op jit(solution)/shard_map/ppermute | solution.py:40
  138.9 6.3 %convolution_convert_fusion.3.refs_5_ = bf16[512,2048]{1,0:T(8,128)(2,1)} fusion(bf16[1024,3072]{1,0:T(8,128)(2,1)} %param.18, bf16[512,1024]{1,0:T(8,128)(2,1)S(1)} %copy-done.14, bf16[512,128]{1,0:T(8,128)(2,1)} %collective-permute-done.12, bf16[128,1024]{1,0:T(8,128)(2,1)S(1)} %copy-done.4), kind=kOutput, calls=%fused_computation.4 | convolution fusion | flops 2284322816 | bytes 7733248 | tf_op jit(solution)/shard_map/dot_general | solution.py:217
  145.2 6.5 %convolution_convert_fusion.2.refs_6_ = bf16[512,2048]{1,0:T(8,128)(2,1)} fusion(bf16[1024,3072]{1,0:T(8,128)(2,1)} %param.18, bf16[512,1024]{1,0:T(8,128)(2,1)} %copy-done.12, bf16[512,128]{1,0:T(8,128)(2,1)} %collective-permute-done.13, bf16[128,1024]{1,0:T(8,128)(2,1)S(1)} %copy-done.4), kind=kOutput, calls=%fused_computation.3 | convolution fusion | flops 2284322816 | bytes 7733248 | tf_op jit(solution)/shard_map/dot_general | solution.py:217
  151.7 6.3 %convolution_convert_fusion.1.refs_7_ = bf16[512,2048]{1,0:T(8,128)(2,1)} fusion(bf16[1024,3072]{1,0:T(8,128)(2,1)} %param.18, bf16[512,1024]{1,0:T(8,128)(2,1)S(1)} %copy-done.11, bf16[512,128]{1,0:T(8,128)(2,1)} %collective-permute-done.14, bf16[128,1024]{1,0:T(8,128)(2,1)S(1)} %copy-done.4), kind=kOutput, calls=%fused_computation.2 | convolution fusion | flops 2284322816 | bytes 7733248 | tf_op jit(solution)/shard_map/dot_general | solution.py:217
  158.0 48.4 %shard_map.100 = bf16[512,1024]{1,0:T(8,128)(2,1)} custom-call(s32[8,8]{1,0:T(8,128)} %pad_add_fusion.table_ref, bf16[512,1024]{1,0:T(8,128)(2,1)} %fusion.11.q_ref, bf16[768,2048]{1,0:T(8,128)(2,1)} %copy-done.1, bf16[768,2048]{1,0:T(8,128)(2,1)} %copy-done.1, bf16[768,2048]{1,0:T(8,128)(2,1)} %copy-done.1, bf16[768,2048]{1,0:T(8,128)(2,1)} %copy-done.1, ...), custom_call_target="tpu_custom_call" | custom-call | tf_op jit(solution)/shard_map/pallas_call | solution.py:160
  206.4 3.4 %convolution_convert_fusion.4 = bf16[512,1024]{1,0:T(8,128)(2,1)} fusion(bf16[512,1024]{1,0:T(8,128)(2,1)} %shard_map.100, bf16[1024,1024]{1,0:T(8,128)(2,1)S(1)} %copy-done), kind=kOutput, calls=%fused_computation.22 | convolution fusion | flops 1074266112 | bytes 4194304 | tf_op jit(solution)/shard_map/dot_general | solution.py:228
  (113 shorter events, 4.5 us)
Async XLA Ops:
  0.0 206.4 %copy-start = (bf16[1024,1024]{1,0:T(8,128)(2,1)S(1)}, bf16[1024,1024]{1,0:T(8,128)(2,1)}, u32[]{:S(2)}) copy-start(bf16[1024,1024]{1,0:T(8,128)(2,1)} %param.19) | copy-start | bytes 6291460
  5.6 8.9 %copy-start.8 = (s32[8,4]{0,1:T(4,128)S(1)}, s32[8,4]{0,1:T(4,128)}, u32[]{:S(2)}) copy-start(s32[8,4]{0,1:T(4,128)} %param.15) | copy-start | bytes 388
  5.6 9.0 %copy-start.9 = (s32[8,3]{0,1:T(4,128)S(1)}, s32[8,3]{0,1:T(4,128)}, u32[]{:S(2)}) copy-start(s32[8,3]{0,1:T(4,128)} %param.14) | copy-start | bytes 292
  9.3 5.5 %collective-permute-start.1 = (f32[8,64,448]{2,1,0:T(8,128)}, f32[8,64,448]{2,1,0:T(8,128)}, u32[]{:S(2)}, u32[]{:S(2)}) collective-permute-start(f32[8,64,448]{2,1,0:T(8,128)} %pad_maximum_fusion.1), channel_id=1, source_target_pairs={{1,0},{2,1},{3,2},{4,3},{5,4},{6,5},{7,6},{8,7},{9,8},{10,9},{11,1... | collective-permute-start | bytes 2752520 | tf_op jit(solution)/shard_map/ppermute | solution.py:27
  10.6 5.7 %collective-permute-start = (f32[8,64,448]{2,1,0:T(8,128)}, f32[8,64,448]{2,1,0:T(8,128)}, u32[]{:S(2)}, u32[]{:S(2)}) collective-permute-start(f32[8,64,448]{2,1,0:T(8,128)} %pad_maximum_fusion.1), channel_id=1, source_target_pairs={{0,1},{1,2},{2,3},{3,4},{4,5},{5,6},{6,7},{7,8},{8,9},{9,10},{10,1... | collective-permute-start | bytes 2752520 | tf_op jit(solution)/shard_map/ppermute | solution.py:27
  18.9 2.3 %copy-start.2 = (f32[8,64,320]{2,1,0:T(8,128)S(1)}, f32[8,64,320]{2,1,0:T(8,128)}, u32[]{:S(2)}) copy-start(f32[8,64,320]{2,1,0:T(8,128)} %copy.34) | copy-start | bytes 1966084
  25.8 28.2 %copy-start.7 = (f32[9]{0:T(128)S(1)}, f32[9]{0:T(128)}, u32[]{:S(2)}) copy-start(f32[9]{0:T(128)} %param.16) | copy-start | bytes 112
  25.8 28.9 %copy-start.5 = (bf16[512,1024]{1,0:T(8,128)(2,1)S(1)}, bf16[512,1024]{1,0:T(8,128)(2,1)}, u32[]{:S(2)}) copy-start(bf16[512,1024]{1,0:T(8,128)(2,1)} %param.10) | copy-start | bytes 3145732
  27.1 27.6 %collective-permute-start.3 = (f32[8,64,256]{2,1,0:T(8,128)S(1)}, f32[8,64,256]{2,1,0:T(8,128)S(1)}, u32[]{:S(2)}, u32[]{:S(2)}) collective-permute-start(f32[8,64,256]{2,1,0:T(8,128)S(1)} %pad_maximum_fusion.4), channel_id=1, source_target_pairs={{1,0},{2,1},{3,2},{4,3},{5,4},{6,5},{7,6},{8,7},{9,8},{10,9},{11,1... | collective-permute-start | bytes 1572872 | tf_op jit(solution)/shard_map/ppermute | solution.py:27
  28.4 26.3 %collective-permute-start.2 = (f32[8,64,256]{2,1,0:T(8,128)S(1)}, f32[8,64,256]{2,1,0:T(8,128)S(1)}, u32[]{:S(2)}, u32[]{:S(2)}) collective-permute-start(f32[8,64,256]{2,1,0:T(8,128)S(1)} %pad_maximum_fusion.4), channel_id=1, source_target_pairs={{0,1},{1,2},{2,3},{3,4},{4,5},{5,6},{6,7},{7,8},{8,9},{9,10},{10,1... | collective-permute-start | bytes 1572872 | tf_op jit(solution)/shard_map/ppermute | solution.py:27
  54.7 32.8 %collective-permute-start.6 = (bf16[512,1024]{1,0:T(8,128)(2,1)S(1)}, bf16[512,1024]{1,0:T(8,128)(2,1)S(1)}, u32[]{:S(2)}, u32[]{:S(2)}) collective-permute-start(bf16[512,1024]{1,0:T(8,128)(2,1)S(1)} %copy-done.5), channel_id=1, source_target_pairs={{0,2},{1,3},{2,0},{3,1},{4,6},{5,7},{6,4},{7,5},{8,10},{9,11},{10,... | collective-permute-start | bytes 3145736 | tf_op jit(solution)/shard_map/ppermute | solution.py:40
  64.1 49.5 %collective-permute-start.7 = (bf16[512,1024]{1,0:T(8,128)(2,1)S(1)}, bf16[512,1024]{1,0:T(8,128)(2,1)S(1)}, u32[]{:S(2)}, u32[]{:S(2)}) collective-permute-start(bf16[512,1024]{1,0:T(8,128)(2,1)S(1)} %copy-done.5), channel_id=1, source_target_pairs={{0,4},{1,5},{2,6},{3,7},{4,0},{5,1},{6,2},{7,3},{8,12},{9,13},{10,... | collective-permute-start | bytes 3145736 | tf_op jit(solution)/shard_map/ppermute | solution.py:40
  67.5 48.7 %collective-permute-start.8 = (bf16[512,1024]{1,0:T(8,128)(2,1)S(1)}, bf16[512,1024]{1,0:T(8,128)(2,1)S(1)}, u32[]{:S(2)}, u32[]{:S(2)}) collective-permute-start(bf16[512,1024]{1,0:T(8,128)(2,1)S(1)} %copy-done.5), channel_id=1, source_target_pairs={{0,8},{1,9},{2,10},{3,11},{4,12},{5,13},{6,14},{7,15},{8,0},{9,1},... | collective-permute-start | bytes 3145736 | tf_op jit(solution)/shard_map/ppermute | solution.py:40
  75.2 3.5 %copy-start.6 = (f32[512,128]{1,0:T(8,128)S(1)}, f32[512,128]{1,0:T(8,128)}, u32[]{:S(2)}) copy-start(f32[512,128]{1,0:T(8,128)} %param.11) | copy-start | bytes 786436
  75.3 47.7 %slice-start = ((s8[6291456]{0:T(1024)(128)(4,1)}), s8[4194304]{0:T(1024)(128)(4,1)S(1)}, s32[]{:S(2)}) async-start(s8[6291456]{0:T(1024)(128)(4,1)} %bitcast.222), calls=%async_computation | async-start | bytes 8388608
  75.5 10.3 %collective-permute-start.4 = (bf16[128,1024]{1,0:T(8,128)(2,1)S(1)}, bf16[128,1024]{1,0:T(8,128)(2,1)S(1)}, u32[]{:S(2)}, u32[]{:S(2)}) collective-permute-start(bf16[128,1024]{1,0:T(8,128)(2,1)S(1)} %get-tuple-element.20), channel_id=1, source_target_pairs={{0,1},{1,2},{2,3},{3,4},{4,5},{5,6},{6,7},{7,8},{8,9},{9,10},{10,1... | collective-permute-start | bytes 786440 | tf_op jit(solution)/shard_map/ppermute | solution.py:27
  77.5 8.3 %collective-permute-start.5 = (bf16[128,1024]{1,0:T(8,128)(2,1)S(1)}, bf16[128,1024]{1,0:T(8,128)(2,1)S(1)}, u32[]{:S(2)}, u32[]{:S(2)}) collective-permute-start(bf16[128,1024]{1,0:T(8,128)(2,1)S(1)} %get-tuple-element.19), channel_id=1, source_target_pairs={{1,0},{2,1},{3,2},{4,3},{5,4},{6,5},{7,6},{8,7},{9,8},{10,9},{11,1... | collective-permute-start | bytes 786440 | tf_op jit(solution)/shard_map/ppermute | solution.py:27
  78.8 38.8 %copy-start.3 = (bf16[128,1024]{1,0:T(8,128)(2,1)S(1)}, bf16[128,1024]{1,0:T(8,128)(2,1)}, u32[]{:S(2)}) copy-start(bf16[128,1024]{1,0:T(8,128)(2,1)} %param.17) | copy-start | bytes 786436
  78.8 44.2 %slice-start.1 = ((s8[6291456]{0:T(1024)(128)(4,1)}), s8[2097152]{0:T(1024)(128)(4,1)S(1)}, s32[]{:S(2)}) async-start(s8[6291456]{0:T(1024)(128)(4,1)} %bitcast.222), calls=%async_computation.1 | async-start | bytes 4194304
  87.6 35.4 %copy-start.13 = (bf16[512,1024]{1,0:T(8,128)(2,1)}, bf16[512,1024]{1,0:T(8,128)(2,1)S(1)}, u32[]{:S(2)}) copy-start(bf16[512,1024]{1,0:T(8,128)(2,1)S(1)} %collective-permute-done.6) | copy-start | bytes 3145732
  113.6 9.4 %copy-start.12 = (bf16[512,1024]{1,0:T(8,128)(2,1)}, bf16[512,1024]{1,0:T(8,128)(2,1)S(1)}, u32[]{:S(2)}) copy-start(bf16[512,1024]{1,0:T(8,128)(2,1)S(1)} %collective-permute-done.7) | copy-start | bytes 3145732
  116.2 6.8 %copy-start.10 = (bf16[512,1024]{1,0:T(8,128)(2,1)}, bf16[512,1024]{1,0:T(8,128)(2,1)S(1)}, u32[]{:S(2)}) copy-start(bf16[512,1024]{1,0:T(8,128)(2,1)S(1)} %collective-permute-done.8) | copy-start | bytes 3145732
  116.2 22.7 %collective-permute-start.12 = (bf16[512,128]{1,0:T(8,128)(2,1)S(1)}, bf16[512,128]{1,0:T(8,128)(2,1)}, u32[]{:S(2)}, u32[]{:S(2)}) collective-permute-start(bf16[512,128]{1,0:T(8,128)(2,1)S(1)} %bitcast.218), channel_id=1, source_target_pairs={{0,2},{1,3},{2,0},{3,1},{4,6},{5,7},{6,4},{7,5},{8,10},{9,11},{10,... | collective-permute-start | bytes 393224 | tf_op jit(solution)/shard_map/ppermute | solution.py:40
  116.3 5.8 %collective-permute-start.10 = (bf16[128,128]{1,0:T(8,128)(2,1)S(1)}, bf16[128,128]{1,0:T(8,128)(2,1)S(1)}, u32[]{:S(2)}, u32[]{:S(2)}) collective-permute-start(bf16[128,128]{1,0:T(8,128)(2,1)S(1)} %get-tuple-element.22), channel_id=1, source_target_pairs={{1,0},{2,1},{3,2},{4,3},{5,4},{6,5},{7,6},{8,7},{9,8},{10,9},{11,1... | collective-permute-start | bytes 98312 | tf_op jit(solution)/shard_map/ppermute | solution.py:27
  118.0 4.7 %collective-permute-start.9 = (bf16[128,128]{1,0:T(8,128)(2,1)S(1)}, bf16[128,128]{1,0:T(8,128)(2,1)S(1)}, u32[]{:S(2)}, u32[]{:S(2)}) collective-permute-start(bf16[128,128]{1,0:T(8,128)(2,1)S(1)} %get-tuple-element.21), channel_id=1, source_target_pairs={{0,1},{1,2},{2,3},{3,4},{4,5},{5,6},{6,7},{7,8},{8,9},{9,10},{10,1... | collective-permute-start | bytes 98312 | tf_op jit(solution)/shard_map/ppermute | solution.py:27
  126.7 2.3 %copy-start.1 = (bf16[768,2048]{1,0:T(8,128)(2,1)}, bf16[768,2048]{1,0:T(8,128)(2,1)S(1)}, u32[]{:S(2)}) copy-start(bf16[768,2048]{1,0:T(8,128)(2,1)S(1)} %convolution_convert_fusion.refs_0_.refs_1_.refs_2_.refs_3_) | copy-start | bytes 9437188
  128.9 10.0 %copy-start.4 = (bf16[128,1024]{1,0:T(8,128)(2,1)S(1)}, bf16[128,1024]{1,0:T(8,128)(2,1)}, u32[]{:S(2)}) copy-start(bf16[128,1024]{1,0:T(8,128)(2,1)} %param.17) | copy-start | bytes 786436
  128.9 10.0 %copy-start.14 = (bf16[512,1024]{1,0:T(8,128)(2,1)S(1)}, bf16[512,1024]{1,0:T(8,128)(2,1)}, u32[]{:S(2)}) copy-start(bf16[512,1024]{1,0:T(8,128)(2,1)} %copy-done.13) | copy-start | bytes 3145732
  128.9 29.1 %collective-permute-start.11 = (bf16[512,2048]{1,0:T(8,128)(2,1)}, bf16[512,2048]{1,0:T(8,128)(2,1)}, u32[]{:S(2)}, u32[]{:S(2)}) collective-permute-start(bf16[512,2048]{1,0:T(8,128)(2,1)} %slice.362), channel_id=1, source_target_pairs={{0,1},{1,0},{2,3},{3,2},{4,5},{5,4},{6,7},{7,6},{8,9},{9,8},{10,11... | collective-permute-start | bytes 6291464 | tf_op jit(solution)/shard_map/ppermute | solution.py:40
  133.0 12.2 %collective-permute-start.13 = (bf16[512,128]{1,0:T(8,128)(2,1)S(1)}, bf16[512,128]{1,0:T(8,128)(2,1)}, u32[]{:S(2)}, u32[]{:S(2)}) collective-permute-start(bf16[512,128]{1,0:T(8,128)(2,1)S(1)} %bitcast.220), channel_id=1, source_target_pairs={{0,4},{1,5},{2,6},{3,7},{4,0},{5,1},{6,2},{7,3},{8,12},{9,13},{10,... | collective-permute-start | bytes 393224 | tf_op jit(solution)/shard_map/ppermute | solution.py:40
  136.0 15.7 %collective-permute-start.14 = (bf16[512,128]{1,0:T(8,128)(2,1)S(1)}, bf16[512,128]{1,0:T(8,128)(2,1)}, u32[]{:S(2)}, u32[]{:S(2)}) collective-permute-start(bf16[512,128]{1,0:T(8,128)(2,1)S(1)} %bitcast.221), channel_id=1, source_target_pairs={{0,8},{1,9},{2,10},{3,11},{4,12},{5,13},{6,14},{7,15},{8,0},{9,1},... | collective-permute-start | bytes 393224 | tf_op jit(solution)/shard_map/ppermute | solution.py:40
  145.2 6.5 %copy-start.11 = (bf16[512,1024]{1,0:T(8,128)(2,1)S(1)}, bf16[512,1024]{1,0:T(8,128)(2,1)}, u32[]{:S(2)}) copy-start(bf16[512,1024]{1,0:T(8,128)(2,1)} %copy-done.10) | copy-start | bytes 3145732

commit v6 on v5

--- a/solution.py
+++ b/solution.py
@@ -119,35 +119,41 @@
 def attention_kernel(table_ref, q_ref, *refs):
     kv_refs = refs[:NKEY]
     out_ref = refs[NKEY]
-    scale = 1.0 / HD**0.5
     lane = lax.broadcasted_iota(jnp.int32, (1, 2 * HD), 1)
     low = lane < HD
     for pair in range(HEADS // 2):
         cols = slice(pair * 2 * HD, (pair + 1) * 2 * HD)
         vcols = slice(D + pair * 2 * HD, D + (pair + 1) * 2 * HD)
-        qs = q_ref[:, cols]
         ks = jnp.concatenate([r[:, cols] for r in kv_refs], axis=0)
         vs = jnp.concatenate([r[:, vcols] for r in kv_refs], axis=0)
-        merged = None
-        for half in range(2):
-            keep = low if half == 0 else jnp.logical_not(low)
-            qm = jnp.where(keep, qs, jnp.zeros_like(qs))
-            scores = lax.dot_general(
-                qm, ks, (((1,), (1,)), ((), ())), preferred_element_type=jnp.float32
-            ) * scale
-            top = jnp.max(scores, axis=-1, keepdims=True)
-            expd = jnp.exp(scores - top)
-            total = jnp.sum(expd, axis=-1, keepdims=True)
-            weights = (expd / total).astype(jnp.bfloat16)
-            part = jnp.dot(weights, vs, preferred_element_type=jnp.float32)
-            merged = part if half == 0 else jnp.where(low, merged, part)
+        scores = jnp.dot(ks, q_ref[0, pair], preferred_element_type=jnp.float32)
+        top = jnp.max(scores, axis=0, keepdims=True)
+        expd = jnp.exp(scores - top)
+        total = jnp.sum(expd, axis=0, keepdims=True)
+        weights = (expd * (1.0 / total)).astype(jnp.bfloat16)
+        both = lax.dot_general(
+            weights, vs, (((0,), (0,)), ((), ())), preferred_element_type=jnp.float32
+        )
+        merged = jnp.where(low, both[:BS], both[BS:])
         out_ref[:, cols] = merged.astype(jnp.bfloat16)
+
+
+def split_queries(queries):
+    count = queries.shape[0] // BS
+    pairs = HEADS // 2
+    qt = queries.reshape(count, BS, pairs, 2 * HD).transpose(0, 2, 3, 1)
+    qt = jnp.concatenate([qt, qt], axis=3)
+    d_head = lax.broadcasted_iota(jnp.int32, (2 * HD, 2 * BS), 0) // HD
+    j_head = lax.broadcasted_iota(jnp.int32, (2 * HD, 2 * BS), 1) // BS
+    scale = jnp.asarray(1.0 / HD**0.5, jnp.bfloat16)
+    return jnp.where(d_head == j_head, qt * scale, jnp.zeros_like(qt))
 
 
 def attend(queries, kv_sources, table):
     count = table.shape[0]
-    in_specs = [pl.BlockSpec((BS, D), lambda b, t: (b, 0))]
-    operands = [queries]
+    pairs = HEADS // 2
+    in_specs = [pl.BlockSpec((1, pairs, 2 * HD, 2 * BS), lambda b, t: (b, 0, 0, 0))]
+    operands = [split_queries(queries)]
     for j, src in enumerate(kv_sources):
         in_specs.append(pl.BlockSpec((BS, 2 * D), lambda b, t, j=j: (t[b, j], 0)))
         operands.append(src)

time: 210 us -> 186 us (0.89); the launches traced: 210 us -> 184 us
  Pallas kernels: 48.4 us -> 14.1 us
  matrix products: 44.5 us -> 49.2 us
  local copies, waits for them, and re-layouts: 14.4 us -> 17.3 us
  other arithmetic: 7.07 us -> 9.95 us
  starting transfers between devices: 63.4 us -> 60.9 us
    pallas_call x1, Pallas kernels: 48.4 us -> 14.1 us  [attend(): pl.pallas_call(attention_kernel, grid_spec=grid_spec, out_shape=jax.Shape...]
    select_n x0 -> x1, other arithmetic: none -> 2.75 us  [split_queries(): return jnp.where(d_head == j_head, qt * scale, jnp.zeros_like(qt))]
    dot_general x1, matrix products: 3.63 us -> 5.93 us  [on_device(): jnp.dot(near_blended, kv_weight, preferred_element_type=jnp.float32)]
  transfers between devices with their start and end apart: 15 -> 15, of which waited for: 5 -> 4; matrix products, arithmetic and copies ran while one was open for 20% -> 28% of each run, Pallas kernels for 0% -> 0%
where the time goes in v6:
time: 186 us; the launch traced here: 184 us
  starting transfers between devices  60.9 us (33%)
  matrix products  49.2 us (26%)
  waiting for transfers between devices  31.3 us (17%)
  local copies, waits for them, and re-layouts  17.3 us (9%)
  Pallas kernels  14.1 us (8%)
  other arithmetic  9.95 us (5%)
    ppermute x8, starting transfers between devices, shift_rows(): return lax.ppermute(x, axis, pairs)  39.1 us
    ppermute x7, waiting for transfers between devices, partner(): return lax.ppermute(value, axis, pairs)  30.8 us
    ppermute x7, starting transfers between devices, partner(): return lax.ppermute(value, axis, pairs)  21.9 us
    dot_general x3, matrix products, on_device(): jnp.dot(blend(f, e), kv_weight, preferred_element_type=jnp.float32)  19.1 us
    dot_general x8, matrix products, step(): jnp.einsum('wsk,wkc->wsc', bands[lo - REACH:hi - REACH], stacked, precisi...  15.1 us
    pallas_call x1, Pallas kernels, attend(): pl.pallas_call(attention_kernel, grid_spec=grid_spec, out_shape=jax.Shape...  14.1 us
    dot_general x1, matrix products, on_device(): jnp.dot(near_blended, kv_weight, preferred_element_type=jnp.float32)  5.93 us
  transfers between devices with their start and end apart: 15, of which 4 were waited for; matrix products, arithmetic and copies ran while one was open for 28% of the time, Pallas kernels for 0%

profile of v6, /device:TPU:0, one launch (start us, length us, event | category | flops | bytes accessed | tf_op | source)
XLA Modules:
  0.0 183.6 jit_solution(4808948076194378116)
XLA Ops:
  0.0 0.9 copy.33
  1.1 2.8 %select_reduce_fusion = f32[8,5,64,64]{3,2,1,0:T(8,128)} fusion(f32[8,3,64,64]{3,2,1,0:T(8,128)} %param.12, pred[8,3,5]{2,1,0:T(4,128)(4,1)S(1)} %iota_compare_fusion), kind=kLoop, calls=%fused_computation | loop fusion | flops 819200 | bytes 1048696 | tf_op jit(solution)/shard_map/reduce_sum | solution.py:61
  3.9 1.7 copy.34
  5.6 1.3 copy.35
  7.0 2.3 %pad_maximum_fusion.1 = f32[8,64,448]{2,1,0:T(8,128)} fusion(f32[8,64,320]{2,1,0:T(8,128)} %copy.35, f32[8,64,128]{2,1,0:T(8,128)} %bitcast.219), kind=kLoop, calls=%fused_computation.45 | loop fusion | flops 229376 | bytes 1835008 | tf_op jit(solution)/shard_map/concatenate | solution.py:64
  9.3 1.3 collective-permute-start.1
  10.6 4.0 %collective-permute-start = (f32[8,64,448]{2,1,0:T(8,128)}, f32[8,64,448]{2,1,0:T(8,128)}, u32[]{:S(2)}, u32[]{:S(2)}) collective-permute-start(f32[8,64,448]{2,1,0:T(8,128)} %pad_maximum_fusion.1), channel_id=1, source_target_pairs={{0,1},{1,2},{2,3},{3,4},{4,5},{5,6},{6,7},{7,8},{8,9},{9,10},{10,1... | collective-permute-start | bytes 2752520 | tf_op jit(solution)/shard_map/ppermute | solution.py:27
  14.8 1.0 slice.307
  16.2 1.0 slice.306
  17.2 1.0 pad_maximum_fusion.2
  18.9 1.2 slice.305
  20.1 1.1 slice.304
  21.2 1.3 fusion.79
  23.0 1.2 fusion.25
  24.5 1.0 fusion.19
  25.8 1.2 fusion.22
  27.1 1.3 collective-permute-start.3
  28.4 24.9 %collective-permute-start.2 = (f32[8,64,256]{2,1,0:T(8,128)S(1)}, f32[8,64,256]{2,1,0:T(8,128)S(1)}, u32[]{:S(2)}, u32[]{:S(2)}) collective-permute-start(f32[8,64,256]{2,1,0:T(8,128)S(1)} %pad_maximum_fusion.4), channel_id=1, source_target_pairs={{0,1},{1,2},{2,3},{3,4},{4,5},{5,6},{6,7},{7,8},{8,9},{9,10},{10,1... | collective-permute-start | bytes 1572872 | tf_op jit(solution)/shard_map/ppermute | solution.py:27
  54.9 9.2 %collective-permute-start.6 = (bf16[512,1024]{1,0:T(8,128)(2,1)S(1)}, bf16[512,1024]{1,0:T(8,128)(2,1)S(1)}, u32[]{:S(2)}, u32[]{:S(2)}) collective-permute-start(bf16[512,1024]{1,0:T(8,128)(2,1)S(1)} %copy-done.6), channel_id=1, source_target_pairs={{0,2},{1,3},{2,0},{3,1},{4,6},{5,7},{6,4},{7,5},{8,10},{9,11},{10,... | collective-permute-start | bytes 3145736 | tf_op jit(solution)/shard_map/ppermute | solution.py:40
  64.1 3.4 %collective-permute-start.7 = (bf16[512,1024]{1,0:T(8,128)(2,1)S(1)}, bf16[512,1024]{1,0:T(8,128)(2,1)S(1)}, u32[]{:S(2)}, u32[]{:S(2)}) collective-permute-start(bf16[512,1024]{1,0:T(8,128)(2,1)S(1)} %copy-done.6), channel_id=1, source_target_pairs={{0,4},{1,5},{2,6},{3,7},{4,0},{5,1},{6,2},{7,3},{8,12},{9,13},{10,... | collective-permute-start | bytes 3145736 | tf_op jit(solution)/shard_map/ppermute | solution.py:40
  67.5 2.6 %collective-permute-start.8 = (bf16[512,1024]{1,0:T(8,128)(2,1)S(1)}, bf16[512,1024]{1,0:T(8,128)(2,1)S(1)}, u32[]{:S(2)}, u32[]{:S(2)}) collective-permute-start(bf16[512,1024]{1,0:T(8,128)(2,1)S(1)} %copy-done.6), channel_id=1, source_target_pairs={{0,8},{1,9},{2,10},{3,11},{4,12},{5,13},{6,14},{7,15},{8,0},{9,1},... | collective-permute-start | bytes 3145736 | tf_op jit(solution)/shard_map/ppermute | solution.py:40
  70.8 1.3 fusion.18
  72.6 1.2 fusion.26
  74.2 1.0 fusion.20
  75.5 1.7 collective-permute-start.4
  77.2 1.3 collective-permute-start.5
  78.5 6.8 %fusion.24 = bf16[8,64,128]{2,1,0:T(8,128)(2,1)S(1)} fusion(f32[8,64,320]{1,2,0:T(8,128)S(1)} %bitcast.209, f32[8,320,128]{2,1,0:T(8,128)S(1)} %bitcast.215, f32[20,64,128]{2,1,0:T(8,128)S(1)} %fusion.18, f32[20,64,128]{2,1,0:T(8,128)S(1)} %fusion.79, f32[16,64,128]{2,1,0:T(8,128)S(1)} %fusion.26, f32[8,64,128]{2,1,0:T(8,128)S(1)} %fusion.22, ...), kind=kOutput, calls=%fused_computation.39 | convolution fusion | flops 127139840 | bytes 4194340 | tf_op jit(solution)/shard_map/wsk,wkc->wsc/dot_general | solution.py:80
  85.4 2.2 %collective-permute-done.6 = bf16[512,1024]{1,0:T(8,128)(2,1)S(1)} collective-permute-done((bf16[512,1024]{1,0:T(8,128)(2,1)S(1)}, bf16[512,1024]{1,0:T(8,128)(2,1)S(1)}, u32[]{:S(2)}, u32[]{:S(2)}) %collective-permute-start.6) | collective-permute-done | bytes 1048608 | tf_op jit(solution)/shard_map/ppermute | solution.py:40
  87.6 26.0 %collective-permute-done.7 = bf16[512,1024]{1,0:T(8,128)(2,1)S(1)} collective-permute-done((bf16[512,1024]{1,0:T(8,128)(2,1)S(1)}, bf16[512,1024]{1,0:T(8,128)(2,1)S(1)}, u32[]{:S(2)}, u32[]{:S(2)}) %collective-permute-start.7) | collective-permute-done | bytes 1048608 | tf_op jit(solution)/shard_map/ppermute | solution.py:40
  113.6 2.6 %collective-permute-done.8 = bf16[512,1024]{1,0:T(8,128)(2,1)S(1)} collective-permute-done((bf16[512,1024]{1,0:T(8,128)(2,1)S(1)}, bf16[512,1024]{1,0:T(8,128)(2,1)S(1)}, u32[]{:S(2)}, u32[]{:S(2)}) %collective-permute-start.8) | collective-permute-done | bytes 1048608 | tf_op jit(solution)/shard_map/ppermute | solution.py:40
  116.8 2.3 %collective-permute-start.13 = (bf16[512,128]{1,0:T(8,128)(2,1)S(1)}, bf16[512,128]{1,0:T(8,128)(2,1)}, u32[]{:S(2)}, u32[]{:S(2)}) collective-permute-start(bf16[512,128]{1,0:T(8,128)(2,1)S(1)} %bitcast.226), channel_id=1, source_target_pairs={{0,4},{1,5},{2,6},{3,7},{4,0},{5,1},{6,2},{7,3},{8,12},{9,13},{10,... | collective-permute-start | bytes 393224 | tf_op jit(solution)/shard_map/ppermute | solution.py:40
  119.2 2.6 %collective-permute-start.14 = (bf16[512,128]{1,0:T(8,128)(2,1)S(1)}, bf16[512,128]{1,0:T(8,128)(2,1)}, u32[]{:S(2)}, u32[]{:S(2)}) collective-permute-start(bf16[512,128]{1,0:T(8,128)(2,1)S(1)} %bitcast.227), channel_id=1, source_target_pairs={{0,8},{1,9},{2,10},{3,11},{4,12},{5,13},{6,14},{7,15},{8,0},{9,1},... | collective-permute-start | bytes 393224 | tf_op jit(solution)/shard_map/ppermute | solution.py:40
  122.2 1.3 collective-permute-start.10
  123.5 2.8 %fusion.15 = bf16[64,8,8,128]{3,1,2,0:T(8,128)(2,1)S(1)} fusion(bf16[512,1024]{1,0:T(8,128)(2,1)S(1)} %add_convert_fusion.3, bf16[1024,3072]{1,0:T(8,128)(2,1)} %param.18), kind=kOutput, calls=%fused_computation.25 | convolution fusion | flops 1074266112 | bytes 4194304 | tf_op jit(solution)/shard_map/dot_general | solution.py:212
  126.7 1.8 copy.47
  128.5 3.2 %collective-permute-start.9 = (bf16[128,128]{1,0:T(8,128)(2,1)}, bf16[128,128]{1,0:T(8,128)(2,1)S(1)}, u32[]{:S(2)}, u32[]{:S(2)}) collective-permute-start(bf16[128,128]{1,0:T(8,128)(2,1)} %get-tuple-element.21), channel_id=1, source_target_pairs={{0,1},{1,2},{2,3},{3,4},{4,5},{5,6},{6,7},{7,8},{8,9},{9,10},{10,1... | collective-permute-start | bytes 98312 | tf_op jit(solution)/shard_map/ppermute | solution.py:27
  131.8 1.2 add_convert_fusion.7
  133.0 1.2 add_convert_fusion.8
  134.2 5.9 %convolution_convert_fusion.refs_0_.refs_1_.refs_2_.refs_3_ = bf16[768,2048]{1,0:T(8,128)(2,1)S(1)} fusion(bf16[1024,3072]{1,0:T(8,128)(2,1)} %param.18, bf16[128,1024]{1,0:T(8,128)(2,1)S(1)} %add_convert_fusion.7, bf16[512,1024]{1,0:T(8,128)(2,1)} %copy-done.8, bf16[128,1024]{1,0:T(8,128)(2,1)S(1)} %add_convert_fusion.8), kind=kOutput, calls=%fused_computation.1 | convolution fusion | flops 3227516928 | bytes 8912896 | tf_op jit(solution)/shard_map/dot_general | solution.py:218
  140.1 1.4 slice.362
  141.6 1.0 copy-done.1
  142.6 1.6 collective-permute-start.11
  144.3 2.7 %fusion.4.q_ref = bf16[8,8,128,128]{3,2,1,0:T(8,128)(2,1)} fusion(bf16[8,8,128,64]{3,2,1,0:T(8,128)(2,1)S(1)} %bitcast.212, pred[128,128]{1,0:T(8,128)(4,1)S(1)} %select_compare_fusion), kind=kLoop, calls=%fused_computation.10 | loop fusion | flops 7340032 | bytes 3162112 | tf_op jit(solution)/shard_map/jit(_where)/select_n | solution.py:149
  147.0 6.3 %convolution_convert_fusion.3.refs_5_ = bf16[512,2048]{1,0:T(8,128)(2,1)} fusion(bf16[1024,3072]{1,0:T(8,128)(2,1)} %param.18, bf16[512,1024]{1,0:T(8,128)(2,1)S(1)} %copy-done.18, bf16[512,128]{1,0:T(8,128)(2,1)} %collective-permute-done.12, bf16[128,1024]{1,0:T(8,128)(2,1)S(1)} %copy-done.5), kind=kOutput, calls=%fused_computation.4 | convolution fusion | flops 2284322816 | bytes 7733248 | tf_op jit(solution)/shard_map/dot_general | solution.py:223
  153.3 6.6 %convolution_convert_fusion.2.refs_6_ = bf16[512,2048]{1,0:T(8,128)(2,1)} fusion(bf16[1024,3072]{1,0:T(8,128)(2,1)} %param.18, bf16[512,1024]{1,0:T(8,128)(2,1)} %copy-done.16, bf16[512,128]{1,0:T(8,128)(2,1)} %collective-permute-done.13, bf16[128,1024]{1,0:T(8,128)(2,1)S(1)} %copy-done.5), kind=kOutput, calls=%fused_computation.3 | convolution fusion | flops 2284322816 | bytes 7733248 | tf_op jit(solution)/shard_map/dot_general | solution.py:223
  159.9 6.2 %convolution_convert_fusion.1.refs_7_ = bf16[512,2048]{1,0:T(8,128)(2,1)} fusion(bf16[1024,3072]{1,0:T(8,128)(2,1)} %param.18, bf16[512,1024]{1,0:T(8,128)(2,1)S(1)} %copy-done.15, bf16[512,128]{1,0:T(8,128)(2,1)} %collective-permute-done.14, bf16[128,1024]{1,0:T(8,128)(2,1)S(1)} %copy-done.5), kind=kOutput, calls=%fused_computation.2 | convolution fusion | flops 2284322816 | bytes 7733248 | tf_op jit(solution)/shard_map/dot_general | solution.py:223
  166.1 14.1 %shard_map.100 = bf16[512,1024]{1,0:T(8,128)(2,1)} custom-call(s32[8,8]{1,0:T(8,128)} %pad_add_fusion.table_ref, bf16[8,8,128,128]{3,2,1,0:T(8,128)(2,1)} %fusion.4.q_ref, bf16[768,2048]{1,0:T(8,128)(2,1)} %copy-done.1, bf16[768,2048]{1,0:T(8,128)(2,1)} %copy-done.1, bf16[768,2048]{1,0:T(8,128)(2,1)} %copy-done.1, bf16[768,2048]{1,0:T(8,128)(2,1)} %copy-done.1, ...), custom_call_target="tpu_custom_call" | custom-call | tf_op jit(solution)/shard_map/pallas_call | solution.py:166
  180.2 3.4 %convolution_convert_fusion.4 = bf16[512,1024]{1,0:T(8,128)(2,1)} fusion(bf16[512,1024]{1,0:T(8,128)(2,1)} %shard_map.100, bf16[1024,1024]{1,0:T(8,128)(2,1)S(1)} %copy-done), kind=kOutput, calls=%fused_computation.24 | convolution fusion | flops 1074266112 | bytes 4194304 | tf_op jit(solution)/shard_map/dot_general | solution.py:234
  (122 shorter events, 6.9 us)
Async XLA Ops:
  0.0 180.2 %copy-start = (bf16[1024,1024]{1,0:T(8,128)(2,1)S(1)}, bf16[1024,1024]{1,0:T(8,128)(2,1)}, u32[]{:S(2)}) copy-start(bf16[1024,1024]{1,0:T(8,128)(2,1)} %param.19) | copy-start | bytes 6291460
  5.6 8.9 %copy-start.12 = (s32[8,4]{0,1:T(4,128)S(1)}, s32[8,4]{0,1:T(4,128)}, u32[]{:S(2)}) copy-start(s32[8,4]{0,1:T(4,128)} %param.15) | copy-start | bytes 388
  5.6 9.0 %copy-start.13 = (s32[8,3]{0,1:T(4,128)S(1)}, s32[8,3]{0,1:T(4,128)}, u32[]{:S(2)}) copy-start(s32[8,3]{0,1:T(4,128)} %param.14) | copy-start | bytes 292
  9.3 5.5 %collective-permute-start.1 = (f32[8,64,448]{2,1,0:T(8,128)}, f32[8,64,448]{2,1,0:T(8,128)}, u32[]{:S(2)}, u32[]{:S(2)}) collective-permute-start(f32[8,64,448]{2,1,0:T(8,128)} %pad_maximum_fusion.1), channel_id=1, source_target_pairs={{1,0},{2,1},{3,2},{4,3},{5,4},{6,5},{7,6},{8,7},{9,8},{10,9},{11,1... | collective-permute-start | bytes 2752520 | tf_op jit(solution)/shard_map/ppermute | solution.py:27
  10.6 5.7 %collective-permute-start = (f32[8,64,448]{2,1,0:T(8,128)}, f32[8,64,448]{2,1,0:T(8,128)}, u32[]{:S(2)}, u32[]{:S(2)}) collective-permute-start(f32[8,64,448]{2,1,0:T(8,128)} %pad_maximum_fusion.1), channel_id=1, source_target_pairs={{0,1},{1,2},{2,3},{3,4},{4,5},{5,6},{6,7},{7,8},{8,9},{9,10},{10,1... | collective-permute-start | bytes 2752520 | tf_op jit(solution)/shard_map/ppermute | solution.py:27
  18.9 2.3 %copy-start.2 = (f32[8,64,320]{2,1,0:T(8,128)S(1)}, f32[8,64,320]{2,1,0:T(8,128)}, u32[]{:S(2)}) copy-start(f32[8,64,320]{2,1,0:T(8,128)} %copy.35) | copy-start | bytes 1966084
  25.8 28.2 %copy-start.11 = (f32[9]{0:T(128)S(1)}, f32[9]{0:T(128)}, u32[]{:S(2)}) copy-start(f32[9]{0:T(128)} %param.16) | copy-start | bytes 112
  25.8 29.0 %copy-start.6 = (bf16[512,1024]{1,0:T(8,128)(2,1)S(1)}, bf16[512,1024]{1,0:T(8,128)(2,1)}, u32[]{:S(2)}) copy-start(bf16[512,1024]{1,0:T(8,128)(2,1)} %param.10) | copy-start | bytes 3145732
  27.1 27.7 %collective-permute-start.3 = (f32[8,64,256]{2,1,0:T(8,128)S(1)}, f32[8,64,256]{2,1,0:T(8,128)S(1)}, u32[]{:S(2)}, u32[]{:S(2)}) collective-permute-start(f32[8,64,256]{2,1,0:T(8,128)S(1)} %pad_maximum_fusion.4), channel_id=1, source_target_pairs={{1,0},{2,1},{3,2},{4,3},{5,4},{6,5},{7,6},{8,7},{9,8},{10,9},{11,1... | collective-permute-start | bytes 1572872 | tf_op jit(solution)/shard_map/ppermute | solution.py:27
  28.4 26.5 %collective-permute-start.2 = (f32[8,64,256]{2,1,0:T(8,128)S(1)}, f32[8,64,256]{2,1,0:T(8,128)S(1)}, u32[]{:S(2)}, u32[]{:S(2)}) collective-permute-start(f32[8,64,256]{2,1,0:T(8,128)S(1)} %pad_maximum_fusion.4), channel_id=1, source_target_pairs={{0,1},{1,2},{2,3},{3,4},{4,5},{5,6},{6,7},{7,8},{8,9},{9,10},{10,1... | collective-permute-start | bytes 1572872 | tf_op jit(solution)/shard_map/ppermute | solution.py:27
  54.9 32.7 %collective-permute-start.6 = (bf16[512,1024]{1,0:T(8,128)(2,1)S(1)}, bf16[512,1024]{1,0:T(8,128)(2,1)S(1)}, u32[]{:S(2)}, u32[]{:S(2)}) collective-permute-start(bf16[512,1024]{1,0:T(8,128)(2,1)S(1)} %copy-done.6), channel_id=1, source_target_pairs={{0,2},{1,3},{2,0},{3,1},{4,6},{5,7},{6,4},{7,5},{8,10},{9,11},{10,... | collective-permute-start | bytes 3145736 | tf_op jit(solution)/shard_map/ppermute | solution.py:40
  64.1 49.5 %collective-permute-start.7 = (bf16[512,1024]{1,0:T(8,128)(2,1)S(1)}, bf16[512,1024]{1,0:T(8,128)(2,1)S(1)}, u32[]{:S(2)}, u32[]{:S(2)}) collective-permute-start(bf16[512,1024]{1,0:T(8,128)(2,1)S(1)} %copy-done.6), channel_id=1, source_target_pairs={{0,4},{1,5},{2,6},{3,7},{4,0},{5,1},{6,2},{7,3},{8,12},{9,13},{10,... | collective-permute-start | bytes 3145736 | tf_op jit(solution)/shard_map/ppermute | solution.py:40
  67.5 48.7 %collective-permute-start.8 = (bf16[512,1024]{1,0:T(8,128)(2,1)S(1)}, bf16[512,1024]{1,0:T(8,128)(2,1)S(1)}, u32[]{:S(2)}, u32[]{:S(2)}) collective-permute-start(bf16[512,1024]{1,0:T(8,128)(2,1)S(1)} %copy-done.6), channel_id=1, source_target_pairs={{0,8},{1,9},{2,10},{3,11},{4,12},{5,13},{6,14},{7,15},{8,0},{9,1},... | collective-permute-start | bytes 3145736 | tf_op jit(solution)/shard_map/ppermute | solution.py:40
  75.2 3.3 %copy-start.7 = (f32[512,128]{1,0:T(8,128)S(1)}, f32[512,128]{1,0:T(8,128)}, u32[]{:S(2)}) copy-start(f32[512,128]{1,0:T(8,128)} %param.11) | copy-start | bytes 786436
  75.5 9.9 %collective-permute-start.4 = (bf16[128,1024]{1,0:T(8,128)(2,1)S(1)}, bf16[128,1024]{1,0:T(8,128)(2,1)S(1)}, u32[]{:S(2)}, u32[]{:S(2)}) collective-permute-start(bf16[128,1024]{1,0:T(8,128)(2,1)S(1)} %get-tuple-element.20), channel_id=1, source_target_pairs={{0,1},{1,2},{2,3},{3,4},{4,5},{5,6},{6,7},{7,8},{8,9},{9,10},{10,1... | collective-permute-start | bytes 786440 | tf_op jit(solution)/shard_map/ppermute | solution.py:27
  77.2 8.2 %collective-permute-start.5 = (bf16[128,1024]{1,0:T(8,128)(2,1)S(1)}, bf16[128,1024]{1,0:T(8,128)(2,1)S(1)}, u32[]{:S(2)}, u32[]{:S(2)}) collective-permute-start(bf16[128,1024]{1,0:T(8,128)(2,1)S(1)} %get-tuple-element.19), channel_id=1, source_target_pairs={{1,0},{2,1},{3,2},{4,3},{5,4},{6,5},{7,6},{8,7},{9,8},{10,9},{11,1... | collective-permute-start | bytes 786440 | tf_op jit(solution)/shard_map/ppermute | solution.py:27
  78.5 43.3 %copy-start.4 = (bf16[128,1024]{1,0:T(8,128)(2,1)S(1)}, bf16[128,1024]{1,0:T(8,128)(2,1)}, u32[]{:S(2)}) copy-start(bf16[128,1024]{1,0:T(8,128)(2,1)} %param.17) | copy-start | bytes 786436
  85.3 33.8 %copy-start.9 = (bf16[128,1024]{1,0:T(8,128)(2,1)}, bf16[128,1024]{1,0:T(8,128)(2,1)S(1)}, u32[]{:S(2)}) copy-start(bf16[128,1024]{1,0:T(8,128)(2,1)S(1)} %collective-permute-done.4) | copy-start | bytes 786436
  85.4 33.8 %copy-start.10 = (bf16[128,1024]{1,0:T(8,128)(2,1)}, bf16[128,1024]{1,0:T(8,128)(2,1)S(1)}, u32[]{:S(2)}) copy-start(bf16[128,1024]{1,0:T(8,128)(2,1)S(1)} %collective-permute-done.5) | copy-start | bytes 786436
  87.6 38.8 %copy-start.17 = (bf16[512,1024]{1,0:T(8,128)(2,1)}, bf16[512,1024]{1,0:T(8,128)(2,1)S(1)}, u32[]{:S(2)}) copy-start(bf16[512,1024]{1,0:T(8,128)(2,1)S(1)} %collective-permute-done.6) | copy-start | bytes 3145732
  113.6 12.8 %copy-start.16 = (bf16[512,1024]{1,0:T(8,128)(2,1)}, bf16[512,1024]{1,0:T(8,128)(2,1)S(1)}, u32[]{:S(2)}) copy-start(bf16[512,1024]{1,0:T(8,128)(2,1)S(1)} %collective-permute-done.7) | copy-start | bytes 3145732
  116.2 10.2 %copy-start.14 = (bf16[512,1024]{1,0:T(8,128)(2,1)}, bf16[512,1024]{1,0:T(8,128)(2,1)S(1)}, u32[]{:S(2)}) copy-start(bf16[512,1024]{1,0:T(8,128)(2,1)S(1)} %collective-permute-done.8) | copy-start | bytes 3145732
  116.8 30.2 %collective-permute-start.12 = (bf16[512,128]{1,0:T(8,128)(2,1)S(1)}, bf16[512,128]{1,0:T(8,128)(2,1)}, u32[]{:S(2)}, u32[]{:S(2)}) collective-permute-start(bf16[512,128]{1,0:T(8,128)(2,1)S(1)} %bitcast.225), channel_id=1, source_target_pairs={{0,2},{1,3},{2,0},{3,1},{4,6},{5,7},{6,4},{7,5},{8,10},{9,11},{10,... | collective-permute-start | bytes 393224 | tf_op jit(solution)/shard_map/ppermute | solution.py:40
  116.8 36.4 %collective-permute-start.13 = (bf16[512,128]{1,0:T(8,128)(2,1)S(1)}, bf16[512,128]{1,0:T(8,128)(2,1)}, u32[]{:S(2)}, u32[]{:S(2)}) collective-permute-start(bf16[512,128]{1,0:T(8,128)(2,1)S(1)} %bitcast.226), channel_id=1, source_target_pairs={{0,4},{1,5},{2,6},{3,7},{4,0},{5,1},{6,2},{7,3},{8,12},{9,13},{10,... | collective-permute-start | bytes 393224 | tf_op jit(solution)/shard_map/ppermute | solution.py:40
  119.2 40.7 %collective-permute-start.14 = (bf16[512,128]{1,0:T(8,128)(2,1)S(1)}, bf16[512,128]{1,0:T(8,128)(2,1)}, u32[]{:S(2)}, u32[]{:S(2)}) collective-permute-start(bf16[512,128]{1,0:T(8,128)(2,1)S(1)} %bitcast.227), channel_id=1, source_target_pairs={{0,8},{1,9},{2,10},{3,11},{4,12},{5,13},{6,14},{7,15},{8,0},{9,1},... | collective-permute-start | bytes 393224 | tf_op jit(solution)/shard_map/ppermute | solution.py:40
  122.2 4.2 %copy-start.8 = (bf16[512,1024]{1,0:T(8,128)(2,1)}, bf16[512,1024]{1,0:T(8,128)(2,1)S(1)}, u32[]{:S(2)}) copy-start(bf16[512,1024]{1,0:T(8,128)(2,1)S(1)} %add_convert_fusion.3) | copy-start | bytes 3145732
  122.2 9.5 %collective-permute-start.10 = (bf16[128,128]{1,0:T(8,128)(2,1)}, bf16[128,128]{1,0:T(8,128)(2,1)}, u32[]{:S(2)}, u32[]{:S(2)}) collective-permute-start(bf16[128,128]{1,0:T(8,128)(2,1)} %get-tuple-element.22), channel_id=1, source_target_pairs={{1,0},{2,1},{3,2},{4,3},{5,4},{6,5},{7,6},{8,7},{9,8},{10,9},{11,1... | collective-permute-start | bytes 98312 | tf_op jit(solution)/shard_map/ppermute | solution.py:27
  126.7 5.1 %copy-start.5 = (bf16[128,1024]{1,0:T(8,128)(2,1)S(1)}, bf16[128,1024]{1,0:T(8,128)(2,1)}, u32[]{:S(2)}) copy-start(bf16[128,1024]{1,0:T(8,128)(2,1)} %param.17) | copy-start | bytes 786436
  128.5 4.5 %collective-permute-start.9 = (bf16[128,128]{1,0:T(8,128)(2,1)}, bf16[128,128]{1,0:T(8,128)(2,1)S(1)}, u32[]{:S(2)}, u32[]{:S(2)}) collective-permute-start(bf16[128,128]{1,0:T(8,128)(2,1)} %get-tuple-element.21), channel_id=1, source_target_pairs={{0,1},{1,2},{2,3},{3,4},{4,5},{5,6},{6,7},{7,8},{8,9},{9,10},{10,1... | collective-permute-start | bytes 98312 | tf_op jit(solution)/shard_map/ppermute | solution.py:27
  140.1 2.5 %copy-start.1 = (bf16[768,2048]{1,0:T(8,128)(2,1)}, bf16[768,2048]{1,0:T(8,128)(2,1)S(1)}, u32[]{:S(2)}) copy-start(bf16[768,2048]{1,0:T(8,128)(2,1)S(1)} %convolution_convert_fusion.refs_0_.refs_1_.refs_2_.refs_3_) | copy-start | bytes 9437188
  140.1 4.1 %copy-start.3 = (bf16[8,64,8,128]{1,3,2,0:T(8,128)(2,1)S(1)}, bf16[8,64,8,128]{1,3,2,0:T(8,128)(2,1)}, u32[]{:S(2)}) copy-start(bf16[8,64,8,128]{1,3,2,0:T(8,128)(2,1)} %copy.47) | copy-start | bytes 3145732
  142.6 23.5 %collective-permute-start.11 = (bf16[512,2048]{1,0:T(8,128)(2,1)}, bf16[512,2048]{1,0:T(8,128)(2,1)}, u32[]{:S(2)}, u32[]{:S(2)}) collective-permute-start(bf16[512,2048]{1,0:T(8,128)(2,1)} %slice.362), channel_id=1, source_target_pairs={{0,1},{1,0},{2,3},{3,2},{4,5},{5,4},{6,7},{7,6},{8,9},{9,8},{10,11... | collective-permute-start | bytes 6291464 | tf_op jit(solution)/shard_map/ppermute | solution.py:40
  144.3 2.8 %copy-start.18 = (bf16[512,1024]{1,0:T(8,128)(2,1)S(1)}, bf16[512,1024]{1,0:T(8,128)(2,1)}, u32[]{:S(2)}) copy-start(bf16[512,1024]{1,0:T(8,128)(2,1)} %copy-done.17) | copy-start | bytes 3145732
  153.3 6.6 %copy-start.15 = (bf16[512,1024]{1,0:T(8,128)(2,1)S(1)}, bf16[512,1024]{1,0:T(8,128)(2,1)}, u32[]{:S(2)}) copy-start(bf16[512,1024]{1,0:T(8,128)(2,1)} %copy-done.14) | copy-start | bytes 3145732

commit v7 on v6

--- a/solution.py
+++ b/solution.py
@@ -15,7 +15,7 @@
 NEXP = 4
 REACH = 2
 NKEY = 1 + 3 + NEXP
-PER_EXCHANGE = 4
+PER_EXCHANGE = 2
 
 
 def shift_rows(x, axis, step):
@@ -62,15 +62,13 @@
     bands = bands.transpose(0, 2, 1, 3).reshape(count, BS, taps * BS)
     own_field = struct_feats.reshape(count, BS, chans)
     payload = jnp.concatenate([own_field, bands], axis=2)
-    left = shift_rows(payload, "seq", 1)
-    right = shift_rows(payload, "seq", -1)
+    left = shift_rows(payload[count - halo :], "seq", 1)
+    right = shift_rows(payload[:halo], "seq", -1)
     edge = halo - REACH
     bands = jnp.concatenate(
-        [left[count - edge :, :, chans:], bands, right[:edge, :, chans:]], axis=0
-    )
-    field = jnp.concatenate(
-        [left[count - halo :, :, :chans], own_field, right[:halo, :, :chans]], axis=0
-    )
+        [left[halo - edge :, :, chans:], bands, right[:edge, :, chans:]], axis=0
+    )
+    field = jnp.concatenate([left[:, :, :chans], own_field, right[:, :, :chans]], axis=0)
     width = field.shape[0]
 
     def step(values, lo, hi, base):
@@ -88,17 +86,15 @@
     encoding = series_coef[0] * field[own]
     for degree in range(1, DEG + 1):
         if degree > 1 and (degree - 1) % PER_EXCHANGE == 0:
-            packed = jnp.concatenate([prev[own.start - prev_base : own.stop - prev_base], cur], axis=2)
-            left = shift_rows(packed, "seq", 1)
-            right = shift_rows(packed, "seq", -1)
             older = prev[own.start - prev_base : own.stop - prev_base]
+            packed = jnp.concatenate([older, cur], axis=2)
+            left = shift_rows(packed[count - halo :], "seq", 1)
+            right = shift_rows(packed[:halo], "seq", -1)
             prev = jnp.concatenate(
-                [left[count - edge :, :, :chans], older, right[:edge, :, :chans]], axis=0
+                [left[halo - edge :, :, :chans], older, right[:edge, :, :chans]], axis=0
             )
             prev_base = REACH
-            cur = jnp.concatenate(
-                [left[count - halo :, :, chans:], cur, right[:halo, :, chans:]], axis=0
-            )
+            cur = jnp.concatenate([left[:, :, chans:], cur, right[:, :, chans:]], axis=0)
             cur_base = 0
             lo, hi = 0, width
         if degree == 1 or (degree - 1) % PER_EXCHANGE == 0:
@@ -190,7 +186,7 @@
     bits = [link * (levels - 1) // (NEXP - 1) for link in range(NEXP)]
 
     encoding, parts = chebyshev(struct_feats, op_blocks, laplace_index, series_coef, first_block)
-    held = lax.optimization_barrier((node_feats, list(parts.values())))[0]
+    held = node_feats
     feats_before = shift_rows(held[rows - rim:], "seq", 1)
     feats_after = shift_rows(held[:rim], "seq", -1)
     feats_far = [partner(held, "seq", bit) for bit in bits[1:]]

time: 186 us -> 202 us (1.086)
  starting transfers between devices: 60.9 us -> 96 us
  waiting for transfers between devices: 31.3 us -> 1.29 us
  local copies, waits for them, and re-layouts: 17.3 us -> 22.4 us
  other arithmetic: 9.95 us -> 13.9 us
    ppermute x8 -> x12, starting transfers between devices: 39.1 us -> 77.6 us  [shift_rows(): return lax.ppermute(x, axis, pairs)]
    ppermute x7, waiting for transfers between devices: 30.8 us -> 0.02 us  [partner(): return lax.ppermute(value, axis, pairs)]
    unnamed x74 -> x106, local copies, waits for them, and re-layouts: 3.55 us -> 7.46 us
    ppermute x7, starting transfers between devices: 21.9 us -> 18.4 us  [partner(): return lax.ppermute(value, axis, pairs)]
    concatenate x3 -> x7, other arithmetic: 1.11 us -> 3.8 us  [the longest x3 2.01 us: chebyshev(): jnp.concatenate([left[:, :, chans:], cur, right[:, :, chans:]], axis=0)]
  transfers between devices with their start and end apart: 15 -> 19, of which waited for: 4 -> 3; matrix products, arithmetic and copies ran while one was open for 28% -> 34% of each run, Pallas kernels for 0% -> 0%
where the time goes in v7:
time: 202 us; the launch traced here: 200 us
  starting transfers between devices  96 us (48%)
  matrix products  50.3 us (25%)
  local copies, waits for them, and re-layouts  22.4 us (11%)
  Pallas kernels  14.5 us (7%)
  other arithmetic  13.9 us (7%)
    ppermute x12, starting transfers between devices, shift_rows(): return lax.ppermute(x, axis, pairs)  77.6 us
    dot_general x3, matrix products, on_device(): jnp.dot(blend(f, e), kv_weight, preferred_element_type=jnp.float32)  19.5 us
    ppermute x7, starting transfers between devices, partner(): return lax.ppermute(value, axis, pairs)  18.4 us
    dot_general x8, matrix products, step(): jnp.einsum('wsk,wkc->wsc', bands[lo - REACH:hi - REACH], stacked, precisi...  14.6 us
    pallas_call x1, Pallas kernels, attend(): pl.pallas_call(attention_kernel, grid_spec=grid_spec, out_shape=jax.Shape...  14.5 us
    unnamed x106, local copies, waits for them, and re-layouts  7.46 us
    dot_general x1, matrix products, on_device(): jnp.dot(near_blended, kv_weight, preferred_element_type=jnp.float32)  5.93 us
  transfers between devices with their start and end apart: 19, of which 3 were waited for; matrix products, arithmetic and copies ran while one was open for 34% of the time, Pallas kernels for 0%

profile of v7, /device:TPU:0, one launch (start us, length us, event | category | flops | bytes accessed | tf_op | source)
XLA Modules:
  0.0 199.6 jit_solution(13879917280451040767)
XLA Ops:
  1.1 2.9 %select_reduce_fusion = f32[8,5,64,64]{3,2,1,0:T(8,128)} fusion(f32[8,3,64,64]{3,2,1,0:T(8,128)} %param.12, pred[8,3,5]{2,1,0:T(4,128)(4,1)S(1)} %iota_compare_fusion), kind=kLoop, calls=%fused_computation | loop fusion | flops 819200 | bytes 1048696 | tf_op jit(solution)/shard_map/reduce_sum | solution.py:61
  3.9 1.7 copy.36
  5.6 1.3 copy.37
  7.0 1.3 pad_maximum_fusion.1
  8.3 2.4 %collective-permute-start = (f32[4,64,448]{2,1,0:T(8,128)S(1)}, f32[4,64,448]{2,1,0:T(8,128)S(1)}, u32[]{:S(2)}, u32[]{:S(2)}) collective-permute-start(f32[4,64,448]{2,1,0:T(8,128)S(1)} %get-tuple-element.20), channel_id=1, source_target_pairs={{0,1},{1,2},{2,3},{3,4},{4,5},{5,6},{6,7},{7,8},{8,9},{9,10},{10,1... | collective-permute-start | bytes 1376264 | tf_op jit(solution)/shard_map/ppermute | solution.py:27
  10.7 2.5 %collective-permute-start.10 = (bf16[512,1024]{1,0:T(8,128)(2,1)}, bf16[512,1024]{1,0:T(8,128)(2,1)}, u32[]{:S(2)}, u32[]{:S(2)}) collective-permute-start(bf16[512,1024]{1,0:T(8,128)(2,1)} %param.10), channel_id=1, source_target_pairs={{0,2},{1,3},{2,0},{3,1},{4,6},{5,7},{6,4},{7,5},{8,10},{9,11},{10,... | collective-permute-start | bytes 3145736 | tf_op jit(solution)/shard_map/ppermute | solution.py:40
  13.3 1.6 collective-permute-start.11
  14.8 2.6 %collective-permute-start.12 = (bf16[512,1024]{1,0:T(8,128)(2,1)}, bf16[512,1024]{1,0:T(8,128)(2,1)}, u32[]{:S(2)}, u32[]{:S(2)}) collective-permute-start(bf16[512,1024]{1,0:T(8,128)(2,1)} %param.10), channel_id=1, source_target_pairs={{0,8},{1,9},{2,10},{3,11},{4,12},{5,13},{6,14},{7,15},{8,0},{9,1},... | collective-permute-start | bytes 3145736 | tf_op jit(solution)/shard_map/ppermute | solution.py:40
  17.4 1.3 collective-permute-start.1
  18.7 1.9 fusion.79
  24.3 1.3 fusion.24
  27.1 24.7 %collective-permute-start.2 = (f32[4,64,256]{2,1,0:T(8,128)}, f32[4,64,256]{2,1,0:T(8,128)}, u32[]{:S(2)}, u32[]{:S(2)}) collective-permute-start(f32[4,64,256]{2,1,0:T(8,128)} %get-tuple-element.26), channel_id=1, source_target_pairs={{0,1},{1,2},{2,3},{3,4},{4,5},{5,6},{6,7},{7,8},{8,9},{9,10},{10,1... | collective-permute-start | bytes 786440 | tf_op jit(solution)/shard_map/ppermute | solution.py:27
  51.9 1.3 collective-permute-start.3
  54.3 1.0 fusion.48
  55.6 1.0 pad_maximum_fusion.3
  57.0 1.0 slice.332
  59.8 1.3 fusion.23
  62.7 30.1 %collective-permute-start.4 = (f32[4,64,256]{2,1,0:T(8,128)}, f32[4,64,256]{2,1,0:T(8,128)}, u32[]{:S(2)}, u32[]{:S(2)}) collective-permute-start(f32[4,64,256]{2,1,0:T(8,128)} %get-tuple-element.24), channel_id=1, source_target_pairs={{0,1},{1,2},{2,3},{3,4},{4,5},{5,6},{6,7},{7,8},{8,9},{9,10},{10,1... | collective-permute-start | bytes 786440 | tf_op jit(solution)/shard_map/ppermute | solution.py:27
  92.9 1.3 collective-permute-start.5
  95.1 1.0 fusion.50
  96.5 1.0 pad_maximum_fusion.4
  97.9 1.0 slice.346
  100.3 1.3 fusion.22
  101.6 6.4 %collective-permute-start.6 = (f32[4,64,256]{2,1,0:T(8,128)S(1)}, f32[4,64,256]{2,1,0:T(8,128)S(1)}, u32[]{:S(2)}, u32[]{:S(2)}) collective-permute-start(f32[4,64,256]{2,1,0:T(8,128)S(1)} %get-tuple-element.22), channel_id=1, source_target_pairs={{0,1},{1,2},{2,3},{3,4},{4,5},{5,6},{6,7},{7,8},{8,9},{9,10},{10,1... | collective-permute-start | bytes 786440 | tf_op jit(solution)/shard_map/ppermute | solution.py:27
  108.0 1.3 collective-permute-start.7
  110.6 3.0 %collective-permute-start.8 = (bf16[128,1024]{1,0:T(8,128)(2,1)S(1)}, bf16[128,1024]{1,0:T(8,128)(2,1)S(1)}, u32[]{:S(2)}, u32[]{:S(2)}) collective-permute-start(bf16[128,1024]{1,0:T(8,128)(2,1)S(1)} %copy-done.33), channel_id=1, source_target_pairs={{0,1},{1,2},{2,3},{3,4},{4,5},{5,6},{6,7},{7,8},{8,9},{9,10},{10,1... | collective-permute-start | bytes 786440 | tf_op jit(solution)/shard_map/ppermute | solution.py:27
  113.8 1.5 collective-permute-start.9
  118.1 7.0 %fusion.26 = bf16[8,64,128]{2,1,0:T(8,128)(2,1)S(1)} fusion(f32[8,64,128]{2,1,0:T(8,128)S(1)} %fusion.22, f32[8,64,320]{1,2,0:T(8,128)S(1)} %bitcast.209, f32[8,320,128]{2,1,0:T(8,128)S(1)} %bitcast.225, f32[8,64,128]{2,1,0:T(8,128)S(1)} %copy-done.9, f32[8,64,128]{2,1,0:T(8,128)S(1)} %copy-done.7, f32[8,64,128]{2,1,0:T(8,128)S(1)} %bitcast.215, ...), kind=kOutput, calls=%fused_computation.41 | convolution fusion | flops 127139840 | bytes 4194340 | tf_op jit(solution)/shard_map/wsk,wkc->wsc/dot_general | solution.py:78
  125.8 5.1 %collective-permute-start.16 = (bf16[512,128]{1,0:T(8,128)(2,1)S(1)}, bf16[512,128]{1,0:T(8,128)(2,1)}, u32[]{:S(2)}, u32[]{:S(2)}) collective-permute-start(bf16[512,128]{1,0:T(8,128)(2,1)S(1)} %bitcast.228), channel_id=1, source_target_pairs={{0,2},{1,3},{2,0},{3,1},{4,6},{5,7},{6,4},{7,5},{8,10},{9,11},{10,... | collective-permute-start | bytes 393224 | tf_op jit(solution)/shard_map/ppermute | solution.py:40
  130.9 3.2 %collective-permute-start.17 = (bf16[512,128]{1,0:T(8,128)(2,1)S(1)}, bf16[512,128]{1,0:T(8,128)(2,1)}, u32[]{:S(2)}, u32[]{:S(2)}) collective-permute-start(bf16[512,128]{1,0:T(8,128)(2,1)S(1)} %bitcast.229), channel_id=1, source_target_pairs={{0,4},{1,5},{2,6},{3,7},{4,0},{5,1},{6,2},{7,3},{8,12},{9,13},{10,... | collective-permute-start | bytes 393224 | tf_op jit(solution)/shard_map/ppermute | solution.py:40
  134.1 1.8 collective-permute-start.18
  135.9 1.6 add_convert_fusion.3
  137.5 1.3 collective-permute-start.14
  138.8 2.8 %fusion.15 = bf16[64,8,8,128]{3,1,2,0:T(8,128)(2,1)S(1)} fusion(bf16[512,1024]{1,0:T(8,128)(2,1)S(1)} %add_convert_fusion.3, bf16[1024,3072]{1,0:T(8,128)(2,1)} %param.18), kind=kOutput, calls=%fused_computation.24 | convolution fusion | flops 1074266112 | bytes 4194304 | tf_op jit(solution)/shard_map/dot_general | solution.py:208
  142.0 1.8 copy.51
  143.8 3.0 %collective-permute-start.13 = (bf16[128,128]{1,0:T(8,128)(2,1)}, bf16[128,128]{1,0:T(8,128)(2,1)S(1)}, u32[]{:S(2)}, u32[]{:S(2)}) collective-permute-start(bf16[128,128]{1,0:T(8,128)(2,1)} %get-tuple-element.27), channel_id=1, source_target_pairs={{0,1},{1,2},{2,3},{3,4},{4,5},{5,6},{6,7},{7,8},{8,9},{9,10},{10,1... | collective-permute-start | bytes 98312 | tf_op jit(solution)/shard_map/ppermute | solution.py:27
  146.9 1.2 add_convert_fusion.7
  148.1 1.2 add_convert_fusion.8
  149.2 5.9 %convolution_convert_fusion.refs_0_.refs_1_.refs_2_.refs_3_ = bf16[768,2048]{1,0:T(8,128)(2,1)S(1)} fusion(bf16[1024,3072]{1,0:T(8,128)(2,1)} %param.18, bf16[128,1024]{1,0:T(8,128)(2,1)S(1)} %add_convert_fusion.7, bf16[512,1024]{1,0:T(8,128)(2,1)} %copy-done.29, bf16[128,1024]{1,0:T(8,128)(2,1)S(1)} %add_convert_fusion.8), kind=kOutput, calls=%fused_computation.1 | convolution fusion | flops 3227516928 | bytes 8912896 | tf_op jit(solution)/shard_map/dot_general | solution.py:214
  155.2 1.4 slice.369
  156.6 1.0 copy-done.1
  157.7 1.7 collective-permute-start.15
  159.4 2.8 %fusion.4.q_ref = bf16[8,8,128,128]{3,2,1,0:T(8,128)(2,1)} fusion(bf16[8,8,128,64]{3,2,1,0:T(8,128)(2,1)S(1)} %bitcast.216, pred[128,128]{1,0:T(8,128)(4,1)S(1)} %select_compare_fusion), kind=kLoop, calls=%fused_computation.10 | loop fusion | flops 7340032 | bytes 3162112 | tf_op jit(solution)/shard_map/jit(_where)/select_n | solution.py:145
  162.1 6.5 %convolution_convert_fusion.3.refs_5_ = bf16[512,2048]{1,0:T(8,128)(2,1)} fusion(bf16[1024,3072]{1,0:T(8,128)(2,1)} %param.18, bf16[512,1024]{1,0:T(8,128)(2,1)} %collective-permute-done.10, bf16[512,128]{1,0:T(8,128)(2,1)} %collective-permute-done.16, bf16[128,1024]{1,0:T(8,128)(2,1)S(1)} %copy-done.24), kind=kOutput, calls=%fused_computation.4 | convolution fusion | flops 2284322816 | bytes 7733248 | tf_op jit(solution)/shard_map/dot_general | solution.py:219
  168.7 6.5 %convolution_convert_fusion.2.refs_6_ = bf16[512,2048]{1,0:T(8,128)(2,1)} fusion(bf16[1024,3072]{1,0:T(8,128)(2,1)} %param.18, bf16[512,1024]{1,0:T(8,128)(2,1)} %collective-permute-done.11, bf16[512,128]{1,0:T(8,128)(2,1)} %collective-permute-done.17, bf16[128,1024]{1,0:T(8,128)(2,1)S(1)} %copy-done.24), kind=kOutput, calls=%fused_computation.3 | convolution fusion | flops 2284322816 | bytes 7733248 | tf_op jit(solution)/shard_map/dot_general | solution.py:219
  175.2 6.5 %convolution_convert_fusion.1.refs_7_ = bf16[512,2048]{1,0:T(8,128)(2,1)} fusion(bf16[1024,3072]{1,0:T(8,128)(2,1)} %param.18, bf16[512,1024]{1,0:T(8,128)(2,1)} %collective-permute-done.12, bf16[512,128]{1,0:T(8,128)(2,1)} %collective-permute-done.18, bf16[128,1024]{1,0:T(8,128)(2,1)S(1)} %copy-done.24), kind=kOutput, calls=%fused_computation.2 | convolution fusion | flops 2284322816 | bytes 7733248 | tf_op jit(solution)/shard_map/dot_general | solution.py:219
  181.7 14.5 %shard_map.100 = bf16[512,1024]{1,0:T(8,128)(2,1)} custom-call(s32[8,8]{1,0:T(8,128)} %pad_add_fusion.table_ref, bf16[8,8,128,128]{3,2,1,0:T(8,128)(2,1)} %fusion.4.q_ref, bf16[768,2048]{1,0:T(8,128)(2,1)} %copy-done.1, bf16[768,2048]{1,0:T(8,128)(2,1)} %copy-done.1, bf16[768,2048]{1,0:T(8,128)(2,1)} %copy-done.1, bf16[768,2048]{1,0:T(8,128)(2,1)} %copy-done.1, ...), custom_call_target="tpu_custom_call" | custom-call | tf_op jit(solution)/shard_map/pallas_call | solution.py:162
  196.1 3.4 %convolution_convert_fusion.4 = bf16[512,1024]{1,0:T(8,128)(2,1)} fusion(bf16[512,1024]{1,0:T(8,128)(2,1)} %shard_map.100, bf16[1024,1024]{1,0:T(8,128)(2,1)S(1)} %copy-done), kind=kOutput, calls=%fused_computation.23 | convolution fusion | flops 1074266112 | bytes 4194304 | tf_op jit(solution)/shard_map/dot_general | solution.py:230
  (180 shorter events, 19.4 us)
Async XLA Ops:
  0.0 196.1 %copy-start = (bf16[1024,1024]{1,0:T(8,128)(2,1)S(1)}, bf16[1024,1024]{1,0:T(8,128)(2,1)}, u32[]{:S(2)}) copy-start(bf16[1024,1024]{1,0:T(8,128)(2,1)} %param.19) | copy-start | bytes 6291460
  7.0 13.6 %copy-start.14 = (f32[512,128]{1,0:T(8,128)S(1)}, f32[512,128]{1,0:T(8,128)}, u32[]{:S(2)}) copy-start(f32[512,128]{1,0:T(8,128)} %param.11) | copy-start | bytes 786436
  8.3 12.3 %collective-permute-start = (f32[4,64,448]{2,1,0:T(8,128)S(1)}, f32[4,64,448]{2,1,0:T(8,128)S(1)}, u32[]{:S(2)}, u32[]{:S(2)}) collective-permute-start(f32[4,64,448]{2,1,0:T(8,128)S(1)} %get-tuple-element.20), channel_id=1, source_target_pairs={{0,1},{1,2},{2,3},{3,4},{4,5},{5,6},{6,7},{7,8},{8,9},{9,10},{10,1... | collective-permute-start | bytes 1376264 | tf_op jit(solution)/shard_map/ppermute | solution.py:27
  10.7 114.4 %collective-permute-start.10 = (bf16[512,1024]{1,0:T(8,128)(2,1)}, bf16[512,1024]{1,0:T(8,128)(2,1)}, u32[]{:S(2)}, u32[]{:S(2)}) collective-permute-start(bf16[512,1024]{1,0:T(8,128)(2,1)} %param.10), channel_id=1, source_target_pairs={{0,2},{1,3},{2,0},{3,1},{4,6},{5,7},{6,4},{7,5},{8,10},{9,11},{10,... | collective-permute-start | bytes 3145736 | tf_op jit(solution)/shard_map/ppermute | solution.py:40
  13.3 111.8 %collective-permute-start.11 = (bf16[512,1024]{1,0:T(8,128)(2,1)}, bf16[512,1024]{1,0:T(8,128)(2,1)}, u32[]{:S(2)}, u32[]{:S(2)}) collective-permute-start(bf16[512,1024]{1,0:T(8,128)(2,1)} %param.10), channel_id=1, source_target_pairs={{0,4},{1,5},{2,6},{3,7},{4,0},{5,1},{6,2},{7,3},{8,12},{9,13},{10,... | collective-permute-start | bytes 3145736 | tf_op jit(solution)/shard_map/ppermute | solution.py:40
  14.8 110.3 %collective-permute-start.12 = (bf16[512,1024]{1,0:T(8,128)(2,1)}, bf16[512,1024]{1,0:T(8,128)(2,1)}, u32[]{:S(2)}, u32[]{:S(2)}) collective-permute-start(bf16[512,1024]{1,0:T(8,128)(2,1)} %param.10), channel_id=1, source_target_pairs={{0,8},{1,9},{2,10},{3,11},{4,12},{5,13},{6,14},{7,15},{8,0},{9,1},... | collective-permute-start | bytes 3145736 | tf_op jit(solution)/shard_map/ppermute | solution.py:40
  17.4 3.8 %collective-permute-start.1 = (f32[4,64,448]{2,1,0:T(8,128)S(1)}, f32[4,64,448]{2,1,0:T(8,128)S(1)}, u32[]{:S(2)}, u32[]{:S(2)}) collective-permute-start(f32[4,64,448]{2,1,0:T(8,128)S(1)} %get-tuple-element.19), channel_id=1, source_target_pairs={{1,0},{2,1},{3,2},{4,3},{5,4},{6,5},{7,6},{8,7},{9,8},{10,9},{11,1... | collective-permute-start | bytes 1376264 | tf_op jit(solution)/shard_map/ppermute | solution.py:27
  21.7 1.8 copy-start.17
  21.7 1.8 copy-start.20
  23.6 1.9 copy-start.25
  24.3 27.6 %copy-start.35 = (s32[8,4]{0,1:T(4,128)S(1)}, s32[8,4]{0,1:T(4,128)}, u32[]{:S(2)}) copy-start(s32[8,4]{0,1:T(4,128)} %param.15) | copy-start | bytes 388
  27.1 26.2 %collective-permute-start.2 = (f32[4,64,256]{2,1,0:T(8,128)}, f32[4,64,256]{2,1,0:T(8,128)}, u32[]{:S(2)}, u32[]{:S(2)}) collective-permute-start(f32[4,64,256]{2,1,0:T(8,128)} %get-tuple-element.26), channel_id=1, source_target_pairs={{0,1},{1,2},{2,3},{3,4},{4,5},{5,6},{6,7},{7,8},{8,9},{9,10},{10,1... | collective-permute-start | bytes 786440 | tf_op jit(solution)/shard_map/ppermute | solution.py:27
  51.9 3.6 %collective-permute-start.3 = (f32[4,64,256]{2,1,0:T(8,128)}, f32[4,64,256]{2,1,0:T(8,128)S(1)}, u32[]{:S(2)}, u32[]{:S(2)}) collective-permute-start(f32[4,64,256]{2,1,0:T(8,128)} %get-tuple-element.25), channel_id=1, source_target_pairs={{1,0},{2,1},{3,2},{4,3},{5,4},{6,5},{7,6},{8,7},{9,8},{10,9},{11,1... | collective-permute-start | bytes 786440 | tf_op jit(solution)/shard_map/ppermute | solution.py:27
  55.3 1.4 copy-start.6
  56.7 1.3 copy-start.3
  56.8 1.3 copy-start.18
  56.8 1.2 copy-start.21
  56.8 1.3 copy-start.26
  59.1 2.0 copy-start.27
  59.8 33.0 %copy-start.36 = (s32[8,3]{0,1:T(4,128)S(1)}, s32[8,3]{0,1:T(4,128)}, u32[]{:S(2)}) copy-start(s32[8,3]{0,1:T(4,128)} %param.14) | copy-start | bytes 292
  62.7 31.5 %collective-permute-start.4 = (f32[4,64,256]{2,1,0:T(8,128)}, f32[4,64,256]{2,1,0:T(8,128)}, u32[]{:S(2)}, u32[]{:S(2)}) collective-permute-start(f32[4,64,256]{2,1,0:T(8,128)} %get-tuple-element.24), channel_id=1, source_target_pairs={{0,1},{1,2},{2,3},{3,4},{4,5},{5,6},{6,7},{7,8},{8,9},{9,10},{10,1... | collective-permute-start | bytes 786440 | tf_op jit(solution)/shard_map/ppermute | solution.py:27
  92.9 3.6 %collective-permute-start.5 = (f32[4,64,256]{2,1,0:T(8,128)}, f32[4,64,256]{2,1,0:T(8,128)S(1)}, u32[]{:S(2)}, u32[]{:S(2)}) collective-permute-start(f32[4,64,256]{2,1,0:T(8,128)} %get-tuple-element.23), channel_id=1, source_target_pairs={{1,0},{2,1},{3,2},{4,3},{5,4},{6,5},{7,6},{8,7},{9,8},{10,9},{11,1... | collective-permute-start | bytes 786440 | tf_op jit(solution)/shard_map/ppermute | solution.py:27
  96.1 1.5 copy-start.9
  97.7 1.3 copy-start.4
  97.7 1.3 copy-start.19
  97.7 1.2 copy-start.22
  97.7 1.3 copy-start.28
  100.2 9.7 %copy-start.34 = (f32[9]{0:T(128)S(1)}, f32[9]{0:T(128)}, u32[]{:S(2)}) copy-start(f32[9]{0:T(128)} %param.16) | copy-start | bytes 112
  100.2 10.4 %copy-start.33 = (bf16[128,1024]{1,0:T(8,128)(2,1)S(1)}, bf16[128,1024]{1,0:T(8,128)(2,1)}, u32[]{:S(2)}) copy-start(bf16[128,1024]{1,0:T(8,128)(2,1)} %get-tuple-element.18) | copy-start | bytes 786436
  100.2 13.5 %copy-start.32 = (bf16[128,1024]{1,0:T(8,128)(2,1)S(1)}, bf16[128,1024]{1,0:T(8,128)(2,1)}, u32[]{:S(2)}) copy-start(bf16[128,1024]{1,0:T(8,128)(2,1)} %get-tuple-element.17) | copy-start | bytes 786436
  101.6 9.1 %collective-permute-start.6 = (f32[4,64,256]{2,1,0:T(8,128)S(1)}, f32[4,64,256]{2,1,0:T(8,128)S(1)}, u32[]{:S(2)}, u32[]{:S(2)}) collective-permute-start(f32[4,64,256]{2,1,0:T(8,128)S(1)} %get-tuple-element.22), channel_id=1, source_target_pairs={{0,1},{1,2},{2,3},{3,4},{4,5},{5,6},{6,7},{7,8},{8,9},{9,10},{10,1... | collective-permute-start | bytes 786440 | tf_op jit(solution)/shard_map/ppermute | solution.py:27
  108.0 5.8 %collective-permute-start.7 = (f32[4,64,256]{2,1,0:T(8,128)S(1)}, f32[4,64,256]{2,1,0:T(8,128)S(1)}, u32[]{:S(2)}, u32[]{:S(2)}) collective-permute-start(f32[4,64,256]{2,1,0:T(8,128)S(1)} %get-tuple-element.21), channel_id=1, source_target_pairs={{1,0},{2,1},{3,2},{4,3},{5,4},{6,5},{7,6},{8,7},{9,8},{10,9},{11,1... | collective-permute-start | bytes 786440 | tf_op jit(solution)/shard_map/ppermute | solution.py:27
  110.6 14.4 %collective-permute-start.8 = (bf16[128,1024]{1,0:T(8,128)(2,1)S(1)}, bf16[128,1024]{1,0:T(8,128)(2,1)S(1)}, u32[]{:S(2)}, u32[]{:S(2)}) collective-permute-start(bf16[128,1024]{1,0:T(8,128)(2,1)S(1)} %copy-done.33), channel_id=1, source_target_pairs={{0,1},{1,2},{2,3},{3,4},{4,5},{5,6},{6,7},{7,8},{8,9},{9,10},{10,1... | collective-permute-start | bytes 786440 | tf_op jit(solution)/shard_map/ppermute | solution.py:27
  113.8 11.3 %collective-permute-start.9 = (bf16[128,1024]{1,0:T(8,128)(2,1)S(1)}, bf16[128,1024]{1,0:T(8,128)(2,1)S(1)}, u32[]{:S(2)}, u32[]{:S(2)}) collective-permute-start(bf16[128,1024]{1,0:T(8,128)(2,1)S(1)} %copy-done.32), channel_id=1, source_target_pairs={{1,0},{2,1},{3,2},{4,3},{5,4},{6,5},{7,6},{8,7},{9,8},{10,9},{11,1... | collective-permute-start | bytes 786440 | tf_op jit(solution)/shard_map/ppermute | solution.py:27
  116.8 1.2 copy-start.15
  118.1 17.8 %copy-start.23 = (bf16[128,1024]{1,0:T(8,128)(2,1)S(1)}, bf16[128,1024]{1,0:T(8,128)(2,1)}, u32[]{:S(2)}) copy-start(bf16[128,1024]{1,0:T(8,128)(2,1)} %param.17) | copy-start | bytes 786436
  125.0 16.6 %copy-start.30 = (bf16[128,1024]{1,0:T(8,128)(2,1)}, bf16[128,1024]{1,0:T(8,128)(2,1)S(1)}, u32[]{:S(2)}) copy-start(bf16[128,1024]{1,0:T(8,128)(2,1)S(1)} %collective-permute-done.8) | copy-start | bytes 786436
  125.1 16.6 %copy-start.31 = (bf16[128,1024]{1,0:T(8,128)(2,1)}, bf16[128,1024]{1,0:T(8,128)(2,1)S(1)}, u32[]{:S(2)}) copy-start(bf16[128,1024]{1,0:T(8,128)(2,1)S(1)} %collective-permute-done.9) | copy-start | bytes 786436
  125.8 36.3 %collective-permute-start.16 = (bf16[512,128]{1,0:T(8,128)(2,1)S(1)}, bf16[512,128]{1,0:T(8,128)(2,1)}, u32[]{:S(2)}, u32[]{:S(2)}) collective-permute-start(bf16[512,128]{1,0:T(8,128)(2,1)S(1)} %bitcast.228), channel_id=1, source_target_pairs={{0,2},{1,3},{2,0},{3,1},{4,6},{5,7},{6,4},{7,5},{8,10},{9,11},{10,... | collective-permute-start | bytes 393224 | tf_op jit(solution)/shard_map/ppermute | solution.py:40
  130.9 37.8 %collective-permute-start.17 = (bf16[512,128]{1,0:T(8,128)(2,1)S(1)}, bf16[512,128]{1,0:T(8,128)(2,1)}, u32[]{:S(2)}, u32[]{:S(2)}) collective-permute-start(bf16[512,128]{1,0:T(8,128)(2,1)S(1)} %bitcast.229), channel_id=1, source_target_pairs={{0,4},{1,5},{2,6},{3,7},{4,0},{5,1},{6,2},{7,3},{8,12},{9,13},{10,... | collective-permute-start | bytes 393224 | tf_op jit(solution)/shard_map/ppermute | solution.py:40
  134.1 41.1 %collective-permute-start.18 = (bf16[512,128]{1,0:T(8,128)(2,1)S(1)}, bf16[512,128]{1,0:T(8,128)(2,1)}, u32[]{:S(2)}, u32[]{:S(2)}) collective-permute-start(bf16[512,128]{1,0:T(8,128)(2,1)S(1)} %bitcast.230), channel_id=1, source_target_pairs={{0,8},{1,9},{2,10},{3,11},{4,12},{5,13},{6,14},{7,15},{8,0},{9,1},... | collective-permute-start | bytes 393224 | tf_op jit(solution)/shard_map/ppermute | solution.py:40
  137.5 1.3 copy-start.29
  137.5 9.3 %collective-permute-start.14 = (bf16[128,128]{1,0:T(8,128)(2,1)}, bf16[128,128]{1,0:T(8,128)(2,1)}, u32[]{:S(2)}, u32[]{:S(2)}) collective-permute-start(bf16[128,128]{1,0:T(8,128)(2,1)} %get-tuple-element.28), channel_id=1, source_target_pairs={{1,0},{2,1},{3,2},{4,3},{5,4},{6,5},{7,6},{8,7},{9,8},{10,9},{11,1... | collective-permute-start | bytes 98312 | tf_op jit(solution)/shard_map/ppermute | solution.py:27
  142.0 4.9 %copy-start.24 = (bf16[128,1024]{1,0:T(8,128)(2,1)S(1)}, bf16[128,1024]{1,0:T(8,128)(2,1)}, u32[]{:S(2)}) copy-start(bf16[128,1024]{1,0:T(8,128)(2,1)} %param.17) | copy-start | bytes 786436
  143.8 4.2 %collective-permute-start.13 = (bf16[128,128]{1,0:T(8,128)(2,1)}, bf16[128,128]{1,0:T(8,128)(2,1)S(1)}, u32[]{:S(2)}, u32[]{:S(2)}) collective-permute-start(bf16[128,128]{1,0:T(8,128)(2,1)} %get-tuple-element.27), channel_id=1, source_target_pairs={{0,1},{1,2},{2,3},{3,4},{4,5},{5,6},{6,7},{7,8},{8,9},{9,10},{10,1... | collective-permute-start | bytes 98312 | tf_op jit(solution)/shard_map/ppermute | solution.py:27
  155.2 2.5 %copy-start.1 = (bf16[768,2048]{1,0:T(8,128)(2,1)}, bf16[768,2048]{1,0:T(8,128)(2,1)S(1)}, u32[]{:S(2)}) copy-start(bf16[768,2048]{1,0:T(8,128)(2,1)S(1)} %convolution_convert_fusion.refs_0_.refs_1_.refs_2_.refs_3_) | copy-start | bytes 9437188
  155.2 4.2 %copy-start.16 = (bf16[8,64,8,128]{1,3,2,0:T(8,128)(2,1)S(1)}, bf16[8,64,8,128]{1,3,2,0:T(8,128)(2,1)}, u32[]{:S(2)}) copy-start(bf16[8,64,8,128]{1,3,2,0:T(8,128)(2,1)} %copy.51) | copy-start | bytes 3145732
  157.7 24.0 %collective-permute-start.15 = (bf16[512,2048]{1,0:T(8,128)(2,1)}, bf16[512,2048]{1,0:T(8,128)(2,1)}, u32[]{:S(2)}, u32[]{:S(2)}) collective-permute-start(bf16[512,2048]{1,0:T(8,128)(2,1)} %slice.369), channel_id=1, source_target_pairs={{0,1},{1,0},{2,3},{3,2},{4,5},{5,4},{6,7},{7,6},{8,9},{9,8},{10,11... | collective-permute-start | bytes 6291464 | tf_op jit(solution)/shard_map/ppermute | solution.py:40
  (8 other events, 7.3 us)

commit v8 on v7

--- a/solution.py
+++ b/solution.py
@@ -15,7 +15,7 @@
 NEXP = 4
 REACH = 2
 NKEY = 1 + 3 + NEXP
-PER_EXCHANGE = 2
+PER_EXCHANGE = 4
 
 
 def shift_rows(x, axis, step):
@@ -50,7 +50,7 @@
     return result.reshape(field.shape)
 
 
-def chebyshev(struct_feats, op_blocks, laplace_index, series_coef, first_block):
+def chebyshev(struct_feats, op_blocks, laplace_index, series_coef, first_block, riders):
     count = op_blocks.shape[0]
     chans = struct_feats.shape[1]
     taps = 2 * REACH + 1
@@ -64,6 +64,7 @@
     payload = jnp.concatenate([own_field, bands], axis=2)
     left = shift_rows(payload[count - halo :], "seq", 1)
     right = shift_rows(payload[:halo], "seq", -1)
+    left, right, riders = lax.optimization_barrier((left, right, riders))
     edge = halo - REACH
     bands = jnp.concatenate(
         [left[halo - edge :, :, chans:], bands, right[:edge, :, chans:]], axis=0
@@ -109,7 +110,7 @@
         encoding = encoding + series_coef[degree] * nxt[own.start - lo : own.stop - lo]
         prev, prev_base = cur, cur_base
         cur, cur_base = nxt, lo
-    return encoding.reshape(count * BS, chans), {0: payload, 1: left, -1: right}
+    return encoding.reshape(count * BS, chans), riders
 
 
 def attention_kernel(table_ref, q_ref, *refs):
@@ -185,14 +186,14 @@
     levels = lax.axis_size("seq").bit_length() - 1
     bits = [link * (levels - 1) // (NEXP - 1) for link in range(NEXP)]
 
-    encoding, parts = chebyshev(struct_feats, op_blocks, laplace_index, series_coef, first_block)
-    held = node_feats
-    feats_before = shift_rows(held[rows - rim:], "seq", 1)
-    feats_after = shift_rows(held[:rim], "seq", -1)
+    feats_before = shift_rows(node_feats[rows - rim:], "seq", 1)
+    feats_after = shift_rows(node_feats[:rim], "seq", -1)
+    encoding, (feats_before, feats_after, held) = chebyshev(
+        struct_feats, op_blocks, laplace_index, series_coef, first_block,
+        (feats_before, feats_after, node_feats),
+    )
     feats_far = [partner(held, "seq", bit) for bit in bits[1:]]
-    encoding, feats_before, feats_after, feats_far = lax.optimization_barrier(
-        (encoding, feats_before, feats_after, feats_far)
-    )
+    encoding, feats_far = lax.optimization_barrier((encoding, feats_far))
     encoding_b = encoding.astype(jnp.bfloat16)
 
     enc_before = shift_rows(encoding_b[rows - rim:], "seq", 1)
@@ -208,24 +209,25 @@
     queries = jnp.dot(blended, qkv_weight[:, :D], preferred_element_type=jnp.float32).astype(
         jnp.bfloat16
     )
-    near_blended = jnp.concatenate(
-        [blend(feats_before, enc_before), blended, blend(feats_after, enc_after)], axis=0
-    )
-    kv_near = jnp.dot(near_blended, kv_weight, preferred_element_type=jnp.float32).astype(
+    all_blended = jnp.concatenate(
+        [blend(feats_before, enc_before), blended, blend(feats_after, enc_after)]
+        + [blend(f, e) for f, e in zip(feats_far, enc_far)],
+        axis=0,
+    )
+    kv_all = jnp.dot(all_blended, kv_weight, preferred_element_type=jnp.float32).astype(
         jnp.bfloat16
     )
-    kv_own = kv_near[rim : rim + rows]
-    kv_far = [partner(kv_own, "seq", bits[0])] + [
-        jnp.dot(blend(f, e), kv_weight, preferred_element_type=jnp.float32).astype(jnp.bfloat16)
-        for f, e in zip(feats_far, enc_far)
-    ]
+    kv_own = kv_all[rim : rim + rows]
+    kv_chip = partner(kv_own, "seq", bits[0])
 
     near_blocks = count + 2 * REACH
     own_slot = jnp.arange(count, dtype=jnp.int32)[:, None] + REACH
     graph_slot = jnp.clip(graph_links - first_block + REACH, 0, near_blocks - 1)
     far_slot = jnp.clip(expander_slot, 0, count - 1)
-    table = jnp.concatenate([own_slot, graph_slot, far_slot], axis=1).astype(jnp.int32)
-    sources = [kv_near] * 4 + kv_far
+    far_base = jnp.asarray([0] + [near_blocks + k * count for k in range(NEXP - 1)], jnp.int32)
+    table = jnp.concatenate([own_slot, graph_slot, far_slot + far_base[None, :]], axis=1)
+    table = table.astype(jnp.int32)
+    sources = [kv_all] * 4 + [kv_chip] + [kv_all] * (NEXP - 1)
     attended = attend(queries, sources, table)
     return jnp.dot(attended, out_weight, preferred_element_type=jnp.float32).astype(jnp.bfloat16)
 

time: 202 us -> 169 us (0.84)
  starting transfers between devices: 96 us -> 47.9 us
  waiting for transfers between devices: 1.29 us -> 44.3 us
  matrix products: 50.3 us -> 34.1 us
  local copies, waits for them, and re-layouts: 22.4 us -> 16.2 us
  other arithmetic: 13.9 us -> 10.4 us
    ppermute x12 -> x8, starting transfers between devices: 77.6 us -> 36.5 us  [shift_rows(): return lax.ppermute(x, axis, pairs)]
    ppermute x7, waiting for transfers between devices: 0.02 us -> 39.3 us  [partner(): return lax.ppermute(value, axis, pairs)]
    dot_general x4 -> x1, matrix products: 25.4 us -> 10.3 us  [on_device(): jnp.dot(all_blended, kv_weight, preferred_element_type=jnp.float32)]
    ppermute x7, starting transfers between devices: 18.4 us -> 11.4 us  [partner(): return lax.ppermute(value, axis, pairs)]
    ppermute x12 -> x8, waiting for transfers between devices: 1.27 us -> 4.96 us  [shift_rows(): return lax.ppermute(x, axis, pairs)]
    slice x3, local copies, waits for them, and re-layouts: 4.01 us -> 1.51 us  [the longest x1 1.47 us: on_device(): kv_own = kv_all[rim:rim + rows]]
    select_n x1, other arithmetic: 2.76 us -> 5.05 us  [split_queries(): return jnp.where(d_head == j_head, qt * scale, jnp.zeros_like(qt))]
    unnamed x106 -> x60, local copies, waits for them, and re-layouts: 7.46 us -> 6.79 us
  transfers between devices with their start and end apart: 19 -> 15, of which waited for: 3 -> 5; matrix products, arithmetic and copies ran while one was open for 34% -> 15% of each run, Pallas kernels for 0% -> 0%
where the time goes in v8:
time: 169 us
  starting transfers between devices  47.9 us (28%)
  waiting for transfers between devices  44.3 us (26%)
  matrix products  34.1 us (20%)
  local copies, waits for them, and re-layouts  16.2 us (10%)
  Pallas kernels  14.8 us (9%)
  other arithmetic  10.4 us (6%)
    ppermute x7, waiting for transfers between devices, partner(): return lax.ppermute(value, axis, pairs)  39.3 us
    ppermute x8, starting transfers between devices, shift_rows(): return lax.ppermute(x, axis, pairs)  36.5 us
    dot_general x8, matrix products, step(): jnp.einsum('wsk,wkc->wsc', bands[lo - REACH:hi - REACH], stacked, precisi...  15.4 us
    pallas_call x1, Pallas kernels, attend(): pl.pallas_call(attention_kernel, grid_spec=grid_spec, out_shape=jax.Shape...  14.8 us
    ppermute x7, starting transfers between devices, partner(): return lax.ppermute(value, axis, pairs)  11.4 us
    dot_general x1, matrix products, on_device(): jnp.dot(all_blended, kv_weight, preferred_element_type=jnp.float32)  10.3 us
    unnamed x60, local copies, waits for them, and re-layouts  6.79 us
    select_n x1, other arithmetic, split_queries(): return jnp.where(d_head == j_head, qt * scale, jnp.zeros_like(qt))  5.05 us
  transfers between devices with their start and end apart: 15, of which 5 were waited for; matrix products, arithmetic and copies ran while one was open for 15% of the time, Pallas kernels for 0%

profile of v8, /device:TPU:0, one launch (start us, length us, event | category | flops | bytes accessed | tf_op | source)
XLA Modules:
  0.0 168.6 jit_solution(6601339357142674538)
XLA Ops:
  0.0 0.9 copy.34
  1.1 2.8 %select_reduce_fusion = f32[8,5,64,64]{3,2,1,0:T(8,128)} fusion(f32[8,3,64,64]{3,2,1,0:T(8,128)} %param.13, pred[8,3,5]{2,1,0:T(4,128)(4,1)S(1)} %iota_compare_fusion), kind=kLoop, calls=%fused_computation.2 | loop fusion | flops 819200 | bytes 1048696 | tf_op jit(solution)/shard_map/reduce_sum | solution.py:61
  3.9 1.7 %copy.35 = f32[8,64,5,64]{1,3,2,0:T(8,128)S(1)} copy(f32[8,64,5,64]{3,1,2,0:T(8,128)} %bitcast.214) | data formatting | bytes 1310720 | tf_op jit(solution)/shard_map/transpose | solution.py:62
  5.6 1.3 copy.36
  7.0 1.4 pad_maximum_fusion.1
  8.4 2.6 %collective-permute-start = (f32[8,64,448]{2,1,0:T(8,128)S(1)}, f32[8,64,448]{2,1,0:T(8,128)S(1)}, u32[]{:S(2)}, u32[]{:S(2)}) collective-permute-start(f32[8,64,448]{2,1,0:T(8,128)S(1)} %pad_maximum_fusion.1), channel_id=1, source_target_pairs={{0,1},{1,2},{2,3},{3,4},{4,5},{5,6},{6,7},{7,8},{8,9},{9,10},{10,1... | collective-permute-start | bytes 2752520 | tf_op jit(solution)/shard_map/ppermute | solution.py:27
  10.9 1.3 collective-permute-start.1
  12.3 5.1 %collective-permute-start.2 = (bf16[128,1024]{1,0:T(8,128)(2,1)S(1)}, bf16[128,1024]{1,0:T(8,128)(2,1)S(1)}, u32[]{:S(2)}, u32[]{:S(2)}) collective-permute-start(bf16[128,1024]{1,0:T(8,128)(2,1)S(1)} %get-tuple-element.24), channel_id=1, source_target_pairs={{0,1},{1,2},{2,3},{3,4},{4,5},{5,6},{6,7},{7,8},{8,9},{9,10},{10,1... | collective-permute-start | bytes 786440 | tf_op jit(solution)/shard_map/ppermute | solution.py:27
  17.4 1.3 collective-permute-start.3
  18.7 3.3 %collective-permute-done.3 = bf16[128,1024]{1,0:T(8,128)(2,1)S(1)} collective-permute-done((bf16[128,1024]{1,0:T(8,128)(2,1)S(1)}, bf16[128,1024]{1,0:T(8,128)(2,1)S(1)}, u32[]{:S(2)}, u32[]{:S(2)}) %collective-permute-start.3) | collective-permute-done | bytes 262176 | tf_op jit(solution)/shard_map/ppermute | solution.py:27
  22.6 0.4 copy.38
  23.0 0.7 copy-done.2
  23.7 1.3 fusion.66
  25.3 0.3 copy.39
  25.6 1.2 fusion.15
  27.3 0.8 fusion.10
  28.5 1.3 fusion.12
  29.8 22.0 %collective-permute-start.4 = (f32[8,64,256]{2,1,0:T(8,128)S(1)}, f32[8,64,256]{2,1,0:T(8,128)S(1)}, u32[]{:S(2)}, u32[]{:S(2)}) collective-permute-start(f32[8,64,256]{2,1,0:T(8,128)S(1)} %pad_maximum_fusion.4), channel_id=1, source_target_pairs={{0,1},{1,2},{2,3},{3,4},{4,5},{5,6},{6,7},{7,8},{8,9},{9,10},{10,1... | collective-permute-start | bytes 1572872 | tf_op jit(solution)/shard_map/ppermute | solution.py:27
  51.7 1.5 collective-permute-start.5
  53.2 0.7 fusion.69
  53.9 4.7 %collective-permute-start.6 = (bf16[512,1024]{1,0:T(8,128)(2,1)S(1)}, bf16[512,1024]{1,0:T(8,128)(2,1)S(1)}, u32[]{:S(2)}, u32[]{:S(2)}) collective-permute-start(bf16[512,1024]{1,0:T(8,128)(2,1)S(1)} %copy-done.4), channel_id=1, source_target_pairs={{0,2},{1,3},{2,0},{3,1},{4,6},{5,7},{6,4},{7,5},{8,10},{9,11},{10,... | collective-permute-start | bytes 3145736 | tf_op jit(solution)/shard_map/ppermute | solution.py:40
  58.6 1.6 collective-permute-start.7
  60.2 1.7 %collective-permute-start.8 = (bf16[512,1024]{1,0:T(8,128)(2,1)S(1)}, bf16[512,1024]{1,0:T(8,128)(2,1)S(1)}, u32[]{:S(2)}, u32[]{:S(2)}) collective-permute-start(bf16[512,1024]{1,0:T(8,128)(2,1)S(1)} %copy-done.4), channel_id=1, source_target_pairs={{0,8},{1,9},{2,10},{3,11},{4,12},{5,13},{6,14},{7,15},{8,0},{9,1},... | collective-permute-start | bytes 3145736 | tf_op jit(solution)/shard_map/ppermute | solution.py:40
  62.6 1.3 maximum_subtract_fusion
  64.4 1.3 slice_subtract_fusion
  66.1 0.9 slice_subtract_fusion.1
  67.3 7.2 %fusion.14 = bf16[8,64,128]{2,1,0:T(8,128)(2,1)S(1)} fusion(f32[8,64,320]{1,2,0:T(8,128)S(1)} %bitcast.210, f32[8,320,128]{2,1,0:T(8,128)S(1)} %bitcast.216, f32[20,64,128]{2,1,0:T(8,128)S(1)} %maximum_subtract_fusion, f32[20,64,128]{2,1,0:T(8,128)S(1)} %fusion.66, f32[16,64,128]{2,1,0:T(8,128)S(1)} %slice_subtract_fusion, f32[8,64,128]{2,1,0:T(8,128)S(1)} %fusion.12, ...), kind=kOutput, calls=%fused_computation.26 | convolution fusion | flops 127139840 | bytes 4194340 | tf_op jit(solution)/shard_map/wsk,wkc->wsc/dot_general | solution.py:79
  74.5 12.8 %collective-permute-done.6 = bf16[512,1024]{1,0:T(8,128)(2,1)S(1)} collective-permute-done((bf16[512,1024]{1,0:T(8,128)(2,1)S(1)}, bf16[512,1024]{1,0:T(8,128)(2,1)S(1)}, u32[]{:S(2)}, u32[]{:S(2)}) %collective-permute-start.6) | collective-permute-done | bytes 1048608 | tf_op jit(solution)/shard_map/ppermute | solution.py:40
  87.3 21.6 %collective-permute-done.7 = bf16[512,1024]{1,0:T(8,128)(2,1)S(1)} collective-permute-done((bf16[512,1024]{1,0:T(8,128)(2,1)S(1)}, bf16[512,1024]{1,0:T(8,128)(2,1)S(1)}, u32[]{:S(2)}, u32[]{:S(2)}) %collective-permute-start.7) | collective-permute-done | bytes 1048608 | tf_op jit(solution)/shard_map/ppermute | solution.py:40
  108.9 1.3 collective-permute-start.9
  110.2 0.3 collective-permute-start.11
  110.5 3.1 %collective-permute-start.12 = (bf16[512,128]{1,0:T(8,128)(2,1)S(1)}, bf16[512,128]{1,0:T(8,128)(2,1)S(1)}, u32[]{:S(2)}, u32[]{:S(2)}) collective-permute-start(bf16[512,128]{1,0:T(8,128)(2,1)S(1)} %bitcast.227), channel_id=1, source_target_pairs={{0,4},{1,5},{2,6},{3,7},{4,0},{5,1},{6,2},{7,3},{8,12},{9,13},{10,... | collective-permute-start | bytes 393224 | tf_op jit(solution)/shard_map/ppermute | solution.py:40
  113.6 1.5 collective-permute-start.10
  115.3 0.4 constant_dynamic-update-slice_fusion
  115.8 1.6 collective-permute-done.10
  117.6 0.4 fusion.16
  118.0 0.4 fusion.17
  118.5 4.9 %collective-permute-done.13 = bf16[512,128]{1,0:T(8,128)(2,1)S(1)} collective-permute-done((bf16[512,128]{1,0:T(8,128)(2,1)S(1)}, bf16[512,128]{1,0:T(8,128)(2,1)S(1)}, u32[]{:S(2)}, u32[]{:S(2)}) %collective-permute-start.13) | collective-permute-done | bytes 131104 | tf_op jit(solution)/shard_map/ppermute | solution.py:40
  123.3 0.4 fusion.18
  123.8 10.3 %convolution_convert_fusion.refs_0_.refs_1_.refs_2_.refs_3_.refs_5_.refs_6_.refs_7_ = bf16[2304,2048]{1,0:T(8,128)(2,1)S(1)} fusion(bf16[2304,1024]{1,0:T(8,128)(2,1)S(1)} %fusion.18, bf16[1024,3072]{1,0:T(8,128)(2,1)S(1)} %bitcast.231), kind=kOutput, calls=%fused_computation | convolution fusion | flops 9668395008 | bytes 18350080 | tf_op jit(solution)/shard_map/dot_general | solution.py:217
  134.1 3.6 %copy-done.1 = bf16[2304,2048]{1,0:T(8,128)(2,1)} copy-done((bf16[2304,2048]{1,0:T(8,128)(2,1)}, bf16[2304,2048]{1,0:T(8,128)(2,1)S(1)}, u32[]{:S(2)}) %copy-start.1) | copy-done | bytes 9437208
  137.8 1.5 slice.357
  139.6 0.7 pad_add_fusion.table_ref
  140.4 2.8 %fusion.7 = bf16[64,8,8,128]{3,1,2,0:T(8,128)(2,1)S(1)} fusion(bf16[512,1024]{1,0:T(8,128)(2,1)S(1)} %get-tuple-element.37, bf16[1024,3072]{1,0:T(8,128)(2,1)} %param.19), kind=kOutput, calls=%fused_computation.14 | convolution fusion | flops 1074266112 | bytes 4194304 | tf_op jit(solution)/shard_map/dot_general | solution.py:209
  143.5 1.8 %copy.48 = bf16[8,64,8,128]{1,3,2,0:T(8,128)(2,1)} copy(bf16[8,64,8,128]{3,2,1,0:T(8,128)(2,1)S(1)} %bitcast.217) | data formatting | bytes 2097152 | tf_op jit(solution)/shard_map/reshape | solution.py:141
  145.3 5.0 %fusion.1.q_ref = bf16[8,8,128,128]{3,2,1,0:T(8,128)(2,1)} fusion(bf16[8,8,128,64]{3,2,1,0:T(8,128)(2,1)} %bitcast.213, pred[128,128]{1,0:T(8,128)(4,1)S(1)} %select_compare_fusion), kind=kLoop, calls=%fused_computation.4 | loop fusion | flops 7340032 | bytes 3162112 | tf_op jit(solution)/shard_map/jit(_where)/select_n | solution.py:146
  150.4 14.8 %shard_map.109 = bf16[512,1024]{1,0:T(8,128)(2,1)} custom-call(s32[8,8]{1,0:T(8,128)} %pad_add_fusion.table_ref, bf16[8,8,128,128]{3,2,1,0:T(8,128)(2,1)} %fusion.1.q_ref, bf16[2304,2048]{1,0:T(8,128)(2,1)} %copy-done.1, bf16[2304,2048]{1,0:T(8,128)(2,1)} %copy-done.1, bf16[2304,2048]{1,0:T(8,128)(2,1)} %copy-done.1, bf16[2304,2048]{1,0:T(8,128)(2,1)} %copy-done.1, ...), custom_call_target="tpu_custom_call" | custom-call | tf_op jit(solution)/shard_map/pallas_call | solution.py:163
  165.1 3.4 %convolution_convert_fusion.1 = bf16[512,1024]{1,0:T(8,128)(2,1)} fusion(bf16[512,1024]{1,0:T(8,128)(2,1)} %shard_map.109, bf16[1024,1024]{1,0:T(8,128)(2,1)S(1)} %copy-done), kind=kOutput, calls=%fused_computation.13 | convolution fusion | flops 1074266112 | bytes 4194304 | tf_op jit(solution)/shard_map/dot_general | solution.py:232
  (109 shorter events, 4.3 us)
Async XLA Ops:
  0.0 165.1 %copy-start = (bf16[1024,1024]{1,0:T(8,128)(2,1)S(1)}, bf16[1024,1024]{1,0:T(8,128)(2,1)}, u32[]{:S(2)}) copy-start(bf16[1024,1024]{1,0:T(8,128)(2,1)} %param.20) | copy-start | bytes 6291460
  7.0 5.3 %copy-start.4 = (bf16[512,1024]{1,0:T(8,128)(2,1)S(1)}, bf16[512,1024]{1,0:T(8,128)(2,1)}, u32[]{:S(2)}) copy-start(bf16[512,1024]{1,0:T(8,128)(2,1)} %param.11) | copy-start | bytes 3145732
  8.4 13.9 %copy-start.5 = (f32[512,128]{1,0:T(8,128)S(1)}, f32[512,128]{1,0:T(8,128)}, u32[]{:S(2)}) copy-start(f32[512,128]{1,0:T(8,128)} %param.12) | copy-start | bytes 786436
  8.4 13.7 %collective-permute-start = (f32[8,64,448]{2,1,0:T(8,128)S(1)}, f32[8,64,448]{2,1,0:T(8,128)S(1)}, u32[]{:S(2)}, u32[]{:S(2)}) collective-permute-start(f32[8,64,448]{2,1,0:T(8,128)S(1)} %pad_maximum_fusion.1), channel_id=1, source_target_pairs={{0,1},{1,2},{2,3},{3,4},{4,5},{5,6},{6,7},{7,8},{8,9},{9,10},{10,1... | collective-permute-start | bytes 2752520 | tf_op jit(solution)/shard_map/ppermute | solution.py:27
  10.9 11.1 %collective-permute-start.1 = (f32[8,64,448]{2,1,0:T(8,128)S(1)}, f32[8,64,448]{2,1,0:T(8,128)S(1)}, u32[]{:S(2)}, u32[]{:S(2)}) collective-permute-start(f32[8,64,448]{2,1,0:T(8,128)S(1)} %pad_maximum_fusion.1), channel_id=1, source_target_pairs={{1,0},{2,1},{3,2},{4,3},{5,4},{6,5},{7,6},{8,7},{9,8},{10,9},{11,1... | collective-permute-start | bytes 2752520 | tf_op jit(solution)/shard_map/ppermute | solution.py:27
  12.3 6.4 %collective-permute-start.2 = (bf16[128,1024]{1,0:T(8,128)(2,1)S(1)}, bf16[128,1024]{1,0:T(8,128)(2,1)S(1)}, u32[]{:S(2)}, u32[]{:S(2)}) collective-permute-start(bf16[128,1024]{1,0:T(8,128)(2,1)S(1)} %get-tuple-element.24), channel_id=1, source_target_pairs={{0,1},{1,2},{2,3},{3,4},{4,5},{5,6},{6,7},{7,8},{8,9},{9,10},{10,1... | collective-permute-start | bytes 786440 | tf_op jit(solution)/shard_map/ppermute | solution.py:27
  17.4 4.7 %collective-permute-start.3 = (bf16[128,1024]{1,0:T(8,128)(2,1)S(1)}, bf16[128,1024]{1,0:T(8,128)(2,1)S(1)}, u32[]{:S(2)}, u32[]{:S(2)}) collective-permute-start(bf16[128,1024]{1,0:T(8,128)(2,1)S(1)} %get-tuple-element.23), channel_id=1, source_target_pairs={{1,0},{2,1},{3,2},{4,3},{5,4},{6,5},{7,6},{8,7},{9,8},{10,9},{11,1... | collective-permute-start | bytes 786440 | tf_op jit(solution)/shard_map/ppermute | solution.py:27
  22.6 1.1 copy-start.2
  28.4 24.8 %copy-start.6 = (f32[9]{0:T(128)S(1)}, f32[9]{0:T(128)}, u32[]{:S(2)}) copy-start(f32[9]{0:T(128)} %param.17) | copy-start | bytes 112
  29.8 32.1 %collective-permute-start.4 = (f32[8,64,256]{2,1,0:T(8,128)S(1)}, f32[8,64,256]{2,1,0:T(8,128)S(1)}, u32[]{:S(2)}, u32[]{:S(2)}) collective-permute-start(f32[8,64,256]{2,1,0:T(8,128)S(1)} %pad_maximum_fusion.4), channel_id=1, source_target_pairs={{0,1},{1,2},{2,3},{3,4},{4,5},{5,6},{6,7},{7,8},{8,9},{9,10},{10,1... | collective-permute-start | bytes 1572872 | tf_op jit(solution)/shard_map/ppermute | solution.py:27
  51.7 10.2 %collective-permute-start.5 = (f32[8,64,256]{2,1,0:T(8,128)S(1)}, f32[8,64,256]{2,1,0:T(8,128)S(1)}, u32[]{:S(2)}, u32[]{:S(2)}) collective-permute-start(f32[8,64,256]{2,1,0:T(8,128)S(1)} %pad_maximum_fusion.4), channel_id=1, source_target_pairs={{1,0},{2,1},{3,2},{4,3},{5,4},{6,5},{7,6},{8,7},{9,8},{10,9},{11,1... | collective-permute-start | bytes 1572872 | tf_op jit(solution)/shard_map/ppermute | solution.py:27
  53.9 33.4 %collective-permute-start.6 = (bf16[512,1024]{1,0:T(8,128)(2,1)S(1)}, bf16[512,1024]{1,0:T(8,128)(2,1)S(1)}, u32[]{:S(2)}, u32[]{:S(2)}) collective-permute-start(bf16[512,1024]{1,0:T(8,128)(2,1)S(1)} %copy-done.4), channel_id=1, source_target_pairs={{0,2},{1,3},{2,0},{3,1},{4,6},{5,7},{6,4},{7,5},{8,10},{9,11},{10,... | collective-permute-start | bytes 3145736 | tf_op jit(solution)/shard_map/ppermute | solution.py:40
  58.6 50.3 %collective-permute-start.7 = (bf16[512,1024]{1,0:T(8,128)(2,1)S(1)}, bf16[512,1024]{1,0:T(8,128)(2,1)S(1)}, u32[]{:S(2)}, u32[]{:S(2)}) collective-permute-start(bf16[512,1024]{1,0:T(8,128)(2,1)S(1)} %copy-done.4), channel_id=1, source_target_pairs={{0,4},{1,5},{2,6},{3,7},{4,0},{5,1},{6,2},{7,3},{8,12},{9,13},{10,... | collective-permute-start | bytes 3145736 | tf_op jit(solution)/shard_map/ppermute | solution.py:40
  60.2 48.7 %collective-permute-start.8 = (bf16[512,1024]{1,0:T(8,128)(2,1)S(1)}, bf16[512,1024]{1,0:T(8,128)(2,1)S(1)}, u32[]{:S(2)}, u32[]{:S(2)}) collective-permute-start(bf16[512,1024]{1,0:T(8,128)(2,1)S(1)} %copy-done.4), channel_id=1, source_target_pairs={{0,8},{1,9},{2,10},{3,11},{4,12},{5,13},{6,14},{7,15},{8,0},{9,1},... | collective-permute-start | bytes 3145736 | tf_op jit(solution)/shard_map/ppermute | solution.py:40
  67.2 47.9 %copy-start.3 = (bf16[128,1024]{1,0:T(8,128)(2,1)S(1)}, bf16[128,1024]{1,0:T(8,128)(2,1)}, u32[]{:S(2)}) copy-start(bf16[128,1024]{1,0:T(8,128)(2,1)} %param.18) | copy-start | bytes 786436
  67.2 56.5 %slice-start = ((s8[6291456]{0:T(1024)(128)(4,1)}), s8[4194304]{0:T(1024)(128)(4,1)S(1)}, s32[]{:S(2)}) async-start(s8[6291456]{0:T(1024)(128)(4,1)} %bitcast.230), calls=%async_computation | async-start | bytes 8388608
  108.9 6.2 %collective-permute-start.9 = (bf16[128,128]{1,0:T(8,128)(2,1)S(1)}, bf16[128,128]{1,0:T(8,128)(2,1)S(1)}, u32[]{:S(2)}, u32[]{:S(2)}) collective-permute-start(bf16[128,128]{1,0:T(8,128)(2,1)S(1)} %get-tuple-element.26), channel_id=1, source_target_pairs={{0,1},{1,2},{2,3},{3,4},{4,5},{5,6},{6,7},{7,8},{8,9},{9,10},{10,1... | collective-permute-start | bytes 98312 | tf_op jit(solution)/shard_map/ppermute | solution.py:27
  110.2 7.4 %collective-permute-start.11 = (bf16[512,128]{1,0:T(8,128)(2,1)S(1)}, bf16[512,128]{1,0:T(8,128)(2,1)S(1)}, u32[]{:S(2)}, u32[]{:S(2)}) collective-permute-start(bf16[512,128]{1,0:T(8,128)(2,1)S(1)} %bitcast.226), channel_id=1, source_target_pairs={{0,2},{1,3},{2,0},{3,1},{4,6},{5,7},{6,4},{7,5},{8,10},{9,11},{10,... | collective-permute-start | bytes 393224 | tf_op jit(solution)/shard_map/ppermute | solution.py:40
  110.5 7.5 %collective-permute-start.12 = (bf16[512,128]{1,0:T(8,128)(2,1)S(1)}, bf16[512,128]{1,0:T(8,128)(2,1)S(1)}, u32[]{:S(2)}, u32[]{:S(2)}) collective-permute-start(bf16[512,128]{1,0:T(8,128)(2,1)S(1)} %bitcast.227), channel_id=1, source_target_pairs={{0,4},{1,5},{2,6},{3,7},{4,0},{5,1},{6,2},{7,3},{8,12},{9,13},{10,... | collective-permute-start | bytes 393224 | tf_op jit(solution)/shard_map/ppermute | solution.py:40
  113.6 9.8 %collective-permute-start.13 = (bf16[512,128]{1,0:T(8,128)(2,1)S(1)}, bf16[512,128]{1,0:T(8,128)(2,1)S(1)}, u32[]{:S(2)}, u32[]{:S(2)}) collective-permute-start(bf16[512,128]{1,0:T(8,128)(2,1)S(1)} %bitcast.228), channel_id=1, source_target_pairs={{0,8},{1,9},{2,10},{3,11},{4,12},{5,13},{6,14},{7,15},{8,0},{9,1},... | collective-permute-start | bytes 393224 | tf_op jit(solution)/shard_map/ppermute | solution.py:40
  113.6 3.8 %collective-permute-start.10 = (bf16[128,128]{1,0:T(8,128)(2,1)S(1)}, bf16[128,128]{1,0:T(8,128)(2,1)S(1)}, u32[]{:S(2)}, u32[]{:S(2)}) collective-permute-start(bf16[128,128]{1,0:T(8,128)(2,1)S(1)} %get-tuple-element.25), channel_id=1, source_target_pairs={{1,0},{2,1},{3,2},{4,3},{5,4},{6,5},{7,6},{8,7},{9,8},{10,9},{11,1... | collective-permute-start | bytes 98312 | tf_op jit(solution)/shard_map/ppermute | solution.py:27
  115.3 8.5 %slice-start.1 = ((s8[6291456]{0:T(1024)(128)(4,1)}), s8[2097152]{0:T(1024)(128)(4,1)S(1)}, s32[]{:S(2)}) async-start(s8[6291456]{0:T(1024)(128)(4,1)} %bitcast.230), calls=%async_computation.1 | async-start | bytes 4194304
  134.1 3.7 %copy-start.1 = (bf16[2304,2048]{1,0:T(8,128)(2,1)}, bf16[2304,2048]{1,0:T(8,128)(2,1)S(1)}, u32[]{:S(2)}) copy-start(bf16[2304,2048]{1,0:T(8,128)(2,1)S(1)} %convolution_convert_fusion.refs_0_.refs_1_.refs_2_.refs_3_.refs_5_.refs_6_.refs_7_) | copy-start | bytes 28311556
  137.8 1.6 copy-start.7
  137.8 1.7 copy-start.8
  137.8 1.8 %copy-start.9 = (s32[4]{0:T(128)S(1)}, s32[4]{0:T(128)}, u32[]{:S(2)}) copy-start(s32[4]{0:T(128)} %constant.58.clone) | copy-start | bytes 52
  139.2 11.1 %collective-permute-start.14 = (bf16[512,2048]{1,0:T(8,128)(2,1)}, bf16[512,2048]{1,0:T(8,128)(2,1)}, u32[]{:S(2)}, u32[]{:S(2)}) collective-permute-start(bf16[512,2048]{1,0:T(8,128)(2,1)} %slice.357), channel_id=1, source_target_pairs={{0,1},{1,0},{2,3},{3,2},{4,5},{5,4},{6,7},{7,6},{8,9},{9,8},{10,11... | collective-permute-start | bytes 6291464 | tf_op jit(solution)/shard_map/ppermute | solution.py:40

commit v9 on v8

--- a/solution.py
+++ b/solution.py
@@ -50,7 +50,7 @@
     return result.reshape(field.shape)
 
 
-def chebyshev(struct_feats, op_blocks, laplace_index, series_coef, first_block, riders):
+def chebyshev(struct_feats, op_blocks, laplace_index, series_coef, first_block, riders, later):
     count = op_blocks.shape[0]
     chans = struct_feats.shape[1]
     taps = 2 * REACH + 1
@@ -91,6 +91,10 @@
             packed = jnp.concatenate([older, cur], axis=2)
             left = shift_rows(packed[count - halo :], "seq", 1)
             right = shift_rows(packed[:halo], "seq", -1)
+            if later is not None:
+                left, right, later = lax.optimization_barrier((left, right, later))
+                riders = riders + (later,)
+                later = None
             prev = jnp.concatenate(
                 [left[halo - edge :, :, :chans], older, right[:edge, :, :chans]], axis=0
             )
@@ -188,12 +192,15 @@
 
     feats_before = shift_rows(node_feats[rows - rim:], "seq", 1)
     feats_after = shift_rows(node_feats[:rim], "seq", -1)
-    encoding, (feats_before, feats_after, held) = chebyshev(
+    half = rows // 2
+    early = [partner(node_feats[:half], "seq", bit) for bit in bits[1:]]
+    encoding, (feats_before, feats_after, early) = chebyshev(
         struct_feats, op_blocks, laplace_index, series_coef, first_block,
-        (feats_before, feats_after, node_feats),
-    )
-    feats_far = [partner(held, "seq", bit) for bit in bits[1:]]
-    encoding, feats_far = lax.optimization_barrier((encoding, feats_far))
+        (feats_before, feats_after), early,
+    )
+    late = [partner(node_feats[half:], "seq", bit) for bit in bits[1:]]
+    encoding, late = lax.optimization_barrier((encoding, late))
+    feats_far = [jnp.concatenate([a, b], axis=0) for a, b in zip(early, late)]
     encoding_b = encoding.astype(jnp.bfloat16)
 
     enc_before = shift_rows(encoding_b[rows - rim:], "seq", 1)

time: 169 us -> 163 us (0.964)
  waiting for transfers between devices: 44.3 us -> 20.1 us
  starting transfers between devices: 47.9 us -> 66.9 us
    ppermute x7 -> x10, waiting for transfers between devices: 39.3 us -> 19.1 us  [partner(): return lax.ppermute(value, axis, pairs)]
    ppermute x7 -> x10, starting transfers between devices: 11.4 us -> 27.6 us  [partner(): return lax.ppermute(value, axis, pairs)]
    ppermute x8, waiting for transfers between devices: 4.96 us -> 0.91 us  [shift_rows(): return lax.ppermute(x, axis, pairs)]
    ppermute x8, starting transfers between devices: 36.5 us -> 39.3 us  [shift_rows(): return lax.ppermute(x, axis, pairs)]
  transfers between devices with their start and end apart: 15 -> 18, of which waited for: 5 -> 5; matrix products, arithmetic and copies ran while one was open for 15% -> 20% of each run, Pallas kernels for 0% -> 0%
where the time goes in v9:
time: 163 us; the launch traced here: 162 us
  starting transfers between devices  66.9 us (41%)
  matrix products  33.7 us (21%)
  waiting for transfers between devices  20.1 us (12%)
  local copies, waits for them, and re-layouts  16.2 us (10%)
  Pallas kernels  14.1 us (9%)
  other arithmetic  10.4 us (6%)
    ppermute x8, starting transfers between devices, shift_rows(): return lax.ppermute(x, axis, pairs)  39.3 us
    ppermute x10, starting transfers between devices, partner(): return lax.ppermute(value, axis, pairs)  27.6 us
    ppermute x10, waiting for transfers between devices, partner(): return lax.ppermute(value, axis, pairs)  19.1 us
    dot_general x8, matrix products, step(): jnp.einsum('wsk,wkc->wsc', bands[lo - REACH:hi - REACH], stacked, precisi...  15 us
    pallas_call x1, Pallas kernels, attend(): pl.pallas_call(attention_kernel, grid_spec=grid_spec, out_shape=jax.Shape...  14.1 us
    dot_general x1, matrix products, on_device(): jnp.dot(all_blended, kv_weight, preferred_element_type=jnp.float32)  10.3 us
    unnamed x60, local copies, waits for them, and re-layouts  6.83 us
    select_n x1, other arithmetic, split_queries(): return jnp.where(d_head == j_head, qt * scale, jnp.zeros_like(qt))  5.06 us
  transfers between devices with their start and end apart: 18, of which 5 were waited for; matrix products, arithmetic and copies ran while one was open for 20% of the time, Pallas kernels for 0%

profile of v9, /device:TPU:0, one launch (start us, length us, event | category | flops | bytes accessed | tf_op | source)
XLA Modules:
  0.0 162.3 jit_solution(10280001608544786391)
XLA Ops:
  0.0 0.9 copy.34
  1.1 2.8 %select_reduce_fusion = f32[8,5,64,64]{3,2,1,0:T(8,128)} fusion(f32[8,3,64,64]{3,2,1,0:T(8,128)} %param.13, pred[8,3,5]{2,1,0:T(4,128)(4,1)S(1)} %iota_compare_fusion), kind=kLoop, calls=%fused_computation.2 | loop fusion | flops 819200 | bytes 1048696 | tf_op jit(solution)/shard_map/reduce_sum | solution.py:61
  3.9 1.7 %copy.35 = f32[8,64,5,64]{1,3,2,0:T(8,128)S(1)} copy(f32[8,64,5,64]{3,1,2,0:T(8,128)} %bitcast.214) | data formatting | bytes 1310720 | tf_op jit(solution)/shard_map/transpose | solution.py:62
  5.6 1.3 copy.36
  7.0 1.4 pad_maximum_fusion.1
  8.4 2.4 %collective-permute-start = (f32[8,64,448]{2,1,0:T(8,128)S(1)}, f32[8,64,448]{2,1,0:T(8,128)S(1)}, u32[]{:S(2)}, u32[]{:S(2)}) collective-permute-start(f32[8,64,448]{2,1,0:T(8,128)S(1)} %pad_maximum_fusion.1), channel_id=1, source_target_pairs={{0,1},{1,2},{2,3},{3,4},{4,5},{5,6},{6,7},{7,8},{8,9},{9,10},{10,1... | collective-permute-start | bytes 2752520 | tf_op jit(solution)/shard_map/ppermute | solution.py:27
  10.8 1.3 collective-permute-start.1
  12.1 5.1 %collective-permute-start.2 = (bf16[128,1024]{1,0:T(8,128)(2,1)S(1)}, bf16[128,1024]{1,0:T(8,128)(2,1)S(1)}, u32[]{:S(2)}, u32[]{:S(2)}) collective-permute-start(bf16[128,1024]{1,0:T(8,128)(2,1)S(1)} %get-tuple-element.34), channel_id=1, source_target_pairs={{0,1},{1,2},{2,3},{3,4},{4,5},{5,6},{6,7},{7,8},{8,9},{9,10},{10,1... | collective-permute-start | bytes 786440 | tf_op jit(solution)/shard_map/ppermute | solution.py:27
  17.2 1.3 collective-permute-start.3
  18.6 4.0 %collective-permute-start.6 = (bf16[256,1024]{1,0:T(8,128)(2,1)S(1)}, bf16[256,1024]{1,0:T(8,128)(2,1)S(1)}, u32[]{:S(2)}, u32[]{:S(2)}) collective-permute-start(bf16[256,1024]{1,0:T(8,128)(2,1)S(1)} %get-tuple-element.32), channel_id=1, source_target_pairs={{0,2},{1,3},{2,0},{3,1},{4,6},{5,7},{6,4},{7,5},{8,10},{9,11},{10,... | collective-permute-start | bytes 1572872 | tf_op jit(solution)/shard_map/ppermute | solution.py:40
  22.7 8.6 %collective-permute-start.7 = (bf16[256,1024]{1,0:T(8,128)(2,1)S(1)}, bf16[256,1024]{1,0:T(8,128)(2,1)S(1)}, u32[]{:S(2)}, u32[]{:S(2)}) collective-permute-start(bf16[256,1024]{1,0:T(8,128)(2,1)S(1)} %get-tuple-element.32), channel_id=1, source_target_pairs={{0,4},{1,5},{2,6},{3,7},{4,0},{5,1},{6,2},{7,3},{8,12},{9,13},{10,... | collective-permute-start | bytes 1572872 | tf_op jit(solution)/shard_map/ppermute | solution.py:40
  31.3 2.7 %collective-permute-start.8 = (bf16[256,1024]{1,0:T(8,128)(2,1)S(1)}, bf16[256,1024]{1,0:T(8,128)(2,1)S(1)}, u32[]{:S(2)}, u32[]{:S(2)}) collective-permute-start(bf16[256,1024]{1,0:T(8,128)(2,1)S(1)} %get-tuple-element.32), channel_id=1, source_target_pairs={{0,8},{1,9},{2,10},{3,11},{4,12},{5,13},{6,14},{7,15},{8,0},{9,1},... | collective-permute-start | bytes 1572872 | tf_op jit(solution)/shard_map/ppermute | solution.py:40
  34.6 0.4 copy.38
  35.0 0.7 copy-done.2
  35.7 1.3 fusion.69
  37.5 1.2 fusion.20
  39.1 0.8 fusion.14
  40.3 1.2 fusion.17
  41.6 25.0 %collective-permute-start.4 = (f32[8,64,256]{2,1,0:T(8,128)S(1)}, f32[8,64,256]{2,1,0:T(8,128)S(1)}, u32[]{:S(2)}, u32[]{:S(2)}) collective-permute-start(f32[8,64,256]{2,1,0:T(8,128)S(1)} %pad_maximum_fusion.4), channel_id=1, source_target_pairs={{0,1},{1,2},{2,3},{3,4},{4,5},{5,6},{6,7},{7,8},{8,9},{9,10},{10,1... | collective-permute-start | bytes 1572872 | tf_op jit(solution)/shard_map/ppermute | solution.py:27
  66.5 1.5 collective-permute-start.5
  68.0 0.7 fusion.73
  68.7 2.2 %collective-permute-start.10 = (bf16[256,1024]{1,0:T(8,128)(2,1)S(1)}, bf16[256,1024]{1,0:T(8,128)(2,1)S(1)}, u32[]{:S(2)}, u32[]{:S(2)}) collective-permute-start(bf16[256,1024]{1,0:T(8,128)(2,1)S(1)} %get-tuple-element.31), channel_id=1, source_target_pairs={{0,4},{1,5},{2,6},{3,7},{4,0},{5,1},{6,2},{7,3},{8,12},{9,13},{10,... | collective-permute-start | bytes 1572872 | tf_op jit(solution)/shard_map/ppermute | solution.py:40
  71.3 1.7 %collective-permute-start.9 = (bf16[256,1024]{1,0:T(8,128)(2,1)S(1)}, bf16[256,1024]{1,0:T(8,128)(2,1)S(1)}, u32[]{:S(2)}, u32[]{:S(2)}) collective-permute-start(bf16[256,1024]{1,0:T(8,128)(2,1)S(1)} %get-tuple-element.31), channel_id=1, source_target_pairs={{0,2},{1,3},{2,0},{3,1},{4,6},{5,7},{6,4},{7,5},{8,10},{9,11},{10,... | collective-permute-start | bytes 1572872 | tf_op jit(solution)/shard_map/ppermute | solution.py:40
  73.7 1.3 fusion.13
  75.5 1.3 fusion.21
  77.2 0.9 fusion.15
  78.4 6.8 %fusion.19 = bf16[8,64,128]{2,1,0:T(8,128)(2,1)S(1)} fusion(f32[8,64,320]{1,2,0:T(8,128)S(1)} %bitcast.210, f32[8,320,128]{2,1,0:T(8,128)S(1)} %bitcast.216, f32[20,64,128]{2,1,0:T(8,128)S(1)} %fusion.13, f32[20,64,128]{2,1,0:T(8,128)S(1)} %fusion.69, f32[16,64,128]{2,1,0:T(8,128)S(1)} %fusion.21, f32[8,64,128]{2,1,0:T(8,128)S(1)} %fusion.17, ...), kind=kOutput, calls=%fused_computation.31 | convolution fusion | flops 127139840 | bytes 4194340 | tf_op jit(solution)/shard_map/wsk,wkc->wsc/dot_general | solution.py:79
  85.2 14.4 %collective-permute-done.10 = bf16[256,1024]{1,0:T(8,128)(2,1)S(1)} collective-permute-done((bf16[256,1024]{1,0:T(8,128)(2,1)S(1)}, bf16[256,1024]{1,0:T(8,128)(2,1)S(1)}, u32[]{:S(2)}, u32[]{:S(2)}) %collective-permute-start.10) | collective-permute-done | bytes 524320 | tf_op jit(solution)/shard_map/ppermute | solution.py:40
  99.7 1.3 collective-permute-start.12
  101.0 7.9 %collective-permute-start.14 = (bf16[512,128]{1,0:T(8,128)(2,1)S(1)}, bf16[512,128]{1,0:T(8,128)(2,1)S(1)}, u32[]{:S(2)}, u32[]{:S(2)}) collective-permute-start(bf16[512,128]{1,0:T(8,128)(2,1)S(1)} %bitcast.226), channel_id=1, source_target_pairs={{0,2},{1,3},{2,0},{3,1},{4,6},{5,7},{6,4},{7,5},{8,10},{9,11},{10,... | collective-permute-start | bytes 393224 | tf_op jit(solution)/shard_map/ppermute | solution.py:40
  108.9 1.5 collective-permute-start.13
  110.7 0.4 constant_dynamic-update-slice_fusion
  111.1 0.9 collective-permute-done.13
  112.2 0.3 collective-permute-done.14
  112.5 0.4 fusion.4
  113.0 2.3 %collective-permute-done.15 = bf16[512,128]{1,0:T(8,128)(2,1)S(1)} collective-permute-done((bf16[512,128]{1,0:T(8,128)(2,1)S(1)}, bf16[512,128]{1,0:T(8,128)(2,1)S(1)}, u32[]{:S(2)}, u32[]{:S(2)}) %collective-permute-start.15) | collective-permute-done | bytes 131104 | tf_op jit(solution)/shard_map/ppermute | solution.py:40
  115.3 0.4 fusion.5
  115.7 2.1 %collective-permute-done.16 = bf16[512,128]{1,0:T(8,128)(2,1)S(1)} collective-permute-done((bf16[512,128]{1,0:T(8,128)(2,1)S(1)}, bf16[512,128]{1,0:T(8,128)(2,1)S(1)}, u32[]{:S(2)}, u32[]{:S(2)}) %collective-permute-start.16) | collective-permute-done | bytes 131104 | tf_op jit(solution)/shard_map/ppermute | solution.py:40
  117.8 0.4 fusion.6
  118.2 10.3 %convolution_convert_fusion.refs_0_.refs_1_.refs_2_.refs_3_.refs_5_.refs_6_.refs_7_ = bf16[2304,2048]{1,0:T(8,128)(2,1)S(1)} fusion(bf16[2304,1024]{1,0:T(8,128)(2,1)S(1)} %fusion.6, bf16[1024,3072]{1,0:T(8,128)(2,1)S(1)} %bitcast.231), kind=kOutput, calls=%fused_computation | convolution fusion | flops 9668395008 | bytes 18350080 | tf_op jit(solution)/shard_map/dot_general | solution.py:224
  128.5 3.7 %copy-done.1 = bf16[2304,2048]{1,0:T(8,128)(2,1)} copy-done((bf16[2304,2048]{1,0:T(8,128)(2,1)}, bf16[2304,2048]{1,0:T(8,128)(2,1)S(1)}, u32[]{:S(2)}) %copy-start.1) | copy-done | bytes 9437208
  132.2 1.5 slice.365
  133.9 0.7 pad_add_fusion.table_ref
  134.7 2.8 %fusion.10 = bf16[64,8,8,128]{3,1,2,0:T(8,128)(2,1)S(1)} fusion(bf16[512,1024]{1,0:T(8,128)(2,1)S(1)} %get-tuple-element.47, bf16[1024,3072]{1,0:T(8,128)(2,1)} %param.19), kind=kOutput, calls=%fused_computation.17 | convolution fusion | flops 1074266112 | bytes 4194304 | tf_op jit(solution)/shard_map/dot_general | solution.py:216
  137.8 1.8 %copy.48 = bf16[8,64,8,128]{1,3,2,0:T(8,128)(2,1)} copy(bf16[8,64,8,128]{3,2,1,0:T(8,128)(2,1)S(1)} %bitcast.217) | data formatting | bytes 2097152 | tf_op jit(solution)/shard_map/reshape | solution.py:145
  139.6 5.1 %fusion.1.q_ref = bf16[8,8,128,128]{3,2,1,0:T(8,128)(2,1)} fusion(bf16[8,8,128,64]{3,2,1,0:T(8,128)(2,1)} %bitcast.213, pred[128,128]{1,0:T(8,128)(4,1)S(1)} %select_compare_fusion), kind=kLoop, calls=%fused_computation.4 | loop fusion | flops 7340032 | bytes 3162112 | tf_op jit(solution)/shard_map/jit(_where)/select_n | solution.py:150
  144.7 14.1 %shard_map.109 = bf16[512,1024]{1,0:T(8,128)(2,1)} custom-call(s32[8,8]{1,0:T(8,128)} %pad_add_fusion.table_ref, bf16[8,8,128,128]{3,2,1,0:T(8,128)(2,1)} %fusion.1.q_ref, bf16[2304,2048]{1,0:T(8,128)(2,1)} %copy-done.1, bf16[2304,2048]{1,0:T(8,128)(2,1)} %copy-done.1, bf16[2304,2048]{1,0:T(8,128)(2,1)} %copy-done.1, bf16[2304,2048]{1,0:T(8,128)(2,1)} %copy-done.1, ...), custom_call_target="tpu_custom_call" | custom-call | tf_op jit(solution)/shard_map/pallas_call | solution.py:167
  158.8 3.4 %convolution_convert_fusion.1 = bf16[512,1024]{1,0:T(8,128)(2,1)} fusion(bf16[512,1024]{1,0:T(8,128)(2,1)} %shard_map.109, bf16[1024,1024]{1,0:T(8,128)(2,1)S(1)} %copy-done), kind=kOutput, calls=%fused_computation.16 | convolution fusion | flops 1074266112 | bytes 4194304 | tf_op jit(solution)/shard_map/dot_general | solution.py:239
  (116 shorter events, 4.8 us)
Async XLA Ops:
  0.0 158.8 %copy-start = (bf16[1024,1024]{1,0:T(8,128)(2,1)S(1)}, bf16[1024,1024]{1,0:T(8,128)(2,1)}, u32[]{:S(2)}) copy-start(bf16[1024,1024]{1,0:T(8,128)(2,1)} %param.20) | copy-start | bytes 6291460
  7.0 5.1 %copy-start.3 = (bf16[512,1024]{1,0:T(8,128)(2,1)S(1)}, bf16[512,1024]{1,0:T(8,128)(2,1)}, u32[]{:S(2)}) copy-start(bf16[512,1024]{1,0:T(8,128)(2,1)} %param.11) | copy-start | bytes 3145732
  8.4 25.7 %collective-permute-start = (f32[8,64,448]{2,1,0:T(8,128)S(1)}, f32[8,64,448]{2,1,0:T(8,128)S(1)}, u32[]{:S(2)}, u32[]{:S(2)}) collective-permute-start(f32[8,64,448]{2,1,0:T(8,128)S(1)} %pad_maximum_fusion.1), channel_id=1, source_target_pairs={{0,1},{1,2},{2,3},{3,4},{4,5},{5,6},{6,7},{7,8},{8,9},{9,10},{10,1... | collective-permute-start | bytes 2752520 | tf_op jit(solution)/shard_map/ppermute | solution.py:27
  10.8 23.2 %collective-permute-start.1 = (f32[8,64,448]{2,1,0:T(8,128)S(1)}, f32[8,64,448]{2,1,0:T(8,128)S(1)}, u32[]{:S(2)}, u32[]{:S(2)}) collective-permute-start(f32[8,64,448]{2,1,0:T(8,128)S(1)} %pad_maximum_fusion.1), channel_id=1, source_target_pairs={{1,0},{2,1},{3,2},{4,3},{5,4},{6,5},{7,6},{8,7},{9,8},{10,9},{11,1... | collective-permute-start | bytes 2752520 | tf_op jit(solution)/shard_map/ppermute | solution.py:27
  12.1 10.5 %collective-permute-start.2 = (bf16[128,1024]{1,0:T(8,128)(2,1)S(1)}, bf16[128,1024]{1,0:T(8,128)(2,1)S(1)}, u32[]{:S(2)}, u32[]{:S(2)}) collective-permute-start(bf16[128,1024]{1,0:T(8,128)(2,1)S(1)} %get-tuple-element.34), channel_id=1, source_target_pairs={{0,1},{1,2},{2,3},{3,4},{4,5},{5,6},{6,7},{7,8},{8,9},{9,10},{10,1... | collective-permute-start | bytes 786440 | tf_op jit(solution)/shard_map/ppermute | solution.py:27
  17.2 14.1 %collective-permute-start.3 = (bf16[128,1024]{1,0:T(8,128)(2,1)S(1)}, bf16[128,1024]{1,0:T(8,128)(2,1)S(1)}, u32[]{:S(2)}, u32[]{:S(2)}) collective-permute-start(bf16[128,1024]{1,0:T(8,128)(2,1)S(1)} %get-tuple-element.33), channel_id=1, source_target_pairs={{1,0},{2,1},{3,2},{4,3},{5,4},{6,5},{7,6},{8,7},{9,8},{10,9},{11,1... | collective-permute-start | bytes 786440 | tf_op jit(solution)/shard_map/ppermute | solution.py:27
  18.6 15.6 %copy-start.5 = (f32[512,128]{1,0:T(8,128)S(1)}, f32[512,128]{1,0:T(8,128)}, u32[]{:S(2)}) copy-start(f32[512,128]{1,0:T(8,128)} %param.12) | copy-start | bytes 786436
  18.6 50.1 %collective-permute-start.6 = (bf16[256,1024]{1,0:T(8,128)(2,1)S(1)}, bf16[256,1024]{1,0:T(8,128)(2,1)S(1)}, u32[]{:S(2)}, u32[]{:S(2)}) collective-permute-start(bf16[256,1024]{1,0:T(8,128)(2,1)S(1)} %get-tuple-element.32), channel_id=1, source_target_pairs={{0,2},{1,3},{2,0},{3,1},{4,6},{5,7},{6,4},{7,5},{8,10},{9,11},{10,... | collective-permute-start | bytes 1572872 | tf_op jit(solution)/shard_map/ppermute | solution.py:40
  22.7 48.3 %collective-permute-start.7 = (bf16[256,1024]{1,0:T(8,128)(2,1)S(1)}, bf16[256,1024]{1,0:T(8,128)(2,1)S(1)}, u32[]{:S(2)}, u32[]{:S(2)}) collective-permute-start(bf16[256,1024]{1,0:T(8,128)(2,1)S(1)} %get-tuple-element.32), channel_id=1, source_target_pairs={{0,4},{1,5},{2,6},{3,7},{4,0},{5,1},{6,2},{7,3},{8,12},{9,13},{10,... | collective-permute-start | bytes 1572872 | tf_op jit(solution)/shard_map/ppermute | solution.py:40
  31.3 40.0 %collective-permute-start.8 = (bf16[256,1024]{1,0:T(8,128)(2,1)S(1)}, bf16[256,1024]{1,0:T(8,128)(2,1)S(1)}, u32[]{:S(2)}, u32[]{:S(2)}) collective-permute-start(bf16[256,1024]{1,0:T(8,128)(2,1)S(1)} %get-tuple-element.32), channel_id=1, source_target_pairs={{0,8},{1,9},{2,10},{3,11},{4,12},{5,13},{6,14},{7,15},{8,0},{9,1},... | collective-permute-start | bytes 1572872 | tf_op jit(solution)/shard_map/ppermute | solution.py:40
  34.6 1.1 copy-start.2
  40.3 27.7 %copy-start.6 = (f32[9]{0:T(128)S(1)}, f32[9]{0:T(128)}, u32[]{:S(2)}) copy-start(f32[9]{0:T(128)} %param.17) | copy-start | bytes 112
  41.6 31.5 %collective-permute-start.4 = (f32[8,64,256]{2,1,0:T(8,128)S(1)}, f32[8,64,256]{2,1,0:T(8,128)S(1)}, u32[]{:S(2)}, u32[]{:S(2)}) collective-permute-start(f32[8,64,256]{2,1,0:T(8,128)S(1)} %pad_maximum_fusion.4), channel_id=1, source_target_pairs={{0,1},{1,2},{2,3},{3,4},{4,5},{5,6},{6,7},{7,8},{8,9},{9,10},{10,1... | collective-permute-start | bytes 1572872 | tf_op jit(solution)/shard_map/ppermute | solution.py:27
  66.5 6.5 %collective-permute-start.5 = (f32[8,64,256]{2,1,0:T(8,128)S(1)}, f32[8,64,256]{2,1,0:T(8,128)S(1)}, u32[]{:S(2)}, u32[]{:S(2)}) collective-permute-start(f32[8,64,256]{2,1,0:T(8,128)S(1)} %pad_maximum_fusion.4), channel_id=1, source_target_pairs={{1,0},{2,1},{3,2},{4,3},{5,4},{6,5},{7,6},{8,7},{9,8},{10,9},{11,1... | collective-permute-start | bytes 1572872 | tf_op jit(solution)/shard_map/ppermute | solution.py:27
  68.7 30.9 %collective-permute-start.10 = (bf16[256,1024]{1,0:T(8,128)(2,1)S(1)}, bf16[256,1024]{1,0:T(8,128)(2,1)S(1)}, u32[]{:S(2)}, u32[]{:S(2)}) collective-permute-start(bf16[256,1024]{1,0:T(8,128)(2,1)S(1)} %get-tuple-element.31), channel_id=1, source_target_pairs={{0,4},{1,5},{2,6},{3,7},{4,0},{5,1},{6,2},{7,3},{8,12},{9,13},{10,... | collective-permute-start | bytes 1572872 | tf_op jit(solution)/shard_map/ppermute | solution.py:40
  71.0 28.7 %collective-permute-start.11 = (bf16[256,1024]{1,0:T(8,128)(2,1)S(1)}, bf16[256,1024]{1,0:T(8,128)(2,1)S(1)}, u32[]{:S(2)}, u32[]{:S(2)}) collective-permute-start(bf16[256,1024]{1,0:T(8,128)(2,1)S(1)} %get-tuple-element.31), channel_id=1, source_target_pairs={{0,8},{1,9},{2,10},{3,11},{4,12},{5,13},{6,14},{7,15},{8,0},{9,1},... | collective-permute-start | bytes 1572872 | tf_op jit(solution)/shard_map/ppermute | solution.py:40
  71.3 28.4 %collective-permute-start.9 = (bf16[256,1024]{1,0:T(8,128)(2,1)S(1)}, bf16[256,1024]{1,0:T(8,128)(2,1)S(1)}, u32[]{:S(2)}, u32[]{:S(2)}) collective-permute-start(bf16[256,1024]{1,0:T(8,128)(2,1)S(1)} %get-tuple-element.31), channel_id=1, source_target_pairs={{0,2},{1,3},{2,0},{3,1},{4,6},{5,7},{6,4},{7,5},{8,10},{9,11},{10,... | collective-permute-start | bytes 1572872 | tf_op jit(solution)/shard_map/ppermute | solution.py:40
  78.4 32.0 %copy-start.4 = (bf16[128,1024]{1,0:T(8,128)(2,1)S(1)}, bf16[128,1024]{1,0:T(8,128)(2,1)}, u32[]{:S(2)}) copy-start(bf16[128,1024]{1,0:T(8,128)(2,1)} %param.18) | copy-start | bytes 786436
  99.7 10.7 %collective-permute-start.12 = (bf16[128,128]{1,0:T(8,128)(2,1)S(1)}, bf16[128,128]{1,0:T(8,128)(2,1)S(1)}, u32[]{:S(2)}, u32[]{:S(2)}) collective-permute-start(bf16[128,128]{1,0:T(8,128)(2,1)S(1)} %get-tuple-element.36), channel_id=1, source_target_pairs={{0,1},{1,2},{2,3},{3,4},{4,5},{5,6},{6,7},{7,8},{8,9},{9,10},{10,1... | collective-permute-start | bytes 98312 | tf_op jit(solution)/shard_map/ppermute | solution.py:27
  101.0 11.6 %collective-permute-start.14 = (bf16[512,128]{1,0:T(8,128)(2,1)S(1)}, bf16[512,128]{1,0:T(8,128)(2,1)S(1)}, u32[]{:S(2)}, u32[]{:S(2)}) collective-permute-start(bf16[512,128]{1,0:T(8,128)(2,1)S(1)} %bitcast.226), channel_id=1, source_target_pairs={{0,2},{1,3},{2,0},{3,1},{4,6},{5,7},{6,4},{7,5},{8,10},{9,11},{10,... | collective-permute-start | bytes 393224 | tf_op jit(solution)/shard_map/ppermute | solution.py:40
  108.9 6.4 %collective-permute-start.15 = (bf16[512,128]{1,0:T(8,128)(2,1)S(1)}, bf16[512,128]{1,0:T(8,128)(2,1)S(1)}, u32[]{:S(2)}, u32[]{:S(2)}) collective-permute-start(bf16[512,128]{1,0:T(8,128)(2,1)S(1)} %bitcast.227), channel_id=1, source_target_pairs={{0,4},{1,5},{2,6},{3,7},{4,0},{5,1},{6,2},{7,3},{8,12},{9,13},{10,... | collective-permute-start | bytes 393224 | tf_op jit(solution)/shard_map/ppermute | solution.py:40
  108.9 8.9 %collective-permute-start.16 = (bf16[512,128]{1,0:T(8,128)(2,1)S(1)}, bf16[512,128]{1,0:T(8,128)(2,1)S(1)}, u32[]{:S(2)}, u32[]{:S(2)}) collective-permute-start(bf16[512,128]{1,0:T(8,128)(2,1)S(1)} %bitcast.228), channel_id=1, source_target_pairs={{0,8},{1,9},{2,10},{3,11},{4,12},{5,13},{6,14},{7,15},{8,0},{9,1},... | collective-permute-start | bytes 393224 | tf_op jit(solution)/shard_map/ppermute | solution.py:40
  108.9 3.1 %collective-permute-start.13 = (bf16[128,128]{1,0:T(8,128)(2,1)S(1)}, bf16[128,128]{1,0:T(8,128)(2,1)S(1)}, u32[]{:S(2)}, u32[]{:S(2)}) collective-permute-start(bf16[128,128]{1,0:T(8,128)(2,1)S(1)} %get-tuple-element.35), channel_id=1, source_target_pairs={{1,0},{2,1},{3,2},{4,3},{5,4},{6,5},{7,6},{8,7},{9,8},{10,9},{11,1... | collective-permute-start | bytes 98312 | tf_op jit(solution)/shard_map/ppermute | solution.py:27
  110.6 7.6 %slice-start = ((s8[6291456]{0:T(1024)(128)(4,1)}), s8[4194304]{0:T(1024)(128)(4,1)S(1)}, s32[]{:S(2)}) async-start(s8[6291456]{0:T(1024)(128)(4,1)} %bitcast.230), calls=%async_computation | async-start | bytes 8388608
  112.2 6.0 %slice-start.1 = ((s8[6291456]{0:T(1024)(128)(4,1)}), s8[2097152]{0:T(1024)(128)(4,1)S(1)}, s32[]{:S(2)}) async-start(s8[6291456]{0:T(1024)(128)(4,1)} %bitcast.230), calls=%async_computation.1 | async-start | bytes 4194304
  128.5 3.7 %copy-start.1 = (bf16[2304,2048]{1,0:T(8,128)(2,1)}, bf16[2304,2048]{1,0:T(8,128)(2,1)S(1)}, u32[]{:S(2)}) copy-start(bf16[2304,2048]{1,0:T(8,128)(2,1)S(1)} %convolution_convert_fusion.refs_0_.refs_1_.refs_2_.refs_3_.refs_5_.refs_6_.refs_7_) | copy-start | bytes 28311556
  132.2 1.5 copy-start.7
  132.2 1.5 copy-start.8
  132.2 1.7 %copy-start.9 = (s32[4]{0:T(128)S(1)}, s32[4]{0:T(128)}, u32[]{:S(2)}) copy-start(s32[4]{0:T(128)} %constant.58.clone) | copy-start | bytes 52
  133.6 11.0 %collective-permute-start.17 = (bf16[512,2048]{1,0:T(8,128)(2,1)}, bf16[512,2048]{1,0:T(8,128)(2,1)}, u32[]{:S(2)}, u32[]{:S(2)}) collective-permute-start(bf16[512,2048]{1,0:T(8,128)(2,1)} %slice.365), channel_id=1, source_target_pairs={{0,1},{1,0},{2,3},{3,2},{4,5},{5,4},{6,7},{7,6},{8,9},{9,8},{10,11... | collective-permute-start | bytes 6291464 | tf_op jit(solution)/shard_map/ppermute | solution.py:40

commit v10 on v9

--- a/solution.py
+++ b/solution.py
@@ -64,7 +64,6 @@
     payload = jnp.concatenate([own_field, bands], axis=2)
     left = shift_rows(payload[count - halo :], "seq", 1)
     right = shift_rows(payload[:halo], "seq", -1)
-    left, right, riders = lax.optimization_barrier((left, right, riders))
     edge = halo - REACH
     bands = jnp.concatenate(
         [left[halo - edge :, :, chans:], bands, right[:edge, :, chans:]], axis=0
@@ -190,16 +189,17 @@
     levels = lax.axis_size("seq").bit_length() - 1
     bits = [link * (levels - 1) // (NEXP - 1) for link in range(NEXP)]
 
+    half = rows // 2
+    early = [partner(node_feats[:half], "seq", bit) for bit in bits[1:]]
+    encoding, (early,) = chebyshev(
+        struct_feats, op_blocks, laplace_index, series_coef, first_block, (), early,
+    )
+    late = [partner(node_feats[half:], "seq", bit) for bit in bits[1:]]
     feats_before = shift_rows(node_feats[rows - rim:], "seq", 1)
     feats_after = shift_rows(node_feats[:rim], "seq", -1)
-    half = rows // 2
-    early = [partner(node_feats[:half], "seq", bit) for bit in bits[1:]]
-    encoding, (feats_before, feats_after, early) = chebyshev(
-        struct_feats, op_blocks, laplace_index, series_coef, first_block,
-        (feats_before, feats_after), early,
-    )
-    late = [partner(node_feats[half:], "seq", bit) for bit in bits[1:]]
-    encoding, late = lax.optimization_barrier((encoding, late))
+    encoding, late, feats_before, feats_after = lax.optimization_barrier(
+        (encoding, late, feats_before, feats_after)
+    )
     feats_far = [jnp.concatenate([a, b], axis=0) for a, b in zip(early, late)]
     encoding_b = encoding.astype(jnp.bfloat16)
 

time: 163 us -> 154 us (0.945)
  waiting for transfers between devices: 20.1 us -> 11 us
    ppermute x10, waiting for transfers between devices: 19.1 us -> 9.35 us  [partner(): return lax.ppermute(value, axis, pairs)]
    ppermute x8, starting transfers between devices: 39.3 us -> 37.5 us  [shift_rows(): return lax.ppermute(x, axis, pairs)]
  transfers between devices with their start and end apart: 18 -> 18, of which waited for: 5 -> 3; matrix products, arithmetic and copies ran while one was open for 20% -> 21% of each run, Pallas kernels for 0% -> 0%
where the time goes in v10:
time: 154 us
  starting transfers between devices  66.3 us (43%)
  matrix products  33.7 us (22%)
  local copies, waits for them, and re-layouts  16.5 us (11%)
  Pallas kernels  14.8 us (10%)
  waiting for transfers between devices  11 us (7%)
  other arithmetic  10.4 us (7%)
    ppermute x8, starting transfers between devices, shift_rows(): return lax.ppermute(x, axis, pairs)  37.5 us
    ppermute x10, starting transfers between devices, partner(): return lax.ppermute(value, axis, pairs)  28.8 us
    dot_general x8, matrix products, step(): jnp.einsum('wsk,wkc->wsc', bands[lo - REACH:hi - REACH], stacked, precisi...  15 us
    pallas_call x1, Pallas kernels, attend(): pl.pallas_call(attention_kernel, grid_spec=grid_spec, out_shape=jax.Shape...  14.8 us
    dot_general x1, matrix products, on_device(): jnp.dot(all_blended, kv_weight, preferred_element_type=jnp.float32)  10.3 us
    ppermute x10, waiting for transfers between devices, partner(): return lax.ppermute(value, axis, pairs)  9.35 us
    unnamed x60, local copies, waits for them, and re-layouts  7.15 us
    select_n x1, other arithmetic, split_queries(): return jnp.where(d_head == j_head, qt * scale, jnp.zeros_like(qt))  5.06 us
  transfers between devices with their start and end apart: 18, of which 3 were waited for; matrix products, arithmetic and copies ran while one was open for 21% of the time, Pallas kernels for 0%

profile of v10, /device:TPU:0, one launch (start us, length us, event | category | flops | bytes accessed | tf_op | source)
XLA Modules:
  0.0 153.6 jit_solution(6617232798914654399)
XLA Ops:
  0.0 0.9 copy.34
  1.1 2.8 %select_reduce_fusion = f32[8,5,64,64]{3,2,1,0:T(8,128)} fusion(f32[8,3,64,64]{3,2,1,0:T(8,128)} %param.13, pred[8,3,5]{2,1,0:T(4,128)(4,1)S(1)} %iota_compare_fusion), kind=kLoop, calls=%fused_computation.2 | loop fusion | flops 819200 | bytes 1048696 | tf_op jit(solution)/shard_map/reduce_sum | solution.py:61
  3.9 1.7 %copy.35 = f32[8,64,5,64]{1,3,2,0:T(8,128)S(1)} copy(f32[8,64,5,64]{3,1,2,0:T(8,128)} %bitcast.214) | data formatting | bytes 1310720 | tf_op jit(solution)/shard_map/transpose | solution.py:62
  5.6 1.3 copy.36
  7.0 1.4 pad_maximum_fusion.1
  8.4 2.6 %collective-permute-start = (f32[8,64,448]{2,1,0:T(8,128)S(1)}, f32[8,64,448]{2,1,0:T(8,128)S(1)}, u32[]{:S(2)}, u32[]{:S(2)}) collective-permute-start(f32[8,64,448]{2,1,0:T(8,128)S(1)} %pad_maximum_fusion.1), channel_id=1, source_target_pairs={{0,1},{1,2},{2,3},{3,4},{4,5},{5,6},{6,7},{7,8},{8,9},{9,10},{10,1... | collective-permute-start | bytes 2752520 | tf_op jit(solution)/shard_map/ppermute | solution.py:27
  10.9 1.3 collective-permute-start.1
  12.3 4.9 %collective-permute-start.4 = (bf16[256,1024]{1,0:T(8,128)(2,1)S(1)}, bf16[256,1024]{1,0:T(8,128)(2,1)S(1)}, u32[]{:S(2)}, u32[]{:S(2)}) collective-permute-start(bf16[256,1024]{1,0:T(8,128)(2,1)S(1)} %get-tuple-element.30), channel_id=1, source_target_pairs={{0,2},{1,3},{2,0},{3,1},{4,6},{5,7},{6,4},{7,5},{8,10},{9,11},{10,... | collective-permute-start | bytes 1572872 | tf_op jit(solution)/shard_map/ppermute | solution.py:40
  17.2 1.6 %collective-permute-start.5 = (bf16[256,1024]{1,0:T(8,128)(2,1)S(1)}, bf16[256,1024]{1,0:T(8,128)(2,1)S(1)}, u32[]{:S(2)}, u32[]{:S(2)}) collective-permute-start(bf16[256,1024]{1,0:T(8,128)(2,1)S(1)} %get-tuple-element.30), channel_id=1, source_target_pairs={{0,4},{1,5},{2,6},{3,7},{4,0},{5,1},{6,2},{7,3},{8,12},{9,13},{10,... | collective-permute-start | bytes 1572872 | tf_op jit(solution)/shard_map/ppermute | solution.py:40
  18.8 2.6 %collective-permute-start.6 = (bf16[256,1024]{1,0:T(8,128)(2,1)S(1)}, bf16[256,1024]{1,0:T(8,128)(2,1)S(1)}, u32[]{:S(2)}, u32[]{:S(2)}) collective-permute-start(bf16[256,1024]{1,0:T(8,128)(2,1)S(1)} %get-tuple-element.30), channel_id=1, source_target_pairs={{0,8},{1,9},{2,10},{3,11},{4,12},{5,13},{6,14},{7,15},{8,0},{9,1},... | collective-permute-start | bytes 1572872 | tf_op jit(solution)/shard_map/ppermute | solution.py:40
  21.8 0.4 copy.38
  22.3 1.0 copy-done.2
  23.3 1.3 fusion.69
  25.1 1.2 fusion.20
  26.8 0.8 fusion.14
  28.0 1.2 fusion.17
  29.2 22.6 %collective-permute-start.2 = (f32[8,64,256]{2,1,0:T(8,128)S(1)}, f32[8,64,256]{2,1,0:T(8,128)S(1)}, u32[]{:S(2)}, u32[]{:S(2)}) collective-permute-start(f32[8,64,256]{2,1,0:T(8,128)S(1)} %pad_maximum_fusion.4), channel_id=1, source_target_pairs={{0,1},{1,2},{2,3},{3,4},{4,5},{5,6},{6,7},{7,8},{8,9},{9,10},{10,1... | collective-permute-start | bytes 1572872 | tf_op jit(solution)/shard_map/ppermute | solution.py:27
  51.9 1.3 collective-permute-start.3
  53.2 0.7 fusion.73
  53.9 4.8 %collective-permute-start.7 = (bf16[256,1024]{1,0:T(8,128)(2,1)S(1)}, bf16[256,1024]{1,0:T(8,128)(2,1)S(1)}, u32[]{:S(2)}, u32[]{:S(2)}) collective-permute-start(bf16[256,1024]{1,0:T(8,128)(2,1)S(1)} %get-tuple-element.29), channel_id=1, source_target_pairs={{0,2},{1,3},{2,0},{3,1},{4,6},{5,7},{6,4},{7,5},{8,10},{9,11},{10,... | collective-permute-start | bytes 1572872 | tf_op jit(solution)/shard_map/ppermute | solution.py:40
  58.7 1.6 %collective-permute-start.8 = (bf16[256,1024]{1,0:T(8,128)(2,1)S(1)}, bf16[256,1024]{1,0:T(8,128)(2,1)S(1)}, u32[]{:S(2)}, u32[]{:S(2)}) collective-permute-start(bf16[256,1024]{1,0:T(8,128)(2,1)S(1)} %get-tuple-element.29), channel_id=1, source_target_pairs={{0,4},{1,5},{2,6},{3,7},{4,0},{5,1},{6,2},{7,3},{8,12},{9,13},{10,... | collective-permute-start | bytes 1572872 | tf_op jit(solution)/shard_map/ppermute | solution.py:40
  60.2 2.7 %collective-permute-start.9 = (bf16[256,1024]{1,0:T(8,128)(2,1)S(1)}, bf16[256,1024]{1,0:T(8,128)(2,1)S(1)}, u32[]{:S(2)}, u32[]{:S(2)}) collective-permute-start(bf16[256,1024]{1,0:T(8,128)(2,1)S(1)} %get-tuple-element.29), channel_id=1, source_target_pairs={{0,8},{1,9},{2,10},{3,11},{4,12},{5,13},{6,14},{7,15},{8,0},{9,1},... | collective-permute-start | bytes 1572872 | tf_op jit(solution)/shard_map/ppermute | solution.py:40
  62.9 5.5 %collective-permute-start.10 = (bf16[128,1024]{1,0:T(8,128)(2,1)S(1)}, bf16[128,1024]{1,0:T(8,128)(2,1)S(1)}, u32[]{:S(2)}, u32[]{:S(2)}) collective-permute-start(bf16[128,1024]{1,0:T(8,128)(2,1)S(1)} %get-tuple-element.28), channel_id=1, source_target_pairs={{0,1},{1,2},{2,3},{3,4},{4,5},{5,6},{6,7},{7,8},{8,9},{9,10},{10,1... | collective-permute-start | bytes 786440 | tf_op jit(solution)/shard_map/ppermute | solution.py:27
  68.4 1.5 collective-permute-start.11
  70.6 1.3 fusion.13
  72.4 1.3 fusion.21
  74.1 0.9 fusion.15
  75.2 6.8 %fusion.19 = bf16[8,64,128]{2,1,0:T(8,128)(2,1)S(1)} fusion(f32[8,64,320]{1,2,0:T(8,128)S(1)} %bitcast.210, f32[8,320,128]{2,1,0:T(8,128)S(1)} %bitcast.216, f32[20,64,128]{2,1,0:T(8,128)S(1)} %fusion.13, f32[20,64,128]{2,1,0:T(8,128)S(1)} %fusion.69, f32[16,64,128]{2,1,0:T(8,128)S(1)} %fusion.21, f32[8,64,128]{2,1,0:T(8,128)S(1)} %fusion.17, ...), kind=kOutput, calls=%fused_computation.31 | convolution fusion | flops 127139840 | bytes 4194340 | tf_op jit(solution)/shard_map/wsk,wkc->wsc/dot_general | solution.py:78
  82.1 4.4 %collective-permute-done.8 = bf16[256,1024]{1,0:T(8,128)(2,1)S(1)} collective-permute-done((bf16[256,1024]{1,0:T(8,128)(2,1)S(1)}, bf16[256,1024]{1,0:T(8,128)(2,1)S(1)}, u32[]{:S(2)}, u32[]{:S(2)}) %collective-permute-start.8) | collective-permute-done | bytes 524320 | tf_op jit(solution)/shard_map/ppermute | solution.py:40
  86.5 1.3 collective-permute-start.12
  87.8 9.3 %collective-permute-start.14 = (bf16[512,128]{1,0:T(8,128)(2,1)S(1)}, bf16[512,128]{1,0:T(8,128)(2,1)S(1)}, u32[]{:S(2)}, u32[]{:S(2)}) collective-permute-start(bf16[512,128]{1,0:T(8,128)(2,1)S(1)} %bitcast.226), channel_id=1, source_target_pairs={{0,2},{1,3},{2,0},{3,1},{4,6},{5,7},{6,4},{7,5},{8,10},{9,11},{10,... | collective-permute-start | bytes 393224 | tf_op jit(solution)/shard_map/ppermute | solution.py:40
  97.2 1.1 collective-permute-start.15
  98.3 1.5 collective-permute-start.13
  100.1 0.4 constant_dynamic-update-slice_fusion
  100.5 1.6 %collective-permute-done.13 = bf16[128,128]{1,0:T(8,128)(2,1)S(1)} collective-permute-done((bf16[128,128]{1,0:T(8,128)(2,1)S(1)}, bf16[128,128]{1,0:T(8,128)(2,1)S(1)}, u32[]{:S(2)}, u32[]{:S(2)}) %collective-permute-start.13) | collective-permute-done | bytes 32800 | tf_op jit(solution)/shard_map/ppermute | solution.py:27
  102.4 0.4 fusion.4
  102.8 0.4 fusion.5
  103.3 4.9 %collective-permute-done.16 = bf16[512,128]{1,0:T(8,128)(2,1)S(1)} collective-permute-done((bf16[512,128]{1,0:T(8,128)(2,1)S(1)}, bf16[512,128]{1,0:T(8,128)(2,1)S(1)}, u32[]{:S(2)}, u32[]{:S(2)}) %collective-permute-start.16) | collective-permute-done | bytes 131104 | tf_op jit(solution)/shard_map/ppermute | solution.py:40
  108.2 0.4 fusion.6
  108.6 10.3 %convolution_convert_fusion.refs_0_.refs_1_.refs_2_.refs_3_.refs_5_.refs_6_.refs_7_ = bf16[2304,2048]{1,0:T(8,128)(2,1)S(1)} fusion(bf16[2304,1024]{1,0:T(8,128)(2,1)S(1)} %fusion.6, bf16[1024,3072]{1,0:T(8,128)(2,1)S(1)} %bitcast.231), kind=kOutput, calls=%fused_computation | convolution fusion | flops 9668395008 | bytes 18350080 | tf_op jit(solution)/shard_map/dot_general | solution.py:224
  118.9 3.7 %copy-done.1 = bf16[2304,2048]{1,0:T(8,128)(2,1)} copy-done((bf16[2304,2048]{1,0:T(8,128)(2,1)}, bf16[2304,2048]{1,0:T(8,128)(2,1)S(1)}, u32[]{:S(2)}) %copy-start.1) | copy-done | bytes 9437208
  122.6 1.5 slice.369
  124.6 0.7 pad_add_fusion.table_ref
  125.4 2.8 %fusion.10 = bf16[64,8,8,128]{3,1,2,0:T(8,128)(2,1)S(1)} fusion(bf16[512,1024]{1,0:T(8,128)(2,1)S(1)} %get-tuple-element.43, bf16[1024,3072]{1,0:T(8,128)(2,1)} %param.19), kind=kOutput, calls=%fused_computation.17 | convolution fusion | flops 1074266112 | bytes 4194304 | tf_op jit(solution)/shard_map/dot_general | solution.py:216
  128.5 1.8 %copy.48 = bf16[8,64,8,128]{1,3,2,0:T(8,128)(2,1)} copy(bf16[8,64,8,128]{3,2,1,0:T(8,128)(2,1)S(1)} %bitcast.217) | data formatting | bytes 2097152 | tf_op jit(solution)/shard_map/reshape | solution.py:144
  130.3 5.1 %fusion.1.q_ref = bf16[8,8,128,128]{3,2,1,0:T(8,128)(2,1)} fusion(bf16[8,8,128,64]{3,2,1,0:T(8,128)(2,1)} %bitcast.213, pred[128,128]{1,0:T(8,128)(4,1)S(1)} %select_compare_fusion), kind=kLoop, calls=%fused_computation.4 | loop fusion | flops 7340032 | bytes 3162112 | tf_op jit(solution)/shard_map/jit(_where)/select_n | solution.py:149
  135.4 14.8 %shard_map.109 = bf16[512,1024]{1,0:T(8,128)(2,1)} custom-call(s32[8,8]{1,0:T(8,128)} %pad_add_fusion.table_ref, bf16[8,8,128,128]{3,2,1,0:T(8,128)(2,1)} %fusion.1.q_ref, bf16[2304,2048]{1,0:T(8,128)(2,1)} %copy-done.1, bf16[2304,2048]{1,0:T(8,128)(2,1)} %copy-done.1, bf16[2304,2048]{1,0:T(8,128)(2,1)} %copy-done.1, bf16[2304,2048]{1,0:T(8,128)(2,1)} %copy-done.1, ...), custom_call_target="tpu_custom_call" | custom-call | tf_op jit(solution)/shard_map/pallas_call | solution.py:166
  150.2 3.4 %convolution_convert_fusion.1 = bf16[512,1024]{1,0:T(8,128)(2,1)} fusion(bf16[512,1024]{1,0:T(8,128)(2,1)} %shard_map.109, bf16[1024,1024]{1,0:T(8,128)(2,1)S(1)} %copy-done), kind=kOutput, calls=%fused_computation.16 | convolution fusion | flops 1074266112 | bytes 4194304 | tf_op jit(solution)/shard_map/dot_general | solution.py:239
  (116 shorter events, 4.8 us)
Async XLA Ops:
  0.0 150.2 %copy-start = (bf16[1024,1024]{1,0:T(8,128)(2,1)S(1)}, bf16[1024,1024]{1,0:T(8,128)(2,1)}, u32[]{:S(2)}) copy-start(bf16[1024,1024]{1,0:T(8,128)(2,1)} %param.20) | copy-start | bytes 6291460
  7.0 5.3 %copy-start.3 = (bf16[512,1024]{1,0:T(8,128)(2,1)S(1)}, bf16[512,1024]{1,0:T(8,128)(2,1)}, u32[]{:S(2)}) copy-start(bf16[512,1024]{1,0:T(8,128)(2,1)} %param.11) | copy-start | bytes 3145732
  8.4 13.1 %copy-start.5 = (f32[512,128]{1,0:T(8,128)S(1)}, f32[512,128]{1,0:T(8,128)}, u32[]{:S(2)}) copy-start(f32[512,128]{1,0:T(8,128)} %param.12) | copy-start | bytes 786436
  8.4 13.0 %collective-permute-start = (f32[8,64,448]{2,1,0:T(8,128)S(1)}, f32[8,64,448]{2,1,0:T(8,128)S(1)}, u32[]{:S(2)}, u32[]{:S(2)}) collective-permute-start(f32[8,64,448]{2,1,0:T(8,128)S(1)} %pad_maximum_fusion.1), channel_id=1, source_target_pairs={{0,1},{1,2},{2,3},{3,4},{4,5},{5,6},{6,7},{7,8},{8,9},{9,10},{10,1... | collective-permute-start | bytes 2752520 | tf_op jit(solution)/shard_map/ppermute | solution.py:27
  10.9 10.5 %collective-permute-start.1 = (f32[8,64,448]{2,1,0:T(8,128)S(1)}, f32[8,64,448]{2,1,0:T(8,128)S(1)}, u32[]{:S(2)}, u32[]{:S(2)}) collective-permute-start(f32[8,64,448]{2,1,0:T(8,128)S(1)} %pad_maximum_fusion.1), channel_id=1, source_target_pairs={{1,0},{2,1},{3,2},{4,3},{5,4},{6,5},{7,6},{8,7},{9,8},{10,9},{11,1... | collective-permute-start | bytes 2752520 | tf_op jit(solution)/shard_map/ppermute | solution.py:27
  12.3 41.6 %collective-permute-start.4 = (bf16[256,1024]{1,0:T(8,128)(2,1)S(1)}, bf16[256,1024]{1,0:T(8,128)(2,1)S(1)}, u32[]{:S(2)}, u32[]{:S(2)}) collective-permute-start(bf16[256,1024]{1,0:T(8,128)(2,1)S(1)} %get-tuple-element.30), channel_id=1, source_target_pairs={{0,2},{1,3},{2,0},{3,1},{4,6},{5,7},{6,4},{7,5},{8,10},{9,11},{10,... | collective-permute-start | bytes 1572872 | tf_op jit(solution)/shard_map/ppermute | solution.py:40
  17.2 41.5 %collective-permute-start.5 = (bf16[256,1024]{1,0:T(8,128)(2,1)S(1)}, bf16[256,1024]{1,0:T(8,128)(2,1)S(1)}, u32[]{:S(2)}, u32[]{:S(2)}) collective-permute-start(bf16[256,1024]{1,0:T(8,128)(2,1)S(1)} %get-tuple-element.30), channel_id=1, source_target_pairs={{0,4},{1,5},{2,6},{3,7},{4,0},{5,1},{6,2},{7,3},{8,12},{9,13},{10,... | collective-permute-start | bytes 1572872 | tf_op jit(solution)/shard_map/ppermute | solution.py:40
  18.8 41.5 %collective-permute-start.6 = (bf16[256,1024]{1,0:T(8,128)(2,1)S(1)}, bf16[256,1024]{1,0:T(8,128)(2,1)S(1)}, u32[]{:S(2)}, u32[]{:S(2)}) collective-permute-start(bf16[256,1024]{1,0:T(8,128)(2,1)S(1)} %get-tuple-element.30), channel_id=1, source_target_pairs={{0,8},{1,9},{2,10},{3,11},{4,12},{5,13},{6,14},{7,15},{8,0},{9,1},... | collective-permute-start | bytes 1572872 | tf_op jit(solution)/shard_map/ppermute | solution.py:40
  22.2 1.1 copy-start.2
  27.9 25.2 %copy-start.6 = (f32[9]{0:T(128)S(1)}, f32[9]{0:T(128)}, u32[]{:S(2)}) copy-start(f32[9]{0:T(128)} %param.17) | copy-start | bytes 112
  29.2 33.7 %collective-permute-start.2 = (f32[8,64,256]{2,1,0:T(8,128)S(1)}, f32[8,64,256]{2,1,0:T(8,128)S(1)}, u32[]{:S(2)}, u32[]{:S(2)}) collective-permute-start(f32[8,64,256]{2,1,0:T(8,128)S(1)} %pad_maximum_fusion.4), channel_id=1, source_target_pairs={{0,1},{1,2},{2,3},{3,4},{4,5},{5,6},{6,7},{7,8},{8,9},{9,10},{10,1... | collective-permute-start | bytes 1572872 | tf_op jit(solution)/shard_map/ppermute | solution.py:27
  51.9 16.5 %collective-permute-start.3 = (f32[8,64,256]{2,1,0:T(8,128)S(1)}, f32[8,64,256]{2,1,0:T(8,128)S(1)}, u32[]{:S(2)}, u32[]{:S(2)}) collective-permute-start(f32[8,64,256]{2,1,0:T(8,128)S(1)} %pad_maximum_fusion.4), channel_id=1, source_target_pairs={{1,0},{2,1},{3,2},{4,3},{5,4},{6,5},{7,6},{8,7},{9,8},{10,9},{11,1... | collective-permute-start | bytes 1572872 | tf_op jit(solution)/shard_map/ppermute | solution.py:27
  53.9 28.2 %collective-permute-start.7 = (bf16[256,1024]{1,0:T(8,128)(2,1)S(1)}, bf16[256,1024]{1,0:T(8,128)(2,1)S(1)}, u32[]{:S(2)}, u32[]{:S(2)}) collective-permute-start(bf16[256,1024]{1,0:T(8,128)(2,1)S(1)} %get-tuple-element.29), channel_id=1, source_target_pairs={{0,2},{1,3},{2,0},{3,1},{4,6},{5,7},{6,4},{7,5},{8,10},{9,11},{10,... | collective-permute-start | bytes 1572872 | tf_op jit(solution)/shard_map/ppermute | solution.py:40
  58.7 27.9 %collective-permute-start.8 = (bf16[256,1024]{1,0:T(8,128)(2,1)S(1)}, bf16[256,1024]{1,0:T(8,128)(2,1)S(1)}, u32[]{:S(2)}, u32[]{:S(2)}) collective-permute-start(bf16[256,1024]{1,0:T(8,128)(2,1)S(1)} %get-tuple-element.29), channel_id=1, source_target_pairs={{0,4},{1,5},{2,6},{3,7},{4,0},{5,1},{6,2},{7,3},{8,12},{9,13},{10,... | collective-permute-start | bytes 1572872 | tf_op jit(solution)/shard_map/ppermute | solution.py:40
  60.2 26.3 %collective-permute-start.9 = (bf16[256,1024]{1,0:T(8,128)(2,1)S(1)}, bf16[256,1024]{1,0:T(8,128)(2,1)S(1)}, u32[]{:S(2)}, u32[]{:S(2)}) collective-permute-start(bf16[256,1024]{1,0:T(8,128)(2,1)S(1)} %get-tuple-element.29), channel_id=1, source_target_pairs={{0,8},{1,9},{2,10},{3,11},{4,12},{5,13},{6,14},{7,15},{8,0},{9,1},... | collective-permute-start | bytes 1572872 | tf_op jit(solution)/shard_map/ppermute | solution.py:40
  62.9 19.2 %collective-permute-start.10 = (bf16[128,1024]{1,0:T(8,128)(2,1)S(1)}, bf16[128,1024]{1,0:T(8,128)(2,1)S(1)}, u32[]{:S(2)}, u32[]{:S(2)}) collective-permute-start(bf16[128,1024]{1,0:T(8,128)(2,1)S(1)} %get-tuple-element.28), channel_id=1, source_target_pairs={{0,1},{1,2},{2,3},{3,4},{4,5},{5,6},{6,7},{7,8},{8,9},{9,10},{10,1... | collective-permute-start | bytes 786440 | tf_op jit(solution)/shard_map/ppermute | solution.py:27
  68.4 13.7 %collective-permute-start.11 = (bf16[128,1024]{1,0:T(8,128)(2,1)S(1)}, bf16[128,1024]{1,0:T(8,128)(2,1)S(1)}, u32[]{:S(2)}, u32[]{:S(2)}) collective-permute-start(bf16[128,1024]{1,0:T(8,128)(2,1)S(1)} %get-tuple-element.27), channel_id=1, source_target_pairs={{1,0},{2,1},{3,2},{4,3},{5,4},{6,5},{7,6},{8,7},{9,8},{10,9},{11,1... | collective-permute-start | bytes 786440 | tf_op jit(solution)/shard_map/ppermute | solution.py:27
  75.2 24.6 %copy-start.4 = (bf16[128,1024]{1,0:T(8,128)(2,1)S(1)}, bf16[128,1024]{1,0:T(8,128)(2,1)}, u32[]{:S(2)}) copy-start(bf16[128,1024]{1,0:T(8,128)(2,1)} %param.18) | copy-start | bytes 786436
  86.5 13.3 %collective-permute-start.12 = (bf16[128,128]{1,0:T(8,128)(2,1)S(1)}, bf16[128,128]{1,0:T(8,128)(2,1)S(1)}, u32[]{:S(2)}, u32[]{:S(2)}) collective-permute-start(bf16[128,128]{1,0:T(8,128)(2,1)S(1)} %get-tuple-element.32), channel_id=1, source_target_pairs={{0,1},{1,2},{2,3},{3,4},{4,5},{5,6},{6,7},{7,8},{8,9},{9,10},{10,1... | collective-permute-start | bytes 98312 | tf_op jit(solution)/shard_map/ppermute | solution.py:27
  87.8 14.5 %collective-permute-start.14 = (bf16[512,128]{1,0:T(8,128)(2,1)S(1)}, bf16[512,128]{1,0:T(8,128)(2,1)S(1)}, u32[]{:S(2)}, u32[]{:S(2)}) collective-permute-start(bf16[512,128]{1,0:T(8,128)(2,1)S(1)} %bitcast.226), channel_id=1, source_target_pairs={{0,2},{1,3},{2,0},{3,1},{4,6},{5,7},{6,4},{7,5},{8,10},{9,11},{10,... | collective-permute-start | bytes 393224 | tf_op jit(solution)/shard_map/ppermute | solution.py:40
  97.2 5.6 %collective-permute-start.15 = (bf16[512,128]{1,0:T(8,128)(2,1)S(1)}, bf16[512,128]{1,0:T(8,128)(2,1)S(1)}, u32[]{:S(2)}, u32[]{:S(2)}) collective-permute-start(bf16[512,128]{1,0:T(8,128)(2,1)S(1)} %bitcast.227), channel_id=1, source_target_pairs={{0,4},{1,5},{2,6},{3,7},{4,0},{5,1},{6,2},{7,3},{8,12},{9,13},{10,... | collective-permute-start | bytes 393224 | tf_op jit(solution)/shard_map/ppermute | solution.py:40
  98.3 9.8 %collective-permute-start.16 = (bf16[512,128]{1,0:T(8,128)(2,1)S(1)}, bf16[512,128]{1,0:T(8,128)(2,1)S(1)}, u32[]{:S(2)}, u32[]{:S(2)}) collective-permute-start(bf16[512,128]{1,0:T(8,128)(2,1)S(1)} %bitcast.228), channel_id=1, source_target_pairs={{0,8},{1,9},{2,10},{3,11},{4,12},{5,13},{6,14},{7,15},{8,0},{9,1},... | collective-permute-start | bytes 393224 | tf_op jit(solution)/shard_map/ppermute | solution.py:40
  98.3 3.8 %collective-permute-start.13 = (bf16[128,128]{1,0:T(8,128)(2,1)S(1)}, bf16[128,128]{1,0:T(8,128)(2,1)S(1)}, u32[]{:S(2)}, u32[]{:S(2)}) collective-permute-start(bf16[128,128]{1,0:T(8,128)(2,1)S(1)} %get-tuple-element.31), channel_id=1, source_target_pairs={{1,0},{2,1},{3,2},{4,3},{5,4},{6,5},{7,6},{8,7},{9,8},{10,9},{11,1... | collective-permute-start | bytes 98312 | tf_op jit(solution)/shard_map/ppermute | solution.py:27
  100.1 8.5 %slice-start = ((s8[6291456]{0:T(1024)(128)(4,1)}), s8[4194304]{0:T(1024)(128)(4,1)S(1)}, s32[]{:S(2)}) async-start(s8[6291456]{0:T(1024)(128)(4,1)} %bitcast.230), calls=%async_computation | async-start | bytes 8388608
  102.4 6.2 %slice-start.1 = ((s8[6291456]{0:T(1024)(128)(4,1)}), s8[2097152]{0:T(1024)(128)(4,1)S(1)}, s32[]{:S(2)}) async-start(s8[6291456]{0:T(1024)(128)(4,1)} %bitcast.230), calls=%async_computation.1 | async-start | bytes 4194304
  118.9 3.7 %copy-start.1 = (bf16[2304,2048]{1,0:T(8,128)(2,1)}, bf16[2304,2048]{1,0:T(8,128)(2,1)S(1)}, u32[]{:S(2)}) copy-start(bf16[2304,2048]{1,0:T(8,128)(2,1)S(1)} %convolution_convert_fusion.refs_0_.refs_1_.refs_2_.refs_3_.refs_5_.refs_6_.refs_7_) | copy-start | bytes 28311556
  122.6 1.8 %copy-start.7 = (s32[8,3]{0,1:T(4,128)S(1)}, s32[8,3]{0,1:T(4,128)}, u32[]{:S(2)}) copy-start(s32[8,3]{0,1:T(4,128)} %param.15) | copy-start | bytes 292
  122.6 1.8 %copy-start.8 = (s32[8,4]{0,1:T(4,128)S(1)}, s32[8,4]{0,1:T(4,128)}, u32[]{:S(2)}) copy-start(s32[8,4]{0,1:T(4,128)} %param.16) | copy-start | bytes 388
  122.6 2.0 %copy-start.9 = (s32[4]{0:T(128)S(1)}, s32[4]{0:T(128)}, u32[]{:S(2)}) copy-start(s32[4]{0:T(128)} %constant.58.clone) | copy-start | bytes 52
  124.0 11.3 %collective-permute-start.17 = (bf16[512,2048]{1,0:T(8,128)(2,1)}, bf16[512,2048]{1,0:T(8,128)(2,1)}, u32[]{:S(2)}, u32[]{:S(2)}) collective-permute-start(bf16[512,2048]{1,0:T(8,128)(2,1)} %slice.369), channel_id=1, source_target_pairs={{0,1},{1,0},{2,3},{3,2},{4,5},{5,4},{6,7},{7,6},{8,9},{9,8},{10,11... | collective-permute-start | bytes 6291464 | tf_op jit(solution)/shard_map/ppermute | solution.py:40

commit v11 on v10

--- a/solution.py
+++ b/solution.py
@@ -121,12 +121,22 @@
     out_ref = refs[NKEY]
     lane = lax.broadcasted_iota(jnp.int32, (1, 2 * HD), 1)
     low = lane < HD
+    row = lax.broadcasted_iota(jnp.int32, (BS, 2 * BS), 0)
+    col = lax.broadcasted_iota(jnp.int32, (BS, 2 * BS), 1)
+    spread = jnp.where(col % BS == row, 1.0 / HD**0.5, 0.0).astype(jnp.bfloat16)
+    d_head = lax.broadcasted_iota(jnp.int32, (2 * HD, 2 * BS), 0) // HD
+    j_head = lax.broadcasted_iota(jnp.int32, (2 * HD, 2 * BS), 1) // BS
+    same = d_head == j_head
     for pair in range(HEADS // 2):
         cols = slice(pair * 2 * HD, (pair + 1) * 2 * HD)
         vcols = slice(D + pair * 2 * HD, D + (pair + 1) * 2 * HD)
         ks = jnp.concatenate([r[:, cols] for r in kv_refs], axis=0)
         vs = jnp.concatenate([r[:, vcols] for r in kv_refs], axis=0)
-        scores = jnp.dot(ks, q_ref[0, pair], preferred_element_type=jnp.float32)
+        spread_q = lax.dot_general(
+            q_ref[:, cols], spread, (((0,), (0,)), ((), ())), preferred_element_type=jnp.float32
+        )
+        qbd = jnp.where(same, spread_q, 0.0).astype(jnp.bfloat16)
+        scores = jnp.dot(ks, qbd, preferred_element_type=jnp.float32)
         top = jnp.max(scores, axis=0, keepdims=True)
         expd = jnp.exp(scores - top)
         total = jnp.sum(expd, axis=0, keepdims=True)
@@ -138,22 +148,11 @@
         out_ref[:, cols] = merged.astype(jnp.bfloat16)
 
 
-def split_queries(queries):
-    count = queries.shape[0] // BS
-    pairs = HEADS // 2
-    qt = queries.reshape(count, BS, pairs, 2 * HD).transpose(0, 2, 3, 1)
-    qt = jnp.concatenate([qt, qt], axis=3)
-    d_head = lax.broadcasted_iota(jnp.int32, (2 * HD, 2 * BS), 0) // HD
-    j_head = lax.broadcasted_iota(jnp.int32, (2 * HD, 2 * BS), 1) // BS
-    scale = jnp.asarray(1.0 / HD**0.5, jnp.bfloat16)
-    return jnp.where(d_head == j_head, qt * scale, jnp.zeros_like(qt))
-
-
 def attend(queries, kv_sources, table):
     count = table.shape[0]
     pairs = HEADS // 2
-    in_specs = [pl.BlockSpec((1, pairs, 2 * HD, 2 * BS), lambda b, t: (b, 0, 0, 0))]
-    operands = [split_queries(queries)]
+    in_specs = [pl.BlockSpec((BS, D), lambda b, t: (b, 0))]
+    operands = [queries]
     for j, src in enumerate(kv_sources):
         in_specs.append(pl.BlockSpec((BS, 2 * D), lambda b, t, j=j: (t[b, j], 0)))
         operands.append(src)

time: 154 us -> 166 us (1.078)
  Pallas kernels: 14.8 us -> 33.5 us
  other arithmetic: 10.4 us -> 5.23 us
  local copies, waits for them, and re-layouts: 16.5 us -> 14.4 us
    pallas_call x1, Pallas kernels: 14.8 us -> 33.5 us  [attend(): pl.pallas_call(attention_kernel, grid_spec=grid_spec, out_shape=jax.Shape...]
    select_n x1 -> x0, other arithmetic: 5.06 us -> none  [split_queries(): return jnp.where(d_head == j_head, qt * scale, jnp.zeros_like(qt))]
    reshape x1 -> x0, local copies, waits for them, and re-layouts: 1.82 us -> none  [split_queries(): qt = queries.reshape(count, BS, pairs, 2 * HD).transpose(0, 2, 3, 1)]
    unnamed x60 -> x59, local copies, waits for them, and re-layouts: 7.15 us -> 6.86 us
  transfers between devices with their start and end apart: 18 -> 18, of which waited for: 3 -> 3; matrix products, arithmetic and copies ran while one was open for 21% -> 15% of each run, Pallas kernels for 0% -> 0%
where the time goes in v11:
time: 166 us
  starting transfers between devices  66.3 us (40%)
  matrix products  34.7 us (21%)
  Pallas kernels  33.5 us (20%)
  local copies, waits for them, and re-layouts  14.4 us (9%)
  waiting for transfers between devices  11 us (7%)
  other arithmetic  5.23 us (3%)
    ppermute x8, starting transfers between devices, shift_rows(): return lax.ppermute(x, axis, pairs)  37.5 us
    pallas_call x1, Pallas kernels, attend(): pl.pallas_call(attention_kernel, grid_spec=grid_spec, out_shape=jax.Shape...  33.5 us
    ppermute x10, starting transfers between devices, partner(): return lax.ppermute(value, axis, pairs)  28.8 us
    dot_general x8, matrix products, step(): jnp.einsum('wsk,wkc->wsc', bands[lo - REACH:hi - REACH], stacked, precisi...  15 us
    dot_general x1, matrix products, on_device(): jnp.dot(all_blended, kv_weight, preferred_element_type=jnp.float32)  10.3 us
    ppermute x10, waiting for transfers between devices, partner(): return lax.ppermute(value, axis, pairs)  9.4 us
    unnamed x59, local copies, waits for them, and re-layouts  6.86 us
    dot_general x1, matrix products, on_device(): jnp.dot(blended, qkv_weight[:, :D], preferred_element_type=jnp.float32)  3.81 us
  transfers between devices with their start and end apart: 18, of which 3 were waited for; matrix products, arithmetic and copies ran while one was open for 15% of the time, Pallas kernels for 0%

profile of v11, /device:TPU:0, one launch (start us, length us, event | category | flops | bytes accessed | tf_op | source)
XLA Modules:
  0.0 166.0 jit_solution(696124272160807864)
XLA Ops:
  0.0 0.9 copy.33
  1.1 2.8 %select_reduce_fusion = f32[8,5,64,64]{3,2,1,0:T(8,128)} fusion(f32[8,3,64,64]{3,2,1,0:T(8,128)} %param.13, pred[8,3,5]{2,1,0:T(4,128)(4,1)S(1)} %iota_compare_fusion), kind=kLoop, calls=%fused_computation.2 | loop fusion | flops 819200 | bytes 1048696 | tf_op jit(solution)/shard_map/reduce_sum | solution.py:61
  3.9 1.7 %copy.34 = f32[8,64,5,64]{1,3,2,0:T(8,128)S(1)} copy(f32[8,64,5,64]{3,1,2,0:T(8,128)} %bitcast.208) | data formatting | bytes 1310720 | tf_op jit(solution)/shard_map/transpose | solution.py:62
  5.6 1.3 copy.35
  7.0 1.4 pad_maximum_fusion.1
  8.4 2.6 %collective-permute-start = (f32[8,64,448]{2,1,0:T(8,128)S(1)}, f32[8,64,448]{2,1,0:T(8,128)S(1)}, u32[]{:S(2)}, u32[]{:S(2)}) collective-permute-start(f32[8,64,448]{2,1,0:T(8,128)S(1)} %pad_maximum_fusion.1), channel_id=1, source_target_pairs={{0,1},{1,2},{2,3},{3,4},{4,5},{5,6},{6,7},{7,8},{8,9},{9,10},{10,1... | collective-permute-start | bytes 2752520 | tf_op jit(solution)/shard_map/ppermute | solution.py:27
  10.9 1.3 collective-permute-start.1
  12.3 4.9 %collective-permute-start.4 = (bf16[256,1024]{1,0:T(8,128)(2,1)S(1)}, bf16[256,1024]{1,0:T(8,128)(2,1)S(1)}, u32[]{:S(2)}, u32[]{:S(2)}) collective-permute-start(bf16[256,1024]{1,0:T(8,128)(2,1)S(1)} %get-tuple-element.30), channel_id=1, source_target_pairs={{0,2},{1,3},{2,0},{3,1},{4,6},{5,7},{6,4},{7,5},{8,10},{9,11},{10,... | collective-permute-start | bytes 1572872 | tf_op jit(solution)/shard_map/ppermute | solution.py:40
  17.2 1.6 collective-permute-start.5
  18.8 2.6 %collective-permute-start.6 = (bf16[256,1024]{1,0:T(8,128)(2,1)S(1)}, bf16[256,1024]{1,0:T(8,128)(2,1)S(1)}, u32[]{:S(2)}, u32[]{:S(2)}) collective-permute-start(bf16[256,1024]{1,0:T(8,128)(2,1)S(1)} %get-tuple-element.30), channel_id=1, source_target_pairs={{0,8},{1,9},{2,10},{3,11},{4,12},{5,13},{6,14},{7,15},{8,0},{9,1},... | collective-permute-start | bytes 1572872 | tf_op jit(solution)/shard_map/ppermute | solution.py:40
  21.8 0.4 copy.37
  22.3 1.0 copy-done.2
  23.4 1.3 fusion.65
  25.1 1.2 fusion.16
  26.8 0.8 fusion.10
  28.0 1.2 fusion.13
  29.2 22.6 %collective-permute-start.2 = (f32[8,64,256]{2,1,0:T(8,128)S(1)}, f32[8,64,256]{2,1,0:T(8,128)S(1)}, u32[]{:S(2)}, u32[]{:S(2)}) collective-permute-start(f32[8,64,256]{2,1,0:T(8,128)S(1)} %pad_maximum_fusion.4), channel_id=1, source_target_pairs={{0,1},{1,2},{2,3},{3,4},{4,5},{5,6},{6,7},{7,8},{8,9},{9,10},{10,1... | collective-permute-start | bytes 1572872 | tf_op jit(solution)/shard_map/ppermute | solution.py:27
  51.9 1.3 collective-permute-start.3
  53.2 0.7 fusion.69
  53.9 4.8 %collective-permute-start.7 = (bf16[256,1024]{1,0:T(8,128)(2,1)S(1)}, bf16[256,1024]{1,0:T(8,128)(2,1)S(1)}, u32[]{:S(2)}, u32[]{:S(2)}) collective-permute-start(bf16[256,1024]{1,0:T(8,128)(2,1)S(1)} %get-tuple-element.29), channel_id=1, source_target_pairs={{0,2},{1,3},{2,0},{3,1},{4,6},{5,7},{6,4},{7,5},{8,10},{9,11},{10,... | collective-permute-start | bytes 1572872 | tf_op jit(solution)/shard_map/ppermute | solution.py:40
  58.7 1.6 collective-permute-start.8
  60.3 2.7 %collective-permute-start.9 = (bf16[256,1024]{1,0:T(8,128)(2,1)S(1)}, bf16[256,1024]{1,0:T(8,128)(2,1)S(1)}, u32[]{:S(2)}, u32[]{:S(2)}) collective-permute-start(bf16[256,1024]{1,0:T(8,128)(2,1)S(1)} %get-tuple-element.29), channel_id=1, source_target_pairs={{0,8},{1,9},{2,10},{3,11},{4,12},{5,13},{6,14},{7,15},{8,0},{9,1},... | collective-permute-start | bytes 1572872 | tf_op jit(solution)/shard_map/ppermute | solution.py:40
  62.9 5.5 %collective-permute-start.10 = (bf16[128,1024]{1,0:T(8,128)(2,1)S(1)}, bf16[128,1024]{1,0:T(8,128)(2,1)S(1)}, u32[]{:S(2)}, u32[]{:S(2)}) collective-permute-start(bf16[128,1024]{1,0:T(8,128)(2,1)S(1)} %get-tuple-element.28), channel_id=1, source_target_pairs={{0,1},{1,2},{2,3},{3,4},{4,5},{5,6},{6,7},{7,8},{8,9},{9,10},{10,1... | collective-permute-start | bytes 786440 | tf_op jit(solution)/shard_map/ppermute | solution.py:27
  68.4 1.5 collective-permute-start.11
  70.3 0.2 copy.42
  70.6 1.3 fusion.9
  72.4 1.2 fusion.17
  73.9 1.0 fusion.11
  75.2 6.9 %fusion.15 = bf16[8,64,128]{2,1,0:T(8,128)(2,1)S(1)} fusion(f32[8,64,320]{1,2,0:T(8,128)S(1)} %bitcast.205, f32[8,320,128]{2,1,0:T(8,128)S(1)} %bitcast.210, f32[20,64,128]{2,1,0:T(8,128)S(1)} %fusion.9, f32[20,64,128]{2,1,0:T(8,128)S(1)} %fusion.65, f32[16,64,128]{2,1,0:T(8,128)S(1)} %fusion.17, f32[8,64,128]{2,1,0:T(8,128)S(1)} %fusion.13, ...), kind=kOutput, calls=%fused_computation.28 | convolution fusion | flops 127139840 | bytes 4194340 | tf_op jit(solution)/shard_map/wsk,wkc->wsc/dot_general | solution.py:78
  82.1 4.5 %collective-permute-done.8 = bf16[256,1024]{1,0:T(8,128)(2,1)S(1)} collective-permute-done((bf16[256,1024]{1,0:T(8,128)(2,1)S(1)}, bf16[256,1024]{1,0:T(8,128)(2,1)S(1)}, u32[]{:S(2)}, u32[]{:S(2)}) %collective-permute-start.8) | collective-permute-done | bytes 524320 | tf_op jit(solution)/shard_map/ppermute | solution.py:40
  86.6 1.3 collective-permute-start.12
  87.9 9.3 %collective-permute-start.14 = (bf16[512,128]{1,0:T(8,128)(2,1)S(1)}, bf16[512,128]{1,0:T(8,128)(2,1)S(1)}, u32[]{:S(2)}, u32[]{:S(2)}) collective-permute-start(bf16[512,128]{1,0:T(8,128)(2,1)S(1)} %bitcast.219), channel_id=1, source_target_pairs={{0,2},{1,3},{2,0},{3,1},{4,6},{5,7},{6,4},{7,5},{8,10},{9,11},{10,... | collective-permute-start | bytes 393224 | tf_op jit(solution)/shard_map/ppermute | solution.py:40
  97.2 1.1 collective-permute-start.15
  98.3 1.5 collective-permute-start.13
  100.1 0.4 constant_dynamic-update-slice_fusion
  100.5 1.6 collective-permute-done.13
  102.3 0.4 fusion.3
  102.8 0.4 fusion.4
  103.2 4.9 %collective-permute-done.16 = bf16[512,128]{1,0:T(8,128)(2,1)S(1)} collective-permute-done((bf16[512,128]{1,0:T(8,128)(2,1)S(1)}, bf16[512,128]{1,0:T(8,128)(2,1)S(1)}, u32[]{:S(2)}, u32[]{:S(2)}) %collective-permute-start.16) | collective-permute-done | bytes 131104 | tf_op jit(solution)/shard_map/ppermute | solution.py:40
  108.1 0.4 fusion.5
  108.6 10.3 %convolution_convert_fusion.refs_0_.refs_1_.refs_2_.refs_3_.refs_5_.refs_6_.refs_7_ = bf16[2304,2048]{1,0:T(8,128)(2,1)S(1)} fusion(bf16[2304,1024]{1,0:T(8,128)(2,1)S(1)} %fusion.5, bf16[1024,3072]{1,0:T(8,128)(2,1)S(1)} %bitcast.224), kind=kOutput, calls=%fused_computation | convolution fusion | flops 9668395008 | bytes 18350080 | tf_op jit(solution)/shard_map/dot_general | solution.py:223
  118.9 3.6 %copy-done.1 = bf16[2304,2048]{1,0:T(8,128)(2,1)} copy-done((bf16[2304,2048]{1,0:T(8,128)(2,1)}, bf16[2304,2048]{1,0:T(8,128)(2,1)S(1)}, u32[]{:S(2)}) %copy-start.1) | copy-done | bytes 9437208
  122.5 1.5 slice.369
  124.1 0.3 collective-permute-start.17
  124.6 0.7 pad_add_fusion.table_ref
  125.2 3.8 %fusion.6.q_ref = bf16[512,1024]{1,0:T(8,128)(2,1)} fusion(bf16[512,1024]{1,0:T(8,128)(2,1)S(1)} %get-tuple-element.43, bf16[1024,3072]{1,0:T(8,128)(2,1)} %param.19), kind=kOutput, calls=%fused_computation.13 | convolution fusion | flops 1074266112 | bytes 4194304 | tf_op jit(solution)/shard_map/dot_general | solution.py:215
  129.0 33.5 %shard_map.109 = bf16[512,1024]{1,0:T(8,128)(2,1)} custom-call(s32[8,8]{1,0:T(8,128)} %pad_add_fusion.table_ref, bf16[512,1024]{1,0:T(8,128)(2,1)} %fusion.6.q_ref, bf16[2304,2048]{1,0:T(8,128)(2,1)} %copy-done.1, bf16[2304,2048]{1,0:T(8,128)(2,1)} %copy-done.1, bf16[2304,2048]{1,0:T(8,128)(2,1)} %copy-done.1, bf16[2304,2048]{1,0:T(8,128)(2,1)} %copy-done.1, ...), custom_call_target="tpu_custom_call" | custom-call | tf_op jit(solution)/shard_map/pallas_call | solution.py:165
  162.5 3.4 %convolution_convert_fusion.1 = bf16[512,1024]{1,0:T(8,128)(2,1)} fusion(bf16[512,1024]{1,0:T(8,128)(2,1)} %shard_map.109, bf16[1024,1024]{1,0:T(8,128)(2,1)S(1)} %copy-done), kind=kOutput, calls=%fused_computation.14 | convolution fusion | flops 1074266112 | bytes 4194304 | tf_op jit(solution)/shard_map/dot_general | solution.py:238
  (110 shorter events, 3.7 us)
Async XLA Ops:
  0.0 162.5 %copy-start = (bf16[1024,1024]{1,0:T(8,128)(2,1)S(1)}, bf16[1024,1024]{1,0:T(8,128)(2,1)}, u32[]{:S(2)}) copy-start(bf16[1024,1024]{1,0:T(8,128)(2,1)} %param.20) | copy-start | bytes 6291460
  7.0 5.3 %copy-start.3 = (bf16[512,1024]{1,0:T(8,128)(2,1)S(1)}, bf16[512,1024]{1,0:T(8,128)(2,1)}, u32[]{:S(2)}) copy-start(bf16[512,1024]{1,0:T(8,128)(2,1)} %param.11) | copy-start | bytes 3145732
  8.4 13.1 %copy-start.5 = (f32[512,128]{1,0:T(8,128)S(1)}, f32[512,128]{1,0:T(8,128)}, u32[]{:S(2)}) copy-start(f32[512,128]{1,0:T(8,128)} %param.12) | copy-start | bytes 786436
  8.4 13.0 %collective-permute-start = (f32[8,64,448]{2,1,0:T(8,128)S(1)}, f32[8,64,448]{2,1,0:T(8,128)S(1)}, u32[]{:S(2)}, u32[]{:S(2)}) collective-permute-start(f32[8,64,448]{2,1,0:T(8,128)S(1)} %pad_maximum_fusion.1), channel_id=1, source_target_pairs={{0,1},{1,2},{2,3},{3,4},{4,5},{5,6},{6,7},{7,8},{8,9},{9,10},{10,1... | collective-permute-start | bytes 2752520 | tf_op jit(solution)/shard_map/ppermute | solution.py:27
  10.9 10.5 %collective-permute-start.1 = (f32[8,64,448]{2,1,0:T(8,128)S(1)}, f32[8,64,448]{2,1,0:T(8,128)S(1)}, u32[]{:S(2)}, u32[]{:S(2)}) collective-permute-start(f32[8,64,448]{2,1,0:T(8,128)S(1)} %pad_maximum_fusion.1), channel_id=1, source_target_pairs={{1,0},{2,1},{3,2},{4,3},{5,4},{6,5},{7,6},{8,7},{9,8},{10,9},{11,1... | collective-permute-start | bytes 2752520 | tf_op jit(solution)/shard_map/ppermute | solution.py:27
  12.3 41.6 %collective-permute-start.4 = (bf16[256,1024]{1,0:T(8,128)(2,1)S(1)}, bf16[256,1024]{1,0:T(8,128)(2,1)S(1)}, u32[]{:S(2)}, u32[]{:S(2)}) collective-permute-start(bf16[256,1024]{1,0:T(8,128)(2,1)S(1)} %get-tuple-element.30), channel_id=1, source_target_pairs={{0,2},{1,3},{2,0},{3,1},{4,6},{5,7},{6,4},{7,5},{8,10},{9,11},{10,... | collective-permute-start | bytes 1572872 | tf_op jit(solution)/shard_map/ppermute | solution.py:40
  17.2 41.5 %collective-permute-start.5 = (bf16[256,1024]{1,0:T(8,128)(2,1)S(1)}, bf16[256,1024]{1,0:T(8,128)(2,1)S(1)}, u32[]{:S(2)}, u32[]{:S(2)}) collective-permute-start(bf16[256,1024]{1,0:T(8,128)(2,1)S(1)} %get-tuple-element.30), channel_id=1, source_target_pairs={{0,4},{1,5},{2,6},{3,7},{4,0},{5,1},{6,2},{7,3},{8,12},{9,13},{10,... | collective-permute-start | bytes 1572872 | tf_op jit(solution)/shard_map/ppermute | solution.py:40
  18.8 41.5 %collective-permute-start.6 = (bf16[256,1024]{1,0:T(8,128)(2,1)S(1)}, bf16[256,1024]{1,0:T(8,128)(2,1)S(1)}, u32[]{:S(2)}, u32[]{:S(2)}) collective-permute-start(bf16[256,1024]{1,0:T(8,128)(2,1)S(1)} %get-tuple-element.30), channel_id=1, source_target_pairs={{0,8},{1,9},{2,10},{3,11},{4,12},{5,13},{6,14},{7,15},{8,0},{9,1},... | collective-permute-start | bytes 1572872 | tf_op jit(solution)/shard_map/ppermute | solution.py:40
  22.2 1.1 copy-start.2
  28.0 25.2 %copy-start.6 = (f32[9]{0:T(128)S(1)}, f32[9]{0:T(128)}, u32[]{:S(2)}) copy-start(f32[9]{0:T(128)} %param.17) | copy-start | bytes 112
  29.2 33.7 %collective-permute-start.2 = (f32[8,64,256]{2,1,0:T(8,128)S(1)}, f32[8,64,256]{2,1,0:T(8,128)S(1)}, u32[]{:S(2)}, u32[]{:S(2)}) collective-permute-start(f32[8,64,256]{2,1,0:T(8,128)S(1)} %pad_maximum_fusion.4), channel_id=1, source_target_pairs={{0,1},{1,2},{2,3},{3,4},{4,5},{5,6},{6,7},{7,8},{8,9},{9,10},{10,1... | collective-permute-start | bytes 1572872 | tf_op jit(solution)/shard_map/ppermute | solution.py:27
  51.9 16.5 %collective-permute-start.3 = (f32[8,64,256]{2,1,0:T(8,128)S(1)}, f32[8,64,256]{2,1,0:T(8,128)S(1)}, u32[]{:S(2)}, u32[]{:S(2)}) collective-permute-start(f32[8,64,256]{2,1,0:T(8,128)S(1)} %pad_maximum_fusion.4), channel_id=1, source_target_pairs={{1,0},{2,1},{3,2},{4,3},{5,4},{6,5},{7,6},{8,7},{9,8},{10,9},{11,1... | collective-permute-start | bytes 1572872 | tf_op jit(solution)/shard_map/ppermute | solution.py:27
  53.9 28.2 %collective-permute-start.7 = (bf16[256,1024]{1,0:T(8,128)(2,1)S(1)}, bf16[256,1024]{1,0:T(8,128)(2,1)S(1)}, u32[]{:S(2)}, u32[]{:S(2)}) collective-permute-start(bf16[256,1024]{1,0:T(8,128)(2,1)S(1)} %get-tuple-element.29), channel_id=1, source_target_pairs={{0,2},{1,3},{2,0},{3,1},{4,6},{5,7},{6,4},{7,5},{8,10},{9,11},{10,... | collective-permute-start | bytes 1572872 | tf_op jit(solution)/shard_map/ppermute | solution.py:40
  58.7 27.9 %collective-permute-start.8 = (bf16[256,1024]{1,0:T(8,128)(2,1)S(1)}, bf16[256,1024]{1,0:T(8,128)(2,1)S(1)}, u32[]{:S(2)}, u32[]{:S(2)}) collective-permute-start(bf16[256,1024]{1,0:T(8,128)(2,1)S(1)} %get-tuple-element.29), channel_id=1, source_target_pairs={{0,4},{1,5},{2,6},{3,7},{4,0},{5,1},{6,2},{7,3},{8,12},{9,13},{10,... | collective-permute-start | bytes 1572872 | tf_op jit(solution)/shard_map/ppermute | solution.py:40
  60.3 26.3 %collective-permute-start.9 = (bf16[256,1024]{1,0:T(8,128)(2,1)S(1)}, bf16[256,1024]{1,0:T(8,128)(2,1)S(1)}, u32[]{:S(2)}, u32[]{:S(2)}) collective-permute-start(bf16[256,1024]{1,0:T(8,128)(2,1)S(1)} %get-tuple-element.29), channel_id=1, source_target_pairs={{0,8},{1,9},{2,10},{3,11},{4,12},{5,13},{6,14},{7,15},{8,0},{9,1},... | collective-permute-start | bytes 1572872 | tf_op jit(solution)/shard_map/ppermute | solution.py:40
  62.9 19.1 %collective-permute-start.10 = (bf16[128,1024]{1,0:T(8,128)(2,1)S(1)}, bf16[128,1024]{1,0:T(8,128)(2,1)S(1)}, u32[]{:S(2)}, u32[]{:S(2)}) collective-permute-start(bf16[128,1024]{1,0:T(8,128)(2,1)S(1)} %get-tuple-element.28), channel_id=1, source_target_pairs={{0,1},{1,2},{2,3},{3,4},{4,5},{5,6},{6,7},{7,8},{8,9},{9,10},{10,1... | collective-permute-start | bytes 786440 | tf_op jit(solution)/shard_map/ppermute | solution.py:27
  68.4 13.6 %collective-permute-start.11 = (bf16[128,1024]{1,0:T(8,128)(2,1)S(1)}, bf16[128,1024]{1,0:T(8,128)(2,1)S(1)}, u32[]{:S(2)}, u32[]{:S(2)}) collective-permute-start(bf16[128,1024]{1,0:T(8,128)(2,1)S(1)} %get-tuple-element.27), channel_id=1, source_target_pairs={{1,0},{2,1},{3,2},{4,3},{5,4},{6,5},{7,6},{8,7},{9,8},{10,9},{11,1... | collective-permute-start | bytes 786440 | tf_op jit(solution)/shard_map/ppermute | solution.py:27
  75.2 24.6 %copy-start.4 = (bf16[128,1024]{1,0:T(8,128)(2,1)S(1)}, bf16[128,1024]{1,0:T(8,128)(2,1)}, u32[]{:S(2)}) copy-start(bf16[128,1024]{1,0:T(8,128)(2,1)} %param.18) | copy-start | bytes 786436
  86.6 13.3 %collective-permute-start.12 = (bf16[128,128]{1,0:T(8,128)(2,1)S(1)}, bf16[128,128]{1,0:T(8,128)(2,1)S(1)}, u32[]{:S(2)}, u32[]{:S(2)}) collective-permute-start(bf16[128,128]{1,0:T(8,128)(2,1)S(1)} %get-tuple-element.32), channel_id=1, source_target_pairs={{0,1},{1,2},{2,3},{3,4},{4,5},{5,6},{6,7},{7,8},{8,9},{9,10},{10,1... | collective-permute-start | bytes 98312 | tf_op jit(solution)/shard_map/ppermute | solution.py:27
  87.9 14.5 %collective-permute-start.14 = (bf16[512,128]{1,0:T(8,128)(2,1)S(1)}, bf16[512,128]{1,0:T(8,128)(2,1)S(1)}, u32[]{:S(2)}, u32[]{:S(2)}) collective-permute-start(bf16[512,128]{1,0:T(8,128)(2,1)S(1)} %bitcast.219), channel_id=1, source_target_pairs={{0,2},{1,3},{2,0},{3,1},{4,6},{5,7},{6,4},{7,5},{8,10},{9,11},{10,... | collective-permute-start | bytes 393224 | tf_op jit(solution)/shard_map/ppermute | solution.py:40
  97.2 5.6 %collective-permute-start.15 = (bf16[512,128]{1,0:T(8,128)(2,1)S(1)}, bf16[512,128]{1,0:T(8,128)(2,1)S(1)}, u32[]{:S(2)}, u32[]{:S(2)}) collective-permute-start(bf16[512,128]{1,0:T(8,128)(2,1)S(1)} %bitcast.220), channel_id=1, source_target_pairs={{0,4},{1,5},{2,6},{3,7},{4,0},{5,1},{6,2},{7,3},{8,12},{9,13},{10,... | collective-permute-start | bytes 393224 | tf_op jit(solution)/shard_map/ppermute | solution.py:40
  98.3 9.8 %collective-permute-start.16 = (bf16[512,128]{1,0:T(8,128)(2,1)S(1)}, bf16[512,128]{1,0:T(8,128)(2,1)S(1)}, u32[]{:S(2)}, u32[]{:S(2)}) collective-permute-start(bf16[512,128]{1,0:T(8,128)(2,1)S(1)} %bitcast.221), channel_id=1, source_target_pairs={{0,8},{1,9},{2,10},{3,11},{4,12},{5,13},{6,14},{7,15},{8,0},{9,1},... | collective-permute-start | bytes 393224 | tf_op jit(solution)/shard_map/ppermute | solution.py:40
  98.3 3.8 %collective-permute-start.13 = (bf16[128,128]{1,0:T(8,128)(2,1)S(1)}, bf16[128,128]{1,0:T(8,128)(2,1)S(1)}, u32[]{:S(2)}, u32[]{:S(2)}) collective-permute-start(bf16[128,128]{1,0:T(8,128)(2,1)S(1)} %get-tuple-element.31), channel_id=1, source_target_pairs={{1,0},{2,1},{3,2},{4,3},{5,4},{6,5},{7,6},{8,7},{9,8},{10,9},{11,1... | collective-permute-start | bytes 98312 | tf_op jit(solution)/shard_map/ppermute | solution.py:27
  100.1 8.5 %slice-start = ((s8[6291456]{0:T(1024)(128)(4,1)}), s8[4194304]{0:T(1024)(128)(4,1)S(1)}, s32[]{:S(2)}) async-start(s8[6291456]{0:T(1024)(128)(4,1)} %bitcast.223), calls=%async_computation | async-start | bytes 8388608
  102.3 6.2 %slice-start.1 = ((s8[6291456]{0:T(1024)(128)(4,1)}), s8[2097152]{0:T(1024)(128)(4,1)S(1)}, s32[]{:S(2)}) async-start(s8[6291456]{0:T(1024)(128)(4,1)} %bitcast.223), calls=%async_computation.1 | async-start | bytes 4194304
  118.9 3.7 %copy-start.1 = (bf16[2304,2048]{1,0:T(8,128)(2,1)}, bf16[2304,2048]{1,0:T(8,128)(2,1)S(1)}, u32[]{:S(2)}) copy-start(bf16[2304,2048]{1,0:T(8,128)(2,1)S(1)} %convolution_convert_fusion.refs_0_.refs_1_.refs_2_.refs_3_.refs_5_.refs_6_.refs_7_) | copy-start | bytes 28311556
  122.5 1.8 %copy-start.7 = (s32[8,3]{0,1:T(4,128)S(1)}, s32[8,3]{0,1:T(4,128)}, u32[]{:S(2)}) copy-start(s32[8,3]{0,1:T(4,128)} %param.15) | copy-start | bytes 292
  122.5 1.9 %copy-start.8 = (s32[8,4]{0,1:T(4,128)S(1)}, s32[8,4]{0,1:T(4,128)}, u32[]{:S(2)}) copy-start(s32[8,4]{0,1:T(4,128)} %param.16) | copy-start | bytes 388
  122.5 2.0 %copy-start.9 = (s32[4]{0:T(128)S(1)}, s32[4]{0:T(128)}, u32[]{:S(2)}) copy-start(s32[4]{0:T(128)} %constant.5.clone) | copy-start | bytes 52
  124.1 5.0 %collective-permute-start.17 = (bf16[512,2048]{1,0:T(8,128)(2,1)}, bf16[512,2048]{1,0:T(8,128)(2,1)}, u32[]{:S(2)}, u32[]{:S(2)}) collective-permute-start(bf16[512,2048]{1,0:T(8,128)(2,1)} %slice.369), channel_id=1, source_target_pairs={{0,1},{1,0},{2,3},{3,2},{4,5},{5,4},{6,7},{7,6},{8,9},{9,8},{10,11... | collective-permute-start | bytes 6291464 | tf_op jit(solution)/shard_map/ppermute | solution.py:40

commit v12 on v10

--- a/solution.py
+++ b/solution.py
@@ -190,17 +190,18 @@
     bits = [link * (levels - 1) // (NEXP - 1) for link in range(NEXP)]
 
     half = rows // 2
-    early = [partner(node_feats[:half], "seq", bit) for bit in bits[1:]]
+    early = [partner(node_feats[:half], "seq", bit) for bit in bits[2:]]
     encoding, (early,) = chebyshev(
         struct_feats, op_blocks, laplace_index, series_coef, first_block, (), early,
     )
-    late = [partner(node_feats[half:], "seq", bit) for bit in bits[1:]]
+    late = [partner(node_feats[half:], "seq", bit) for bit in bits[2:]]
+    near_far = partner(node_feats, "seq", bits[1])
     feats_before = shift_rows(node_feats[rows - rim:], "seq", 1)
     feats_after = shift_rows(node_feats[:rim], "seq", -1)
-    encoding, late, feats_before, feats_after = lax.optimization_barrier(
-        (encoding, late, feats_before, feats_after)
-    )
-    feats_far = [jnp.concatenate([a, b], axis=0) for a, b in zip(early, late)]
+    encoding, late, near_far, feats_before, feats_after = lax.optimization_barrier(
+        (encoding, late, near_far, feats_before, feats_after)
+    )
+    feats_far = [near_far] + [jnp.concatenate([a, b], axis=0) for a, b in zip(early, late)]
     encoding_b = encoding.astype(jnp.bfloat16)
 
     enc_before = shift_rows(encoding_b[rows - rim:], "seq", 1)

time: 154 us -> 154 us (level)
  starting transfers between devices: 66.3 us -> 63 us
  waiting for transfers between devices: 11 us -> 13.3 us
    ppermute x8, starting transfers between devices: 37.5 us -> 25.4 us  [shift_rows(): return lax.ppermute(x, axis, pairs)]
    ppermute x10 -> x9, starting transfers between devices: 28.8 us -> 37.6 us  [partner(): return lax.ppermute(value, axis, pairs)]
    ppermute x10 -> x9, waiting for transfers between devices: 9.35 us -> 12.4 us  [partner(): return lax.ppermute(value, axis, pairs)]
  transfers between devices with their start and end apart: 18 -> 17, of which waited for: 3 -> 4; matrix products, arithmetic and copies ran while one was open for 21% -> 21% of each run, Pallas kernels for 0% -> 0%
where the time goes in v12:
time: 154 us; the launch traced here: 152 us
  starting transfers between devices  63 us (41%)
  matrix products  33.7 us (22%)
  local copies, waits for them, and re-layouts  16.5 us (11%)
  Pallas kernels  14.5 us (9%)
  waiting for transfers between devices  13.3 us (9%)
  other arithmetic  10.4 us (7%)
    ppermute x9, starting transfers between devices, partner(): return lax.ppermute(value, axis, pairs)  37.6 us
    ppermute x8, starting transfers between devices, shift_rows(): return lax.ppermute(x, axis, pairs)  25.4 us
    dot_general x8, matrix products, step(): jnp.einsum('wsk,wkc->wsc', bands[lo - REACH:hi - REACH], stacked, precisi...  15 us
    pallas_call x1, Pallas kernels, attend(): pl.pallas_call(attention_kernel, grid_spec=grid_spec, out_shape=jax.Shape...  14.5 us
    ppermute x9, waiting for transfers between devices, partner(): return lax.ppermute(value, axis, pairs)  12.4 us
    dot_general x1, matrix products, on_device(): jnp.dot(all_blended, kv_weight, preferred_element_type=jnp.float32)  10.3 us
    unnamed x60, local copies, waits for them, and re-layouts  7.17 us
    select_n x1, other arithmetic, split_queries(): return jnp.where(d_head == j_head, qt * scale, jnp.zeros_like(qt))  5.05 us
  transfers between devices with their start and end apart: 17, of which 4 were waited for; matrix products, arithmetic and copies ran while one was open for 21% of the time, Pallas kernels for 0%

profile of v12, /device:TPU:0, one launch (start us, length us, event | category | flops | bytes accessed | tf_op | source)
XLA Modules:
  0.0 152.3 jit_solution(12329827311016561842)
XLA Ops:
  0.0 0.9 copy.34
  1.1 2.8 %select_reduce_fusion = f32[8,5,64,64]{3,2,1,0:T(8,128)} fusion(f32[8,3,64,64]{3,2,1,0:T(8,128)} %param.13, pred[8,3,5]{2,1,0:T(4,128)(4,1)S(1)} %iota_compare_fusion), kind=kLoop, calls=%fused_computation.2 | loop fusion | flops 819200 | bytes 1048696 | tf_op jit(solution)/shard_map/reduce_sum | solution.py:61
  3.9 1.7 %copy.35 = f32[8,64,5,64]{1,3,2,0:T(8,128)S(1)} copy(f32[8,64,5,64]{3,1,2,0:T(8,128)} %bitcast.214) | data formatting | bytes 1310720 | tf_op jit(solution)/shard_map/transpose | solution.py:62
  5.6 1.3 copy.36
  7.0 1.4 pad_maximum_fusion.1
  8.4 2.6 %collective-permute-start = (f32[8,64,448]{2,1,0:T(8,128)S(1)}, f32[8,64,448]{2,1,0:T(8,128)S(1)}, u32[]{:S(2)}, u32[]{:S(2)}) collective-permute-start(f32[8,64,448]{2,1,0:T(8,128)S(1)} %pad_maximum_fusion.1), channel_id=1, source_target_pairs={{0,1},{1,2},{2,3},{3,4},{4,5},{5,6},{6,7},{7,8},{8,9},{9,10},{10,1... | collective-permute-start | bytes 2752520 | tf_op jit(solution)/shard_map/ppermute | solution.py:27
  10.9 1.3 collective-permute-start.1
  12.3 5.8 %collective-permute-start.4 = (bf16[256,1024]{1,0:T(8,128)(2,1)S(1)}, bf16[256,1024]{1,0:T(8,128)(2,1)S(1)}, u32[]{:S(2)}, u32[]{:S(2)}) collective-permute-start(bf16[256,1024]{1,0:T(8,128)(2,1)S(1)} %get-tuple-element.28), channel_id=1, source_target_pairs={{0,4},{1,5},{2,6},{3,7},{4,0},{5,1},{6,2},{7,3},{8,12},{9,13},{10,... | collective-permute-start | bytes 1572872 | tf_op jit(solution)/shard_map/ppermute | solution.py:40
  18.2 2.6 %collective-permute-start.5 = (bf16[256,1024]{1,0:T(8,128)(2,1)S(1)}, bf16[256,1024]{1,0:T(8,128)(2,1)S(1)}, u32[]{:S(2)}, u32[]{:S(2)}) collective-permute-start(bf16[256,1024]{1,0:T(8,128)(2,1)S(1)} %get-tuple-element.28), channel_id=1, source_target_pairs={{0,8},{1,9},{2,10},{3,11},{4,12},{5,13},{6,14},{7,15},{8,0},{9,1},... | collective-permute-start | bytes 1572872 | tf_op jit(solution)/shard_map/ppermute | solution.py:40
  21.2 0.4 copy.38
  21.8 1.0 copy-done.2
  22.8 1.3 fusion.69
  24.5 1.2 fusion.19
  26.2 0.8 fusion.13
  27.4 1.2 fusion.16
  28.6 10.7 %collective-permute-start.2 = (f32[8,64,256]{2,1,0:T(8,128)S(1)}, f32[8,64,256]{2,1,0:T(8,128)S(1)}, u32[]{:S(2)}, u32[]{:S(2)}) collective-permute-start(f32[8,64,256]{2,1,0:T(8,128)S(1)} %pad_maximum_fusion.4), channel_id=1, source_target_pairs={{0,1},{1,2},{2,3},{3,4},{4,5},{5,6},{6,7},{7,8},{8,9},{9,10},{10,1... | collective-permute-start | bytes 1572872 | tf_op jit(solution)/shard_map/ppermute | solution.py:27
  39.4 1.3 collective-permute-start.3
  40.7 14.3 %collective-permute-start.6 = (bf16[256,1024]{1,0:T(8,128)(2,1)S(1)}, bf16[256,1024]{1,0:T(8,128)(2,1)S(1)}, u32[]{:S(2)}, u32[]{:S(2)}) collective-permute-start(bf16[256,1024]{1,0:T(8,128)(2,1)S(1)} %get-tuple-element.27), channel_id=1, source_target_pairs={{0,4},{1,5},{2,6},{3,7},{4,0},{5,1},{6,2},{7,3},{8,12},{9,13},{10,... | collective-permute-start | bytes 1572872 | tf_op jit(solution)/shard_map/ppermute | solution.py:40
  55.0 0.7 fusion.73
  55.7 6.2 %collective-permute-start.7 = (bf16[256,1024]{1,0:T(8,128)(2,1)S(1)}, bf16[256,1024]{1,0:T(8,128)(2,1)S(1)}, u32[]{:S(2)}, u32[]{:S(2)}) collective-permute-start(bf16[256,1024]{1,0:T(8,128)(2,1)S(1)} %get-tuple-element.27), channel_id=1, source_target_pairs={{0,8},{1,9},{2,10},{3,11},{4,12},{5,13},{6,14},{7,15},{8,0},{9,1},... | collective-permute-start | bytes 1572872 | tf_op jit(solution)/shard_map/ppermute | solution.py:40
  62.0 1.3 collective-permute-start.10
  63.3 3.2 %collective-permute-start.9 = (bf16[128,1024]{1,0:T(8,128)(2,1)S(1)}, bf16[128,1024]{1,0:T(8,128)(2,1)S(1)}, u32[]{:S(2)}, u32[]{:S(2)}) collective-permute-start(bf16[128,1024]{1,0:T(8,128)(2,1)S(1)} %get-tuple-element.26), channel_id=1, source_target_pairs={{0,1},{1,2},{2,3},{3,4},{4,5},{5,6},{6,7},{7,8},{8,9},{9,10},{10,1... | collective-permute-start | bytes 786440 | tf_op jit(solution)/shard_map/ppermute | solution.py:27
  67.2 1.3 fusion.12
  69.0 1.3 fusion.20
  70.7 0.9 fusion.14
  71.9 6.9 %fusion.18 = bf16[8,64,128]{2,1,0:T(8,128)(2,1)S(1)} fusion(f32[8,64,320]{1,2,0:T(8,128)S(1)} %bitcast.210, f32[8,320,128]{2,1,0:T(8,128)S(1)} %bitcast.216, f32[20,64,128]{2,1,0:T(8,128)S(1)} %fusion.12, f32[20,64,128]{2,1,0:T(8,128)S(1)} %fusion.69, f32[16,64,128]{2,1,0:T(8,128)S(1)} %fusion.20, f32[8,64,128]{2,1,0:T(8,128)S(1)} %fusion.16, ...), kind=kOutput, calls=%fused_computation.30 | convolution fusion | flops 127139840 | bytes 4194340 | tf_op jit(solution)/shard_map/wsk,wkc->wsc/dot_general | solution.py:78
  78.8 2.7 %collective-permute-done.6 = bf16[256,1024]{1,0:T(8,128)(2,1)S(1)} collective-permute-done((bf16[256,1024]{1,0:T(8,128)(2,1)S(1)}, bf16[256,1024]{1,0:T(8,128)(2,1)S(1)}, u32[]{:S(2)}, u32[]{:S(2)}) %collective-permute-start.6) | collective-permute-done | bytes 524320 | tf_op jit(solution)/shard_map/ppermute | solution.py:40
  81.5 9.3 %collective-permute-done.8 = bf16[512,1024]{1,0:T(8,128)(2,1)S(1)} collective-permute-done((bf16[512,1024]{1,0:T(8,128)(2,1)S(1)}, bf16[512,1024]{1,0:T(8,128)(2,1)S(1)}, u32[]{:S(2)}, u32[]{:S(2)}) %collective-permute-start.8) | collective-permute-done | bytes 1048608 | tf_op jit(solution)/shard_map/ppermute | solution.py:40
  90.7 3.5 %collective-permute-start.11 = (bf16[128,128]{1,0:T(8,128)(2,1)S(1)}, bf16[128,128]{1,0:T(8,128)(2,1)S(1)}, u32[]{:S(2)}, u32[]{:S(2)}) collective-permute-start(bf16[128,128]{1,0:T(8,128)(2,1)S(1)} %get-tuple-element.30), channel_id=1, source_target_pairs={{0,1},{1,2},{2,3},{3,4},{4,5},{5,6},{6,7},{7,8},{8,9},{9,10},{10,1... | collective-permute-start | bytes 98312 | tf_op jit(solution)/shard_map/ppermute | solution.py:27
  94.2 2.4 %collective-permute-start.13 = (bf16[512,128]{1,0:T(8,128)(2,1)S(1)}, bf16[512,128]{1,0:T(8,128)(2,1)S(1)}, u32[]{:S(2)}, u32[]{:S(2)}) collective-permute-start(bf16[512,128]{1,0:T(8,128)(2,1)S(1)} %bitcast.226), channel_id=1, source_target_pairs={{0,2},{1,3},{2,0},{3,1},{4,6},{5,7},{6,4},{7,5},{8,10},{9,11},{10,... | collective-permute-start | bytes 393224 | tf_op jit(solution)/shard_map/ppermute | solution.py:40
  96.7 0.9 collective-permute-start.14
  97.6 3.3 %collective-permute-start.15 = (bf16[512,128]{1,0:T(8,128)(2,1)S(1)}, bf16[512,128]{1,0:T(8,128)(2,1)S(1)}, u32[]{:S(2)}, u32[]{:S(2)}) collective-permute-start(bf16[512,128]{1,0:T(8,128)(2,1)S(1)} %bitcast.228), channel_id=1, source_target_pairs={{0,8},{1,9},{2,10},{3,11},{4,12},{5,13},{6,14},{7,15},{8,0},{9,1},... | collective-permute-start | bytes 393224 | tf_op jit(solution)/shard_map/ppermute | solution.py:40
  100.9 1.5 collective-permute-start.12
  102.7 0.4 constant_dynamic-update-slice_fusion
  103.1 0.9 collective-permute-done.12
  104.2 0.4 fusion.21
  105.1 0.4 fusion.4
  105.5 0.4 fusion.5
  106.0 10.3 %convolution_convert_fusion.refs_0_.refs_1_.refs_2_.refs_3_.refs_5_.refs_6_.refs_7_ = bf16[2304,2048]{1,0:T(8,128)(2,1)S(1)} fusion(bf16[2304,1024]{1,0:T(8,128)(2,1)S(1)} %fusion.5, bf16[1024,3072]{1,0:T(8,128)(2,1)S(1)} %bitcast.231), kind=kOutput, calls=%fused_computation | convolution fusion | flops 9668395008 | bytes 18350080 | tf_op jit(solution)/shard_map/dot_general | solution.py:225
  116.3 3.6 %copy-done.1 = bf16[2304,2048]{1,0:T(8,128)(2,1)} copy-done((bf16[2304,2048]{1,0:T(8,128)(2,1)}, bf16[2304,2048]{1,0:T(8,128)(2,1)S(1)}, u32[]{:S(2)}) %copy-start.1) | copy-done | bytes 9437208
  119.9 1.5 slice.367
  121.4 1.9 %collective-permute-start.16 = (bf16[512,2048]{1,0:T(8,128)(2,1)}, bf16[512,2048]{1,0:T(8,128)(2,1)}, u32[]{:S(2)}, u32[]{:S(2)}) collective-permute-start(bf16[512,2048]{1,0:T(8,128)(2,1)} %slice.367), channel_id=1, source_target_pairs={{0,1},{1,0},{2,3},{3,2},{4,5},{5,4},{6,7},{7,6},{8,9},{9,8},{10,11... | collective-permute-start | bytes 6291464 | tf_op jit(solution)/shard_map/ppermute | solution.py:40
  123.5 0.7 pad_add_fusion.table_ref
  124.3 2.8 %fusion.9 = bf16[64,8,8,128]{3,1,2,0:T(8,128)(2,1)S(1)} fusion(bf16[512,1024]{1,0:T(8,128)(2,1)S(1)} %get-tuple-element.41, bf16[1024,3072]{1,0:T(8,128)(2,1)} %param.19), kind=kOutput, calls=%fused_computation.16 | convolution fusion | flops 1074266112 | bytes 4194304 | tf_op jit(solution)/shard_map/dot_general | solution.py:217
  127.4 1.8 %copy.48 = bf16[8,64,8,128]{1,3,2,0:T(8,128)(2,1)} copy(bf16[8,64,8,128]{3,2,1,0:T(8,128)(2,1)S(1)} %bitcast.217) | data formatting | bytes 2097152 | tf_op jit(solution)/shard_map/reshape | solution.py:144
  129.3 5.0 %fusion.1.q_ref = bf16[8,8,128,128]{3,2,1,0:T(8,128)(2,1)} fusion(bf16[8,8,128,64]{3,2,1,0:T(8,128)(2,1)} %bitcast.213, pred[128,128]{1,0:T(8,128)(4,1)S(1)} %select_compare_fusion), kind=kLoop, calls=%fused_computation.4 | loop fusion | flops 7340032 | bytes 3162112 | tf_op jit(solution)/shard_map/jit(_where)/select_n | solution.py:149
  134.3 14.5 %shard_map.109 = bf16[512,1024]{1,0:T(8,128)(2,1)} custom-call(s32[8,8]{1,0:T(8,128)} %pad_add_fusion.table_ref, bf16[8,8,128,128]{3,2,1,0:T(8,128)(2,1)} %fusion.1.q_ref, bf16[2304,2048]{1,0:T(8,128)(2,1)} %copy-done.1, bf16[2304,2048]{1,0:T(8,128)(2,1)} %copy-done.1, bf16[2304,2048]{1,0:T(8,128)(2,1)} %copy-done.1, bf16[2304,2048]{1,0:T(8,128)(2,1)} %copy-done.1, ...), custom_call_target="tpu_custom_call" | custom-call | tf_op jit(solution)/shard_map/pallas_call | solution.py:166
  148.8 3.4 %convolution_convert_fusion.1 = bf16[512,1024]{1,0:T(8,128)(2,1)} fusion(bf16[512,1024]{1,0:T(8,128)(2,1)} %shard_map.109, bf16[1024,1024]{1,0:T(8,128)(2,1)S(1)} %copy-done), kind=kOutput, calls=%fused_computation.15 | convolution fusion | flops 1074266112 | bytes 4194304 | tf_op jit(solution)/shard_map/dot_general | solution.py:240
  (114 shorter events, 4.9 us)
Async XLA Ops:
  0.0 148.8 %copy-start = (bf16[1024,1024]{1,0:T(8,128)(2,1)S(1)}, bf16[1024,1024]{1,0:T(8,128)(2,1)}, u32[]{:S(2)}) copy-start(bf16[1024,1024]{1,0:T(8,128)(2,1)} %param.20) | copy-start | bytes 6291460
  7.0 5.3 %copy-start.3 = (bf16[512,1024]{1,0:T(8,128)(2,1)S(1)}, bf16[512,1024]{1,0:T(8,128)(2,1)}, u32[]{:S(2)}) copy-start(bf16[512,1024]{1,0:T(8,128)(2,1)} %param.11) | copy-start | bytes 3145732
  8.4 12.5 %copy-start.5 = (f32[512,128]{1,0:T(8,128)S(1)}, f32[512,128]{1,0:T(8,128)}, u32[]{:S(2)}) copy-start(f32[512,128]{1,0:T(8,128)} %param.12) | copy-start | bytes 786436
  8.4 12.4 %collective-permute-start = (f32[8,64,448]{2,1,0:T(8,128)S(1)}, f32[8,64,448]{2,1,0:T(8,128)S(1)}, u32[]{:S(2)}, u32[]{:S(2)}) collective-permute-start(f32[8,64,448]{2,1,0:T(8,128)S(1)} %pad_maximum_fusion.1), channel_id=1, source_target_pairs={{0,1},{1,2},{2,3},{3,4},{4,5},{5,6},{6,7},{7,8},{8,9},{9,10},{10,1... | collective-permute-start | bytes 2752520 | tf_op jit(solution)/shard_map/ppermute | solution.py:27
  10.9 9.9 %collective-permute-start.1 = (f32[8,64,448]{2,1,0:T(8,128)S(1)}, f32[8,64,448]{2,1,0:T(8,128)S(1)}, u32[]{:S(2)}, u32[]{:S(2)}) collective-permute-start(f32[8,64,448]{2,1,0:T(8,128)S(1)} %pad_maximum_fusion.1), channel_id=1, source_target_pairs={{1,0},{2,1},{3,2},{4,3},{5,4},{6,5},{7,6},{8,7},{9,8},{10,9},{11,1... | collective-permute-start | bytes 2752520 | tf_op jit(solution)/shard_map/ppermute | solution.py:27
  12.3 43.4 %collective-permute-start.4 = (bf16[256,1024]{1,0:T(8,128)(2,1)S(1)}, bf16[256,1024]{1,0:T(8,128)(2,1)S(1)}, u32[]{:S(2)}, u32[]{:S(2)}) collective-permute-start(bf16[256,1024]{1,0:T(8,128)(2,1)S(1)} %get-tuple-element.28), channel_id=1, source_target_pairs={{0,4},{1,5},{2,6},{3,7},{4,0},{5,1},{6,2},{7,3},{8,12},{9,13},{10,... | collective-permute-start | bytes 1572872 | tf_op jit(solution)/shard_map/ppermute | solution.py:40
  18.2 43.8 %collective-permute-start.5 = (bf16[256,1024]{1,0:T(8,128)(2,1)S(1)}, bf16[256,1024]{1,0:T(8,128)(2,1)S(1)}, u32[]{:S(2)}, u32[]{:S(2)}) collective-permute-start(bf16[256,1024]{1,0:T(8,128)(2,1)S(1)} %get-tuple-element.28), channel_id=1, source_target_pairs={{0,8},{1,9},{2,10},{3,11},{4,12},{5,13},{6,14},{7,15},{8,0},{9,1},... | collective-permute-start | bytes 1572872 | tf_op jit(solution)/shard_map/ppermute | solution.py:40
  21.6 1.1 copy-start.2
  27.4 27.6 %copy-start.6 = (f32[9]{0:T(128)S(1)}, f32[9]{0:T(128)}, u32[]{:S(2)}) copy-start(f32[9]{0:T(128)} %param.17) | copy-start | bytes 112
  28.6 33.3 %collective-permute-start.2 = (f32[8,64,256]{2,1,0:T(8,128)S(1)}, f32[8,64,256]{2,1,0:T(8,128)S(1)}, u32[]{:S(2)}, u32[]{:S(2)}) collective-permute-start(f32[8,64,256]{2,1,0:T(8,128)S(1)} %pad_maximum_fusion.4), channel_id=1, source_target_pairs={{0,1},{1,2},{2,3},{3,4},{4,5},{5,6},{6,7},{7,8},{8,9},{9,10},{10,1... | collective-permute-start | bytes 1572872 | tf_op jit(solution)/shard_map/ppermute | solution.py:27
  39.4 23.9 %collective-permute-start.3 = (f32[8,64,256]{2,1,0:T(8,128)S(1)}, f32[8,64,256]{2,1,0:T(8,128)S(1)}, u32[]{:S(2)}, u32[]{:S(2)}) collective-permute-start(f32[8,64,256]{2,1,0:T(8,128)S(1)} %pad_maximum_fusion.4), channel_id=1, source_target_pairs={{1,0},{2,1},{3,2},{4,3},{5,4},{6,5},{7,6},{8,7},{9,8},{10,9},{11,1... | collective-permute-start | bytes 1572872 | tf_op jit(solution)/shard_map/ppermute | solution.py:27
  40.7 40.8 %collective-permute-start.6 = (bf16[256,1024]{1,0:T(8,128)(2,1)S(1)}, bf16[256,1024]{1,0:T(8,128)(2,1)S(1)}, u32[]{:S(2)}, u32[]{:S(2)}) collective-permute-start(bf16[256,1024]{1,0:T(8,128)(2,1)S(1)} %get-tuple-element.27), channel_id=1, source_target_pairs={{0,4},{1,5},{2,6},{3,7},{4,0},{5,1},{6,2},{7,3},{8,12},{9,13},{10,... | collective-permute-start | bytes 1572872 | tf_op jit(solution)/shard_map/ppermute | solution.py:40
  55.7 25.7 %collective-permute-start.7 = (bf16[256,1024]{1,0:T(8,128)(2,1)S(1)}, bf16[256,1024]{1,0:T(8,128)(2,1)S(1)}, u32[]{:S(2)}, u32[]{:S(2)}) collective-permute-start(bf16[256,1024]{1,0:T(8,128)(2,1)S(1)} %get-tuple-element.27), channel_id=1, source_target_pairs={{0,8},{1,9},{2,10},{3,11},{4,12},{5,13},{6,14},{7,15},{8,0},{9,1},... | collective-permute-start | bytes 1572872 | tf_op jit(solution)/shard_map/ppermute | solution.py:40
  62.0 28.8 %collective-permute-start.8 = (bf16[512,1024]{1,0:T(8,128)(2,1)S(1)}, bf16[512,1024]{1,0:T(8,128)(2,1)S(1)}, u32[]{:S(2)}, u32[]{:S(2)}) collective-permute-start(bf16[512,1024]{1,0:T(8,128)(2,1)S(1)} %copy-done.3), channel_id=1, source_target_pairs={{0,2},{1,3},{2,0},{3,1},{4,6},{5,7},{6,4},{7,5},{8,10},{9,11},{10,... | collective-permute-start | bytes 3145736 | tf_op jit(solution)/shard_map/ppermute | solution.py:40
  62.0 16.8 %collective-permute-start.10 = (bf16[128,1024]{1,0:T(8,128)(2,1)S(1)}, bf16[128,1024]{1,0:T(8,128)(2,1)S(1)}, u32[]{:S(2)}, u32[]{:S(2)}) collective-permute-start(bf16[128,1024]{1,0:T(8,128)(2,1)S(1)} %get-tuple-element.25), channel_id=1, source_target_pairs={{1,0},{2,1},{3,2},{4,3},{5,4},{6,5},{7,6},{8,7},{9,8},{10,9},{11,1... | collective-permute-start | bytes 786440 | tf_op jit(solution)/shard_map/ppermute | solution.py:27
  63.3 15.5 %collective-permute-start.9 = (bf16[128,1024]{1,0:T(8,128)(2,1)S(1)}, bf16[128,1024]{1,0:T(8,128)(2,1)S(1)}, u32[]{:S(2)}, u32[]{:S(2)}) collective-permute-start(bf16[128,1024]{1,0:T(8,128)(2,1)S(1)} %get-tuple-element.26), channel_id=1, source_target_pairs={{0,1},{1,2},{2,3},{3,4},{4,5},{5,6},{6,7},{7,8},{8,9},{9,10},{10,1... | collective-permute-start | bytes 786440 | tf_op jit(solution)/shard_map/ppermute | solution.py:27
  71.9 30.6 %copy-start.4 = (bf16[128,1024]{1,0:T(8,128)(2,1)S(1)}, bf16[128,1024]{1,0:T(8,128)(2,1)}, u32[]{:S(2)}) copy-start(bf16[128,1024]{1,0:T(8,128)(2,1)} %param.18) | copy-start | bytes 786436
  90.7 11.7 %collective-permute-start.11 = (bf16[128,128]{1,0:T(8,128)(2,1)S(1)}, bf16[128,128]{1,0:T(8,128)(2,1)S(1)}, u32[]{:S(2)}, u32[]{:S(2)}) collective-permute-start(bf16[128,128]{1,0:T(8,128)(2,1)S(1)} %get-tuple-element.30), channel_id=1, source_target_pairs={{0,1},{1,2},{2,3},{3,4},{4,5},{5,6},{6,7},{7,8},{8,9},{9,10},{10,1... | collective-permute-start | bytes 98312 | tf_op jit(solution)/shard_map/ppermute | solution.py:27
  94.2 10.0 %collective-permute-start.13 = (bf16[512,128]{1,0:T(8,128)(2,1)S(1)}, bf16[512,128]{1,0:T(8,128)(2,1)S(1)}, u32[]{:S(2)}, u32[]{:S(2)}) collective-permute-start(bf16[512,128]{1,0:T(8,128)(2,1)S(1)} %bitcast.226), channel_id=1, source_target_pairs={{0,2},{1,3},{2,0},{3,1},{4,6},{5,7},{6,4},{7,5},{8,10},{9,11},{10,... | collective-permute-start | bytes 393224 | tf_op jit(solution)/shard_map/ppermute | solution.py:40
  96.7 8.4 %collective-permute-start.14 = (bf16[512,128]{1,0:T(8,128)(2,1)S(1)}, bf16[512,128]{1,0:T(8,128)(2,1)S(1)}, u32[]{:S(2)}, u32[]{:S(2)}) collective-permute-start(bf16[512,128]{1,0:T(8,128)(2,1)S(1)} %bitcast.227), channel_id=1, source_target_pairs={{0,4},{1,5},{2,6},{3,7},{4,0},{5,1},{6,2},{7,3},{8,12},{9,13},{10,... | collective-permute-start | bytes 393224 | tf_op jit(solution)/shard_map/ppermute | solution.py:40
  97.6 7.9 %collective-permute-start.15 = (bf16[512,128]{1,0:T(8,128)(2,1)S(1)}, bf16[512,128]{1,0:T(8,128)(2,1)S(1)}, u32[]{:S(2)}, u32[]{:S(2)}) collective-permute-start(bf16[512,128]{1,0:T(8,128)(2,1)S(1)} %bitcast.228), channel_id=1, source_target_pairs={{0,8},{1,9},{2,10},{3,11},{4,12},{5,13},{6,14},{7,15},{8,0},{9,1},... | collective-permute-start | bytes 393224 | tf_op jit(solution)/shard_map/ppermute | solution.py:40
  100.9 3.1 %collective-permute-start.12 = (bf16[128,128]{1,0:T(8,128)(2,1)S(1)}, bf16[128,128]{1,0:T(8,128)(2,1)S(1)}, u32[]{:S(2)}, u32[]{:S(2)}) collective-permute-start(bf16[128,128]{1,0:T(8,128)(2,1)S(1)} %get-tuple-element.29), channel_id=1, source_target_pairs={{1,0},{2,1},{3,2},{4,3},{5,4},{6,5},{7,6},{8,7},{9,8},{10,9},{11,1... | collective-permute-start | bytes 98312 | tf_op jit(solution)/shard_map/ppermute | solution.py:27
  102.7 3.3 %slice-start = ((s8[6291456]{0:T(1024)(128)(4,1)}), s8[4194304]{0:T(1024)(128)(4,1)S(1)}, s32[]{:S(2)}) async-start(s8[6291456]{0:T(1024)(128)(4,1)} %bitcast.230), calls=%async_computation | async-start | bytes 8388608
  104.2 1.8 %slice-start.1 = ((s8[6291456]{0:T(1024)(128)(4,1)}), s8[2097152]{0:T(1024)(128)(4,1)S(1)}, s32[]{:S(2)}) async-start(s8[6291456]{0:T(1024)(128)(4,1)} %bitcast.230), calls=%async_computation.1 | async-start | bytes 4194304
  116.3 3.7 %copy-start.1 = (bf16[2304,2048]{1,0:T(8,128)(2,1)}, bf16[2304,2048]{1,0:T(8,128)(2,1)S(1)}, u32[]{:S(2)}) copy-start(bf16[2304,2048]{1,0:T(8,128)(2,1)S(1)} %convolution_convert_fusion.refs_0_.refs_1_.refs_2_.refs_3_.refs_5_.refs_6_.refs_7_) | copy-start | bytes 28311556
  119.9 3.4 %copy-start.7 = (s32[8,3]{0,1:T(4,128)S(1)}, s32[8,3]{0,1:T(4,128)}, u32[]{:S(2)}) copy-start(s32[8,3]{0,1:T(4,128)} %param.15) | copy-start | bytes 292
  119.9 3.5 %copy-start.8 = (s32[8,4]{0,1:T(4,128)S(1)}, s32[8,4]{0,1:T(4,128)}, u32[]{:S(2)}) copy-start(s32[8,4]{0,1:T(4,128)} %param.16) | copy-start | bytes 388
  119.9 3.6 %copy-start.9 = (s32[4]{0:T(128)S(1)}, s32[4]{0:T(128)}, u32[]{:S(2)}) copy-start(s32[4]{0:T(128)} %constant.58.clone) | copy-start | bytes 52
  121.4 12.9 %collective-permute-start.16 = (bf16[512,2048]{1,0:T(8,128)(2,1)}, bf16[512,2048]{1,0:T(8,128)(2,1)}, u32[]{:S(2)}, u32[]{:S(2)}) collective-permute-start(bf16[512,2048]{1,0:T(8,128)(2,1)} %slice.367), channel_id=1, source_target_pairs={{0,1},{1,0},{2,3},{3,2},{4,5},{5,4},{6,7},{7,6},{8,9},{9,8},{10,11... | collective-permute-start | bytes 6291464 | tf_op jit(solution)/shard_map/ppermute | solution.py:40

commit v13 on v12

--- a/solution.py
+++ b/solution.py
@@ -196,16 +196,10 @@
     )
     late = [partner(node_feats[half:], "seq", bit) for bit in bits[2:]]
     near_far = partner(node_feats, "seq", bits[1])
-    feats_before = shift_rows(node_feats[rows - rim:], "seq", 1)
-    feats_after = shift_rows(node_feats[:rim], "seq", -1)
-    encoding, late, near_far, feats_before, feats_after = lax.optimization_barrier(
-        (encoding, late, near_far, feats_before, feats_after)
-    )
+    encoding, late, near_far = lax.optimization_barrier((encoding, late, near_far))
     feats_far = [near_far] + [jnp.concatenate([a, b], axis=0) for a, b in zip(early, late)]
     encoding_b = encoding.astype(jnp.bfloat16)
 
-    enc_before = shift_rows(encoding_b[rows - rim:], "seq", 1)
-    enc_after = shift_rows(encoding_b[:rim], "seq", -1)
     enc_far = [partner(encoding_b, "seq", bit) for bit in bits[1:]]
 
     def blend(feats, enc):
@@ -218,7 +212,7 @@
         jnp.bfloat16
     )
     all_blended = jnp.concatenate(
-        [blend(feats_before, enc_before), blended, blend(feats_after, enc_after)]
+        [shift_rows(blended[rows - rim:], "seq", 1), blended, shift_rows(blended[:rim], "seq", -1)]
         + [blend(f, e) for f, e in zip(feats_far, enc_far)],
         axis=0,
     )

time: 154 us -> 154 us (level)
  the two profiles are of different devices: /device:TPU:0 before, /device:TPU:13 now
where the time goes in v13:
time: 154 us; the launch traced here: 153 us
  starting transfers between devices  39.2 us (25%)
  waiting for transfers between devices  38.3 us (25%)
  matrix products  33.4 us (22%)
  local copies, waits for them, and re-layouts  16.4 us (11%)
  Pallas kernels  14.7 us (10%)
  other arithmetic  10.5 us (7%)
    ppermute x6, waiting for transfers between devices, shift_rows(): return lax.ppermute(x, axis, pairs)  26.2 us
    ppermute x9, starting transfers between devices, partner(): return lax.ppermute(value, axis, pairs)  21.3 us
    ppermute x6, starting transfers between devices, shift_rows(): return lax.ppermute(x, axis, pairs)  17.9 us
    dot_general x8, matrix products, step(): jnp.einsum('wsk,wkc->wsc', bands[lo - REACH:hi - REACH], stacked, precisi...  15.1 us
    pallas_call x1, Pallas kernels, attend(): pl.pallas_call(attention_kernel, grid_spec=grid_spec, out_shape=jax.Shape...  14.7 us
    ppermute x9, waiting for transfers between devices, partner(): return lax.ppermute(value, axis, pairs)  12.1 us
    dot_general x1, matrix products, on_device(): jnp.dot(all_blended, kv_weight, preferred_element_type=jnp.float32)  10.3 us
    unnamed x63, local copies, waits for them, and re-layouts  7.28 us
  transfers between devices with their start and end apart: 15, of which 8 were waited for; matrix products, arithmetic and copies ran while one was open for 20% of the time, Pallas kernels for 0%

profile of v13, /device:TPU:13, one launch (start us, length us, event | category | flops | bytes accessed | tf_op | source)
XLA Modules:
  0.0 153.3 jit_solution(7680404343585557832)
XLA Ops:
  0.0 0.9 copy.34
  1.1 2.9 %select_reduce_fusion = f32[8,5,64,64]{3,2,1,0:T(8,128)} fusion(f32[8,3,64,64]{3,2,1,0:T(8,128)} %param.13, pred[8,3,5]{2,1,0:T(4,128)(4,1)S(1)} %iota_compare_fusion), kind=kLoop, calls=%fused_computation.2 | loop fusion | flops 819200 | bytes 1048696 | tf_op jit(solution)/shard_map/reduce_sum | solution.py:61
  3.9 1.7 %copy.35 = f32[8,64,5,64]{1,3,2,0:T(8,128)S(1)} copy(f32[8,64,5,64]{3,1,2,0:T(8,128)} %bitcast.210) | data formatting | bytes 1310720 | tf_op jit(solution)/shard_map/transpose | solution.py:62
  5.6 1.3 copy.36
  7.0 1.4 pad_maximum_fusion.1
  8.4 3.8 %collective-permute-start = (f32[8,64,448]{2,1,0:T(8,128)S(1)}, f32[8,64,448]{2,1,0:T(8,128)S(1)}, u32[]{:S(2)}, u32[]{:S(2)}) collective-permute-start(f32[8,64,448]{2,1,0:T(8,128)S(1)} %pad_maximum_fusion.1), channel_id=1, source_target_pairs={{0,1},{1,2},{2,3},{3,4},{4,5},{5,6},{6,7},{7,8},{8,9},{9,10},{10,1... | collective-permute-start | bytes 2752520 | tf_op jit(solution)/shard_map/ppermute | solution.py:27
  12.2 1.9 %collective-permute-start.1 = (f32[8,64,448]{2,1,0:T(8,128)S(1)}, f32[8,64,448]{2,1,0:T(8,128)S(1)}, u32[]{:S(2)}, u32[]{:S(2)}) collective-permute-start(f32[8,64,448]{2,1,0:T(8,128)S(1)} %pad_maximum_fusion.1), channel_id=1, source_target_pairs={{1,0},{2,1},{3,2},{4,3},{5,4},{6,5},{7,6},{8,7},{9,8},{10,9},{11,1... | collective-permute-start | bytes 2752520 | tf_op jit(solution)/shard_map/ppermute | solution.py:27
  14.5 2.3 %collective-permute-start.5 = (bf16[256,1024]{1,0:T(8,128)(2,1)S(1)}, bf16[256,1024]{1,0:T(8,128)(2,1)S(1)}, u32[]{:S(2)}, u32[]{:S(2)}) collective-permute-start(bf16[256,1024]{1,0:T(8,128)(2,1)S(1)} %get-tuple-element.24), channel_id=1, source_target_pairs={{0,8},{1,9},{2,10},{3,11},{4,12},{5,13},{6,14},{7,15},{8,0},{9,1},... | collective-permute-start | bytes 1572872 | tf_op jit(solution)/shard_map/ppermute | solution.py:40
  16.8 12.5 %collective-permute-done = f32[8,64,448]{2,1,0:T(8,128)S(1)} collective-permute-done((f32[8,64,448]{2,1,0:T(8,128)S(1)}, f32[8,64,448]{2,1,0:T(8,128)S(1)}, u32[]{:S(2)}, u32[]{:S(2)}) %collective-permute-start) | collective-permute-done | bytes 917536 | tf_op jit(solution)/shard_map/ppermute | solution.py:27
  29.3 7.5 %collective-permute-done.1 = f32[8,64,448]{2,1,0:T(8,128)S(1)} collective-permute-done((f32[8,64,448]{2,1,0:T(8,128)S(1)}, f32[8,64,448]{2,1,0:T(8,128)S(1)}, u32[]{:S(2)}, u32[]{:S(2)}) %collective-permute-start.1) | collective-permute-done | bytes 917536 | tf_op jit(solution)/shard_map/ppermute | solution.py:27
  37.6 1.0 copy-done.2
  38.6 1.3 fusion.67
  40.4 1.2 fusion.19
  42.0 0.8 fusion.13
  43.2 1.2 fusion.16
  44.5 1.9 %collective-permute-start.2 = (f32[8,64,256]{2,1,0:T(8,128)S(1)}, f32[8,64,256]{2,1,0:T(8,128)S(1)}, u32[]{:S(2)}, u32[]{:S(2)}) collective-permute-start(f32[8,64,256]{2,1,0:T(8,128)S(1)} %pad_maximum_fusion.4), channel_id=1, source_target_pairs={{0,1},{1,2},{2,3},{3,4},{4,5},{5,6},{6,7},{7,8},{8,9},{9,10},{10,1... | collective-permute-start | bytes 1572872 | tf_op jit(solution)/shard_map/ppermute | solution.py:27
  46.4 3.2 %collective-permute-start.3 = (f32[8,64,256]{2,1,0:T(8,128)S(1)}, f32[8,64,256]{2,1,0:T(8,128)S(1)}, u32[]{:S(2)}, u32[]{:S(2)}) collective-permute-start(f32[8,64,256]{2,1,0:T(8,128)S(1)} %pad_maximum_fusion.4), channel_id=1, source_target_pairs={{1,0},{2,1},{3,2},{4,3},{5,4},{6,5},{7,6},{8,7},{9,8},{10,9},{11,1... | collective-permute-start | bytes 1572872 | tf_op jit(solution)/shard_map/ppermute | solution.py:27
  49.6 0.7 fusion.70
  50.3 6.4 %collective-permute-start.7 = (bf16[256,1024]{1,0:T(8,128)(2,1)S(1)}, bf16[256,1024]{1,0:T(8,128)(2,1)S(1)}, u32[]{:S(2)}, u32[]{:S(2)}) collective-permute-start(bf16[256,1024]{1,0:T(8,128)(2,1)S(1)} %get-tuple-element.23), channel_id=1, source_target_pairs={{0,8},{1,9},{2,10},{3,11},{4,12},{5,13},{6,14},{7,15},{8,0},{9,1},... | collective-permute-start | bytes 1572872 | tf_op jit(solution)/shard_map/ppermute | solution.py:40
  56.8 2.5 %collective-permute-start.8 = (bf16[512,1024]{1,0:T(8,128)(2,1)S(1)}, bf16[512,1024]{1,0:T(8,128)(2,1)S(1)}, u32[]{:S(2)}, u32[]{:S(2)}) collective-permute-start(bf16[512,1024]{1,0:T(8,128)(2,1)S(1)} %copy-done.3), channel_id=1, source_target_pairs={{0,2},{1,3},{2,0},{3,1},{4,6},{5,7},{6,4},{7,5},{8,10},{9,11},{10,... | collective-permute-start | bytes 3145736 | tf_op jit(solution)/shard_map/ppermute | solution.py:40
  59.3 5.4 %collective-permute-done.3 = f32[8,64,256]{2,1,0:T(8,128)S(1)} collective-permute-done((f32[8,64,256]{2,1,0:T(8,128)S(1)}, f32[8,64,256]{2,1,0:T(8,128)S(1)}, u32[]{:S(2)}, u32[]{:S(2)}) %collective-permute-start.3) | collective-permute-done | bytes 524320 | tf_op jit(solution)/shard_map/ppermute | solution.py:27
  65.3 1.3 fusion.12
  67.1 1.3 fusion.20
  68.8 0.9 fusion.14
  69.9 6.9 %fusion.18 = bf16[8,64,128]{2,1,0:T(8,128)(2,1)S(1)} fusion(f32[8,64,320]{1,2,0:T(8,128)S(1)} %bitcast.206, f32[8,320,128]{2,1,0:T(8,128)S(1)} %bitcast.212, f32[20,64,128]{2,1,0:T(8,128)S(1)} %fusion.12, f32[20,64,128]{2,1,0:T(8,128)S(1)} %fusion.67, f32[16,64,128]{2,1,0:T(8,128)S(1)} %fusion.20, f32[8,64,128]{2,1,0:T(8,128)S(1)} %fusion.16, ...), kind=kOutput, calls=%fused_computation.30 | convolution fusion | flops 127139840 | bytes 4194340 | tf_op jit(solution)/shard_map/wsk,wkc->wsc/dot_general | solution.py:78
  76.9 0.5 collective-permute-done.7
  77.4 6.9 %collective-permute-done.8 = bf16[512,1024]{1,0:T(8,128)(2,1)S(1)} collective-permute-done((bf16[512,1024]{1,0:T(8,128)(2,1)S(1)}, bf16[512,1024]{1,0:T(8,128)(2,1)S(1)}, u32[]{:S(2)}, u32[]{:S(2)}) %collective-permute-start.8) | collective-permute-done | bytes 1048608 | tf_op jit(solution)/shard_map/ppermute | solution.py:40
  84.3 0.4 add_convert_fusion.3
  84.8 4.9 %collective-permute-start.9 = (bf16[128,1024]{1,0:T(8,128)(2,1)S(1)}, bf16[128,1024]{1,0:T(8,128)(2,1)S(1)}, u32[]{:S(2)}, u32[]{:S(2)}) collective-permute-start(bf16[128,1024]{1,0:T(8,128)(2,1)S(1)} %get-tuple-element.22), channel_id=1, source_target_pairs={{0,1},{1,2},{2,3},{3,4},{4,5},{5,6},{6,7},{7,8},{8,9},{9,10},{10,1... | collective-permute-start | bytes 786440 | tf_op jit(solution)/shard_map/ppermute | solution.py:27
  89.8 2.1 %collective-permute-start.10 = (bf16[128,1024]{1,0:T(8,128)(2,1)S(1)}, bf16[128,1024]{1,0:T(8,128)(2,1)S(1)}, u32[]{:S(2)}, u32[]{:S(2)}) collective-permute-start(bf16[128,1024]{1,0:T(8,128)(2,1)S(1)} %get-tuple-element.21), channel_id=1, source_target_pairs={{1,0},{2,1},{3,2},{4,3},{5,4},{6,5},{7,6},{8,7},{9,8},{10,9},{11,1... | collective-permute-start | bytes 786440 | tf_op jit(solution)/shard_map/ppermute | solution.py:27
  91.9 2.0 %collective-permute-start.11 = (bf16[512,128]{1,0:T(8,128)(2,1)S(1)}, bf16[512,128]{1,0:T(8,128)(2,1)S(1)}, u32[]{:S(2)}, u32[]{:S(2)}) collective-permute-start(bf16[512,128]{1,0:T(8,128)(2,1)S(1)} %bitcast.222), channel_id=1, source_target_pairs={{0,2},{1,3},{2,0},{3,1},{4,6},{5,7},{6,4},{7,5},{8,10},{9,11},{10,... | collective-permute-start | bytes 393224 | tf_op jit(solution)/shard_map/ppermute | solution.py:40
  93.9 4.3 %collective-permute-start.13 = (bf16[512,128]{1,0:T(8,128)(2,1)S(1)}, bf16[512,128]{1,0:T(8,128)(2,1)S(1)}, u32[]{:S(2)}, u32[]{:S(2)}) collective-permute-start(bf16[512,128]{1,0:T(8,128)(2,1)S(1)} %bitcast.224), channel_id=1, source_target_pairs={{0,8},{1,9},{2,10},{3,11},{4,12},{5,13},{6,14},{7,15},{8,0},{9,1},... | collective-permute-start | bytes 393224 | tf_op jit(solution)/shard_map/ppermute | solution.py:40
  98.2 0.9 collective-permute-done.10
  99.3 0.4 fusion.21
  99.7 0.4 fusion.4
  100.2 4.5 %collective-permute-done.13 = bf16[512,128]{1,0:T(8,128)(2,1)S(1)} collective-permute-done((bf16[512,128]{1,0:T(8,128)(2,1)S(1)}, bf16[512,128]{1,0:T(8,128)(2,1)S(1)}, u32[]{:S(2)}, u32[]{:S(2)}) %collective-permute-start.13) | collective-permute-done | bytes 131104 | tf_op jit(solution)/shard_map/ppermute | solution.py:40
  104.7 0.4 fusion.5
  105.2 10.3 %convolution_convert_fusion.refs_0_.refs_1_.refs_2_.refs_3_.refs_5_.refs_6_.refs_7_ = bf16[2304,2048]{1,0:T(8,128)(2,1)S(1)} fusion(bf16[2304,1024]{1,0:T(8,128)(2,1)S(1)} %fusion.5, bf16[1024,3072]{1,0:T(8,128)(2,1)S(1)} %bitcast.226), kind=kOutput, calls=%fused_computation | convolution fusion | flops 9668395008 | bytes 18350080 | tf_op jit(solution)/shard_map/dot_general | solution.py:219
  115.5 3.6 %copy-done.1 = bf16[2304,2048]{1,0:T(8,128)(2,1)} copy-done((bf16[2304,2048]{1,0:T(8,128)(2,1)}, bf16[2304,2048]{1,0:T(8,128)(2,1)S(1)}, u32[]{:S(2)}) %copy-start.1) | copy-done | bytes 9437208
  119.1 1.5 slice.359
  120.6 3.5 %collective-permute-start.14 = (bf16[512,2048]{1,0:T(8,128)(2,1)}, bf16[512,2048]{1,0:T(8,128)(2,1)}, u32[]{:S(2)}, u32[]{:S(2)}) collective-permute-start(bf16[512,2048]{1,0:T(8,128)(2,1)} %slice.359), channel_id=1, source_target_pairs={{0,1},{1,0},{2,3},{3,2},{4,5},{5,4},{6,7},{7,6},{8,9},{9,8},{10,11... | collective-permute-start | bytes 6291464 | tf_op jit(solution)/shard_map/ppermute | solution.py:40
  124.3 0.7 pad_add_fusion.table_ref
  125.1 2.8 %fusion.9 = bf16[64,8,8,128]{3,1,2,0:T(8,128)(2,1)S(1)} fusion(bf16[512,1024]{1,0:T(8,128)(2,1)S(1)} %add_convert_fusion.3, bf16[1024,3072]{1,0:T(8,128)(2,1)} %param.19), kind=kOutput, calls=%fused_computation.16 | convolution fusion | flops 1074266112 | bytes 4194304 | tf_op jit(solution)/shard_map/dot_general | solution.py:211
  127.9 0.3 copy.51
  128.2 1.8 %copy.48 = bf16[8,64,8,128]{1,3,2,0:T(8,128)(2,1)} copy(bf16[8,64,8,128]{3,2,1,0:T(8,128)(2,1)S(1)} %bitcast.213) | data formatting | bytes 2097152 | tf_op jit(solution)/shard_map/reshape | solution.py:144
  130.1 5.1 %fusion.1.q_ref = bf16[8,8,128,128]{3,2,1,0:T(8,128)(2,1)} fusion(bf16[8,8,128,64]{3,2,1,0:T(8,128)(2,1)} %bitcast.209, pred[128,128]{1,0:T(8,128)(4,1)S(1)} %select_compare_fusion), kind=kLoop, calls=%fused_computation.4 | loop fusion | flops 7340032 | bytes 3162112 | tf_op jit(solution)/shard_map/jit(_where)/select_n | solution.py:149
  135.1 14.7 %shard_map.109 = bf16[512,1024]{1,0:T(8,128)(2,1)} custom-call(s32[8,8]{1,0:T(8,128)} %pad_add_fusion.table_ref, bf16[8,8,128,128]{3,2,1,0:T(8,128)(2,1)} %fusion.1.q_ref, bf16[2304,2048]{1,0:T(8,128)(2,1)} %copy-done.1, bf16[2304,2048]{1,0:T(8,128)(2,1)} %copy-done.1, bf16[2304,2048]{1,0:T(8,128)(2,1)} %copy-done.1, bf16[2304,2048]{1,0:T(8,128)(2,1)} %copy-done.1, ...), custom_call_target="tpu_custom_call" | custom-call | tf_op jit(solution)/shard_map/pallas_call | solution.py:166
  149.8 3.4 %convolution_convert_fusion.1 = bf16[512,1024]{1,0:T(8,128)(2,1)} fusion(bf16[512,1024]{1,0:T(8,128)(2,1)} %shard_map.109, bf16[1024,1024]{1,0:T(8,128)(2,1)S(1)} %copy-done), kind=kOutput, calls=%fused_computation.15 | convolution fusion | flops 1074266112 | bytes 4194304 | tf_op jit(solution)/shard_map/dot_general | solution.py:234
  (110 shorter events, 4.5 us)
Async XLA Ops:
  0.0 149.8 %copy-start = (bf16[1024,1024]{1,0:T(8,128)(2,1)S(1)}, bf16[1024,1024]{1,0:T(8,128)(2,1)}, u32[]{:S(2)}) copy-start(bf16[1024,1024]{1,0:T(8,128)(2,1)} %param.20) | copy-start | bytes 6291460
  7.0 7.2 %copy-start.3 = (bf16[512,1024]{1,0:T(8,128)(2,1)S(1)}, bf16[512,1024]{1,0:T(8,128)(2,1)}, u32[]{:S(2)}) copy-start(bf16[512,1024]{1,0:T(8,128)(2,1)} %param.11) | copy-start | bytes 3145732
  8.4 28.4 %copy-start.4 = (f32[512,128]{1,0:T(8,128)S(1)}, f32[512,128]{1,0:T(8,128)}, u32[]{:S(2)}) copy-start(f32[512,128]{1,0:T(8,128)} %param.12) | copy-start | bytes 786436
  8.4 20.9 %collective-permute-start = (f32[8,64,448]{2,1,0:T(8,128)S(1)}, f32[8,64,448]{2,1,0:T(8,128)S(1)}, u32[]{:S(2)}, u32[]{:S(2)}) collective-permute-start(f32[8,64,448]{2,1,0:T(8,128)S(1)} %pad_maximum_fusion.1), channel_id=1, source_target_pairs={{0,1},{1,2},{2,3},{3,4},{4,5},{5,6},{6,7},{7,8},{8,9},{9,10},{10,1... | collective-permute-start | bytes 2752520 | tf_op jit(solution)/shard_map/ppermute | solution.py:27
  12.2 24.6 %collective-permute-start.1 = (f32[8,64,448]{2,1,0:T(8,128)S(1)}, f32[8,64,448]{2,1,0:T(8,128)S(1)}, u32[]{:S(2)}, u32[]{:S(2)}) collective-permute-start(f32[8,64,448]{2,1,0:T(8,128)S(1)} %pad_maximum_fusion.1), channel_id=1, source_target_pairs={{1,0},{2,1},{3,2},{4,3},{5,4},{6,5},{7,6},{8,7},{9,8},{10,9},{11,1... | collective-permute-start | bytes 2752520 | tf_op jit(solution)/shard_map/ppermute | solution.py:27
  14.2 36.1 %collective-permute-start.4 = (bf16[256,1024]{1,0:T(8,128)(2,1)S(1)}, bf16[256,1024]{1,0:T(8,128)(2,1)S(1)}, u32[]{:S(2)}, u32[]{:S(2)}) collective-permute-start(bf16[256,1024]{1,0:T(8,128)(2,1)S(1)} %get-tuple-element.24), channel_id=1, source_target_pairs={{0,4},{1,5},{2,6},{3,7},{4,0},{5,1},{6,2},{7,3},{8,12},{9,13},{10,... | collective-permute-start | bytes 1572872 | tf_op jit(solution)/shard_map/ppermute | solution.py:40
  14.5 42.3 %collective-permute-start.5 = (bf16[256,1024]{1,0:T(8,128)(2,1)S(1)}, bf16[256,1024]{1,0:T(8,128)(2,1)S(1)}, u32[]{:S(2)}, u32[]{:S(2)}) collective-permute-start(bf16[256,1024]{1,0:T(8,128)(2,1)S(1)} %get-tuple-element.24), channel_id=1, source_target_pairs={{0,8},{1,9},{2,10},{3,11},{4,12},{5,13},{6,14},{7,15},{8,0},{9,1},... | collective-permute-start | bytes 1572872 | tf_op jit(solution)/shard_map/ppermute | solution.py:40
  37.5 1.1 copy-start.2
  43.1 6.5 %copy-start.6 = (f32[9]{0:T(128)S(1)}, f32[9]{0:T(128)}, u32[]{:S(2)}) copy-start(f32[9]{0:T(128)} %param.17) | copy-start | bytes 112
  44.5 14.8 %collective-permute-start.2 = (f32[8,64,256]{2,1,0:T(8,128)S(1)}, f32[8,64,256]{2,1,0:T(8,128)S(1)}, u32[]{:S(2)}, u32[]{:S(2)}) collective-permute-start(f32[8,64,256]{2,1,0:T(8,128)S(1)} %pad_maximum_fusion.4), channel_id=1, source_target_pairs={{0,1},{1,2},{2,3},{3,4},{4,5},{5,6},{6,7},{7,8},{8,9},{9,10},{10,1... | collective-permute-start | bytes 1572872 | tf_op jit(solution)/shard_map/ppermute | solution.py:27
  46.4 18.3 %collective-permute-start.3 = (f32[8,64,256]{2,1,0:T(8,128)S(1)}, f32[8,64,256]{2,1,0:T(8,128)S(1)}, u32[]{:S(2)}, u32[]{:S(2)}) collective-permute-start(f32[8,64,256]{2,1,0:T(8,128)S(1)} %pad_maximum_fusion.4), channel_id=1, source_target_pairs={{1,0},{2,1},{3,2},{4,3},{5,4},{6,5},{7,6},{8,7},{9,8},{10,9},{11,1... | collective-permute-start | bytes 1572872 | tf_op jit(solution)/shard_map/ppermute | solution.py:27
  49.6 27.3 %collective-permute-start.6 = (bf16[256,1024]{1,0:T(8,128)(2,1)S(1)}, bf16[256,1024]{1,0:T(8,128)(2,1)S(1)}, u32[]{:S(2)}, u32[]{:S(2)}) collective-permute-start(bf16[256,1024]{1,0:T(8,128)(2,1)S(1)} %get-tuple-element.23), channel_id=1, source_target_pairs={{0,4},{1,5},{2,6},{3,7},{4,0},{5,1},{6,2},{7,3},{8,12},{9,13},{10,... | collective-permute-start | bytes 1572872 | tf_op jit(solution)/shard_map/ppermute | solution.py:40
  50.3 27.1 %collective-permute-start.7 = (bf16[256,1024]{1,0:T(8,128)(2,1)S(1)}, bf16[256,1024]{1,0:T(8,128)(2,1)S(1)}, u32[]{:S(2)}, u32[]{:S(2)}) collective-permute-start(bf16[256,1024]{1,0:T(8,128)(2,1)S(1)} %get-tuple-element.23), channel_id=1, source_target_pairs={{0,8},{1,9},{2,10},{3,11},{4,12},{5,13},{6,14},{7,15},{8,0},{9,1},... | collective-permute-start | bytes 1572872 | tf_op jit(solution)/shard_map/ppermute | solution.py:40
  56.8 27.6 %collective-permute-start.8 = (bf16[512,1024]{1,0:T(8,128)(2,1)S(1)}, bf16[512,1024]{1,0:T(8,128)(2,1)S(1)}, u32[]{:S(2)}, u32[]{:S(2)}) collective-permute-start(bf16[512,1024]{1,0:T(8,128)(2,1)S(1)} %copy-done.3), channel_id=1, source_target_pairs={{0,2},{1,3},{2,0},{3,1},{4,6},{5,7},{6,4},{7,5},{8,10},{9,11},{10,... | collective-permute-start | bytes 3145736 | tf_op jit(solution)/shard_map/ppermute | solution.py:40
  69.9 14.4 %copy-start.5 = (bf16[128,1024]{1,0:T(8,128)(2,1)S(1)}, bf16[128,1024]{1,0:T(8,128)(2,1)}, u32[]{:S(2)}) copy-start(bf16[128,1024]{1,0:T(8,128)(2,1)} %param.18) | copy-start | bytes 786436
  84.3 20.8 %slice-start = ((s8[6291456]{0:T(1024)(128)(4,1)}), s8[4194304]{0:T(1024)(128)(4,1)S(1)}, s32[]{:S(2)}) async-start(s8[6291456]{0:T(1024)(128)(4,1)} %bitcast.225), calls=%async_computation | async-start | bytes 8388608
  84.8 13.3 %collective-permute-start.9 = (bf16[128,1024]{1,0:T(8,128)(2,1)S(1)}, bf16[128,1024]{1,0:T(8,128)(2,1)S(1)}, u32[]{:S(2)}, u32[]{:S(2)}) collective-permute-start(bf16[128,1024]{1,0:T(8,128)(2,1)S(1)} %get-tuple-element.22), channel_id=1, source_target_pairs={{0,1},{1,2},{2,3},{3,4},{4,5},{5,6},{6,7},{7,8},{8,9},{9,10},{10,1... | collective-permute-start | bytes 786440 | tf_op jit(solution)/shard_map/ppermute | solution.py:27
  89.8 9.4 %collective-permute-start.10 = (bf16[128,1024]{1,0:T(8,128)(2,1)S(1)}, bf16[128,1024]{1,0:T(8,128)(2,1)S(1)}, u32[]{:S(2)}, u32[]{:S(2)}) collective-permute-start(bf16[128,1024]{1,0:T(8,128)(2,1)S(1)} %get-tuple-element.21), channel_id=1, source_target_pairs={{1,0},{2,1},{3,2},{4,3},{5,4},{6,5},{7,6},{8,7},{9,8},{10,9},{11,1... | collective-permute-start | bytes 786440 | tf_op jit(solution)/shard_map/ppermute | solution.py:27
  91.9 7.4 %collective-permute-start.11 = (bf16[512,128]{1,0:T(8,128)(2,1)S(1)}, bf16[512,128]{1,0:T(8,128)(2,1)S(1)}, u32[]{:S(2)}, u32[]{:S(2)}) collective-permute-start(bf16[512,128]{1,0:T(8,128)(2,1)S(1)} %bitcast.222), channel_id=1, source_target_pairs={{0,2},{1,3},{2,0},{3,1},{4,6},{5,7},{6,4},{7,5},{8,10},{9,11},{10,... | collective-permute-start | bytes 393224 | tf_op jit(solution)/shard_map/ppermute | solution.py:40
  93.9 5.9 %collective-permute-start.12 = (bf16[512,128]{1,0:T(8,128)(2,1)S(1)}, bf16[512,128]{1,0:T(8,128)(2,1)S(1)}, u32[]{:S(2)}, u32[]{:S(2)}) collective-permute-start(bf16[512,128]{1,0:T(8,128)(2,1)S(1)} %bitcast.223), channel_id=1, source_target_pairs={{0,4},{1,5},{2,6},{3,7},{4,0},{5,1},{6,2},{7,3},{8,12},{9,13},{10,... | collective-permute-start | bytes 393224 | tf_op jit(solution)/shard_map/ppermute | solution.py:40
  93.9 10.8 %collective-permute-start.13 = (bf16[512,128]{1,0:T(8,128)(2,1)S(1)}, bf16[512,128]{1,0:T(8,128)(2,1)S(1)}, u32[]{:S(2)}, u32[]{:S(2)}) collective-permute-start(bf16[512,128]{1,0:T(8,128)(2,1)S(1)} %bitcast.224), channel_id=1, source_target_pairs={{0,8},{1,9},{2,10},{3,11},{4,12},{5,13},{6,14},{7,15},{8,0},{9,1},... | collective-permute-start | bytes 393224 | tf_op jit(solution)/shard_map/ppermute | solution.py:40
  99.2 6.0 %slice-start.1 = ((s8[6291456]{0:T(1024)(128)(4,1)}), s8[2097152]{0:T(1024)(128)(4,1)S(1)}, s32[]{:S(2)}) async-start(s8[6291456]{0:T(1024)(128)(4,1)} %bitcast.225), calls=%async_computation.1 | async-start | bytes 4194304
  115.5 3.7 %copy-start.1 = (bf16[2304,2048]{1,0:T(8,128)(2,1)}, bf16[2304,2048]{1,0:T(8,128)(2,1)S(1)}, u32[]{:S(2)}) copy-start(bf16[2304,2048]{1,0:T(8,128)(2,1)S(1)} %convolution_convert_fusion.refs_0_.refs_1_.refs_2_.refs_3_.refs_5_.refs_6_.refs_7_) | copy-start | bytes 28311556
  119.1 5.0 %copy-start.7 = (s32[8,3]{0,1:T(4,128)S(1)}, s32[8,3]{0,1:T(4,128)}, u32[]{:S(2)}) copy-start(s32[8,3]{0,1:T(4,128)} %param.15) | copy-start | bytes 292
  119.1 5.0 %copy-start.8 = (s32[8,4]{0,1:T(4,128)S(1)}, s32[8,4]{0,1:T(4,128)}, u32[]{:S(2)}) copy-start(s32[8,4]{0,1:T(4,128)} %param.16) | copy-start | bytes 388
  119.1 5.2 %copy-start.9 = (s32[4]{0:T(128)S(1)}, s32[4]{0:T(128)}, u32[]{:S(2)}) copy-start(s32[4]{0:T(128)} %constant.58.clone) | copy-start | bytes 52
  120.6 14.5 %collective-permute-start.14 = (bf16[512,2048]{1,0:T(8,128)(2,1)}, bf16[512,2048]{1,0:T(8,128)(2,1)}, u32[]{:S(2)}, u32[]{:S(2)}) collective-permute-start(bf16[512,2048]{1,0:T(8,128)(2,1)} %slice.359), channel_id=1, source_target_pairs={{0,1},{1,0},{2,3},{3,2},{4,5},{5,4},{6,7},{7,6},{8,9},{9,8},{10,11... | collective-permute-start | bytes 6291464 | tf_op jit(solution)/shard_map/ppermute | solution.py:40

commit v14 on v13

--- a/solution.py
+++ b/solution.py
@@ -153,7 +153,7 @@
     count = table.shape[0]
     pairs = HEADS // 2
     in_specs = [pl.BlockSpec((1, pairs, 2 * HD, 2 * BS), lambda b, t: (b, 0, 0, 0))]
-    operands = [split_queries(queries)]
+    operands = [queries]
     for j, src in enumerate(kv_sources):
         in_specs.append(pl.BlockSpec((BS, 2 * D), lambda b, t, j=j: (t[b, j], 0)))
         operands.append(src)
@@ -211,6 +211,7 @@
     queries = jnp.dot(blended, qkv_weight[:, :D], preferred_element_type=jnp.float32).astype(
         jnp.bfloat16
     )
+    queries, enc_far = lax.optimization_barrier((split_queries(queries), enc_far))
     all_blended = jnp.concatenate(
         [shift_rows(blended[rows - rim:], "seq", 1), blended, shift_rows(blended[:rim], "seq", -1)]
         + [blend(f, e) for f, e in zip(feats_far, enc_far)],

time: 154 us -> 163 us (1.058)
  the two profiles are of different devices: /device:TPU:13 before, /device:TPU:0 now
where the time goes in v14:
time: 163 us; the launch traced here: 162 us
  starting transfers between devices  43 us (26%)
  matrix products  37.9 us (23%)
  waiting for transfers between devices  35.1 us (22%)
  local copies, waits for them, and re-layouts  20.3 us (12%)
  Pallas kernels  14.7 us (9%)
  other arithmetic  10.3 us (6%)
    ppermute x9, waiting for transfers between devices, partner(): return lax.ppermute(value, axis, pairs)  35.1 us
    ppermute x9, starting transfers between devices, partner(): return lax.ppermute(value, axis, pairs)  23.9 us
    ppermute x6, starting transfers between devices, shift_rows(): return lax.ppermute(x, axis, pairs)  19.1 us
    dot_general x8, matrix products, step(): jnp.einsum('wsk,wkc->wsc', bands[lo - REACH:hi - REACH], stacked, precisi...  15.1 us
    pallas_call x1, Pallas kernels, attend(): pl.pallas_call(attention_kernel, grid_spec=grid_spec, out_shape=jax.Shape...  14.7 us
    dot_general x1, matrix products, on_device(): jnp.dot(all_blended, kv_weight, preferred_element_type=jnp.float32)  11.8 us
    unnamed x77, local copies, waits for them, and re-layouts  9.45 us
    select_n x1, other arithmetic, split_queries(): return jnp.where(d_head == j_head, qt * scale, jnp.zeros_like(qt))  4.96 us
  transfers between devices with their start and end apart: 15, of which 4 were waited for; matrix products, arithmetic and copies ran while one was open for 21% of the time, Pallas kernels for 0%

profile of v14, /device:TPU:0, one launch (start us, length us, event | category | flops | bytes accessed | tf_op | source)
XLA Modules:
  0.0 162.3 jit_solution(18110939718932163185)
XLA Ops:
  0.0 0.9 copy.34
  1.1 2.8 %select_reduce_fusion = f32[8,5,64,64]{3,2,1,0:T(8,128)} fusion(f32[8,3,64,64]{3,2,1,0:T(8,128)} %param.13, pred[8,3,5]{2,1,0:T(4,128)(4,1)S(1)} %iota_compare_fusion), kind=kLoop, calls=%fused_computation.2 | loop fusion | flops 819200 | bytes 1048696 | tf_op jit(solution)/shard_map/reduce_sum | solution.py:61
  3.9 1.7 %copy.35 = f32[8,64,5,64]{1,3,2,0:T(8,128)S(1)} copy(f32[8,64,5,64]{3,1,2,0:T(8,128)} %bitcast.210) | data formatting | bytes 1310720 | tf_op jit(solution)/shard_map/transpose | solution.py:62
  5.6 1.3 copy.36
  7.0 1.4 pad_maximum_fusion.1
  8.4 2.6 %collective-permute-start = (f32[8,64,448]{2,1,0:T(8,128)S(1)}, f32[8,64,448]{2,1,0:T(8,128)S(1)}, u32[]{:S(2)}, u32[]{:S(2)}) collective-permute-start(f32[8,64,448]{2,1,0:T(8,128)S(1)} %pad_maximum_fusion.1), channel_id=1, source_target_pairs={{0,1},{1,2},{2,3},{3,4},{4,5},{5,6},{6,7},{7,8},{8,9},{9,10},{10,1... | collective-permute-start | bytes 2752520 | tf_op jit(solution)/shard_map/ppermute | solution.py:27
  11.0 1.3 collective-permute-start.1
  12.3 5.8 %collective-permute-start.4 = (bf16[256,1024]{1,0:T(8,128)(2,1)S(1)}, bf16[256,1024]{1,0:T(8,128)(2,1)S(1)}, u32[]{:S(2)}, u32[]{:S(2)}) collective-permute-start(bf16[256,1024]{1,0:T(8,128)(2,1)S(1)} %get-tuple-element.32), channel_id=1, source_target_pairs={{0,4},{1,5},{2,6},{3,7},{4,0},{5,1},{6,2},{7,3},{8,12},{9,13},{10,... | collective-permute-start | bytes 1572872 | tf_op jit(solution)/shard_map/ppermute | solution.py:40
  18.2 2.6 %collective-permute-start.5 = (bf16[256,1024]{1,0:T(8,128)(2,1)S(1)}, bf16[256,1024]{1,0:T(8,128)(2,1)}, u32[]{:S(2)}, u32[]{:S(2)}) collective-permute-start(bf16[256,1024]{1,0:T(8,128)(2,1)S(1)} %get-tuple-element.32), channel_id=1, source_target_pairs={{0,8},{1,9},{2,10},{3,11},{4,12},{5,13},{6,14},{7,15},{8,0},{9,1},... | collective-permute-start | bytes 1572872 | tf_op jit(solution)/shard_map/ppermute | solution.py:40
  20.8 0.4 collective-permute-start.6
  21.7 0.4 copy.38
  22.2 1.0 copy-done.2
  23.2 1.3 fusion.67
  25.0 1.2 fusion.19
  26.6 1.0 fusion.13
  27.9 1.2 fusion.16
  29.1 10.3 %collective-permute-start.2 = (f32[8,64,256]{2,1,0:T(8,128)S(1)}, f32[8,64,256]{2,1,0:T(8,128)S(1)}, u32[]{:S(2)}, u32[]{:S(2)}) collective-permute-start(f32[8,64,256]{2,1,0:T(8,128)S(1)} %pad_maximum_fusion.4), channel_id=1, source_target_pairs={{0,1},{1,2},{2,3},{3,4},{4,5},{5,6},{6,7},{7,8},{8,9},{9,10},{10,1... | collective-permute-start | bytes 1572872 | tf_op jit(solution)/shard_map/ppermute | solution.py:27
  39.4 1.5 collective-permute-start.3
  40.9 0.7 fusion.70
  41.7 15.9 %collective-permute-done.4 = bf16[256,1024]{1,0:T(8,128)(2,1)S(1)} collective-permute-done((bf16[256,1024]{1,0:T(8,128)(2,1)S(1)}, bf16[256,1024]{1,0:T(8,128)(2,1)S(1)}, u32[]{:S(2)}, u32[]{:S(2)}) %collective-permute-start.4) | collective-permute-done | bytes 524320 | tf_op jit(solution)/shard_map/ppermute | solution.py:40
  57.6 0.8 collective-permute-start.7
  58.4 8.3 %collective-permute-start.8 = (bf16[512,1024]{1,0:T(8,128)(2,1)S(1)}, bf16[512,1024]{1,0:T(8,128)(2,1)S(1)}, u32[]{:S(2)}, u32[]{:S(2)}) collective-permute-start(bf16[512,1024]{1,0:T(8,128)(2,1)S(1)} %copy-done.3), channel_id=1, source_target_pairs={{0,2},{1,3},{2,0},{3,1},{4,6},{5,7},{6,4},{7,5},{8,10},{9,11},{10,... | collective-permute-start | bytes 3145736 | tf_op jit(solution)/shard_map/ppermute | solution.py:40
  67.4 1.3 fusion.12
  69.1 1.2 fusion.20
  70.7 1.0 fusion.14
  72.0 6.8 %fusion.18 = bf16[8,64,128]{2,1,0:T(8,128)(2,1)S(1)} fusion(f32[8,64,320]{1,2,0:T(8,128)S(1)} %bitcast.206, f32[8,320,128]{2,1,0:T(8,128)S(1)} %bitcast.212, f32[20,64,128]{2,1,0:T(8,128)S(1)} %fusion.12, f32[20,64,128]{2,1,0:T(8,128)S(1)} %fusion.67, f32[16,64,128]{2,1,0:T(8,128)S(1)} %fusion.20, f32[8,64,128]{2,1,0:T(8,128)S(1)} %fusion.16, ...), kind=kOutput, calls=%fused_computation.30 | convolution fusion | flops 127139840 | bytes 4194340 | tf_op jit(solution)/shard_map/wsk,wkc->wsc/dot_general | solution.py:78
  78.8 8.8 %collective-permute-done.7 = bf16[256,1024]{1,0:T(8,128)(2,1)S(1)} collective-permute-done((bf16[256,1024]{1,0:T(8,128)(2,1)S(1)}, bf16[256,1024]{1,0:T(8,128)(2,1)S(1)}, u32[]{:S(2)}, u32[]{:S(2)}) %collective-permute-start.7) | collective-permute-done | bytes 524320 | tf_op jit(solution)/shard_map/ppermute | solution.py:40
  87.6 7.2 %collective-permute-done.8 = bf16[512,1024]{1,0:T(8,128)(2,1)S(1)} collective-permute-done((bf16[512,1024]{1,0:T(8,128)(2,1)S(1)}, bf16[512,1024]{1,0:T(8,128)(2,1)S(1)}, u32[]{:S(2)}, u32[]{:S(2)}) %collective-permute-start.8) | collective-permute-done | bytes 1048608 | tf_op jit(solution)/shard_map/ppermute | solution.py:40
  94.8 3.3 %collective-permute-start.11 = (bf16[512,128]{1,0:T(8,128)(2,1)S(1)}, bf16[512,128]{1,0:T(8,128)(2,1)}, u32[]{:S(2)}, u32[]{:S(2)}) collective-permute-start(bf16[512,128]{1,0:T(8,128)(2,1)S(1)} %bitcast.222), channel_id=1, source_target_pairs={{0,8},{1,9},{2,10},{3,11},{4,12},{5,13},{6,14},{7,15},{8,0},{9,1},... | collective-permute-start | bytes 393224 | tf_op jit(solution)/shard_map/ppermute | solution.py:40
  98.5 0.8 fusion.68
  99.3 2.0 %collective-permute-start.12 = (bf16[128,1024]{1,0:T(8,128)(2,1)}, bf16[128,1024]{1,0:T(8,128)(2,1)}, u32[]{:S(2)}, u32[]{:S(2)}) collective-permute-start(bf16[128,1024]{1,0:T(8,128)(2,1)} %get-tuple-element.30), channel_id=1, source_target_pairs={{0,1},{1,2},{2,3},{3,4},{4,5},{5,6},{6,7},{7,8},{8,9},{9,10},{10,1... | collective-permute-start | bytes 786440 | tf_op jit(solution)/shard_map/ppermute | solution.py:27
  101.3 1.5 collective-permute-start.13
  102.8 2.8 %fusion.9 = bf16[64,8,8,128]{3,1,2,0:T(8,128)(2,1)S(1)} fusion(bf16[512,1024]{1,0:T(8,128)(2,1)S(1)} %add_convert_fusion.3, bf16[1024,3072]{1,0:T(8,128)(2,1)} %param.19), kind=kOutput, calls=%fused_computation.16 | convolution fusion | flops 1074266112 | bytes 4194304 | tf_op jit(solution)/shard_map/dot_general | solution.py:211
  105.7 1.2 copy.51
  107.0 2.8 %copy.48 = bf16[8,64,8,128]{1,3,2,0:T(8,128)(2,1)} copy(bf16[8,64,8,128]{3,2,1,0:T(8,128)(2,1)} %bitcast.213) | data formatting | bytes 2097152 | tf_op jit(solution)/shard_map/reshape | solution.py:144
  109.7 5.0 %fusion.1.q_ref = bf16[8,8,128,128]{3,2,1,0:T(8,128)(2,1)} fusion(bf16[8,8,128,64]{3,2,1,0:T(8,128)(2,1)} %bitcast.209, pred[128,128]{1,0:T(8,128)(4,1)S(1)} %select_compare_fusion), kind=kLoop, calls=%fused_computation.4 | loop fusion | flops 7340032 | bytes 3162112 | tf_op jit(solution)/shard_map/jit(_where)/select_n | solution.py:149
  114.7 1.1 constant_dynamic-update-slice_fusion.2
  116.1 1.4 fusion.21
  117.5 1.3 fusion.4
  118.8 1.5 fusion.5
  120.4 11.8 %convolution_convert_fusion.refs_0_.refs_1_.refs_2_.refs_3_.refs_5_.refs_6_.refs_7_ = bf16[2304,2048]{1,0:T(8,128)(2,1)S(1)} fusion(bf16[2304,1024]{1,0:T(8,128)(2,1)S(1)} %fusion.5, bf16[1024,3072]{1,0:T(8,128)(2,1)} %param.19), kind=kOutput, calls=%fused_computation | convolution fusion | flops 9668395008 | bytes 18350080 | tf_op jit(solution)/shard_map/dot_general | solution.py:220
  132.2 3.7 %copy-done.1 = bf16[2304,2048]{1,0:T(8,128)(2,1)} copy-done((bf16[2304,2048]{1,0:T(8,128)(2,1)}, bf16[2304,2048]{1,0:T(8,128)(2,1)S(1)}, u32[]{:S(2)}) %copy-start.1) | copy-done | bytes 9437208
  135.8 1.5 slice.359
  137.3 2.7 %collective-permute-start.14 = (bf16[512,2048]{1,0:T(8,128)(2,1)}, bf16[512,2048]{1,0:T(8,128)(2,1)}, u32[]{:S(2)}, u32[]{:S(2)}) collective-permute-start(bf16[512,2048]{1,0:T(8,128)(2,1)} %slice.359), channel_id=1, source_target_pairs={{0,1},{1,0},{2,3},{3,2},{4,5},{5,4},{6,7},{7,6},{8,9},{9,8},{10,11... | collective-permute-start | bytes 6291464 | tf_op jit(solution)/shard_map/ppermute | solution.py:40
  140.2 0.7 pad_add_fusion.table_ref
  140.8 3.3 %collective-permute-done.14.refs_4_ = bf16[512,2048]{1,0:T(8,128)(2,1)} collective-permute-done((bf16[512,2048]{1,0:T(8,128)(2,1)}, bf16[512,2048]{1,0:T(8,128)(2,1)}, u32[]{:S(2)}, u32[]{:S(2)}) %collective-permute-start.14) | collective-permute-done | bytes 2097184 | tf_op jit(solution)/shard_map/ppermute | solution.py:40
  144.1 14.7 %shard_map.109 = bf16[512,1024]{1,0:T(8,128)(2,1)} custom-call(s32[8,8]{1,0:T(8,128)} %pad_add_fusion.table_ref, bf16[8,8,128,128]{3,2,1,0:T(8,128)(2,1)} %fusion.1.q_ref, bf16[2304,2048]{1,0:T(8,128)(2,1)} %copy-done.1, bf16[2304,2048]{1,0:T(8,128)(2,1)} %copy-done.1, bf16[2304,2048]{1,0:T(8,128)(2,1)} %copy-done.1, bf16[2304,2048]{1,0:T(8,128)(2,1)} %copy-done.1, ...), custom_call_target="tpu_custom_call" | custom-call | tf_op jit(solution)/shard_map/pallas_call | solution.py:166
  158.8 3.4 %convolution_convert_fusion.1 = bf16[512,1024]{1,0:T(8,128)(2,1)} fusion(bf16[512,1024]{1,0:T(8,128)(2,1)} %shard_map.109, bf16[1024,1024]{1,0:T(8,128)(2,1)S(1)} %copy-done), kind=kOutput, calls=%fused_computation.15 | convolution fusion | flops 1074266112 | bytes 4194304 | tf_op jit(solution)/shard_map/dot_general | solution.py:235
  (123 shorter events, 4.2 us)
Async XLA Ops:
  0.0 158.8 %copy-start = (bf16[1024,1024]{1,0:T(8,128)(2,1)S(1)}, bf16[1024,1024]{1,0:T(8,128)(2,1)}, u32[]{:S(2)}) copy-start(bf16[1024,1024]{1,0:T(8,128)(2,1)} %param.20) | copy-start | bytes 6291460
  7.0 5.3 %copy-start.3 = (bf16[512,1024]{1,0:T(8,128)(2,1)S(1)}, bf16[512,1024]{1,0:T(8,128)(2,1)}, u32[]{:S(2)}) copy-start(bf16[512,1024]{1,0:T(8,128)(2,1)} %param.11) | copy-start | bytes 3145732
  8.4 12.9 %copy-start.4 = (f32[512,128]{1,0:T(8,128)S(1)}, f32[512,128]{1,0:T(8,128)}, u32[]{:S(2)}) copy-start(f32[512,128]{1,0:T(8,128)} %param.12) | copy-start | bytes 786436
  8.4 12.8 %collective-permute-start = (f32[8,64,448]{2,1,0:T(8,128)S(1)}, f32[8,64,448]{2,1,0:T(8,128)S(1)}, u32[]{:S(2)}, u32[]{:S(2)}) collective-permute-start(f32[8,64,448]{2,1,0:T(8,128)S(1)} %pad_maximum_fusion.1), channel_id=1, source_target_pairs={{0,1},{1,2},{2,3},{3,4},{4,5},{5,6},{6,7},{7,8},{8,9},{9,10},{10,1... | collective-permute-start | bytes 2752520 | tf_op jit(solution)/shard_map/ppermute | solution.py:27
  11.0 10.3 %collective-permute-start.1 = (f32[8,64,448]{2,1,0:T(8,128)S(1)}, f32[8,64,448]{2,1,0:T(8,128)S(1)}, u32[]{:S(2)}, u32[]{:S(2)}) collective-permute-start(f32[8,64,448]{2,1,0:T(8,128)S(1)} %pad_maximum_fusion.1), channel_id=1, source_target_pairs={{1,0},{2,1},{3,2},{4,3},{5,4},{6,5},{7,6},{8,7},{9,8},{10,9},{11,1... | collective-permute-start | bytes 2752520 | tf_op jit(solution)/shard_map/ppermute | solution.py:27
  12.3 45.2 %collective-permute-start.4 = (bf16[256,1024]{1,0:T(8,128)(2,1)S(1)}, bf16[256,1024]{1,0:T(8,128)(2,1)S(1)}, u32[]{:S(2)}, u32[]{:S(2)}) collective-permute-start(bf16[256,1024]{1,0:T(8,128)(2,1)S(1)} %get-tuple-element.32), channel_id=1, source_target_pairs={{0,4},{1,5},{2,6},{3,7},{4,0},{5,1},{6,2},{7,3},{8,12},{9,13},{10,... | collective-permute-start | bytes 1572872 | tf_op jit(solution)/shard_map/ppermute | solution.py:40
  18.2 40.2 %collective-permute-start.5 = (bf16[256,1024]{1,0:T(8,128)(2,1)S(1)}, bf16[256,1024]{1,0:T(8,128)(2,1)}, u32[]{:S(2)}, u32[]{:S(2)}) collective-permute-start(bf16[256,1024]{1,0:T(8,128)(2,1)S(1)} %get-tuple-element.32), channel_id=1, source_target_pairs={{0,8},{1,9},{2,10},{3,11},{4,12},{5,13},{6,14},{7,15},{8,0},{9,1},... | collective-permute-start | bytes 1572872 | tf_op jit(solution)/shard_map/ppermute | solution.py:40
  20.8 58.0 %collective-permute-start.6 = (bf16[256,1024]{1,0:T(8,128)(2,1)S(1)}, bf16[256,1024]{1,0:T(8,128)(2,1)S(1)}, u32[]{:S(2)}, u32[]{:S(2)}) collective-permute-start(bf16[256,1024]{1,0:T(8,128)(2,1)S(1)} %get-tuple-element.31), channel_id=1, source_target_pairs={{0,4},{1,5},{2,6},{3,7},{4,0},{5,1},{6,2},{7,3},{8,12},{9,13},{10,... | collective-permute-start | bytes 1572872 | tf_op jit(solution)/shard_map/ppermute | solution.py:40
  22.1 1.1 copy-start.2
  27.9 13.1 %copy-start.9 = (f32[9]{0:T(128)S(1)}, f32[9]{0:T(128)}, u32[]{:S(2)}) copy-start(f32[9]{0:T(128)} %param.17) | copy-start | bytes 112
  29.1 37.6 %collective-permute-start.2 = (f32[8,64,256]{2,1,0:T(8,128)S(1)}, f32[8,64,256]{2,1,0:T(8,128)S(1)}, u32[]{:S(2)}, u32[]{:S(2)}) collective-permute-start(f32[8,64,256]{2,1,0:T(8,128)S(1)} %pad_maximum_fusion.4), channel_id=1, source_target_pairs={{0,1},{1,2},{2,3},{3,4},{4,5},{5,6},{6,7},{7,8},{8,9},{9,10},{10,1... | collective-permute-start | bytes 1572872 | tf_op jit(solution)/shard_map/ppermute | solution.py:27
  39.4 27.3 %collective-permute-start.3 = (f32[8,64,256]{2,1,0:T(8,128)S(1)}, f32[8,64,256]{2,1,0:T(8,128)S(1)}, u32[]{:S(2)}, u32[]{:S(2)}) collective-permute-start(f32[8,64,256]{2,1,0:T(8,128)S(1)} %pad_maximum_fusion.4), channel_id=1, source_target_pairs={{1,0},{2,1},{3,2},{4,3},{5,4},{6,5},{7,6},{8,7},{9,8},{10,9},{11,1... | collective-permute-start | bytes 1572872 | tf_op jit(solution)/shard_map/ppermute | solution.py:27
  57.6 0.8 copy-start.13
  57.6 30.0 %collective-permute-start.7 = (bf16[256,1024]{1,0:T(8,128)(2,1)S(1)}, bf16[256,1024]{1,0:T(8,128)(2,1)S(1)}, u32[]{:S(2)}, u32[]{:S(2)}) collective-permute-start(bf16[256,1024]{1,0:T(8,128)(2,1)S(1)} %get-tuple-element.31), channel_id=1, source_target_pairs={{0,8},{1,9},{2,10},{3,11},{4,12},{5,13},{6,14},{7,15},{8,0},{9,1},... | collective-permute-start | bytes 1572872 | tf_op jit(solution)/shard_map/ppermute | solution.py:40
  58.4 36.4 %collective-permute-start.8 = (bf16[512,1024]{1,0:T(8,128)(2,1)S(1)}, bf16[512,1024]{1,0:T(8,128)(2,1)S(1)}, u32[]{:S(2)}, u32[]{:S(2)}) collective-permute-start(bf16[512,1024]{1,0:T(8,128)(2,1)S(1)} %copy-done.3), channel_id=1, source_target_pairs={{0,2},{1,3},{2,0},{3,1},{4,6},{5,7},{6,4},{7,5},{8,10},{9,11},{10,... | collective-permute-start | bytes 3145736 | tf_op jit(solution)/shard_map/ppermute | solution.py:40
  72.0 26.1 %copy-start.5 = (bf16[128,1024]{1,0:T(8,128)(2,1)S(1)}, bf16[128,1024]{1,0:T(8,128)(2,1)}, u32[]{:S(2)}) copy-start(bf16[128,1024]{1,0:T(8,128)(2,1)} %param.18) | copy-start | bytes 786436
  78.8 26.9 %copy-start.15 = (bf16[256,1024]{1,0:T(8,128)(2,1)}, bf16[256,1024]{1,0:T(8,128)(2,1)S(1)}, u32[]{:S(2)}) copy-start(bf16[256,1024]{1,0:T(8,128)(2,1)S(1)} %collective-permute-done.6) | copy-start | bytes 1572868
  87.6 18.1 %copy-start.17 = (bf16[256,1024]{1,0:T(8,128)(2,1)}, bf16[256,1024]{1,0:T(8,128)(2,1)S(1)}, u32[]{:S(2)}) copy-start(bf16[256,1024]{1,0:T(8,128)(2,1)S(1)} %collective-permute-done.7) | copy-start | bytes 1572868
  94.8 10.9 %copy-start.7 = (bf16[512,1024]{1,0:T(8,128)(2,1)}, bf16[512,1024]{1,0:T(8,128)(2,1)S(1)}, u32[]{:S(2)}) copy-start(bf16[512,1024]{1,0:T(8,128)(2,1)S(1)} %collective-permute-done.8) | copy-start | bytes 3145732
  94.8 19.9 %collective-permute-start.10 = (bf16[512,128]{1,0:T(8,128)(2,1)S(1)}, bf16[512,128]{1,0:T(8,128)(2,1)}, u32[]{:S(2)}, u32[]{:S(2)}) collective-permute-start(bf16[512,128]{1,0:T(8,128)(2,1)S(1)} %bitcast.221), channel_id=1, source_target_pairs={{0,4},{1,5},{2,6},{3,7},{4,0},{5,1},{6,2},{7,3},{8,12},{9,13},{10,... | collective-permute-start | bytes 393224 | tf_op jit(solution)/shard_map/ppermute | solution.py:40
  94.8 19.9 %collective-permute-start.11 = (bf16[512,128]{1,0:T(8,128)(2,1)S(1)}, bf16[512,128]{1,0:T(8,128)(2,1)}, u32[]{:S(2)}, u32[]{:S(2)}) collective-permute-start(bf16[512,128]{1,0:T(8,128)(2,1)S(1)} %bitcast.222), channel_id=1, source_target_pairs={{0,8},{1,9},{2,10},{3,11},{4,12},{5,13},{6,14},{7,15},{8,0},{9,1},... | collective-permute-start | bytes 393224 | tf_op jit(solution)/shard_map/ppermute | solution.py:40
  98.1 16.6 %collective-permute-start.9 = (bf16[512,128]{1,0:T(8,128)(2,1)S(1)}, bf16[512,128]{1,0:T(8,128)(2,1)}, u32[]{:S(2)}, u32[]{:S(2)}) collective-permute-start(bf16[512,128]{1,0:T(8,128)(2,1)S(1)} %bitcast.223), channel_id=1, source_target_pairs={{0,2},{1,3},{2,0},{3,1},{4,6},{5,7},{6,4},{7,5},{8,10},{9,11},{10,... | collective-permute-start | bytes 393224 | tf_op jit(solution)/shard_map/ppermute | solution.py:40
  99.3 15.4 %collective-permute-start.12 = (bf16[128,1024]{1,0:T(8,128)(2,1)}, bf16[128,1024]{1,0:T(8,128)(2,1)}, u32[]{:S(2)}, u32[]{:S(2)}) collective-permute-start(bf16[128,1024]{1,0:T(8,128)(2,1)} %get-tuple-element.30), channel_id=1, source_target_pairs={{0,1},{1,2},{2,3},{3,4},{4,5},{5,6},{6,7},{7,8},{8,9},{9,10},{10,1... | collective-permute-start | bytes 786440 | tf_op jit(solution)/shard_map/ppermute | solution.py:27
  101.3 14.6 %collective-permute-start.13 = (bf16[128,1024]{1,0:T(8,128)(2,1)}, bf16[128,1024]{1,0:T(8,128)(2,1)S(1)}, u32[]{:S(2)}, u32[]{:S(2)}) collective-permute-start(bf16[128,1024]{1,0:T(8,128)(2,1)} %get-tuple-element.29), channel_id=1, source_target_pairs={{1,0},{2,1},{3,2},{4,3},{5,4},{6,5},{7,6},{8,7},{9,8},{10,9},{11,1... | collective-permute-start | bytes 786440 | tf_op jit(solution)/shard_map/ppermute | solution.py:27
  114.7 1.2 copy-start.6
  114.7 1.4 copy-start.8
  115.8 1.7 %copy-start.14 = (bf16[256,1024]{1,0:T(8,128)(2,1)S(1)}, bf16[256,1024]{1,0:T(8,128)(2,1)}, u32[]{:S(2)}) copy-start(bf16[256,1024]{1,0:T(8,128)(2,1)} %copy-done.13) | copy-start | bytes 1572868
  115.8 1.7 %copy-start.16 = (bf16[256,1024]{1,0:T(8,128)(2,1)S(1)}, bf16[256,1024]{1,0:T(8,128)(2,1)}, u32[]{:S(2)}) copy-start(bf16[256,1024]{1,0:T(8,128)(2,1)} %copy-done.15) | copy-start | bytes 1572868
  116.1 2.8 %copy-start.18 = (bf16[256,1024]{1,0:T(8,128)(2,1)S(1)}, bf16[256,1024]{1,0:T(8,128)(2,1)}, u32[]{:S(2)}) copy-start(bf16[256,1024]{1,0:T(8,128)(2,1)} %copy-done.17) | copy-start | bytes 1572868
  132.1 3.7 %copy-start.1 = (bf16[2304,2048]{1,0:T(8,128)(2,1)}, bf16[2304,2048]{1,0:T(8,128)(2,1)S(1)}, u32[]{:S(2)}) copy-start(bf16[2304,2048]{1,0:T(8,128)(2,1)S(1)} %convolution_convert_fusion.refs_0_.refs_1_.refs_2_.refs_3_.refs_5_.refs_6_.refs_7_) | copy-start | bytes 28311556
  135.8 4.2 %copy-start.10 = (s32[8,3]{0,1:T(4,128)S(1)}, s32[8,3]{0,1:T(4,128)}, u32[]{:S(2)}) copy-start(s32[8,3]{0,1:T(4,128)} %param.15) | copy-start | bytes 292
  135.8 4.2 %copy-start.11 = (s32[8,4]{0,1:T(4,128)S(1)}, s32[8,4]{0,1:T(4,128)}, u32[]{:S(2)}) copy-start(s32[8,4]{0,1:T(4,128)} %param.16) | copy-start | bytes 388
  135.8 4.3 %copy-start.12 = (s32[4]{0:T(128)S(1)}, s32[4]{0:T(128)}, u32[]{:S(2)}) copy-start(s32[4]{0:T(128)} %constant.58.clone) | copy-start | bytes 52
  137.3 6.8 %collective-permute-start.14 = (bf16[512,2048]{1,0:T(8,128)(2,1)}, bf16[512,2048]{1,0:T(8,128)(2,1)}, u32[]{:S(2)}, u32[]{:S(2)}) collective-permute-start(bf16[512,2048]{1,0:T(8,128)(2,1)} %slice.359), channel_id=1, source_target_pairs={{0,1},{1,0},{2,3},{3,2},{4,5},{5,4},{6,7},{7,6},{8,9},{9,8},{10,11... | collective-permute-start | bytes 6291464 | tf_op jit(solution)/shard_map/ppermute | solution.py:40

commit v15 on v13

--- a/solution.py
+++ b/solution.py
@@ -118,7 +118,7 @@
 
 def attention_kernel(table_ref, q_ref, *refs):
     kv_refs = refs[:NKEY]
-    out_ref = refs[NKEY]
+    w_ref, out_ref, att_ref = refs[NKEY:]
     lane = lax.broadcasted_iota(jnp.int32, (1, 2 * HD), 1)
     low = lane < HD
     for pair in range(HEADS // 2):
@@ -135,7 +135,10 @@
             weights, vs, (((0,), (0,)), ((), ())), preferred_element_type=jnp.float32
         )
         merged = jnp.where(low, both[:BS], both[BS:])
-        out_ref[:, cols] = merged.astype(jnp.bfloat16)
+        att_ref[:, cols] = merged.astype(jnp.bfloat16)
+    out_ref[...] = jnp.dot(att_ref[...], w_ref[...], preferred_element_type=jnp.float32).astype(
+        jnp.bfloat16
+    )
 
 
 def split_queries(queries):
@@ -149,7 +152,7 @@
     return jnp.where(d_head == j_head, qt * scale, jnp.zeros_like(qt))
 
 
-def attend(queries, kv_sources, table):
+def attend(queries, kv_sources, table, out_weight):
     count = table.shape[0]
     pairs = HEADS // 2
     in_specs = [pl.BlockSpec((1, pairs, 2 * HD, 2 * BS), lambda b, t: (b, 0, 0, 0))]
@@ -157,11 +160,14 @@
     for j, src in enumerate(kv_sources):
         in_specs.append(pl.BlockSpec((BS, 2 * D), lambda b, t, j=j: (t[b, j], 0)))
         operands.append(src)
+    in_specs.append(pl.BlockSpec(out_weight.shape, lambda b, t: (0, 0)))
+    operands.append(out_weight)
     grid_spec = pltpu.PrefetchScalarGridSpec(
         num_scalar_prefetch=1,
         grid=(count,),
         in_specs=in_specs,
         out_specs=pl.BlockSpec((BS, D), lambda b, t: (b, 0)),
+        scratch_shapes=[pltpu.VMEM((BS, D), jnp.bfloat16)],
     )
     return pl.pallas_call(
         attention_kernel,
@@ -230,8 +236,7 @@
     table = jnp.concatenate([own_slot, graph_slot, far_slot + far_base[None, :]], axis=1)
     table = table.astype(jnp.int32)
     sources = [kv_all] * 4 + [kv_chip] + [kv_all] * (NEXP - 1)
-    attended = attend(queries, sources, table)
-    return jnp.dot(attended, out_weight, preferred_element_type=jnp.float32).astype(jnp.bfloat16)
+    return attend(queries, sources, table, out_weight)
 
 
 def solution(mesh):

time: 154 us -> 146 us (0.948)
  local copies, waits for them, and re-layouts: 16.4 us -> 12.3 us
  other arithmetic: 10.5 us -> 6.7 us
  matrix products: 33.4 us -> 29.9 us
  Pallas kernels: 14.7 us -> 17.4 us
    dot_general x1 -> x0, matrix products: 3.45 us -> none  [on_device(): jnp.dot(attended, out_weight, preferred_element_type=jnp.float32)]
    pallas_call x1, Pallas kernels: 14.7 us -> 17.4 us  [attend(): pl.pallas_call(attention_kernel, grid_spec=grid_spec, out_shape=jax.Shape...]
    select_n x1, other arithmetic: 5.07 us -> 2.73 us  [split_queries(): return jnp.where(d_head == j_head, qt * scale, jnp.zeros_like(qt))]
    unnamed x63 -> x61, local copies, waits for them, and re-layouts: 7.28 us -> 6.12 us
  transfers between devices with their start and end apart: 15 -> 15, of which waited for: 8 -> 7; matrix products, arithmetic and copies ran while one was open for 20% -> 19% of each run, Pallas kernels for 0% -> 0%
where the time goes in v15:
time: 146 us; the launch traced here: 145 us
  starting transfers between devices  39 us (27%)
  waiting for transfers between devices  38.5 us (26%)
  matrix products  29.9 us (20%)
  Pallas kernels  17.4 us (12%)
  local copies, waits for them, and re-layouts  12.3 us (8%)
  other arithmetic  6.7 us (5%)
    ppermute x6, waiting for transfers between devices, shift_rows(): return lax.ppermute(x, axis, pairs)  26.4 us
    ppermute x9, starting transfers between devices, partner(): return lax.ppermute(value, axis, pairs)  21.1 us
    ppermute x6, starting transfers between devices, shift_rows(): return lax.ppermute(x, axis, pairs)  17.9 us
    pallas_call x1, Pallas kernels, attend(): pl.pallas_call(attention_kernel, grid_spec=grid_spec, out_shape=jax.Shape...  17.4 us
    dot_general x8, matrix products, step(): jnp.einsum('wsk,wkc->wsc', bands[lo - REACH:hi - REACH], stacked, precisi...  15.1 us
    ppermute x9, waiting for transfers between devices, partner(): return lax.ppermute(value, axis, pairs)  12.1 us
    dot_general x1, matrix products, on_device(): jnp.dot(all_blended, kv_weight, preferred_element_type=jnp.float32)  10.3 us
    unnamed x61, local copies, waits for them, and re-layouts  6.12 us
  transfers between devices with their start and end apart: 15, of which 7 were waited for; matrix products, arithmetic and copies ran while one was open for 19% of the time, Pallas kernels for 0%

profile of v15, /device:TPU:13, one launch (start us, length us, event | category | flops | bytes accessed | tf_op | source)
XLA Modules:
  0.0 144.9 jit_solution(17004522363652194327)
XLA Ops:
  0.0 0.8 copy.34
  1.0 1.8 %select_reduce_fusion = f32[8,5,64,64]{3,2,1,0:T(8,128)S(1)} fusion(f32[8,3,64,64]{3,2,1,0:T(8,128)} %param.13, pred[8,3,5]{2,1,0:T(4,128)(4,1)S(1)} %iota_compare_fusion), kind=kLoop, calls=%fused_computation.2 | loop fusion | flops 819200 | bytes 1048696 | tf_op jit(solution)/shard_map/reduce_sum | solution.py:61
  2.7 0.4 copy.35
  3.1 0.4 copy.36
  3.6 1.1 pad_maximum_fusion.1
  4.7 3.8 %collective-permute-start = (f32[8,64,448]{2,1,0:T(8,128)S(1)}, f32[8,64,448]{2,1,0:T(8,128)S(1)}, u32[]{:S(2)}, u32[]{:S(2)}) collective-permute-start(f32[8,64,448]{2,1,0:T(8,128)S(1)} %pad_maximum_fusion.1), channel_id=1, source_target_pairs={{0,1},{1,2},{2,3},{3,4},{4,5},{5,6},{6,7},{7,8},{8,9},{9,10},{10,1... | collective-permute-start | bytes 2752520 | tf_op jit(solution)/shard_map/ppermute | solution.py:27
  8.5 1.9 %collective-permute-start.1 = (f32[8,64,448]{2,1,0:T(8,128)S(1)}, f32[8,64,448]{2,1,0:T(8,128)S(1)}, u32[]{:S(2)}, u32[]{:S(2)}) collective-permute-start(f32[8,64,448]{2,1,0:T(8,128)S(1)} %pad_maximum_fusion.1), channel_id=1, source_target_pairs={{1,0},{2,1},{3,2},{4,3},{5,4},{6,5},{7,6},{8,7},{9,8},{10,9},{11,1... | collective-permute-start | bytes 2752520 | tf_op jit(solution)/shard_map/ppermute | solution.py:27
  10.5 0.2 collective-permute-start.4
  10.8 2.3 %collective-permute-start.5 = (bf16[256,1024]{1,0:T(8,128)(2,1)S(1)}, bf16[256,1024]{1,0:T(8,128)(2,1)S(1)}, u32[]{:S(2)}, u32[]{:S(2)}) collective-permute-start(bf16[256,1024]{1,0:T(8,128)(2,1)S(1)} %get-tuple-element.24), channel_id=1, source_target_pairs={{0,8},{1,9},{2,10},{3,11},{4,12},{5,13},{6,14},{7,15},{8,0},{9,1},... | collective-permute-start | bytes 1572872 | tf_op jit(solution)/shard_map/ppermute | solution.py:40
  13.1 12.5 %collective-permute-done = f32[8,64,448]{2,1,0:T(8,128)S(1)} collective-permute-done((f32[8,64,448]{2,1,0:T(8,128)S(1)}, f32[8,64,448]{2,1,0:T(8,128)S(1)}, u32[]{:S(2)}, u32[]{:S(2)}) %collective-permute-start) | collective-permute-done | bytes 917536 | tf_op jit(solution)/shard_map/ppermute | solution.py:27
  25.6 7.5 %collective-permute-done.1 = f32[8,64,448]{2,1,0:T(8,128)S(1)} collective-permute-done((f32[8,64,448]{2,1,0:T(8,128)S(1)}, f32[8,64,448]{2,1,0:T(8,128)S(1)}, u32[]{:S(2)}, u32[]{:S(2)}) %collective-permute-start.1) | collective-permute-done | bytes 917536 | tf_op jit(solution)/shard_map/ppermute | solution.py:27
  33.5 0.4 copy.38
  34.0 1.3 fusion.67
  35.8 1.2 fusion.19
  37.4 1.0 fusion.13
  38.6 1.2 fusion.16
  39.9 1.9 %collective-permute-start.2 = (f32[8,64,256]{2,1,0:T(8,128)S(1)}, f32[8,64,256]{2,1,0:T(8,128)S(1)}, u32[]{:S(2)}, u32[]{:S(2)}) collective-permute-start(f32[8,64,256]{2,1,0:T(8,128)S(1)} %pad_maximum_fusion.4), channel_id=1, source_target_pairs={{0,1},{1,2},{2,3},{3,4},{4,5},{5,6},{6,7},{7,8},{8,9},{9,10},{10,1... | collective-permute-start | bytes 1572872 | tf_op jit(solution)/shard_map/ppermute | solution.py:27
  41.8 3.2 %collective-permute-start.3 = (f32[8,64,256]{2,1,0:T(8,128)S(1)}, f32[8,64,256]{2,1,0:T(8,128)S(1)}, u32[]{:S(2)}, u32[]{:S(2)}) collective-permute-start(f32[8,64,256]{2,1,0:T(8,128)S(1)} %pad_maximum_fusion.4), channel_id=1, source_target_pairs={{1,0},{2,1},{3,2},{4,3},{5,4},{6,5},{7,6},{8,7},{9,8},{10,9},{11,1... | collective-permute-start | bytes 1572872 | tf_op jit(solution)/shard_map/ppermute | solution.py:27
  45.1 0.7 fusion.70
  45.8 6.4 %collective-permute-start.7 = (bf16[256,1024]{1,0:T(8,128)(2,1)S(1)}, bf16[256,1024]{1,0:T(8,128)(2,1)S(1)}, u32[]{:S(2)}, u32[]{:S(2)}) collective-permute-start(bf16[256,1024]{1,0:T(8,128)(2,1)S(1)} %get-tuple-element.23), channel_id=1, source_target_pairs={{0,8},{1,9},{2,10},{3,11},{4,12},{5,13},{6,14},{7,15},{8,0},{9,1},... | collective-permute-start | bytes 1572872 | tf_op jit(solution)/shard_map/ppermute | solution.py:40
  52.2 2.5 %collective-permute-start.8 = (bf16[512,1024]{1,0:T(8,128)(2,1)S(1)}, bf16[512,1024]{1,0:T(8,128)(2,1)S(1)}, u32[]{:S(2)}, u32[]{:S(2)}) collective-permute-start(bf16[512,1024]{1,0:T(8,128)(2,1)S(1)} %copy-done.3), channel_id=1, source_target_pairs={{0,2},{1,3},{2,0},{3,1},{4,6},{5,7},{6,4},{7,5},{8,10},{9,11},{10,... | collective-permute-start | bytes 3145736 | tf_op jit(solution)/shard_map/ppermute | solution.py:40
  54.7 5.4 %collective-permute-done.3 = f32[8,64,256]{2,1,0:T(8,128)S(1)} collective-permute-done((f32[8,64,256]{2,1,0:T(8,128)S(1)}, f32[8,64,256]{2,1,0:T(8,128)S(1)}, u32[]{:S(2)}, u32[]{:S(2)}) %collective-permute-start.3) | collective-permute-done | bytes 524320 | tf_op jit(solution)/shard_map/ppermute | solution.py:27
  60.8 1.3 fusion.12
  62.6 1.2 fusion.20
  64.1 1.0 fusion.14
  65.3 6.8 %fusion.18 = bf16[8,64,128]{2,1,0:T(8,128)(2,1)S(1)} fusion(f32[8,64,320]{1,2,0:T(8,128)S(1)} %bitcast.204, f32[8,320,128]{2,1,0:T(8,128)S(1)} %bitcast.210, f32[20,64,128]{2,1,0:T(8,128)S(1)} %fusion.12, f32[20,64,128]{2,1,0:T(8,128)S(1)} %fusion.67, f32[16,64,128]{2,1,0:T(8,128)S(1)} %fusion.20, f32[8,64,128]{2,1,0:T(8,128)S(1)} %fusion.16, ...), kind=kOutput, calls=%fused_computation.29 | convolution fusion | flops 127139840 | bytes 4194340 | tf_op jit(solution)/shard_map/wsk,wkc->wsc/dot_general | solution.py:78
  72.2 0.6 collective-permute-done.7
  72.8 7.0 %collective-permute-done.8 = bf16[512,1024]{1,0:T(8,128)(2,1)S(1)} collective-permute-done((bf16[512,1024]{1,0:T(8,128)(2,1)S(1)}, bf16[512,1024]{1,0:T(8,128)(2,1)S(1)}, u32[]{:S(2)}, u32[]{:S(2)}) %collective-permute-start.8) | collective-permute-done | bytes 1048608 | tf_op jit(solution)/shard_map/ppermute | solution.py:40
  79.8 0.4 add_convert_fusion.3
  80.2 4.9 %collective-permute-start.9 = (bf16[128,1024]{1,0:T(8,128)(2,1)S(1)}, bf16[128,1024]{1,0:T(8,128)(2,1)S(1)}, u32[]{:S(2)}, u32[]{:S(2)}) collective-permute-start(bf16[128,1024]{1,0:T(8,128)(2,1)S(1)} %get-tuple-element.22), channel_id=1, source_target_pairs={{0,1},{1,2},{2,3},{3,4},{4,5},{5,6},{6,7},{7,8},{8,9},{9,10},{10,1... | collective-permute-start | bytes 786440 | tf_op jit(solution)/shard_map/ppermute | solution.py:27
  85.2 2.1 %collective-permute-start.10 = (bf16[128,1024]{1,0:T(8,128)(2,1)S(1)}, bf16[128,1024]{1,0:T(8,128)(2,1)S(1)}, u32[]{:S(2)}, u32[]{:S(2)}) collective-permute-start(bf16[128,1024]{1,0:T(8,128)(2,1)S(1)} %get-tuple-element.21), channel_id=1, source_target_pairs={{1,0},{2,1},{3,2},{4,3},{5,4},{6,5},{7,6},{8,7},{9,8},{10,9},{11,1... | collective-permute-start | bytes 786440 | tf_op jit(solution)/shard_map/ppermute | solution.py:27
  87.4 2.0 %collective-permute-start.11 = (bf16[512,128]{1,0:T(8,128)(2,1)S(1)}, bf16[512,128]{1,0:T(8,128)(2,1)S(1)}, u32[]{:S(2)}, u32[]{:S(2)}) collective-permute-start(bf16[512,128]{1,0:T(8,128)(2,1)S(1)} %bitcast.220), channel_id=1, source_target_pairs={{0,2},{1,3},{2,0},{3,1},{4,6},{5,7},{6,4},{7,5},{8,10},{9,11},{10,... | collective-permute-start | bytes 393224 | tf_op jit(solution)/shard_map/ppermute | solution.py:40
  89.3 4.1 %collective-permute-start.13 = (bf16[512,128]{1,0:T(8,128)(2,1)S(1)}, bf16[512,128]{1,0:T(8,128)(2,1)S(1)}, u32[]{:S(2)}, u32[]{:S(2)}) collective-permute-start(bf16[512,128]{1,0:T(8,128)(2,1)S(1)} %bitcast.222), channel_id=1, source_target_pairs={{0,8},{1,9},{2,10},{3,11},{4,12},{5,13},{6,14},{7,15},{8,0},{9,1},... | collective-permute-start | bytes 393224 | tf_op jit(solution)/shard_map/ppermute | solution.py:40
  93.5 1.0 collective-permute-done.10
  94.6 0.4 fusion.21
  95.1 0.4 fusion.4
  95.5 4.5 %collective-permute-done.13 = bf16[512,128]{1,0:T(8,128)(2,1)S(1)} collective-permute-done((bf16[512,128]{1,0:T(8,128)(2,1)S(1)}, bf16[512,128]{1,0:T(8,128)(2,1)S(1)}, u32[]{:S(2)}, u32[]{:S(2)}) %collective-permute-start.13) | collective-permute-done | bytes 131104 | tf_op jit(solution)/shard_map/ppermute | solution.py:40
  100.0 0.4 fusion.5
  100.5 10.3 %convolution_convert_fusion.refs_0_.refs_1_.refs_2_.refs_3_.refs_5_.refs_6_.refs_7_ = bf16[2304,2048]{1,0:T(8,128)(2,1)S(1)} fusion(bf16[2304,1024]{1,0:T(8,128)(2,1)S(1)} %fusion.5, bf16[1024,3072]{1,0:T(8,128)(2,1)S(1)} %bitcast.224), kind=kOutput, calls=%fused_computation | convolution fusion | flops 9668395008 | bytes 18350080 | tf_op jit(solution)/shard_map/dot_general | solution.py:225
  110.8 3.7 %copy-done.2 = bf16[2304,2048]{1,0:T(8,128)(2,1)} copy-done((bf16[2304,2048]{1,0:T(8,128)(2,1)}, bf16[2304,2048]{1,0:T(8,128)(2,1)S(1)}, u32[]{:S(2)}) %copy-start.2) | copy-done | bytes 9437208
  114.4 1.5 %slice.359 = bf16[512,2048]{1,0:T(8,128)(2,1)} slice(bf16[2304,2048]{1,0:T(8,128)(2,1)S(1)} %convolution_convert_fusion.refs_0_.refs_1_.refs_2_.refs_3_.refs_5_.refs_6_.refs_7_), slice={[128:640], [0:2048]} | slice | bytes 4194304 | tf_op jit(solution)/shard_map/slice | solution.py:228
  115.9 3.5 %collective-permute-start.14 = (bf16[512,2048]{1,0:T(8,128)(2,1)}, bf16[512,2048]{1,0:T(8,128)(2,1)}, u32[]{:S(2)}, u32[]{:S(2)}) collective-permute-start(bf16[512,2048]{1,0:T(8,128)(2,1)} %slice.359), channel_id=1, source_target_pairs={{0,1},{1,0},{2,3},{3,2},{4,5},{5,4},{6,7},{7,6},{8,9},{9,8},{10,11... | collective-permute-start | bytes 6291464 | tf_op jit(solution)/shard_map/ppermute | solution.py:40
  119.6 0.7 pad_add_fusion.table_ref
  120.4 2.8 %fusion.9 = bf16[64,8,8,128]{3,1,2,0:T(8,128)(2,1)S(1)} fusion(bf16[512,1024]{1,0:T(8,128)(2,1)S(1)} %add_convert_fusion.3, bf16[1024,3072]{1,0:T(8,128)(2,1)} %param.19), kind=kOutput, calls=%fused_computation.15 | convolution fusion | flops 1074266112 | bytes 4194304 | tf_op jit(solution)/shard_map/dot_general | solution.py:217
  123.2 0.3 copy.51
  123.5 1.1 copy.48
  124.6 2.7 %fusion.1.q_ref = bf16[8,8,128,128]{3,2,1,0:T(8,128)(2,1)} fusion(bf16[8,8,128,64]{3,2,1,0:T(8,128)(2,1)S(1)} %bitcast.207, pred[128,128]{1,0:T(8,128)(4,1)S(1)} %select_compare_fusion), kind=kLoop, calls=%fused_computation.4 | loop fusion | flops 7340032 | bytes 3162112 | tf_op jit(solution)/shard_map/jit(_where)/select_n | solution.py:152
  127.3 17.4 %shard_map.109 = bf16[512,1024]{1,0:T(8,128)(2,1)} custom-call(s32[8,8]{1,0:T(8,128)} %pad_add_fusion.table_ref, bf16[8,8,128,128]{3,2,1,0:T(8,128)(2,1)} %fusion.1.q_ref, bf16[2304,2048]{1,0:T(8,128)(2,1)} %copy-done.2, bf16[2304,2048]{1,0:T(8,128)(2,1)} %copy-done.2, bf16[2304,2048]{1,0:T(8,128)(2,1)} %copy-done.2, bf16[2304,2048]{1,0:T(8,128)(2,1)} %copy-done.2, ...), custom_call_target="tpu_custom_call" | custom-call | tf_op jit(solution)/shard_map/pallas_call | solution.py:172
  (107 shorter events, 3.7 us)
Async XLA Ops:
  0.0 79.8 %copy-start = (bf16[128,1024]{1,0:T(8,128)(2,1)S(1)}, bf16[128,1024]{1,0:T(8,128)(2,1)}, u32[]{:S(2)}) copy-start(bf16[128,1024]{1,0:T(8,128)(2,1)} %param.18) | copy-start | bytes 786436
  3.1 7.3 %copy-start.3 = (bf16[512,1024]{1,0:T(8,128)(2,1)S(1)}, bf16[512,1024]{1,0:T(8,128)(2,1)}, u32[]{:S(2)}) copy-start(bf16[512,1024]{1,0:T(8,128)(2,1)} %param.11) | copy-start | bytes 3145732
  4.7 28.4 %copy-start.4 = (f32[512,128]{1,0:T(8,128)S(1)}, f32[512,128]{1,0:T(8,128)}, u32[]{:S(2)}) copy-start(f32[512,128]{1,0:T(8,128)} %param.12) | copy-start | bytes 786436
  4.7 20.9 %collective-permute-start = (f32[8,64,448]{2,1,0:T(8,128)S(1)}, f32[8,64,448]{2,1,0:T(8,128)S(1)}, u32[]{:S(2)}, u32[]{:S(2)}) collective-permute-start(f32[8,64,448]{2,1,0:T(8,128)S(1)} %pad_maximum_fusion.1), channel_id=1, source_target_pairs={{0,1},{1,2},{2,3},{3,4},{4,5},{5,6},{6,7},{7,8},{8,9},{9,10},{10,1... | collective-permute-start | bytes 2752520 | tf_op jit(solution)/shard_map/ppermute | solution.py:27
  8.5 24.6 %collective-permute-start.1 = (f32[8,64,448]{2,1,0:T(8,128)S(1)}, f32[8,64,448]{2,1,0:T(8,128)S(1)}, u32[]{:S(2)}, u32[]{:S(2)}) collective-permute-start(f32[8,64,448]{2,1,0:T(8,128)S(1)} %pad_maximum_fusion.1), channel_id=1, source_target_pairs={{1,0},{2,1},{3,2},{4,3},{5,4},{6,5},{7,6},{8,7},{9,8},{10,9},{11,1... | collective-permute-start | bytes 2752520 | tf_op jit(solution)/shard_map/ppermute | solution.py:27
  10.5 35.2 %collective-permute-start.4 = (bf16[256,1024]{1,0:T(8,128)(2,1)S(1)}, bf16[256,1024]{1,0:T(8,128)(2,1)S(1)}, u32[]{:S(2)}, u32[]{:S(2)}) collective-permute-start(bf16[256,1024]{1,0:T(8,128)(2,1)S(1)} %get-tuple-element.24), channel_id=1, source_target_pairs={{0,4},{1,5},{2,6},{3,7},{4,0},{5,1},{6,2},{7,3},{8,12},{9,13},{10,... | collective-permute-start | bytes 1572872 | tf_op jit(solution)/shard_map/ppermute | solution.py:40
  10.8 41.4 %collective-permute-start.5 = (bf16[256,1024]{1,0:T(8,128)(2,1)S(1)}, bf16[256,1024]{1,0:T(8,128)(2,1)S(1)}, u32[]{:S(2)}, u32[]{:S(2)}) collective-permute-start(bf16[256,1024]{1,0:T(8,128)(2,1)S(1)} %get-tuple-element.24), channel_id=1, source_target_pairs={{0,8},{1,9},{2,10},{3,11},{4,12},{5,13},{6,14},{7,15},{8,0},{9,1},... | collective-permute-start | bytes 1572872 | tf_op jit(solution)/shard_map/ppermute | solution.py:40
  38.6 6.4 %copy-start.5 = (f32[9]{0:T(128)S(1)}, f32[9]{0:T(128)}, u32[]{:S(2)}) copy-start(f32[9]{0:T(128)} %param.17) | copy-start | bytes 112
  39.9 14.8 %collective-permute-start.2 = (f32[8,64,256]{2,1,0:T(8,128)S(1)}, f32[8,64,256]{2,1,0:T(8,128)S(1)}, u32[]{:S(2)}, u32[]{:S(2)}) collective-permute-start(f32[8,64,256]{2,1,0:T(8,128)S(1)} %pad_maximum_fusion.4), channel_id=1, source_target_pairs={{0,1},{1,2},{2,3},{3,4},{4,5},{5,6},{6,7},{7,8},{8,9},{9,10},{10,1... | collective-permute-start | bytes 1572872 | tf_op jit(solution)/shard_map/ppermute | solution.py:27
  41.8 18.3 %collective-permute-start.3 = (f32[8,64,256]{2,1,0:T(8,128)S(1)}, f32[8,64,256]{2,1,0:T(8,128)S(1)}, u32[]{:S(2)}, u32[]{:S(2)}) collective-permute-start(f32[8,64,256]{2,1,0:T(8,128)S(1)} %pad_maximum_fusion.4), channel_id=1, source_target_pairs={{1,0},{2,1},{3,2},{4,3},{5,4},{6,5},{7,6},{8,7},{9,8},{10,9},{11,1... | collective-permute-start | bytes 1572872 | tf_op jit(solution)/shard_map/ppermute | solution.py:27
  45.0 27.2 %collective-permute-start.6 = (bf16[256,1024]{1,0:T(8,128)(2,1)S(1)}, bf16[256,1024]{1,0:T(8,128)(2,1)S(1)}, u32[]{:S(2)}, u32[]{:S(2)}) collective-permute-start(bf16[256,1024]{1,0:T(8,128)(2,1)S(1)} %get-tuple-element.23), channel_id=1, source_target_pairs={{0,4},{1,5},{2,6},{3,7},{4,0},{5,1},{6,2},{7,3},{8,12},{9,13},{10,... | collective-permute-start | bytes 1572872 | tf_op jit(solution)/shard_map/ppermute | solution.py:40
  45.8 27.0 %collective-permute-start.7 = (bf16[256,1024]{1,0:T(8,128)(2,1)S(1)}, bf16[256,1024]{1,0:T(8,128)(2,1)S(1)}, u32[]{:S(2)}, u32[]{:S(2)}) collective-permute-start(bf16[256,1024]{1,0:T(8,128)(2,1)S(1)} %get-tuple-element.23), channel_id=1, source_target_pairs={{0,8},{1,9},{2,10},{3,11},{4,12},{5,13},{6,14},{7,15},{8,0},{9,1},... | collective-permute-start | bytes 1572872 | tf_op jit(solution)/shard_map/ppermute | solution.py:40
  52.2 27.6 %collective-permute-start.8 = (bf16[512,1024]{1,0:T(8,128)(2,1)S(1)}, bf16[512,1024]{1,0:T(8,128)(2,1)S(1)}, u32[]{:S(2)}, u32[]{:S(2)}) collective-permute-start(bf16[512,1024]{1,0:T(8,128)(2,1)S(1)} %copy-done.3), channel_id=1, source_target_pairs={{0,2},{1,3},{2,0},{3,1},{4,6},{5,7},{6,4},{7,5},{8,10},{9,11},{10,... | collective-permute-start | bytes 3145736 | tf_op jit(solution)/shard_map/ppermute | solution.py:40
  79.8 20.7 %slice-start = ((s8[6291456]{0:T(1024)(128)(4,1)}), s8[4194304]{0:T(1024)(128)(4,1)S(1)}, s32[]{:S(2)}) async-start(s8[6291456]{0:T(1024)(128)(4,1)} %bitcast.223), calls=%async_computation | async-start | bytes 8388608
  80.2 13.2 %collective-permute-start.9 = (bf16[128,1024]{1,0:T(8,128)(2,1)S(1)}, bf16[128,1024]{1,0:T(8,128)(2,1)S(1)}, u32[]{:S(2)}, u32[]{:S(2)}) collective-permute-start(bf16[128,1024]{1,0:T(8,128)(2,1)S(1)} %get-tuple-element.22), channel_id=1, source_target_pairs={{0,1},{1,2},{2,3},{3,4},{4,5},{5,6},{6,7},{7,8},{8,9},{9,10},{10,1... | collective-permute-start | bytes 786440 | tf_op jit(solution)/shard_map/ppermute | solution.py:27
  85.2 9.4 %collective-permute-start.10 = (bf16[128,1024]{1,0:T(8,128)(2,1)S(1)}, bf16[128,1024]{1,0:T(8,128)(2,1)S(1)}, u32[]{:S(2)}, u32[]{:S(2)}) collective-permute-start(bf16[128,1024]{1,0:T(8,128)(2,1)S(1)} %get-tuple-element.21), channel_id=1, source_target_pairs={{1,0},{2,1},{3,2},{4,3},{5,4},{6,5},{7,6},{8,7},{9,8},{10,9},{11,1... | collective-permute-start | bytes 786440 | tf_op jit(solution)/shard_map/ppermute | solution.py:27
  87.4 7.3 %collective-permute-start.11 = (bf16[512,128]{1,0:T(8,128)(2,1)S(1)}, bf16[512,128]{1,0:T(8,128)(2,1)S(1)}, u32[]{:S(2)}, u32[]{:S(2)}) collective-permute-start(bf16[512,128]{1,0:T(8,128)(2,1)S(1)} %bitcast.220), channel_id=1, source_target_pairs={{0,2},{1,3},{2,0},{3,1},{4,6},{5,7},{6,4},{7,5},{8,10},{9,11},{10,... | collective-permute-start | bytes 393224 | tf_op jit(solution)/shard_map/ppermute | solution.py:40
  89.3 5.8 %collective-permute-start.12 = (bf16[512,128]{1,0:T(8,128)(2,1)S(1)}, bf16[512,128]{1,0:T(8,128)(2,1)S(1)}, u32[]{:S(2)}, u32[]{:S(2)}) collective-permute-start(bf16[512,128]{1,0:T(8,128)(2,1)S(1)} %bitcast.221), channel_id=1, source_target_pairs={{0,4},{1,5},{2,6},{3,7},{4,0},{5,1},{6,2},{7,3},{8,12},{9,13},{10,... | collective-permute-start | bytes 393224 | tf_op jit(solution)/shard_map/ppermute | solution.py:40
  89.3 10.7 %collective-permute-start.13 = (bf16[512,128]{1,0:T(8,128)(2,1)S(1)}, bf16[512,128]{1,0:T(8,128)(2,1)S(1)}, u32[]{:S(2)}, u32[]{:S(2)}) collective-permute-start(bf16[512,128]{1,0:T(8,128)(2,1)S(1)} %bitcast.222), channel_id=1, source_target_pairs={{0,8},{1,9},{2,10},{3,11},{4,12},{5,13},{6,14},{7,15},{8,0},{9,1},... | collective-permute-start | bytes 393224 | tf_op jit(solution)/shard_map/ppermute | solution.py:40
  94.6 5.8 %slice-start.1 = ((s8[6291456]{0:T(1024)(128)(4,1)}), s8[2097152]{0:T(1024)(128)(4,1)S(1)}, s32[]{:S(2)}) async-start(s8[6291456]{0:T(1024)(128)(4,1)} %bitcast.223), calls=%async_computation.1 | async-start | bytes 4194304
  110.8 3.7 %copy-start.2 = (bf16[2304,2048]{1,0:T(8,128)(2,1)}, bf16[2304,2048]{1,0:T(8,128)(2,1)S(1)}, u32[]{:S(2)}) copy-start(bf16[2304,2048]{1,0:T(8,128)(2,1)S(1)} %convolution_convert_fusion.refs_0_.refs_1_.refs_2_.refs_3_.refs_5_.refs_6_.refs_7_) | copy-start | bytes 28311556
  114.4 4.9 %copy-start.6 = (s32[8,3]{0,1:T(4,128)S(1)}, s32[8,3]{0,1:T(4,128)}, u32[]{:S(2)}) copy-start(s32[8,3]{0,1:T(4,128)} %param.15) | copy-start | bytes 292
  114.4 5.0 %copy-start.7 = (s32[8,4]{0,1:T(4,128)S(1)}, s32[8,4]{0,1:T(4,128)}, u32[]{:S(2)}) copy-start(s32[8,4]{0,1:T(4,128)} %param.16) | copy-start | bytes 388
  114.4 5.1 %copy-start.8 = (s32[4]{0:T(128)S(1)}, s32[4]{0:T(128)}, u32[]{:S(2)}) copy-start(s32[4]{0:T(128)} %constant.58.clone) | copy-start | bytes 52
  115.9 11.4 %collective-permute-start.14 = (bf16[512,2048]{1,0:T(8,128)(2,1)}, bf16[512,2048]{1,0:T(8,128)(2,1)}, u32[]{:S(2)}, u32[]{:S(2)}) collective-permute-start(bf16[512,2048]{1,0:T(8,128)(2,1)} %slice.359), channel_id=1, source_target_pairs={{0,1},{1,0},{2,3},{3,2},{4,5},{5,4},{6,7},{7,6},{8,9},{9,8},{10,11... | collective-permute-start | bytes 6291464 | tf_op jit(solution)/shard_map/ppermute | solution.py:40
  127.3 17.5 %copy-start.1 = (bf16[128,1024]{1,0:T(8,128)(2,1)S(1)}, bf16[128,1024]{1,0:T(8,128)(2,1)}, u32[]{:S(2)}) copy-start(bf16[128,1024]{1,0:T(8,128)(2,1)} %param.18) | copy-start | bytes 786436

commit v16 on v15

--- a/solution.py
+++ b/solution.py
@@ -124,16 +124,19 @@
     for pair in range(HEADS // 2):
         cols = slice(pair * 2 * HD, (pair + 1) * 2 * HD)
         vcols = slice(D + pair * 2 * HD, D + (pair + 1) * 2 * HD)
-        ks = jnp.concatenate([r[:, cols] for r in kv_refs], axis=0)
-        vs = jnp.concatenate([r[:, vcols] for r in kv_refs], axis=0)
-        scores = jnp.dot(ks, q_ref[0, pair], preferred_element_type=jnp.float32)
-        top = jnp.max(scores, axis=0, keepdims=True)
-        expd = jnp.exp(scores - top)
-        total = jnp.sum(expd, axis=0, keepdims=True)
-        weights = (expd * (1.0 / total)).astype(jnp.bfloat16)
-        both = lax.dot_general(
-            weights, vs, (((0,), (0,)), ((), ())), preferred_element_type=jnp.float32
-        )
+        qbd = q_ref[0, pair]
+        scores = [jnp.dot(r[:, cols], qbd, preferred_element_type=jnp.float32) for r in kv_refs]
+        top = functools.reduce(jnp.maximum, scores).max(axis=0, keepdims=True)
+        expd = [jnp.exp(s - top) for s in scores]
+        total = functools.reduce(jnp.add, expd).sum(axis=0, keepdims=True)
+        scale = 1.0 / total
+        both = None
+        for r, e in zip(kv_refs, expd):
+            part = lax.dot_general(
+                (e * scale).astype(jnp.bfloat16), r[:, vcols], (((0,), (0,)), ((), ())),
+                preferred_element_type=jnp.float32,
+            )
+            both = part if both is None else both + part
         merged = jnp.where(low, both[:BS], both[BS:])
         att_ref[:, cols] = merged.astype(jnp.bfloat16)
     out_ref[...] = jnp.dot(att_ref[...], w_ref[...], preferred_element_type=jnp.float32).astype(

time: 146 us -> 149 us (1.021)
  the two profiles are of different devices: /device:TPU:13 before, /device:TPU:0 now
where the time goes in v16:
time: 149 us; the launch traced here: 147 us
  starting transfers between devices  58.8 us (39%)
  matrix products  29.9 us (20%)
  Pallas kernels  21.5 us (14%)
  waiting for transfers between devices  16.3 us (11%)
  local copies, waits for them, and re-layouts  12.3 us (8%)
  other arithmetic  6.7 us (4%)
    ppermute x9, starting transfers between devices, partner(): return lax.ppermute(value, axis, pairs)  39.7 us
    pallas_call x1, Pallas kernels, attend(): pl.pallas_call(attention_kernel, grid_spec=grid_spec, out_shape=jax.Shape...  21.5 us
    ppermute x6, starting transfers between devices, shift_rows(): return lax.ppermute(x, axis, pairs)  19.1 us
    ppermute x9, waiting for transfers between devices, partner(): return lax.ppermute(value, axis, pairs)  16.3 us
    dot_general x8, matrix products, step(): jnp.einsum('wsk,wkc->wsc', bands[lo - REACH:hi - REACH], stacked, precisi...  15.1 us
    dot_general x1, matrix products, on_device(): jnp.dot(all_blended, kv_weight, preferred_element_type=jnp.float32)  10.3 us
    unnamed x61, local copies, waits for them, and re-layouts  6.12 us
  transfers between devices with their start and end apart: 15, of which 4 were waited for; matrix products, arithmetic and copies ran while one was open for 19% of the time, Pallas kernels for 0%

profile of v16, /device:TPU:0, one launch (start us, length us, event | category | flops | bytes accessed | tf_op | source)
XLA Modules:
  0.0 146.6 jit_solution(3180823837492431980)
XLA Ops:
  0.0 0.8 copy.34
  1.0 1.8 %select_reduce_fusion = f32[8,5,64,64]{3,2,1,0:T(8,128)S(1)} fusion(f32[8,3,64,64]{3,2,1,0:T(8,128)} %param.13, pred[8,3,5]{2,1,0:T(4,128)(4,1)S(1)} %iota_compare_fusion), kind=kLoop, calls=%fused_computation.2 | loop fusion | flops 819200 | bytes 1048696 | tf_op jit(solution)/shard_map/reduce_sum | solution.py:61
  2.7 0.4 copy.35
  3.1 0.4 copy.36
  3.6 1.1 pad_maximum_fusion.1
  4.7 2.6 %collective-permute-start = (f32[8,64,448]{2,1,0:T(8,128)S(1)}, f32[8,64,448]{2,1,0:T(8,128)S(1)}, u32[]{:S(2)}, u32[]{:S(2)}) collective-permute-start(f32[8,64,448]{2,1,0:T(8,128)S(1)} %pad_maximum_fusion.1), channel_id=1, source_target_pairs={{0,1},{1,2},{2,3},{3,4},{4,5},{5,6},{6,7},{7,8},{8,9},{9,10},{10,1... | collective-permute-start | bytes 2752520 | tf_op jit(solution)/shard_map/ppermute | solution.py:27
  7.3 1.3 collective-permute-start.1
  8.7 5.8 %collective-permute-start.4 = (bf16[256,1024]{1,0:T(8,128)(2,1)S(1)}, bf16[256,1024]{1,0:T(8,128)(2,1)S(1)}, u32[]{:S(2)}, u32[]{:S(2)}) collective-permute-start(bf16[256,1024]{1,0:T(8,128)(2,1)S(1)} %get-tuple-element.24), channel_id=1, source_target_pairs={{0,4},{1,5},{2,6},{3,7},{4,0},{5,1},{6,2},{7,3},{8,12},{9,13},{10,... | collective-permute-start | bytes 1572872 | tf_op jit(solution)/shard_map/ppermute | solution.py:40
  14.5 2.6 %collective-permute-start.5 = (bf16[256,1024]{1,0:T(8,128)(2,1)S(1)}, bf16[256,1024]{1,0:T(8,128)(2,1)S(1)}, u32[]{:S(2)}, u32[]{:S(2)}) collective-permute-start(bf16[256,1024]{1,0:T(8,128)(2,1)S(1)} %get-tuple-element.24), channel_id=1, source_target_pairs={{0,8},{1,9},{2,10},{3,11},{4,12},{5,13},{6,14},{7,15},{8,0},{9,1},... | collective-permute-start | bytes 1572872 | tf_op jit(solution)/shard_map/ppermute | solution.py:40
  17.5 0.4 copy.38
  18.1 1.3 fusion.67
  19.7 0.2 copy.39
  19.9 1.2 fusion.19
  21.4 1.0 fusion.13
  22.7 1.2 fusion.16
  24.0 10.7 %collective-permute-start.2 = (f32[8,64,256]{2,1,0:T(8,128)S(1)}, f32[8,64,256]{2,1,0:T(8,128)S(1)}, u32[]{:S(2)}, u32[]{:S(2)}) collective-permute-start(f32[8,64,256]{2,1,0:T(8,128)S(1)} %pad_maximum_fusion.4), channel_id=1, source_target_pairs={{0,1},{1,2},{2,3},{3,4},{4,5},{5,6},{6,7},{7,8},{8,9},{9,10},{10,1... | collective-permute-start | bytes 1572872 | tf_op jit(solution)/shard_map/ppermute | solution.py:27
  34.7 1.5 %collective-permute-start.3 = (f32[8,64,256]{2,1,0:T(8,128)S(1)}, f32[8,64,256]{2,1,0:T(8,128)S(1)}, u32[]{:S(2)}, u32[]{:S(2)}) collective-permute-start(f32[8,64,256]{2,1,0:T(8,128)S(1)} %pad_maximum_fusion.4), channel_id=1, source_target_pairs={{1,0},{2,1},{3,2},{4,3},{5,4},{6,5},{7,6},{8,7},{9,8},{10,9},{11,1... | collective-permute-start | bytes 1572872 | tf_op jit(solution)/shard_map/ppermute | solution.py:27
  36.2 14.3 %collective-permute-start.6 = (bf16[256,1024]{1,0:T(8,128)(2,1)S(1)}, bf16[256,1024]{1,0:T(8,128)(2,1)S(1)}, u32[]{:S(2)}, u32[]{:S(2)}) collective-permute-start(bf16[256,1024]{1,0:T(8,128)(2,1)S(1)} %get-tuple-element.23), channel_id=1, source_target_pairs={{0,4},{1,5},{2,6},{3,7},{4,0},{5,1},{6,2},{7,3},{8,12},{9,13},{10,... | collective-permute-start | bytes 1572872 | tf_op jit(solution)/shard_map/ppermute | solution.py:40
  50.5 0.7 fusion.70
  51.2 6.2 %collective-permute-start.7 = (bf16[256,1024]{1,0:T(8,128)(2,1)S(1)}, bf16[256,1024]{1,0:T(8,128)(2,1)S(1)}, u32[]{:S(2)}, u32[]{:S(2)}) collective-permute-start(bf16[256,1024]{1,0:T(8,128)(2,1)S(1)} %get-tuple-element.23), channel_id=1, source_target_pairs={{0,8},{1,9},{2,10},{3,11},{4,12},{5,13},{6,14},{7,15},{8,0},{9,1},... | collective-permute-start | bytes 1572872 | tf_op jit(solution)/shard_map/ppermute | solution.py:40
  57.9 0.2 copy.43
  58.1 1.3 fusion.12
  59.7 0.2 copy.44
  59.9 1.2 fusion.20
  61.5 1.0 fusion.14
  62.7 6.8 %fusion.18 = bf16[8,64,128]{2,1,0:T(8,128)(2,1)S(1)} fusion(f32[8,64,320]{1,2,0:T(8,128)S(1)} %bitcast.204, f32[8,320,128]{2,1,0:T(8,128)S(1)} %bitcast.210, f32[20,64,128]{2,1,0:T(8,128)S(1)} %fusion.12, f32[20,64,128]{2,1,0:T(8,128)S(1)} %fusion.67, f32[16,64,128]{2,1,0:T(8,128)S(1)} %fusion.20, f32[8,64,128]{2,1,0:T(8,128)S(1)} %fusion.16, ...), kind=kOutput, calls=%fused_computation.29 | convolution fusion | flops 127139840 | bytes 4194340 | tf_op jit(solution)/shard_map/wsk,wkc->wsc/dot_general | solution.py:78
  69.5 7.5 %collective-permute-done.6 = bf16[256,1024]{1,0:T(8,128)(2,1)S(1)} collective-permute-done((bf16[256,1024]{1,0:T(8,128)(2,1)S(1)}, bf16[256,1024]{1,0:T(8,128)(2,1)S(1)}, u32[]{:S(2)}, u32[]{:S(2)}) %collective-permute-start.6) | collective-permute-done | bytes 524320 | tf_op jit(solution)/shard_map/ppermute | solution.py:40
  77.0 5.0 %collective-permute-done.8 = bf16[512,1024]{1,0:T(8,128)(2,1)S(1)} collective-permute-done((bf16[512,1024]{1,0:T(8,128)(2,1)S(1)}, bf16[512,1024]{1,0:T(8,128)(2,1)S(1)}, u32[]{:S(2)}, u32[]{:S(2)}) %collective-permute-start.8) | collective-permute-done | bytes 1048608 | tf_op jit(solution)/shard_map/ppermute | solution.py:40
  82.0 0.4 add_convert_fusion.3
  82.4 1.6 %collective-permute-start.9 = (bf16[128,1024]{1,0:T(8,128)(2,1)S(1)}, bf16[128,1024]{1,0:T(8,128)(2,1)S(1)}, u32[]{:S(2)}, u32[]{:S(2)}) collective-permute-start(bf16[128,1024]{1,0:T(8,128)(2,1)S(1)} %get-tuple-element.22), channel_id=1, source_target_pairs={{0,1},{1,2},{2,3},{3,4},{4,5},{5,6},{6,7},{7,8},{8,9},{9,10},{10,1... | collective-permute-start | bytes 786440 | tf_op jit(solution)/shard_map/ppermute | solution.py:27
  84.0 1.5 %collective-permute-start.10 = (bf16[128,1024]{1,0:T(8,128)(2,1)S(1)}, bf16[128,1024]{1,0:T(8,128)(2,1)S(1)}, u32[]{:S(2)}, u32[]{:S(2)}) collective-permute-start(bf16[128,1024]{1,0:T(8,128)(2,1)S(1)} %get-tuple-element.21), channel_id=1, source_target_pairs={{1,0},{2,1},{3,2},{4,3},{5,4},{6,5},{7,6},{8,7},{9,8},{10,9},{11,1... | collective-permute-start | bytes 786440 | tf_op jit(solution)/shard_map/ppermute | solution.py:27
  85.5 5.5 %collective-permute-start.11 = (bf16[512,128]{1,0:T(8,128)(2,1)S(1)}, bf16[512,128]{1,0:T(8,128)(2,1)S(1)}, u32[]{:S(2)}, u32[]{:S(2)}) collective-permute-start(bf16[512,128]{1,0:T(8,128)(2,1)S(1)} %bitcast.220), channel_id=1, source_target_pairs={{0,2},{1,3},{2,0},{3,1},{4,6},{5,7},{6,4},{7,5},{8,10},{9,11},{10,... | collective-permute-start | bytes 393224 | tf_op jit(solution)/shard_map/ppermute | solution.py:40
  91.0 0.9 collective-permute-start.12
  91.9 4.3 %collective-permute-start.13 = (bf16[512,128]{1,0:T(8,128)(2,1)S(1)}, bf16[512,128]{1,0:T(8,128)(2,1)S(1)}, u32[]{:S(2)}, u32[]{:S(2)}) collective-permute-start(bf16[512,128]{1,0:T(8,128)(2,1)S(1)} %bitcast.222), channel_id=1, source_target_pairs={{0,8},{1,9},{2,10},{3,11},{4,12},{5,13},{6,14},{7,15},{8,0},{9,1},... | collective-permute-start | bytes 393224 | tf_op jit(solution)/shard_map/ppermute | solution.py:40
  96.4 1.2 collective-permute-done.11
  97.6 0.4 fusion.21
  98.1 2.6 %collective-permute-done.12 = bf16[512,128]{1,0:T(8,128)(2,1)S(1)} collective-permute-done((bf16[512,128]{1,0:T(8,128)(2,1)S(1)}, bf16[512,128]{1,0:T(8,128)(2,1)S(1)}, u32[]{:S(2)}, u32[]{:S(2)}) %collective-permute-start.12) | collective-permute-done | bytes 131104 | tf_op jit(solution)/shard_map/ppermute | solution.py:40
  100.7 0.4 fusion.4
  101.1 0.4 fusion.5
  101.6 10.3 %convolution_convert_fusion.refs_0_.refs_1_.refs_2_.refs_3_.refs_5_.refs_6_.refs_7_ = bf16[2304,2048]{1,0:T(8,128)(2,1)S(1)} fusion(bf16[2304,1024]{1,0:T(8,128)(2,1)S(1)} %fusion.5, bf16[1024,3072]{1,0:T(8,128)(2,1)S(1)} %bitcast.224), kind=kOutput, calls=%fused_computation | convolution fusion | flops 9668395008 | bytes 18350080 | tf_op jit(solution)/shard_map/dot_general | solution.py:228
  111.9 3.7 %copy-done.2 = bf16[2304,2048]{1,0:T(8,128)(2,1)} copy-done((bf16[2304,2048]{1,0:T(8,128)(2,1)}, bf16[2304,2048]{1,0:T(8,128)(2,1)S(1)}, u32[]{:S(2)}) %copy-start.2) | copy-done | bytes 9437208
  115.5 1.5 slice.359
  117.2 0.7 pad_add_fusion.table_ref
  118.0 2.8 %fusion.9 = bf16[64,8,8,128]{3,1,2,0:T(8,128)(2,1)S(1)} fusion(bf16[512,1024]{1,0:T(8,128)(2,1)S(1)} %add_convert_fusion.3, bf16[1024,3072]{1,0:T(8,128)(2,1)} %param.19), kind=kOutput, calls=%fused_computation.15 | convolution fusion | flops 1074266112 | bytes 4194304 | tf_op jit(solution)/shard_map/dot_general | solution.py:220
  120.9 0.3 copy.51
  121.2 1.1 copy.48
  122.2 2.7 %fusion.1.q_ref = bf16[8,8,128,128]{3,2,1,0:T(8,128)(2,1)} fusion(bf16[8,8,128,64]{3,2,1,0:T(8,128)(2,1)S(1)} %bitcast.207, pred[128,128]{1,0:T(8,128)(4,1)S(1)} %select_compare_fusion), kind=kLoop, calls=%fused_computation.4 | loop fusion | flops 7340032 | bytes 3162112 | tf_op jit(solution)/shard_map/jit(_where)/select_n | solution.py:155
  125.0 21.5 %shard_map.109 = bf16[512,1024]{1,0:T(8,128)(2,1)} custom-call(s32[8,8]{1,0:T(8,128)} %pad_add_fusion.table_ref, bf16[8,8,128,128]{3,2,1,0:T(8,128)(2,1)} %fusion.1.q_ref, bf16[2304,2048]{1,0:T(8,128)(2,1)} %copy-done.2, bf16[2304,2048]{1,0:T(8,128)(2,1)} %copy-done.2, bf16[2304,2048]{1,0:T(8,128)(2,1)} %copy-done.2, bf16[2304,2048]{1,0:T(8,128)(2,1)} %copy-done.2, ...), custom_call_target="tpu_custom_call" | custom-call | tf_op jit(solution)/shard_map/pallas_call | solution.py:175
  (107 shorter events, 3.0 us)
Async XLA Ops:
  0.0 81.9 %copy-start = (bf16[128,1024]{1,0:T(8,128)(2,1)S(1)}, bf16[128,1024]{1,0:T(8,128)(2,1)}, u32[]{:S(2)}) copy-start(bf16[128,1024]{1,0:T(8,128)(2,1)} %param.18) | copy-start | bytes 786436
  3.1 5.4 %copy-start.3 = (bf16[512,1024]{1,0:T(8,128)(2,1)S(1)}, bf16[512,1024]{1,0:T(8,128)(2,1)}, u32[]{:S(2)}) copy-start(bf16[512,1024]{1,0:T(8,128)(2,1)} %param.11) | copy-start | bytes 3145732
  4.7 12.5 %copy-start.4 = (f32[512,128]{1,0:T(8,128)S(1)}, f32[512,128]{1,0:T(8,128)}, u32[]{:S(2)}) copy-start(f32[512,128]{1,0:T(8,128)} %param.12) | copy-start | bytes 786436
  4.7 12.4 %collective-permute-start = (f32[8,64,448]{2,1,0:T(8,128)S(1)}, f32[8,64,448]{2,1,0:T(8,128)S(1)}, u32[]{:S(2)}, u32[]{:S(2)}) collective-permute-start(f32[8,64,448]{2,1,0:T(8,128)S(1)} %pad_maximum_fusion.1), channel_id=1, source_target_pairs={{0,1},{1,2},{2,3},{3,4},{4,5},{5,6},{6,7},{7,8},{8,9},{9,10},{10,1... | collective-permute-start | bytes 2752520 | tf_op jit(solution)/shard_map/ppermute | solution.py:27
  7.3 9.9 %collective-permute-start.1 = (f32[8,64,448]{2,1,0:T(8,128)S(1)}, f32[8,64,448]{2,1,0:T(8,128)S(1)}, u32[]{:S(2)}, u32[]{:S(2)}) collective-permute-start(f32[8,64,448]{2,1,0:T(8,128)S(1)} %pad_maximum_fusion.1), channel_id=1, source_target_pairs={{1,0},{2,1},{3,2},{4,3},{5,4},{6,5},{7,6},{8,7},{9,8},{10,9},{11,1... | collective-permute-start | bytes 2752520 | tf_op jit(solution)/shard_map/ppermute | solution.py:27
  8.7 42.5 %collective-permute-start.4 = (bf16[256,1024]{1,0:T(8,128)(2,1)S(1)}, bf16[256,1024]{1,0:T(8,128)(2,1)S(1)}, u32[]{:S(2)}, u32[]{:S(2)}) collective-permute-start(bf16[256,1024]{1,0:T(8,128)(2,1)S(1)} %get-tuple-element.24), channel_id=1, source_target_pairs={{0,4},{1,5},{2,6},{3,7},{4,0},{5,1},{6,2},{7,3},{8,12},{9,13},{10,... | collective-permute-start | bytes 1572872 | tf_op jit(solution)/shard_map/ppermute | solution.py:40
  14.5 42.9 %collective-permute-start.5 = (bf16[256,1024]{1,0:T(8,128)(2,1)S(1)}, bf16[256,1024]{1,0:T(8,128)(2,1)S(1)}, u32[]{:S(2)}, u32[]{:S(2)}) collective-permute-start(bf16[256,1024]{1,0:T(8,128)(2,1)S(1)} %get-tuple-element.24), channel_id=1, source_target_pairs={{0,8},{1,9},{2,10},{3,11},{4,12},{5,13},{6,14},{7,15},{8,0},{9,1},... | collective-permute-start | bytes 1572872 | tf_op jit(solution)/shard_map/ppermute | solution.py:40
  22.7 27.8 %copy-start.5 = (f32[9]{0:T(128)S(1)}, f32[9]{0:T(128)}, u32[]{:S(2)}) copy-start(f32[9]{0:T(128)} %param.17) | copy-start | bytes 112
  24.0 33.5 %collective-permute-start.2 = (f32[8,64,256]{2,1,0:T(8,128)S(1)}, f32[8,64,256]{2,1,0:T(8,128)S(1)}, u32[]{:S(2)}, u32[]{:S(2)}) collective-permute-start(f32[8,64,256]{2,1,0:T(8,128)S(1)} %pad_maximum_fusion.4), channel_id=1, source_target_pairs={{0,1},{1,2},{2,3},{3,4},{4,5},{5,6},{6,7},{7,8},{8,9},{9,10},{10,1... | collective-permute-start | bytes 1572872 | tf_op jit(solution)/shard_map/ppermute | solution.py:27
  34.7 22.7 %collective-permute-start.3 = (f32[8,64,256]{2,1,0:T(8,128)S(1)}, f32[8,64,256]{2,1,0:T(8,128)S(1)}, u32[]{:S(2)}, u32[]{:S(2)}) collective-permute-start(f32[8,64,256]{2,1,0:T(8,128)S(1)} %pad_maximum_fusion.4), channel_id=1, source_target_pairs={{1,0},{2,1},{3,2},{4,3},{5,4},{6,5},{7,6},{8,7},{9,8},{10,9},{11,1... | collective-permute-start | bytes 1572872 | tf_op jit(solution)/shard_map/ppermute | solution.py:27
  36.2 40.8 %collective-permute-start.6 = (bf16[256,1024]{1,0:T(8,128)(2,1)S(1)}, bf16[256,1024]{1,0:T(8,128)(2,1)S(1)}, u32[]{:S(2)}, u32[]{:S(2)}) collective-permute-start(bf16[256,1024]{1,0:T(8,128)(2,1)S(1)} %get-tuple-element.23), channel_id=1, source_target_pairs={{0,4},{1,5},{2,6},{3,7},{4,0},{5,1},{6,2},{7,3},{8,12},{9,13},{10,... | collective-permute-start | bytes 1572872 | tf_op jit(solution)/shard_map/ppermute | solution.py:40
  51.2 25.8 %collective-permute-start.7 = (bf16[256,1024]{1,0:T(8,128)(2,1)S(1)}, bf16[256,1024]{1,0:T(8,128)(2,1)S(1)}, u32[]{:S(2)}, u32[]{:S(2)}) collective-permute-start(bf16[256,1024]{1,0:T(8,128)(2,1)S(1)} %get-tuple-element.23), channel_id=1, source_target_pairs={{0,8},{1,9},{2,10},{3,11},{4,12},{5,13},{6,14},{7,15},{8,0},{9,1},... | collective-permute-start | bytes 1572872 | tf_op jit(solution)/shard_map/ppermute | solution.py:40
  57.4 24.5 %collective-permute-start.8 = (bf16[512,1024]{1,0:T(8,128)(2,1)S(1)}, bf16[512,1024]{1,0:T(8,128)(2,1)S(1)}, u32[]{:S(2)}, u32[]{:S(2)}) collective-permute-start(bf16[512,1024]{1,0:T(8,128)(2,1)S(1)} %copy-done.3), channel_id=1, source_target_pairs={{0,2},{1,3},{2,0},{3,1},{4,6},{5,7},{6,4},{7,5},{8,10},{9,11},{10,... | collective-permute-start | bytes 3145736 | tf_op jit(solution)/shard_map/ppermute | solution.py:40
  82.0 19.6 %slice-start = ((s8[6291456]{0:T(1024)(128)(4,1)}), s8[4194304]{0:T(1024)(128)(4,1)S(1)}, s32[]{:S(2)}) async-start(s8[6291456]{0:T(1024)(128)(4,1)} %bitcast.223), calls=%async_computation | async-start | bytes 8388608
  82.4 13.8 %collective-permute-start.9 = (bf16[128,1024]{1,0:T(8,128)(2,1)S(1)}, bf16[128,1024]{1,0:T(8,128)(2,1)S(1)}, u32[]{:S(2)}, u32[]{:S(2)}) collective-permute-start(bf16[128,1024]{1,0:T(8,128)(2,1)S(1)} %get-tuple-element.22), channel_id=1, source_target_pairs={{0,1},{1,2},{2,3},{3,4},{4,5},{5,6},{6,7},{7,8},{8,9},{9,10},{10,1... | collective-permute-start | bytes 786440 | tf_op jit(solution)/shard_map/ppermute | solution.py:27
  84.0 12.3 %collective-permute-start.10 = (bf16[128,1024]{1,0:T(8,128)(2,1)S(1)}, bf16[128,1024]{1,0:T(8,128)(2,1)S(1)}, u32[]{:S(2)}, u32[]{:S(2)}) collective-permute-start(bf16[128,1024]{1,0:T(8,128)(2,1)S(1)} %get-tuple-element.21), channel_id=1, source_target_pairs={{1,0},{2,1},{3,2},{4,3},{5,4},{6,5},{7,6},{8,7},{9,8},{10,9},{11,1... | collective-permute-start | bytes 786440 | tf_op jit(solution)/shard_map/ppermute | solution.py:27
  85.5 12.1 %collective-permute-start.11 = (bf16[512,128]{1,0:T(8,128)(2,1)S(1)}, bf16[512,128]{1,0:T(8,128)(2,1)S(1)}, u32[]{:S(2)}, u32[]{:S(2)}) collective-permute-start(bf16[512,128]{1,0:T(8,128)(2,1)S(1)} %bitcast.220), channel_id=1, source_target_pairs={{0,2},{1,3},{2,0},{3,1},{4,6},{5,7},{6,4},{7,5},{8,10},{9,11},{10,... | collective-permute-start | bytes 393224 | tf_op jit(solution)/shard_map/ppermute | solution.py:40
  91.0 9.6 %collective-permute-start.12 = (bf16[512,128]{1,0:T(8,128)(2,1)S(1)}, bf16[512,128]{1,0:T(8,128)(2,1)S(1)}, u32[]{:S(2)}, u32[]{:S(2)}) collective-permute-start(bf16[512,128]{1,0:T(8,128)(2,1)S(1)} %bitcast.221), channel_id=1, source_target_pairs={{0,4},{1,5},{2,6},{3,7},{4,0},{5,1},{6,2},{7,3},{8,12},{9,13},{10,... | collective-permute-start | bytes 393224 | tf_op jit(solution)/shard_map/ppermute | solution.py:40
  91.9 9.2 %collective-permute-start.13 = (bf16[512,128]{1,0:T(8,128)(2,1)S(1)}, bf16[512,128]{1,0:T(8,128)(2,1)S(1)}, u32[]{:S(2)}, u32[]{:S(2)}) collective-permute-start(bf16[512,128]{1,0:T(8,128)(2,1)S(1)} %bitcast.222), channel_id=1, source_target_pairs={{0,8},{1,9},{2,10},{3,11},{4,12},{5,13},{6,14},{7,15},{8,0},{9,1},... | collective-permute-start | bytes 393224 | tf_op jit(solution)/shard_map/ppermute | solution.py:40
  96.4 5.2 %slice-start.1 = ((s8[6291456]{0:T(1024)(128)(4,1)}), s8[2097152]{0:T(1024)(128)(4,1)S(1)}, s32[]{:S(2)}) async-start(s8[6291456]{0:T(1024)(128)(4,1)} %bitcast.223), calls=%async_computation.1 | async-start | bytes 4194304
  111.9 3.7 %copy-start.2 = (bf16[2304,2048]{1,0:T(8,128)(2,1)}, bf16[2304,2048]{1,0:T(8,128)(2,1)S(1)}, u32[]{:S(2)}) copy-start(bf16[2304,2048]{1,0:T(8,128)(2,1)S(1)} %convolution_convert_fusion.refs_0_.refs_1_.refs_2_.refs_3_.refs_5_.refs_6_.refs_7_) | copy-start | bytes 28311556
  115.5 1.5 %copy-start.6 = (s32[8,3]{0,1:T(4,128)S(1)}, s32[8,3]{0,1:T(4,128)}, u32[]{:S(2)}) copy-start(s32[8,3]{0,1:T(4,128)} %param.15) | copy-start | bytes 292
  115.5 1.6 %copy-start.7 = (s32[8,4]{0,1:T(4,128)S(1)}, s32[8,4]{0,1:T(4,128)}, u32[]{:S(2)}) copy-start(s32[8,4]{0,1:T(4,128)} %param.16) | copy-start | bytes 388
  115.5 1.7 %copy-start.8 = (s32[4]{0:T(128)S(1)}, s32[4]{0:T(128)}, u32[]{:S(2)}) copy-start(s32[4]{0:T(128)} %constant.58.clone) | copy-start | bytes 52
  117.0 8.0 %collective-permute-start.14 = (bf16[512,2048]{1,0:T(8,128)(2,1)}, bf16[512,2048]{1,0:T(8,128)(2,1)}, u32[]{:S(2)}, u32[]{:S(2)}) collective-permute-start(bf16[512,2048]{1,0:T(8,128)(2,1)} %slice.359), channel_id=1, source_target_pairs={{0,1},{1,0},{2,3},{3,2},{4,5},{5,4},{6,7},{7,6},{8,9},{9,8},{10,11... | collective-permute-start | bytes 6291464 | tf_op jit(solution)/shard_map/ppermute | solution.py:40
  125.0 21.5 %copy-start.1 = (bf16[128,1024]{1,0:T(8,128)(2,1)S(1)}, bf16[128,1024]{1,0:T(8,128)(2,1)}, u32[]{:S(2)}) copy-start(bf16[128,1024]{1,0:T(8,128)(2,1)} %param.18) | copy-start | bytes 786436

commit v17 on v15

--- a/solution.py
+++ b/solution.py
@@ -219,23 +219,22 @@
     )
     all_blended = jnp.concatenate(
         [shift_rows(blended[rows - rim:], "seq", 1), blended, shift_rows(blended[:rim], "seq", -1)]
+        + [partner(blended, "seq", bits[0])]
         + [blend(f, e) for f, e in zip(feats_far, enc_far)],
         axis=0,
     )
     kv_all = jnp.dot(all_blended, kv_weight, preferred_element_type=jnp.float32).astype(
         jnp.bfloat16
     )
-    kv_own = kv_all[rim : rim + rows]
-    kv_chip = partner(kv_own, "seq", bits[0])
 
     near_blocks = count + 2 * REACH
     own_slot = jnp.arange(count, dtype=jnp.int32)[:, None] + REACH
     graph_slot = jnp.clip(graph_links - first_block + REACH, 0, near_blocks - 1)
     far_slot = jnp.clip(expander_slot, 0, count - 1)
-    far_base = jnp.asarray([0] + [near_blocks + k * count for k in range(NEXP - 1)], jnp.int32)
+    far_base = jnp.asarray([near_blocks + k * count for k in range(NEXP)], jnp.int32)
     table = jnp.concatenate([own_slot, graph_slot, far_slot + far_base[None, :]], axis=1)
     table = table.astype(jnp.int32)
-    sources = [kv_all] * 4 + [kv_chip] + [kv_all] * (NEXP - 1)
+    sources = [kv_all] * NKEY
     return attend(queries, sources, table, out_weight)
 
 

time: 146 us -> 159 us (1.089)
  the two profiles are of different devices: /device:TPU:13 before, /device:TPU:0 now
where the time goes in v17:
time: 159 us; the launch traced here: 158 us
  starting transfers between devices  44.2 us (28%)
  matrix products  38.2 us (24%)
  waiting for transfers between devices  28.8 us (18%)
  local copies, waits for them, and re-layouts  19.4 us (12%)
  Pallas kernels  17.4 us (11%)
  other arithmetic  8.74 us (5%)
    ppermute x9, waiting for transfers between devices, partner(): return lax.ppermute(value, axis, pairs)  28.8 us
    ppermute x9, starting transfers between devices, partner(): return lax.ppermute(value, axis, pairs)  25.2 us
    ppermute x6, starting transfers between devices, shift_rows(): return lax.ppermute(x, axis, pairs)  19 us
    pallas_call x1, Pallas kernels, attend(): pl.pallas_call(attention_kernel, grid_spec=grid_spec, out_shape=jax.Shape...  17.4 us
    dot_general x8, matrix products, step(): jnp.einsum('wsk,wkc->wsc', bands[lo - REACH:hi - REACH], stacked, precisi...  15.2 us
    dot_general x1, matrix products, on_device(): jnp.dot(all_blended, kv_weight, preferred_element_type=jnp.float32)  15.1 us
    unnamed x70, local copies, waits for them, and re-layouts  7.97 us
    dot_general x4, matrix products, blend(): encoded = jnp.dot(enc, encode_weight, preferred_element_type=jnp.float32)  5.05 us
  transfers between devices with their start and end apart: 15, of which 4 were waited for; matrix products, arithmetic and copies ran while one was open for 27% of the time, Pallas kernels for 0%

profile of v17, /device:TPU:0, one launch (start us, length us, event | category | flops | bytes accessed | tf_op | source)
XLA Modules:
  0.0 157.7 jit_solution(9621686048541164794)
XLA Ops:
  0.0 0.8 copy.34
  1.0 1.8 %select_reduce_fusion = f32[8,5,64,64]{3,2,1,0:T(8,128)S(1)} fusion(f32[8,3,64,64]{3,2,1,0:T(8,128)} %param.13, pred[8,3,5]{2,1,0:T(4,128)(4,1)S(1)} %iota_compare_fusion), kind=kLoop, calls=%fused_computation.2 | loop fusion | flops 819200 | bytes 1048696 | tf_op jit(solution)/shard_map/reduce_sum | solution.py:61
  3.6 2.1 %pad_maximum_fusion.1 = f32[8,64,448]{2,1,0:T(8,128)} fusion(f32[8,64,320]{2,1,0:T(8,128)S(1)} %copy.36, f32[8,64,128]{2,1,0:T(8,128)} %bitcast.214), kind=kLoop, calls=%fused_computation.33 | loop fusion | flops 229376 | bytes 1835008 | tf_op jit(solution)/shard_map/concatenate | solution.py:64
  5.7 3.3 %collective-permute-start = (f32[8,64,448]{2,1,0:T(8,128)}, f32[8,64,448]{2,1,0:T(8,128)}, u32[]{:S(2)}, u32[]{:S(2)}) collective-permute-start(f32[8,64,448]{2,1,0:T(8,128)} %pad_maximum_fusion.1), channel_id=1, source_target_pairs={{0,1},{1,2},{2,3},{3,4},{4,5},{5,6},{6,7},{7,8},{8,9},{9,10},{10,1... | collective-permute-start | bytes 2752520 | tf_op jit(solution)/shard_map/ppermute | solution.py:27
  9.0 1.3 collective-permute-start.1
  10.3 1.0 fusion.69
  11.4 4.9 %collective-permute-start.4 = (bf16[256,1024]{1,0:T(8,128)(2,1)}, bf16[256,1024]{1,0:T(8,128)(2,1)}, u32[]{:S(2)}, u32[]{:S(2)}) collective-permute-start(bf16[256,1024]{1,0:T(8,128)(2,1)} %get-tuple-element.24), channel_id=1, source_target_pairs={{0,4},{1,5},{2,6},{3,7},{4,0},{5,1},{6,2},{7,3},{8,12},{9,13},{10,... | collective-permute-start | bytes 1572872 | tf_op jit(solution)/shard_map/ppermute | solution.py:40
  16.2 2.6 %collective-permute-start.5 = (bf16[256,1024]{1,0:T(8,128)(2,1)}, bf16[256,1024]{1,0:T(8,128)(2,1)}, u32[]{:S(2)}, u32[]{:S(2)}) collective-permute-start(bf16[256,1024]{1,0:T(8,128)(2,1)} %get-tuple-element.24), channel_id=1, source_target_pairs={{0,8},{1,9},{2,10},{3,11},{4,12},{5,13},{6,14},{7,15},{8,0},{9,1},... | collective-permute-start | bytes 1572872 | tf_op jit(solution)/shard_map/ppermute | solution.py:40
  19.5 1.0 slice.303
  20.5 1.0 slice.304
  21.5 1.0 pad_maximum_fusion.2
  23.2 1.1 slice.301
  24.3 1.1 slice.302
  25.4 1.3 fusion.67
  27.2 1.2 fusion.19
  28.7 1.0 fusion.13
  30.0 1.2 fusion.16
  31.3 8.6 %collective-permute-start.2 = (f32[8,64,256]{2,1,0:T(8,128)S(1)}, f32[8,64,256]{2,1,0:T(8,128)S(1)}, u32[]{:S(2)}, u32[]{:S(2)}) collective-permute-start(f32[8,64,256]{2,1,0:T(8,128)S(1)} %pad_maximum_fusion.4), channel_id=1, source_target_pairs={{0,1},{1,2},{2,3},{3,4},{4,5},{5,6},{6,7},{7,8},{8,9},{9,10},{10,1... | collective-permute-start | bytes 1572872 | tf_op jit(solution)/shard_map/ppermute | solution.py:27
  39.8 1.5 collective-permute-start.3
  41.3 0.7 pad_add_fusion.table_ref
  42.0 0.7 fusion.70
  42.8 13.1 %collective-permute-done.4 = bf16[256,1024]{1,0:T(8,128)(2,1)} collective-permute-done((bf16[256,1024]{1,0:T(8,128)(2,1)}, bf16[256,1024]{1,0:T(8,128)(2,1)}, u32[]{:S(2)}, u32[]{:S(2)}) %collective-permute-start.4) | collective-permute-done | bytes 524320 | tf_op jit(solution)/shard_map/ppermute | solution.py:40
  55.9 3.5 %collective-permute-start.7 = (bf16[256,1024]{1,0:T(8,128)(2,1)}, bf16[256,1024]{1,0:T(8,128)(2,1)S(1)}, u32[]{:S(2)}, u32[]{:S(2)}) collective-permute-start(bf16[256,1024]{1,0:T(8,128)(2,1)} %get-tuple-element.23), channel_id=1, source_target_pairs={{0,8},{1,9},{2,10},{3,11},{4,12},{5,13},{6,14},{7,15},{8,0},{9,1},... | collective-permute-start | bytes 1572872 | tf_op jit(solution)/shard_map/ppermute | solution.py:40
  59.4 8.7 %collective-permute-start.8 = (bf16[512,1024]{1,0:T(8,128)(2,1)S(1)}, bf16[512,1024]{1,0:T(8,128)(2,1)S(1)}, u32[]{:S(2)}, u32[]{:S(2)}) collective-permute-start(bf16[512,1024]{1,0:T(8,128)(2,1)S(1)} %copy-done.2), channel_id=1, source_target_pairs={{0,2},{1,3},{2,0},{3,1},{4,6},{5,7},{6,4},{7,5},{8,10},{9,11},{10,... | collective-permute-start | bytes 3145736 | tf_op jit(solution)/shard_map/ppermute | solution.py:40
  68.8 1.3 fusion.12
  70.6 1.2 fusion.20
  72.1 1.0 fusion.14
  73.4 0.8 copy-done.4
  74.1 6.9 %fusion.18 = bf16[8,64,128]{2,1,0:T(8,128)(2,1)S(1)} fusion(f32[8,64,320]{1,2,0:T(8,128)S(1)} %bitcast.204, f32[8,320,128]{2,1,0:T(8,128)S(1)} %bitcast.210, f32[20,64,128]{2,1,0:T(8,128)S(1)} %fusion.12, f32[20,64,128]{2,1,0:T(8,128)S(1)} %fusion.67, f32[16,64,128]{2,1,0:T(8,128)S(1)} %fusion.20, f32[8,64,128]{2,1,0:T(8,128)S(1)} %fusion.16, ...), kind=kOutput, calls=%fused_computation.29 | convolution fusion | flops 127139840 | bytes 4194340 | tf_op jit(solution)/shard_map/wsk,wkc->wsc/dot_general | solution.py:78
  81.0 4.9 %collective-permute-done.7 = bf16[256,1024]{1,0:T(8,128)(2,1)S(1)} collective-permute-done((bf16[256,1024]{1,0:T(8,128)(2,1)}, bf16[256,1024]{1,0:T(8,128)(2,1)S(1)}, u32[]{:S(2)}, u32[]{:S(2)}) %collective-permute-start.7) | collective-permute-done | bytes 524320 | tf_op jit(solution)/shard_map/ppermute | solution.py:40
  86.0 10.5 %collective-permute-done.8 = bf16[512,1024]{1,0:T(8,128)(2,1)S(1)} collective-permute-done((bf16[512,1024]{1,0:T(8,128)(2,1)S(1)}, bf16[512,1024]{1,0:T(8,128)(2,1)S(1)}, u32[]{:S(2)}, u32[]{:S(2)}) %collective-permute-start.8) | collective-permute-done | bytes 1048608 | tf_op jit(solution)/shard_map/ppermute | solution.py:40
  97.0 0.8 fusion.68
  97.8 2.5 %collective-permute-start.12 = (bf16[512,128]{1,0:T(8,128)(2,1)S(1)}, bf16[512,128]{1,0:T(8,128)(2,1)}, u32[]{:S(2)}, u32[]{:S(2)}) collective-permute-start(bf16[512,128]{1,0:T(8,128)(2,1)S(1)} %bitcast.220), channel_id=1, source_target_pairs={{0,2},{1,3},{2,0},{3,1},{4,6},{5,7},{6,4},{7,5},{8,10},{9,11},{10,... | collective-permute-start | bytes 393224 | tf_op jit(solution)/shard_map/ppermute | solution.py:40
  100.3 2.8 %collective-permute-start.9 = (bf16[128,1024]{1,0:T(8,128)(2,1)}, bf16[128,1024]{1,0:T(8,128)(2,1)}, u32[]{:S(2)}, u32[]{:S(2)}) collective-permute-start(bf16[128,1024]{1,0:T(8,128)(2,1)} %get-tuple-element.22), channel_id=1, source_target_pairs={{0,1},{1,2},{2,3},{3,4},{4,5},{5,6},{6,7},{7,8},{8,9},{9,10},{10,1... | collective-permute-start | bytes 786440 | tf_op jit(solution)/shard_map/ppermute | solution.py:27
  103.1 1.5 collective-permute-start.10
  104.6 2.8 %fusion.9 = bf16[64,8,8,128]{3,1,2,0:T(8,128)(2,1)S(1)} fusion(bf16[512,1024]{1,0:T(8,128)(2,1)S(1)} %add_convert_fusion.3, bf16[1024,3072]{1,0:T(8,128)(2,1)} %param.19), kind=kOutput, calls=%fused_computation.15 | convolution fusion | flops 1074266112 | bytes 4194304 | tf_op jit(solution)/shard_map/dot_general | solution.py:217
  107.5 1.2 copy.51
  108.8 2.0 %copy.48 = bf16[8,64,8,128]{1,3,2,0:T(8,128)(2,1)S(1)} copy(bf16[8,64,8,128]{3,2,1,0:T(8,128)(2,1)} %bitcast.211) | data formatting | bytes 2097152 | tf_op jit(solution)/shard_map/reshape | solution.py:147
  110.8 2.8 %fusion.1.q_ref = bf16[8,8,128,128]{3,2,1,0:T(8,128)(2,1)} fusion(bf16[8,8,128,64]{3,2,1,0:T(8,128)(2,1)S(1)} %bitcast.207, pred[128,128]{1,0:T(8,128)(4,1)S(1)} %select_compare_fusion), kind=kLoop, calls=%fused_computation.4 | loop fusion | flops 7340032 | bytes 3162112 | tf_op jit(solution)/shard_map/jit(_where)/select_n | solution.py:152
  113.6 2.5 %collective-permute-start.14 = (bf16[512,128]{1,0:T(8,128)(2,1)S(1)}, bf16[512,128]{1,0:T(8,128)(2,1)S(1)}, u32[]{:S(2)}, u32[]{:S(2)}) collective-permute-start(bf16[512,128]{1,0:T(8,128)(2,1)S(1)} %bitcast.222), channel_id=1, source_target_pairs={{0,8},{1,9},{2,10},{3,11},{4,12},{5,13},{6,14},{7,15},{8,0},{9,1},... | collective-permute-start | bytes 393224 | tf_op jit(solution)/shard_map/ppermute | solution.py:40
  116.1 1.0 constant_dynamic-update-slice_fusion.3
  117.2 1.1 constant_dynamic-update-slice_fusion.1
  118.3 1.7 %constant_dynamic-update-slice_fusion = bf16[2816,1024]{1,0:T(8,128)(2,1)S(1)} fusion(bf16[2816,1024]{1,0:T(8,128)(2,1)S(1)} %constant_dynamic-update-slice_fusion.1, bf16[512,1024]{1,0:T(8,128)(2,1)} %collective-permute-done.11), kind=kLoop, calls=%fused_computation.124 | loop fusion | bytes 2097152
  120.0 1.5 fusion.21
  121.5 1.7 %fusion.4 = bf16[2816,1024]{1,0:T(8,128)(2,1)S(1)} fusion(bf16[2816,1024]{1,0:T(8,128)(2,1)S(1)} %fusion.21, bf16[512,128]{1,0:T(8,128)(2,1)} %collective-permute-done.13, bf16[128,1024]{1,0:T(8,128)(2,1)S(1)} %copy-done, bf16[256,1024]{1,0:T(8,128)(2,1)} %collective-permute-done.6, bf16[256,1024]{1,0:T(8,128)(2,1)} %collective-permute-done.4), kind=kOutput, calls=%fused_computation.12 | convolution fusion | flops 137363456 | bytes 2490368 | tf_op jit(solution)/shard_map/dot_general | solution.py:212
  123.5 1.5 fusion.5
  125.0 15.1 %convolution_convert_fusion.refs_0_.refs_1_.refs_2_.refs_3_.refs_4_.refs_5_.refs_6_.refs_7_ = bf16[2816,2048]{1,0:T(8,128)(2,1)} fusion(bf16[2816,1024]{1,0:T(8,128)(2,1)S(1)} %fusion.5, bf16[1024,3072]{1,0:T(8,128)(2,1)S(1)} %bitcast.224), kind=kOutput, calls=%fused_computation | convolution fusion | flops 11816927232 | bytes 21495808 | tf_op jit(solution)/shard_map/dot_general | solution.py:226
  140.1 17.4 %shard_map.109 = bf16[512,1024]{1,0:T(8,128)(2,1)} custom-call(s32[8,8]{1,0:T(8,128)} %pad_add_fusion.table_ref, bf16[8,8,128,128]{3,2,1,0:T(8,128)(2,1)} %fusion.1.q_ref, bf16[2816,2048]{1,0:T(8,128)(2,1)} %convolution_convert_fusion.refs_0_.refs_1_.refs_2_.refs_3_.refs_4_.refs_5_.refs_6_.refs_7_, ...), custom_call_target="tpu_custom_call" | custom-call | tf_op jit(solution)/shard_map/pallas_call | solution.py:172
  (115 shorter events, 5.8 us)
Async XLA Ops:
  0.0 96.5 %copy-start = (bf16[128,1024]{1,0:T(8,128)(2,1)S(1)}, bf16[128,1024]{1,0:T(8,128)(2,1)}, u32[]{:S(2)}) copy-start(bf16[128,1024]{1,0:T(8,128)(2,1)} %param.18) | copy-start | bytes 786436
  3.1 7.2 %copy-start.2 = (bf16[512,1024]{1,0:T(8,128)(2,1)S(1)}, bf16[512,1024]{1,0:T(8,128)(2,1)}, u32[]{:S(2)}) copy-start(bf16[512,1024]{1,0:T(8,128)(2,1)} %param.11) | copy-start | bytes 3145732
  3.6 15.7 %copy-start.8 = (s32[8,3]{0,1:T(4,128)S(1)}, s32[8,3]{0,1:T(4,128)}, u32[]{:S(2)}) copy-start(s32[8,3]{0,1:T(4,128)} %param.15) | copy-start | bytes 292
  3.6 15.8 %copy-start.9 = (s32[8,4]{0,1:T(4,128)S(1)}, s32[8,4]{0,1:T(4,128)}, u32[]{:S(2)}) copy-start(s32[8,4]{0,1:T(4,128)} %param.16) | copy-start | bytes 388
  3.6 15.8 %copy-start.10 = (s32[4]{0:T(128)S(1)}, s32[4]{0:T(128)}, u32[]{:S(2)}) copy-start(s32[4]{0:T(128)} %constant.58.clone) | copy-start | bytes 52
  5.7 13.8 %collective-permute-start = (f32[8,64,448]{2,1,0:T(8,128)}, f32[8,64,448]{2,1,0:T(8,128)}, u32[]{:S(2)}, u32[]{:S(2)}) collective-permute-start(f32[8,64,448]{2,1,0:T(8,128)} %pad_maximum_fusion.1), channel_id=1, source_target_pairs={{0,1},{1,2},{2,3},{3,4},{4,5},{5,6},{6,7},{7,8},{8,9},{9,10},{10,1... | collective-permute-start | bytes 2752520 | tf_op jit(solution)/shard_map/ppermute | solution.py:27
  9.0 11.4 %collective-permute-start.1 = (f32[8,64,448]{2,1,0:T(8,128)}, f32[8,64,448]{2,1,0:T(8,128)}, u32[]{:S(2)}, u32[]{:S(2)}) collective-permute-start(f32[8,64,448]{2,1,0:T(8,128)} %pad_maximum_fusion.1), channel_id=1, source_target_pairs={{1,0},{2,1},{3,2},{4,3},{5,4},{6,5},{7,6},{8,7},{9,8},{10,9},{11,1... | collective-permute-start | bytes 2752520 | tf_op jit(solution)/shard_map/ppermute | solution.py:27
  11.4 44.5 %collective-permute-start.4 = (bf16[256,1024]{1,0:T(8,128)(2,1)}, bf16[256,1024]{1,0:T(8,128)(2,1)}, u32[]{:S(2)}, u32[]{:S(2)}) collective-permute-start(bf16[256,1024]{1,0:T(8,128)(2,1)} %get-tuple-element.24), channel_id=1, source_target_pairs={{0,4},{1,5},{2,6},{3,7},{4,0},{5,1},{6,2},{7,3},{8,12},{9,13},{10,... | collective-permute-start | bytes 1572872 | tf_op jit(solution)/shard_map/ppermute | solution.py:40
  16.2 43.2 %collective-permute-start.5 = (bf16[256,1024]{1,0:T(8,128)(2,1)}, bf16[256,1024]{1,0:T(8,128)(2,1)}, u32[]{:S(2)}, u32[]{:S(2)}) collective-permute-start(bf16[256,1024]{1,0:T(8,128)(2,1)} %get-tuple-element.24), channel_id=1, source_target_pairs={{0,8},{1,9},{2,10},{3,11},{4,12},{5,13},{6,14},{7,15},{8,0},{9,1},... | collective-permute-start | bytes 1572872 | tf_op jit(solution)/shard_map/ppermute | solution.py:40
  18.8 62.2 %collective-permute-start.6 = (bf16[256,1024]{1,0:T(8,128)(2,1)}, bf16[256,1024]{1,0:T(8,128)(2,1)}, u32[]{:S(2)}, u32[]{:S(2)}) collective-permute-start(bf16[256,1024]{1,0:T(8,128)(2,1)} %get-tuple-element.23), channel_id=1, source_target_pairs={{0,4},{1,5},{2,6},{3,7},{4,0},{5,1},{6,2},{7,3},{8,12},{9,13},{10,... | collective-permute-start | bytes 1572872 | tf_op jit(solution)/shard_map/ppermute | solution.py:40
  30.0 12.0 %copy-start.7 = (f32[9]{0:T(128)S(1)}, f32[9]{0:T(128)}, u32[]{:S(2)}) copy-start(f32[9]{0:T(128)} %param.17) | copy-start | bytes 112
  31.3 36.8 %collective-permute-start.2 = (f32[8,64,256]{2,1,0:T(8,128)S(1)}, f32[8,64,256]{2,1,0:T(8,128)S(1)}, u32[]{:S(2)}, u32[]{:S(2)}) collective-permute-start(f32[8,64,256]{2,1,0:T(8,128)S(1)} %pad_maximum_fusion.4), channel_id=1, source_target_pairs={{0,1},{1,2},{2,3},{3,4},{4,5},{5,6},{6,7},{7,8},{8,9},{9,10},{10,1... | collective-permute-start | bytes 1572872 | tf_op jit(solution)/shard_map/ppermute | solution.py:27
  39.8 28.3 %collective-permute-start.3 = (f32[8,64,256]{2,1,0:T(8,128)S(1)}, f32[8,64,256]{2,1,0:T(8,128)S(1)}, u32[]{:S(2)}, u32[]{:S(2)}) collective-permute-start(f32[8,64,256]{2,1,0:T(8,128)S(1)} %pad_maximum_fusion.4), channel_id=1, source_target_pairs={{1,0},{2,1},{3,2},{4,3},{5,4},{6,5},{7,6},{8,7},{9,8},{10,9},{11,1... | collective-permute-start | bytes 1572872 | tf_op jit(solution)/shard_map/ppermute | solution.py:27
  55.9 30.1 %collective-permute-start.7 = (bf16[256,1024]{1,0:T(8,128)(2,1)}, bf16[256,1024]{1,0:T(8,128)(2,1)S(1)}, u32[]{:S(2)}, u32[]{:S(2)}) collective-permute-start(bf16[256,1024]{1,0:T(8,128)(2,1)} %get-tuple-element.23), channel_id=1, source_target_pairs={{0,8},{1,9},{2,10},{3,11},{4,12},{5,13},{6,14},{7,15},{8,0},{9,1},... | collective-permute-start | bytes 1572872 | tf_op jit(solution)/shard_map/ppermute | solution.py:40
  59.4 37.0 %collective-permute-start.8 = (bf16[512,1024]{1,0:T(8,128)(2,1)S(1)}, bf16[512,1024]{1,0:T(8,128)(2,1)S(1)}, u32[]{:S(2)}, u32[]{:S(2)}) collective-permute-start(bf16[512,1024]{1,0:T(8,128)(2,1)S(1)} %copy-done.2), channel_id=1, source_target_pairs={{0,2},{1,3},{2,0},{3,1},{4,6},{5,7},{6,4},{7,5},{8,10},{9,11},{10,... | collective-permute-start | bytes 3145736 | tf_op jit(solution)/shard_map/ppermute | solution.py:40
  73.2 1.0 copy-start.4
  74.1 22.3 %copy-start.3 = (bf16[512,1024]{1,0:T(8,128)(2,1)S(1)}, bf16[512,1024]{1,0:T(8,128)(2,1)}, u32[]{:S(2)}) copy-start(bf16[512,1024]{1,0:T(8,128)(2,1)} %param.11) | copy-start | bytes 3145732
  86.0 21.5 %copy-start.11 = (bf16[256,1024]{1,0:T(8,128)(2,1)}, bf16[256,1024]{1,0:T(8,128)(2,1)S(1)}, u32[]{:S(2)}) copy-start(bf16[256,1024]{1,0:T(8,128)(2,1)S(1)} %collective-permute-done.7) | copy-start | bytes 1572868
  96.4 11.1 %copy-start.5 = (bf16[512,1024]{1,0:T(8,128)(2,1)}, bf16[512,1024]{1,0:T(8,128)(2,1)S(1)}, u32[]{:S(2)}) copy-start(bf16[512,1024]{1,0:T(8,128)(2,1)S(1)} %collective-permute-done.8) | copy-start | bytes 3145732
  96.9 21.4 %collective-permute-start.11 = (bf16[512,1024]{1,0:T(8,128)(2,1)S(1)}, bf16[512,1024]{1,0:T(8,128)(2,1)}, u32[]{:S(2)}, u32[]{:S(2)}) collective-permute-start(bf16[512,1024]{1,0:T(8,128)(2,1)S(1)} %add_convert_fusion.3), channel_id=1, source_target_pairs={{0,1},{1,0},{2,3},{3,2},{4,5},{5,4},{6,7},{7,6},{8,9},{9,8},{10,11... | collective-permute-start | bytes 3145736 | tf_op jit(solution)/shard_map/ppermute | solution.py:40
  97.8 22.2 %collective-permute-start.12 = (bf16[512,128]{1,0:T(8,128)(2,1)S(1)}, bf16[512,128]{1,0:T(8,128)(2,1)}, u32[]{:S(2)}, u32[]{:S(2)}) collective-permute-start(bf16[512,128]{1,0:T(8,128)(2,1)S(1)} %bitcast.220), channel_id=1, source_target_pairs={{0,2},{1,3},{2,0},{3,1},{4,6},{5,7},{6,4},{7,5},{8,10},{9,11},{10,... | collective-permute-start | bytes 393224 | tf_op jit(solution)/shard_map/ppermute | solution.py:40
  100.3 21.2 %collective-permute-start.13 = (bf16[512,128]{1,0:T(8,128)(2,1)S(1)}, bf16[512,128]{1,0:T(8,128)(2,1)}, u32[]{:S(2)}, u32[]{:S(2)}) collective-permute-start(bf16[512,128]{1,0:T(8,128)(2,1)S(1)} %bitcast.221), channel_id=1, source_target_pairs={{0,4},{1,5},{2,6},{3,7},{4,0},{5,1},{6,2},{7,3},{8,12},{9,13},{10,... | collective-permute-start | bytes 393224 | tf_op jit(solution)/shard_map/ppermute | solution.py:40
  100.3 13.3 %collective-permute-start.9 = (bf16[128,1024]{1,0:T(8,128)(2,1)}, bf16[128,1024]{1,0:T(8,128)(2,1)}, u32[]{:S(2)}, u32[]{:S(2)}) collective-permute-start(bf16[128,1024]{1,0:T(8,128)(2,1)} %get-tuple-element.22), channel_id=1, source_target_pairs={{0,1},{1,2},{2,3},{3,4},{4,5},{5,6},{6,7},{7,8},{8,9},{9,10},{10,1... | collective-permute-start | bytes 786440 | tf_op jit(solution)/shard_map/ppermute | solution.py:27
  103.1 14.0 %collective-permute-start.10 = (bf16[128,1024]{1,0:T(8,128)(2,1)}, bf16[128,1024]{1,0:T(8,128)(2,1)}, u32[]{:S(2)}, u32[]{:S(2)}) collective-permute-start(bf16[128,1024]{1,0:T(8,128)(2,1)} %get-tuple-element.21), channel_id=1, source_target_pairs={{1,0},{2,1},{3,2},{4,3},{5,4},{6,5},{7,6},{8,7},{9,8},{10,9},{11,1... | collective-permute-start | bytes 786440 | tf_op jit(solution)/shard_map/ppermute | solution.py:27
  113.6 9.9 %collective-permute-start.14 = (bf16[512,128]{1,0:T(8,128)(2,1)S(1)}, bf16[512,128]{1,0:T(8,128)(2,1)S(1)}, u32[]{:S(2)}, u32[]{:S(2)}) collective-permute-start(bf16[512,128]{1,0:T(8,128)(2,1)S(1)} %bitcast.222), channel_id=1, source_target_pairs={{0,8},{1,9},{2,10},{3,11},{4,12},{5,13},{6,14},{7,15},{8,0},{9,1},... | collective-permute-start | bytes 393224 | tf_op jit(solution)/shard_map/ppermute | solution.py:40
  117.1 3.0 %copy-start.6 = (bf16[512,1024]{1,0:T(8,128)(2,1)S(1)}, bf16[512,1024]{1,0:T(8,128)(2,1)}, u32[]{:S(2)}) copy-start(bf16[512,1024]{1,0:T(8,128)(2,1)} %copy-done.5) | copy-start | bytes 3145732
  117.1 7.9 %slice-start = ((s8[6291456]{0:T(1024)(128)(4,1)}), s8[4194304]{0:T(1024)(128)(4,1)S(1)}, s32[]{:S(2)}) async-start(s8[6291456]{0:T(1024)(128)(4,1)} %bitcast.223), calls=%async_computation | async-start | bytes 8388608
  120.0 3.5 %copy-start.12 = (bf16[256,1024]{1,0:T(8,128)(2,1)S(1)}, bf16[256,1024]{1,0:T(8,128)(2,1)}, u32[]{:S(2)}) copy-start(bf16[256,1024]{1,0:T(8,128)(2,1)} %copy-done.11) | copy-start | bytes 1572868
  120.0 5.0 %slice-start.1 = ((s8[6291456]{0:T(1024)(128)(4,1)}), s8[2097152]{0:T(1024)(128)(4,1)S(1)}, s32[]{:S(2)}) async-start(s8[6291456]{0:T(1024)(128)(4,1)} %bitcast.223), calls=%async_computation.1 | async-start | bytes 4194304
  140.1 17.4 %copy-start.1 = (bf16[128,1024]{1,0:T(8,128)(2,1)S(1)}, bf16[128,1024]{1,0:T(8,128)(2,1)}, u32[]{:S(2)}) copy-start(bf16[128,1024]{1,0:T(8,128)(2,1)} %param.18) | copy-start | bytes 786436

commit v18 on v15

--- a/solution.py
+++ b/solution.py
@@ -121,12 +121,20 @@
     w_ref, out_ref, att_ref = refs[NKEY:]
     lane = lax.broadcasted_iota(jnp.int32, (1, 2 * HD), 1)
     low = lane < HD
+    first = (pl.program_id(0) % 2) == 0
+    d_head = lax.broadcasted_iota(jnp.int32, (2 * HD, 2 * BS), 0) // HD
+    j_head = lax.broadcasted_iota(jnp.int32, (2 * HD, 2 * BS), 1) // BS
+    same = d_head == j_head
     for pair in range(HEADS // 2):
         cols = slice(pair * 2 * HD, (pair + 1) * 2 * HD)
         vcols = slice(D + pair * 2 * HD, D + (pair + 1) * 2 * HD)
         ks = jnp.concatenate([r[:, cols] for r in kv_refs], axis=0)
         vs = jnp.concatenate([r[:, vcols] for r in kv_refs], axis=0)
-        scores = jnp.dot(ks, q_ref[0, pair], preferred_element_type=jnp.float32)
+        tile = q_ref[cols, :].astype(jnp.float32)
+        turned = pltpu.roll(tile, BS, 1)
+        spread = jnp.where(low == first, tile, turned)
+        qbd = jnp.where(same, spread, 0.0).astype(jnp.bfloat16)
+        scores = jnp.dot(ks, qbd, preferred_element_type=jnp.float32)
         top = jnp.max(scores, axis=0, keepdims=True)
         expd = jnp.exp(scores - top)
         total = jnp.sum(expd, axis=0, keepdims=True)
@@ -141,22 +149,11 @@
     )
 
 
-def split_queries(queries):
-    count = queries.shape[0] // BS
-    pairs = HEADS // 2
-    qt = queries.reshape(count, BS, pairs, 2 * HD).transpose(0, 2, 3, 1)
-    qt = jnp.concatenate([qt, qt], axis=3)
-    d_head = lax.broadcasted_iota(jnp.int32, (2 * HD, 2 * BS), 0) // HD
-    j_head = lax.broadcasted_iota(jnp.int32, (2 * HD, 2 * BS), 1) // BS
-    scale = jnp.asarray(1.0 / HD**0.5, jnp.bfloat16)
-    return jnp.where(d_head == j_head, qt * scale, jnp.zeros_like(qt))
-
-
 def attend(queries, kv_sources, table, out_weight):
     count = table.shape[0]
     pairs = HEADS // 2
-    in_specs = [pl.BlockSpec((1, pairs, 2 * HD, 2 * BS), lambda b, t: (b, 0, 0, 0))]
-    operands = [split_queries(queries)]
+    in_specs = [pl.BlockSpec((D, 2 * BS), lambda b, t: (0, b // 2))]
+    operands = [queries]
     for j, src in enumerate(kv_sources):
         in_specs.append(pl.BlockSpec((BS, 2 * D), lambda b, t, j=j: (t[b, j], 0)))
         operands.append(src)
@@ -214,9 +211,9 @@
 
     kv_weight = qkv_weight[:, D:]
     blended = blend(node_feats, encoding_b)
-    queries = jnp.dot(blended, qkv_weight[:, :D], preferred_element_type=jnp.float32).astype(
-        jnp.bfloat16
-    )
+    queries = lax.dot_general(
+        qkv_weight[:, :D], blended, (((0,), (1,)), ((), ())), preferred_element_type=jnp.float32
+    ).astype(jnp.bfloat16) * jnp.asarray(1.0 / HD**0.5, jnp.bfloat16)
     all_blended = jnp.concatenate(
         [shift_rows(blended[rows - rim:], "seq", 1), blended, shift_rows(blended[:rim], "seq", -1)]
         + [blend(f, e) for f, e in zip(feats_far, enc_far)],

time: 146 us -> 145 us (level)
  the two profiles are of different devices: /device:TPU:13 before, /device:TPU:0 now
where the time goes in v18:
time: 145 us; the launch traced here: 142 us
  starting transfers between devices  58.8 us (41%)
  matrix products  31 us (21%)
  Pallas kernels  18.8 us (13%)
  waiting for transfers between devices  16.3 us (11%)
  local copies, waits for them, and re-layouts  12.3 us (8%)
  other arithmetic  3.84 us (3%)
    ppermute x9, starting transfers between devices, partner(): return lax.ppermute(value, axis, pairs)  39.7 us
    ppermute x6, starting transfers between devices, shift_rows(): return lax.ppermute(x, axis, pairs)  19.1 us
    pallas_call x1, Pallas kernels, attend(): pl.pallas_call(attention_kernel, grid_spec=grid_spec, out_shape=jax.Shape...  18.8 us
    ppermute x9, waiting for transfers between devices, partner(): return lax.ppermute(value, axis, pairs)  16.3 us
    dot_general x8, matrix products, step(): jnp.einsum('wsk,wkc->wsc', bands[lo - REACH:hi - REACH], stacked, precisi...  15.1 us
    dot_general x1, matrix products, on_device(): jnp.dot(all_blended, kv_weight, preferred_element_type=jnp.float32)  10.3 us
    unnamed x62, local copies, waits for them, and re-layouts  7.15 us
    dot_general x1, matrix products, on_device(): lax.dot_general(qkv_weight[:, :D], blended, (((0,), (1,)), ((), ())), pre...  3.89 us
  transfers between devices with their start and end apart: 15, of which 4 were waited for; matrix products, arithmetic and copies ran while one was open for 17% of the time, Pallas kernels for 0%

profile of v18, /device:TPU:0, one launch (start us, length us, event | category | flops | bytes accessed | tf_op | source)
XLA Modules:
  0.0 142.0 jit_solution(18048254625997324658)
XLA Ops:
  0.0 0.8 copy.35
  1.0 1.8 %select_reduce_fusion = f32[8,5,64,64]{3,2,1,0:T(8,128)S(1)} fusion(f32[8,3,64,64]{3,2,1,0:T(8,128)} %param.13, pred[8,3,5]{2,1,0:T(4,128)(4,1)S(1)} %iota_compare_fusion), kind=kLoop, calls=%fused_computation.2 | loop fusion | flops 819200 | bytes 1048696 | tf_op jit(solution)/shard_map/reduce_sum | solution.py:61
  2.7 0.4 copy.36
  3.1 0.4 copy.37
  3.6 1.1 pad_maximum_fusion.1
  4.7 2.6 %collective-permute-start = (f32[8,64,448]{2,1,0:T(8,128)S(1)}, f32[8,64,448]{2,1,0:T(8,128)S(1)}, u32[]{:S(2)}, u32[]{:S(2)}) collective-permute-start(f32[8,64,448]{2,1,0:T(8,128)S(1)} %pad_maximum_fusion.1), channel_id=1, source_target_pairs={{0,1},{1,2},{2,3},{3,4},{4,5},{5,6},{6,7},{7,8},{8,9},{9,10},{10,1... | collective-permute-start | bytes 2752520 | tf_op jit(solution)/shard_map/ppermute | solution.py:27
  7.3 1.3 collective-permute-start.1
  8.7 5.8 %collective-permute-start.4 = (bf16[256,1024]{1,0:T(8,128)(2,1)S(1)}, bf16[256,1024]{1,0:T(8,128)(2,1)S(1)}, u32[]{:S(2)}, u32[]{:S(2)}) collective-permute-start(bf16[256,1024]{1,0:T(8,128)(2,1)S(1)} %get-tuple-element.24), channel_id=1, source_target_pairs={{0,4},{1,5},{2,6},{3,7},{4,0},{5,1},{6,2},{7,3},{8,12},{9,13},{10,... | collective-permute-start | bytes 1572872 | tf_op jit(solution)/shard_map/ppermute | solution.py:40
  14.5 2.6 %collective-permute-start.5 = (bf16[256,1024]{1,0:T(8,128)(2,1)S(1)}, bf16[256,1024]{1,0:T(8,128)(2,1)S(1)}, u32[]{:S(2)}, u32[]{:S(2)}) collective-permute-start(bf16[256,1024]{1,0:T(8,128)(2,1)S(1)} %get-tuple-element.24), channel_id=1, source_target_pairs={{0,8},{1,9},{2,10},{3,11},{4,12},{5,13},{6,14},{7,15},{8,0},{9,1},... | collective-permute-start | bytes 1572872 | tf_op jit(solution)/shard_map/ppermute | solution.py:40
  17.5 0.4 copy.39
  18.1 1.3 fusion.69
  19.7 0.2 copy.40
  19.9 1.2 fusion.21
  21.3 0.1 copy.41
  21.4 1.0 fusion.15
  22.5 0.1 copy.42
  22.7 1.2 fusion.18
  24.0 10.7 %collective-permute-start.2 = (f32[8,64,256]{2,1,0:T(8,128)S(1)}, f32[8,64,256]{2,1,0:T(8,128)S(1)}, u32[]{:S(2)}, u32[]{:S(2)}) collective-permute-start(f32[8,64,256]{2,1,0:T(8,128)S(1)} %pad_maximum_fusion.4), channel_id=1, source_target_pairs={{0,1},{1,2},{2,3},{3,4},{4,5},{5,6},{6,7},{7,8},{8,9},{9,10},{10,1... | collective-permute-start | bytes 1572872 | tf_op jit(solution)/shard_map/ppermute | solution.py:27
  34.7 1.5 %collective-permute-start.3 = (f32[8,64,256]{2,1,0:T(8,128)S(1)}, f32[8,64,256]{2,1,0:T(8,128)S(1)}, u32[]{:S(2)}, u32[]{:S(2)}) collective-permute-start(f32[8,64,256]{2,1,0:T(8,128)S(1)} %pad_maximum_fusion.4), channel_id=1, source_target_pairs={{1,0},{2,1},{3,2},{4,3},{5,4},{6,5},{7,6},{8,7},{9,8},{10,9},{11,1... | collective-permute-start | bytes 1572872 | tf_op jit(solution)/shard_map/ppermute | solution.py:27
  36.2 14.3 %collective-permute-start.6 = (bf16[256,1024]{1,0:T(8,128)(2,1)S(1)}, bf16[256,1024]{1,0:T(8,128)(2,1)S(1)}, u32[]{:S(2)}, u32[]{:S(2)}) collective-permute-start(bf16[256,1024]{1,0:T(8,128)(2,1)S(1)} %get-tuple-element.23), channel_id=1, source_target_pairs={{0,4},{1,5},{2,6},{3,7},{4,0},{5,1},{6,2},{7,3},{8,12},{9,13},{10,... | collective-permute-start | bytes 1572872 | tf_op jit(solution)/shard_map/ppermute | solution.py:40
  50.5 0.7 fusion.72
  51.2 6.2 %collective-permute-start.7 = (bf16[256,1024]{1,0:T(8,128)(2,1)S(1)}, bf16[256,1024]{1,0:T(8,128)(2,1)S(1)}, u32[]{:S(2)}, u32[]{:S(2)}) collective-permute-start(bf16[256,1024]{1,0:T(8,128)(2,1)S(1)} %get-tuple-element.23), channel_id=1, source_target_pairs={{0,8},{1,9},{2,10},{3,11},{4,12},{5,13},{6,14},{7,15},{8,0},{9,1},... | collective-permute-start | bytes 1572872 | tf_op jit(solution)/shard_map/ppermute | solution.py:40
  57.9 0.2 copy.44
  58.1 1.3 fusion.14
  59.7 0.2 copy.45
  59.9 1.2 fusion.22
  61.5 1.0 fusion.16
  62.7 6.8 %fusion.20 = bf16[8,64,128]{2,1,0:T(8,128)(2,1)S(1)} fusion(f32[8,64,320]{1,2,0:T(8,128)S(1)} %bitcast.201, f32[8,320,128]{2,1,0:T(8,128)S(1)} %bitcast.206, f32[20,64,128]{2,1,0:T(8,128)S(1)} %fusion.14, f32[20,64,128]{2,1,0:T(8,128)S(1)} %fusion.69, f32[16,64,128]{2,1,0:T(8,128)S(1)} %fusion.22, f32[8,64,128]{2,1,0:T(8,128)S(1)} %fusion.18, ...), kind=kOutput, calls=%fused_computation.28 | convolution fusion | flops 127139840 | bytes 4194340 | tf_op jit(solution)/shard_map/wsk,wkc->wsc/dot_general | solution.py:78
  69.5 7.5 %collective-permute-done.6 = bf16[256,1024]{1,0:T(8,128)(2,1)S(1)} collective-permute-done((bf16[256,1024]{1,0:T(8,128)(2,1)S(1)}, bf16[256,1024]{1,0:T(8,128)(2,1)S(1)}, u32[]{:S(2)}, u32[]{:S(2)}) %collective-permute-start.6) | collective-permute-done | bytes 524320 | tf_op jit(solution)/shard_map/ppermute | solution.py:40
  77.0 5.0 %collective-permute-done.8 = bf16[512,1024]{1,0:T(8,128)(2,1)S(1)} collective-permute-done((bf16[512,1024]{1,0:T(8,128)(2,1)S(1)}, bf16[512,1024]{1,0:T(8,128)(2,1)S(1)}, u32[]{:S(2)}, u32[]{:S(2)}) %collective-permute-start.8) | collective-permute-done | bytes 1048608 | tf_op jit(solution)/shard_map/ppermute | solution.py:40
  82.0 0.4 add_convert_fusion.3
  82.4 1.6 %collective-permute-start.9 = (bf16[128,1024]{1,0:T(8,128)(2,1)S(1)}, bf16[128,1024]{1,0:T(8,128)(2,1)S(1)}, u32[]{:S(2)}, u32[]{:S(2)}) collective-permute-start(bf16[128,1024]{1,0:T(8,128)(2,1)S(1)} %get-tuple-element.22), channel_id=1, source_target_pairs={{0,1},{1,2},{2,3},{3,4},{4,5},{5,6},{6,7},{7,8},{8,9},{9,10},{10,1... | collective-permute-start | bytes 786440 | tf_op jit(solution)/shard_map/ppermute | solution.py:27
  84.0 1.5 %collective-permute-start.10 = (bf16[128,1024]{1,0:T(8,128)(2,1)S(1)}, bf16[128,1024]{1,0:T(8,128)(2,1)S(1)}, u32[]{:S(2)}, u32[]{:S(2)}) collective-permute-start(bf16[128,1024]{1,0:T(8,128)(2,1)S(1)} %get-tuple-element.21), channel_id=1, source_target_pairs={{1,0},{2,1},{3,2},{4,3},{5,4},{6,5},{7,6},{8,7},{9,8},{10,9},{11,1... | collective-permute-start | bytes 786440 | tf_op jit(solution)/shard_map/ppermute | solution.py:27
  85.5 5.5 %collective-permute-start.11 = (bf16[512,128]{1,0:T(8,128)(2,1)S(1)}, bf16[512,128]{1,0:T(8,128)(2,1)S(1)}, u32[]{:S(2)}, u32[]{:S(2)}) collective-permute-start(bf16[512,128]{1,0:T(8,128)(2,1)S(1)} %bitcast.215), channel_id=1, source_target_pairs={{0,2},{1,3},{2,0},{3,1},{4,6},{5,7},{6,4},{7,5},{8,10},{9,11},{10,... | collective-permute-start | bytes 393224 | tf_op jit(solution)/shard_map/ppermute | solution.py:40
  91.0 0.9 collective-permute-start.12
  91.9 4.3 %collective-permute-start.13 = (bf16[512,128]{1,0:T(8,128)(2,1)S(1)}, bf16[512,128]{1,0:T(8,128)(2,1)S(1)}, u32[]{:S(2)}, u32[]{:S(2)}) collective-permute-start(bf16[512,128]{1,0:T(8,128)(2,1)S(1)} %bitcast.217), channel_id=1, source_target_pairs={{0,8},{1,9},{2,10},{3,11},{4,12},{5,13},{6,14},{7,15},{8,0},{9,1},... | collective-permute-start | bytes 393224 | tf_op jit(solution)/shard_map/ppermute | solution.py:40
  96.4 1.2 collective-permute-done.11
  97.6 0.4 fusion.23
  98.1 2.6 %collective-permute-done.12 = bf16[512,128]{1,0:T(8,128)(2,1)S(1)} collective-permute-done((bf16[512,128]{1,0:T(8,128)(2,1)S(1)}, bf16[512,128]{1,0:T(8,128)(2,1)S(1)}, u32[]{:S(2)}, u32[]{:S(2)}) %collective-permute-start.12) | collective-permute-done | bytes 131104 | tf_op jit(solution)/shard_map/ppermute | solution.py:40
  100.7 0.4 fusion.3
  101.1 0.4 fusion.4
  101.6 10.3 %convolution_convert_fusion.refs_0_.refs_1_.refs_2_.refs_3_.refs_5_.refs_6_.refs_7_ = bf16[2304,2048]{1,0:T(8,128)(2,1)S(1)} fusion(bf16[2304,1024]{1,0:T(8,128)(2,1)S(1)} %fusion.4, bf16[1024,3072]{1,0:T(8,128)(2,1)S(1)} %bitcast.219), kind=kOutput, calls=%fused_computation | convolution fusion | flops 9668395008 | bytes 18350080 | tf_op jit(solution)/shard_map/dot_general | solution.py:222
  111.9 3.7 %copy-done.2 = bf16[2304,2048]{1,0:T(8,128)(2,1)} copy-done((bf16[2304,2048]{1,0:T(8,128)(2,1)}, bf16[2304,2048]{1,0:T(8,128)(2,1)S(1)}, u32[]{:S(2)}) %copy-start.2) | copy-done | bytes 9437208
  115.5 1.4 %slice.359 = bf16[512,2048]{1,0:T(8,128)(2,1)} slice(bf16[2304,2048]{1,0:T(8,128)(2,1)S(1)} %convolution_convert_fusion.refs_0_.refs_1_.refs_2_.refs_3_.refs_5_.refs_6_.refs_7_), slice={[128:640], [0:2048]} | slice | bytes 4194304 | tf_op jit(solution)/shard_map/slice | solution.py:225
  117.2 0.7 pad_add_fusion.table_ref
  117.8 3.9 %fusion.11.q_ref = bf16[1024,512]{1,0:T(8,128)(2,1)} fusion(bf16[512,1024]{1,0:T(8,128)(2,1)S(1)} %add_convert_fusion.3, bf16[1024,3072]{1,0:T(8,128)(2,1)} %param.19), kind=kOutput, calls=%fused_computation.14 | convolution fusion | flops 1074790400 | bytes 4194304 | tf_op jit(solution)/shard_map/dot_general | solution.py:214
  121.7 1.3 copy-done.5
  123.0 18.8 %shard_map.109 = bf16[512,1024]{1,0:T(8,128)(2,1)} custom-call(s32[8,8]{1,0:T(8,128)} %pad_add_fusion.table_ref, bf16[1024,512]{1,0:T(8,128)(2,1)} %fusion.11.q_ref, bf16[2304,2048]{1,0:T(8,128)(2,1)} %copy-done.2, bf16[2304,2048]{1,0:T(8,128)(2,1)} %copy-done.2, bf16[2304,2048]{1,0:T(8,128)(2,1)} %copy-done.2, bf16[2304,2048]{1,0:T(8,128)(2,1)} %copy-done.2, ...), custom_call_target="tpu_custom_call" | custom-call | tf_op jit(solution)/shard_map/pallas_call | solution.py:169
  (103 shorter events, 2.6 us)
Async XLA Ops:
  0.0 81.9 %copy-start = (bf16[128,1024]{1,0:T(8,128)(2,1)S(1)}, bf16[128,1024]{1,0:T(8,128)(2,1)}, u32[]{:S(2)}) copy-start(bf16[128,1024]{1,0:T(8,128)(2,1)} %param.18) | copy-start | bytes 786436
  3.1 5.4 %copy-start.3 = (bf16[512,1024]{1,0:T(8,128)(2,1)S(1)}, bf16[512,1024]{1,0:T(8,128)(2,1)}, u32[]{:S(2)}) copy-start(bf16[512,1024]{1,0:T(8,128)(2,1)} %param.11) | copy-start | bytes 3145732
  4.7 12.5 %copy-start.4 = (f32[512,128]{1,0:T(8,128)S(1)}, f32[512,128]{1,0:T(8,128)}, u32[]{:S(2)}) copy-start(f32[512,128]{1,0:T(8,128)} %param.12) | copy-start | bytes 786436
  4.7 12.4 %collective-permute-start = (f32[8,64,448]{2,1,0:T(8,128)S(1)}, f32[8,64,448]{2,1,0:T(8,128)S(1)}, u32[]{:S(2)}, u32[]{:S(2)}) collective-permute-start(f32[8,64,448]{2,1,0:T(8,128)S(1)} %pad_maximum_fusion.1), channel_id=1, source_target_pairs={{0,1},{1,2},{2,3},{3,4},{4,5},{5,6},{6,7},{7,8},{8,9},{9,10},{10,1... | collective-permute-start | bytes 2752520 | tf_op jit(solution)/shard_map/ppermute | solution.py:27
  7.3 9.9 %collective-permute-start.1 = (f32[8,64,448]{2,1,0:T(8,128)S(1)}, f32[8,64,448]{2,1,0:T(8,128)S(1)}, u32[]{:S(2)}, u32[]{:S(2)}) collective-permute-start(f32[8,64,448]{2,1,0:T(8,128)S(1)} %pad_maximum_fusion.1), channel_id=1, source_target_pairs={{1,0},{2,1},{3,2},{4,3},{5,4},{6,5},{7,6},{8,7},{9,8},{10,9},{11,1... | collective-permute-start | bytes 2752520 | tf_op jit(solution)/shard_map/ppermute | solution.py:27
  8.7 42.5 %collective-permute-start.4 = (bf16[256,1024]{1,0:T(8,128)(2,1)S(1)}, bf16[256,1024]{1,0:T(8,128)(2,1)S(1)}, u32[]{:S(2)}, u32[]{:S(2)}) collective-permute-start(bf16[256,1024]{1,0:T(8,128)(2,1)S(1)} %get-tuple-element.24), channel_id=1, source_target_pairs={{0,4},{1,5},{2,6},{3,7},{4,0},{5,1},{6,2},{7,3},{8,12},{9,13},{10,... | collective-permute-start | bytes 1572872 | tf_op jit(solution)/shard_map/ppermute | solution.py:40
  14.5 42.9 %collective-permute-start.5 = (bf16[256,1024]{1,0:T(8,128)(2,1)S(1)}, bf16[256,1024]{1,0:T(8,128)(2,1)S(1)}, u32[]{:S(2)}, u32[]{:S(2)}) collective-permute-start(bf16[256,1024]{1,0:T(8,128)(2,1)S(1)} %get-tuple-element.24), channel_id=1, source_target_pairs={{0,8},{1,9},{2,10},{3,11},{4,12},{5,13},{6,14},{7,15},{8,0},{9,1},... | collective-permute-start | bytes 1572872 | tf_op jit(solution)/shard_map/ppermute | solution.py:40
  22.7 27.8 %copy-start.6 = (f32[9]{0:T(128)S(1)}, f32[9]{0:T(128)}, u32[]{:S(2)}) copy-start(f32[9]{0:T(128)} %param.17) | copy-start | bytes 112
  24.0 33.5 %collective-permute-start.2 = (f32[8,64,256]{2,1,0:T(8,128)S(1)}, f32[8,64,256]{2,1,0:T(8,128)S(1)}, u32[]{:S(2)}, u32[]{:S(2)}) collective-permute-start(f32[8,64,256]{2,1,0:T(8,128)S(1)} %pad_maximum_fusion.4), channel_id=1, source_target_pairs={{0,1},{1,2},{2,3},{3,4},{4,5},{5,6},{6,7},{7,8},{8,9},{9,10},{10,1... | collective-permute-start | bytes 1572872 | tf_op jit(solution)/shard_map/ppermute | solution.py:27
  34.7 22.7 %collective-permute-start.3 = (f32[8,64,256]{2,1,0:T(8,128)S(1)}, f32[8,64,256]{2,1,0:T(8,128)S(1)}, u32[]{:S(2)}, u32[]{:S(2)}) collective-permute-start(f32[8,64,256]{2,1,0:T(8,128)S(1)} %pad_maximum_fusion.4), channel_id=1, source_target_pairs={{1,0},{2,1},{3,2},{4,3},{5,4},{6,5},{7,6},{8,7},{9,8},{10,9},{11,1... | collective-permute-start | bytes 1572872 | tf_op jit(solution)/shard_map/ppermute | solution.py:27
  36.2 40.8 %collective-permute-start.6 = (bf16[256,1024]{1,0:T(8,128)(2,1)S(1)}, bf16[256,1024]{1,0:T(8,128)(2,1)S(1)}, u32[]{:S(2)}, u32[]{:S(2)}) collective-permute-start(bf16[256,1024]{1,0:T(8,128)(2,1)S(1)} %get-tuple-element.23), channel_id=1, source_target_pairs={{0,4},{1,5},{2,6},{3,7},{4,0},{5,1},{6,2},{7,3},{8,12},{9,13},{10,... | collective-permute-start | bytes 1572872 | tf_op jit(solution)/shard_map/ppermute | solution.py:40
  51.2 25.8 %collective-permute-start.7 = (bf16[256,1024]{1,0:T(8,128)(2,1)S(1)}, bf16[256,1024]{1,0:T(8,128)(2,1)S(1)}, u32[]{:S(2)}, u32[]{:S(2)}) collective-permute-start(bf16[256,1024]{1,0:T(8,128)(2,1)S(1)} %get-tuple-element.23), channel_id=1, source_target_pairs={{0,8},{1,9},{2,10},{3,11},{4,12},{5,13},{6,14},{7,15},{8,0},{9,1},... | collective-permute-start | bytes 1572872 | tf_op jit(solution)/shard_map/ppermute | solution.py:40
  57.4 24.5 %collective-permute-start.8 = (bf16[512,1024]{1,0:T(8,128)(2,1)S(1)}, bf16[512,1024]{1,0:T(8,128)(2,1)S(1)}, u32[]{:S(2)}, u32[]{:S(2)}) collective-permute-start(bf16[512,1024]{1,0:T(8,128)(2,1)S(1)} %copy-done.3), channel_id=1, source_target_pairs={{0,2},{1,3},{2,0},{3,1},{4,6},{5,7},{6,4},{7,5},{8,10},{9,11},{10,... | collective-permute-start | bytes 3145736 | tf_op jit(solution)/shard_map/ppermute | solution.py:40
  82.0 19.6 %slice-start = ((s8[6291456]{0:T(1024)(128)(4,1)}), s8[4194304]{0:T(1024)(128)(4,1)S(1)}, s32[]{:S(2)}) async-start(s8[6291456]{0:T(1024)(128)(4,1)} %bitcast.218), calls=%async_computation | async-start | bytes 8388608
  82.4 13.8 %collective-permute-start.9 = (bf16[128,1024]{1,0:T(8,128)(2,1)S(1)}, bf16[128,1024]{1,0:T(8,128)(2,1)S(1)}, u32[]{:S(2)}, u32[]{:S(2)}) collective-permute-start(bf16[128,1024]{1,0:T(8,128)(2,1)S(1)} %get-tuple-element.22), channel_id=1, source_target_pairs={{0,1},{1,2},{2,3},{3,4},{4,5},{5,6},{6,7},{7,8},{8,9},{9,10},{10,1... | collective-permute-start | bytes 786440 | tf_op jit(solution)/shard_map/ppermute | solution.py:27
  84.0 12.3 %collective-permute-start.10 = (bf16[128,1024]{1,0:T(8,128)(2,1)S(1)}, bf16[128,1024]{1,0:T(8,128)(2,1)S(1)}, u32[]{:S(2)}, u32[]{:S(2)}) collective-permute-start(bf16[128,1024]{1,0:T(8,128)(2,1)S(1)} %get-tuple-element.21), channel_id=1, source_target_pairs={{1,0},{2,1},{3,2},{4,3},{5,4},{6,5},{7,6},{8,7},{9,8},{10,9},{11,1... | collective-permute-start | bytes 786440 | tf_op jit(solution)/shard_map/ppermute | solution.py:27
  85.5 12.1 %collective-permute-start.11 = (bf16[512,128]{1,0:T(8,128)(2,1)S(1)}, bf16[512,128]{1,0:T(8,128)(2,1)S(1)}, u32[]{:S(2)}, u32[]{:S(2)}) collective-permute-start(bf16[512,128]{1,0:T(8,128)(2,1)S(1)} %bitcast.215), channel_id=1, source_target_pairs={{0,2},{1,3},{2,0},{3,1},{4,6},{5,7},{6,4},{7,5},{8,10},{9,11},{10,... | collective-permute-start | bytes 393224 | tf_op jit(solution)/shard_map/ppermute | solution.py:40
  91.0 9.6 %collective-permute-start.12 = (bf16[512,128]{1,0:T(8,128)(2,1)S(1)}, bf16[512,128]{1,0:T(8,128)(2,1)S(1)}, u32[]{:S(2)}, u32[]{:S(2)}) collective-permute-start(bf16[512,128]{1,0:T(8,128)(2,1)S(1)} %bitcast.216), channel_id=1, source_target_pairs={{0,4},{1,5},{2,6},{3,7},{4,0},{5,1},{6,2},{7,3},{8,12},{9,13},{10,... | collective-permute-start | bytes 393224 | tf_op jit(solution)/shard_map/ppermute | solution.py:40
  91.9 9.2 %collective-permute-start.13 = (bf16[512,128]{1,0:T(8,128)(2,1)S(1)}, bf16[512,128]{1,0:T(8,128)(2,1)S(1)}, u32[]{:S(2)}, u32[]{:S(2)}) collective-permute-start(bf16[512,128]{1,0:T(8,128)(2,1)S(1)} %bitcast.217), channel_id=1, source_target_pairs={{0,8},{1,9},{2,10},{3,11},{4,12},{5,13},{6,14},{7,15},{8,0},{9,1},... | collective-permute-start | bytes 393224 | tf_op jit(solution)/shard_map/ppermute | solution.py:40
  96.4 5.2 %slice-start.1 = ((s8[6291456]{0:T(1024)(128)(4,1)}), s8[2097152]{0:T(1024)(128)(4,1)S(1)}, s32[]{:S(2)}) async-start(s8[6291456]{0:T(1024)(128)(4,1)} %bitcast.218), calls=%async_computation.1 | async-start | bytes 4194304
  111.9 3.7 %copy-start.2 = (bf16[2304,2048]{1,0:T(8,128)(2,1)}, bf16[2304,2048]{1,0:T(8,128)(2,1)S(1)}, u32[]{:S(2)}) copy-start(bf16[2304,2048]{1,0:T(8,128)(2,1)S(1)} %convolution_convert_fusion.refs_0_.refs_1_.refs_2_.refs_3_.refs_5_.refs_6_.refs_7_) | copy-start | bytes 28311556
  115.5 1.4 %copy-start.7 = (s32[8,3]{0,1:T(4,128)S(1)}, s32[8,3]{0,1:T(4,128)}, u32[]{:S(2)}) copy-start(s32[8,3]{0,1:T(4,128)} %param.15) | copy-start | bytes 292
  115.5 1.5 %copy-start.8 = (s32[8,4]{0,1:T(4,128)S(1)}, s32[8,4]{0,1:T(4,128)}, u32[]{:S(2)}) copy-start(s32[8,4]{0,1:T(4,128)} %param.16) | copy-start | bytes 388
  115.5 1.6 %copy-start.9 = (s32[4]{0:T(128)S(1)}, s32[4]{0:T(128)}, u32[]{:S(2)}) copy-start(s32[4]{0:T(128)} %constant.6.clone) | copy-start | bytes 52
  117.0 4.8 %collective-permute-start.14 = (bf16[512,2048]{1,0:T(8,128)(2,1)}, bf16[512,2048]{1,0:T(8,128)(2,1)S(1)}, u32[]{:S(2)}, u32[]{:S(2)}) collective-permute-start(bf16[512,2048]{1,0:T(8,128)(2,1)} %slice.359), channel_id=1, source_target_pairs={{0,1},{1,0},{2,3},{3,2},{4,5},{5,4},{6,7},{7,6},{8,9},{9,8},{10,11... | collective-permute-start | bytes 6291464 | tf_op jit(solution)/shard_map/ppermute | solution.py:40
  121.7 1.3 copy-start.5
  123.0 18.8 %copy-start.1 = (bf16[128,1024]{1,0:T(8,128)(2,1)S(1)}, bf16[128,1024]{1,0:T(8,128)(2,1)}, u32[]{:S(2)}) copy-start(bf16[128,1024]{1,0:T(8,128)(2,1)} %param.18) | copy-start | bytes 786436

commit v19 on v18

--- a/solution.py
+++ b/solution.py
@@ -214,25 +214,29 @@
     queries = lax.dot_general(
         qkv_weight[:, :D], blended, (((0,), (1,)), ((), ())), preferred_element_type=jnp.float32
     ).astype(jnp.bfloat16) * jnp.asarray(1.0 / HD**0.5, jnp.bfloat16)
-    all_blended = jnp.concatenate(
-        [shift_rows(blended[rows - rim:], "seq", 1), blended, shift_rows(blended[:rim], "seq", -1)]
-        + [blend(f, e) for f, e in zip(feats_far, enc_far)],
+    near_blended = jnp.concatenate(
+        [shift_rows(blended[rows - rim:], "seq", 1), blended, shift_rows(blended[:rim], "seq", -1)],
         axis=0,
     )
-    kv_all = jnp.dot(all_blended, kv_weight, preferred_element_type=jnp.float32).astype(
+    far_blended = jnp.concatenate([blend(f, e) for f, e in zip(feats_far, enc_far)], axis=0)
+    kv_near = jnp.dot(near_blended, kv_weight, preferred_element_type=jnp.float32).astype(
         jnp.bfloat16
     )
-    kv_own = kv_all[rim : rim + rows]
+    kv_own = kv_near[rim : rim + rows]
     kv_chip = partner(kv_own, "seq", bits[0])
+    kv_far = jnp.dot(far_blended, kv_weight, preferred_element_type=jnp.float32).astype(
+        jnp.bfloat16
+    )
 
     near_blocks = count + 2 * REACH
     own_slot = jnp.arange(count, dtype=jnp.int32)[:, None] + REACH
     graph_slot = jnp.clip(graph_links - first_block + REACH, 0, near_blocks - 1)
     far_slot = jnp.clip(expander_slot, 0, count - 1)
-    far_base = jnp.asarray([0] + [near_blocks + k * count for k in range(NEXP - 1)], jnp.int32)
+    far_base = jnp.asarray([k * count for k in range(NEXP)], jnp.int32) - count
+    far_base = jnp.maximum(far_base, 0)
     table = jnp.concatenate([own_slot, graph_slot, far_slot + far_base[None, :]], axis=1)
     table = table.astype(jnp.int32)
-    sources = [kv_all] * 4 + [kv_chip] + [kv_all] * (NEXP - 1)
+    sources = [kv_near] * 4 + [kv_chip] + [kv_far] * (NEXP - 1)
     return attend(queries, sources, table, out_weight)
 
 

time: 145 us -> 146 us (level); the launches traced: 142 us -> 145 us
  starting transfers between devices: 58.8 us -> 43.9 us
  waiting for transfers between devices: 16.3 us -> 28 us
  matrix products: 31 us -> 33.9 us
  other arithmetic: 3.84 us -> 5.78 us
  local copies, waits for them, and re-layouts: 12.3 us -> 13.8 us
    ppermute x9, starting transfers between devices: 39.7 us -> 24.7 us  [partner(): return lax.ppermute(value, axis, pairs)]
    ppermute x9, waiting for transfers between devices: 16.3 us -> 28 us  [partner(): return lax.ppermute(value, axis, pairs)]
    unnamed x62 -> x53, local copies, waits for them, and re-layouts: 7.15 us -> 4.89 us
    dot_general x4, matrix products: 1.68 us -> 3.93 us  [blend(): encoded = jnp.dot(enc, encode_weight, preferred_element_type=jnp.float32)]
    dot_general x1 -> x2, matrix products: 10.3 us -> 12.4 us  [the longest x1 8.76 us: on_device(): jnp.dot(far_blended, kv_weight, preferred_element_type=jnp.float32)]
    dot_general x1, matrix products: 3.89 us -> 2.31 us  [on_device(): lax.dot_general(qkv_weight[:, :D], blended, (((0,), (1,)), ((), ())), pre...]
  transfers between devices with their start and end apart: 15 -> 15, of which waited for: 4 -> 3; matrix products, arithmetic and copies ran while one was open for 17% -> 31% of each run, Pallas kernels for 0% -> 0%
where the time goes in v19:
time: 146 us; the launch traced here: 145 us
  starting transfers between devices  43.9 us (30%)
  matrix products  33.9 us (23%)
  waiting for transfers between devices  28 us (19%)
  Pallas kernels  18.8 us (13%)
  local copies, waits for them, and re-layouts  13.8 us (9%)
  other arithmetic  5.78 us (4%)
    ppermute x9, waiting for transfers between devices, partner(): return lax.ppermute(value, axis, pairs)  28 us
    ppermute x9, starting transfers between devices, partner(): return lax.ppermute(value, axis, pairs)  24.7 us
    ppermute x6, starting transfers between devices, shift_rows(): return lax.ppermute(x, axis, pairs)  19.2 us
    pallas_call x1, Pallas kernels, attend(): pl.pallas_call(attention_kernel, grid_spec=grid_spec, out_shape=jax.Shape...  18.8 us
    dot_general x8, matrix products, step(): jnp.einsum('wsk,wkc->wsc', bands[lo - REACH:hi - REACH], stacked, precisi...  15.2 us
    dot_general x1, matrix products, on_device(): jnp.dot(far_blended, kv_weight, preferred_element_type=jnp.float32)  8.76 us
    unnamed x53, local copies, waits for them, and re-layouts  4.89 us
    dot_general x4, matrix products, blend(): encoded = jnp.dot(enc, encode_weight, preferred_element_type=jnp.float32)  3.93 us
  transfers between devices with their start and end apart: 15, of which 3 were waited for; matrix products, arithmetic and copies ran while one was open for 31% of the time, Pallas kernels for 0%

profile of v19, /device:TPU:0, one launch (start us, length us, event | category | flops | bytes accessed | tf_op | source)
XLA Modules:
  0.0 144.9 jit_solution(12612288395254026291)
XLA Ops:
  0.0 0.8 copy.35
  1.0 1.8 %select_reduce_fusion = f32[8,5,64,64]{3,2,1,0:T(8,128)S(1)} fusion(f32[8,3,64,64]{3,2,1,0:T(8,128)} %param.13, pred[8,3,5]{2,1,0:T(4,128)(4,1)S(1)} %iota_compare_fusion), kind=kLoop, calls=%fused_computation.1 | loop fusion | flops 819200 | bytes 1048696 | tf_op jit(solution)/shard_map/reduce_sum | solution.py:61
  2.7 0.4 copy.36
  3.1 0.4 copy.37
  3.6 2.1 %pad_maximum_fusion.1 = f32[8,64,448]{2,1,0:T(8,128)} fusion(f32[8,64,320]{2,1,0:T(8,128)S(1)} %copy.37, f32[8,64,128]{2,1,0:T(8,128)} %bitcast.208), kind=kLoop, calls=%fused_computation.42 | loop fusion | flops 229376 | bytes 1835008 | tf_op jit(solution)/shard_map/concatenate | solution.py:64
  5.7 3.3 %collective-permute-start = (f32[8,64,448]{2,1,0:T(8,128)}, f32[8,64,448]{2,1,0:T(8,128)}, u32[]{:S(2)}, u32[]{:S(2)}) collective-permute-start(f32[8,64,448]{2,1,0:T(8,128)} %pad_maximum_fusion.1), channel_id=1, source_target_pairs={{0,1},{1,2},{2,3},{3,4},{4,5},{5,6},{6,7},{7,8},{8,9},{9,10},{10,1... | collective-permute-start | bytes 2752520 | tf_op jit(solution)/shard_map/ppermute | solution.py:27
  9.0 1.3 collective-permute-start.1
  10.3 1.1 fusion.85
  11.4 4.9 %collective-permute-start.4 = (bf16[256,1024]{1,0:T(8,128)(2,1)}, bf16[256,1024]{1,0:T(8,128)(2,1)}, u32[]{:S(2)}, u32[]{:S(2)}) collective-permute-start(bf16[256,1024]{1,0:T(8,128)(2,1)} %get-tuple-element.24), channel_id=1, source_target_pairs={{0,4},{1,5},{2,6},{3,7},{4,0},{5,1},{6,2},{7,3},{8,12},{9,13},{10,... | collective-permute-start | bytes 1572872 | tf_op jit(solution)/shard_map/ppermute | solution.py:40
  16.3 2.6 %collective-permute-start.5 = (bf16[256,1024]{1,0:T(8,128)(2,1)}, bf16[256,1024]{1,0:T(8,128)(2,1)}, u32[]{:S(2)}, u32[]{:S(2)}) collective-permute-start(bf16[256,1024]{1,0:T(8,128)(2,1)} %get-tuple-element.24), channel_id=1, source_target_pairs={{0,8},{1,9},{2,10},{3,11},{4,12},{5,13},{6,14},{7,15},{8,0},{9,1},... | collective-permute-start | bytes 1572872 | tf_op jit(solution)/shard_map/ppermute | solution.py:40
  18.9 0.4 collective-permute-start.6
  19.5 1.0 slice.307
  20.5 1.0 slice.308
  21.4 1.0 pad_maximum_fusion.2
  22.7 0.4 copy.39
  23.1 1.1 slice.305
  24.3 1.1 slice.306
  25.4 1.3 fusion.83
  27.1 1.2 fusion.34
  28.7 1.0 fusion.28
  30.0 1.2 fusion.31
  31.3 8.6 %collective-permute-start.2 = (f32[8,64,256]{2,1,0:T(8,128)S(1)}, f32[8,64,256]{2,1,0:T(8,128)S(1)}, u32[]{:S(2)}, u32[]{:S(2)}) collective-permute-start(f32[8,64,256]{2,1,0:T(8,128)S(1)} %pad_maximum_fusion.4), channel_id=1, source_target_pairs={{0,1},{1,2},{2,3},{3,4},{4,5},{5,6},{6,7},{7,8},{8,9},{9,10},{10,1... | collective-permute-start | bytes 1572872 | tf_op jit(solution)/shard_map/ppermute | solution.py:27
  39.8 1.5 %collective-permute-start.3 = (f32[8,64,256]{2,1,0:T(8,128)S(1)}, f32[8,64,256]{2,1,0:T(8,128)S(1)}, u32[]{:S(2)}, u32[]{:S(2)}) collective-permute-start(f32[8,64,256]{2,1,0:T(8,128)S(1)} %pad_maximum_fusion.4), channel_id=1, source_target_pairs={{1,0},{2,1},{3,2},{4,3},{5,4},{6,5},{7,6},{8,7},{9,8},{10,9},{11,1... | collective-permute-start | bytes 1572872 | tf_op jit(solution)/shard_map/ppermute | solution.py:27
  41.3 0.7 pad_add_fusion.table_ref
  42.0 0.7 fusion.86
  42.7 13.2 %collective-permute-done.4 = bf16[256,1024]{1,0:T(8,128)(2,1)} collective-permute-done((bf16[256,1024]{1,0:T(8,128)(2,1)}, bf16[256,1024]{1,0:T(8,128)(2,1)}, u32[]{:S(2)}, u32[]{:S(2)}) %collective-permute-start.4) | collective-permute-done | bytes 524320 | tf_op jit(solution)/shard_map/ppermute | solution.py:40
  55.9 3.3 %collective-permute-start.7 = (bf16[256,1024]{1,0:T(8,128)(2,1)}, bf16[256,1024]{1,0:T(8,128)(2,1)S(1)}, u32[]{:S(2)}, u32[]{:S(2)}) collective-permute-start(bf16[256,1024]{1,0:T(8,128)(2,1)} %get-tuple-element.23), channel_id=1, source_target_pairs={{0,8},{1,9},{2,10},{3,11},{4,12},{5,13},{6,14},{7,15},{8,0},{9,1},... | collective-permute-start | bytes 1572872 | tf_op jit(solution)/shard_map/ppermute | solution.py:40
  59.2 8.8 %collective-permute-start.8 = (bf16[512,1024]{1,0:T(8,128)(2,1)S(1)}, bf16[512,1024]{1,0:T(8,128)(2,1)S(1)}, u32[]{:S(2)}, u32[]{:S(2)}) collective-permute-start(bf16[512,1024]{1,0:T(8,128)(2,1)S(1)} %copy-done.2), channel_id=1, source_target_pairs={{0,2},{1,3},{2,0},{3,1},{4,6},{5,7},{6,4},{7,5},{8,10},{9,11},{10,... | collective-permute-start | bytes 3145736 | tf_op jit(solution)/shard_map/ppermute | solution.py:40
  68.7 1.3 fusion.27
  70.5 1.2 fusion.35
  72.1 1.0 fusion.29
  73.3 1.3 copy-done.3
  74.6 6.9 %fusion.33 = bf16[8,64,128]{2,1,0:T(8,128)(2,1)S(1)} fusion(f32[8,64,320]{1,2,0:T(8,128)S(1)} %bitcast.200, f32[8,320,128]{2,1,0:T(8,128)S(1)} %bitcast.205, f32[20,64,128]{2,1,0:T(8,128)S(1)} %fusion.27, f32[20,64,128]{2,1,0:T(8,128)S(1)} %fusion.83, f32[16,64,128]{2,1,0:T(8,128)S(1)} %fusion.35, f32[8,64,128]{2,1,0:T(8,128)S(1)} %fusion.31, ...), kind=kOutput, calls=%fused_computation.39 | convolution fusion | flops 127139840 | bytes 4194340 | tf_op jit(solution)/shard_map/wsk,wkc->wsc/dot_general | solution.py:78
  81.5 4.5 %collective-permute-done.7 = bf16[256,1024]{1,0:T(8,128)(2,1)S(1)} collective-permute-done((bf16[256,1024]{1,0:T(8,128)(2,1)}, bf16[256,1024]{1,0:T(8,128)(2,1)S(1)}, u32[]{:S(2)}, u32[]{:S(2)}) %collective-permute-start.7) | collective-permute-done | bytes 524320 | tf_op jit(solution)/shard_map/ppermute | solution.py:40
  86.0 10.4 %collective-permute-done.8 = bf16[512,1024]{1,0:T(8,128)(2,1)S(1)} collective-permute-done((bf16[512,1024]{1,0:T(8,128)(2,1)S(1)}, bf16[512,1024]{1,0:T(8,128)(2,1)S(1)}, u32[]{:S(2)}, u32[]{:S(2)}) %collective-permute-start.8) | collective-permute-done | bytes 1048608 | tf_op jit(solution)/shard_map/ppermute | solution.py:40
  96.3 2.5 %collective-permute-start.12 = (bf16[512,128]{1,0:T(8,128)(2,1)S(1)}, bf16[512,128]{1,0:T(8,128)(2,1)S(1)}, u32[]{:S(2)}, u32[]{:S(2)}) collective-permute-start(bf16[512,128]{1,0:T(8,128)(2,1)S(1)} %bitcast.213), channel_id=1, source_target_pairs={{0,2},{1,3},{2,0},{3,1},{4,6},{5,7},{6,4},{7,5},{8,10},{9,11},{10,... | collective-permute-start | bytes 393224 | tf_op jit(solution)/shard_map/ppermute | solution.py:40
  99.0 0.4 add_convert_fusion.3
  99.5 1.3 collective-permute-start.10
  100.8 3.3 %collective-permute-start.9 = (bf16[128,1024]{1,0:T(8,128)(2,1)S(1)}, bf16[128,1024]{1,0:T(8,128)(2,1)S(1)}, u32[]{:S(2)}, u32[]{:S(2)}) collective-permute-start(bf16[128,1024]{1,0:T(8,128)(2,1)S(1)} %get-tuple-element.21), channel_id=1, source_target_pairs={{0,1},{1,2},{2,3},{3,4},{4,5},{5,6},{6,7},{7,8},{8,9},{9,10},{10,1... | collective-permute-start | bytes 786440 | tf_op jit(solution)/shard_map/ppermute | solution.py:27
  104.1 2.3 %fusion.24.q_ref = bf16[1024,512]{1,0:T(8,128)(2,1)} fusion(bf16[512,1024]{1,0:T(8,128)(2,1)S(1)} %add_convert_fusion.3, bf16[1024,3072]{1,0:T(8,128)(2,1)S(1)} %bitcast.218), kind=kOutput, calls=%fused_computation.25 | convolution fusion | flops 1074790400 | bytes 4194304 | tf_op jit(solution)/shard_map/dot_general | solution.py:214
  106.4 0.4 add_convert_fusion.2
  106.8 1.6 %add_convert_fusion.1 = bf16[512,1024]{1,0:T(8,128)(2,1)S(1)} fusion(bf16[512,128]{1,0:T(8,128)(2,1)S(1)} %collective-permute-done.13, bf16[128,1024]{1,0:T(8,128)(2,1)S(1)} %copy-done, bf16[256,1024]{1,0:T(8,128)(2,1)} %collective-permute-done.6, bf16[256,1024]{1,0:T(8,128)(2,1)} %collective-permute-done.4), kind=kOutput, calls=%fused_computation.12 | convolution fusion | flops 137363456 | bytes 2490368 | tf_op jit(solution)/shard_map/dot_general | solution.py:209
  108.5 3.7 %fusion.3.refs_0_.refs_1_.refs_2_.refs_3_ = bf16[768,2048]{1,0:T(8,128)(2,1)S(1)} fusion(bf16[1024,3072]{1,0:T(8,128)(2,1)S(1)} %bitcast.218, bf16[128,1024]{1,0:T(8,128)(2,1)S(1)} %collective-permute-done.10, bf16[512,1024]{1,0:T(8,128)(2,1)S(1)} %add_convert_fusion.3, bf16[128,1024]{1,0:T(8,128)(2,1)S(1)} %collective-permute-done.9), kind=kOutput, calls=%fused_computation.5 | convolution fusion | flops 3227516928 | bytes 8912896 | tf_op jit(solution)/shard_map/dot_general | solution.py:222
  112.4 1.5 %copy-done.1 = bf16[768,2048]{1,0:T(8,128)(2,1)} copy-done((bf16[768,2048]{1,0:T(8,128)(2,1)}, bf16[768,2048]{1,0:T(8,128)(2,1)S(1)}, u32[]{:S(2)}) %copy-start.1) | copy-done | bytes 3145752
  113.9 2.0 %collective-permute-start.11 = (bf16[512,2048]{1,0:T(8,128)(2,1)S(1)}, bf16[512,2048]{1,0:T(8,128)(2,1)}, u32[]{:S(2)}, u32[]{:S(2)}) collective-permute-start(bf16[512,2048]{1,0:T(8,128)(2,1)S(1)} %slice.359), channel_id=1, source_target_pairs={{0,1},{1,0},{2,3},{3,2},{4,5},{5,4},{6,7},{7,6},{8,9},{9,8},{10,11... | collective-permute-start | bytes 6291464 | tf_op jit(solution)/shard_map/ppermute | solution.py:40
  115.9 1.5 %add_convert_fusion = bf16[512,1024]{1,0:T(8,128)(2,1)S(1)} fusion(bf16[512,128]{1,0:T(8,128)(2,1)S(1)} %collective-permute-done.14, bf16[128,1024]{1,0:T(8,128)(2,1)S(1)} %copy-done, bf16[256,1024]{1,0:T(8,128)(2,1)S(1)} %collective-permute-done.7, bf16[256,1024]{1,0:T(8,128)(2,1)} %collective-permute-done.5), kind=kOutput, calls=%fused_computation.11 | convolution fusion | flops 137363456 | bytes 2490368 | tf_op jit(solution)/shard_map/dot_general | solution.py:209
  117.4 8.8 %convolution_convert_fusion.refs_5_.refs_6_.refs_7_ = bf16[1536,2048]{1,0:T(8,128)(2,1)} fusion(bf16[1024,3072]{1,0:T(8,128)(2,1)S(1)} %bitcast.218, bf16[512,1024]{1,0:T(8,128)(2,1)S(1)} %add_convert_fusion, bf16[512,1024]{1,0:T(8,128)(2,1)S(1)} %add_convert_fusion.1, bf16[512,1024]{1,0:T(8,128)(2,1)S(1)} %add_convert_fusion.2), kind=kOutput, calls=%fused_computation | convolution fusion | flops 6455033856 | bytes 13631488 | tf_op jit(solution)/shard_map/dot_general | solution.py:227
  126.1 18.8 %shard_map.109 = bf16[512,1024]{1,0:T(8,128)(2,1)} custom-call(s32[8,8]{1,0:T(8,128)} %pad_add_fusion.table_ref, bf16[1024,512]{1,0:T(8,128)(2,1)} %fusion.24.q_ref, bf16[768,2048]{1,0:T(8,128)(2,1)} %copy-done.1, bf16[768,2048]{1,0:T(8,128)(2,1)} %copy-done.1, bf16[768,2048]{1,0:T(8,128)(2,1)} %copy-done.1, bf16[768,2048]{1,0:T(8,128)(2,1)} %copy-done.1, ...), custom_call_target="tpu_custom_call" | custom-call | tf_op jit(solution)/shard_map/pallas_call | solution.py:169
  (96 shorter events, 3.5 us)
Async XLA Ops:
  0.0 99.0 %copy-start = (bf16[128,1024]{1,0:T(8,128)(2,1)S(1)}, bf16[128,1024]{1,0:T(8,128)(2,1)}, u32[]{:S(2)}) copy-start(bf16[128,1024]{1,0:T(8,128)(2,1)} %param.18) | copy-start | bytes 786436
  3.1 7.2 %copy-start.2 = (bf16[512,1024]{1,0:T(8,128)(2,1)S(1)}, bf16[512,1024]{1,0:T(8,128)(2,1)}, u32[]{:S(2)}) copy-start(bf16[512,1024]{1,0:T(8,128)(2,1)} %param.11) | copy-start | bytes 3145732
  3.6 15.7 %copy-start.5 = (s32[8,3]{0,1:T(4,128)S(1)}, s32[8,3]{0,1:T(4,128)}, u32[]{:S(2)}) copy-start(s32[8,3]{0,1:T(4,128)} %param.15) | copy-start | bytes 292
  3.6 15.8 %copy-start.6 = (s32[8,4]{0,1:T(4,128)S(1)}, s32[8,4]{0,1:T(4,128)}, u32[]{:S(2)}) copy-start(s32[8,4]{0,1:T(4,128)} %param.16) | copy-start | bytes 388
  5.7 13.8 %collective-permute-start = (f32[8,64,448]{2,1,0:T(8,128)}, f32[8,64,448]{2,1,0:T(8,128)}, u32[]{:S(2)}, u32[]{:S(2)}) collective-permute-start(f32[8,64,448]{2,1,0:T(8,128)} %pad_maximum_fusion.1), channel_id=1, source_target_pairs={{0,1},{1,2},{2,3},{3,4},{4,5},{5,6},{6,7},{7,8},{8,9},{9,10},{10,1... | collective-permute-start | bytes 2752520 | tf_op jit(solution)/shard_map/ppermute | solution.py:27
  9.0 11.4 %collective-permute-start.1 = (f32[8,64,448]{2,1,0:T(8,128)}, f32[8,64,448]{2,1,0:T(8,128)}, u32[]{:S(2)}, u32[]{:S(2)}) collective-permute-start(f32[8,64,448]{2,1,0:T(8,128)} %pad_maximum_fusion.1), channel_id=1, source_target_pairs={{1,0},{2,1},{3,2},{4,3},{5,4},{6,5},{7,6},{8,7},{9,8},{10,9},{11,1... | collective-permute-start | bytes 2752520 | tf_op jit(solution)/shard_map/ppermute | solution.py:27
  11.4 44.5 %collective-permute-start.4 = (bf16[256,1024]{1,0:T(8,128)(2,1)}, bf16[256,1024]{1,0:T(8,128)(2,1)}, u32[]{:S(2)}, u32[]{:S(2)}) collective-permute-start(bf16[256,1024]{1,0:T(8,128)(2,1)} %get-tuple-element.24), channel_id=1, source_target_pairs={{0,4},{1,5},{2,6},{3,7},{4,0},{5,1},{6,2},{7,3},{8,12},{9,13},{10,... | collective-permute-start | bytes 1572872 | tf_op jit(solution)/shard_map/ppermute | solution.py:40
  16.3 42.9 %collective-permute-start.5 = (bf16[256,1024]{1,0:T(8,128)(2,1)}, bf16[256,1024]{1,0:T(8,128)(2,1)}, u32[]{:S(2)}, u32[]{:S(2)}) collective-permute-start(bf16[256,1024]{1,0:T(8,128)(2,1)} %get-tuple-element.24), channel_id=1, source_target_pairs={{0,8},{1,9},{2,10},{3,11},{4,12},{5,13},{6,14},{7,15},{8,0},{9,1},... | collective-permute-start | bytes 1572872 | tf_op jit(solution)/shard_map/ppermute | solution.py:40
  18.9 62.7 %collective-permute-start.6 = (bf16[256,1024]{1,0:T(8,128)(2,1)}, bf16[256,1024]{1,0:T(8,128)(2,1)}, u32[]{:S(2)}, u32[]{:S(2)}) collective-permute-start(bf16[256,1024]{1,0:T(8,128)(2,1)} %get-tuple-element.23), channel_id=1, source_target_pairs={{0,4},{1,5},{2,6},{3,7},{4,0},{5,1},{6,2},{7,3},{8,12},{9,13},{10,... | collective-permute-start | bytes 1572872 | tf_op jit(solution)/shard_map/ppermute | solution.py:40
  30.0 12.0 %copy-start.4 = (f32[9]{0:T(128)S(1)}, f32[9]{0:T(128)}, u32[]{:S(2)}) copy-start(f32[9]{0:T(128)} %param.17) | copy-start | bytes 112
  31.3 36.8 %collective-permute-start.2 = (f32[8,64,256]{2,1,0:T(8,128)S(1)}, f32[8,64,256]{2,1,0:T(8,128)S(1)}, u32[]{:S(2)}, u32[]{:S(2)}) collective-permute-start(f32[8,64,256]{2,1,0:T(8,128)S(1)} %pad_maximum_fusion.4), channel_id=1, source_target_pairs={{0,1},{1,2},{2,3},{3,4},{4,5},{5,6},{6,7},{7,8},{8,9},{9,10},{10,1... | collective-permute-start | bytes 1572872 | tf_op jit(solution)/shard_map/ppermute | solution.py:27
  39.8 28.2 %collective-permute-start.3 = (f32[8,64,256]{2,1,0:T(8,128)S(1)}, f32[8,64,256]{2,1,0:T(8,128)S(1)}, u32[]{:S(2)}, u32[]{:S(2)}) collective-permute-start(f32[8,64,256]{2,1,0:T(8,128)S(1)} %pad_maximum_fusion.4), channel_id=1, source_target_pairs={{1,0},{2,1},{3,2},{4,3},{5,4},{6,5},{7,6},{8,7},{9,8},{10,9},{11,1... | collective-permute-start | bytes 1572872 | tf_op jit(solution)/shard_map/ppermute | solution.py:27
  55.9 30.1 %collective-permute-start.7 = (bf16[256,1024]{1,0:T(8,128)(2,1)}, bf16[256,1024]{1,0:T(8,128)(2,1)S(1)}, u32[]{:S(2)}, u32[]{:S(2)}) collective-permute-start(bf16[256,1024]{1,0:T(8,128)(2,1)} %get-tuple-element.23), channel_id=1, source_target_pairs={{0,8},{1,9},{2,10},{3,11},{4,12},{5,13},{6,14},{7,15},{8,0},{9,1},... | collective-permute-start | bytes 1572872 | tf_op jit(solution)/shard_map/ppermute | solution.py:40
  59.2 37.1 %collective-permute-start.8 = (bf16[512,1024]{1,0:T(8,128)(2,1)S(1)}, bf16[512,1024]{1,0:T(8,128)(2,1)S(1)}, u32[]{:S(2)}, u32[]{:S(2)}) collective-permute-start(bf16[512,1024]{1,0:T(8,128)(2,1)S(1)} %copy-done.2), channel_id=1, source_target_pairs={{0,2},{1,3},{2,0},{3,1},{4,6},{5,7},{6,4},{7,5},{8,10},{9,11},{10,... | collective-permute-start | bytes 3145736 | tf_op jit(solution)/shard_map/ppermute | solution.py:40
  71.9 32.1 %slice-start = ((s8[6291456]{0:T(1024)(128)(4,1)}), s8[4194304]{0:T(1024)(128)(4,1)S(1)}, s32[]{:S(2)}) async-start(s8[6291456]{0:T(1024)(128)(4,1)} %bitcast.217), calls=%async_computation | async-start | bytes 8388608
  72.1 32.0 %slice-start.1 = ((s8[6291456]{0:T(1024)(128)(4,1)}), s8[2097152]{0:T(1024)(128)(4,1)S(1)}, s32[]{:S(2)}) async-start(s8[6291456]{0:T(1024)(128)(4,1)} %bitcast.217), calls=%async_computation.1 | async-start | bytes 4194304
  73.1 1.5 %copy-start.3 = (f32[512,128]{1,0:T(8,128)S(1)}, f32[512,128]{1,0:T(8,128)}, u32[]{:S(2)}) copy-start(f32[512,128]{1,0:T(8,128)} %param.12) | copy-start | bytes 786436
  96.3 10.1 %collective-permute-start.12 = (bf16[512,128]{1,0:T(8,128)(2,1)S(1)}, bf16[512,128]{1,0:T(8,128)(2,1)S(1)}, u32[]{:S(2)}, u32[]{:S(2)}) collective-permute-start(bf16[512,128]{1,0:T(8,128)(2,1)S(1)} %bitcast.213), channel_id=1, source_target_pairs={{0,2},{1,3},{2,0},{3,1},{4,6},{5,7},{6,4},{7,5},{8,10},{9,11},{10,... | collective-permute-start | bytes 393224 | tf_op jit(solution)/shard_map/ppermute | solution.py:40
  98.8 8.0 %collective-permute-start.13 = (bf16[512,128]{1,0:T(8,128)(2,1)S(1)}, bf16[512,128]{1,0:T(8,128)(2,1)S(1)}, u32[]{:S(2)}, u32[]{:S(2)}) collective-permute-start(bf16[512,128]{1,0:T(8,128)(2,1)S(1)} %bitcast.214), channel_id=1, source_target_pairs={{0,4},{1,5},{2,6},{3,7},{4,0},{5,1},{6,2},{7,3},{8,12},{9,13},{10,... | collective-permute-start | bytes 393224 | tf_op jit(solution)/shard_map/ppermute | solution.py:40
  98.8 17.1 %collective-permute-start.14 = (bf16[512,128]{1,0:T(8,128)(2,1)S(1)}, bf16[512,128]{1,0:T(8,128)(2,1)S(1)}, u32[]{:S(2)}, u32[]{:S(2)}) collective-permute-start(bf16[512,128]{1,0:T(8,128)(2,1)S(1)} %bitcast.215), channel_id=1, source_target_pairs={{0,8},{1,9},{2,10},{3,11},{4,12},{5,13},{6,14},{7,15},{8,0},{9,1},... | collective-permute-start | bytes 393224 | tf_op jit(solution)/shard_map/ppermute | solution.py:40
  99.5 9.0 %collective-permute-start.10 = (bf16[128,1024]{1,0:T(8,128)(2,1)S(1)}, bf16[128,1024]{1,0:T(8,128)(2,1)S(1)}, u32[]{:S(2)}, u32[]{:S(2)}) collective-permute-start(bf16[128,1024]{1,0:T(8,128)(2,1)S(1)} %get-tuple-element.22), channel_id=1, source_target_pairs={{1,0},{2,1},{3,2},{4,3},{5,4},{6,5},{7,6},{8,7},{9,8},{10,9},{11,1... | collective-permute-start | bytes 786440 | tf_op jit(solution)/shard_map/ppermute | solution.py:27
  100.8 7.7 %collective-permute-start.9 = (bf16[128,1024]{1,0:T(8,128)(2,1)S(1)}, bf16[128,1024]{1,0:T(8,128)(2,1)S(1)}, u32[]{:S(2)}, u32[]{:S(2)}) collective-permute-start(bf16[128,1024]{1,0:T(8,128)(2,1)S(1)} %get-tuple-element.21), channel_id=1, source_target_pairs={{0,1},{1,2},{2,3},{3,4},{4,5},{5,6},{6,7},{7,8},{8,9},{9,10},{10,1... | collective-permute-start | bytes 786440 | tf_op jit(solution)/shard_map/ppermute | solution.py:27
  112.2 1.7 %copy-start.1 = (bf16[768,2048]{1,0:T(8,128)(2,1)}, bf16[768,2048]{1,0:T(8,128)(2,1)S(1)}, u32[]{:S(2)}) copy-start(bf16[768,2048]{1,0:T(8,128)(2,1)S(1)} %fusion.3.refs_0_.refs_1_.refs_2_.refs_3_) | copy-start | bytes 9437188
  113.9 12.2 %collective-permute-start.11 = (bf16[512,2048]{1,0:T(8,128)(2,1)S(1)}, bf16[512,2048]{1,0:T(8,128)(2,1)}, u32[]{:S(2)}, u32[]{:S(2)}) collective-permute-start(bf16[512,2048]{1,0:T(8,128)(2,1)S(1)} %slice.359), channel_id=1, source_target_pairs={{0,1},{1,0},{2,3},{3,2},{4,5},{5,4},{6,7},{7,6},{8,9},{9,8},{10,11... | collective-permute-start | bytes 6291464 | tf_op jit(solution)/shard_map/ppermute | solution.py:40

commit v20 on v18

--- a/solution.py
+++ b/solution.py
@@ -192,7 +192,7 @@
     levels = lax.axis_size("seq").bit_length() - 1
     bits = [link * (levels - 1) // (NEXP - 1) for link in range(NEXP)]
 
-    half = rows // 2
+    half = rows * 5 // 8
     early = [partner(node_feats[:half], "seq", bit) for bit in bits[2:]]
     encoding, (early,) = chebyshev(
         struct_feats, op_blocks, laplace_index, series_coef, first_block, (), early,

time: 145 us -> 147 us (1.014); the launches traced: 142 us -> 147 us
  starting transfers between devices: 58.8 us -> 61.1 us
  waiting for transfers between devices: 16.3 us -> 18.4 us
    ppermute x9, starting transfers between devices: 39.7 us -> 42.1 us  [partner(): return lax.ppermute(value, axis, pairs)]
    ppermute x9, waiting for transfers between devices: 16.3 us -> 18.4 us  [partner(): return lax.ppermute(value, axis, pairs)]
  transfers between devices with their start and end apart: 15 -> 15, of which waited for: 4 -> 6; matrix products, arithmetic and copies ran while one was open for 17% -> 17% of each run, Pallas kernels for 0% -> 0%
where the time goes in v20:
time: 147 us
  starting transfers between devices  61.1 us (42%)
  matrix products  31 us (21%)
  Pallas kernels  18.9 us (13%)
  waiting for transfers between devices  18.4 us (13%)
  local copies, waits for them, and re-layouts  12.3 us (8%)
  other arithmetic  3.9 us (3%)
    ppermute x9, starting transfers between devices, partner(): return lax.ppermute(value, axis, pairs)  42.1 us
    ppermute x6, starting transfers between devices, shift_rows(): return lax.ppermute(x, axis, pairs)  19 us
    pallas_call x1, Pallas kernels, attend(): pl.pallas_call(attention_kernel, grid_spec=grid_spec, out_shape=jax.Shape...  18.9 us
    ppermute x9, waiting for transfers between devices, partner(): return lax.ppermute(value, axis, pairs)  18.4 us
    dot_general x8, matrix products, step(): jnp.einsum('wsk,wkc->wsc', bands[lo - REACH:hi - REACH], stacked, precisi...  15.1 us
    dot_general x1, matrix products, on_device(): jnp.dot(all_blended, kv_weight, preferred_element_type=jnp.float32)  10.3 us
    unnamed x62, local copies, waits for them, and re-layouts  7.16 us
    dot_general x1, matrix products, on_device(): lax.dot_general(qkv_weight[:, :D], blended, (((0,), (1,)), ((), ())), pre...  3.9 us
  transfers between devices with their start and end apart: 15, of which 6 were waited for; matrix products, arithmetic and copies ran while one was open for 17% of the time, Pallas kernels for 0%

profile of v20, /device:TPU:0, one launch (start us, length us, event | category | flops | bytes accessed | tf_op | source)
XLA Modules:
  0.0 146.6 jit_solution(6691559004963690377)
XLA Ops:
  0.0 0.8 copy.35
  1.0 1.8 %select_reduce_fusion = f32[8,5,64,64]{3,2,1,0:T(8,128)S(1)} fusion(f32[8,3,64,64]{3,2,1,0:T(8,128)} %param.13, pred[8,3,5]{2,1,0:T(4,128)(4,1)S(1)} %iota_compare_fusion), kind=kLoop, calls=%fused_computation.2 | loop fusion | flops 819200 | bytes 1048696 | tf_op jit(solution)/shard_map/reduce_sum | solution.py:61
  2.7 0.4 copy.36
  3.1 0.4 copy.37
  3.6 1.1 pad_maximum_fusion.1
  4.8 2.4 %collective-permute-start = (f32[8,64,448]{2,1,0:T(8,128)S(1)}, f32[8,64,448]{2,1,0:T(8,128)S(1)}, u32[]{:S(2)}, u32[]{:S(2)}) collective-permute-start(f32[8,64,448]{2,1,0:T(8,128)S(1)} %pad_maximum_fusion.1), channel_id=1, source_target_pairs={{0,1},{1,2},{2,3},{3,4},{4,5},{5,6},{6,7},{7,8},{8,9},{9,10},{10,1... | collective-permute-start | bytes 2752520 | tf_op jit(solution)/shard_map/ppermute | solution.py:27
  7.2 1.3 collective-permute-start.1
  8.6 5.8 %collective-permute-start.4 = (bf16[320,1024]{1,0:T(8,128)(2,1)S(1)}, bf16[320,1024]{1,0:T(8,128)(2,1)S(1)}, u32[]{:S(2)}, u32[]{:S(2)}) collective-permute-start(bf16[320,1024]{1,0:T(8,128)(2,1)S(1)} %slice.267), channel_id=1, source_target_pairs={{0,4},{1,5},{2,6},{3,7},{4,0},{5,1},{6,2},{7,3},{8,12},{9,13},{10,... | collective-permute-start | bytes 1966088 | tf_op jit(solution)/shard_map/ppermute | solution.py:40
  14.4 2.6 %collective-permute-start.5 = (bf16[320,1024]{1,0:T(8,128)(2,1)S(1)}, bf16[320,1024]{1,0:T(8,128)(2,1)S(1)}, u32[]{:S(2)}, u32[]{:S(2)}) collective-permute-start(bf16[320,1024]{1,0:T(8,128)(2,1)S(1)} %slice.267), channel_id=1, source_target_pairs={{0,8},{1,9},{2,10},{3,11},{4,12},{5,13},{6,14},{7,15},{8,0},{9,1},... | collective-permute-start | bytes 1966088 | tf_op jit(solution)/shard_map/ppermute | solution.py:40
  17.4 0.4 copy.39
  18.0 1.3 fusion.69
  19.6 0.2 copy.40
  19.8 1.2 fusion.21
  21.3 1.0 fusion.15
  22.4 0.1 copy.42
  22.6 1.2 fusion.18
  23.9 10.8 %collective-permute-start.2 = (f32[8,64,256]{2,1,0:T(8,128)S(1)}, f32[8,64,256]{2,1,0:T(8,128)S(1)}, u32[]{:S(2)}, u32[]{:S(2)}) collective-permute-start(f32[8,64,256]{2,1,0:T(8,128)S(1)} %pad_maximum_fusion.4), channel_id=1, source_target_pairs={{0,1},{1,2},{2,3},{3,4},{4,5},{5,6},{6,7},{7,8},{8,9},{9,10},{10,1... | collective-permute-start | bytes 1572872 | tf_op jit(solution)/shard_map/ppermute | solution.py:27
  34.6 1.5 %collective-permute-start.3 = (f32[8,64,256]{2,1,0:T(8,128)S(1)}, f32[8,64,256]{2,1,0:T(8,128)S(1)}, u32[]{:S(2)}, u32[]{:S(2)}) collective-permute-start(f32[8,64,256]{2,1,0:T(8,128)S(1)} %pad_maximum_fusion.4), channel_id=1, source_target_pairs={{1,0},{2,1},{3,2},{4,3},{5,4},{6,5},{7,6},{8,7},{9,8},{10,9},{11,1... | collective-permute-start | bytes 1572872 | tf_op jit(solution)/shard_map/ppermute | solution.py:27
  36.1 17.2 %collective-permute-start.6 = (bf16[192,1024]{1,0:T(8,128)(2,1)S(1)}, bf16[192,1024]{1,0:T(8,128)(2,1)S(1)}, u32[]{:S(2)}, u32[]{:S(2)}) collective-permute-start(bf16[192,1024]{1,0:T(8,128)(2,1)S(1)} %slice.299), channel_id=1, source_target_pairs={{0,4},{1,5},{2,6},{3,7},{4,0},{5,1},{6,2},{7,3},{8,12},{9,13},{10,... | collective-permute-start | bytes 1179656 | tf_op jit(solution)/shard_map/ppermute | solution.py:40
  53.3 0.7 fusion.71
  54.0 1.6 %collective-permute-done.4 = bf16[320,1024]{1,0:T(8,128)(2,1)S(1)} collective-permute-done((bf16[320,1024]{1,0:T(8,128)(2,1)S(1)}, bf16[320,1024]{1,0:T(8,128)(2,1)S(1)}, u32[]{:S(2)}, u32[]{:S(2)}) %collective-permute-start.4) | collective-permute-done | bytes 655392 | tf_op jit(solution)/shard_map/ppermute | solution.py:40
  55.6 6.9 %collective-permute-start.7 = (bf16[192,1024]{1,0:T(8,128)(2,1)S(1)}, bf16[192,1024]{1,0:T(8,128)(2,1)S(1)}, u32[]{:S(2)}, u32[]{:S(2)}) collective-permute-start(bf16[192,1024]{1,0:T(8,128)(2,1)S(1)} %slice.299), channel_id=1, source_target_pairs={{0,8},{1,9},{2,10},{3,11},{4,12},{5,13},{6,14},{7,15},{8,0},{9,1},... | collective-permute-start | bytes 1179656 | tf_op jit(solution)/shard_map/ppermute | solution.py:40
  63.0 0.2 copy.44
  63.2 1.3 fusion.14
  64.8 0.2 copy.45
  65.0 1.2 fusion.22
  66.6 1.0 fusion.16
  67.8 6.8 %fusion.20 = bf16[8,64,128]{2,1,0:T(8,128)(2,1)S(1)} fusion(f32[8,64,320]{1,2,0:T(8,128)S(1)} %bitcast.201, f32[8,320,128]{2,1,0:T(8,128)S(1)} %bitcast.206, f32[20,64,128]{2,1,0:T(8,128)S(1)} %fusion.14, f32[20,64,128]{2,1,0:T(8,128)S(1)} %fusion.69, f32[16,64,128]{2,1,0:T(8,128)S(1)} %fusion.22, f32[8,64,128]{2,1,0:T(8,128)S(1)} %fusion.18, ...), kind=kOutput, calls=%fused_computation.28 | convolution fusion | flops 127139840 | bytes 4194340 | tf_op jit(solution)/shard_map/wsk,wkc->wsc/dot_general | solution.py:78
  74.6 1.6 %collective-permute-done.6 = bf16[192,1024]{1,0:T(8,128)(2,1)S(1)} collective-permute-done((bf16[192,1024]{1,0:T(8,128)(2,1)S(1)}, bf16[192,1024]{1,0:T(8,128)(2,1)S(1)}, u32[]{:S(2)}, u32[]{:S(2)}) %collective-permute-start.6) | collective-permute-done | bytes 393248 | tf_op jit(solution)/shard_map/ppermute | solution.py:40
  76.2 9.5 %collective-permute-done.8 = bf16[512,1024]{1,0:T(8,128)(2,1)S(1)} collective-permute-done((bf16[512,1024]{1,0:T(8,128)(2,1)S(1)}, bf16[512,1024]{1,0:T(8,128)(2,1)S(1)}, u32[]{:S(2)}, u32[]{:S(2)}) %collective-permute-start.8) | collective-permute-done | bytes 1048608 | tf_op jit(solution)/shard_map/ppermute | solution.py:40
  85.7 0.4 add_convert_fusion.3
  86.2 1.6 %collective-permute-start.9 = (bf16[128,1024]{1,0:T(8,128)(2,1)S(1)}, bf16[128,1024]{1,0:T(8,128)(2,1)S(1)}, u32[]{:S(2)}, u32[]{:S(2)}) collective-permute-start(bf16[128,1024]{1,0:T(8,128)(2,1)S(1)} %get-tuple-element.22), channel_id=1, source_target_pairs={{0,1},{1,2},{2,3},{3,4},{4,5},{5,6},{6,7},{7,8},{8,9},{9,10},{10,1... | collective-permute-start | bytes 786440 | tf_op jit(solution)/shard_map/ppermute | solution.py:27
  87.8 1.5 %collective-permute-start.10 = (bf16[128,1024]{1,0:T(8,128)(2,1)S(1)}, bf16[128,1024]{1,0:T(8,128)(2,1)S(1)}, u32[]{:S(2)}, u32[]{:S(2)}) collective-permute-start(bf16[128,1024]{1,0:T(8,128)(2,1)S(1)} %get-tuple-element.21), channel_id=1, source_target_pairs={{1,0},{2,1},{3,2},{4,3},{5,4},{6,5},{7,6},{8,7},{9,8},{10,9},{11,1... | collective-permute-start | bytes 786440 | tf_op jit(solution)/shard_map/ppermute | solution.py:27
  89.3 5.5 %collective-permute-start.11 = (bf16[512,128]{1,0:T(8,128)(2,1)S(1)}, bf16[512,128]{1,0:T(8,128)(2,1)S(1)}, u32[]{:S(2)}, u32[]{:S(2)}) collective-permute-start(bf16[512,128]{1,0:T(8,128)(2,1)S(1)} %bitcast.215), channel_id=1, source_target_pairs={{0,2},{1,3},{2,0},{3,1},{4,6},{5,7},{6,4},{7,5},{8,10},{9,11},{10,... | collective-permute-start | bytes 393224 | tf_op jit(solution)/shard_map/ppermute | solution.py:40
  94.8 4.1 %collective-permute-start.13 = (bf16[512,128]{1,0:T(8,128)(2,1)S(1)}, bf16[512,128]{1,0:T(8,128)(2,1)S(1)}, u32[]{:S(2)}, u32[]{:S(2)}) collective-permute-start(bf16[512,128]{1,0:T(8,128)(2,1)S(1)} %bitcast.217), channel_id=1, source_target_pairs={{0,8},{1,9},{2,10},{3,11},{4,12},{5,13},{6,14},{7,15},{8,0},{9,1},... | collective-permute-start | bytes 393224 | tf_op jit(solution)/shard_map/ppermute | solution.py:40
  99.0 2.4 %collective-permute-done.11 = bf16[512,128]{1,0:T(8,128)(2,1)S(1)} collective-permute-done((bf16[512,128]{1,0:T(8,128)(2,1)S(1)}, bf16[512,128]{1,0:T(8,128)(2,1)S(1)}, u32[]{:S(2)}, u32[]{:S(2)}) %collective-permute-start.11) | collective-permute-done | bytes 131104 | tf_op jit(solution)/shard_map/ppermute | solution.py:40
  101.4 0.4 fusion.23
  101.8 0.4 collective-permute-done.12
  102.3 0.4 fusion.3
  102.7 2.9 %collective-permute-done.13 = bf16[512,128]{1,0:T(8,128)(2,1)S(1)} collective-permute-done((bf16[512,128]{1,0:T(8,128)(2,1)S(1)}, bf16[512,128]{1,0:T(8,128)(2,1)S(1)}, u32[]{:S(2)}, u32[]{:S(2)}) %collective-permute-start.13) | collective-permute-done | bytes 131104 | tf_op jit(solution)/shard_map/ppermute | solution.py:40
  105.6 0.4 fusion.4
  106.1 10.3 %convolution_convert_fusion.refs_0_.refs_1_.refs_2_.refs_3_.refs_5_.refs_6_.refs_7_ = bf16[2304,2048]{1,0:T(8,128)(2,1)S(1)} fusion(bf16[2304,1024]{1,0:T(8,128)(2,1)S(1)} %fusion.4, bf16[1024,3072]{1,0:T(8,128)(2,1)S(1)} %bitcast.219), kind=kOutput, calls=%fused_computation | convolution fusion | flops 9668395008 | bytes 18350080 | tf_op jit(solution)/shard_map/dot_general | solution.py:222
  116.4 3.7 %copy-done.2 = bf16[2304,2048]{1,0:T(8,128)(2,1)} copy-done((bf16[2304,2048]{1,0:T(8,128)(2,1)}, bf16[2304,2048]{1,0:T(8,128)(2,1)S(1)}, u32[]{:S(2)}) %copy-start.2) | copy-done | bytes 9437208
  120.0 1.4 slice.359
  121.7 0.7 pad_add_fusion.table_ref
  122.3 3.9 %fusion.11.q_ref = bf16[1024,512]{1,0:T(8,128)(2,1)} fusion(bf16[512,1024]{1,0:T(8,128)(2,1)S(1)} %add_convert_fusion.3, bf16[1024,3072]{1,0:T(8,128)(2,1)} %param.19), kind=kOutput, calls=%fused_computation.14 | convolution fusion | flops 1074790400 | bytes 4194304 | tf_op jit(solution)/shard_map/dot_general | solution.py:214
  126.2 1.3 copy-done.5
  127.5 18.9 %shard_map.109 = bf16[512,1024]{1,0:T(8,128)(2,1)} custom-call(s32[8,8]{1,0:T(8,128)} %pad_add_fusion.table_ref, bf16[1024,512]{1,0:T(8,128)(2,1)} %fusion.11.q_ref, bf16[2304,2048]{1,0:T(8,128)(2,1)} %copy-done.2, bf16[2304,2048]{1,0:T(8,128)(2,1)} %copy-done.2, bf16[2304,2048]{1,0:T(8,128)(2,1)} %copy-done.2, bf16[2304,2048]{1,0:T(8,128)(2,1)} %copy-done.2, ...), custom_call_target="tpu_custom_call" | custom-call | tf_op jit(solution)/shard_map/pallas_call | solution.py:169
  (104 shorter events, 2.8 us)
Async XLA Ops:
  0.0 85.7 %copy-start = (bf16[128,1024]{1,0:T(8,128)(2,1)S(1)}, bf16[128,1024]{1,0:T(8,128)(2,1)}, u32[]{:S(2)}) copy-start(bf16[128,1024]{1,0:T(8,128)(2,1)} %param.18) | copy-start | bytes 786436
  3.1 5.4 %copy-start.3 = (bf16[512,1024]{1,0:T(8,128)(2,1)S(1)}, bf16[512,1024]{1,0:T(8,128)(2,1)}, u32[]{:S(2)}) copy-start(bf16[512,1024]{1,0:T(8,128)(2,1)} %param.11) | copy-start | bytes 3145732
  3.6 13.5 %copy-start.4 = (f32[512,128]{1,0:T(8,128)S(1)}, f32[512,128]{1,0:T(8,128)}, u32[]{:S(2)}) copy-start(f32[512,128]{1,0:T(8,128)} %param.12) | copy-start | bytes 786436
  4.8 12.2 %collective-permute-start = (f32[8,64,448]{2,1,0:T(8,128)S(1)}, f32[8,64,448]{2,1,0:T(8,128)S(1)}, u32[]{:S(2)}, u32[]{:S(2)}) collective-permute-start(f32[8,64,448]{2,1,0:T(8,128)S(1)} %pad_maximum_fusion.1), channel_id=1, source_target_pairs={{0,1},{1,2},{2,3},{3,4},{4,5},{5,6},{6,7},{7,8},{8,9},{9,10},{10,1... | collective-permute-start | bytes 2752520 | tf_op jit(solution)/shard_map/ppermute | solution.py:27
  7.2 9.8 %collective-permute-start.1 = (f32[8,64,448]{2,1,0:T(8,128)S(1)}, f32[8,64,448]{2,1,0:T(8,128)S(1)}, u32[]{:S(2)}, u32[]{:S(2)}) collective-permute-start(f32[8,64,448]{2,1,0:T(8,128)S(1)} %pad_maximum_fusion.1), channel_id=1, source_target_pairs={{1,0},{2,1},{3,2},{4,3},{5,4},{6,5},{7,6},{8,7},{9,8},{10,9},{11,1... | collective-permute-start | bytes 2752520 | tf_op jit(solution)/shard_map/ppermute | solution.py:27
  8.6 47.1 %collective-permute-start.4 = (bf16[320,1024]{1,0:T(8,128)(2,1)S(1)}, bf16[320,1024]{1,0:T(8,128)(2,1)S(1)}, u32[]{:S(2)}, u32[]{:S(2)}) collective-permute-start(bf16[320,1024]{1,0:T(8,128)(2,1)S(1)} %slice.267), channel_id=1, source_target_pairs={{0,4},{1,5},{2,6},{3,7},{4,0},{5,1},{6,2},{7,3},{8,12},{9,13},{10,... | collective-permute-start | bytes 1966088 | tf_op jit(solution)/shard_map/ppermute | solution.py:40
  14.4 48.1 %collective-permute-start.5 = (bf16[320,1024]{1,0:T(8,128)(2,1)S(1)}, bf16[320,1024]{1,0:T(8,128)(2,1)S(1)}, u32[]{:S(2)}, u32[]{:S(2)}) collective-permute-start(bf16[320,1024]{1,0:T(8,128)(2,1)S(1)} %slice.267), channel_id=1, source_target_pairs={{0,8},{1,9},{2,10},{3,11},{4,12},{5,13},{6,14},{7,15},{8,0},{9,1},... | collective-permute-start | bytes 1966088 | tf_op jit(solution)/shard_map/ppermute | solution.py:40
  22.6 30.7 %copy-start.6 = (f32[9]{0:T(128)S(1)}, f32[9]{0:T(128)}, u32[]{:S(2)}) copy-start(f32[9]{0:T(128)} %param.17) | copy-start | bytes 112
  23.9 38.7 %collective-permute-start.2 = (f32[8,64,256]{2,1,0:T(8,128)S(1)}, f32[8,64,256]{2,1,0:T(8,128)S(1)}, u32[]{:S(2)}, u32[]{:S(2)}) collective-permute-start(f32[8,64,256]{2,1,0:T(8,128)S(1)} %pad_maximum_fusion.4), channel_id=1, source_target_pairs={{0,1},{1,2},{2,3},{3,4},{4,5},{5,6},{6,7},{7,8},{8,9},{9,10},{10,1... | collective-permute-start | bytes 1572872 | tf_op jit(solution)/shard_map/ppermute | solution.py:27
  34.6 27.9 %collective-permute-start.3 = (f32[8,64,256]{2,1,0:T(8,128)S(1)}, f32[8,64,256]{2,1,0:T(8,128)S(1)}, u32[]{:S(2)}, u32[]{:S(2)}) collective-permute-start(f32[8,64,256]{2,1,0:T(8,128)S(1)} %pad_maximum_fusion.4), channel_id=1, source_target_pairs={{1,0},{2,1},{3,2},{4,3},{5,4},{6,5},{7,6},{8,7},{9,8},{10,9},{11,1... | collective-permute-start | bytes 1572872 | tf_op jit(solution)/shard_map/ppermute | solution.py:27
  36.1 40.1 %collective-permute-start.6 = (bf16[192,1024]{1,0:T(8,128)(2,1)S(1)}, bf16[192,1024]{1,0:T(8,128)(2,1)S(1)}, u32[]{:S(2)}, u32[]{:S(2)}) collective-permute-start(bf16[192,1024]{1,0:T(8,128)(2,1)S(1)} %slice.299), channel_id=1, source_target_pairs={{0,4},{1,5},{2,6},{3,7},{4,0},{5,1},{6,2},{7,3},{8,12},{9,13},{10,... | collective-permute-start | bytes 1179656 | tf_op jit(solution)/shard_map/ppermute | solution.py:40
  55.6 20.6 %collective-permute-start.7 = (bf16[192,1024]{1,0:T(8,128)(2,1)S(1)}, bf16[192,1024]{1,0:T(8,128)(2,1)S(1)}, u32[]{:S(2)}, u32[]{:S(2)}) collective-permute-start(bf16[192,1024]{1,0:T(8,128)(2,1)S(1)} %slice.299), channel_id=1, source_target_pairs={{0,8},{1,9},{2,10},{3,11},{4,12},{5,13},{6,14},{7,15},{8,0},{9,1},... | collective-permute-start | bytes 1179656 | tf_op jit(solution)/shard_map/ppermute | solution.py:40
  62.5 23.2 %collective-permute-start.8 = (bf16[512,1024]{1,0:T(8,128)(2,1)S(1)}, bf16[512,1024]{1,0:T(8,128)(2,1)S(1)}, u32[]{:S(2)}, u32[]{:S(2)}) collective-permute-start(bf16[512,1024]{1,0:T(8,128)(2,1)S(1)} %copy-done.3), channel_id=1, source_target_pairs={{0,2},{1,3},{2,0},{3,1},{4,6},{5,7},{6,4},{7,5},{8,10},{9,11},{10,... | collective-permute-start | bytes 3145736 | tf_op jit(solution)/shard_map/ppermute | solution.py:40
  85.7 20.3 %slice-start = ((s8[6291456]{0:T(1024)(128)(4,1)}), s8[4194304]{0:T(1024)(128)(4,1)S(1)}, s32[]{:S(2)}) async-start(s8[6291456]{0:T(1024)(128)(4,1)} %bitcast.218), calls=%async_computation | async-start | bytes 8388608
  86.2 12.7 %collective-permute-start.9 = (bf16[128,1024]{1,0:T(8,128)(2,1)S(1)}, bf16[128,1024]{1,0:T(8,128)(2,1)S(1)}, u32[]{:S(2)}, u32[]{:S(2)}) collective-permute-start(bf16[128,1024]{1,0:T(8,128)(2,1)S(1)} %get-tuple-element.22), channel_id=1, source_target_pairs={{0,1},{1,2},{2,3},{3,4},{4,5},{5,6},{6,7},{7,8},{8,9},{9,10},{10,1... | collective-permute-start | bytes 786440 | tf_op jit(solution)/shard_map/ppermute | solution.py:27
  87.8 11.2 %collective-permute-start.10 = (bf16[128,1024]{1,0:T(8,128)(2,1)S(1)}, bf16[128,1024]{1,0:T(8,128)(2,1)S(1)}, u32[]{:S(2)}, u32[]{:S(2)}) collective-permute-start(bf16[128,1024]{1,0:T(8,128)(2,1)S(1)} %get-tuple-element.21), channel_id=1, source_target_pairs={{1,0},{2,1},{3,2},{4,3},{5,4},{6,5},{7,6},{8,7},{9,8},{10,9},{11,1... | collective-permute-start | bytes 786440 | tf_op jit(solution)/shard_map/ppermute | solution.py:27
  89.3 12.1 %collective-permute-start.11 = (bf16[512,128]{1,0:T(8,128)(2,1)S(1)}, bf16[512,128]{1,0:T(8,128)(2,1)S(1)}, u32[]{:S(2)}, u32[]{:S(2)}) collective-permute-start(bf16[512,128]{1,0:T(8,128)(2,1)S(1)} %bitcast.215), channel_id=1, source_target_pairs={{0,2},{1,3},{2,0},{3,1},{4,6},{5,7},{6,4},{7,5},{8,10},{9,11},{10,... | collective-permute-start | bytes 393224 | tf_op jit(solution)/shard_map/ppermute | solution.py:40
  94.8 7.5 %collective-permute-start.12 = (bf16[512,128]{1,0:T(8,128)(2,1)S(1)}, bf16[512,128]{1,0:T(8,128)(2,1)S(1)}, u32[]{:S(2)}, u32[]{:S(2)}) collective-permute-start(bf16[512,128]{1,0:T(8,128)(2,1)S(1)} %bitcast.216), channel_id=1, source_target_pairs={{0,4},{1,5},{2,6},{3,7},{4,0},{5,1},{6,2},{7,3},{8,12},{9,13},{10,... | collective-permute-start | bytes 393224 | tf_op jit(solution)/shard_map/ppermute | solution.py:40
  94.8 10.8 %collective-permute-start.13 = (bf16[512,128]{1,0:T(8,128)(2,1)S(1)}, bf16[512,128]{1,0:T(8,128)(2,1)S(1)}, u32[]{:S(2)}, u32[]{:S(2)}) collective-permute-start(bf16[512,128]{1,0:T(8,128)(2,1)S(1)} %bitcast.217), channel_id=1, source_target_pairs={{0,8},{1,9},{2,10},{3,11},{4,12},{5,13},{6,14},{7,15},{8,0},{9,1},... | collective-permute-start | bytes 393224 | tf_op jit(solution)/shard_map/ppermute | solution.py:40
  99.0 7.0 %slice-start.1 = ((s8[6291456]{0:T(1024)(128)(4,1)}), s8[2097152]{0:T(1024)(128)(4,1)S(1)}, s32[]{:S(2)}) async-start(s8[6291456]{0:T(1024)(128)(4,1)} %bitcast.218), calls=%async_computation.1 | async-start | bytes 4194304
  116.3 3.7 %copy-start.2 = (bf16[2304,2048]{1,0:T(8,128)(2,1)}, bf16[2304,2048]{1,0:T(8,128)(2,1)S(1)}, u32[]{:S(2)}) copy-start(bf16[2304,2048]{1,0:T(8,128)(2,1)S(1)} %convolution_convert_fusion.refs_0_.refs_1_.refs_2_.refs_3_.refs_5_.refs_6_.refs_7_) | copy-start | bytes 28311556
  120.0 1.5 copy-start.7
  120.0 1.5 %copy-start.8 = (s32[8,4]{0,1:T(4,128)S(1)}, s32[8,4]{0,1:T(4,128)}, u32[]{:S(2)}) copy-start(s32[8,4]{0,1:T(4,128)} %param.16) | copy-start | bytes 388
  120.0 1.6 %copy-start.9 = (s32[4]{0:T(128)S(1)}, s32[4]{0:T(128)}, u32[]{:S(2)}) copy-start(s32[4]{0:T(128)} %constant.6.clone) | copy-start | bytes 52
  121.5 4.8 %collective-permute-start.14 = (bf16[512,2048]{1,0:T(8,128)(2,1)}, bf16[512,2048]{1,0:T(8,128)(2,1)S(1)}, u32[]{:S(2)}, u32[]{:S(2)}) collective-permute-start(bf16[512,2048]{1,0:T(8,128)(2,1)} %slice.359), channel_id=1, source_target_pairs={{0,1},{1,0},{2,3},{3,2},{4,5},{5,4},{6,7},{7,6},{8,9},{9,8},{10,11... | collective-permute-start | bytes 6291464 | tf_op jit(solution)/shard_map/ppermute | solution.py:40
  126.2 1.3 copy-start.5
  127.5 18.9 %copy-start.1 = (bf16[128,1024]{1,0:T(8,128)(2,1)S(1)}, bf16[128,1024]{1,0:T(8,128)(2,1)}, u32[]{:S(2)}) copy-start(bf16[128,1024]{1,0:T(8,128)(2,1)} %param.18) | copy-start | bytes 786436

commit v21 on v20

--- a/solution.py
+++ b/solution.py
@@ -192,7 +192,7 @@
     levels = lax.axis_size("seq").bit_length() - 1
     bits = [link * (levels - 1) // (NEXP - 1) for link in range(NEXP)]
 
-    half = rows * 5 // 8
+    half = rows * 3 // 8
     early = [partner(node_feats[:half], "seq", bit) for bit in bits[2:]]
     encoding, (early,) = chebyshev(
         struct_feats, op_blocks, laplace_index, series_coef, first_block, (), early,

time: 147 us -> 163 us (1.11)
  waiting for transfers between devices: 18.4 us -> 56.4 us
  starting transfers between devices: 61.1 us -> 39.7 us
    ppermute x9, waiting for transfers between devices: 18.4 us -> 51.1 us  [partner(): return lax.ppermute(value, axis, pairs)]
    ppermute x9, starting transfers between devices: 42.1 us -> 10.7 us  [partner(): return lax.ppermute(value, axis, pairs)]
    ppermute x6, starting transfers between devices: 19 us -> 29 us  [shift_rows(): return lax.ppermute(x, axis, pairs)]
    ppermute x6, waiting for transfers between devices: 0.02 us -> 5.27 us  [shift_rows(): return lax.ppermute(x, axis, pairs)]
  transfers between devices with their start and end apart: 15 -> 15, of which waited for: 6 -> 7; matrix products, arithmetic and copies ran while one was open for 17% -> 11% of each run, Pallas kernels for 0% -> 0%
where the time goes in v21:
time: 163 us; the launch traced here: 162 us
  waiting for transfers between devices  56.4 us (35%)
  starting transfers between devices  39.7 us (24%)
  matrix products  31 us (19%)
  Pallas kernels  18.7 us (11%)
  local copies, waits for them, and re-layouts  12.4 us (8%)
  other arithmetic  2.88 us (2%)
    ppermute x9, waiting for transfers between devices, partner(): return lax.ppermute(value, axis, pairs)  51.1 us
    ppermute x6, starting transfers between devices, shift_rows(): return lax.ppermute(x, axis, pairs)  29 us
    pallas_call x1, Pallas kernels, attend(): pl.pallas_call(attention_kernel, grid_spec=grid_spec, out_shape=jax.Shape...  18.7 us
    dot_general x8, matrix products, step(): jnp.einsum('wsk,wkc->wsc', bands[lo - REACH:hi - REACH], stacked, precisi...  15.1 us
    ppermute x9, starting transfers between devices, partner(): return lax.ppermute(value, axis, pairs)  10.7 us
    dot_general x1, matrix products, on_device(): jnp.dot(all_blended, kv_weight, preferred_element_type=jnp.float32)  10.3 us
    unnamed x62, local copies, waits for them, and re-layouts  7.24 us
    ppermute x6, waiting for transfers between devices, shift_rows(): return lax.ppermute(x, axis, pairs)  5.27 us
  transfers between devices with their start and end apart: 15, of which 7 were waited for; matrix products, arithmetic and copies ran while one was open for 11% of the time, Pallas kernels for 0%

profile of v21, /device:TPU:0, one launch (start us, length us, event | category | flops | bytes accessed | tf_op | source)
XLA Modules:
  0.0 162.0 jit_solution(14718370981610843561)
XLA Ops:
  0.0 0.8 copy.35
  1.0 1.8 %select_reduce_fusion = f32[8,5,64,64]{3,2,1,0:T(8,128)S(1)} fusion(f32[8,3,64,64]{3,2,1,0:T(8,128)} %param.13, pred[8,3,5]{2,1,0:T(4,128)(4,1)S(1)} %iota_compare_fusion), kind=kLoop, calls=%fused_computation.2 | loop fusion | flops 819200 | bytes 1048696 | tf_op jit(solution)/shard_map/reduce_sum | solution.py:61
  2.7 0.4 copy.36
  3.1 0.4 copy.37
  3.8 2.4 %collective-permute-start = (f32[8,64,448]{2,1,0:T(8,128)S(1)}, f32[8,64,448]{2,1,0:T(8,128)S(1)}, u32[]{:S(2)}, u32[]{:S(2)}) collective-permute-start(f32[8,64,448]{2,1,0:T(8,128)S(1)} %pad_maximum_fusion.1), channel_id=1, source_target_pairs={{0,1},{1,2},{2,3},{3,4},{4,5},{5,6},{6,7},{7,8},{8,9},{9,10},{10,1... | collective-permute-start | bytes 2752520 | tf_op jit(solution)/shard_map/ppermute | solution.py:27
  6.2 1.3 collective-permute-start.1
  7.5 0.9 collective-permute-done
  8.5 4.4 %collective-permute-done.1 = f32[8,64,448]{2,1,0:T(8,128)S(1)} collective-permute-done((f32[8,64,448]{2,1,0:T(8,128)S(1)}, f32[8,64,448]{2,1,0:T(8,128)S(1)}, u32[]{:S(2)}, u32[]{:S(2)}) %collective-permute-start.1) | collective-permute-done | bytes 917536 | tf_op jit(solution)/shard_map/ppermute | solution.py:27
  13.2 0.4 copy.39
  13.8 1.3 fusion.69
  15.4 0.2 copy.40
  15.6 1.2 fusion.21
  17.0 0.1 copy.41
  17.1 1.0 fusion.15
  18.3 0.1 copy.42
  18.4 1.2 fusion.18
  19.7 20.9 %collective-permute-start.2 = (f32[8,64,256]{2,1,0:T(8,128)S(1)}, f32[8,64,256]{2,1,0:T(8,128)S(1)}, u32[]{:S(2)}, u32[]{:S(2)}) collective-permute-start(f32[8,64,256]{2,1,0:T(8,128)S(1)} %pad_maximum_fusion.4), channel_id=1, source_target_pairs={{0,1},{1,2},{2,3},{3,4},{4,5},{5,6},{6,7},{7,8},{8,9},{9,10},{10,1... | collective-permute-start | bytes 1572872 | tf_op jit(solution)/shard_map/ppermute | solution.py:27
  40.6 1.5 collective-permute-start.3
  42.1 3.8 %collective-permute-start.4 = (bf16[192,1024]{1,0:T(8,128)(2,1)S(1)}, bf16[192,1024]{1,0:T(8,128)(2,1)S(1)}, u32[]{:S(2)}, u32[]{:S(2)}) collective-permute-start(bf16[192,1024]{1,0:T(8,128)(2,1)S(1)} %slice.267), channel_id=1, source_target_pairs={{0,4},{1,5},{2,6},{3,7},{4,0},{5,1},{6,2},{7,3},{8,12},{9,13},{10,... | collective-permute-start | bytes 1179656 | tf_op jit(solution)/shard_map/ppermute | solution.py:40
  45.9 2.6 %collective-permute-start.5 = (bf16[192,1024]{1,0:T(8,128)(2,1)S(1)}, bf16[192,1024]{1,0:T(8,128)(2,1)S(1)}, u32[]{:S(2)}, u32[]{:S(2)}) collective-permute-start(bf16[192,1024]{1,0:T(8,128)(2,1)S(1)} %slice.267), channel_id=1, source_target_pairs={{0,8},{1,9},{2,10},{3,11},{4,12},{5,13},{6,14},{7,15},{8,0},{9,1},... | collective-permute-start | bytes 1179656 | tf_op jit(solution)/shard_map/ppermute | solution.py:40
  48.5 0.5 collective-permute-start.6
  49.1 0.7 fusion.71
  49.7 31.8 %collective-permute-done.4 = bf16[192,1024]{1,0:T(8,128)(2,1)S(1)} collective-permute-done((bf16[192,1024]{1,0:T(8,128)(2,1)S(1)}, bf16[192,1024]{1,0:T(8,128)(2,1)S(1)}, u32[]{:S(2)}, u32[]{:S(2)}) %collective-permute-start.4) | collective-permute-done | bytes 393248 | tf_op jit(solution)/shard_map/ppermute | solution.py:40
  82.0 0.2 copy.44
  82.2 1.3 fusion.14
  83.8 0.2 copy.45
  84.0 1.2 fusion.22
  85.5 0.1 copy.46
  85.6 1.0 fusion.16
  86.8 6.8 %fusion.20 = bf16[8,64,128]{2,1,0:T(8,128)(2,1)S(1)} fusion(f32[8,64,320]{1,2,0:T(8,128)S(1)} %bitcast.201, f32[8,320,128]{2,1,0:T(8,128)S(1)} %bitcast.206, f32[20,64,128]{2,1,0:T(8,128)S(1)} %fusion.14, f32[20,64,128]{2,1,0:T(8,128)S(1)} %fusion.69, f32[16,64,128]{2,1,0:T(8,128)S(1)} %fusion.22, f32[8,64,128]{2,1,0:T(8,128)S(1)} %fusion.18, ...), kind=kOutput, calls=%fused_computation.28 | convolution fusion | flops 127139840 | bytes 4194340 | tf_op jit(solution)/shard_map/wsk,wkc->wsc/dot_general | solution.py:78
  93.6 10.8 %collective-permute-done.7 = bf16[320,1024]{1,0:T(8,128)(2,1)S(1)} collective-permute-done((bf16[320,1024]{1,0:T(8,128)(2,1)S(1)}, bf16[320,1024]{1,0:T(8,128)(2,1)S(1)}, u32[]{:S(2)}, u32[]{:S(2)}) %collective-permute-start.7) | collective-permute-done | bytes 655392 | tf_op jit(solution)/shard_map/ppermute | solution.py:40
  104.4 0.4 add_convert_fusion.3
  104.9 1.4 collective-permute-start.9
  106.4 1.5 collective-permute-start.10
  108.0 3.6 %collective-permute-start.13 = (bf16[512,128]{1,0:T(8,128)(2,1)S(1)}, bf16[512,128]{1,0:T(8,128)(2,1)S(1)}, u32[]{:S(2)}, u32[]{:S(2)}) collective-permute-start(bf16[512,128]{1,0:T(8,128)(2,1)S(1)} %bitcast.217), channel_id=1, source_target_pairs={{0,8},{1,9},{2,10},{3,11},{4,12},{5,13},{6,14},{7,15},{8,0},{9,1},... | collective-permute-start | bytes 393224 | tf_op jit(solution)/shard_map/ppermute | solution.py:40
  111.8 2.4 %collective-permute-done.11 = bf16[512,128]{1,0:T(8,128)(2,1)S(1)} collective-permute-done((bf16[512,128]{1,0:T(8,128)(2,1)S(1)}, bf16[512,128]{1,0:T(8,128)(2,1)S(1)}, u32[]{:S(2)}, u32[]{:S(2)}) %collective-permute-start.11) | collective-permute-done | bytes 131104 | tf_op jit(solution)/shard_map/ppermute | solution.py:40
  114.2 0.4 fusion.23
  114.6 0.8 collective-permute-done.12
  115.4 0.4 fusion.3
  115.8 5.4 %collective-permute-done.13 = bf16[512,128]{1,0:T(8,128)(2,1)S(1)} collective-permute-done((bf16[512,128]{1,0:T(8,128)(2,1)S(1)}, bf16[512,128]{1,0:T(8,128)(2,1)S(1)}, u32[]{:S(2)}, u32[]{:S(2)}) %collective-permute-start.13) | collective-permute-done | bytes 131104 | tf_op jit(solution)/shard_map/ppermute | solution.py:40
  121.2 0.4 fusion.4
  121.6 10.3 %convolution_convert_fusion.refs_0_.refs_1_.refs_2_.refs_3_.refs_5_.refs_6_.refs_7_ = bf16[2304,2048]{1,0:T(8,128)(2,1)S(1)} fusion(bf16[2304,1024]{1,0:T(8,128)(2,1)S(1)} %fusion.4, bf16[1024,3072]{1,0:T(8,128)(2,1)S(1)} %bitcast.219), kind=kOutput, calls=%fused_computation | convolution fusion | flops 9668395008 | bytes 18350080 | tf_op jit(solution)/shard_map/dot_general | solution.py:222
  131.9 3.7 %copy-done.2 = bf16[2304,2048]{1,0:T(8,128)(2,1)} copy-done((bf16[2304,2048]{1,0:T(8,128)(2,1)}, bf16[2304,2048]{1,0:T(8,128)(2,1)S(1)}, u32[]{:S(2)}) %copy-start.2) | copy-done | bytes 9437208
  135.6 1.4 slice.359
  137.2 0.7 pad_add_fusion.table_ref
  137.9 3.9 %fusion.11.q_ref = bf16[1024,512]{1,0:T(8,128)(2,1)} fusion(bf16[512,1024]{1,0:T(8,128)(2,1)S(1)} %add_convert_fusion.3, bf16[1024,3072]{1,0:T(8,128)(2,1)} %param.19), kind=kOutput, calls=%fused_computation.14 | convolution fusion | flops 1074790400 | bytes 4194304 | tf_op jit(solution)/shard_map/dot_general | solution.py:214
  141.8 1.3 copy-done.5
  143.1 18.7 %shard_map.109 = bf16[512,1024]{1,0:T(8,128)(2,1)} custom-call(s32[8,8]{1,0:T(8,128)} %pad_add_fusion.table_ref, bf16[1024,512]{1,0:T(8,128)(2,1)} %fusion.11.q_ref, bf16[2304,2048]{1,0:T(8,128)(2,1)} %copy-done.2, bf16[2304,2048]{1,0:T(8,128)(2,1)} %copy-done.2, bf16[2304,2048]{1,0:T(8,128)(2,1)} %copy-done.2, bf16[2304,2048]{1,0:T(8,128)(2,1)} %copy-done.2, ...), custom_call_target="tpu_custom_call" | custom-call | tf_op jit(solution)/shard_map/pallas_call | solution.py:169
  (104 shorter events, 2.8 us)
Async XLA Ops:
  0.0 104.4 %copy-start = (bf16[128,1024]{1,0:T(8,128)(2,1)S(1)}, bf16[128,1024]{1,0:T(8,128)(2,1)}, u32[]{:S(2)}) copy-start(bf16[128,1024]{1,0:T(8,128)(2,1)} %param.18) | copy-start | bytes 786436
  2.7 1.0 copy-start.4
  3.8 4.6 %collective-permute-start = (f32[8,64,448]{2,1,0:T(8,128)S(1)}, f32[8,64,448]{2,1,0:T(8,128)S(1)}, u32[]{:S(2)}, u32[]{:S(2)}) collective-permute-start(f32[8,64,448]{2,1,0:T(8,128)S(1)} %pad_maximum_fusion.1), channel_id=1, source_target_pairs={{0,1},{1,2},{2,3},{3,4},{4,5},{5,6},{6,7},{7,8},{8,9},{9,10},{10,1... | collective-permute-start | bytes 2752520 | tf_op jit(solution)/shard_map/ppermute | solution.py:27
  6.2 6.6 %collective-permute-start.1 = (f32[8,64,448]{2,1,0:T(8,128)S(1)}, f32[8,64,448]{2,1,0:T(8,128)S(1)}, u32[]{:S(2)}, u32[]{:S(2)}) collective-permute-start(f32[8,64,448]{2,1,0:T(8,128)S(1)} %pad_maximum_fusion.1), channel_id=1, source_target_pairs={{1,0},{2,1},{3,2},{4,3},{5,4},{6,5},{7,6},{8,7},{9,8},{10,9},{11,1... | collective-permute-start | bytes 2752520 | tf_op jit(solution)/shard_map/ppermute | solution.py:27
  18.4 23.7 %copy-start.3 = (bf16[512,1024]{1,0:T(8,128)(2,1)S(1)}, bf16[512,1024]{1,0:T(8,128)(2,1)}, u32[]{:S(2)}) copy-start(bf16[512,1024]{1,0:T(8,128)(2,1)} %param.11) | copy-start | bytes 3145732
  19.6 29.4 %copy-start.6 = (f32[9]{0:T(128)S(1)}, f32[9]{0:T(128)}, u32[]{:S(2)}) copy-start(f32[9]{0:T(128)} %param.17) | copy-start | bytes 112
  19.7 61.9 %collective-permute-start.2 = (f32[8,64,256]{2,1,0:T(8,128)S(1)}, f32[8,64,256]{2,1,0:T(8,128)S(1)}, u32[]{:S(2)}, u32[]{:S(2)}) collective-permute-start(f32[8,64,256]{2,1,0:T(8,128)S(1)} %pad_maximum_fusion.4), channel_id=1, source_target_pairs={{0,1},{1,2},{2,3},{3,4},{4,5},{5,6},{6,7},{7,8},{8,9},{9,10},{10,1... | collective-permute-start | bytes 1572872 | tf_op jit(solution)/shard_map/ppermute | solution.py:27
  40.6 41.0 %collective-permute-start.3 = (f32[8,64,256]{2,1,0:T(8,128)S(1)}, f32[8,64,256]{2,1,0:T(8,128)S(1)}, u32[]{:S(2)}, u32[]{:S(2)}) collective-permute-start(f32[8,64,256]{2,1,0:T(8,128)S(1)} %pad_maximum_fusion.4), channel_id=1, source_target_pairs={{1,0},{2,1},{3,2},{4,3},{5,4},{6,5},{7,6},{8,7},{9,8},{10,9},{11,1... | collective-permute-start | bytes 1572872 | tf_op jit(solution)/shard_map/ppermute | solution.py:27
  42.1 39.4 %collective-permute-start.4 = (bf16[192,1024]{1,0:T(8,128)(2,1)S(1)}, bf16[192,1024]{1,0:T(8,128)(2,1)S(1)}, u32[]{:S(2)}, u32[]{:S(2)}) collective-permute-start(bf16[192,1024]{1,0:T(8,128)(2,1)S(1)} %slice.267), channel_id=1, source_target_pairs={{0,4},{1,5},{2,6},{3,7},{4,0},{5,1},{6,2},{7,3},{8,12},{9,13},{10,... | collective-permute-start | bytes 1179656 | tf_op jit(solution)/shard_map/ppermute | solution.py:40
  45.9 35.6 %collective-permute-start.5 = (bf16[192,1024]{1,0:T(8,128)(2,1)S(1)}, bf16[192,1024]{1,0:T(8,128)(2,1)S(1)}, u32[]{:S(2)}, u32[]{:S(2)}) collective-permute-start(bf16[192,1024]{1,0:T(8,128)(2,1)S(1)} %slice.267), channel_id=1, source_target_pairs={{0,8},{1,9},{2,10},{3,11},{4,12},{5,13},{6,14},{7,15},{8,0},{9,1},... | collective-permute-start | bytes 1179656 | tf_op jit(solution)/shard_map/ppermute | solution.py:40
  48.5 45.1 %collective-permute-start.6 = (bf16[320,1024]{1,0:T(8,128)(2,1)S(1)}, bf16[320,1024]{1,0:T(8,128)(2,1)S(1)}, u32[]{:S(2)}, u32[]{:S(2)}) collective-permute-start(bf16[320,1024]{1,0:T(8,128)(2,1)S(1)} %slice.299), channel_id=1, source_target_pairs={{0,4},{1,5},{2,6},{3,7},{4,0},{5,1},{6,2},{7,3},{8,12},{9,13},{10,... | collective-permute-start | bytes 1966088 | tf_op jit(solution)/shard_map/ppermute | solution.py:40
  81.5 22.9 %collective-permute-start.7 = (bf16[320,1024]{1,0:T(8,128)(2,1)S(1)}, bf16[320,1024]{1,0:T(8,128)(2,1)S(1)}, u32[]{:S(2)}, u32[]{:S(2)}) collective-permute-start(bf16[320,1024]{1,0:T(8,128)(2,1)S(1)} %slice.299), channel_id=1, source_target_pairs={{0,8},{1,9},{2,10},{3,11},{4,12},{5,13},{6,14},{7,15},{8,0},{9,1},... | collective-permute-start | bytes 1966088 | tf_op jit(solution)/shard_map/ppermute | solution.py:40
  81.5 22.9 %collective-permute-start.8 = (bf16[512,1024]{1,0:T(8,128)(2,1)S(1)}, bf16[512,1024]{1,0:T(8,128)(2,1)S(1)}, u32[]{:S(2)}, u32[]{:S(2)}) collective-permute-start(bf16[512,1024]{1,0:T(8,128)(2,1)S(1)} %copy-done.3), channel_id=1, source_target_pairs={{0,2},{1,3},{2,0},{3,1},{4,6},{5,7},{6,4},{7,5},{8,10},{9,11},{10,... | collective-permute-start | bytes 3145736 | tf_op jit(solution)/shard_map/ppermute | solution.py:40
  104.4 17.2 %slice-start = ((s8[6291456]{0:T(1024)(128)(4,1)}), s8[4194304]{0:T(1024)(128)(4,1)S(1)}, s32[]{:S(2)}) async-start(s8[6291456]{0:T(1024)(128)(4,1)} %bitcast.218), calls=%async_computation | async-start | bytes 8388608
  104.9 6.7 %collective-permute-start.9 = (bf16[128,1024]{1,0:T(8,128)(2,1)S(1)}, bf16[128,1024]{1,0:T(8,128)(2,1)S(1)}, u32[]{:S(2)}, u32[]{:S(2)}) collective-permute-start(bf16[128,1024]{1,0:T(8,128)(2,1)S(1)} %get-tuple-element.22), channel_id=1, source_target_pairs={{0,1},{1,2},{2,3},{3,4},{4,5},{5,6},{6,7},{7,8},{8,9},{9,10},{10,1... | collective-permute-start | bytes 786440 | tf_op jit(solution)/shard_map/ppermute | solution.py:27
  106.4 5.4 %collective-permute-start.10 = (bf16[128,1024]{1,0:T(8,128)(2,1)S(1)}, bf16[128,1024]{1,0:T(8,128)(2,1)S(1)}, u32[]{:S(2)}, u32[]{:S(2)}) collective-permute-start(bf16[128,1024]{1,0:T(8,128)(2,1)S(1)} %get-tuple-element.21), channel_id=1, source_target_pairs={{1,0},{2,1},{3,2},{4,3},{5,4},{6,5},{7,6},{8,7},{9,8},{10,9},{11,1... | collective-permute-start | bytes 786440 | tf_op jit(solution)/shard_map/ppermute | solution.py:27
  107.9 6.3 %collective-permute-start.11 = (bf16[512,128]{1,0:T(8,128)(2,1)S(1)}, bf16[512,128]{1,0:T(8,128)(2,1)S(1)}, u32[]{:S(2)}, u32[]{:S(2)}) collective-permute-start(bf16[512,128]{1,0:T(8,128)(2,1)S(1)} %bitcast.215), channel_id=1, source_target_pairs={{0,2},{1,3},{2,0},{3,1},{4,6},{5,7},{6,4},{7,5},{8,10},{9,11},{10,... | collective-permute-start | bytes 393224 | tf_op jit(solution)/shard_map/ppermute | solution.py:40
  108.0 7.4 %collective-permute-start.12 = (bf16[512,128]{1,0:T(8,128)(2,1)S(1)}, bf16[512,128]{1,0:T(8,128)(2,1)S(1)}, u32[]{:S(2)}, u32[]{:S(2)}) collective-permute-start(bf16[512,128]{1,0:T(8,128)(2,1)S(1)} %bitcast.216), channel_id=1, source_target_pairs={{0,4},{1,5},{2,6},{3,7},{4,0},{5,1},{6,2},{7,3},{8,12},{9,13},{10,... | collective-permute-start | bytes 393224 | tf_op jit(solution)/shard_map/ppermute | solution.py:40
  108.0 13.1 %collective-permute-start.13 = (bf16[512,128]{1,0:T(8,128)(2,1)S(1)}, bf16[512,128]{1,0:T(8,128)(2,1)S(1)}, u32[]{:S(2)}, u32[]{:S(2)}) collective-permute-start(bf16[512,128]{1,0:T(8,128)(2,1)S(1)} %bitcast.217), channel_id=1, source_target_pairs={{0,8},{1,9},{2,10},{3,11},{4,12},{5,13},{6,14},{7,15},{8,0},{9,1},... | collective-permute-start | bytes 393224 | tf_op jit(solution)/shard_map/ppermute | solution.py:40
  111.8 9.8 %slice-start.1 = ((s8[6291456]{0:T(1024)(128)(4,1)}), s8[2097152]{0:T(1024)(128)(4,1)S(1)}, s32[]{:S(2)}) async-start(s8[6291456]{0:T(1024)(128)(4,1)} %bitcast.218), calls=%async_computation.1 | async-start | bytes 4194304
  131.9 3.7 %copy-start.2 = (bf16[2304,2048]{1,0:T(8,128)(2,1)}, bf16[2304,2048]{1,0:T(8,128)(2,1)S(1)}, u32[]{:S(2)}) copy-start(bf16[2304,2048]{1,0:T(8,128)(2,1)S(1)} %convolution_convert_fusion.refs_0_.refs_1_.refs_2_.refs_3_.refs_5_.refs_6_.refs_7_) | copy-start | bytes 28311556
  135.6 1.5 copy-start.7
  135.6 1.5 copy-start.8
  135.6 1.6 %copy-start.9 = (s32[4]{0:T(128)S(1)}, s32[4]{0:T(128)}, u32[]{:S(2)}) copy-start(s32[4]{0:T(128)} %constant.6.clone) | copy-start | bytes 52
  137.0 4.8 %collective-permute-start.14 = (bf16[512,2048]{1,0:T(8,128)(2,1)}, bf16[512,2048]{1,0:T(8,128)(2,1)S(1)}, u32[]{:S(2)}, u32[]{:S(2)}) collective-permute-start(bf16[512,2048]{1,0:T(8,128)(2,1)} %slice.359), channel_id=1, source_target_pairs={{0,1},{1,0},{2,3},{3,2},{4,5},{5,4},{6,7},{7,6},{8,9},{9,8},{10,11... | collective-permute-start | bytes 6291464 | tf_op jit(solution)/shard_map/ppermute | solution.py:40
  141.8 1.3 copy-start.5
  143.1 18.7 %copy-start.1 = (bf16[128,1024]{1,0:T(8,128)(2,1)S(1)}, bf16[128,1024]{1,0:T(8,128)(2,1)}, u32[]{:S(2)}) copy-start(bf16[128,1024]{1,0:T(8,128)(2,1)} %param.18) | copy-start | bytes 786436

commit v22 on v18

--- a/solution.py
+++ b/solution.py
@@ -57,11 +57,15 @@
     halo = PER_EXCHANGE * REACH
     block_ids = first_block + jnp.arange(count, dtype=jnp.int32)
     offsets = laplace_index - block_ids[:, None] + REACH
-    hit = offsets[:, :, None] == jnp.arange(taps, dtype=jnp.int32)[None, None, :]
-    bands = jnp.sum(jnp.where(hit[:, :, :, None, None], op_blocks[:, :, None], 0.0), axis=1)
-    bands = bands.transpose(0, 2, 1, 3).reshape(count, BS, taps * BS)
     own_field = struct_feats.reshape(count, BS, chans)
-    payload = jnp.concatenate([own_field, bands], axis=2)
+    taps_out = []
+    for o in range(taps):
+        tap = jnp.zeros((count, BS, BS), jnp.float32)
+        for j in range(op_blocks.shape[1]):
+            tap = tap + jnp.where((offsets[:, j] == o)[:, None, None], op_blocks[:, j], 0.0)
+        taps_out.append(tap)
+    payload = jnp.concatenate([own_field] + taps_out, axis=2)
+    bands = payload[:, :, chans:]
     left = shift_rows(payload[count - halo :], "seq", 1)
     right = shift_rows(payload[:halo], "seq", -1)
     edge = halo - REACH

time: 145 us -> 149 us (1.028); the launches traced: 142 us -> 148 us
  local copies, waits for them, and re-layouts: 12.3 us -> 16.7 us
    add x0 -> x2, other arithmetic: none -> 2.69 us  [chebyshev(): tap + jnp.where((offsets[:, j] == o)[:, None, None], op_blocks[:, j], 0.0)]
    dot_general x4, matrix products: 1.68 us -> 3.77 us  [blend(): encoded = jnp.dot(enc, encode_weight, preferred_element_type=jnp.float32)]
    ppermute x9, starting transfers between devices: 39.7 us -> 41.5 us  [partner(): return lax.ppermute(value, axis, pairs)]
    reduce_sum x1 -> x0, other arithmetic: 1.76 us -> none  [chebyshev(): jnp.sum(jnp.where(hit[:, :, :, None, None], op_blocks[:, :, None], 0.0),...]
    concatenate x0 -> x2, local copies, waits for them, and re-layouts: none -> 1.51 us  [chebyshev(): payload = jnp.concatenate([own_field] + taps_out, axis=2)]
    unnamed x62 -> x64, local copies, waits for them, and re-layouts: 7.15 us -> 7.06 us
  transfers between devices with their start and end apart: 15 -> 15, of which waited for: 4 -> 4; matrix products, arithmetic and copies ran while one was open for 17% -> 21% of each run, Pallas kernels for 0% -> 0%
where the time goes in v22:
time: 149 us; the launch traced here: 148 us
  starting transfers between devices  59.5 us (40%)
  matrix products  32.1 us (22%)
  Pallas kernels  18.9 us (13%)
  local copies, waits for them, and re-layouts  16.7 us (11%)
  waiting for transfers between devices  15.2 us (10%)
  other arithmetic  4.94 us (3%)
    ppermute x9, starting transfers between devices, partner(): return lax.ppermute(value, axis, pairs)  41.5 us
    pallas_call x1, Pallas kernels, attend(): pl.pallas_call(attention_kernel, grid_spec=grid_spec, out_shape=jax.Shape...  18.9 us
    ppermute x6, starting transfers between devices, shift_rows(): return lax.ppermute(x, axis, pairs)  18 us
    ppermute x9, waiting for transfers between devices, partner(): return lax.ppermute(value, axis, pairs)  15.2 us
    dot_general x8, matrix products, step(): jnp.einsum('wsk,wkc->wsc', bands[lo - REACH:hi - REACH], stacked, precisi...  14.1 us
    dot_general x1, matrix products, on_device(): jnp.dot(all_blended, kv_weight, preferred_element_type=jnp.float32)  10.3 us
    unnamed x64, local copies, waits for them, and re-layouts  7.06 us
    dot_general x1, matrix products, on_device(): lax.dot_general(qkv_weight[:, :D], blended, (((0,), (1,)), ((), ())), pre...  3.86 us
  transfers between devices with their start and end apart: 15, of which 4 were waited for; matrix products, arithmetic and copies ran while one was open for 21% of the time, Pallas kernels for 0%

profile of v22, /device:TPU:0, one launch (start us, length us, event | category | flops | bytes accessed | tf_op | source)
XLA Modules:
  0.0 148.3 jit_solution(12664942399641991833)
XLA Ops:
  0.0 0.8 copy.22
  0.9 0.4 compare_reduce_fusion.2
  1.3 1.3 fusion.72
  2.6 1.4 fusion.73
  4.0 1.2 concatenate.34
  5.2 3.4 %collective-permute-start = (f32[8,64,448]{2,1,0:T(8,128)}, f32[8,64,448]{2,1,0:T(8,128)}, u32[]{:S(2)}, u32[]{:S(2)}) collective-permute-start(f32[8,64,448]{2,1,0:T(8,128)} %concatenate.34), channel_id=1, source_target_pairs={{0,1},{1,2},{2,3},{3,4},{4,5},{5,6},{6,7},{7,8},{8,9},{9,10},{10,1... | collective-permute-start | bytes 2752520 | tf_op jit(solution)/shard_map/ppermute | solution.py:27
  8.6 1.3 collective-permute-start.1
  9.9 1.0 fusion.81
  11.0 4.8 %collective-permute-start.4 = (bf16[256,1024]{1,0:T(8,128)(2,1)}, bf16[256,1024]{1,0:T(8,128)(2,1)}, u32[]{:S(2)}, u32[]{:S(2)}) collective-permute-start(bf16[256,1024]{1,0:T(8,128)(2,1)} %get-tuple-element.39), channel_id=1, source_target_pairs={{0,4},{1,5},{2,6},{3,7},{4,0},{5,1},{6,2},{7,3},{8,12},{9,13},{10,... | collective-permute-start | bytes 1572872 | tf_op jit(solution)/shard_map/ppermute | solution.py:40
  15.8 2.6 %collective-permute-start.5 = (bf16[256,1024]{1,0:T(8,128)(2,1)}, bf16[256,1024]{1,0:T(8,128)(2,1)}, u32[]{:S(2)}, u32[]{:S(2)}) collective-permute-start(bf16[256,1024]{1,0:T(8,128)(2,1)} %get-tuple-element.39), channel_id=1, source_target_pairs={{0,8},{1,9},{2,10},{3,11},{4,12},{5,13},{6,14},{7,15},{8,0},{9,1},... | collective-permute-start | bytes 1572872 | tf_op jit(solution)/shard_map/ppermute | solution.py:40
  18.7 1.0 slice.357
  19.7 1.0 slice.358
  20.6 1.0 pad_maximum_fusion.1
  22.2 1.1 slice.355
  23.3 1.1 slice.356
  24.4 1.3 fusion.79
  26.3 1.2 fusion.21
  27.9 1.0 fusion.15
  29.2 0.6 fusion.20
  29.8 8.9 %collective-permute-start.2 = (f32[8,64,256]{2,1,0:T(8,128)S(1)}, f32[8,64,256]{2,1,0:T(8,128)S(1)}, u32[]{:S(2)}, u32[]{:S(2)}) collective-permute-start(f32[8,64,256]{2,1,0:T(8,128)S(1)} %pad_maximum_fusion.3), channel_id=1, source_target_pairs={{0,1},{1,2},{2,3},{3,4},{4,5},{5,6},{6,7},{7,8},{8,9},{9,10},{10,1... | collective-permute-start | bytes 1572872 | tf_op jit(solution)/shard_map/ppermute | solution.py:27
  38.8 1.5 collective-permute-start.3
  40.2 15.2 %collective-permute-start.6 = (bf16[256,1024]{1,0:T(8,128)(2,1)S(1)}, bf16[256,1024]{1,0:T(8,128)(2,1)S(1)}, u32[]{:S(2)}, u32[]{:S(2)}) collective-permute-start(bf16[256,1024]{1,0:T(8,128)(2,1)S(1)} %copy-done.6), channel_id=1, source_target_pairs={{0,4},{1,5},{2,6},{3,7},{4,0},{5,1},{6,2},{7,3},{8,12},{9,13},{10,... | collective-permute-start | bytes 1572872 | tf_op jit(solution)/shard_map/ppermute | solution.py:40
  55.5 0.7 fusion.82
  56.2 7.5 %collective-permute-start.7 = (bf16[256,1024]{1,0:T(8,128)(2,1)S(1)}, bf16[256,1024]{1,0:T(8,128)(2,1)S(1)}, u32[]{:S(2)}, u32[]{:S(2)}) collective-permute-start(bf16[256,1024]{1,0:T(8,128)(2,1)S(1)} %copy-done.6), channel_id=1, source_target_pairs={{0,8},{1,9},{2,10},{3,11},{4,12},{5,13},{6,14},{7,15},{8,0},{9,1},... | collective-permute-start | bytes 1572872 | tf_op jit(solution)/shard_map/ppermute | solution.py:40
  64.4 1.3 fusion.14
  66.3 1.3 fusion.22
  68.0 1.0 fusion.16
  69.2 0.8 copy-done.5
  70.0 6.4 %fusion.19 = bf16[8,64,128]{2,1,0:T(8,128)(2,1)S(1)} fusion(f32[8,64,320]{2,1,0:T(8,128)S(1)} %concatenate.35, f32[8,320,128]{2,1,0:T(8,128)S(1)} %bitcast.264, f32[20,64,128]{2,1,0:T(8,128)S(1)} %fusion.14, f32[20,64,128]{2,1,0:T(8,128)S(1)} %fusion.79, f32[16,64,128]{2,1,0:T(8,128)S(1)} %fusion.22, f32[8,64,128]{2,1,0:T(8,128)S(1)} %fusion.20, ...), kind=kOutput, calls=%fused_computation.25 | convolution fusion | flops 127139840 | bytes 4194340 | tf_op jit(solution)/shard_map/wsk,wkc->wsc/dot_general | solution.py:82
  76.4 5.4 %collective-permute-done.6 = bf16[256,1024]{1,0:T(8,128)(2,1)S(1)} collective-permute-done((bf16[256,1024]{1,0:T(8,128)(2,1)S(1)}, bf16[256,1024]{1,0:T(8,128)(2,1)S(1)}, u32[]{:S(2)}, u32[]{:S(2)}) %collective-permute-start.6) | collective-permute-done | bytes 524320 | tf_op jit(solution)/shard_map/ppermute | solution.py:40
  81.8 5.2 %collective-permute-done.8 = bf16[512,1024]{1,0:T(8,128)(2,1)S(1)} collective-permute-done((bf16[512,1024]{1,0:T(8,128)(2,1)S(1)}, bf16[512,1024]{1,0:T(8,128)(2,1)S(1)}, u32[]{:S(2)}, u32[]{:S(2)}) %collective-permute-start.8) | collective-permute-done | bytes 1048608 | tf_op jit(solution)/shard_map/ppermute | solution.py:40
  87.1 0.4 add_convert_fusion.3
  87.6 1.4 collective-permute-start.9
  89.0 1.5 %collective-permute-start.10 = (bf16[128,1024]{1,0:T(8,128)(2,1)S(1)}, bf16[128,1024]{1,0:T(8,128)(2,1)S(1)}, u32[]{:S(2)}, u32[]{:S(2)}) collective-permute-start(bf16[128,1024]{1,0:T(8,128)(2,1)S(1)} %get-tuple-element.36), channel_id=1, source_target_pairs={{1,0},{2,1},{3,2},{4,3},{5,4},{6,5},{7,6},{8,7},{9,8},{10,9},{11,1... | collective-permute-start | bytes 786440 | tf_op jit(solution)/shard_map/ppermute | solution.py:27
  90.5 5.6 %collective-permute-start.11 = (bf16[512,128]{1,0:T(8,128)(2,1)S(1)}, bf16[512,128]{1,0:T(8,128)(2,1)S(1)}, u32[]{:S(2)}, u32[]{:S(2)}) collective-permute-start(bf16[512,128]{1,0:T(8,128)(2,1)S(1)} %bitcast.273), channel_id=1, source_target_pairs={{0,2},{1,3},{2,0},{3,1},{4,6},{5,7},{6,4},{7,5},{8,10},{9,11},{10,... | collective-permute-start | bytes 393224 | tf_op jit(solution)/shard_map/ppermute | solution.py:40
  96.2 1.2 collective-permute-start.12
  97.4 4.5 %collective-permute-start.13 = (bf16[512,128]{1,0:T(8,128)(2,1)S(1)}, bf16[512,128]{1,0:T(8,128)(2,1)S(1)}, u32[]{:S(2)}, u32[]{:S(2)}) collective-permute-start(bf16[512,128]{1,0:T(8,128)(2,1)S(1)} %bitcast.275), channel_id=1, source_target_pairs={{0,8},{1,9},{2,10},{3,11},{4,12},{5,13},{6,14},{7,15},{8,0},{9,1},... | collective-permute-start | bytes 393224 | tf_op jit(solution)/shard_map/ppermute | solution.py:40
  102.0 0.8 collective-permute-done.11
  102.8 0.4 fusion.23
  103.2 3.7 %collective-permute-done.12 = bf16[512,128]{1,0:T(8,128)(2,1)S(1)} collective-permute-done((bf16[512,128]{1,0:T(8,128)(2,1)S(1)}, bf16[512,128]{1,0:T(8,128)(2,1)S(1)}, u32[]{:S(2)}, u32[]{:S(2)}) %collective-permute-start.12) | collective-permute-done | bytes 131104 | tf_op jit(solution)/shard_map/ppermute | solution.py:40
  106.9 1.5 fusion.3
  108.4 1.5 fusion.4
  109.9 10.3 %convolution_convert_fusion.refs_0_.refs_1_.refs_2_.refs_3_.refs_5_.refs_6_.refs_7_ = bf16[2304,2048]{1,0:T(8,128)(2,1)S(1)} fusion(bf16[2304,1024]{1,0:T(8,128)(2,1)S(1)} %fusion.4, bf16[1024,3072]{1,0:T(8,128)(2,1)S(1)} %bitcast.277), kind=kOutput, calls=%fused_computation | convolution fusion | flops 9668395008 | bytes 18350080 | tf_op jit(solution)/shard_map/dot_general | solution.py:226
  120.2 3.6 %copy-done.2 = bf16[2304,2048]{1,0:T(8,128)(2,1)} copy-done((bf16[2304,2048]{1,0:T(8,128)(2,1)}, bf16[2304,2048]{1,0:T(8,128)(2,1)S(1)}, u32[]{:S(2)}) %copy-start.2) | copy-done | bytes 9437208
  124.1 0.5 copy-done.8
  124.7 0.7 pad_add_fusion.table_ref
  125.4 3.9 %fusion.11.q_ref = bf16[1024,512]{1,0:T(8,128)(2,1)} fusion(bf16[512,1024]{1,0:T(8,128)(2,1)S(1)} %add_convert_fusion.3, bf16[1024,3072]{1,0:T(8,128)(2,1)} %param.19), kind=kOutput, calls=%fused_computation.13 | convolution fusion | flops 1074790400 | bytes 4194304 | tf_op jit(solution)/shard_map/dot_general | solution.py:218
  129.2 18.9 %shard_map.109 = bf16[512,1024]{1,0:T(8,128)(2,1)} custom-call(s32[8,8]{1,0:T(8,128)} %pad_add_fusion.table_ref, bf16[1024,512]{1,0:T(8,128)(2,1)} %fusion.11.q_ref, bf16[2304,2048]{1,0:T(8,128)(2,1)} %copy-done.2, bf16[2304,2048]{1,0:T(8,128)(2,1)} %copy-done.2, bf16[2304,2048]{1,0:T(8,128)(2,1)} %copy-done.2, bf16[2304,2048]{1,0:T(8,128)(2,1)} %copy-done.2, ...), custom_call_target="tpu_custom_call" | custom-call | tf_op jit(solution)/shard_map/pallas_call | solution.py:173
  (105 shorter events, 4.2 us)
Async XLA Ops:
  0.0 87.1 %copy-start = (bf16[128,1024]{1,0:T(8,128)(2,1)S(1)}, bf16[128,1024]{1,0:T(8,128)(2,1)}, u32[]{:S(2)}) copy-start(bf16[128,1024]{1,0:T(8,128)(2,1)} %param.18) | copy-start | bytes 786436
  0.0 4.0 %copy-start.4 = (f32[512,128]{1,0:T(8,128)S(1)}, f32[512,128]{1,0:T(8,128)}, u32[]{:S(2)}) copy-start(f32[512,128]{1,0:T(8,128)} %param.12) | copy-start | bytes 786436
  2.6 7.4 %copy-start.3 = (bf16[512,1024]{1,0:T(8,128)(2,1)S(1)}, bf16[512,1024]{1,0:T(8,128)(2,1)}, u32[]{:S(2)}) copy-start(bf16[512,1024]{1,0:T(8,128)(2,1)} %param.11) | copy-start | bytes 3145732
  5.2 13.4 %collective-permute-start = (f32[8,64,448]{2,1,0:T(8,128)}, f32[8,64,448]{2,1,0:T(8,128)}, u32[]{:S(2)}, u32[]{:S(2)}) collective-permute-start(f32[8,64,448]{2,1,0:T(8,128)} %concatenate.34), channel_id=1, source_target_pairs={{0,1},{1,2},{2,3},{3,4},{4,5},{5,6},{6,7},{7,8},{8,9},{9,10},{10,1... | collective-permute-start | bytes 2752520 | tf_op jit(solution)/shard_map/ppermute | solution.py:27
  8.6 11.0 %collective-permute-start.1 = (f32[8,64,448]{2,1,0:T(8,128)}, f32[8,64,448]{2,1,0:T(8,128)}, u32[]{:S(2)}, u32[]{:S(2)}) collective-permute-start(f32[8,64,448]{2,1,0:T(8,128)} %concatenate.34), channel_id=1, source_target_pairs={{1,0},{2,1},{3,2},{4,3},{5,4},{6,5},{7,6},{8,7},{9,8},{10,9},{11,1... | collective-permute-start | bytes 2752520 | tf_op jit(solution)/shard_map/ppermute | solution.py:27
  11.0 45.2 %collective-permute-start.4 = (bf16[256,1024]{1,0:T(8,128)(2,1)}, bf16[256,1024]{1,0:T(8,128)(2,1)}, u32[]{:S(2)}, u32[]{:S(2)}) collective-permute-start(bf16[256,1024]{1,0:T(8,128)(2,1)} %get-tuple-element.39), channel_id=1, source_target_pairs={{0,4},{1,5},{2,6},{3,7},{4,0},{5,1},{6,2},{7,3},{8,12},{9,13},{10,... | collective-permute-start | bytes 1572872 | tf_op jit(solution)/shard_map/ppermute | solution.py:40
  15.8 47.9 %collective-permute-start.5 = (bf16[256,1024]{1,0:T(8,128)(2,1)}, bf16[256,1024]{1,0:T(8,128)(2,1)}, u32[]{:S(2)}, u32[]{:S(2)}) collective-permute-start(bf16[256,1024]{1,0:T(8,128)(2,1)} %get-tuple-element.39), channel_id=1, source_target_pairs={{0,8},{1,9},{2,10},{3,11},{4,12},{5,13},{6,14},{7,15},{8,0},{9,1},... | collective-permute-start | bytes 1572872 | tf_op jit(solution)/shard_map/ppermute | solution.py:40
  29.1 11.1 %copy-start.6 = (bf16[256,1024]{1,0:T(8,128)(2,1)S(1)}, bf16[256,1024]{1,0:T(8,128)(2,1)}, u32[]{:S(2)}) copy-start(bf16[256,1024]{1,0:T(8,128)(2,1)} %get-tuple-element.38) | copy-start | bytes 1572868
  29.2 26.3 %copy-start.7 = (f32[9]{0:T(128)S(1)}, f32[9]{0:T(128)}, u32[]{:S(2)}) copy-start(f32[9]{0:T(128)} %param.17) | copy-start | bytes 112
  29.8 33.9 %collective-permute-start.2 = (f32[8,64,256]{2,1,0:T(8,128)S(1)}, f32[8,64,256]{2,1,0:T(8,128)S(1)}, u32[]{:S(2)}, u32[]{:S(2)}) collective-permute-start(f32[8,64,256]{2,1,0:T(8,128)S(1)} %pad_maximum_fusion.3), channel_id=1, source_target_pairs={{0,1},{1,2},{2,3},{3,4},{4,5},{5,6},{6,7},{7,8},{8,9},{9,10},{10,1... | collective-permute-start | bytes 1572872 | tf_op jit(solution)/shard_map/ppermute | solution.py:27
  38.8 25.0 %collective-permute-start.3 = (f32[8,64,256]{2,1,0:T(8,128)S(1)}, f32[8,64,256]{2,1,0:T(8,128)S(1)}, u32[]{:S(2)}, u32[]{:S(2)}) collective-permute-start(f32[8,64,256]{2,1,0:T(8,128)S(1)} %pad_maximum_fusion.3), channel_id=1, source_target_pairs={{1,0},{2,1},{3,2},{4,3},{5,4},{6,5},{7,6},{8,7},{9,8},{10,9},{11,1... | collective-permute-start | bytes 1572872 | tf_op jit(solution)/shard_map/ppermute | solution.py:27
  40.2 41.6 %collective-permute-start.6 = (bf16[256,1024]{1,0:T(8,128)(2,1)S(1)}, bf16[256,1024]{1,0:T(8,128)(2,1)S(1)}, u32[]{:S(2)}, u32[]{:S(2)}) collective-permute-start(bf16[256,1024]{1,0:T(8,128)(2,1)S(1)} %copy-done.6), channel_id=1, source_target_pairs={{0,4},{1,5},{2,6},{3,7},{4,0},{5,1},{6,2},{7,3},{8,12},{9,13},{10,... | collective-permute-start | bytes 1572872 | tf_op jit(solution)/shard_map/ppermute | solution.py:40
  56.2 25.7 %collective-permute-start.7 = (bf16[256,1024]{1,0:T(8,128)(2,1)S(1)}, bf16[256,1024]{1,0:T(8,128)(2,1)S(1)}, u32[]{:S(2)}, u32[]{:S(2)}) collective-permute-start(bf16[256,1024]{1,0:T(8,128)(2,1)S(1)} %copy-done.6), channel_id=1, source_target_pairs={{0,8},{1,9},{2,10},{3,11},{4,12},{5,13},{6,14},{7,15},{8,0},{9,1},... | collective-permute-start | bytes 1572872 | tf_op jit(solution)/shard_map/ppermute | solution.py:40
  63.7 23.4 %collective-permute-start.8 = (bf16[512,1024]{1,0:T(8,128)(2,1)S(1)}, bf16[512,1024]{1,0:T(8,128)(2,1)S(1)}, u32[]{:S(2)}, u32[]{:S(2)}) collective-permute-start(bf16[512,1024]{1,0:T(8,128)(2,1)S(1)} %copy-done.3), channel_id=1, source_target_pairs={{0,2},{1,3},{2,0},{3,1},{4,6},{5,7},{6,4},{7,5},{8,10},{9,11},{10,... | collective-permute-start | bytes 3145736 | tf_op jit(solution)/shard_map/ppermute | solution.py:40
  69.1 1.0 copy-start.5
  87.1 22.8 %slice-start = ((s8[6291456]{0:T(1024)(128)(4,1)}), s8[4194304]{0:T(1024)(128)(4,1)S(1)}, s32[]{:S(2)}) async-start(s8[6291456]{0:T(1024)(128)(4,1)} %bitcast.276), calls=%async_computation | async-start | bytes 8388608
  87.6 14.3 %collective-permute-start.9 = (bf16[128,1024]{1,0:T(8,128)(2,1)S(1)}, bf16[128,1024]{1,0:T(8,128)(2,1)S(1)}, u32[]{:S(2)}, u32[]{:S(2)}) collective-permute-start(bf16[128,1024]{1,0:T(8,128)(2,1)S(1)} %get-tuple-element.37), channel_id=1, source_target_pairs={{0,1},{1,2},{2,3},{3,4},{4,5},{5,6},{6,7},{7,8},{8,9},{9,10},{10,1... | collective-permute-start | bytes 786440 | tf_op jit(solution)/shard_map/ppermute | solution.py:27
  89.0 12.9 %collective-permute-start.10 = (bf16[128,1024]{1,0:T(8,128)(2,1)S(1)}, bf16[128,1024]{1,0:T(8,128)(2,1)S(1)}, u32[]{:S(2)}, u32[]{:S(2)}) collective-permute-start(bf16[128,1024]{1,0:T(8,128)(2,1)S(1)} %get-tuple-element.36), channel_id=1, source_target_pairs={{1,0},{2,1},{3,2},{4,3},{5,4},{6,5},{7,6},{8,7},{9,8},{10,9},{11,1... | collective-permute-start | bytes 786440 | tf_op jit(solution)/shard_map/ppermute | solution.py:27
  90.5 12.2 %collective-permute-start.11 = (bf16[512,128]{1,0:T(8,128)(2,1)S(1)}, bf16[512,128]{1,0:T(8,128)(2,1)S(1)}, u32[]{:S(2)}, u32[]{:S(2)}) collective-permute-start(bf16[512,128]{1,0:T(8,128)(2,1)S(1)} %bitcast.273), channel_id=1, source_target_pairs={{0,2},{1,3},{2,0},{3,1},{4,6},{5,7},{6,4},{7,5},{8,10},{9,11},{10,... | collective-permute-start | bytes 393224 | tf_op jit(solution)/shard_map/ppermute | solution.py:40
  96.2 10.8 %collective-permute-start.12 = (bf16[512,128]{1,0:T(8,128)(2,1)S(1)}, bf16[512,128]{1,0:T(8,128)(2,1)S(1)}, u32[]{:S(2)}, u32[]{:S(2)}) collective-permute-start(bf16[512,128]{1,0:T(8,128)(2,1)S(1)} %bitcast.274), channel_id=1, source_target_pairs={{0,4},{1,5},{2,6},{3,7},{4,0},{5,1},{6,2},{7,3},{8,12},{9,13},{10,... | collective-permute-start | bytes 393224 | tf_op jit(solution)/shard_map/ppermute | solution.py:40
  97.4 11.0 %collective-permute-start.13 = (bf16[512,128]{1,0:T(8,128)(2,1)S(1)}, bf16[512,128]{1,0:T(8,128)(2,1)S(1)}, u32[]{:S(2)}, u32[]{:S(2)}) collective-permute-start(bf16[512,128]{1,0:T(8,128)(2,1)S(1)} %bitcast.275), channel_id=1, source_target_pairs={{0,8},{1,9},{2,10},{3,11},{4,12},{5,13},{6,14},{7,15},{8,0},{9,1},... | collective-permute-start | bytes 393224 | tf_op jit(solution)/shard_map/ppermute | solution.py:40
  102.0 7.9 %slice-start.1 = ((s8[6291456]{0:T(1024)(128)(4,1)}), s8[2097152]{0:T(1024)(128)(4,1)S(1)}, s32[]{:S(2)}) async-start(s8[6291456]{0:T(1024)(128)(4,1)} %bitcast.276), calls=%async_computation.1 | async-start | bytes 4194304
  120.2 3.6 %copy-start.2 = (bf16[2304,2048]{1,0:T(8,128)(2,1)}, bf16[2304,2048]{1,0:T(8,128)(2,1)S(1)}, u32[]{:S(2)}) copy-start(bf16[2304,2048]{1,0:T(8,128)(2,1)S(1)} %convolution_convert_fusion.refs_0_.refs_1_.refs_2_.refs_3_.refs_5_.refs_6_.refs_7_) | copy-start | bytes 28311556
  123.8 0.7 copy-start.8
  123.8 0.8 copy-start.9
  123.8 0.9 copy-start.10
  124.0 5.3 %collective-permute-start.14 = (bf16[512,2048]{1,0:T(8,128)(2,1)S(1)}, bf16[512,2048]{1,0:T(8,128)(2,1)}, u32[]{:S(2)}, u32[]{:S(2)}) collective-permute-start(bf16[512,2048]{1,0:T(8,128)(2,1)S(1)} %slice.409), channel_id=1, source_target_pairs={{0,1},{1,0},{2,3},{3,2},{4,5},{5,4},{6,7},{7,6},{8,9},{9,8},{10,11... | collective-permute-start | bytes 6291464 | tf_op jit(solution)/shard_map/ppermute | solution.py:40
  129.2 18.9 %copy-start.1 = (bf16[128,1024]{1,0:T(8,128)(2,1)S(1)}, bf16[128,1024]{1,0:T(8,128)(2,1)}, u32[]{:S(2)}) copy-start(bf16[128,1024]{1,0:T(8,128)(2,1)} %param.18) | copy-start | bytes 786436

commit v23 on v18

--- a/solution.py
+++ b/solution.py
@@ -77,7 +77,7 @@
         ).reshape(hi - lo, taps * BS, chans)
         return jnp.einsum(
             "wsk,wkc->wsc", bands[lo - REACH : hi - REACH], stacked,
-            precision=lax.Precision.HIGH, preferred_element_type=jnp.float32,
+            precision=lax.Precision.HIGHEST, preferred_element_type=jnp.float32,
         )
 
     own = slice(halo, halo + count)

time: 145 us -> 152 us (1.048)
  the two profiles are of different devices: /device:TPU:0 before, /device:TPU:9 now
where the time goes in v23:
time: 152 us
  starting transfers between devices  42.7 us (28%)
  matrix products  38.3 us (25%)
  waiting for transfers between devices  34.8 us (23%)
  Pallas kernels  18.9 us (12%)
  local copies, waits for them, and re-layouts  12.3 us (8%)
  other arithmetic  3.84 us (3%)
    ppermute x6, waiting for transfers between devices, shift_rows(): return lax.ppermute(x, axis, pairs)  25.3 us
    ppermute x9, starting transfers between devices, partner(): return lax.ppermute(value, axis, pairs)  24.8 us
    dot_general x8, matrix products, step(): jnp.einsum('wsk,wkc->wsc', bands[lo - REACH:hi - REACH], stacked, precisi...  22.5 us
    pallas_call x1, Pallas kernels, attend(): pl.pallas_call(attention_kernel, grid_spec=grid_spec, out_shape=jax.Shape...  18.9 us
    ppermute x6, starting transfers between devices, shift_rows(): return lax.ppermute(x, axis, pairs)  17.9 us
    dot_general x1, matrix products, on_device(): jnp.dot(all_blended, kv_weight, preferred_element_type=jnp.float32)  10.3 us
    ppermute x9, waiting for transfers between devices, partner(): return lax.ppermute(value, axis, pairs)  9.5 us
    unnamed x62, local copies, waits for them, and re-layouts  7.16 us
  transfers between devices with their start and end apart: 15, of which 5 were waited for; matrix products, arithmetic and copies ran while one was open for 21% of the time, Pallas kernels for 0%

profile of v23, /device:TPU:9, one launch (start us, length us, event | category | flops | bytes accessed | tf_op | source)
XLA Modules:
  0.0 151.8 jit_solution(8111952939027644306)
XLA Ops:
  0.0 0.8 copy.35
  1.0 1.8 %select_reduce_fusion = f32[8,5,64,64]{3,2,1,0:T(8,128)S(1)} fusion(f32[8,3,64,64]{3,2,1,0:T(8,128)} %param.13, pred[8,3,5]{2,1,0:T(4,128)(4,1)S(1)} %iota_compare_fusion), kind=kLoop, calls=%fused_computation.2 | loop fusion | flops 819200 | bytes 1048696 | tf_op jit(solution)/shard_map/reduce_sum | solution.py:61
  2.7 0.4 copy.36
  3.1 0.4 copy.37
  3.6 1.1 pad_maximum_fusion.1
  4.7 3.8 %collective-permute-start = (f32[8,64,448]{2,1,0:T(8,128)S(1)}, f32[8,64,448]{2,1,0:T(8,128)S(1)}, u32[]{:S(2)}, u32[]{:S(2)}) collective-permute-start(f32[8,64,448]{2,1,0:T(8,128)S(1)} %pad_maximum_fusion.1), channel_id=1, source_target_pairs={{0,1},{1,2},{2,3},{3,4},{4,5},{5,6},{6,7},{7,8},{8,9},{9,10},{10,1... | collective-permute-start | bytes 2752520 | tf_op jit(solution)/shard_map/ppermute | solution.py:27
  8.5 1.9 %collective-permute-start.1 = (f32[8,64,448]{2,1,0:T(8,128)S(1)}, f32[8,64,448]{2,1,0:T(8,128)S(1)}, u32[]{:S(2)}, u32[]{:S(2)}) collective-permute-start(f32[8,64,448]{2,1,0:T(8,128)S(1)} %pad_maximum_fusion.1), channel_id=1, source_target_pairs={{1,0},{2,1},{3,2},{4,3},{5,4},{6,5},{7,6},{8,7},{9,8},{10,9},{11,1... | collective-permute-start | bytes 2752520 | tf_op jit(solution)/shard_map/ppermute | solution.py:27
  10.5 0.2 collective-permute-start.4
  10.8 2.3 %collective-permute-start.5 = (bf16[256,1024]{1,0:T(8,128)(2,1)S(1)}, bf16[256,1024]{1,0:T(8,128)(2,1)S(1)}, u32[]{:S(2)}, u32[]{:S(2)}) collective-permute-start(bf16[256,1024]{1,0:T(8,128)(2,1)S(1)} %get-tuple-element.24), channel_id=1, source_target_pairs={{0,8},{1,9},{2,10},{3,11},{4,12},{5,13},{6,14},{7,15},{8,0},{9,1},... | collective-permute-start | bytes 1572872 | tf_op jit(solution)/shard_map/ppermute | solution.py:40
  13.1 12.5 %collective-permute-done = f32[8,64,448]{2,1,0:T(8,128)S(1)} collective-permute-done((f32[8,64,448]{2,1,0:T(8,128)S(1)}, f32[8,64,448]{2,1,0:T(8,128)S(1)}, u32[]{:S(2)}, u32[]{:S(2)}) %collective-permute-start) | collective-permute-done | bytes 917536 | tf_op jit(solution)/shard_map/ppermute | solution.py:27
  25.6 7.5 %collective-permute-done.1 = f32[8,64,448]{2,1,0:T(8,128)S(1)} collective-permute-done((f32[8,64,448]{2,1,0:T(8,128)S(1)}, f32[8,64,448]{2,1,0:T(8,128)S(1)}, u32[]{:S(2)}, u32[]{:S(2)}) %collective-permute-start.1) | collective-permute-done | bytes 917536 | tf_op jit(solution)/shard_map/ppermute | solution.py:27
  33.5 0.4 copy.39
  34.0 2.5 %fusion.69 = f32[20,64,128]{2,1,0:T(8,128)S(1)} fusion(f32[20,320,128]{2,1,0:T(8,128)S(1)} %bitcast.203, f32[6,64,320]{2,1,0:T(8,128)S(1)} %slice.306, f32[8,64,320]{2,1,0:T(8,128)S(1)} %copy.37, f32[6,64,320]{2,1,0:T(8,128)S(1)} %slice.305), kind=kOutput, calls=%fused_computation.133 | convolution fusion | flops 629964800 | bytes 5570560 | tf_op jit(solution)/shard_map/wsk,wkc->wsc/dot_general | solution.py:78
  36.8 0.2 copy.40
  37.0 2.1 %fusion.21 = f32[16,64,128]{2,1,0:T(8,128)S(1)} fusion(f32[16,320,128]{2,1,0:T(8,128)S(1)} %bitcast.207, f32[24,64,128]{2,1,0:T(8,128)S(1)} %pad_maximum_fusion.2, f32[6,64,320]{2,1,0:T(8,128)S(1)} %slice.306, f32[8,64,320]{2,1,0:T(8,128)S(1)} %copy.37, f32[6,64,320]{2,1,0:T(8,128)S(1)} %slice.305), kind=kOutput, calls=%fused_computation.29 | convolution fusion | flops 504397824 | bytes 5308416 | tf_op jit(solution)/shard_map/wsk,wkc->wsc/dot_general | solution.py:78
  39.4 1.6 %fusion.15 = f32[12,64,128]{2,1,0:T(8,128)S(1)} fusion(f32[12,320,128]{2,1,0:T(8,128)S(1)} %bitcast.213, f32[20,64,128]{2,1,0:T(8,128)S(1)} %fusion.69, f32[6,64,320]{2,1,0:T(8,128)S(1)} %slice.306, f32[8,64,320]{2,1,0:T(8,128)S(1)} %copy.37, f32[6,64,320]{2,1,0:T(8,128)S(1)} %slice.305), kind=kOutput, calls=%fused_computation.19 | convolution fusion | flops 378503168 | bytes 4390912 | tf_op jit(solution)/shard_map/wsk,wkc->wsc/dot_general | solution.py:78
  41.1 0.1 copy.42
  41.3 2.2 %fusion.18 = f32[8,64,128]{2,1,0:T(8,128)S(1)} fusion(f32[8,64,320]{1,2,0:T(8,128)S(1)} %bitcast.200, f32[8,320,128]{2,1,0:T(8,128)S(1)} %bitcast.205, f32[16,64,128]{2,1,0:T(8,128)S(1)} %fusion.21), kind=kOutput, calls=%fused_computation.26 | convolution fusion | flops 251789312 | bytes 2490368 | tf_op jit(solution)/shard_map/wsk,wkc->wsc/dot_general | solution.py:78
  43.6 1.9 %collective-permute-start.2 = (f32[8,64,256]{2,1,0:T(8,128)S(1)}, f32[8,64,256]{2,1,0:T(8,128)S(1)}, u32[]{:S(2)}, u32[]{:S(2)}) collective-permute-start(f32[8,64,256]{2,1,0:T(8,128)S(1)} %pad_maximum_fusion.4), channel_id=1, source_target_pairs={{0,1},{1,2},{2,3},{3,4},{4,5},{5,6},{6,7},{7,8},{8,9},{9,10},{10,1... | collective-permute-start | bytes 1572872 | tf_op jit(solution)/shard_map/ppermute | solution.py:27
  45.5 3.1 %collective-permute-start.3 = (f32[8,64,256]{2,1,0:T(8,128)S(1)}, f32[8,64,256]{2,1,0:T(8,128)S(1)}, u32[]{:S(2)}, u32[]{:S(2)}) collective-permute-start(f32[8,64,256]{2,1,0:T(8,128)S(1)} %pad_maximum_fusion.4), channel_id=1, source_target_pairs={{1,0},{2,1},{3,2},{4,3},{5,4},{6,5},{7,6},{8,7},{9,8},{10,9},{11,1... | collective-permute-start | bytes 1572872 | tf_op jit(solution)/shard_map/ppermute | solution.py:27
  48.8 0.7 fusion.72
  49.4 6.5 %collective-permute-start.7 = (bf16[256,1024]{1,0:T(8,128)(2,1)S(1)}, bf16[256,1024]{1,0:T(8,128)(2,1)S(1)}, u32[]{:S(2)}, u32[]{:S(2)}) collective-permute-start(bf16[256,1024]{1,0:T(8,128)(2,1)S(1)} %get-tuple-element.23), channel_id=1, source_target_pairs={{0,8},{1,9},{2,10},{3,11},{4,12},{5,13},{6,14},{7,15},{8,0},{9,1},... | collective-permute-start | bytes 1572872 | tf_op jit(solution)/shard_map/ppermute | solution.py:40
  55.9 2.5 %collective-permute-start.8 = (bf16[512,1024]{1,0:T(8,128)(2,1)S(1)}, bf16[512,1024]{1,0:T(8,128)(2,1)S(1)}, u32[]{:S(2)}, u32[]{:S(2)}) collective-permute-start(bf16[512,1024]{1,0:T(8,128)(2,1)S(1)} %copy-done.3), channel_id=1, source_target_pairs={{0,2},{1,3},{2,0},{3,1},{4,6},{5,7},{6,4},{7,5},{8,10},{9,11},{10,... | collective-permute-start | bytes 3145736 | tf_op jit(solution)/shard_map/ppermute | solution.py:40
  58.4 5.4 %collective-permute-done.3 = f32[8,64,256]{2,1,0:T(8,128)S(1)} collective-permute-done((f32[8,64,256]{2,1,0:T(8,128)S(1)}, f32[8,64,256]{2,1,0:T(8,128)S(1)}, u32[]{:S(2)}, u32[]{:S(2)}) %collective-permute-start.3) | collective-permute-done | bytes 524320 | tf_op jit(solution)/shard_map/ppermute | solution.py:27
  64.2 0.2 copy.44
  64.5 2.5 %fusion.14 = f32[20,64,128]{2,1,0:T(8,128)S(1)} fusion(f32[20,320,128]{2,1,0:T(8,128)S(1)} %bitcast.202, f32[6,64,128]{2,1,0:T(8,128)S(1)} %slice.276, f32[8,64,128]{2,1,0:T(8,128)S(1)} %slice.328, f32[6,64,128]{2,1,0:T(8,128)S(1)} %slice.275, f32[6,64,320]{2,1,0:T(8,128)S(1)} %slice.306, f32[8,64,320]{2,1,0:T(8,128)S(1)} %copy.37, ...), kind=kOutput, calls=%fused_computation.16 | convolution fusion | flops 630620160 | bytes 6225920 | tf_op jit(solution)/shard_map/wsk,wkc->wsc/dot_general | solution.py:78
  67.2 0.2 copy.45
  67.4 2.1 %fusion.22 = f32[16,64,128]{2,1,0:T(8,128)S(1)} fusion(f32[16,320,128]{2,1,0:T(8,128)S(1)} %bitcast.208, f32[24,64,128]{2,1,0:T(8,128)S(1)} %pad_maximum_fusion.3, f32[6,64,320]{2,1,0:T(8,128)S(1)} %slice.306, f32[8,64,320]{2,1,0:T(8,128)S(1)} %copy.37, f32[6,64,320]{2,1,0:T(8,128)S(1)} %slice.305), kind=kOutput, calls=%fused_computation.30 | convolution fusion | flops 504397824 | bytes 5308416 | tf_op jit(solution)/shard_map/wsk,wkc->wsc/dot_general | solution.py:78
  69.8 1.6 %fusion.16 = f32[12,64,128]{2,1,0:T(8,128)S(1)} fusion(f32[12,320,128]{2,1,0:T(8,128)S(1)} %bitcast.212, f32[20,64,128]{2,1,0:T(8,128)S(1)} %fusion.14, f32[6,64,320]{2,1,0:T(8,128)S(1)} %slice.306, f32[8,64,320]{2,1,0:T(8,128)S(1)} %copy.37, f32[6,64,320]{2,1,0:T(8,128)S(1)} %slice.305), kind=kOutput, calls=%fused_computation.20 | convolution fusion | flops 378503168 | bytes 4390912 | tf_op jit(solution)/shard_map/wsk,wkc->wsc/dot_general | solution.py:78
  71.6 7.9 %fusion.20 = bf16[8,64,128]{2,1,0:T(8,128)(2,1)S(1)} fusion(f32[8,64,320]{1,2,0:T(8,128)S(1)} %bitcast.201, f32[8,320,128]{2,1,0:T(8,128)S(1)} %bitcast.206, f32[20,64,128]{2,1,0:T(8,128)S(1)} %fusion.14, f32[20,64,128]{2,1,0:T(8,128)S(1)} %fusion.69, f32[16,64,128]{2,1,0:T(8,128)S(1)} %fusion.22, f32[8,64,128]{2,1,0:T(8,128)S(1)} %fusion.18, ...), kind=kOutput, calls=%fused_computation.28 | convolution fusion | flops 252968960 | bytes 4194340 | tf_op jit(solution)/shard_map/wsk,wkc->wsc/dot_general | solution.py:78
  79.5 3.9 %collective-permute-done.8 = bf16[512,1024]{1,0:T(8,128)(2,1)S(1)} collective-permute-done((bf16[512,1024]{1,0:T(8,128)(2,1)S(1)}, bf16[512,1024]{1,0:T(8,128)(2,1)S(1)}, u32[]{:S(2)}, u32[]{:S(2)}) %collective-permute-start.8) | collective-permute-done | bytes 1048608 | tf_op jit(solution)/shard_map/ppermute | solution.py:40
  83.5 0.4 add_convert_fusion.3
  83.9 4.9 %collective-permute-start.9 = (bf16[128,1024]{1,0:T(8,128)(2,1)S(1)}, bf16[128,1024]{1,0:T(8,128)(2,1)S(1)}, u32[]{:S(2)}, u32[]{:S(2)}) collective-permute-start(bf16[128,1024]{1,0:T(8,128)(2,1)S(1)} %get-tuple-element.22), channel_id=1, source_target_pairs={{0,1},{1,2},{2,3},{3,4},{4,5},{5,6},{6,7},{7,8},{8,9},{9,10},{10,1... | collective-permute-start | bytes 786440 | tf_op jit(solution)/shard_map/ppermute | solution.py:27
  88.9 2.1 %collective-permute-start.10 = (bf16[128,1024]{1,0:T(8,128)(2,1)S(1)}, bf16[128,1024]{1,0:T(8,128)(2,1)S(1)}, u32[]{:S(2)}, u32[]{:S(2)}) collective-permute-start(bf16[128,1024]{1,0:T(8,128)(2,1)S(1)} %get-tuple-element.21), channel_id=1, source_target_pairs={{1,0},{2,1},{3,2},{4,3},{5,4},{6,5},{7,6},{8,7},{9,8},{10,9},{11,1... | collective-permute-start | bytes 786440 | tf_op jit(solution)/shard_map/ppermute | solution.py:27
  91.0 2.0 %collective-permute-start.11 = (bf16[512,128]{1,0:T(8,128)(2,1)S(1)}, bf16[512,128]{1,0:T(8,128)(2,1)S(1)}, u32[]{:S(2)}, u32[]{:S(2)}) collective-permute-start(bf16[512,128]{1,0:T(8,128)(2,1)S(1)} %bitcast.215), channel_id=1, source_target_pairs={{0,2},{1,3},{2,0},{3,1},{4,6},{5,7},{6,4},{7,5},{8,10},{9,11},{10,... | collective-permute-start | bytes 393224 | tf_op jit(solution)/shard_map/ppermute | solution.py:40
  93.0 7.8 %collective-permute-start.13 = (bf16[512,128]{1,0:T(8,128)(2,1)S(1)}, bf16[512,128]{1,0:T(8,128)(2,1)S(1)}, u32[]{:S(2)}, u32[]{:S(2)}) collective-permute-start(bf16[512,128]{1,0:T(8,128)(2,1)S(1)} %bitcast.217), channel_id=1, source_target_pairs={{0,8},{1,9},{2,10},{3,11},{4,12},{5,13},{6,14},{7,15},{8,0},{9,1},... | collective-permute-start | bytes 393224 | tf_op jit(solution)/shard_map/ppermute | solution.py:40
  101.0 0.4 fusion.23
  101.4 0.4 fusion.3
  101.8 5.5 %collective-permute-done.13 = bf16[512,128]{1,0:T(8,128)(2,1)S(1)} collective-permute-done((bf16[512,128]{1,0:T(8,128)(2,1)S(1)}, bf16[512,128]{1,0:T(8,128)(2,1)S(1)}, u32[]{:S(2)}, u32[]{:S(2)}) %collective-permute-start.13) | collective-permute-done | bytes 131104 | tf_op jit(solution)/shard_map/ppermute | solution.py:40
  107.4 0.4 fusion.4
  107.8 10.3 %convolution_convert_fusion.refs_0_.refs_1_.refs_2_.refs_3_.refs_5_.refs_6_.refs_7_ = bf16[2304,2048]{1,0:T(8,128)(2,1)S(1)} fusion(bf16[2304,1024]{1,0:T(8,128)(2,1)S(1)} %fusion.4, bf16[1024,3072]{1,0:T(8,128)(2,1)S(1)} %bitcast.219), kind=kOutput, calls=%fused_computation | convolution fusion | flops 9668395008 | bytes 18350080 | tf_op jit(solution)/shard_map/dot_general | solution.py:222
  118.1 3.7 %copy-done.2 = bf16[2304,2048]{1,0:T(8,128)(2,1)} copy-done((bf16[2304,2048]{1,0:T(8,128)(2,1)}, bf16[2304,2048]{1,0:T(8,128)(2,1)S(1)}, u32[]{:S(2)}) %copy-start.2) | copy-done | bytes 9437208
  121.8 1.4 slice.359
  123.2 3.5 %collective-permute-start.14 = (bf16[512,2048]{1,0:T(8,128)(2,1)}, bf16[512,2048]{1,0:T(8,128)(2,1)S(1)}, u32[]{:S(2)}, u32[]{:S(2)}) collective-permute-start(bf16[512,2048]{1,0:T(8,128)(2,1)} %slice.359), channel_id=1, source_target_pairs={{0,1},{1,0},{2,3},{3,2},{4,5},{5,4},{6,7},{7,6},{8,9},{9,8},{10,11... | collective-permute-start | bytes 6291464 | tf_op jit(solution)/shard_map/ppermute | solution.py:40
  126.9 0.7 pad_add_fusion.table_ref
  127.6 3.9 %fusion.11.q_ref = bf16[1024,512]{1,0:T(8,128)(2,1)} fusion(bf16[512,1024]{1,0:T(8,128)(2,1)S(1)} %add_convert_fusion.3, bf16[1024,3072]{1,0:T(8,128)(2,1)} %param.19), kind=kOutput, calls=%fused_computation.14 | convolution fusion | flops 1074790400 | bytes 4194304 | tf_op jit(solution)/shard_map/dot_general | solution.py:214
  131.4 1.3 copy-done.5
  132.8 18.9 %shard_map.109 = bf16[512,1024]{1,0:T(8,128)(2,1)} custom-call(s32[8,8]{1,0:T(8,128)} %pad_add_fusion.table_ref, bf16[1024,512]{1,0:T(8,128)(2,1)} %fusion.11.q_ref, bf16[2304,2048]{1,0:T(8,128)(2,1)} %copy-done.2, bf16[2304,2048]{1,0:T(8,128)(2,1)} %copy-done.2, bf16[2304,2048]{1,0:T(8,128)(2,1)} %copy-done.2, bf16[2304,2048]{1,0:T(8,128)(2,1)} %copy-done.2, ...), custom_call_target="tpu_custom_call" | custom-call | tf_op jit(solution)/shard_map/pallas_call | solution.py:169
  (103 shorter events, 2.8 us)
Async XLA Ops:
  0.0 83.5 %copy-start = (bf16[128,1024]{1,0:T(8,128)(2,1)S(1)}, bf16[128,1024]{1,0:T(8,128)(2,1)}, u32[]{:S(2)}) copy-start(bf16[128,1024]{1,0:T(8,128)(2,1)} %param.18) | copy-start | bytes 786436
  3.1 7.3 %copy-start.3 = (bf16[512,1024]{1,0:T(8,128)(2,1)S(1)}, bf16[512,1024]{1,0:T(8,128)(2,1)}, u32[]{:S(2)}) copy-start(bf16[512,1024]{1,0:T(8,128)(2,1)} %param.11) | copy-start | bytes 3145732
  4.7 28.4 %copy-start.4 = (f32[512,128]{1,0:T(8,128)S(1)}, f32[512,128]{1,0:T(8,128)}, u32[]{:S(2)}) copy-start(f32[512,128]{1,0:T(8,128)} %param.12) | copy-start | bytes 786436
  4.7 20.9 %collective-permute-start = (f32[8,64,448]{2,1,0:T(8,128)S(1)}, f32[8,64,448]{2,1,0:T(8,128)S(1)}, u32[]{:S(2)}, u32[]{:S(2)}) collective-permute-start(f32[8,64,448]{2,1,0:T(8,128)S(1)} %pad_maximum_fusion.1), channel_id=1, source_target_pairs={{0,1},{1,2},{2,3},{3,4},{4,5},{5,6},{6,7},{7,8},{8,9},{9,10},{10,1... | collective-permute-start | bytes 2752520 | tf_op jit(solution)/shard_map/ppermute | solution.py:27
  8.5 24.6 %collective-permute-start.1 = (f32[8,64,448]{2,1,0:T(8,128)S(1)}, f32[8,64,448]{2,1,0:T(8,128)S(1)}, u32[]{:S(2)}, u32[]{:S(2)}) collective-permute-start(f32[8,64,448]{2,1,0:T(8,128)S(1)} %pad_maximum_fusion.1), channel_id=1, source_target_pairs={{1,0},{2,1},{3,2},{4,3},{5,4},{6,5},{7,6},{8,7},{9,8},{10,9},{11,1... | collective-permute-start | bytes 2752520 | tf_op jit(solution)/shard_map/ppermute | solution.py:27
  10.5 38.9 %collective-permute-start.4 = (bf16[256,1024]{1,0:T(8,128)(2,1)S(1)}, bf16[256,1024]{1,0:T(8,128)(2,1)S(1)}, u32[]{:S(2)}, u32[]{:S(2)}) collective-permute-start(bf16[256,1024]{1,0:T(8,128)(2,1)S(1)} %get-tuple-element.24), channel_id=1, source_target_pairs={{0,4},{1,5},{2,6},{3,7},{4,0},{5,1},{6,2},{7,3},{8,12},{9,13},{10,... | collective-permute-start | bytes 1572872 | tf_op jit(solution)/shard_map/ppermute | solution.py:40
  10.8 45.1 %collective-permute-start.5 = (bf16[256,1024]{1,0:T(8,128)(2,1)S(1)}, bf16[256,1024]{1,0:T(8,128)(2,1)S(1)}, u32[]{:S(2)}, u32[]{:S(2)}) collective-permute-start(bf16[256,1024]{1,0:T(8,128)(2,1)S(1)} %get-tuple-element.24), channel_id=1, source_target_pairs={{0,8},{1,9},{2,10},{3,11},{4,12},{5,13},{6,14},{7,15},{8,0},{9,1},... | collective-permute-start | bytes 1572872 | tf_op jit(solution)/shard_map/ppermute | solution.py:40
  41.3 7.5 %copy-start.6 = (f32[9]{0:T(128)S(1)}, f32[9]{0:T(128)}, u32[]{:S(2)}) copy-start(f32[9]{0:T(128)} %param.17) | copy-start | bytes 112
  43.6 14.8 %collective-permute-start.2 = (f32[8,64,256]{2,1,0:T(8,128)S(1)}, f32[8,64,256]{2,1,0:T(8,128)S(1)}, u32[]{:S(2)}, u32[]{:S(2)}) collective-permute-start(f32[8,64,256]{2,1,0:T(8,128)S(1)} %pad_maximum_fusion.4), channel_id=1, source_target_pairs={{0,1},{1,2},{2,3},{3,4},{4,5},{5,6},{6,7},{7,8},{8,9},{9,10},{10,1... | collective-permute-start | bytes 1572872 | tf_op jit(solution)/shard_map/ppermute | solution.py:27
  45.5 18.3 %collective-permute-start.3 = (f32[8,64,256]{2,1,0:T(8,128)S(1)}, f32[8,64,256]{2,1,0:T(8,128)S(1)}, u32[]{:S(2)}, u32[]{:S(2)}) collective-permute-start(f32[8,64,256]{2,1,0:T(8,128)S(1)} %pad_maximum_fusion.4), channel_id=1, source_target_pairs={{1,0},{2,1},{3,2},{4,3},{5,4},{6,5},{7,6},{8,7},{9,8},{10,9},{11,1... | collective-permute-start | bytes 1572872 | tf_op jit(solution)/shard_map/ppermute | solution.py:27
  48.7 30.8 %collective-permute-start.6 = (bf16[256,1024]{1,0:T(8,128)(2,1)S(1)}, bf16[256,1024]{1,0:T(8,128)(2,1)S(1)}, u32[]{:S(2)}, u32[]{:S(2)}) collective-permute-start(bf16[256,1024]{1,0:T(8,128)(2,1)S(1)} %get-tuple-element.23), channel_id=1, source_target_pairs={{0,4},{1,5},{2,6},{3,7},{4,0},{5,1},{6,2},{7,3},{8,12},{9,13},{10,... | collective-permute-start | bytes 1572872 | tf_op jit(solution)/shard_map/ppermute | solution.py:40
  49.4 30.1 %collective-permute-start.7 = (bf16[256,1024]{1,0:T(8,128)(2,1)S(1)}, bf16[256,1024]{1,0:T(8,128)(2,1)S(1)}, u32[]{:S(2)}, u32[]{:S(2)}) collective-permute-start(bf16[256,1024]{1,0:T(8,128)(2,1)S(1)} %get-tuple-element.23), channel_id=1, source_target_pairs={{0,8},{1,9},{2,10},{3,11},{4,12},{5,13},{6,14},{7,15},{8,0},{9,1},... | collective-permute-start | bytes 1572872 | tf_op jit(solution)/shard_map/ppermute | solution.py:40
  55.9 27.6 %collective-permute-start.8 = (bf16[512,1024]{1,0:T(8,128)(2,1)S(1)}, bf16[512,1024]{1,0:T(8,128)(2,1)S(1)}, u32[]{:S(2)}, u32[]{:S(2)}) collective-permute-start(bf16[512,1024]{1,0:T(8,128)(2,1)S(1)} %copy-done.3), channel_id=1, source_target_pairs={{0,2},{1,3},{2,0},{3,1},{4,6},{5,7},{6,4},{7,5},{8,10},{9,11},{10,... | collective-permute-start | bytes 3145736 | tf_op jit(solution)/shard_map/ppermute | solution.py:40
  83.5 24.3 %slice-start = ((s8[6291456]{0:T(1024)(128)(4,1)}), s8[4194304]{0:T(1024)(128)(4,1)S(1)}, s32[]{:S(2)}) async-start(s8[6291456]{0:T(1024)(128)(4,1)} %bitcast.218), calls=%async_computation | async-start | bytes 8388608
  83.9 16.9 %collective-permute-start.9 = (bf16[128,1024]{1,0:T(8,128)(2,1)S(1)}, bf16[128,1024]{1,0:T(8,128)(2,1)S(1)}, u32[]{:S(2)}, u32[]{:S(2)}) collective-permute-start(bf16[128,1024]{1,0:T(8,128)(2,1)S(1)} %get-tuple-element.22), channel_id=1, source_target_pairs={{0,1},{1,2},{2,3},{3,4},{4,5},{5,6},{6,7},{7,8},{8,9},{9,10},{10,1... | collective-permute-start | bytes 786440 | tf_op jit(solution)/shard_map/ppermute | solution.py:27
  88.9 12.0 %collective-permute-start.10 = (bf16[128,1024]{1,0:T(8,128)(2,1)S(1)}, bf16[128,1024]{1,0:T(8,128)(2,1)S(1)}, u32[]{:S(2)}, u32[]{:S(2)}) collective-permute-start(bf16[128,1024]{1,0:T(8,128)(2,1)S(1)} %get-tuple-element.21), channel_id=1, source_target_pairs={{1,0},{2,1},{3,2},{4,3},{5,4},{6,5},{7,6},{8,7},{9,8},{10,9},{11,1... | collective-permute-start | bytes 786440 | tf_op jit(solution)/shard_map/ppermute | solution.py:27
  91.0 9.9 %collective-permute-start.11 = (bf16[512,128]{1,0:T(8,128)(2,1)S(1)}, bf16[512,128]{1,0:T(8,128)(2,1)S(1)}, u32[]{:S(2)}, u32[]{:S(2)}) collective-permute-start(bf16[512,128]{1,0:T(8,128)(2,1)S(1)} %bitcast.215), channel_id=1, source_target_pairs={{0,2},{1,3},{2,0},{3,1},{4,6},{5,7},{6,4},{7,5},{8,10},{9,11},{10,... | collective-permute-start | bytes 393224 | tf_op jit(solution)/shard_map/ppermute | solution.py:40
  93.0 8.4 %collective-permute-start.12 = (bf16[512,128]{1,0:T(8,128)(2,1)S(1)}, bf16[512,128]{1,0:T(8,128)(2,1)S(1)}, u32[]{:S(2)}, u32[]{:S(2)}) collective-permute-start(bf16[512,128]{1,0:T(8,128)(2,1)S(1)} %bitcast.216), channel_id=1, source_target_pairs={{0,4},{1,5},{2,6},{3,7},{4,0},{5,1},{6,2},{7,3},{8,12},{9,13},{10,... | collective-permute-start | bytes 393224 | tf_op jit(solution)/shard_map/ppermute | solution.py:40
  93.0 14.4 %collective-permute-start.13 = (bf16[512,128]{1,0:T(8,128)(2,1)S(1)}, bf16[512,128]{1,0:T(8,128)(2,1)S(1)}, u32[]{:S(2)}, u32[]{:S(2)}) collective-permute-start(bf16[512,128]{1,0:T(8,128)(2,1)S(1)} %bitcast.217), channel_id=1, source_target_pairs={{0,8},{1,9},{2,10},{3,11},{4,12},{5,13},{6,14},{7,15},{8,0},{9,1},... | collective-permute-start | bytes 393224 | tf_op jit(solution)/shard_map/ppermute | solution.py:40
  100.9 6.9 %slice-start.1 = ((s8[6291456]{0:T(1024)(128)(4,1)}), s8[2097152]{0:T(1024)(128)(4,1)S(1)}, s32[]{:S(2)}) async-start(s8[6291456]{0:T(1024)(128)(4,1)} %bitcast.218), calls=%async_computation.1 | async-start | bytes 4194304
  118.1 3.7 %copy-start.2 = (bf16[2304,2048]{1,0:T(8,128)(2,1)}, bf16[2304,2048]{1,0:T(8,128)(2,1)S(1)}, u32[]{:S(2)}) copy-start(bf16[2304,2048]{1,0:T(8,128)(2,1)S(1)} %convolution_convert_fusion.refs_0_.refs_1_.refs_2_.refs_3_.refs_5_.refs_6_.refs_7_) | copy-start | bytes 28311556
  121.8 4.9 %copy-start.7 = (s32[8,3]{0,1:T(4,128)S(1)}, s32[8,3]{0,1:T(4,128)}, u32[]{:S(2)}) copy-start(s32[8,3]{0,1:T(4,128)} %param.15) | copy-start | bytes 292
  121.8 5.0 %copy-start.8 = (s32[8,4]{0,1:T(4,128)S(1)}, s32[8,4]{0,1:T(4,128)}, u32[]{:S(2)}) copy-start(s32[8,4]{0,1:T(4,128)} %param.16) | copy-start | bytes 388
  121.8 5.1 %copy-start.9 = (s32[4]{0:T(128)S(1)}, s32[4]{0:T(128)}, u32[]{:S(2)}) copy-start(s32[4]{0:T(128)} %constant.6.clone) | copy-start | bytes 52
  123.2 8.2 %collective-permute-start.14 = (bf16[512,2048]{1,0:T(8,128)(2,1)}, bf16[512,2048]{1,0:T(8,128)(2,1)S(1)}, u32[]{:S(2)}, u32[]{:S(2)}) collective-permute-start(bf16[512,2048]{1,0:T(8,128)(2,1)} %slice.359), channel_id=1, source_target_pairs={{0,1},{1,0},{2,3},{3,2},{4,5},{5,4},{6,7},{7,6},{8,9},{9,8},{10,11... | collective-permute-start | bytes 6291464 | tf_op jit(solution)/shard_map/ppermute | solution.py:40
  131.4 1.3 copy-start.5
  132.7 18.9 %copy-start.1 = (bf16[128,1024]{1,0:T(8,128)(2,1)S(1)}, bf16[128,1024]{1,0:T(8,128)(2,1)}, u32[]{:S(2)}) copy-start(bf16[128,1024]{1,0:T(8,128)(2,1)} %param.18) | copy-start | bytes 786436

commit v24 on v18

--- a/solution.py
+++ b/solution.py
@@ -87,18 +87,17 @@
     for degree in range(1, DEG + 1):
         if degree > 1 and (degree - 1) % PER_EXCHANGE == 0:
             older = prev[own.start - prev_base : own.stop - prev_base]
-            packed = jnp.concatenate([older, cur], axis=2)
-            left = shift_rows(packed[count - halo :], "seq", 1)
-            right = shift_rows(packed[:halo], "seq", -1)
+            left = shift_rows(
+                jnp.concatenate([older[count - edge :], cur[count - halo :]], axis=0), "seq", 1
+            )
+            right = shift_rows(jnp.concatenate([older[:edge], cur[:halo]], axis=0), "seq", -1)
             if later is not None:
                 left, right, later = lax.optimization_barrier((left, right, later))
                 riders = riders + (later,)
                 later = None
-            prev = jnp.concatenate(
-                [left[halo - edge :, :, :chans], older, right[:edge, :, :chans]], axis=0
-            )
+            prev = jnp.concatenate([left[:edge], older, right[:edge]], axis=0)
             prev_base = REACH
-            cur = jnp.concatenate([left[:, :, chans:], cur, right[:, :, chans:]], axis=0)
+            cur = jnp.concatenate([left[edge:], cur, right[edge:]], axis=0)
             cur_base = 0
             lo, hi = 0, width
         if degree == 1 or (degree - 1) % PER_EXCHANGE == 0:

time: 145 us -> 146 us (level)
  the two profiles are of different devices: /device:TPU:0 before, /device:TPU:13 now
where the time goes in v24:
time: 146 us; the launch traced here: 145 us
  starting transfers between devices  40.4 us (28%)
  waiting for transfers between devices  35.7 us (24%)
  matrix products  30.9 us (21%)
  Pallas kernels  18.8 us (13%)
  local copies, waits for them, and re-layouts  14.5 us (10%)
  other arithmetic  3.9 us (3%)
    ppermute x6, waiting for transfers between devices, shift_rows(): return lax.ppermute(x, axis, pairs)  22.5 us
    ppermute x9, starting transfers between devices, partner(): return lax.ppermute(value, axis, pairs)  22.5 us
    pallas_call x1, Pallas kernels, attend(): pl.pallas_call(attention_kernel, grid_spec=grid_spec, out_shape=jax.Shape...  18.8 us
    ppermute x6, starting transfers between devices, shift_rows(): return lax.ppermute(x, axis, pairs)  17.9 us
    dot_general x8, matrix products, step(): jnp.einsum('wsk,wkc->wsc', bands[lo - REACH:hi - REACH], stacked, precisi...  15 us
    ppermute x9, waiting for transfers between devices, partner(): return lax.ppermute(value, axis, pairs)  13.2 us
    dot_general x1, matrix products, on_device(): jnp.dot(all_blended, kv_weight, preferred_element_type=jnp.float32)  10.3 us
    unnamed x70, local copies, waits for them, and re-layouts  8.49 us
  transfers between devices with their start and end apart: 15, of which 6 were waited for; matrix products, arithmetic and copies ran while one was open for 17% of the time, Pallas kernels for 0%

profile of v24, /device:TPU:13, one launch (start us, length us, event | category | flops | bytes accessed | tf_op | source)
XLA Modules:
  0.0 145.2 jit_solution(7674858656778798385)
XLA Ops:
  0.0 0.8 copy.35
  1.0 1.8 %select_reduce_fusion = f32[8,5,64,64]{3,2,1,0:T(8,128)S(1)} fusion(f32[8,3,64,64]{3,2,1,0:T(8,128)} %param.13, pred[8,3,5]{2,1,0:T(4,128)(4,1)S(1)} %iota_compare_fusion), kind=kLoop, calls=%fused_computation.2 | loop fusion | flops 819200 | bytes 1048696 | tf_op jit(solution)/shard_map/reduce_sum | solution.py:61
  2.7 0.4 copy.36
  3.1 0.4 copy.37
  3.6 1.1 pad_maximum_fusion.1
  4.7 3.8 %collective-permute-start = (f32[8,64,448]{2,1,0:T(8,128)S(1)}, f32[8,64,448]{2,1,0:T(8,128)S(1)}, u32[]{:S(2)}, u32[]{:S(2)}) collective-permute-start(f32[8,64,448]{2,1,0:T(8,128)S(1)} %pad_maximum_fusion.1), channel_id=1, source_target_pairs={{0,1},{1,2},{2,3},{3,4},{4,5},{5,6},{6,7},{7,8},{8,9},{9,10},{10,1... | collective-permute-start | bytes 2752520 | tf_op jit(solution)/shard_map/ppermute | solution.py:27
  8.5 1.9 %collective-permute-start.1 = (f32[8,64,448]{2,1,0:T(8,128)S(1)}, f32[8,64,448]{2,1,0:T(8,128)S(1)}, u32[]{:S(2)}, u32[]{:S(2)}) collective-permute-start(f32[8,64,448]{2,1,0:T(8,128)S(1)} %pad_maximum_fusion.1), channel_id=1, source_target_pairs={{1,0},{2,1},{3,2},{4,3},{5,4},{6,5},{7,6},{8,7},{9,8},{10,9},{11,1... | collective-permute-start | bytes 2752520 | tf_op jit(solution)/shard_map/ppermute | solution.py:27
  10.5 0.2 collective-permute-start.4
  10.8 2.3 %collective-permute-start.5 = (bf16[256,1024]{1,0:T(8,128)(2,1)S(1)}, bf16[256,1024]{1,0:T(8,128)(2,1)S(1)}, u32[]{:S(2)}, u32[]{:S(2)}) collective-permute-start(bf16[256,1024]{1,0:T(8,128)(2,1)S(1)} %get-tuple-element.24), channel_id=1, source_target_pairs={{0,8},{1,9},{2,10},{3,11},{4,12},{5,13},{6,14},{7,15},{8,0},{9,1},... | collective-permute-start | bytes 1572872 | tf_op jit(solution)/shard_map/ppermute | solution.py:40
  13.1 12.5 %collective-permute-done = f32[8,64,448]{2,1,0:T(8,128)S(1)} collective-permute-done((f32[8,64,448]{2,1,0:T(8,128)S(1)}, f32[8,64,448]{2,1,0:T(8,128)S(1)}, u32[]{:S(2)}, u32[]{:S(2)}) %collective-permute-start) | collective-permute-done | bytes 917536 | tf_op jit(solution)/shard_map/ppermute | solution.py:27
  25.6 7.5 %collective-permute-done.1 = f32[8,64,448]{2,1,0:T(8,128)S(1)} collective-permute-done((f32[8,64,448]{2,1,0:T(8,128)S(1)}, f32[8,64,448]{2,1,0:T(8,128)S(1)}, u32[]{:S(2)}, u32[]{:S(2)}) %collective-permute-start.1) | collective-permute-done | bytes 917536 | tf_op jit(solution)/shard_map/ppermute | solution.py:27
  33.5 0.4 copy.39
  34.0 1.3 fusion.69
  35.8 1.2 fusion.21
  37.4 1.0 fusion.15
  38.7 1.2 fusion.18
  40.0 1.9 %collective-permute-start.2 = (f32[14,64,128]{2,1,0:T(8,128)S(1)}, f32[14,64,128]{2,1,0:T(8,128)S(1)}, u32[]{:S(2)}, u32[]{:S(2)}) collective-permute-start(f32[14,64,128]{2,1,0:T(8,128)S(1)} %get-tuple-element.28), channel_id=1, source_target_pairs={{0,1},{1,2},{2,3},{3,4},{4,5},{5,6},{6,7},{7,8},{8,9},{9,10},{10,1... | collective-permute-start | bytes 1376264 | tf_op jit(solution)/shard_map/ppermute | solution.py:27
  41.9 3.2 %collective-permute-start.3 = (f32[14,64,128]{2,1,0:T(8,128)S(1)}, f32[14,64,128]{2,1,0:T(8,128)S(1)}, u32[]{:S(2)}, u32[]{:S(2)}) collective-permute-start(f32[14,64,128]{2,1,0:T(8,128)S(1)} %get-tuple-element.27), channel_id=1, source_target_pairs={{1,0},{2,1},{3,2},{4,3},{5,4},{6,5},{7,6},{8,7},{9,8},{10,9},{11,1... | collective-permute-start | bytes 1376264 | tf_op jit(solution)/shard_map/ppermute | solution.py:27
  45.2 0.7 fusion.73
  45.8 6.4 %collective-permute-start.7 = (bf16[256,1024]{1,0:T(8,128)(2,1)S(1)}, bf16[256,1024]{1,0:T(8,128)(2,1)S(1)}, u32[]{:S(2)}, u32[]{:S(2)}) collective-permute-start(bf16[256,1024]{1,0:T(8,128)(2,1)S(1)} %get-tuple-element.23), channel_id=1, source_target_pairs={{0,8},{1,9},{2,10},{3,11},{4,12},{5,13},{6,14},{7,15},{8,0},{9,1},... | collective-permute-start | bytes 1572872 | tf_op jit(solution)/shard_map/ppermute | solution.py:40
  52.3 2.5 %collective-permute-start.8 = (bf16[512,1024]{1,0:T(8,128)(2,1)S(1)}, bf16[512,1024]{1,0:T(8,128)(2,1)S(1)}, u32[]{:S(2)}, u32[]{:S(2)}) collective-permute-start(bf16[512,1024]{1,0:T(8,128)(2,1)S(1)} %copy-done.5), channel_id=1, source_target_pairs={{0,2},{1,3},{2,0},{3,1},{4,6},{5,7},{6,4},{7,5},{8,10},{9,11},{10,... | collective-permute-start | bytes 3145736 | tf_op jit(solution)/shard_map/ppermute | solution.py:40
  54.8 2.6 %collective-permute-done.3 = f32[14,64,128]{2,1,0:T(8,128)S(1)} collective-permute-done((f32[14,64,128]{2,1,0:T(8,128)S(1)}, f32[14,64,128]{2,1,0:T(8,128)S(1)}, u32[]{:S(2)}, u32[]{:S(2)}) %collective-permute-start.3) | collective-permute-done | bytes 458784 | tf_op jit(solution)/shard_map/ppermute | solution.py:27
  57.6 0.6 copy-done.9
  58.6 0.7 slice-done
  59.5 1.3 fusion.14
  61.2 1.2 fusion.22
  62.8 1.0 fusion.16
  64.1 0.8 copy-done.4
  64.8 6.7 %fusion.20 = bf16[8,64,128]{2,1,0:T(8,128)(2,1)S(1)} fusion(f32[8,64,320]{1,2,0:T(8,128)S(1)} %bitcast.201, f32[8,320,128]{2,1,0:T(8,128)S(1)} %bitcast.206, f32[20,64,128]{2,1,0:T(8,128)S(1)} %fusion.14, f32[20,64,128]{2,1,0:T(8,128)S(1)} %fusion.69, f32[16,64,128]{2,1,0:T(8,128)S(1)} %fusion.22, f32[8,64,128]{2,1,0:T(8,128)S(1)} %fusion.18, ...), kind=kOutput, calls=%fused_computation.28 | convolution fusion | flops 127139840 | bytes 4194340 | tf_op jit(solution)/shard_map/wsk,wkc->wsc/dot_general | solution.py:78
  71.5 1.4 collective-permute-done.7
  72.9 6.2 %collective-permute-done.8 = bf16[512,1024]{1,0:T(8,128)(2,1)S(1)} collective-permute-done((bf16[512,1024]{1,0:T(8,128)(2,1)S(1)}, bf16[512,1024]{1,0:T(8,128)(2,1)S(1)}, u32[]{:S(2)}, u32[]{:S(2)}) %collective-permute-start.8) | collective-permute-done | bytes 1048608 | tf_op jit(solution)/shard_map/ppermute | solution.py:40
  79.2 0.4 add_convert_fusion.3
  79.6 4.9 %collective-permute-start.9 = (bf16[128,1024]{1,0:T(8,128)(2,1)S(1)}, bf16[128,1024]{1,0:T(8,128)(2,1)S(1)}, u32[]{:S(2)}, u32[]{:S(2)}) collective-permute-start(bf16[128,1024]{1,0:T(8,128)(2,1)S(1)} %get-tuple-element.22), channel_id=1, source_target_pairs={{0,1},{1,2},{2,3},{3,4},{4,5},{5,6},{6,7},{7,8},{8,9},{9,10},{10,1... | collective-permute-start | bytes 786440 | tf_op jit(solution)/shard_map/ppermute | solution.py:27
  84.6 2.1 %collective-permute-start.10 = (bf16[128,1024]{1,0:T(8,128)(2,1)S(1)}, bf16[128,1024]{1,0:T(8,128)(2,1)S(1)}, u32[]{:S(2)}, u32[]{:S(2)}) collective-permute-start(bf16[128,1024]{1,0:T(8,128)(2,1)S(1)} %get-tuple-element.21), channel_id=1, source_target_pairs={{1,0},{2,1},{3,2},{4,3},{5,4},{6,5},{7,6},{8,7},{9,8},{10,9},{11,1... | collective-permute-start | bytes 786440 | tf_op jit(solution)/shard_map/ppermute | solution.py:27
  86.7 1.3 collective-permute-start.11
  88.0 6.2 %collective-permute-start.13 = (bf16[512,128]{1,0:T(8,128)(2,1)S(1)}, bf16[512,128]{1,0:T(8,128)(2,1)S(1)}, u32[]{:S(2)}, u32[]{:S(2)}) collective-permute-start(bf16[512,128]{1,0:T(8,128)(2,1)S(1)} %bitcast.217), channel_id=1, source_target_pairs={{0,8},{1,9},{2,10},{3,11},{4,12},{5,13},{6,14},{7,15},{8,0},{9,1},... | collective-permute-start | bytes 393224 | tf_op jit(solution)/shard_map/ppermute | solution.py:40
  94.4 0.4 fusion.23
  94.8 0.4 fusion.3
  95.2 5.5 %collective-permute-done.13 = bf16[512,128]{1,0:T(8,128)(2,1)S(1)} collective-permute-done((bf16[512,128]{1,0:T(8,128)(2,1)S(1)}, bf16[512,128]{1,0:T(8,128)(2,1)S(1)}, u32[]{:S(2)}, u32[]{:S(2)}) %collective-permute-start.13) | collective-permute-done | bytes 131104 | tf_op jit(solution)/shard_map/ppermute | solution.py:40
  100.8 0.4 fusion.4
  101.2 10.3 %convolution_convert_fusion.refs_0_.refs_1_.refs_2_.refs_3_.refs_5_.refs_6_.refs_7_ = bf16[2304,2048]{1,0:T(8,128)(2,1)S(1)} fusion(bf16[2304,1024]{1,0:T(8,128)(2,1)S(1)} %fusion.4, bf16[1024,3072]{1,0:T(8,128)(2,1)S(1)} %bitcast.219), kind=kOutput, calls=%fused_computation | convolution fusion | flops 9668395008 | bytes 18350080 | tf_op jit(solution)/shard_map/dot_general | solution.py:221
  111.5 3.6 %copy-done.2 = bf16[2304,2048]{1,0:T(8,128)(2,1)} copy-done((bf16[2304,2048]{1,0:T(8,128)(2,1)}, bf16[2304,2048]{1,0:T(8,128)(2,1)S(1)}, u32[]{:S(2)}) %copy-start.2) | copy-done | bytes 9437208
  115.2 1.4 slice.371
  116.6 3.5 %collective-permute-start.14 = (bf16[512,2048]{1,0:T(8,128)(2,1)}, bf16[512,2048]{1,0:T(8,128)(2,1)S(1)}, u32[]{:S(2)}, u32[]{:S(2)}) collective-permute-start(bf16[512,2048]{1,0:T(8,128)(2,1)} %slice.371), channel_id=1, source_target_pairs={{0,1},{1,0},{2,3},{3,2},{4,5},{5,4},{6,7},{7,6},{8,9},{9,8},{10,11... | collective-permute-start | bytes 6291464 | tf_op jit(solution)/shard_map/ppermute | solution.py:40
  120.3 0.7 pad_add_fusion.table_ref
  121.0 3.9 %fusion.11.q_ref = bf16[1024,512]{1,0:T(8,128)(2,1)} fusion(bf16[512,1024]{1,0:T(8,128)(2,1)S(1)} %add_convert_fusion.3, bf16[1024,3072]{1,0:T(8,128)(2,1)} %param.19), kind=kOutput, calls=%fused_computation.14 | convolution fusion | flops 1074790400 | bytes 4194304 | tf_op jit(solution)/shard_map/dot_general | solution.py:213
  124.9 1.3 copy-done.7
  126.2 18.8 %shard_map.109 = bf16[512,1024]{1,0:T(8,128)(2,1)} custom-call(s32[8,8]{1,0:T(8,128)} %pad_add_fusion.table_ref, bf16[1024,512]{1,0:T(8,128)(2,1)} %fusion.11.q_ref, bf16[2304,2048]{1,0:T(8,128)(2,1)} %copy-done.2, bf16[2304,2048]{1,0:T(8,128)(2,1)} %copy-done.2, bf16[2304,2048]{1,0:T(8,128)(2,1)} %copy-done.2, bf16[2304,2048]{1,0:T(8,128)(2,1)} %copy-done.2, ...), custom_call_target="tpu_custom_call" | custom-call | tf_op jit(solution)/shard_map/pallas_call | solution.py:168
  (115 shorter events, 3.8 us)
Async XLA Ops:
  0.0 79.2 %copy-start = (bf16[128,1024]{1,0:T(8,128)(2,1)S(1)}, bf16[128,1024]{1,0:T(8,128)(2,1)}, u32[]{:S(2)}) copy-start(bf16[128,1024]{1,0:T(8,128)(2,1)} %param.18) | copy-start | bytes 786436
  3.1 7.3 %copy-start.5 = (bf16[512,1024]{1,0:T(8,128)(2,1)S(1)}, bf16[512,1024]{1,0:T(8,128)(2,1)}, u32[]{:S(2)}) copy-start(bf16[512,1024]{1,0:T(8,128)(2,1)} %param.11) | copy-start | bytes 3145732
  4.7 28.4 %copy-start.6 = (f32[512,128]{1,0:T(8,128)S(1)}, f32[512,128]{1,0:T(8,128)}, u32[]{:S(2)}) copy-start(f32[512,128]{1,0:T(8,128)} %param.12) | copy-start | bytes 786436
  4.7 20.9 %collective-permute-start = (f32[8,64,448]{2,1,0:T(8,128)S(1)}, f32[8,64,448]{2,1,0:T(8,128)S(1)}, u32[]{:S(2)}, u32[]{:S(2)}) collective-permute-start(f32[8,64,448]{2,1,0:T(8,128)S(1)} %pad_maximum_fusion.1), channel_id=1, source_target_pairs={{0,1},{1,2},{2,3},{3,4},{4,5},{5,6},{6,7},{7,8},{8,9},{9,10},{10,1... | collective-permute-start | bytes 2752520 | tf_op jit(solution)/shard_map/ppermute | solution.py:27
  8.5 24.6 %collective-permute-start.1 = (f32[8,64,448]{2,1,0:T(8,128)S(1)}, f32[8,64,448]{2,1,0:T(8,128)S(1)}, u32[]{:S(2)}, u32[]{:S(2)}) collective-permute-start(f32[8,64,448]{2,1,0:T(8,128)S(1)} %pad_maximum_fusion.1), channel_id=1, source_target_pairs={{1,0},{2,1},{3,2},{4,3},{5,4},{6,5},{7,6},{8,7},{9,8},{10,9},{11,1... | collective-permute-start | bytes 2752520 | tf_op jit(solution)/shard_map/ppermute | solution.py:27
  10.5 35.3 %collective-permute-start.4 = (bf16[256,1024]{1,0:T(8,128)(2,1)S(1)}, bf16[256,1024]{1,0:T(8,128)(2,1)S(1)}, u32[]{:S(2)}, u32[]{:S(2)}) collective-permute-start(bf16[256,1024]{1,0:T(8,128)(2,1)S(1)} %get-tuple-element.24), channel_id=1, source_target_pairs={{0,4},{1,5},{2,6},{3,7},{4,0},{5,1},{6,2},{7,3},{8,12},{9,13},{10,... | collective-permute-start | bytes 1572872 | tf_op jit(solution)/shard_map/ppermute | solution.py:40
  10.8 41.5 %collective-permute-start.5 = (bf16[256,1024]{1,0:T(8,128)(2,1)S(1)}, bf16[256,1024]{1,0:T(8,128)(2,1)S(1)}, u32[]{:S(2)}, u32[]{:S(2)}) collective-permute-start(bf16[256,1024]{1,0:T(8,128)(2,1)S(1)} %get-tuple-element.24), channel_id=1, source_target_pairs={{0,8},{1,9},{2,10},{3,11},{4,12},{5,13},{6,14},{7,15},{8,0},{9,1},... | collective-permute-start | bytes 1572872 | tf_op jit(solution)/shard_map/ppermute | solution.py:40
  38.3 7.5 %copy-start.3 = (f32[12,64,128]{2,1,0:T(8,128)}, f32[12,64,128]{2,1,0:T(8,128)S(1)}, u32[]{:S(2)}) copy-start(f32[12,64,128]{2,1,0:T(8,128)S(1)} %fusion.15) | copy-start | bytes 1179652
  38.6 6.5 %copy-start.10 = (f32[9]{0:T(128)S(1)}, f32[9]{0:T(128)}, u32[]{:S(2)}) copy-start(f32[9]{0:T(128)} %param.17) | copy-start | bytes 112
  40.0 14.8 %collective-permute-start.2 = (f32[14,64,128]{2,1,0:T(8,128)S(1)}, f32[14,64,128]{2,1,0:T(8,128)S(1)}, u32[]{:S(2)}, u32[]{:S(2)}) collective-permute-start(f32[14,64,128]{2,1,0:T(8,128)S(1)} %get-tuple-element.28), channel_id=1, source_target_pairs={{0,1},{1,2},{2,3},{3,4},{4,5},{5,6},{6,7},{7,8},{8,9},{9,10},{10,1... | collective-permute-start | bytes 1376264 | tf_op jit(solution)/shard_map/ppermute | solution.py:27
  41.9 15.5 %collective-permute-start.3 = (f32[14,64,128]{2,1,0:T(8,128)S(1)}, f32[14,64,128]{2,1,0:T(8,128)S(1)}, u32[]{:S(2)}, u32[]{:S(2)}) collective-permute-start(f32[14,64,128]{2,1,0:T(8,128)S(1)} %get-tuple-element.27), channel_id=1, source_target_pairs={{1,0},{2,1},{3,2},{4,3},{5,4},{6,5},{7,6},{8,7},{9,8},{10,9},{11,1... | collective-permute-start | bytes 1376264 | tf_op jit(solution)/shard_map/ppermute | solution.py:27
  45.1 26.4 %collective-permute-start.6 = (bf16[256,1024]{1,0:T(8,128)(2,1)S(1)}, bf16[256,1024]{1,0:T(8,128)(2,1)S(1)}, u32[]{:S(2)}, u32[]{:S(2)}) collective-permute-start(bf16[256,1024]{1,0:T(8,128)(2,1)S(1)} %get-tuple-element.23), channel_id=1, source_target_pairs={{0,4},{1,5},{2,6},{3,7},{4,0},{5,1},{6,2},{7,3},{8,12},{9,13},{10,... | collective-permute-start | bytes 1572872 | tf_op jit(solution)/shard_map/ppermute | solution.py:40
  45.8 27.1 %collective-permute-start.7 = (bf16[256,1024]{1,0:T(8,128)(2,1)S(1)}, bf16[256,1024]{1,0:T(8,128)(2,1)S(1)}, u32[]{:S(2)}, u32[]{:S(2)}) collective-permute-start(bf16[256,1024]{1,0:T(8,128)(2,1)S(1)} %get-tuple-element.23), channel_id=1, source_target_pairs={{0,8},{1,9},{2,10},{3,11},{4,12},{5,13},{6,14},{7,15},{8,0},{9,1},... | collective-permute-start | bytes 1572872 | tf_op jit(solution)/shard_map/ppermute | solution.py:40
  52.3 26.9 %collective-permute-start.8 = (bf16[512,1024]{1,0:T(8,128)(2,1)S(1)}, bf16[512,1024]{1,0:T(8,128)(2,1)S(1)}, u32[]{:S(2)}, u32[]{:S(2)}) collective-permute-start(bf16[512,1024]{1,0:T(8,128)(2,1)S(1)} %copy-done.5), channel_id=1, source_target_pairs={{0,2},{1,3},{2,0},{3,1},{4,6},{5,7},{6,4},{7,5},{8,10},{9,11},{10,... | collective-permute-start | bytes 3145736 | tf_op jit(solution)/shard_map/ppermute | solution.py:40
  54.8 2.8 %copy-start.8 = (f32[14,64,128]{2,1,0:T(8,128)}, f32[14,64,128]{2,1,0:T(8,128)S(1)}, u32[]{:S(2)}) copy-start(f32[14,64,128]{2,1,0:T(8,128)S(1)} %collective-permute-done.2) | copy-start | bytes 1376260
  57.4 0.8 copy-start.9
  58.3 1.0 slice-start
  58.4 1.0 slice-start.1
  58.4 1.1 slice-start.2
  63.8 1.0 copy-start.4
  79.2 22.0 %slice-start.3 = ((s8[6291456]{0:T(1024)(128)(4,1)}), s8[4194304]{0:T(1024)(128)(4,1)S(1)}, s32[]{:S(2)}) async-start(s8[6291456]{0:T(1024)(128)(4,1)} %bitcast.218), calls=%async_computation.3 | async-start | bytes 8388608
  79.6 14.6 %collective-permute-start.9 = (bf16[128,1024]{1,0:T(8,128)(2,1)S(1)}, bf16[128,1024]{1,0:T(8,128)(2,1)S(1)}, u32[]{:S(2)}, u32[]{:S(2)}) collective-permute-start(bf16[128,1024]{1,0:T(8,128)(2,1)S(1)} %get-tuple-element.22), channel_id=1, source_target_pairs={{0,1},{1,2},{2,3},{3,4},{4,5},{5,6},{6,7},{7,8},{8,9},{9,10},{10,1... | collective-permute-start | bytes 786440 | tf_op jit(solution)/shard_map/ppermute | solution.py:27
  84.6 9.7 %collective-permute-start.10 = (bf16[128,1024]{1,0:T(8,128)(2,1)S(1)}, bf16[128,1024]{1,0:T(8,128)(2,1)S(1)}, u32[]{:S(2)}, u32[]{:S(2)}) collective-permute-start(bf16[128,1024]{1,0:T(8,128)(2,1)S(1)} %get-tuple-element.21), channel_id=1, source_target_pairs={{1,0},{2,1},{3,2},{4,3},{5,4},{6,5},{7,6},{8,7},{9,8},{10,9},{11,1... | collective-permute-start | bytes 786440 | tf_op jit(solution)/shard_map/ppermute | solution.py:27
  86.7 7.6 %collective-permute-start.11 = (bf16[512,128]{1,0:T(8,128)(2,1)S(1)}, bf16[512,128]{1,0:T(8,128)(2,1)S(1)}, u32[]{:S(2)}, u32[]{:S(2)}) collective-permute-start(bf16[512,128]{1,0:T(8,128)(2,1)S(1)} %bitcast.215), channel_id=1, source_target_pairs={{0,2},{1,3},{2,0},{3,1},{4,6},{5,7},{6,4},{7,5},{8,10},{9,11},{10,... | collective-permute-start | bytes 393224 | tf_op jit(solution)/shard_map/ppermute | solution.py:40
  88.0 6.8 %collective-permute-start.12 = (bf16[512,128]{1,0:T(8,128)(2,1)S(1)}, bf16[512,128]{1,0:T(8,128)(2,1)S(1)}, u32[]{:S(2)}, u32[]{:S(2)}) collective-permute-start(bf16[512,128]{1,0:T(8,128)(2,1)S(1)} %bitcast.216), channel_id=1, source_target_pairs={{0,4},{1,5},{2,6},{3,7},{4,0},{5,1},{6,2},{7,3},{8,12},{9,13},{10,... | collective-permute-start | bytes 393224 | tf_op jit(solution)/shard_map/ppermute | solution.py:40
  88.0 12.8 %collective-permute-start.13 = (bf16[512,128]{1,0:T(8,128)(2,1)S(1)}, bf16[512,128]{1,0:T(8,128)(2,1)S(1)}, u32[]{:S(2)}, u32[]{:S(2)}) collective-permute-start(bf16[512,128]{1,0:T(8,128)(2,1)S(1)} %bitcast.217), channel_id=1, source_target_pairs={{0,8},{1,9},{2,10},{3,11},{4,12},{5,13},{6,14},{7,15},{8,0},{9,1},... | collective-permute-start | bytes 393224 | tf_op jit(solution)/shard_map/ppermute | solution.py:40
  94.3 6.9 %slice-start.4 = ((s8[6291456]{0:T(1024)(128)(4,1)}), s8[2097152]{0:T(1024)(128)(4,1)S(1)}, s32[]{:S(2)}) async-start(s8[6291456]{0:T(1024)(128)(4,1)} %bitcast.218), calls=%async_computation.4 | async-start | bytes 4194304
  111.5 3.6 %copy-start.2 = (bf16[2304,2048]{1,0:T(8,128)(2,1)}, bf16[2304,2048]{1,0:T(8,128)(2,1)S(1)}, u32[]{:S(2)}) copy-start(bf16[2304,2048]{1,0:T(8,128)(2,1)S(1)} %convolution_convert_fusion.refs_0_.refs_1_.refs_2_.refs_3_.refs_5_.refs_6_.refs_7_) | copy-start | bytes 28311556
  115.2 4.9 %copy-start.11 = (s32[8,3]{0,1:T(4,128)S(1)}, s32[8,3]{0,1:T(4,128)}, u32[]{:S(2)}) copy-start(s32[8,3]{0,1:T(4,128)} %param.15) | copy-start | bytes 292
  115.2 5.0 %copy-start.12 = (s32[8,4]{0,1:T(4,128)S(1)}, s32[8,4]{0,1:T(4,128)}, u32[]{:S(2)}) copy-start(s32[8,4]{0,1:T(4,128)} %param.16) | copy-start | bytes 388
  115.2 5.1 %copy-start.13 = (s32[4]{0:T(128)S(1)}, s32[4]{0:T(128)}, u32[]{:S(2)}) copy-start(s32[4]{0:T(128)} %constant.6.clone) | copy-start | bytes 52
  116.6 8.2 %collective-permute-start.14 = (bf16[512,2048]{1,0:T(8,128)(2,1)}, bf16[512,2048]{1,0:T(8,128)(2,1)S(1)}, u32[]{:S(2)}, u32[]{:S(2)}) collective-permute-start(bf16[512,2048]{1,0:T(8,128)(2,1)} %slice.371), channel_id=1, source_target_pairs={{0,1},{1,0},{2,3},{3,2},{4,5},{5,4},{6,7},{7,6},{8,9},{9,8},{10,11... | collective-permute-start | bytes 6291464 | tf_op jit(solution)/shard_map/ppermute | solution.py:40
  124.9 1.3 copy-start.7
  126.2 18.8 %copy-start.1 = (bf16[128,1024]{1,0:T(8,128)(2,1)S(1)}, bf16[128,1024]{1,0:T(8,128)(2,1)}, u32[]{:S(2)}) copy-start(bf16[128,1024]{1,0:T(8,128)(2,1)} %param.18) | copy-start | bytes 786436
